TPU v7x, 32 devices: a whole 2x2x4 slice. The times are simulated.
32 devices in a mesh: group: 2 (over x), seq: 8 (over z, y), dp: 2 (over core).
Axes of the slice: x: 2, y: 2, z: 4, core: 2. Of those that a mesh axis runs over, the one named last changes fastest.
Arguments:
- queries: bfloat16 [4, 1024, 512], P(('group', 'dp'), 'seq'), parts along dimension 0, may hold values from -6 to 6
- key_rows: bfloat16 [4, 1024, 512], P(('group', 'dp'), 'seq'), parts along dimension 0, may hold values from -6 to 6
- value_rows: bfloat16 [4, 1024, 768], P(('group', 'dp'), 'seq'), parts along dimension 0, may hold values from -6 to 6
- trunk_state: bfloat16 [4, 1024, 768], P(('group', 'dp'), 'seq'), parts along dimension 0, may hold values from -6 to 6
- skip_input: bfloat16 [4, 2048, 768], P(('group', 'dp'), 'seq'), parts along dimension 0, may hold values from -6 to 6
- norm_gain: bfloat16 [768], replicated, may hold values from 0.099609375 to 1.8984375
- conv_weight: bfloat16 [3840, 384], replicated, may hold values from -0.09375 to 0.09375
- cotangent: bfloat16 [4, 2048, 384], P(('group', 'dp'), 'seq'), parts along dimension 0, may hold values from -6 to 6
Outputs:
- decoded: bfloat16 [4, 2048, 384], P(('group', 'dp'), 'seq'), parts along dimension 0
- grad_queries: bfloat16 [4, 1024, 512], P(('group', 'dp'), 'seq'), parts along dimension 0
- grad_keys: bfloat16 [4, 1024, 512], P(('group', 'dp'), 'seq'), parts along dimension 0
- grad_values: bfloat16 [4, 1024, 768], P(('group', 'dp'), 'seq'), parts along dimension 0
- grad_trunk: bfloat16 [4, 1024, 768], P(('group', 'dp'), 'seq'), parts along dimension 0
- grad_skip: bfloat16 [4, 2048, 768], P(('group', 'dp'), 'seq'), parts along dimension 0
- grad_weight: float32 [7680, 384], P(('group', 'seq', 'dp')), parts along dimension 0
There are 2 independent parts, one for each index of `group`. A program takes and returns all parts, laid end to end along the dimension named above; an argument that names none is the same for every part. Nothing has to cross between parts.
All inputs are finite; a program needn't handle non-finite values.
Results may differ from a plain program's by a relative error of at most 0.029.
Values may be sent and summed in bfloat16 or wider, within the bound.
No kernel may reach another device: no remote copies, remote signals or barrier semaphores. Data moves between devices by JAX's collectives and lax.ppermute only.
A program may use at most 128 MiB of HBM per device.

v0:
```python
import math

import jax
import jax.numpy as jnp
from jax import lax
from jax.sharding import PartitionSpec as P

H = 4
DK = 128
DV = 192
C = 768
CO = 384
KW = 5


def extended(array, sides, width):
    for axis, dim in sides:
        count, length = (lax.axis_size(axis), array.shape[dim])
        up = [(i, (i + 1) % count) for i in range(count - 1)]
        down = [(j, i) for i, j in up]
        last = lax.slice_in_dim(array, length - width, length, axis=dim)
        initial = lax.slice_in_dim(array, 0, width, axis=dim)
        before = lax.ppermute(last, axis, up)
        after = lax.ppermute(initial, axis, down)
        array = jnp.concatenate([before, array, after], axis=dim)
    return array


def gelu_parts(preact):
    cdf_value = 0.5 * (1.0 + jax.scipy.special.erf(preact * (1.0 / math.sqrt(2.0))))
    density = jnp.exp(-0.5 * preact * preact) * (1.0 / math.sqrt(2.0 * math.pi))
    return (preact * cdf_value, cdf_value + preact * density)


def window_rows(padded, kernel, row_count):
    return jnp.concatenate(
        [padded[offset : offset + row_count] for offset in range(kernel)], axis=1
    )


def body(queries, key_rows, value_rows, trunk_state, skip_input, norm_gain, conv_weight, cotangent):
    score_scale = DK ** (-0.5)
    local_tokens = queries.shape[1]
    positions = 2 * local_tokens
    half_kernel = KW // 2
    query_heads = queries[0].reshape(local_tokens, H, DK)
    gathered = (
        lax.all_gather(key_rows, "seq", axis=1, tiled=True),
        lax.all_gather(value_rows, "seq", axis=1, tiled=True),
    )
    all_keys = gathered[0][0].reshape(-1, H, DK)
    all_values = gathered[1][0].reshape(-1, H, DV)
    scores = (
        jnp.einsum("ihd,jhd->hij", query_heads, all_keys, preferred_element_type=jnp.float32)
        * score_scale
    )
    row_peak = jnp.max(scores, axis=2, keepdims=True)
    row_total = jnp.sum(jnp.exp(scores - row_peak), axis=2, keepdims=True)
    logsum = row_peak + jnp.log(row_total)
    softmax = jnp.exp(scores - logsum)
    rounded = softmax.astype(jnp.bfloat16)
    attended = jnp.einsum(
        "hij,jhd->ihd", rounded, all_values, preferred_element_type=jnp.float32
    ).astype(jnp.bfloat16)
    hidden = trunk_state[0].astype(jnp.float32) + attended.reshape(local_tokens, H * DV).astype(
        jnp.float32
    )
    merged = jnp.repeat(hidden, 2, axis=0) + skip_input[0].astype(jnp.float32)
    inverse = lax.rsqrt(jnp.mean(merged * merged, axis=1, keepdims=True) + 1e-06)
    channel_gain = norm_gain.astype(jnp.float32)
    normed = (merged * inverse * channel_gain).astype(jnp.bfloat16)
    padded = extended(normed, (("seq", 0),), half_kernel)
    columns = window_rows(padded, KW, positions)
    preact = jnp.dot(columns, conv_weight, preferred_element_type=jnp.float32)
    activated, derivative = gelu_parts(preact)
    decoded = activated.astype(jnp.bfloat16)
    grad_pre = (cotangent[0].astype(jnp.float32) * derivative).astype(jnp.bfloat16)
    grad_padded = extended(grad_pre, (("seq", 0),), half_kernel)
    norm_scale = (lax.axis_size("dp") * positions * lax.axis_size("seq")) ** (-0.5)
    grad_weight = lax.psum_scatter(
        lax.dot_general(
            columns, grad_pre, (((0,), (0,)), ((), ())), preferred_element_type=jnp.float32
        )
        * norm_scale,
        ("seq", "dp"),
        scatter_dimension=0,
        tiled=True,
    )
    stacked = jnp.stack(
        [
            grad_padded[2 * half_kernel - offset : 2 * half_kernel - offset + positions]
            for offset in range(KW)
        ],
        axis=1,
    )
    weight_blocks = conv_weight.reshape(KW, C, CO)
    grad_normed = jnp.einsum(
        "pko,kco->pc", stacked, weight_blocks, preferred_element_type=jnp.float32
    )
    scaled_grad = grad_normed * channel_gain
    grad_merged = inverse * scaled_grad - merged * inverse**3 * jnp.mean(
        scaled_grad * merged, axis=1, keepdims=True
    )
    grad_skip = grad_merged.astype(jnp.bfloat16)
    grad_trunk = grad_merged.reshape(local_tokens, 2, C).sum(axis=1).astype(jnp.bfloat16)
    grad_heads = grad_trunk.reshape(local_tokens, H, DV)
    row_delta = jnp.sum(grad_heads.astype(jnp.float32) * attended.astype(jnp.float32), axis=2)
    value_grad = jnp.einsum(
        "ihd,jhd->hij", grad_heads, all_values, preferred_element_type=jnp.float32
    )
    slopes = (softmax * (value_grad - row_delta.T[:, :, None])).astype(jnp.bfloat16)
    grad_queries = (
        jnp.einsum("hij,jhd->ihd", slopes, all_keys, preferred_element_type=jnp.float32)
        * score_scale
    ).astype(jnp.bfloat16)
    key_part = (
        jnp.einsum("hij,ihd->jhd", slopes, query_heads, preferred_element_type=jnp.float32)
        * score_scale
    )
    value_part = jnp.einsum("hij,ihd->jhd", rounded, grad_heads, preferred_element_type=jnp.float32)
    summed = lax.psum_scatter(
        jnp.concatenate(
            [
                key_part.reshape(lax.axis_size("seq") * local_tokens, H * DK),
                value_part.reshape(lax.axis_size("seq") * local_tokens, H * DV),
            ],
            axis=1,
        ).astype(jnp.bfloat16),
        "seq",
        scatter_dimension=0,
        tiled=True,
    ).astype(jnp.float32)
    grad_keys = summed[:, : H * DK].astype(jnp.bfloat16)
    grad_values = summed[:, H * DK :].astype(jnp.bfloat16)
    return (
        decoded[None],
        grad_queries.reshape(local_tokens, H * DK)[None],
        grad_keys[None],
        grad_values[None],
        grad_trunk[None],
        grad_skip[None],
        grad_weight,
    )


def solution(mesh):
    return jax.shard_map(
        body,
        mesh=mesh,
        in_specs=(
            P(("group", "dp"), "seq", None),
            P(("group", "dp"), "seq", None),
            P(("group", "dp"), "seq", None),
            P(("group", "dp"), "seq", None),
            P(("group", "dp"), "seq", None),
            P(),
            P(),
            P(("group", "dp"), "seq", None),
        ),
        out_specs=(
            P(("group", "dp"), "seq", None),
            P(("group", "dp"), "seq", None),
            P(("group", "dp"), "seq", None),
            P(("group", "dp"), "seq", None),
            P(("group", "dp"), "seq", None),
            P(("group", "dp"), "seq", None),
            P(("group", "seq", "dp"), None),
        ),
        check_vma=False,
    )
```

profile of v0, /device:TPU:0, one launch (start us, length us, event | category | flops | bytes accessed | tf_op | source)
XLA Modules:
  0.0 324.4 jit_solution(8928119127070148307)
XLA Ops:
  7.2 1.8 copy.24
  9.1 0.7 all-gather.5.cloned.1.call-update
  9.9 0.7 convert_element_type.100
  10.6 1.0 copy.35
  11.6 41.2 %all-gather.3.cloned.1.call-done = bf16[1,1024,512]{1,2,0:T(8,128)(2,1)} async-done(((bf16[1,128,512]{1,2,0:T(8,128)(2,1)}), bf16[1,1024,512]{1,2,0:T(8,128)(2,1)}) %all-gather.3.cloned.1.call-update) | async-done | bytes 1048592 | tf_op jit(solution)/shard_map/all_gather | solution.py:48
  52.8 1.8 multiply_reduce_fusion
  54.6 1.3 copy-done.1
  55.9 0.5 exponential_reduce_fusion
  56.4 41.8 %all-gather.5.cloned.1.call-done = bf16[1,1024,768]{2,1,0:T(8,128)(2,1)} async-done(((bf16[1,128,768]{2,1,0:T(8,128)(2,1)}), bf16[1,1024,768]{2,1,0:T(8,128)(2,1)}) %all-gather.5.cloned.1.call-update) | async-done | bytes 1572880 | tf_op jit(solution)/shard_map/all_gather | solution.py:49
  98.2 2.6 copy.27
  100.8 2.8 fusion.2
  103.5 0.9 copy.28
  104.5 1.0 convert_add_fusion.1
  105.5 1.2 broadcast_in_dim.12
  106.7 2.6 reshape.93
  109.2 2.6 broadcast_in_dim.26
  111.8 1.3 fusion.6
  113.2 1.3 multiply_convert_fusion.2
  114.5 2.6 collective-permute-start
  117.1 1.3 collective-permute-start.1
  118.5 0.1 fusion.18
  118.6 4.3 %collective-permute-done.1 = bf16[2,768]{1,0:T(2,128)(2,1)S(1)} collective-permute-done((bf16[2,768]{1,0:T(2,128)(2,1)S(1)}, bf16[2,768]{1,0:T(2,128)(2,1)S(1)}, u32[]{:S(2)}, u32[]{:S(2)}) %collective-permute-start.1) | collective-permute-done | bytes 3104 | tf_op jit(solution)/shard_map/ppermute | solution.py:24
  122.9 0.1 fusion.8
  123.0 0.1 fusion.17
  123.1 2.0 fusion.16
  125.2 1.4 collective-permute-start.2
  126.6 5.4 %collective-permute-start.3 = (bf16[2,384]{1,0:T(2,128)(2,1)S(1)}, bf16[2,384]{1,0:T(2,128)(2,1)S(1)}, u32[]{:S(2)}, u32[]{:S(2)}) collective-permute-start(bf16[2,384]{1,0:T(2,128)(2,1)S(1)} %get-tuple-element.27), channel_id=1, source_target_pairs={{0,2},{2,4},{4,6},{6,8},{8,10},{10,12},{12,14},{1,3},{3,5},{5,7},{... | collective-permute-start | bytes 4616 | tf_op jit(solution)/shard_map/ppermute | solution.py:23
  132.2 1.1 collective-permute-done.3
  133.5 1.1 multiply_reduce_fusion.1
  134.6 1.3 convert_bitcast_fusion.1
  135.9 2.5 reshape.95
  138.4 2.8 reduce_sum.48
  141.2 1.7 copy.29
  142.9 1.1 fusion.19
  144.1 3.6 %convolution_convert_fusion = bf16[4,192,1024]{2,1,0:T(8,128)(2,1)} fusion(bf16[128,4,192]{0,2,1:T(8,128)(2,1)} %bitcast.94, f32[4,128,1024]{2,1,0:T(8,128)} %copy-done.1, f32[4,128]{1,0:T(4,128)S(1)} %log_add_fusion), kind=kOutput, calls=%fused_computation.8 | convolution fusion | flops 203685888 | bytes 3868672 | tf_op jit(solution)/shard_map/hij,ihd->jhd/dot_general | solution.py:120
  147.7 0.8 multiply_convert_fusion.1
  148.6 1.0 copy-done.5
  149.6 1.4 multiply_convert_fusion
  151.0 2.3 copy.31
  153.2 2.6 copy.32
  155.9 3.4 %pad_maximum_fusion = bf16[1024,1280]{1,0:T(8,128)(2,1)} fusion(bf16[1024,768]{1,0:T(8,128)(2,1)} %copy.32, bf16[1024,512]{1,0:T(8,128)(2,1)} %copy.31), kind=kLoop, calls=%fused_computation.1 | loop fusion | flops 5242880 | bytes 5242880 | tf_op jit(solution)/shard_map/concatenate | solution.py:122
  159.3 5.3 %convolution_multiply_fusion = f32[3840,384]{1,0:T(8,128)} fusion(bf16[256,3840]{1,0:T(8,128)(2,1)} %copy-done.7, bf16[256,384]{1,0:T(8,128)(2,1)S(1)} %get-tuple-element.23), kind=kOutput, calls=%fused_computation | convolution fusion | flops 756449280 | bytes 8060928 | tf_op jit(solution)/shard_map/dot_general | solution.py:81
  164.7 2.0 fusion.3
  166.6 0.8 copy.33
  167.4 64.6 %reduce-scatter.3.cloned.1.call-done = bf16[128,1280]{1,0:T(8,128)(2,1)} async-done(((bf16[1024,1280]{1,0:T(8,128)(2,1)}), bf16[128,1280]{1,0:T(8,128)(2,1)}) %reduce-scatter.3.cloned.1.call-update) | async-done | bytes 327696 | tf_op jit(solution)/shard_map/reduce_scatter | solution.py:121
  232.0 1.6 slice_bitcast_fusion.1
  233.6 1.6 slice_bitcast_fusion
  235.2 82.7 %reduce-scatter.5.cloned.1.call-done = f32[240,384]{1,0:T(8,128)} async-done(((f32[3840,384]{1,0:T(8,128)}), f32[240,384]{1,0:T(8,128)}) %reduce-scatter.5.cloned.1.call-update) | async-done | bytes 368656 | tf_op jit(solution)/shard_map/reduce_scatter | solution.py:80
  (49 shorter events, 0.7 us)
Async XLA Ops:
  7.2 115.9 %copy-start = (bf16[3840,384]{1,0:T(8,128)(2,1)S(1)}, bf16[3840,384]{1,0:T(8,128)(2,1)}, u32[]{:S(2)}) copy-start(bf16[3840,384]{1,0:T(8,128)(2,1)} %param.14) | copy-start | bytes 8847364
  7.2 45.6 %all-gather.3.cloned.1.call-start = ((), (), s32[]{:S(2)}) async-start(), calls=%async_computation.2 | async-start | bytes 1179648 | tf_op jit(solution)/shard_map/all_gather | solution.py:48
  9.1 89.1 %all-gather.5.cloned.1.call-start = ((), (), s32[]{:S(2)}) async-start(), calls=%async_computation.3 | async-start | bytes 1769472 | tf_op jit(solution)/shard_map/all_gather | solution.py:49
  9.8 222.2 %reduce-scatter.3.cloned.1.call-start = ((), (), s32[]{:S(2)}) async-start(), calls=%async_computation.4 | async-start | bytes 2949120 | tf_op jit(solution)/shard_map/reduce_scatter | solution.py:121
  11.6 44.8 %copy-start.11 = (bf16[1,128,512]{1,2,0:T(8,128)(2,1)}, bf16[1,128,512]{1,2,0:T(8,128)(2,1)S(1)}, u32[]{:S(2)}) copy-start(bf16[1,128,512]{1,2,0:T(8,128)(2,1)S(1)} %copy.35) | copy-start | bytes 393220
  54.5 1.3 copy-start.1
  100.8 3.7 %copy-start.13 = (bf16[1,128,768]{2,1,0:T(8,128)(2,1)S(1)}, bf16[1,128,768]{2,1,0:T(8,128)(2,1)}, u32[]{:S(2)}) copy-start(bf16[1,128,768]{2,1,0:T(8,128)(2,1)} %param.11) | copy-start | bytes 589828
  103.5 0.9 copy-start.8
  105.5 6.3 %copy-start.6 = (bf16[1,256,768]{2,1,0:T(8,128)(2,1)S(1)}, bf16[1,256,768]{2,1,0:T(8,128)(2,1)}, u32[]{:S(2)}) copy-start(bf16[1,256,768]{2,1,0:T(8,128)(2,1)} %param.12) | copy-start | bytes 1179652
  114.4 8.7 %copy-start.14 = (bf16[1,256,384]{2,1,0:T(8,128)(2,1)S(1)}, bf16[1,256,384]{2,1,0:T(8,128)(2,1)}, u32[]{:S(2)}) copy-start(bf16[1,256,384]{2,1,0:T(8,128)(2,1)} %param.15) | copy-start | bytes 589828
  114.5 3.9 %collective-permute-start = (bf16[2,768]{1,0:T(2,128)(2,1)S(1)}, bf16[2,768]{1,0:T(2,128)(2,1)S(1)}, u32[]{:S(2)}, u32[]{:S(2)}) collective-permute-start(bf16[2,768]{1,0:T(2,128)(2,1)S(1)} %get-tuple-element.26), channel_id=1, source_target_pairs={{0,2},{2,4},{4,6},{6,8},{8,10},{10,12},{12,14},{1,3},{3,5},{5,7},{... | collective-permute-start | bytes 9224 | tf_op jit(solution)/shard_map/ppermute | solution.py:23
  117.1 5.8 %collective-permute-start.1 = (bf16[2,768]{1,0:T(2,128)(2,1)S(1)}, bf16[2,768]{1,0:T(2,128)(2,1)S(1)}, u32[]{:S(2)}, u32[]{:S(2)}) collective-permute-start(bf16[2,768]{1,0:T(2,128)(2,1)S(1)} %get-tuple-element.25), channel_id=1, source_target_pairs={{2,0},{4,2},{6,4},{8,6},{10,8},{12,10},{14,12},{3,1},{5,3},{7,5},{... | collective-permute-start | bytes 9224 | tf_op jit(solution)/shard_map/ppermute | solution.py:24
  123.1 2.0 copy-start.7
  125.1 8.3 %copy-start.4 = (f32[256,768]{1,0:T(8,128)S(1)}, f32[256,768]{1,0:T(8,128)}, u32[]{:S(2)}) copy-start(f32[256,768]{1,0:T(8,128)} %reshape.93) | copy-start | bytes 2359300
  125.2 6.9 %collective-permute-start.2 = (bf16[2,384]{1,0:T(2,128)(2,1)S(1)}, bf16[2,384]{1,0:T(2,128)(2,1)S(1)}, u32[]{:S(2)}, u32[]{:S(2)}) collective-permute-start(bf16[2,384]{1,0:T(2,128)(2,1)S(1)} %get-tuple-element.28), channel_id=1, source_target_pairs={{2,0},{4,2},{6,4},{8,6},{10,8},{12,10},{14,12},{3,1},{5,3},{7,5},{... | collective-permute-start | bytes 4616 | tf_op jit(solution)/shard_map/ppermute | solution.py:24
  126.6 6.7 %collective-permute-start.3 = (bf16[2,384]{1,0:T(2,128)(2,1)S(1)}, bf16[2,384]{1,0:T(2,128)(2,1)S(1)}, u32[]{:S(2)}, u32[]{:S(2)}) collective-permute-start(bf16[2,384]{1,0:T(2,128)(2,1)S(1)} %get-tuple-element.27), channel_id=1, source_target_pairs={{0,2},{2,4},{4,6},{6,8},{8,10},{10,12},{12,14},{1,3},{3,5},{5,7},{... | collective-permute-start | bytes 4616 | tf_op jit(solution)/shard_map/ppermute | solution.py:23
  135.9 7.0 %copy-start.9 = (f32[4,128,192]{1,2,0:T(8,128)S(1)}, f32[4,128,192]{1,2,0:T(8,128)}, u32[]{:S(2)}) copy-start(f32[4,128,192]{1,2,0:T(8,128)} %copy-done.8) | copy-start | bytes 1179652
  142.9 4.8 %copy-start.2 = (f32[4,128,1024]{2,1,0:T(8,128)S(1)}, f32[4,128,1024]{2,1,0:T(8,128)}, u32[]{:S(2)}) copy-start(f32[4,128,1024]{2,1,0:T(8,128)} %copy-done.1) | copy-start | bytes 6291460
  142.9 4.8 %copy-start.3 = (bf16[1,1024,768]{1,2,0:T(8,128)(2,1)S(1)}, bf16[1,1024,768]{1,2,0:T(8,128)(2,1)}, u32[]{:S(2)}) copy-start(bf16[1,1024,768]{1,2,0:T(8,128)(2,1)} %copy.27) | copy-start | bytes 4718596
  142.9 4.8 %copy-start.10 = (bf16[128,768]{0,1:T(8,128)(2,1)S(1)}, bf16[128,768]{0,1:T(8,128)(2,1)}, u32[]{:S(2)}) copy-start(bf16[128,768]{0,1:T(8,128)(2,1)} %copy.29) | copy-start | bytes 589828
  147.7 1.9 copy-start.12
  148.6 1.0 copy-start.5
  159.3 158.6 %reduce-scatter.5.cloned.1.call-start = ((), (), s32[]{:S(2)}) async-start(), calls=%async_computation.5 | async-start | bytes 6266880 | tf_op jit(solution)/shard_map/reduce_scatter | solution.py:80
Sparse Core Ops, SparseCore 0:
  10.6 42.1 all-gather.2
  54.9 43.1 all-gather.4
  159.4 72.5 reduce-scatter.2
  236.4 81.4 reduce-scatter.4
where the time goes:
time: 325 us; the launch traced here: 324 us
  waiting for transfers between devices  236 us (73%)
  local copies, waits for them, and re-layouts  28.3 us (9%)
  matrix products  20.8 us (6%)
  other arithmetic  14 us (4%)
  between operations  14 us (4%)
  starting transfers between devices  10.9 us (3%)
    reduce_scatter x1, waiting for transfers between devices, body(): lax.psum_scatter(lax.dot_general(columns, grad_pre, (((0,), (0,)), ((), (...  82.7 us
    reduce_scatter x1, waiting for transfers between devices, body(): lax.psum_scatter(jnp.concatenate([key_part.reshape(lax.axis_size('seq') *...  64.6 us
    all_gather x1, waiting for transfers between devices, body(): lax.all_gather(value_rows, 'seq', axis=1, tiled=True)  41.8 us
    all_gather x1, waiting for transfers between devices, body(): lax.all_gather(key_rows, 'seq', axis=1, tiled=True)  41.2 us
    ppermute x2, starting transfers between devices, extended(): before = lax.ppermute(last, axis, up)  8.03 us
  transfers between devices with their start and end apart: 8, of which 6 were waited for; matrix products, arithmetic and copies ran while one was open for 5% of the time, Pallas kernels for 0%

commit v1 on v0

--- a/solution.py
+++ b/solution.py
@@ -1,3 +1,4 @@
+import functools
 import math
 
 import jax
@@ -38,18 +39,108 @@
     )
 
 
-def body(queries, key_rows, value_rows, trunk_state, skip_input, norm_gain, conv_weight, cotangent):
+def ring_order(mesh):
+    count = mesh.shape["seq"]
+    try:
+        row = mesh.devices.reshape(mesh.shape["group"], count, -1)[0, :, 0]
+        coords = [tuple(device.coords) for device in row]
+    except (AttributeError, TypeError):
+        return list(range(count))
+    varying = [d for d in range(3) if len({c[d] for c in coords}) > 1]
+    if len(varying) == 2:
+        for minor, major in (varying, varying[::-1]):
+            if len({c[minor] for c in coords}) == 2:
+                low = min(c[minor] for c in coords)
+                first = sorted((c[major], s) for s, c in enumerate(coords) if c[minor] == low)
+                second = sorted((c[major], s) for s, c in enumerate(coords) if c[minor] != low)
+                return [s for _, s in first] + [s for _, s in second[::-1]]
+    return list(range(count))
+
+
+def ring_perms(ring):
+    count = len(ring)
+    forward = [(ring[q], ring[(q + 1) % count]) for q in range(count)]
+    backward = [(ring[q], ring[(q - 1) % count]) for q in range(count)]
+    return forward, backward
+
+
+def ring_gather(block, ring):
+    count = len(ring)
+    forward, backward = ring_perms(ring)
+    left_steps = count // 2
+    right_steps = count - 1 - left_steps
+    lefts, rights = [], []
+    current = block
+    for _ in range(left_steps):
+        current = lax.ppermute(current, "seq", forward)
+        lefts.append(current)
+    current = block
+    for _ in range(right_steps):
+        current = lax.ppermute(current, "seq", backward)
+        rights.append(current)
+    return [block] + lefts + rights
+
+
+def ring_scatter_back(blocks, ring):
+    count = len(ring)
+    forward, backward = ring_perms(ring)
+    left_steps = count // 2
+    right_steps = count - 1 - left_steps
+    own = blocks[0].astype(jnp.float32)
+    lefts = blocks[1 : 1 + left_steps]
+    rights = blocks[1 + left_steps :]
+    total = own
+    if left_steps:
+        acc = lefts[-1]
+        for t in range(left_steps, 0, -1):
+            received = lax.ppermute(acc, "seq", backward).astype(jnp.float32)
+            if t == 1:
+                total = total + received
+            else:
+                acc = (received + lefts[t - 2].astype(jnp.float32)).astype(jnp.bfloat16)
+    if right_steps:
+        acc = rights[-1]
+        for t in range(right_steps, 0, -1):
+            received = lax.ppermute(acc, "seq", forward).astype(jnp.float32)
+            if t == 1:
+                total = total + received
+            else:
+                acc = (received + rights[t - 2].astype(jnp.float32)).astype(jnp.bfloat16)
+    return total
+
+
+def ring_reduce_scatter(blocks, axis, ring, forward_dir=True):
+    count = len(ring)
+    if count == 1:
+        return blocks[0]
+    forward, backward = ring_perms(ring)
+    perm = forward if forward_dir else backward
+    sign = 1 if forward_dir else -1
+    ring_table = jnp.array(ring, jnp.int32)
+    position_table = jnp.array([ring.index(s) for s in range(count)], jnp.int32)
+    position = position_table[lax.axis_index(axis)]
+
+    def block_at(offset):
+        index = ring_table[(position + count - sign * offset) % count]
+        return lax.dynamic_index_in_dim(blocks, index, axis=0, keepdims=False)
+
+    acc = block_at(1)
+    for t in range(count - 1):
+        received = lax.ppermute(acc, axis, perm)
+        acc = received + block_at(t + 2)
+    return acc
+
+
+def body(ring, queries, key_rows, value_rows, trunk_state, skip_input, norm_gain, conv_weight, cotangent):
     score_scale = DK ** (-0.5)
     local_tokens = queries.shape[1]
     positions = 2 * local_tokens
     half_kernel = KW // 2
     query_heads = queries[0].reshape(local_tokens, H, DK)
-    gathered = (
-        lax.all_gather(key_rows, "seq", axis=1, tiled=True),
-        lax.all_gather(value_rows, "seq", axis=1, tiled=True),
-    )
-    all_keys = gathered[0][0].reshape(-1, H, DK)
-    all_values = gathered[1][0].reshape(-1, H, DV)
+    key_value_blocks = ring_gather(jnp.concatenate([key_rows[0], value_rows[0]], axis=1), ring)
+    gathered = jnp.concatenate(key_value_blocks, axis=0)
+    all_keys = gathered[:, : H * DK].reshape(-1, H, DK)
+    all_values = gathered[:, H * DK :].reshape(-1, H, DV)
     scores = (
         jnp.einsum("ihd,jhd->hij", query_heads, all_keys, preferred_element_type=jnp.float32)
         * score_scale
@@ -77,14 +168,24 @@
     grad_pre = (cotangent[0].astype(jnp.float32) * derivative).astype(jnp.bfloat16)
     grad_padded = extended(grad_pre, (("seq", 0),), half_kernel)
     norm_scale = (lax.axis_size("dp") * positions * lax.axis_size("seq")) ** (-0.5)
-    grad_weight = lax.psum_scatter(
+    weight_part = (
         lax.dot_general(
             columns, grad_pre, (((0,), (0,)), ((), ())), preferred_element_type=jnp.float32
         )
-        * norm_scale,
-        ("seq", "dp"),
-        scatter_dimension=0,
-        tiled=True,
+        * norm_scale
+    )
+    seq_count, dp_count = lax.axis_size("seq"), lax.axis_size("dp")
+    weight_blocks_all = weight_part.reshape(seq_count, dp_count, -1, CO)
+    dp_summed = ring_reduce_scatter(
+        jnp.swapaxes(weight_blocks_all, 0, 1), "dp", list(range(dp_count))
+    )
+    half_co = CO // 2
+    grad_weight = jnp.concatenate(
+        [
+            ring_reduce_scatter(dp_summed[:, :, :half_co], "seq", ring, True),
+            ring_reduce_scatter(dp_summed[:, :, half_co:], "seq", ring, False),
+        ],
+        axis=1,
     )
     stacked = jnp.stack(
         [
@@ -118,18 +219,17 @@
         * score_scale
     )
     value_part = jnp.einsum("hij,ihd->jhd", rounded, grad_heads, preferred_element_type=jnp.float32)
-    summed = lax.psum_scatter(
-        jnp.concatenate(
-            [
-                key_part.reshape(lax.axis_size("seq") * local_tokens, H * DK),
-                value_part.reshape(lax.axis_size("seq") * local_tokens, H * DV),
-            ],
-            axis=1,
-        ).astype(jnp.bfloat16),
-        "seq",
-        scatter_dimension=0,
-        tiled=True,
-    ).astype(jnp.float32)
+    terms = jnp.concatenate(
+        [
+            key_part.reshape(-1, H * DK),
+            value_part.reshape(-1, H * DV),
+        ],
+        axis=1,
+    ).astype(jnp.bfloat16)
+    term_blocks = [
+        terms[m * local_tokens : (m + 1) * local_tokens] for m in range(lax.axis_size("seq"))
+    ]
+    summed = ring_scatter_back(term_blocks, ring)
     grad_keys = summed[:, : H * DK].astype(jnp.bfloat16)
     grad_values = summed[:, H * DK :].astype(jnp.bfloat16)
     return (
@@ -145,7 +245,7 @@
 
 def solution(mesh):
     return jax.shard_map(
-        body,
+        functools.partial(body, ring_order(mesh)),
         mesh=mesh,
         in_specs=(
             P(("group", "dp"), "seq", None),

time: 325 us -> 249 us (0.77)
  waiting for transfers between devices: 236 us -> 81.4 us
  starting transfers between devices: 10.9 us -> 43.4 us
  between operations: 14 us -> 43.2 us
  local copies, waits for them, and re-layouts: 28.3 us -> 43.5 us
  other arithmetic: 14 us -> 20.2 us
  matrix products: 20.8 us -> 15.8 us
    reduce_scatter x2 -> x0, waiting for transfers between devices: 147 us -> none  [the longest x1 82.7 us: body(): lax.psum_scatter(lax.dot_general(columns, grad_pre, (((0,), (0,)), ((), (...]
    all_gather x2 -> x0, waiting for transfers between devices: 82.9 us -> none  [the longest x1 41.8 us: body(): lax.all_gather(value_rows, 'seq', axis=1, tiled=True)]
    ppermute x0 -> x29, waiting for transfers between devices: none -> 76 us  [the longest x15 39.2 us: ring_reduce_scatter(): received = lax.ppermute(acc, axis, perm)]
    ppermute x0 -> x29, starting transfers between devices: none -> 32.2 us  [the longest x15 13.8 us: ring_reduce_scatter(): received = lax.ppermute(acc, axis, perm)]
    unnamed x34 -> x59, local copies, waits for them, and re-layouts: 5.04 us -> 13.8 us
    dot_general x1, matrix products: 5.3 us -> 1.22 us  [body(): lax.dot_general(columns, grad_pre, (((0,), (0,)), ((), ())), preferred_el...]
    slice x0 -> x3, local copies, waits for them, and re-layouts: none -> 4.06 us  [the longest x1 1.86 us: body(): all_keys = gathered[:, :H * DK].reshape(-1, H, DK)]
    add x0 -> x15, other arithmetic: none -> 3.49 us  [ring_reduce_scatter(): acc = received + block_at(t + 2)]
  transfers between devices with their start and end apart: 8 -> 33, of which waited for: 6 -> 25; matrix products, arithmetic and copies ran while one was open for 5% -> 9% of each run, Pallas kernels for 0% -> 0%
where the time goes in v1:
time: 249 us; the launch traced here: 247 us
  waiting for transfers between devices  81.4 us (33%)
  local copies, waits for them, and re-layouts  43.5 us (17%)
  starting transfers between devices  43.4 us (17%)
  between operations  43.2 us (17%)
  other arithmetic  20.2 us (8%)
  matrix products  15.8 us (6%)
    ppermute x15, waiting for transfers between devices, ring_reduce_scatter(): received = lax.ppermute(acc, axis, perm)  39.2 us
    ppermute x4, waiting for transfers between devices, ring_gather(): current = lax.ppermute(current, 'seq', forward)  19.4 us
    unnamed x59, local copies, waits for them, and re-layouts  13.8 us
    ppermute x15, starting transfers between devices, ring_reduce_scatter(): received = lax.ppermute(acc, axis, perm)  13.8 us
    ppermute x4, waiting for transfers between devices, ring_scatter_back(): received = lax.ppermute(acc, 'seq', backward).astype(jnp.float32)  8.98 us
    ppermute x2, starting transfers between devices, extended(): before = lax.ppermute(last, axis, up)  8.57 us
    ppermute x3, waiting for transfers between devices, ring_scatter_back(): received = lax.ppermute(acc, 'seq', forward).astype(jnp.float32)  8.1 us
    ppermute x4, starting transfers between devices, ring_gather(): current = lax.ppermute(current, 'seq', forward)  7.61 us
  transfers between devices with their start and end apart: 33, of which 25 were waited for; matrix products, arithmetic and copies ran while one was open for 9% of the time, Pallas kernels for 0%

profile of v1, /device:TPU:0, one launch (start us, length us, event | category | flops | bytes accessed | tf_op | source)
XLA Modules:
  0.0 247.4 jit_solution(11014969972983245708)
XLA Ops:
  3.9 3.1 %collective-permute-start = (bf16[128,1280]{0,1:T(8,128)(2,1)}, bf16[128,1280]{0,1:T(8,128)(2,1)S(1)}, u32[]{:S(2)}, u32[]{:S(2)}) collective-permute-start(bf16[128,1280]{0,1:T(8,128)(2,1)} %get-tuple-element.35), channel_id=1, source_target_pairs={{0,4},{4,8},{8,12},{12,14},{14,10},{10,6},{6,2},{2,0},{1,5},{5,9},... | collective-permute-start | bytes 983048 | tf_op jit(solution)/shard_map/ppermute | solution.py:75
  6.9 7.9 %collective-permute-done = bf16[128,1280]{0,1:T(8,128)(2,1)S(1)} collective-permute-done((bf16[128,1280]{0,1:T(8,128)(2,1)}, bf16[128,1280]{0,1:T(8,128)(2,1)S(1)}, u32[]{:S(2)}, u32[]{:S(2)}) %collective-permute-start) | collective-permute-done | bytes 327712 | tf_op jit(solution)/shard_map/ppermute | solution.py:75
  15.5 1.8 collective-permute-start.1
  17.5 7.0 %collective-permute-done.1 = bf16[128,1280]{0,1:T(8,128)(2,1)} collective-permute-done((bf16[128,1280]{0,1:T(8,128)(2,1)S(1)}, bf16[128,1280]{0,1:T(8,128)(2,1)}, u32[]{:S(2)}, u32[]{:S(2)}) %collective-permute-start.1) | collective-permute-done | bytes 327712 | tf_op jit(solution)/shard_map/ppermute | solution.py:75
  24.5 1.5 collective-permute-start.2
  28.3 1.8 constant_dynamic-update-slice_fusion.6
  30.1 2.8 %collective-permute-done.2 = bf16[128,1280]{0,1:T(8,128)(2,1)} collective-permute-done((bf16[128,1280]{0,1:T(8,128)(2,1)}, bf16[128,1280]{0,1:T(8,128)(2,1)}, u32[]{:S(2)}, u32[]{:S(2)}) %collective-permute-start.2) | collective-permute-done | bytes 327712 | tf_op jit(solution)/shard_map/ppermute | solution.py:75
  34.1 1.7 constant_dynamic-update-slice_fusion.5
  36.6 1.7 constant_dynamic-update-slice_fusion.4
  38.3 1.8 collective-permute-done.3
  43.7 1.5 slice.114
  45.3 1.9 slice.115
  52.2 2.6 %broadcast_in_dim.26 = f32[1,256,768]{2,1,0:T(8,128)} reshape(f32[128,2,768]{2,1,0:T(2,128)} %broadcast_in_dim.12) | data formatting | bytes 1572864 | tf_op jit(solution)/shard_map/broadcast_in_dim | solution.py:159
  54.7 2.6 %reshape.124 = f32[256,768]{1,0:T(8,128)} reshape(f32[128,2,768]{2,1,0:T(2,128)} %broadcast_in_dim.12) | data formatting | bytes 1572864 | tf_op jit(solution)/shard_map/reshape | solution.py:159
  60.5 2.8 %collective-permute-start.7 = (bf16[2,768]{1,0:T(2,128)(2,1)S(1)}, bf16[2,768]{1,0:T(2,128)(2,1)S(1)}, u32[]{:S(2)}, u32[]{:S(2)}) collective-permute-start(bf16[2,768]{1,0:T(2,128)(2,1)S(1)} %get-tuple-element.34), channel_id=1, source_target_pairs={{0,2},{2,4},{4,6},{6,8},{8,10},{10,12},{12,14},{1,3},{3,5},{5,7},{... | collective-permute-start | bytes 9224 | tf_op jit(solution)/shard_map/ppermute | solution.py:24
  64.9 4.2 %collective-permute-done.8 = bf16[2,768]{1,0:T(2,128)(2,1)S(1)} collective-permute-done((bf16[2,768]{1,0:T(2,128)(2,1)S(1)}, bf16[2,768]{1,0:T(2,128)(2,1)S(1)}, u32[]{:S(2)}, u32[]{:S(2)}) %collective-permute-start.8) | collective-permute-done | bytes 3104 | tf_op jit(solution)/shard_map/ppermute | solution.py:25
  69.3 2.0 fusion.20
  73.2 5.7 %collective-permute-start.10 = (bf16[2,384]{1,0:T(2,128)(2,1)}, bf16[2,384]{1,0:T(2,128)(2,1)S(1)}, u32[]{:S(2)}, u32[]{:S(2)}) collective-permute-start(bf16[2,384]{1,0:T(2,128)(2,1)} %get-tuple-element.37), channel_id=1, source_target_pairs={{0,2},{2,4},{4,6},{6,8},{8,10},{10,12},{12,14},{1,3},{3,5},{5,7},{... | collective-permute-start | bytes 4616 | tf_op jit(solution)/shard_map/ppermute | solution.py:24
  82.8 2.5 %reshape.126 = f32[128,2,768]{2,1,0:T(2,128)} reshape(f32[256,768]{1,0:T(8,128)} %get-tuple-element.22) | data formatting | bytes 1572864 | tf_op jit(solution)/shard_map/reshape | solution.py:206
  85.4 2.8 %reduce_sum.48 = bf16[128,768]{1,0:T(8,128)(2,1)} reduce(f32[128,2,768]{2,1,0:T(2,128)} %reshape.126, f32[]{:T(128)} %constant.210.clone.1), dimensions={1}, to_apply=%region_4.5 | reduce | flops 98304 | bytes 983044 | tf_op jit(solution)/shard_map/reduce_sum | solution.py:206
  88.1 1.7 copy.41
  91.0 3.5 %convolution_convert_fusion = bf16[4,192,1024]{2,1,0:T(8,128)(2,1)} fusion(bf16[128,4,192]{0,2,1:T(8,128)(2,1)} %bitcast.176, f32[4,1024,128]{2,1,0:T(8,128)} %copy-done.2, f32[4,128]{1,0:T(4,128)S(1)} %log_add_fusion), kind=kOutput, calls=%fused_computation.26 | convolution fusion | flops 203685888 | bytes 3868672 | tf_op jit(solution)/shard_map/hij,ihd->jhd/dot_general | solution.py:221
  94.6 2.1 multiply_convert_fusion.1
  96.7 2.6 %copy.50 = bf16[1024,768]{1,0:T(8,128)(2,1)} copy(bf16[1024,768]{0,1:T(8,128)(2,1)} %bitcast.172) | data formatting | bytes 3145728 | tf_op jit(solution)/shard_map/reshape | solution.py:225
  99.3 2.6 %fusion.4 = bf16[1024,4,128]{2,0,1:T(8,128)(2,1)} fusion(bf16[4,128,1024]{1,2,0:T(8,128)(2,1)} %multiply_convert_fusion.1, bf16[128,4,128]{0,2,1:T(8,128)(2,1)S(1)} %bitcast.179), kind=kOutput, calls=%fused_computation.27 | convolution fusion | flops 135266304 | bytes 2228224 | tf_op jit(solution)/shard_map/hij,ihd->jhd/dot_general | solution.py:218
  102.0 2.3 copy.47
  104.2 2.3 copy.49
  107.9 3.0 %collective-permute-start.11 = (bf16[128,1280]{1,0:T(8,128)(2,1)S(1)}, bf16[128,1280]{1,0:T(8,128)(2,1)S(1)}, u32[]{:S(2)}, u32[]{:S(2)}) collective-permute-start(bf16[128,1280]{1,0:T(8,128)(2,1)S(1)} %get-tuple-element.29), channel_id=1, source_target_pairs={{0,2},{4,0},{8,4},{12,8},{14,12},{10,14},{6,10},{2,6},{1,3},{5,1},... | collective-permute-start | bytes 983048 | tf_op jit(solution)/shard_map/ppermute | solution.py:96
  112.1 1.8 dynamic-slice_bitcast_fusion
  113.8 2.0 copy-done.5
  115.9 2.2 collective-permute-start.15
  118.2 7.8 %collective-permute-done.15 = bf16[128,1280]{1,0:T(8,128)(2,1)S(1)} collective-permute-done((bf16[128,1280]{1,0:T(8,128)(2,1)S(1)}, bf16[128,1280]{1,0:T(8,128)(2,1)S(1)}, u32[]{:S(2)}, u32[]{:S(2)}) %collective-permute-start.15) | collective-permute-done | bytes 327712 | tf_op jit(solution)/shard_map/ppermute | solution.py:104
  126.0 2.0 collective-permute-done.12
  128.5 1.7 collective-permute-start.16
  130.3 7.0 %collective-permute-done.13 = bf16[128,1280]{1,0:T(8,128)(2,1)S(1)} collective-permute-done((bf16[128,1280]{1,0:T(8,128)(2,1)S(1)}, bf16[128,1280]{1,0:T(8,128)(2,1)S(1)}, u32[]{:S(2)}, u32[]{:S(2)}) %collective-permute-start.13) | collective-permute-done | bytes 327712 | tf_op jit(solution)/shard_map/ppermute | solution.py:96
  138.5 1.5 collective-permute-start.17
  184.0 2.0 fusion.7
  188.7 3.0 %bitcast_add_fusion = f32[8,240,384]{2,1,0:T(8,128)S(1)} fusion(f32[8,240,384]{2,1,0:T(8,128)} %collective-permute-done.18, f32[8,2,240,384]{3,2,1,0:T(8,128)} %bitcast.167, s32[]{:T(128)S(6)} %select_n.198), kind=kLoop, calls=%fused_computation.15 | loop fusion | flops 737280 | bytes 8847364 | tf_op jit(solution)/shard_map/add | solution.py:130
  195.2 3.9 %collective-permute-done.26 = f32[240,192]{1,0:T(8,128)S(1)} collective-permute-done((f32[240,192]{1,0:T(8,128)S(1)}, f32[240,192]{1,0:T(8,128)S(1)}, u32[]{:S(2)}, u32[]{:S(2)}) %collective-permute-start.26) | collective-permute-done | bytes 184352 | tf_op jit(solution)/shard_map/ppermute | solution.py:129
  202.0 5.1 %collective-permute-done.27 = f32[240,192]{1,0:T(8,128)S(1)} collective-permute-done((f32[240,192]{1,0:T(8,128)S(1)}, f32[240,192]{1,0:T(8,128)S(1)}, u32[]{:S(2)}, u32[]{:S(2)}) %collective-permute-start.27) | collective-permute-done | bytes 184352 | tf_op jit(solution)/shard_map/ppermute | solution.py:129
  208.3 1.6 collective-permute-start.21
  209.9 6.0 %collective-permute-done.28 = f32[240,192]{1,0:T(8,128)S(1)} collective-permute-done((f32[240,192]{1,0:T(8,128)S(1)}, f32[240,192]{1,0:T(8,128)S(1)}, u32[]{:S(2)}, u32[]{:S(2)}) %collective-permute-start.28) | collective-permute-done | bytes 184352 | tf_op jit(solution)/shard_map/ppermute | solution.py:129
  216.5 2.2 collective-permute-start.22
  218.7 5.4 %collective-permute-done.29 = f32[240,192]{1,0:T(8,128)S(1)} collective-permute-done((f32[240,192]{1,0:T(8,128)S(1)}, f32[240,192]{1,0:T(8,128)S(1)}, u32[]{:S(2)}, u32[]{:S(2)}) %collective-permute-start.29) | collective-permute-done | bytes 184352 | tf_op jit(solution)/shard_map/ppermute | solution.py:129
  226.6 4.8 %collective-permute-done.30 = f32[240,192]{1,0:T(8,128)S(1)} collective-permute-done((f32[240,192]{1,0:T(8,128)S(1)}, f32[240,192]{1,0:T(8,128)S(1)}, u32[]{:S(2)}, u32[]{:S(2)}) %collective-permute-start.30) | collective-permute-done | bytes 184352 | tf_op jit(solution)/shard_map/ppermute | solution.py:129
  233.6 4.3 %collective-permute-done.31 = f32[240,192]{1,0:T(8,128)S(1)} collective-permute-done((f32[240,192]{1,0:T(8,128)S(1)}, f32[240,192]{1,0:T(8,128)S(1)}, u32[]{:S(2)}, u32[]{:S(2)}) %collective-permute-start.31) | collective-permute-done | bytes 184352 | tf_op jit(solution)/shard_map/ppermute | solution.py:129
  240.5 3.7 %collective-permute-done.32 = f32[240,192]{1,0:T(8,128)S(1)} collective-permute-done((f32[240,192]{1,0:T(8,128)S(1)}, f32[240,192]{1,0:T(8,128)S(1)}, u32[]{:S(2)}, u32[]{:S(2)}) %collective-permute-start.32) | collective-permute-done | bytes 184352 | tf_op jit(solution)/shard_map/ppermute | solution.py:129
  244.2 2.3 collective-permute-done.25
  (150 shorter events, 54.1 us)
Async XLA Ops:
  0.6 68.6 %copy-start = (bf16[3840,384]{1,0:T(8,128)(2,1)S(1)}, bf16[3840,384]{1,0:T(8,128)(2,1)}, u32[]{:S(2)}) copy-start(bf16[3840,384]{1,0:T(8,128)(2,1)} %param.20) | copy-start | bytes 8847364
  3.9 10.9 %collective-permute-start = (bf16[128,1280]{0,1:T(8,128)(2,1)}, bf16[128,1280]{0,1:T(8,128)(2,1)S(1)}, u32[]{:S(2)}, u32[]{:S(2)}) collective-permute-start(bf16[128,1280]{0,1:T(8,128)(2,1)} %get-tuple-element.35), channel_id=1, source_target_pairs={{0,4},{4,8},{8,12},{12,14},{14,10},{10,6},{6,2},{2,0},{1,5},{5,9},... | collective-permute-start | bytes 983048 | tf_op jit(solution)/shard_map/ppermute | solution.py:75
  15.5 9.0 %collective-permute-start.1 = (bf16[128,1280]{0,1:T(8,128)(2,1)S(1)}, bf16[128,1280]{0,1:T(8,128)(2,1)}, u32[]{:S(2)}, u32[]{:S(2)}) collective-permute-start(bf16[128,1280]{0,1:T(8,128)(2,1)S(1)} %collective-permute-done), channel_id=1, source_target_pairs={{0,4},{4,8},{8,12},{12,14},{14,10},{10,6},{6,2},{2,0},{1,5},{5,9},... | collective-permute-start | bytes 983048 | tf_op jit(solution)/shard_map/ppermute | solution.py:75
  17.3 10.4 %collective-permute-start.4 = (bf16[128,1280]{0,1:T(8,128)(2,1)}, bf16[128,1280]{0,1:T(8,128)(2,1)S(1)}, u32[]{:S(2)}, u32[]{:S(2)}) collective-permute-start(bf16[128,1280]{0,1:T(8,128)(2,1)} %get-tuple-element.35), channel_id=1, source_target_pairs={{0,2},{4,0},{8,4},{12,8},{14,12},{10,14},{6,10},{2,6},{1,3},{5,1},... | collective-permute-start | bytes 983048 | tf_op jit(solution)/shard_map/ppermute | solution.py:79
  24.5 8.3 %collective-permute-start.2 = (bf16[128,1280]{0,1:T(8,128)(2,1)}, bf16[128,1280]{0,1:T(8,128)(2,1)}, u32[]{:S(2)}, u32[]{:S(2)}) collective-permute-start(bf16[128,1280]{0,1:T(8,128)(2,1)} %collective-permute-done.1), channel_id=1, source_target_pairs={{0,4},{4,8},{8,12},{12,14},{14,10},{10,6},{6,2},{2,0},{1,5},{5,9},... | collective-permute-start | bytes 983048 | tf_op jit(solution)/shard_map/ppermute | solution.py:75
  27.7 19.4 %copy-start.16 = (bf16[1,128,512]{1,2,0:T(8,128)(2,1)}, bf16[1,128,512]{1,2,0:T(8,128)(2,1)S(1)}, u32[]{:S(2)}) copy-start(bf16[1,128,512]{1,2,0:T(8,128)(2,1)S(1)} %copy.59) | copy-start | bytes 393220
  27.7 8.1 %collective-permute-start.5 = (bf16[128,1280]{0,1:T(8,128)(2,1)S(1)}, bf16[128,1280]{0,1:T(8,128)(2,1)S(1)}, u32[]{:S(2)}, u32[]{:S(2)}) collective-permute-start(bf16[128,1280]{0,1:T(8,128)(2,1)S(1)} %collective-permute-done.4), channel_id=1, source_target_pairs={{0,2},{4,0},{8,4},{12,8},{14,12},{10,14},{6,10},{2,6},{1,3},{5,1},... | collective-permute-start | bytes 983048 | tf_op jit(solution)/shard_map/ppermute | solution.py:79
  32.8 7.4 %collective-permute-start.3 = (bf16[128,1280]{0,1:T(8,128)(2,1)}, bf16[128,1280]{0,1:T(8,128)(2,1)S(1)}, u32[]{:S(2)}, u32[]{:S(2)}) collective-permute-start(bf16[128,1280]{0,1:T(8,128)(2,1)} %collective-permute-done.2), channel_id=1, source_target_pairs={{0,4},{4,8},{8,12},{12,14},{14,10},{10,6},{6,2},{2,0},{1,5},{5,9},... | collective-permute-start | bytes 983048 | tf_op jit(solution)/shard_map/ppermute | solution.py:75
  35.8 7.1 %collective-permute-start.6 = (bf16[128,1280]{0,1:T(8,128)(2,1)S(1)}, bf16[128,1280]{0,1:T(8,128)(2,1)S(1)}, u32[]{:S(2)}, u32[]{:S(2)}) collective-permute-start(bf16[128,1280]{0,1:T(8,128)(2,1)S(1)} %collective-permute-done.5), channel_id=1, source_target_pairs={{0,2},{4,0},{8,4},{12,8},{14,12},{10,14},{6,10},{2,6},{1,3},{5,1},... | collective-permute-start | bytes 983048 | tf_op jit(solution)/shard_map/ppermute | solution.py:79
  51.0 6.3 %copy-start.10 = (bf16[1,256,768]{2,1,0:T(8,128)(2,1)S(1)}, bf16[1,256,768]{2,1,0:T(8,128)(2,1)}, u32[]{:S(2)}) copy-start(bf16[1,256,768]{2,1,0:T(8,128)(2,1)} %param.18) | copy-start | bytes 1179652
  60.5 8.8 %copy-start.22 = (bf16[1,256,384]{2,1,0:T(8,128)(2,1)S(1)}, bf16[1,256,384]{2,1,0:T(8,128)(2,1)}, u32[]{:S(2)}) copy-start(bf16[1,256,384]{2,1,0:T(8,128)(2,1)} %param.21) | copy-start | bytes 589828
  60.5 4.1 %collective-permute-start.7 = (bf16[2,768]{1,0:T(2,128)(2,1)S(1)}, bf16[2,768]{1,0:T(2,128)(2,1)S(1)}, u32[]{:S(2)}, u32[]{:S(2)}) collective-permute-start(bf16[2,768]{1,0:T(2,128)(2,1)S(1)} %get-tuple-element.34), channel_id=1, source_target_pairs={{0,2},{2,4},{4,6},{6,8},{8,10},{10,12},{12,14},{1,3},{3,5},{5,7},{... | collective-permute-start | bytes 9224 | tf_op jit(solution)/shard_map/ppermute | solution.py:24
  63.3 5.7 %collective-permute-start.8 = (bf16[2,768]{1,0:T(2,128)(2,1)S(1)}, bf16[2,768]{1,0:T(2,128)(2,1)S(1)}, u32[]{:S(2)}, u32[]{:S(2)}) collective-permute-start(bf16[2,768]{1,0:T(2,128)(2,1)S(1)} %get-tuple-element.33), channel_id=1, source_target_pairs={{2,0},{4,2},{6,4},{8,6},{10,8},{12,10},{14,12},{3,1},{5,3},{7,5},{... | collective-permute-start | bytes 9224 | tf_op jit(solution)/shard_map/ppermute | solution.py:25
  71.9 7.1 %collective-permute-start.9 = (bf16[2,384]{1,0:T(2,128)(2,1)}, bf16[2,384]{1,0:T(2,128)(2,1)S(1)}, u32[]{:S(2)}, u32[]{:S(2)}) collective-permute-start(bf16[2,384]{1,0:T(2,128)(2,1)} %get-tuple-element.38), channel_id=1, source_target_pairs={{2,0},{4,2},{6,4},{8,6},{10,8},{12,10},{14,12},{3,1},{5,3},{7,5},{... | collective-permute-start | bytes 4616 | tf_op jit(solution)/shard_map/ppermute | solution.py:25
  73.2 7.2 %copy-start.8 = (f32[256,768]{1,0:T(8,128)S(1)}, f32[256,768]{1,0:T(8,128)}, u32[]{:S(2)}) copy-start(f32[256,768]{1,0:T(8,128)} %reshape.124) | copy-start | bytes 2359300
  73.2 7.1 %collective-permute-start.10 = (bf16[2,384]{1,0:T(2,128)(2,1)}, bf16[2,384]{1,0:T(2,128)(2,1)S(1)}, u32[]{:S(2)}, u32[]{:S(2)}) collective-permute-start(bf16[2,384]{1,0:T(2,128)(2,1)} %get-tuple-element.37), channel_id=1, source_target_pairs={{0,2},{2,4},{4,6},{6,8},{8,10},{10,12},{12,14},{1,3},{3,5},{5,7},{... | collective-permute-start | bytes 4616 | tf_op jit(solution)/shard_map/ppermute | solution.py:24
  82.8 7.0 %copy-start.14 = (f32[4,192,128]{2,1,0:T(8,128)S(1)}, f32[4,192,128]{2,1,0:T(8,128)}, u32[]{:S(2)}) copy-start(f32[4,192,128]{2,1,0:T(8,128)} %copy-done.13) | copy-start | bytes 1179652
  89.9 4.7 %copy-start.3 = (f32[4,1024,128]{2,1,0:T(8,128)S(1)}, f32[4,1024,128]{2,1,0:T(8,128)}, u32[]{:S(2)}) copy-start(f32[4,1024,128]{2,1,0:T(8,128)} %copy-done.2) | copy-start | bytes 6291460
  89.9 4.7 %copy-start.7 = (bf16[1024,768]{0,1:T(8,128)(2,1)S(1)}, bf16[1024,768]{0,1:T(8,128)(2,1)}, u32[]{:S(2)}) copy-start(bf16[1024,768]{0,1:T(8,128)(2,1)} %copy-done.6) | copy-start | bytes 4718596
  89.9 4.7 %copy-start.15 = (bf16[128,768]{0,1:T(8,128)(2,1)S(1)}, bf16[128,768]{0,1:T(8,128)(2,1)}, u32[]{:S(2)}) copy-start(bf16[128,768]{0,1:T(8,128)(2,1)} %copy.41) | copy-start | bytes 589828
  106.5 4.3 %copy-start.12 = (bf16[256,3840]{1,0:T(8,128)(2,1)S(1)}, bf16[256,3840]{1,0:T(8,128)(2,1)}, u32[]{:S(2)}) copy-start(bf16[256,3840]{1,0:T(8,128)(2,1)} %copy-done.11) | copy-start | bytes 5898244
  107.9 10.1 %collective-permute-start.11 = (bf16[128,1280]{1,0:T(8,128)(2,1)S(1)}, bf16[128,1280]{1,0:T(8,128)(2,1)S(1)}, u32[]{:S(2)}, u32[]{:S(2)}) collective-permute-start(bf16[128,1280]{1,0:T(8,128)(2,1)S(1)} %get-tuple-element.29), channel_id=1, source_target_pairs={{0,2},{4,0},{8,4},{12,8},{14,12},{10,14},{6,10},{2,6},{1,3},{5,1},... | collective-permute-start | bytes 983048 | tf_op jit(solution)/shard_map/ppermute | solution.py:96
  112.0 3.8 %copy-start.5 = (f32[3840,384]{1,0:T(8,128)}, f32[3840,384]{1,0:T(8,128)S(1)}, u32[]{:S(2)}) copy-start(f32[3840,384]{1,0:T(8,128)S(1)} %convolution_multiply_fusion) | copy-start | bytes 17694724
  112.1 6.0 %copy-start.1 = (bf16[1024,768]{1,0:T(8,128)(2,1)S(1)}, bf16[1024,768]{1,0:T(8,128)(2,1)}, u32[]{:S(2)}) copy-start(bf16[1024,768]{1,0:T(8,128)(2,1)} %copy.50) | copy-start | bytes 4718596
  112.1 5.9 %copy-start.4 = (bf16[1024,512]{1,0:T(8,128)(2,1)S(1)}, bf16[1024,512]{1,0:T(8,128)(2,1)}, u32[]{:S(2)}) copy-start(bf16[1024,512]{1,0:T(8,128)(2,1)} %copy.49) | copy-start | bytes 3145732
  115.8 72.8 %collective-permute-start.18 = (f32[8,240,384]{2,1,0:T(8,128)}, f32[8,240,384]{2,1,0:T(8,128)}, u32[]{:S(2)}, u32[]{:S(2)}) collective-permute-start(f32[8,240,384]{2,1,0:T(8,128)} %dynamic-slice_bitcast_fusion), channel_id=1, source_target_pairs={{0,1},{1,0},{2,3},{3,2},{4,5},{5,4},{6,7},{7,6},{8,9},{9,8},{10,11... | collective-permute-start | bytes 8847368 | tf_op jit(solution)/shard_map/ppermute | solution.py:129
  115.9 10.1 %collective-permute-start.15 = (bf16[128,1280]{1,0:T(8,128)(2,1)S(1)}, bf16[128,1280]{1,0:T(8,128)(2,1)S(1)}, u32[]{:S(2)}, u32[]{:S(2)}) collective-permute-start(bf16[128,1280]{1,0:T(8,128)(2,1)S(1)} %get-tuple-element.30), channel_id=1, source_target_pairs={{0,4},{4,8},{8,12},{12,14},{14,10},{10,6},{6,2},{2,0},{1,5},{5,9},... | collective-permute-start | bytes 983048 | tf_op jit(solution)/shard_map/ppermute | solution.py:104
  118.1 9.9 %collective-permute-start.12 = (bf16[128,1280]{1,0:T(8,128)(2,1)S(1)}, bf16[128,1280]{1,0:T(8,128)(2,1)S(1)}, u32[]{:S(2)}, u32[]{:S(2)}) collective-permute-start(bf16[128,1280]{1,0:T(8,128)(2,1)S(1)} %add_convert_fusion.5), channel_id=1, source_target_pairs={{0,2},{4,0},{8,4},{12,8},{14,12},{10,14},{6,10},{2,6},{1,3},{5,1},... | collective-permute-start | bytes 983048 | tf_op jit(solution)/shard_map/ppermute | solution.py:96
  128.2 12.4 %copy-start.23 = (s32[8]{0:T(128)S(1)}, s32[8]{0:T(128)}, u32[]{:S(2)}) copy-start(s32[8]{0:T(128)} %constant.239.clone) | copy-start | bytes 100
  128.2 9.0 %collective-permute-start.13 = (bf16[128,1280]{1,0:T(8,128)(2,1)S(1)}, bf16[128,1280]{1,0:T(8,128)(2,1)S(1)}, u32[]{:S(2)}, u32[]{:S(2)}) collective-permute-start(bf16[128,1280]{1,0:T(8,128)(2,1)S(1)} %get-tuple-element.27), channel_id=1, source_target_pairs={{0,2},{4,0},{8,4},{12,8},{14,12},{10,14},{6,10},{2,6},{1,3},{5,1},... | collective-permute-start | bytes 983048 | tf_op jit(solution)/shard_map/ppermute | solution.py:96
  128.5 24.6 %copy-start.20 = (s32[8]{0:T(128)S(1)}, s32[8]{0:T(128)}, u32[]{:S(2)}) copy-start(s32[8]{0:T(128)} %constant.238.clone) | copy-start | bytes 100
  128.5 9.0 %collective-permute-start.16 = (bf16[128,1280]{1,0:T(8,128)(2,1)S(1)}, bf16[128,1280]{1,0:T(8,128)(2,1)S(1)}, u32[]{:S(2)}, u32[]{:S(2)}) collective-permute-start(bf16[128,1280]{1,0:T(8,128)(2,1)S(1)} %get-tuple-element.28), channel_id=1, source_target_pairs={{0,4},{4,8},{8,12},{12,14},{14,10},{10,6},{6,2},{2,0},{1,5},{5,9},... | collective-permute-start | bytes 983048 | tf_op jit(solution)/shard_map/ppermute | solution.py:104
  138.5 48.2 %collective-permute-start.17 = (bf16[128,1280]{1,0:T(8,128)(2,1)}, bf16[128,1280]{1,0:T(8,128)(2,1)S(1)}, u32[]{:S(2)}, u32[]{:S(2)}) collective-permute-start(bf16[128,1280]{1,0:T(8,128)(2,1)} %get-tuple-element.26), channel_id=1, source_target_pairs={{0,4},{4,8},{8,12},{12,14},{14,10},{10,6},{6,2},{2,0},{1,5},{5,9},... | collective-permute-start | bytes 983048 | tf_op jit(solution)/shard_map/ppermute | solution.py:104
  140.0 46.8 %collective-permute-start.14 = (bf16[128,1280]{1,0:T(8,128)(2,1)}, bf16[128,1280]{1,0:T(8,128)(2,1)}, u32[]{:S(2)}, u32[]{:S(2)}) collective-permute-start(bf16[128,1280]{1,0:T(8,128)(2,1)} %get-tuple-element.25), channel_id=1, source_target_pairs={{0,2},{4,0},{8,4},{12,8},{14,12},{10,14},{6,10},{2,6},{1,3},{5,1},... | collective-permute-start | bytes 983048 | tf_op jit(solution)/shard_map/ppermute | solution.py:96
  192.4 6.8 %collective-permute-start.26 = (f32[240,192]{1,0:T(8,128)S(1)}, f32[240,192]{1,0:T(8,128)S(1)}, u32[]{:S(2)}, u32[]{:S(2)}) collective-permute-start(f32[240,192]{1,0:T(8,128)S(1)} %dynamic-slice_bitcast_fusion.1), channel_id=1, source_target_pairs={{0,2},{4,0},{8,4},{12,8},{14,12},{10,14},{6,10},{2,6},{1,3},{5,1},... | collective-permute-start | bytes 552968 | tf_op jit(solution)/shard_map/ppermute | solution.py:129
  194.5 6.5 %collective-permute-start.19 = (f32[240,192]{1,0:T(8,128)S(1)}, f32[240,192]{1,0:T(8,128)S(1)}, u32[]{:S(2)}, u32[]{:S(2)}) collective-permute-start(f32[240,192]{1,0:T(8,128)S(1)} %dynamic-slice_bitcast_fusion.2), channel_id=1, source_target_pairs={{0,4},{4,8},{8,12},{12,14},{14,10},{10,6},{6,2},{2,0},{1,5},{5,9},... | collective-permute-start | bytes 552968 | tf_op jit(solution)/shard_map/ppermute | solution.py:129
  199.2 7.9 %collective-permute-start.27 = (f32[240,192]{1,0:T(8,128)S(1)}, f32[240,192]{1,0:T(8,128)S(1)}, u32[]{:S(2)}, u32[]{:S(2)}) collective-permute-start(f32[240,192]{1,0:T(8,128)S(1)} %bitcast_add_fusion.7), channel_id=1, source_target_pairs={{0,2},{4,0},{8,4},{12,8},{14,12},{10,14},{6,10},{2,6},{1,3},{5,1},... | collective-permute-start | bytes 552968 | tf_op jit(solution)/shard_map/ppermute | solution.py:129
  201.0 7.3 %collective-permute-start.20 = (f32[240,192]{1,0:T(8,128)S(1)}, f32[240,192]{1,0:T(8,128)S(1)}, u32[]{:S(2)}, u32[]{:S(2)}) collective-permute-start(f32[240,192]{1,0:T(8,128)S(1)} %bitcast_add_fusion.14), channel_id=1, source_target_pairs={{0,4},{4,8},{8,12},{12,14},{14,10},{10,6},{6,2},{2,0},{1,5},{5,9},... | collective-permute-start | bytes 552968 | tf_op jit(solution)/shard_map/ppermute | solution.py:129
  207.1 8.8 %collective-permute-start.28 = (f32[240,192]{1,0:T(8,128)S(1)}, f32[240,192]{1,0:T(8,128)S(1)}, u32[]{:S(2)}, u32[]{:S(2)}) collective-permute-start(f32[240,192]{1,0:T(8,128)S(1)} %bitcast_add_fusion.6), channel_id=1, source_target_pairs={{0,2},{4,0},{8,4},{12,8},{14,12},{10,14},{6,10},{2,6},{1,3},{5,1},... | collective-permute-start | bytes 552968 | tf_op jit(solution)/shard_map/ppermute | solution.py:129
  208.3 8.2 %collective-permute-start.21 = (f32[240,192]{1,0:T(8,128)S(1)}, f32[240,192]{1,0:T(8,128)S(1)}, u32[]{:S(2)}, u32[]{:S(2)}) collective-permute-start(f32[240,192]{1,0:T(8,128)S(1)} %bitcast_add_fusion.13), channel_id=1, source_target_pairs={{0,4},{4,8},{8,12},{12,14},{14,10},{10,6},{6,2},{2,0},{1,5},{5,9},... | collective-permute-start | bytes 552968 | tf_op jit(solution)/shard_map/ppermute | solution.py:129
  215.9 8.2 %collective-permute-start.29 = (f32[240,192]{1,0:T(8,128)S(1)}, f32[240,192]{1,0:T(8,128)S(1)}, u32[]{:S(2)}, u32[]{:S(2)}) collective-permute-start(f32[240,192]{1,0:T(8,128)S(1)} %bitcast_add_fusion.5), channel_id=1, source_target_pairs={{0,2},{4,0},{8,4},{12,8},{14,12},{10,14},{6,10},{2,6},{1,3},{5,1},... | collective-permute-start | bytes 552968 | tf_op jit(solution)/shard_map/ppermute | solution.py:129
  216.5 8.6 %collective-permute-start.22 = (f32[240,192]{1,0:T(8,128)S(1)}, f32[240,192]{1,0:T(8,128)S(1)}, u32[]{:S(2)}, u32[]{:S(2)}) collective-permute-start(f32[240,192]{1,0:T(8,128)S(1)} %bitcast_add_fusion.12), channel_id=1, source_target_pairs={{0,4},{4,8},{8,12},{12,14},{14,10},{10,6},{6,2},{2,0},{1,5},{5,9},... | collective-permute-start | bytes 552968 | tf_op jit(solution)/shard_map/ppermute | solution.py:129
  224.1 7.3 %collective-permute-start.30 = (f32[240,192]{1,0:T(8,128)S(1)}, f32[240,192]{1,0:T(8,128)S(1)}, u32[]{:S(2)}, u32[]{:S(2)}) collective-permute-start(f32[240,192]{1,0:T(8,128)S(1)} %bitcast_add_fusion.4), channel_id=1, source_target_pairs={{0,2},{4,0},{8,4},{12,8},{14,12},{10,14},{6,10},{2,6},{1,3},{5,1},... | collective-permute-start | bytes 552968 | tf_op jit(solution)/shard_map/ppermute | solution.py:129
  225.2 7.9 %collective-permute-start.23 = (f32[240,192]{1,0:T(8,128)S(1)}, f32[240,192]{1,0:T(8,128)S(1)}, u32[]{:S(2)}, u32[]{:S(2)}) collective-permute-start(f32[240,192]{1,0:T(8,128)S(1)} %bitcast_add_fusion.11), channel_id=1, source_target_pairs={{0,4},{4,8},{8,12},{12,14},{14,10},{10,6},{6,2},{2,0},{1,5},{5,9},... | collective-permute-start | bytes 552968 | tf_op jit(solution)/shard_map/ppermute | solution.py:129
  231.5 6.4 %collective-permute-start.31 = (f32[240,192]{1,0:T(8,128)S(1)}, f32[240,192]{1,0:T(8,128)S(1)}, u32[]{:S(2)}, u32[]{:S(2)}) collective-permute-start(f32[240,192]{1,0:T(8,128)S(1)} %bitcast_add_fusion.3), channel_id=1, source_target_pairs={{0,2},{4,0},{8,4},{12,8},{14,12},{10,14},{6,10},{2,6},{1,3},{5,1},... | collective-permute-start | bytes 552968 | tf_op jit(solution)/shard_map/ppermute | solution.py:129
  233.1 7.2 %collective-permute-start.24 = (f32[240,192]{1,0:T(8,128)S(1)}, f32[240,192]{1,0:T(8,128)S(1)}, u32[]{:S(2)}, u32[]{:S(2)}) collective-permute-start(f32[240,192]{1,0:T(8,128)S(1)} %bitcast_add_fusion.10), channel_id=1, source_target_pairs={{0,4},{4,8},{8,12},{12,14},{14,10},{10,6},{6,2},{2,0},{1,5},{5,9},... | collective-permute-start | bytes 552968 | tf_op jit(solution)/shard_map/ppermute | solution.py:129
  237.9 6.2 %collective-permute-start.32 = (f32[240,192]{1,0:T(8,128)S(1)}, f32[240,192]{1,0:T(8,128)S(1)}, u32[]{:S(2)}, u32[]{:S(2)}) collective-permute-start(f32[240,192]{1,0:T(8,128)S(1)} %bitcast_add_fusion.2), channel_id=1, source_target_pairs={{0,2},{4,0},{8,4},{12,8},{14,12},{10,14},{6,10},{2,6},{1,3},{5,1},... | collective-permute-start | bytes 552968 | tf_op jit(solution)/shard_map/ppermute | solution.py:129
  240.3 6.2 %collective-permute-start.25 = (f32[240,192]{1,0:T(8,128)S(1)}, f32[240,192]{1,0:T(8,128)S(1)}, u32[]{:S(2)}, u32[]{:S(2)}) collective-permute-start(f32[240,192]{1,0:T(8,128)S(1)} %bitcast_add_fusion.9), channel_id=1, source_target_pairs={{0,4},{4,8},{8,12},{12,14},{14,10},{10,6},{6,2},{2,0},{1,5},{5,9},... | collective-permute-start | bytes 552968 | tf_op jit(solution)/shard_map/ppermute | solution.py:129
  (9 other events, 14.5 us)

commit v2 on v1

--- a/solution.py
+++ b/solution.py
@@ -168,17 +168,36 @@
     grad_pre = (cotangent[0].astype(jnp.float32) * derivative).astype(jnp.bfloat16)
     grad_padded = extended(grad_pre, (("seq", 0),), half_kernel)
     norm_scale = (lax.axis_size("dp") * positions * lax.axis_size("seq")) ** (-0.5)
-    weight_part = (
-        lax.dot_general(
-            columns, grad_pre, (((0,), (0,)), ((), ())), preferred_element_type=jnp.float32
+    seq_count, dp_count = lax.axis_size("seq"), lax.axis_size("dp")
+    rows_per = KW * C // (seq_count * dp_count)
+    if dp_count == 2:
+        partner = [(0, 1), (1, 0)]
+        partner_padded = lax.ppermute(padded, "dp", partner)
+        partner_grad = lax.ppermute(grad_pre, "dp", partner)
+        both_columns = jnp.concatenate(
+            [columns, window_rows(partner_padded, KW, positions)], axis=0
+        ).reshape(2 * positions, seq_count, dp_count, rows_per)
+        mine = lax.dynamic_index_in_dim(both_columns, lax.axis_index("dp"), axis=2, keepdims=False)
+        dp_summed = (
+            jnp.einsum(
+                "psr,po->sro",
+                mine,
+                jnp.concatenate([grad_pre, partner_grad], axis=0),
+                preferred_element_type=jnp.float32,
+            )
+            * norm_scale
         )
-        * norm_scale
-    )
-    seq_count, dp_count = lax.axis_size("seq"), lax.axis_size("dp")
-    weight_blocks_all = weight_part.reshape(seq_count, dp_count, -1, CO)
-    dp_summed = ring_reduce_scatter(
-        jnp.swapaxes(weight_blocks_all, 0, 1), "dp", list(range(dp_count))
-    )
+    else:
+        weight_part = (
+            lax.dot_general(
+                columns, grad_pre, (((0,), (0,)), ((), ())), preferred_element_type=jnp.float32
+            )
+            * norm_scale
+        )
+        weight_blocks_all = weight_part.reshape(seq_count, dp_count, -1, CO)
+        dp_summed = ring_reduce_scatter(
+            jnp.swapaxes(weight_blocks_all, 0, 1), "dp", list(range(dp_count))
+        )
     half_co = CO // 2
     grad_weight = jnp.concatenate(
         [

time: 249 us -> 238 us (0.956)
  waiting for transfers between devices: 81.4 us -> 65.5 us
  local copies, waits for them, and re-layouts: 43.5 us -> 47.2 us
    ppermute x15 -> x14, waiting for transfers between devices: 39.2 us -> 30.2 us  [ring_reduce_scatter(): received = lax.ppermute(acc, axis, perm)]
    concatenate x0 -> x2, local copies, waits for them, and re-layouts: none -> 6.39 us  [the longest x1 6.3 us: body(): jnp.concatenate([columns, window_rows(partner_padded, KW, positions)], ax...]
    ppermute x4, waiting for transfers between devices: 19.4 us -> 14.8 us  [ring_gather(): current = lax.ppermute(current, 'seq', forward)]
    ppermute x3, waiting for transfers between devices: 0.33 us -> 4.81 us  [ring_gather(): current = lax.ppermute(current, 'seq', backward)]
    ppermute x4, waiting for transfers between devices: 8.98 us -> 4.81 us  [ring_scatter_back(): received = lax.ppermute(acc, 'seq', backward).astype(jnp.float32)]
    add x15 -> x14, other arithmetic: 3.49 us -> 0.44 us  [ring_reduce_scatter(): acc = received + block_at(t + 2)]
    concatenate x0 -> x2, other arithmetic: none -> 3.04 us  [the longest x1 2.19 us: body(): jnp.concatenate([columns, window_rows(partner_padded, KW, positions)], ax...]
    ppermute x15 -> x14, starting transfers between devices: 13.8 us -> 13.2 us  [ring_reduce_scatter(): received = lax.ppermute(acc, axis, perm)]
  transfers between devices with their start and end apart: 33 -> 34, of which waited for: 25 -> 15; matrix products, arithmetic and copies ran while one was open for 9% -> 24% of each run, Pallas kernels for 0% -> 0%
where the time goes in v2:
time: 238 us; the launch traced here: 236 us
  waiting for transfers between devices  65.5 us (28%)
  local copies, waits for them, and re-layouts  47.2 us (20%)
  starting transfers between devices  43.2 us (18%)
  between operations  43 us (18%)
  other arithmetic  20.4 us (9%)
  matrix products  16.6 us (7%)
    ppermute x14, waiting for transfers between devices, ring_reduce_scatter(): received = lax.ppermute(acc, axis, perm)  30.2 us
    ppermute x4, waiting for transfers between devices, ring_gather(): current = lax.ppermute(current, 'seq', forward)  14.8 us
    unnamed x71, local copies, waits for them, and re-layouts  13.8 us
    ppermute x14, starting transfers between devices, ring_reduce_scatter(): received = lax.ppermute(acc, axis, perm)  13.2 us
    ppermute x2, starting transfers between devices, extended(): before = lax.ppermute(last, axis, up)  8.04 us
    ppermute x4, starting transfers between devices, ring_gather(): current = lax.ppermute(current, 'seq', forward)  7.89 us
    ppermute x3, waiting for transfers between devices, ring_scatter_back(): received = lax.ppermute(acc, 'seq', forward).astype(jnp.float32)  6.44 us
    concatenate x1, local copies, waits for them, and re-layouts, body(): jnp.concatenate([columns, window_rows(partner_padded, KW, positions)], ax...  6.3 us
  transfers between devices with their start and end apart: 34, of which 15 were waited for; matrix products, arithmetic and copies ran while one was open for 24% of the time, Pallas kernels for 0%

profile of v2, /device:TPU:0, one launch (start us, length us, event | category | flops | bytes accessed | tf_op | source)
XLA Modules:
  0.0 235.9 jit_solution(16476032988908299127)
XLA Ops:
  3.9 3.1 %collective-permute-start = (bf16[128,1280]{0,1:T(8,128)(2,1)}, bf16[128,1280]{0,1:T(8,128)(2,1)S(1)}, u32[]{:S(2)}, u32[]{:S(2)}) collective-permute-start(bf16[128,1280]{0,1:T(8,128)(2,1)} %get-tuple-element.35), channel_id=1, source_target_pairs={{0,4},{4,8},{8,12},{12,14},{14,10},{10,6},{6,2},{2,0},{1,5},{5,9},... | collective-permute-start | bytes 983048 | tf_op jit(solution)/shard_map/ppermute | solution.py:75
  6.9 7.9 %collective-permute-done = bf16[128,1280]{0,1:T(8,128)(2,1)S(1)} collective-permute-done((bf16[128,1280]{0,1:T(8,128)(2,1)}, bf16[128,1280]{0,1:T(8,128)(2,1)S(1)}, u32[]{:S(2)}, u32[]{:S(2)}) %collective-permute-start) | collective-permute-done | bytes 327712 | tf_op jit(solution)/shard_map/ppermute | solution.py:75
  15.5 1.8 collective-permute-start.1
  17.6 7.0 %collective-permute-done.1 = bf16[128,1280]{0,1:T(8,128)(2,1)} collective-permute-done((bf16[128,1280]{0,1:T(8,128)(2,1)S(1)}, bf16[128,1280]{0,1:T(8,128)(2,1)}, u32[]{:S(2)}, u32[]{:S(2)}) %collective-permute-start.1) | collective-permute-done | bytes 327712 | tf_op jit(solution)/shard_map/ppermute | solution.py:75
  24.5 1.5 collective-permute-start.2
  46.9 1.8 constant_dynamic-update-slice_fusion.6
  48.7 1.5 collective-permute-start.3
  50.2 1.7 constant_dynamic-update-slice_fusion.5
  51.9 2.3 collective-permute-done.5
  54.8 1.7 constant_dynamic-update-slice_fusion.4
  58.9 2.5 %collective-permute-done.6 = bf16[128,1280]{0,1:T(8,128)(2,1)S(1)} collective-permute-done((bf16[128,1280]{0,1:T(8,128)(2,1)S(1)}, bf16[128,1280]{0,1:T(8,128)(2,1)S(1)}, u32[]{:S(2)}, u32[]{:S(2)}) %collective-permute-start.6) | collective-permute-done | bytes 327712 | tf_op jit(solution)/shard_map/ppermute | solution.py:79
  62.2 1.5 slice.134
  63.7 1.9 slice.135
  70.6 2.6 %broadcast_in_dim.26 = f32[1,256,768]{2,1,0:T(8,128)} reshape(f32[128,2,768]{2,1,0:T(2,128)} %broadcast_in_dim.12) | data formatting | bytes 1572864 | tf_op jit(solution)/shard_map/broadcast_in_dim | solution.py:159
  73.2 2.6 %reshape.120 = f32[256,768]{1,0:T(8,128)} reshape(f32[128,2,768]{2,1,0:T(2,128)} %broadcast_in_dim.12) | data formatting | bytes 1572864 | tf_op jit(solution)/shard_map/reshape | solution.py:159
  79.1 2.4 %collective-permute-start.7 = (bf16[2,768]{1,0:T(2,128)(2,1)S(1)}, bf16[2,768]{1,0:T(2,128)(2,1)S(1)}, u32[]{:S(2)}, u32[]{:S(2)}) collective-permute-start(bf16[2,768]{1,0:T(2,128)(2,1)S(1)} %get-tuple-element.34), channel_id=1, source_target_pairs={{0,2},{2,4},{4,6},{6,8},{8,10},{10,12},{12,14},{1,3},{3,5},{5,7},{... | collective-permute-start | bytes 9224 | tf_op jit(solution)/shard_map/ppermute | solution.py:24
  106.7 4.5 %collective-permute-done.8 = bf16[2,768]{1,0:T(2,128)(2,1)S(1)} collective-permute-done((bf16[2,768]{1,0:T(2,128)(2,1)S(1)}, bf16[2,768]{1,0:T(2,128)(2,1)S(1)}, u32[]{:S(2)}, u32[]{:S(2)}) %collective-permute-start.8) | collective-permute-done | bytes 3104 | tf_op jit(solution)/shard_map/ppermute | solution.py:25
  111.4 3.1 %fusion.26 = (bf16[256,384]{1,0:T(8,128)(2,1)S(1)}, bf16[1,256,384]{2,1,0:T(8,128)(2,1)}) fusion(bf16[1,256,384]{2,1,0:T(8,128)(2,1)} %param.19, bf16[256,3840]{1,0:T(8,128)(2,1)S(1)} %fusion.27, bf16[3840,384]{1,0:T(8,128)(2,1)S(1)} %copy-done), kind=kOutput, calls=%fused_computation.65 | convolution fusion | flops 756252672 | bytes 5505024 | tf_op jit(solution)/shard_map/dot_general | solution.py:165
  116.1 5.6 %collective-permute-start.10 = (bf16[2,384]{1,0:T(2,128)(2,1)S(1)}, bf16[2,384]{1,0:T(2,128)(2,1)S(1)}, u32[]{:S(2)}, u32[]{:S(2)}) collective-permute-start(bf16[2,384]{1,0:T(2,128)(2,1)S(1)} %get-tuple-element.37), channel_id=1, source_target_pairs={{0,2},{2,4},{4,6},{6,8},{8,10},{10,12},{12,14},{1,3},{3,5},{5,7},{... | collective-permute-start | bytes 4616 | tf_op jit(solution)/shard_map/ppermute | solution.py:24
  125.4 2.5 %reshape.122 = f32[128,2,768]{2,1,0:T(2,128)} reshape(f32[256,768]{1,0:T(8,128)} %get-tuple-element.22) | data formatting | bytes 1572864 | tf_op jit(solution)/shard_map/reshape | solution.py:225
  127.9 2.8 %reduce_sum.48 = bf16[128,768]{1,0:T(8,128)(2,1)} reduce(f32[128,2,768]{2,1,0:T(2,128)} %reshape.122, f32[]{:T(128)} %constant.191.clone.1), dimensions={1}, to_apply=%region_4.5 | reduce | flops 98304 | bytes 983044 | tf_op jit(solution)/shard_map/reduce_sum | solution.py:225
  130.7 1.7 copy.40
  133.7 3.5 %convolution_convert_fusion = bf16[4,192,1024]{2,1,0:T(8,128)(2,1)} fusion(bf16[128,4,192]{0,2,1:T(8,128)(2,1)} %bitcast.177, f32[4,1024,128]{2,1,0:T(8,128)} %copy-done.2, f32[4,128]{1,0:T(4,128)S(1)} %copy-done.23), kind=kOutput, calls=%fused_computation.28 | convolution fusion | flops 203685888 | bytes 3868672 | tf_op jit(solution)/shard_map/hij,ihd->jhd/dot_general | solution.py:240
  139.5 1.7 copy.51
  141.2 2.6 %copy.49 = bf16[1024,768]{1,0:T(8,128)(2,1)} copy(bf16[1024,768]{0,1:T(8,128)(2,1)} %bitcast.173) | data formatting | bytes 3145728 | tf_op jit(solution)/shard_map/reshape | solution.py:244
  143.8 2.7 %fusion.10 = bf16[1024,4,128]{2,0,1:T(8,128)(2,1)} fusion(bf16[4,128,1024]{1,2,0:T(8,128)(2,1)} %copy-done.10, bf16[128,4,128]{0,2,1:T(8,128)(2,1)} %bitcast.180), kind=kOutput, calls=%fused_computation.29 | convolution fusion | flops 135266304 | bytes 2228224 | tf_op jit(solution)/shard_map/hij,ihd->jhd/dot_general | solution.py:237
  146.4 2.3 copy.46
  148.7 2.3 copy.48
  151.0 2.0 fusion.34
  153.0 2.9 %collective-permute-start.11 = (bf16[128,1280]{1,0:T(8,128)(2,1)}, bf16[128,1280]{1,0:T(8,128)(2,1)}, u32[]{:S(2)}, u32[]{:S(2)}) collective-permute-start(bf16[128,1280]{1,0:T(8,128)(2,1)} %get-tuple-element.29), channel_id=1, source_target_pairs={{0,2},{4,0},{8,4},{12,8},{14,12},{10,14},{6,10},{2,6},{1,3},{5,1},... | collective-permute-start | bytes 983048 | tf_op jit(solution)/shard_map/ppermute | solution.py:96
  155.9 1.8 collective-permute-start.15
  158.1 2.2 pad_maximum_fusion
  160.3 6.3 %copy.50 = bf16[512,3840]{0,1:T(8,128)(2,1)} copy(bf16[512,3840]{1,0:T(8,128)(2,1)} %pad_maximum_fusion) | data formatting | bytes 7864320 | tf_op jit(solution)/shard_map/concatenate | solution.py:177
  166.6 2.8 %fusion.7 = f32[8,240,384]{2,1,0:T(8,128)S(1)} fusion(bf16[512,8,2,240]{0,3,2,1:T(8,128)(2,1)} %bitcast.172, s32[]{:T(128)S(6)} %select_n.172, bf16[256,384]{1,0:T(8,128)(2,1)} %collective-permute-done.19, bf16[256,384]{1,0:T(8,128)(2,1)S(1)} %get-tuple-element.31), kind=kOutput, calls=%fused_computation.27 | convolution fusion | flops 756498432 | bytes 5308420 | tf_op jit(solution)/shard_map/psr,po->sro/dot_general | solution.py:182
  174.3 4.7 %collective-permute-done.27 = f32[240,192]{1,0:T(8,128)S(1)} collective-permute-done((f32[240,192]{1,0:T(8,128)S(1)}, f32[240,192]{1,0:T(8,128)S(1)}, u32[]{:S(2)}, u32[]{:S(2)}) %collective-permute-start.27) | collective-permute-done | bytes 184352 | tf_op jit(solution)/shard_map/ppermute | solution.py:129
  181.2 4.8 %collective-permute-done.12 = bf16[128,1280]{1,0:T(8,128)(2,1)S(1)} collective-permute-done((bf16[128,1280]{1,0:T(8,128)(2,1)S(1)}, bf16[128,1280]{1,0:T(8,128)(2,1)S(1)}, u32[]{:S(2)}, u32[]{:S(2)}) %collective-permute-start.12) | collective-permute-done | bytes 327712 | tf_op jit(solution)/shard_map/ppermute | solution.py:96
  187.5 1.8 collective-permute-start.16
  189.3 2.0 collective-permute-done.28
  191.7 1.8 collective-permute-start.22
  193.5 7.7 %collective-permute-done.29 = f32[240,192]{1,0:T(8,128)S(1)} collective-permute-done((f32[240,192]{1,0:T(8,128)S(1)}, f32[240,192]{1,0:T(8,128)S(1)}, u32[]{:S(2)}, u32[]{:S(2)}) %collective-permute-start.29) | collective-permute-done | bytes 184352 | tf_op jit(solution)/shard_map/ppermute | solution.py:129
  201.3 1.6 collective-permute-start.30
  203.6 1.8 collective-permute-start.17
  205.7 4.5 %collective-permute-done.30 = f32[240,192]{1,0:T(8,128)S(1)} collective-permute-done((f32[240,192]{1,0:T(8,128)S(1)}, f32[240,192]{1,0:T(8,128)S(1)}, u32[]{:S(2)}, u32[]{:S(2)}) %collective-permute-start.30) | collective-permute-done | bytes 184352 | tf_op jit(solution)/shard_map/ppermute | solution.py:129
  210.2 1.6 collective-permute-start.31
  212.4 6.4 %collective-permute-done.17 = bf16[128,1280]{1,0:T(8,128)(2,1)S(1)} collective-permute-done((bf16[128,1280]{1,0:T(8,128)(2,1)S(1)}, bf16[128,1280]{1,0:T(8,128)(2,1)S(1)}, u32[]{:S(2)}, u32[]{:S(2)}) %collective-permute-start.17) | collective-permute-done | bytes 327712 | tf_op jit(solution)/shard_map/ppermute | solution.py:104
  220.3 1.8 collective-permute-start.32
  222.5 4.8 %collective-permute-done.32 = f32[240,192]{1,0:T(8,128)S(1)} collective-permute-done((f32[240,192]{1,0:T(8,128)S(1)}, f32[240,192]{1,0:T(8,128)S(1)}, u32[]{:S(2)}, u32[]{:S(2)}) %collective-permute-start.32) | collective-permute-done | bytes 184352 | tf_op jit(solution)/shard_map/ppermute | solution.py:129
  229.5 4.1 %collective-permute-done.33 = f32[240,192]{1,0:T(8,128)S(1)} collective-permute-done((f32[240,192]{1,0:T(8,128)S(1)}, f32[240,192]{1,0:T(8,128)S(1)}, u32[]{:S(2)}, u32[]{:S(2)}) %collective-permute-start.33) | collective-permute-done | bytes 184352 | tf_op jit(solution)/shard_map/ppermute | solution.py:129
  (166 shorter events, 46.7 us)
Async XLA Ops:
  0.6 110.8 %copy-start = (bf16[3840,384]{1,0:T(8,128)(2,1)S(1)}, bf16[3840,384]{1,0:T(8,128)(2,1)}, u32[]{:S(2)}) copy-start(bf16[3840,384]{1,0:T(8,128)(2,1)} %param.18) | copy-start | bytes 8847364
  0.6 38.6 %copy-start.20 = (s32[8]{0:T(128)S(1)}, s32[8]{0:T(128)}, u32[]{:S(2)}) copy-start(s32[8]{0:T(128)} %constant.219.clone) | copy-start | bytes 100
  0.7 45.5 %copy-start.27 = (bf16[768]{0:T(1024)(128)(2,1)S(1)}, bf16[768]{0:T(1024)(128)(2,1)}, u32[]{:S(2)}) copy-start(bf16[768]{0:T(1024)(128)(2,1)} %param.17) | copy-start | bytes 4612
  0.7 45.5 %copy-start.21 = (bf16[1,128,512]{2,1,0:T(8,128)(2,1)S(1)}, bf16[1,128,512]{2,1,0:T(8,128)(2,1)}, u32[]{:S(2)}) copy-start(bf16[1,128,512]{2,1,0:T(8,128)(2,1)} %param.12) | copy-start | bytes 393220
  3.9 10.9 %collective-permute-start = (bf16[128,1280]{0,1:T(8,128)(2,1)}, bf16[128,1280]{0,1:T(8,128)(2,1)S(1)}, u32[]{:S(2)}, u32[]{:S(2)}) collective-permute-start(bf16[128,1280]{0,1:T(8,128)(2,1)} %get-tuple-element.35), channel_id=1, source_target_pairs={{0,4},{4,8},{8,12},{12,14},{14,10},{10,6},{6,2},{2,0},{1,5},{5,9},... | collective-permute-start | bytes 983048 | tf_op jit(solution)/shard_map/ppermute | solution.py:75
  15.5 9.0 %collective-permute-start.1 = (bf16[128,1280]{0,1:T(8,128)(2,1)S(1)}, bf16[128,1280]{0,1:T(8,128)(2,1)}, u32[]{:S(2)}, u32[]{:S(2)}) collective-permute-start(bf16[128,1280]{0,1:T(8,128)(2,1)S(1)} %collective-permute-done), channel_id=1, source_target_pairs={{0,4},{4,8},{8,12},{12,14},{14,10},{10,6},{6,2},{2,0},{1,5},{5,9},... | collective-permute-start | bytes 983048 | tf_op jit(solution)/shard_map/ppermute | solution.py:75
  17.3 29.0 %collective-permute-start.4 = (bf16[128,1280]{0,1:T(8,128)(2,1)}, bf16[128,1280]{0,1:T(8,128)(2,1)S(1)}, u32[]{:S(2)}, u32[]{:S(2)}) collective-permute-start(bf16[128,1280]{0,1:T(8,128)(2,1)} %get-tuple-element.35), channel_id=1, source_target_pairs={{0,2},{4,0},{8,4},{12,8},{14,12},{10,14},{6,10},{2,6},{1,3},{5,1},... | collective-permute-start | bytes 983048 | tf_op jit(solution)/shard_map/ppermute | solution.py:79
  24.5 24.2 %collective-permute-start.2 = (bf16[128,1280]{0,1:T(8,128)(2,1)}, bf16[128,1280]{0,1:T(8,128)(2,1)}, u32[]{:S(2)}, u32[]{:S(2)}) collective-permute-start(bf16[128,1280]{0,1:T(8,128)(2,1)} %collective-permute-done.1), channel_id=1, source_target_pairs={{0,4},{4,8},{8,12},{12,14},{14,10},{10,6},{6,2},{2,0},{1,5},{5,9},... | collective-permute-start | bytes 983048 | tf_op jit(solution)/shard_map/ppermute | solution.py:75
  46.3 19.3 %copy-start.17 = (bf16[1,128,512]{1,2,0:T(8,128)(2,1)}, bf16[1,128,512]{1,2,0:T(8,128)(2,1)S(1)}, u32[]{:S(2)}) copy-start(bf16[1,128,512]{1,2,0:T(8,128)(2,1)S(1)} %copy.59) | copy-start | bytes 393220
  46.4 7.9 %collective-permute-start.5 = (bf16[128,1280]{0,1:T(8,128)(2,1)S(1)}, bf16[128,1280]{0,1:T(8,128)(2,1)S(1)}, u32[]{:S(2)}, u32[]{:S(2)}) collective-permute-start(bf16[128,1280]{0,1:T(8,128)(2,1)S(1)} %collective-permute-done.4), channel_id=1, source_target_pairs={{0,2},{4,0},{8,4},{12,8},{14,12},{10,14},{6,10},{2,6},{1,3},{5,1},... | collective-permute-start | bytes 983048 | tf_op jit(solution)/shard_map/ppermute | solution.py:79
  48.7 7.9 %collective-permute-start.3 = (bf16[128,1280]{0,1:T(8,128)(2,1)}, bf16[128,1280]{0,1:T(8,128)(2,1)S(1)}, u32[]{:S(2)}, u32[]{:S(2)}) collective-permute-start(bf16[128,1280]{0,1:T(8,128)(2,1)} %collective-permute-done.2), channel_id=1, source_target_pairs={{0,4},{4,8},{8,12},{12,14},{14,10},{10,6},{6,2},{2,0},{1,5},{5,9},... | collective-permute-start | bytes 983048 | tf_op jit(solution)/shard_map/ppermute | solution.py:75
  54.3 7.1 %collective-permute-start.6 = (bf16[128,1280]{0,1:T(8,128)(2,1)S(1)}, bf16[128,1280]{0,1:T(8,128)(2,1)S(1)}, u32[]{:S(2)}, u32[]{:S(2)}) collective-permute-start(bf16[128,1280]{0,1:T(8,128)(2,1)S(1)} %collective-permute-done.5), channel_id=1, source_target_pairs={{0,2},{4,0},{8,4},{12,8},{14,12},{10,14},{6,10},{2,6},{1,3},{5,1},... | collective-permute-start | bytes 983048 | tf_op jit(solution)/shard_map/ppermute | solution.py:79
  69.5 6.3 %copy-start.11 = (bf16[1,256,768]{2,1,0:T(8,128)(2,1)S(1)}, bf16[1,256,768]{2,1,0:T(8,128)(2,1)}, u32[]{:S(2)}) copy-start(bf16[1,256,768]{2,1,0:T(8,128)(2,1)} %param.16) | copy-start | bytes 1179652
  79.1 27.4 %collective-permute-start.7 = (bf16[2,768]{1,0:T(2,128)(2,1)S(1)}, bf16[2,768]{1,0:T(2,128)(2,1)S(1)}, u32[]{:S(2)}, u32[]{:S(2)}) collective-permute-start(bf16[2,768]{1,0:T(2,128)(2,1)S(1)} %get-tuple-element.34), channel_id=1, source_target_pairs={{0,2},{2,4},{4,6},{6,8},{8,10},{10,12},{12,14},{1,3},{3,5},{5,7},{... | collective-permute-start | bytes 9224 | tf_op jit(solution)/shard_map/ppermute | solution.py:24
  105.2 6.0 %collective-permute-start.8 = (bf16[2,768]{1,0:T(2,128)(2,1)S(1)}, bf16[2,768]{1,0:T(2,128)(2,1)S(1)}, u32[]{:S(2)}, u32[]{:S(2)}) collective-permute-start(bf16[2,768]{1,0:T(2,128)(2,1)S(1)} %get-tuple-element.33), channel_id=1, source_target_pairs={{2,0},{4,2},{6,4},{8,6},{10,8},{12,10},{14,12},{3,1},{5,3},{7,5},{... | collective-permute-start | bytes 9224 | tf_op jit(solution)/shard_map/ppermute | solution.py:25
  111.4 3.2 %copy-start.15 = (bf16[256,3840]{1,0:T(8,128)(2,1)}, bf16[256,3840]{1,0:T(8,128)(2,1)S(1)}, u32[]{:S(2)}) copy-start(bf16[256,3840]{1,0:T(8,128)(2,1)S(1)} %fusion.27) | copy-start | bytes 5898244
  114.6 8.4 %copy-start.7 = (f32[256,768]{1,0:T(8,128)S(1)}, f32[256,768]{1,0:T(8,128)}, u32[]{:S(2)}) copy-start(f32[256,768]{1,0:T(8,128)} %reshape.120) | copy-start | bytes 2359300
  114.6 8.4 %copy-start.12 = (bf16[1,256,768]{2,1,0:T(8,128)(2,1)S(1)}, bf16[1,256,768]{2,1,0:T(8,128)(2,1)}, u32[]{:S(2)}) copy-start(bf16[1,256,768]{2,1,0:T(8,128)(2,1)} %param.16) | copy-start | bytes 1179652
  114.6 52.0 %collective-permute-start.19 = (bf16[256,384]{1,0:T(8,128)(2,1)S(1)}, bf16[256,384]{1,0:T(8,128)(2,1)}, u32[]{:S(2)}, u32[]{:S(2)}) collective-permute-start(bf16[256,384]{1,0:T(8,128)(2,1)S(1)} %get-tuple-element.31), channel_id=1, source_target_pairs={{0,1},{1,0},{2,3},{3,2},{4,5},{5,4},{6,7},{7,6},{8,9},{9,8},{10,11... | collective-permute-start | bytes 589832 | tf_op jit(solution)/shard_map/ppermute | solution.py:176
  114.7 8.0 %collective-permute-start.9 = (bf16[2,384]{1,0:T(2,128)(2,1)S(1)}, bf16[2,384]{1,0:T(2,128)(2,1)S(1)}, u32[]{:S(2)}, u32[]{:S(2)}) collective-permute-start(bf16[2,384]{1,0:T(2,128)(2,1)S(1)} %get-tuple-element.38), channel_id=1, source_target_pairs={{2,0},{4,2},{6,4},{8,6},{10,8},{12,10},{14,12},{3,1},{5,3},{7,5},{... | collective-permute-start | bytes 4616 | tf_op jit(solution)/shard_map/ppermute | solution.py:25
  116.1 6.7 %collective-permute-start.10 = (bf16[2,384]{1,0:T(2,128)(2,1)S(1)}, bf16[2,384]{1,0:T(2,128)(2,1)S(1)}, u32[]{:S(2)}, u32[]{:S(2)}) collective-permute-start(bf16[2,384]{1,0:T(2,128)(2,1)S(1)} %get-tuple-element.37), channel_id=1, source_target_pairs={{0,2},{2,4},{4,6},{6,8},{8,10},{10,12},{12,14},{1,3},{3,5},{5,7},{... | collective-permute-start | bytes 4616 | tf_op jit(solution)/shard_map/ppermute | solution.py:24
  122.6 35.1 %collective-permute-start.18 = (bf16[260,768]{1,0:T(8,128)(2,1)}, bf16[260,768]{1,0:T(8,128)(2,1)S(1)}, u32[]{:S(2)}, u32[]{:S(2)}) collective-permute-start(bf16[260,768]{1,0:T(8,128)(2,1)} %pad_maximum_fusion.1), channel_id=1, source_target_pairs={{0,1},{1,0},{2,3},{3,2},{4,5},{5,4},{6,7},{7,6},{8,9},{9,8},{10,11... | collective-permute-start | bytes 1198088 | tf_op jit(solution)/shard_map/ppermute | solution.py:175
  125.4 8.2 %copy-start.23 = (f32[4,128]{1,0:T(4,128)S(1)}, f32[4,128]{1,0:T(4,128)}, u32[]{:S(2)}) copy-start(f32[4,128]{1,0:T(4,128)} %copy-done.22) | copy-start | bytes 6148
  132.4 4.8 %copy-start.3 = (f32[4,1024,128]{2,1,0:T(8,128)S(1)}, f32[4,1024,128]{2,1,0:T(8,128)}, u32[]{:S(2)}) copy-start(f32[4,1024,128]{2,1,0:T(8,128)} %copy-done.2) | copy-start | bytes 6291460
  132.4 4.8 %copy-start.6 = (bf16[1024,768]{0,1:T(8,128)(2,1)S(1)}, bf16[1024,768]{0,1:T(8,128)(2,1)}, u32[]{:S(2)}) copy-start(bf16[1024,768]{0,1:T(8,128)(2,1)} %copy-done.5) | copy-start | bytes 4718596
  132.4 4.8 %copy-start.14 = (bf16[128,768]{0,1:T(8,128)(2,1)S(1)}, bf16[128,768]{0,1:T(8,128)(2,1)}, u32[]{:S(2)}) copy-start(bf16[128,768]{0,1:T(8,128)(2,1)} %copy.40) | copy-start | bytes 589828
  153.0 5.1 %copy-start.16 = (bf16[256,3840]{1,0:T(8,128)(2,1)S(1)}, bf16[256,3840]{1,0:T(8,128)(2,1)}, u32[]{:S(2)}) copy-start(bf16[256,3840]{1,0:T(8,128)(2,1)} %copy-done.15) | copy-start | bytes 5898244
  153.0 17.4 %collective-permute-start.11 = (bf16[128,1280]{1,0:T(8,128)(2,1)}, bf16[128,1280]{1,0:T(8,128)(2,1)}, u32[]{:S(2)}, u32[]{:S(2)}) collective-permute-start(bf16[128,1280]{1,0:T(8,128)(2,1)} %get-tuple-element.29), channel_id=1, source_target_pairs={{0,2},{4,0},{8,4},{12,8},{14,12},{10,14},{6,10},{2,6},{1,3},{5,1},... | collective-permute-start | bytes 983048 | tf_op jit(solution)/shard_map/ppermute | solution.py:96
  155.9 25.3 %collective-permute-start.15 = (bf16[128,1280]{1,0:T(8,128)(2,1)}, bf16[128,1280]{1,0:T(8,128)(2,1)}, u32[]{:S(2)}, u32[]{:S(2)}) collective-permute-start(bf16[128,1280]{1,0:T(8,128)(2,1)} %get-tuple-element.30), channel_id=1, source_target_pairs={{0,4},{4,8},{8,12},{12,14},{14,10},{10,6},{6,2},{2,0},{1,5},{5,9},... | collective-permute-start | bytes 983048 | tf_op jit(solution)/shard_map/ppermute | solution.py:104
  170.1 8.9 %collective-permute-start.27 = (f32[240,192]{1,0:T(8,128)S(1)}, f32[240,192]{1,0:T(8,128)S(1)}, u32[]{:S(2)}, u32[]{:S(2)}) collective-permute-start(f32[240,192]{1,0:T(8,128)S(1)} %dynamic-slice_bitcast_fusion), channel_id=1, source_target_pairs={{0,2},{4,0},{8,4},{12,8},{14,12},{10,14},{6,10},{2,6},{1,3},{5,1},... | collective-permute-start | bytes 552968 | tf_op jit(solution)/shard_map/ppermute | solution.py:129
  172.2 13.9 %collective-permute-start.12 = (bf16[128,1280]{1,0:T(8,128)(2,1)S(1)}, bf16[128,1280]{1,0:T(8,128)(2,1)S(1)}, u32[]{:S(2)}, u32[]{:S(2)}) collective-permute-start(bf16[128,1280]{1,0:T(8,128)(2,1)S(1)} %add_convert_fusion.5), channel_id=1, source_target_pairs={{0,2},{4,0},{8,4},{12,8},{14,12},{10,14},{6,10},{2,6},{1,3},{5,1},... | collective-permute-start | bytes 983048 | tf_op jit(solution)/shard_map/ppermute | solution.py:96
  173.2 7.2 %collective-permute-start.20 = (f32[240,192]{1,0:T(8,128)S(1)}, f32[240,192]{1,0:T(8,128)S(1)}, u32[]{:S(2)}, u32[]{:S(2)}) collective-permute-start(f32[240,192]{1,0:T(8,128)S(1)} %dynamic-slice_bitcast_fusion.1), channel_id=1, source_target_pairs={{0,4},{4,8},{8,12},{12,14},{14,10},{10,6},{6,2},{2,0},{1,5},{5,9},... | collective-permute-start | bytes 552968 | tf_op jit(solution)/shard_map/ppermute | solution.py:129
  179.0 12.3 %collective-permute-start.28 = (f32[240,192]{1,0:T(8,128)S(1)}, f32[240,192]{1,0:T(8,128)S(1)}, u32[]{:S(2)}, u32[]{:S(2)}) collective-permute-start(f32[240,192]{1,0:T(8,128)S(1)} %bitcast_add_fusion.6), channel_id=1, source_target_pairs={{0,2},{4,0},{8,4},{12,8},{14,12},{10,14},{6,10},{2,6},{1,3},{5,1},... | collective-permute-start | bytes 552968 | tf_op jit(solution)/shard_map/ppermute | solution.py:129
  180.4 11.2 %collective-permute-start.21 = (f32[240,192]{1,0:T(8,128)S(1)}, f32[240,192]{1,0:T(8,128)S(1)}, u32[]{:S(2)}, u32[]{:S(2)}) collective-permute-start(f32[240,192]{1,0:T(8,128)S(1)} %bitcast_add_fusion.13), channel_id=1, source_target_pairs={{0,4},{4,8},{8,12},{12,14},{14,10},{10,6},{6,2},{2,0},{1,5},{5,9},... | collective-permute-start | bytes 552968 | tf_op jit(solution)/shard_map/ppermute | solution.py:129
  187.2 16.3 %collective-permute-start.13 = (bf16[128,1280]{1,0:T(8,128)(2,1)S(1)}, bf16[128,1280]{1,0:T(8,128)(2,1)S(1)}, u32[]{:S(2)}, u32[]{:S(2)}) collective-permute-start(bf16[128,1280]{1,0:T(8,128)(2,1)S(1)} %get-tuple-element.27), channel_id=1, source_target_pairs={{0,2},{4,0},{8,4},{12,8},{14,12},{10,14},{6,10},{2,6},{1,3},{5,1},... | collective-permute-start | bytes 983048 | tf_op jit(solution)/shard_map/ppermute | solution.py:96
  187.5 16.0 %collective-permute-start.16 = (bf16[128,1280]{1,0:T(8,128)(2,1)S(1)}, bf16[128,1280]{1,0:T(8,128)(2,1)S(1)}, u32[]{:S(2)}, u32[]{:S(2)}) collective-permute-start(bf16[128,1280]{1,0:T(8,128)(2,1)S(1)} %get-tuple-element.28), channel_id=1, source_target_pairs={{0,4},{4,8},{8,12},{12,14},{14,10},{10,6},{6,2},{2,0},{1,5},{5,9},... | collective-permute-start | bytes 983048 | tf_op jit(solution)/shard_map/ppermute | solution.py:104
  191.3 9.9 %collective-permute-start.29 = (f32[240,192]{1,0:T(8,128)S(1)}, f32[240,192]{1,0:T(8,128)S(1)}, u32[]{:S(2)}, u32[]{:S(2)}) collective-permute-start(f32[240,192]{1,0:T(8,128)S(1)} %bitcast_add_fusion.5), channel_id=1, source_target_pairs={{0,2},{4,0},{8,4},{12,8},{14,12},{10,14},{6,10},{2,6},{1,3},{5,1},... | collective-permute-start | bytes 552968 | tf_op jit(solution)/shard_map/ppermute | solution.py:129
  191.7 11.2 %collective-permute-start.22 = (f32[240,192]{1,0:T(8,128)S(1)}, f32[240,192]{1,0:T(8,128)S(1)}, u32[]{:S(2)}, u32[]{:S(2)}) collective-permute-start(f32[240,192]{1,0:T(8,128)S(1)} %bitcast_add_fusion.12), channel_id=1, source_target_pairs={{0,4},{4,8},{8,12},{12,14},{14,10},{10,6},{6,2},{2,0},{1,5},{5,9},... | collective-permute-start | bytes 552968 | tf_op jit(solution)/shard_map/ppermute | solution.py:129
  201.3 8.9 %collective-permute-start.30 = (f32[240,192]{1,0:T(8,128)S(1)}, f32[240,192]{1,0:T(8,128)S(1)}, u32[]{:S(2)}, u32[]{:S(2)}) collective-permute-start(f32[240,192]{1,0:T(8,128)S(1)} %bitcast_add_fusion.4), channel_id=1, source_target_pairs={{0,2},{4,0},{8,4},{12,8},{14,12},{10,14},{6,10},{2,6},{1,3},{5,1},... | collective-permute-start | bytes 552968 | tf_op jit(solution)/shard_map/ppermute | solution.py:129
  202.9 8.9 %collective-permute-start.23 = (f32[240,192]{1,0:T(8,128)S(1)}, f32[240,192]{1,0:T(8,128)S(1)}, u32[]{:S(2)}, u32[]{:S(2)}) collective-permute-start(f32[240,192]{1,0:T(8,128)S(1)} %bitcast_add_fusion.11), channel_id=1, source_target_pairs={{0,4},{4,8},{8,12},{12,14},{14,10},{10,6},{6,2},{2,0},{1,5},{5,9},... | collective-permute-start | bytes 552968 | tf_op jit(solution)/shard_map/ppermute | solution.py:129
  203.6 15.2 %collective-permute-start.17 = (bf16[128,1280]{1,0:T(8,128)(2,1)S(1)}, bf16[128,1280]{1,0:T(8,128)(2,1)S(1)}, u32[]{:S(2)}, u32[]{:S(2)}) collective-permute-start(bf16[128,1280]{1,0:T(8,128)(2,1)S(1)} %get-tuple-element.26), channel_id=1, source_target_pairs={{0,4},{4,8},{8,12},{12,14},{14,10},{10,6},{6,2},{2,0},{1,5},{5,9},... | collective-permute-start | bytes 983048 | tf_op jit(solution)/shard_map/ppermute | solution.py:104
  205.4 13.4 %collective-permute-start.14 = (bf16[128,1280]{1,0:T(8,128)(2,1)S(1)}, bf16[128,1280]{1,0:T(8,128)(2,1)S(1)}, u32[]{:S(2)}, u32[]{:S(2)}) collective-permute-start(bf16[128,1280]{1,0:T(8,128)(2,1)S(1)} %get-tuple-element.25), channel_id=1, source_target_pairs={{0,2},{4,0},{8,4},{12,8},{14,12},{10,14},{6,10},{2,6},{1,3},{5,1},... | collective-permute-start | bytes 983048 | tf_op jit(solution)/shard_map/ppermute | solution.py:96
  210.2 10.1 %collective-permute-start.31 = (f32[240,192]{1,0:T(8,128)S(1)}, f32[240,192]{1,0:T(8,128)S(1)}, u32[]{:S(2)}, u32[]{:S(2)}) collective-permute-start(f32[240,192]{1,0:T(8,128)S(1)} %bitcast_add_fusion.3), channel_id=1, source_target_pairs={{0,2},{4,0},{8,4},{12,8},{14,12},{10,14},{6,10},{2,6},{1,3},{5,1},... | collective-permute-start | bytes 552968 | tf_op jit(solution)/shard_map/ppermute | solution.py:129
  211.8 10.3 %collective-permute-start.24 = (f32[240,192]{1,0:T(8,128)S(1)}, f32[240,192]{1,0:T(8,128)S(1)}, u32[]{:S(2)}, u32[]{:S(2)}) collective-permute-start(f32[240,192]{1,0:T(8,128)S(1)} %bitcast_add_fusion.10), channel_id=1, source_target_pairs={{0,4},{4,8},{8,12},{12,14},{14,10},{10,6},{6,2},{2,0},{1,5},{5,9},... | collective-permute-start | bytes 552968 | tf_op jit(solution)/shard_map/ppermute | solution.py:129
  220.3 7.0 %collective-permute-start.32 = (f32[240,192]{1,0:T(8,128)S(1)}, f32[240,192]{1,0:T(8,128)S(1)}, u32[]{:S(2)}, u32[]{:S(2)}) collective-permute-start(f32[240,192]{1,0:T(8,128)S(1)} %bitcast_add_fusion.2), channel_id=1, source_target_pairs={{0,2},{4,0},{8,4},{12,8},{14,12},{10,14},{6,10},{2,6},{1,3},{5,1},... | collective-permute-start | bytes 552968 | tf_op jit(solution)/shard_map/ppermute | solution.py:129
  222.2 6.5 %collective-permute-start.25 = (f32[240,192]{1,0:T(8,128)S(1)}, f32[240,192]{1,0:T(8,128)S(1)}, u32[]{:S(2)}, u32[]{:S(2)}) collective-permute-start(f32[240,192]{1,0:T(8,128)S(1)} %bitcast_add_fusion.9), channel_id=1, source_target_pairs={{0,4},{4,8},{8,12},{12,14},{14,10},{10,6},{6,2},{2,0},{1,5},{5,9},... | collective-permute-start | bytes 552968 | tf_op jit(solution)/shard_map/ppermute | solution.py:129
  227.3 6.2 %collective-permute-start.33 = (f32[240,192]{1,0:T(8,128)S(1)}, f32[240,192]{1,0:T(8,128)S(1)}, u32[]{:S(2)}, u32[]{:S(2)}) collective-permute-start(f32[240,192]{1,0:T(8,128)S(1)} %bitcast_add_fusion.1), channel_id=1, source_target_pairs={{0,2},{4,0},{8,4},{12,8},{14,12},{10,14},{6,10},{2,6},{1,3},{5,1},... | collective-permute-start | bytes 552968 | tf_op jit(solution)/shard_map/ppermute | solution.py:129
  228.7 6.2 %collective-permute-start.26 = (f32[240,192]{1,0:T(8,128)S(1)}, f32[240,192]{1,0:T(8,128)S(1)}, u32[]{:S(2)}, u32[]{:S(2)}) collective-permute-start(f32[240,192]{1,0:T(8,128)S(1)} %bitcast_add_fusion.8), channel_id=1, source_target_pairs={{0,4},{4,8},{8,12},{12,14},{14,10},{10,6},{6,2},{2,0},{1,5},{5,9},... | collective-permute-start | bytes 552968 | tf_op jit(solution)/shard_map/ppermute | solution.py:129
  (14 other events, 19.7 us)

commit v3 on v2

--- a/solution.py
+++ b/solution.py
@@ -116,18 +116,19 @@
     forward, backward = ring_perms(ring)
     perm = forward if forward_dir else backward
     sign = 1 if forward_dir else -1
-    ring_table = jnp.array(ring, jnp.int32)
-    position_table = jnp.array([ring.index(s) for s in range(count)], jnp.int32)
-    position = position_table[lax.axis_index(axis)]
-
-    def block_at(offset):
-        index = ring_table[(position + count - sign * offset) % count]
-        return lax.dynamic_index_in_dim(blocks, index, axis=0, keepdims=False)
-
-    acc = block_at(1)
+    position = jnp.zeros((), jnp.int32)
+    index = lax.axis_index(axis)
+    for q, s in enumerate(ring):
+        position = jnp.where(index == s, q, position)
+    offsets = (position + count - sign * jnp.arange(count, dtype=jnp.int32)) % count
+    order = jnp.zeros((count,), jnp.int32)
+    for q, s in enumerate(ring):
+        order = jnp.where(offsets == q, s, order)
+    relative = jnp.take(blocks, order, axis=0)
+    acc = relative[1]
     for t in range(count - 1):
         received = lax.ppermute(acc, axis, perm)
-        acc = received + block_at(t + 2)
+        acc = received + relative[(t + 2) % count]
     return acc
 
 

time: 238 us -> 203 us (0.85)
  between operations: 43 us -> 1.29 us
  other arithmetic: 20.4 us -> 25.5 us
  matrix products: 16.6 us -> 12.8 us
  local copies, waits for them, and re-layouts: 47.2 us -> 50.9 us
    gather x0 -> x2, local copies, waits for them, and re-layouts: none -> 7.37 us  [ring_reduce_scatter(): relative = jnp.take(blocks, order, axis=0)]
    ppermute x4, waiting for transfers between devices: 14.8 us -> 19.3 us  [ring_gather(): current = lax.ppermute(current, 'seq', forward)]
    select_n x0 -> x3, other arithmetic: none -> 4.21 us  [the longest x2 3.69 us: ring_reduce_scatter(): relative = jnp.take(blocks, order, axis=0)]
    ppermute x3, waiting for transfers between devices: 4.81 us -> 0.7 us  [ring_gather(): current = lax.ppermute(current, 'seq', backward)]
    unnamed x71 -> x75, local copies, waits for them, and re-layouts: 13.8 us -> 11.8 us
  transfers between devices with their start and end apart: 34 -> 34, of which waited for: 15 -> 19; matrix products, arithmetic and copies ran while one was open for 24% -> 31% of each run, Pallas kernels for 0% -> 0%
where the time goes in v3:
time: 203 us; the launch traced here: 202 us
  waiting for transfers between devices  65.9 us (32%)
  local copies, waits for them, and re-layouts  50.9 us (25%)
  starting transfers between devices  45.1 us (22%)
  other arithmetic  25.5 us (13%)
  matrix products  12.8 us (6%)
    ppermute x14, waiting for transfers between devices, ring_reduce_scatter(): received = lax.ppermute(acc, axis, perm)  31 us
    ppermute x4, waiting for transfers between devices, ring_gather(): current = lax.ppermute(current, 'seq', forward)  19.3 us
    ppermute x14, starting transfers between devices, ring_reduce_scatter(): received = lax.ppermute(acc, axis, perm)  15.2 us
    unnamed x75, local copies, waits for them, and re-layouts  11.8 us
    ppermute x2, starting transfers between devices, extended(): before = lax.ppermute(last, axis, up)  8.44 us
    ppermute x4, starting transfers between devices, ring_gather(): current = lax.ppermute(current, 'seq', forward)  7.75 us
    gather x2, local copies, waits for them, and re-layouts, ring_reduce_scatter(): relative = jnp.take(blocks, order, axis=0)  7.37 us
    ppermute x4, starting transfers between devices, ring_scatter_back(): received = lax.ppermute(acc, 'seq', backward).astype(jnp.float32)  6.62 us
  transfers between devices with their start and end apart: 34, of which 19 were waited for; matrix products, arithmetic and copies ran while one was open for 31% of the time, Pallas kernels for 0%

profile of v3, /device:TPU:0, one launch (start us, length us, event | category | flops | bytes accessed | tf_op | source)
XLA Modules:
  0.0 201.5 jit_solution(15747133972037888687)
XLA Ops:
  3.9 3.1 %collective-permute-start = (bf16[128,1280]{0,1:T(8,128)(2,1)}, bf16[128,1280]{0,1:T(8,128)(2,1)}, u32[]{:S(2)}, u32[]{:S(2)}) collective-permute-start(bf16[128,1280]{0,1:T(8,128)(2,1)} %get-tuple-element.36), channel_id=1, source_target_pairs={{0,4},{4,8},{8,12},{12,14},{14,10},{10,6},{6,2},{2,0},{1,5},{5,9},... | collective-permute-start | bytes 983048 | tf_op jit(solution)/shard_map/ppermute | solution.py:75
  6.9 8.0 %collective-permute-done = bf16[128,1280]{0,1:T(8,128)(2,1)} collective-permute-done((bf16[128,1280]{0,1:T(8,128)(2,1)}, bf16[128,1280]{0,1:T(8,128)(2,1)}, u32[]{:S(2)}, u32[]{:S(2)}) %collective-permute-start) | collective-permute-done | bytes 327712 | tf_op jit(solution)/shard_map/ppermute | solution.py:75
  14.9 1.8 collective-permute-start.1
  19.2 4.9 %collective-permute-done.1 = bf16[128,1280]{0,1:T(8,128)(2,1)} collective-permute-done((bf16[128,1280]{0,1:T(8,128)(2,1)}, bf16[128,1280]{0,1:T(8,128)(2,1)}, u32[]{:S(2)}, u32[]{:S(2)}) %collective-permute-start.1) | collective-permute-done | bytes 327712 | tf_op jit(solution)/shard_map/ppermute | solution.py:75
  26.7 1.8 constant_dynamic-update-slice_fusion.6
  28.5 3.9 %collective-permute-done.2 = bf16[128,1280]{0,1:T(8,128)(2,1)S(1)} collective-permute-done((bf16[128,1280]{0,1:T(8,128)(2,1)}, bf16[128,1280]{0,1:T(8,128)(2,1)S(1)}, u32[]{:S(2)}, u32[]{:S(2)}) %collective-permute-start.2) | collective-permute-done | bytes 327712 | tf_op jit(solution)/shard_map/ppermute | solution.py:75
  33.7 1.8 constant_dynamic-update-slice_fusion.5
  36.9 2.6 %collective-permute-done.3 = bf16[128,1280]{0,1:T(8,128)(2,1)S(1)} collective-permute-done((bf16[128,1280]{0,1:T(8,128)(2,1)S(1)}, bf16[128,1280]{0,1:T(8,128)(2,1)S(1)}, u32[]{:S(2)}, u32[]{:S(2)}) %collective-permute-start.3) | collective-permute-done | bytes 327712 | tf_op jit(solution)/shard_map/ppermute | solution.py:75
  43.3 1.5 slice.202
  44.9 1.9 slice.203
  51.8 2.5 %broadcast_in_dim.56 = f32[1,256,768]{2,1,0:T(8,128)} reshape(f32[128,2,768]{2,1,0:T(2,128)} %broadcast_in_dim.55) | data formatting | bytes 1572864 | tf_op jit(solution)/shard_map/broadcast_in_dim | solution.py:160
  54.4 2.6 %reshape.109 = f32[256,768]{1,0:T(8,128)} reshape(f32[128,2,768]{2,1,0:T(2,128)} %broadcast_in_dim.55) | data formatting | bytes 1572864 | tf_op jit(solution)/shard_map/reshape | solution.py:160
  60.3 2.7 %collective-permute-start.7 = (bf16[2,768]{1,0:T(2,128)(2,1)S(1)}, bf16[2,768]{1,0:T(2,128)(2,1)S(1)}, u32[]{:S(2)}, u32[]{:S(2)}) collective-permute-start(bf16[2,768]{1,0:T(2,128)(2,1)S(1)} %get-tuple-element.35), channel_id=1, source_target_pairs={{0,2},{2,4},{4,6},{6,8},{8,10},{10,12},{12,14},{1,3},{3,5},{5,7},{... | collective-permute-start | bytes 9224 | tf_op jit(solution)/shard_map/ppermute | solution.py:24
  65.1 4.3 %collective-permute-done.8 = bf16[2,768]{1,0:T(2,128)(2,1)S(1)} collective-permute-done((bf16[2,768]{1,0:T(2,128)(2,1)S(1)}, bf16[2,768]{1,0:T(2,128)(2,1)S(1)}, u32[]{:S(2)}, u32[]{:S(2)}) %collective-permute-start.8) | collective-permute-done | bytes 3104 | tf_op jit(solution)/shard_map/ppermute | solution.py:25
  69.7 2.0 fusion.26
  74.1 5.8 %collective-permute-start.10 = (bf16[2,384]{1,0:T(2,128)(2,1)}, bf16[2,384]{1,0:T(2,128)(2,1)S(1)}, u32[]{:S(2)}, u32[]{:S(2)}) collective-permute-start(bf16[2,384]{1,0:T(2,128)(2,1)} %get-tuple-element.38), channel_id=1, source_target_pairs={{0,2},{2,4},{4,6},{6,8},{8,10},{10,12},{12,14},{1,3},{3,5},{5,7},{... | collective-permute-start | bytes 4616 | tf_op jit(solution)/shard_map/ppermute | solution.py:24
  84.0 2.7 %reshape.111 = f32[128,2,768]{2,1,0:T(2,128)} reshape(f32[256,768]{1,0:T(8,128)} %get-tuple-element.23) | data formatting | bytes 1572864 | tf_op jit(solution)/shard_map/reshape | solution.py:226
  86.6 2.1 %reduce_sum.48 = bf16[128,768]{1,0:T(8,128)(2,1)S(1)} reduce(f32[128,2,768]{2,1,0:T(2,128)} %reshape.111, f32[]{:T(128)} %constant.33.clone.1), dimensions={1}, to_apply=%region_4.5 | reduce | flops 98304 | bytes 983044 | tf_op jit(solution)/shard_map/reduce_sum | solution.py:226
  89.0 1.8 convolution_convert_fusion
  90.8 2.1 %multiply_convert_fusion.1 = bf16[4,128,1024]{1,2,0:T(8,128)(2,1)} fusion(f32[4,1024,128]{2,1,0:T(8,128)S(1)} %copy-done.3, bf16[128,4,192]{0,2,1:T(8,128)(2,1)S(1)} %bitcast.181, bf16[1024,4,192]{0,2,1:T(8,128)(2,1)S(1)} %bitcast.172, f32[4,128]{1,0:T(4,128)S(1)} %bitcast.188, f32[4,128]{1,0:T(4,128)S(1)} %copy-done.24), kind=kOutput, calls=%fused_computation.24 | convolution fusion | flops 203948032 | bytes 4919296 | tf_op jit(solution)/shard_map/ihd,jhd->hij/dot_general | solution.py:229
  92.9 1.8 copy.45
  96.2 2.3 %copy.42 = bf16[1024,4,128]{0,2,1:T(8,128)(2,1)} copy(bf16[1024,4,128]{2,0,1:T(8,128)(2,1)} %fusion.10) | data formatting | bytes 2097152 | tf_op jit(solution)/shard_map/mul | solution.py:238
  100.9 2.9 %collective-permute-start.11 = (bf16[128,1280]{1,0:T(8,128)(2,1)}, bf16[128,1280]{1,0:T(8,128)(2,1)}, u32[]{:S(2)}, u32[]{:S(2)}) collective-permute-start(bf16[128,1280]{1,0:T(8,128)(2,1)} %get-tuple-element.30), channel_id=1, source_target_pairs={{0,2},{4,0},{8,4},{12,8},{14,12},{10,14},{6,10},{2,6},{1,3},{5,1},... | collective-permute-start | bytes 983048 | tf_op jit(solution)/shard_map/ppermute | solution.py:96
  107.3 5.3 %collective-permute-done.11 = bf16[128,1280]{1,0:T(8,128)(2,1)} collective-permute-done((bf16[128,1280]{1,0:T(8,128)(2,1)}, bf16[128,1280]{1,0:T(8,128)(2,1)}, u32[]{:S(2)}, u32[]{:S(2)}) %collective-permute-start.11) | collective-permute-done | bytes 327712 | tf_op jit(solution)/shard_map/ppermute | solution.py:96
  115.4 2.2 %pad_maximum_fusion = bf16[512,3840]{1,0:T(8,128)(2,1)} fusion(bf16[256,3840]{1,0:T(8,128)(2,1)S(1)} %slice_dynamic-update-slice_fusion, bf16[256,3840]{1,0:T(8,128)(2,1)S(1)} %copy-done.18), kind=kLoop, calls=%fused_computation.9 | loop fusion | flops 7864320 | bytes 7864320 | tf_op jit(solution)/shard_map/concatenate | solution.py:178
  117.6 6.3 %copy.46 = bf16[512,3840]{0,1:T(8,128)(2,1)} copy(bf16[512,3840]{1,0:T(8,128)(2,1)} %pad_maximum_fusion) | data formatting | bytes 7864320 | tf_op jit(solution)/shard_map/concatenate | solution.py:178
  123.9 2.8 %fusion.7 = f32[8,240,384]{2,1,0:T(8,128)S(1)} fusion(bf16[512,8,2,240]{0,3,2,1:T(8,128)(2,1)} %bitcast.175, s32[]{:T(128)S(6)} %select_n.98, bf16[256,384]{1,0:T(8,128)(2,1)} %collective-permute-done.19, bf16[256,384]{1,0:T(8,128)(2,1)S(1)} %get-tuple-element.32), kind=kOutput, calls=%fused_computation.29 | convolution fusion | flops 756498432 | bytes 5308420 | tf_op jit(solution)/shard_map/psr,po->sro/dot_general | solution.py:183
  126.6 2.6 %fusion.72 = (f32[8,240,192]{2,1,0:T(8,128)}, f32[8,240,192]{2,1,0:T(8,128)}) fusion(f32[8,240,384]{2,1,0:T(8,128)S(1)} %fusion.7), kind=kLoop, calls=%fused_computation.191 | loop fusion | bytes 5898240 | tf_op jit(solution)/shard_map/slice | solution.py:205
  129.2 3.7 %gather_fusion.1 = f32[8,240,192]{2,1,0:T(8,128)} fusion(f32[8,240,192]{2,1,0:T(8,128)} %get-tuple-element.25, s32[1024]{0:T(1024)} %pad_clamp_fusion), kind=kCustom, calls=%fused_computation.1.clone | custom fusion | bytes 2949152 | tf_op jit(solution)/shard_map/jit(_take)/gather | solution.py:127
  132.9 1.8 broadcast_select_fusion
  136.0 1.6 collective-permute-start.27
  137.6 3.7 %gather_fusion = f32[8,240,192]{2,1,0:T(8,128)} fusion(f32[8,240,192]{2,1,0:T(8,128)} %get-tuple-element.24, s32[1024]{0:T(1024)} %pad_clamp_fusion.1), kind=kCustom, calls=%fused_computation.clone | custom fusion | bytes 2949152 | tf_op jit(solution)/shard_map/jit(_take)/gather | solution.py:127
  141.3 1.9 broadcast_select_fusion.1
  143.8 1.6 collective-permute-start.28
  145.4 4.4 %collective-permute-done.20 = f32[240,192]{1,0:T(8,128)S(1)} collective-permute-done((f32[240,192]{1,0:T(8,128)S(1)}, f32[240,192]{1,0:T(8,128)S(1)}, u32[]{:S(2)}, u32[]{:S(2)}) %collective-permute-start.20) | collective-permute-done | bytes 184352 | tf_op jit(solution)/shard_map/ppermute | solution.py:130
  151.6 1.6 collective-permute-start.13
  153.7 1.6 collective-permute-start.29
  155.3 3.4 %collective-permute-done.21 = f32[240,192]{1,0:T(8,128)S(1)} collective-permute-done((f32[240,192]{1,0:T(8,128)S(1)}, f32[240,192]{1,0:T(8,128)S(1)}, u32[]{:S(2)}, u32[]{:S(2)}) %collective-permute-start.21) | collective-permute-done | bytes 184352 | tf_op jit(solution)/shard_map/ppermute | solution.py:130
  159.3 5.4 %collective-permute-done.29 = f32[240,192]{1,0:T(8,128)S(1)} collective-permute-done((f32[240,192]{1,0:T(8,128)S(1)}, f32[240,192]{1,0:T(8,128)S(1)}, u32[]{:S(2)}, u32[]{:S(2)}) %collective-permute-start.29) | collective-permute-done | bytes 184352 | tf_op jit(solution)/shard_map/ppermute | solution.py:130
  164.7 1.6 collective-permute-start.30
  166.4 1.9 collective-permute-done.22
  171.0 2.6 %collective-permute-done.30 = f32[240,192]{1,0:T(8,128)S(1)} collective-permute-done((f32[240,192]{1,0:T(8,128)S(1)}, f32[240,192]{1,0:T(8,128)S(1)}, u32[]{:S(2)}, u32[]{:S(2)}) %collective-permute-start.30) | collective-permute-done | bytes 184352 | tf_op jit(solution)/shard_map/ppermute | solution.py:130
  173.7 1.6 collective-permute-start.31
  175.3 1.9 collective-permute-done.23
  177.7 5.2 %collective-permute-done.17 = bf16[128,1280]{1,0:T(8,128)(2,1)S(1)} collective-permute-done((bf16[128,1280]{1,0:T(8,128)(2,1)S(1)}, bf16[128,1280]{1,0:T(8,128)(2,1)S(1)}, u32[]{:S(2)}, u32[]{:S(2)}) %collective-permute-start.17) | collective-permute-done | bytes 327712 | tf_op jit(solution)/shard_map/ppermute | solution.py:104
  184.4 1.6 collective-permute-start.32
  187.1 5.7 %collective-permute-done.32 = f32[240,192]{1,0:T(8,128)S(1)} collective-permute-done((f32[240,192]{1,0:T(8,128)S(1)}, f32[240,192]{1,0:T(8,128)S(1)}, u32[]{:S(2)}, u32[]{:S(2)}) %collective-permute-start.32) | collective-permute-done | bytes 184352 | tf_op jit(solution)/shard_map/ppermute | solution.py:130
  195.4 3.7 %collective-permute-done.33 = f32[240,192]{1,0:T(8,128)S(1)} collective-permute-done((f32[240,192]{1,0:T(8,128)S(1)}, f32[240,192]{1,0:T(8,128)S(1)}, u32[]{:S(2)}, u32[]{:S(2)}) %collective-permute-start.33) | collective-permute-done | bytes 184352 | tf_op jit(solution)/shard_map/ppermute | solution.py:130
  (176 shorter events, 58.0 us)
Async XLA Ops:
  0.6 69.0 %copy-start = (bf16[3840,384]{1,0:T(8,128)(2,1)S(1)}, bf16[3840,384]{1,0:T(8,128)(2,1)}, u32[]{:S(2)}) copy-start(bf16[3840,384]{1,0:T(8,128)(2,1)} %param.16) | copy-start | bytes 8847364
  3.9 11.0 %collective-permute-start = (bf16[128,1280]{0,1:T(8,128)(2,1)}, bf16[128,1280]{0,1:T(8,128)(2,1)}, u32[]{:S(2)}, u32[]{:S(2)}) collective-permute-start(bf16[128,1280]{0,1:T(8,128)(2,1)} %get-tuple-element.36), channel_id=1, source_target_pairs={{0,4},{4,8},{8,12},{12,14},{14,10},{10,6},{6,2},{2,0},{1,5},{5,9},... | collective-permute-start | bytes 983048 | tf_op jit(solution)/shard_map/ppermute | solution.py:75
  14.9 9.2 %collective-permute-start.1 = (bf16[128,1280]{0,1:T(8,128)(2,1)}, bf16[128,1280]{0,1:T(8,128)(2,1)}, u32[]{:S(2)}, u32[]{:S(2)}) collective-permute-start(bf16[128,1280]{0,1:T(8,128)(2,1)} %collective-permute-done), channel_id=1, source_target_pairs={{0,4},{4,8},{8,12},{12,14},{14,10},{10,6},{6,2},{2,0},{1,5},{5,9},... | collective-permute-start | bytes 983048 | tf_op jit(solution)/shard_map/ppermute | solution.py:75
  16.7 9.5 %collective-permute-start.4 = (bf16[128,1280]{0,1:T(8,128)(2,1)}, bf16[128,1280]{0,1:T(8,128)(2,1)S(1)}, u32[]{:S(2)}, u32[]{:S(2)}) collective-permute-start(bf16[128,1280]{0,1:T(8,128)(2,1)} %get-tuple-element.36), channel_id=1, source_target_pairs={{0,2},{4,0},{8,4},{12,8},{14,12},{10,14},{6,10},{2,6},{1,3},{5,1},... | collective-permute-start | bytes 983048 | tf_op jit(solution)/shard_map/ppermute | solution.py:79
  18.6 28.1 %copy-start.19 = (bf16[1,128,512]{1,2,0:T(8,128)(2,1)}, bf16[1,128,512]{1,2,0:T(8,128)(2,1)S(1)}, u32[]{:S(2)}) copy-start(bf16[1,128,512]{1,2,0:T(8,128)(2,1)S(1)} %copy.55) | copy-start | bytes 393220
  24.1 8.2 %collective-permute-start.2 = (bf16[128,1280]{0,1:T(8,128)(2,1)}, bf16[128,1280]{0,1:T(8,128)(2,1)S(1)}, u32[]{:S(2)}, u32[]{:S(2)}) collective-permute-start(bf16[128,1280]{0,1:T(8,128)(2,1)} %collective-permute-done.1), channel_id=1, source_target_pairs={{0,4},{4,8},{8,12},{12,14},{14,10},{10,6},{6,2},{2,0},{1,5},{5,9},... | collective-permute-start | bytes 983048 | tf_op jit(solution)/shard_map/ppermute | solution.py:75
  26.2 9.3 %collective-permute-start.5 = (bf16[128,1280]{0,1:T(8,128)(2,1)S(1)}, bf16[128,1280]{0,1:T(8,128)(2,1)S(1)}, u32[]{:S(2)}, u32[]{:S(2)}) collective-permute-start(bf16[128,1280]{0,1:T(8,128)(2,1)S(1)} %collective-permute-done.4), channel_id=1, source_target_pairs={{0,2},{4,0},{8,4},{12,8},{14,12},{10,14},{6,10},{2,6},{1,3},{5,1},... | collective-permute-start | bytes 983048 | tf_op jit(solution)/shard_map/ppermute | solution.py:79
  32.3 7.2 %collective-permute-start.3 = (bf16[128,1280]{0,1:T(8,128)(2,1)S(1)}, bf16[128,1280]{0,1:T(8,128)(2,1)S(1)}, u32[]{:S(2)}, u32[]{:S(2)}) collective-permute-start(bf16[128,1280]{0,1:T(8,128)(2,1)S(1)} %collective-permute-done.2), channel_id=1, source_target_pairs={{0,4},{4,8},{8,12},{12,14},{14,10},{10,6},{6,2},{2,0},{1,5},{5,9},... | collective-permute-start | bytes 983048 | tf_op jit(solution)/shard_map/ppermute | solution.py:75
  35.4 7.1 %collective-permute-start.6 = (bf16[128,1280]{0,1:T(8,128)(2,1)S(1)}, bf16[128,1280]{0,1:T(8,128)(2,1)S(1)}, u32[]{:S(2)}, u32[]{:S(2)}) collective-permute-start(bf16[128,1280]{0,1:T(8,128)(2,1)S(1)} %collective-permute-done.5), channel_id=1, source_target_pairs={{0,2},{4,0},{8,4},{12,8},{14,12},{10,14},{6,10},{2,6},{1,3},{5,1},... | collective-permute-start | bytes 983048 | tf_op jit(solution)/shard_map/ppermute | solution.py:79
  50.6 6.3 %copy-start.13 = (bf16[1,256,768]{2,1,0:T(8,128)(2,1)S(1)}, bf16[1,256,768]{2,1,0:T(8,128)(2,1)}, u32[]{:S(2)}) copy-start(bf16[1,256,768]{2,1,0:T(8,128)(2,1)} %param.14) | copy-start | bytes 1179652
  54.4 8.6 %copy-start.28 = (s32[8]{0:T(128)S(1)}, s32[8]{0:T(128)}, u32[]{:S(2)}) copy-start(s32[8]{0:T(128)} %get-tuple-element.47) | copy-start | bytes 100
  60.2 9.4 %copy-start.29 = (bf16[1,256,384]{2,1,0:T(8,128)(2,1)S(1)}, bf16[1,256,384]{2,1,0:T(8,128)(2,1)}, u32[]{:S(2)}) copy-start(bf16[1,256,384]{2,1,0:T(8,128)(2,1)} %param.17) | copy-start | bytes 589828
  60.3 4.6 %collective-permute-start.7 = (bf16[2,768]{1,0:T(2,128)(2,1)S(1)}, bf16[2,768]{1,0:T(2,128)(2,1)S(1)}, u32[]{:S(2)}, u32[]{:S(2)}) collective-permute-start(bf16[2,768]{1,0:T(2,128)(2,1)S(1)} %get-tuple-element.35), channel_id=1, source_target_pairs={{0,2},{2,4},{4,6},{6,8},{8,10},{10,12},{12,14},{1,3},{3,5},{5,7},{... | collective-permute-start | bytes 9224 | tf_op jit(solution)/shard_map/ppermute | solution.py:24
  63.6 5.9 %collective-permute-start.8 = (bf16[2,768]{1,0:T(2,128)(2,1)S(1)}, bf16[2,768]{1,0:T(2,128)(2,1)S(1)}, u32[]{:S(2)}, u32[]{:S(2)}) collective-permute-start(bf16[2,768]{1,0:T(2,128)(2,1)S(1)} %get-tuple-element.34), channel_id=1, source_target_pairs={{2,0},{4,2},{6,4},{8,6},{10,8},{12,10},{14,12},{3,1},{5,3},{7,5},{... | collective-permute-start | bytes 9224 | tf_op jit(solution)/shard_map/ppermute | solution.py:25
  72.2 7.6 %collective-permute-start.9 = (bf16[2,384]{1,0:T(2,128)(2,1)}, bf16[2,384]{1,0:T(2,128)(2,1)}, u32[]{:S(2)}, u32[]{:S(2)}) collective-permute-start(bf16[2,384]{1,0:T(2,128)(2,1)} %get-tuple-element.39), channel_id=1, source_target_pairs={{2,0},{4,2},{6,4},{8,6},{10,8},{12,10},{14,12},{3,1},{5,3},{7,5},{... | collective-permute-start | bytes 4616 | tf_op jit(solution)/shard_map/ppermute | solution.py:25
  74.1 7.5 %copy-start.6 = (f32[256,768]{1,0:T(8,128)S(1)}, f32[256,768]{1,0:T(8,128)}, u32[]{:S(2)}) copy-start(f32[256,768]{1,0:T(8,128)} %reshape.109) | copy-start | bytes 2359300
  74.1 7.5 %copy-start.14 = (bf16[1,256,768]{2,1,0:T(8,128)(2,1)S(1)}, bf16[1,256,768]{2,1,0:T(8,128)(2,1)}, u32[]{:S(2)}) copy-start(bf16[1,256,768]{2,1,0:T(8,128)(2,1)} %param.14) | copy-start | bytes 1179652
  74.1 49.8 %collective-permute-start.19 = (bf16[256,384]{1,0:T(8,128)(2,1)S(1)}, bf16[256,384]{1,0:T(8,128)(2,1)}, u32[]{:S(2)}, u32[]{:S(2)}) collective-permute-start(bf16[256,384]{1,0:T(8,128)(2,1)S(1)} %get-tuple-element.32), channel_id=1, source_target_pairs={{0,1},{1,0},{2,3},{3,2},{4,5},{5,4},{6,7},{7,6},{8,9},{9,8},{10,11... | collective-permute-start | bytes 589832 | tf_op jit(solution)/shard_map/ppermute | solution.py:177
  74.1 7.3 %collective-permute-start.10 = (bf16[2,384]{1,0:T(2,128)(2,1)}, bf16[2,384]{1,0:T(2,128)(2,1)S(1)}, u32[]{:S(2)}, u32[]{:S(2)}) collective-permute-start(bf16[2,384]{1,0:T(2,128)(2,1)} %get-tuple-element.38), channel_id=1, source_target_pairs={{0,2},{2,4},{4,6},{6,8},{8,10},{10,12},{12,14},{1,3},{3,5},{5,7},{... | collective-permute-start | bytes 4616 | tf_op jit(solution)/shard_map/ppermute | solution.py:24
  84.0 5.0 %copy-start.16 = (f32[4,192,128]{2,1,0:T(8,128)S(1)}, f32[4,192,128]{2,1,0:T(8,128)}, u32[]{:S(2)}) copy-start(f32[4,192,128]{2,1,0:T(8,128)} %copy-done.15) | copy-start | bytes 1179652
  84.0 5.0 %copy-start.3 = (f32[4,1024,128]{2,1,0:T(8,128)S(1)}, f32[4,1024,128]{2,1,0:T(8,128)}, u32[]{:S(2)}) copy-start(f32[4,1024,128]{2,1,0:T(8,128)} %copy-done.2) | copy-start | bytes 6291460
  84.0 5.0 %copy-start.24 = (f32[4,128]{1,0:T(4,128)S(1)}, f32[4,128]{1,0:T(4,128)}, u32[]{:S(2)}) copy-start(f32[4,128]{1,0:T(4,128)} %copy-done.23) | copy-start | bytes 6148
  99.9 4.7 %copy-start.8 = (bf16[1024,512]{0,1:T(8,128)(2,1)S(1)}, bf16[1024,512]{0,1:T(8,128)(2,1)}, u32[]{:S(2)}) copy-start(bf16[1024,512]{0,1:T(8,128)(2,1)} %copy-done.7) | copy-start | bytes 3145732
  99.9 4.7 %copy-start.10 = (bf16[4,128,1024]{1,2,0:T(8,128)(2,1)S(1)}, bf16[4,128,1024]{1,2,0:T(8,128)(2,1)}, u32[]{:S(2)}) copy-start(bf16[4,128,1024]{1,2,0:T(8,128)(2,1)} %multiply_convert_fusion.1) | copy-start | bytes 3145732
  100.9 11.8 %collective-permute-start.11 = (bf16[128,1280]{1,0:T(8,128)(2,1)}, bf16[128,1280]{1,0:T(8,128)(2,1)}, u32[]{:S(2)}, u32[]{:S(2)}) collective-permute-start(bf16[128,1280]{1,0:T(8,128)(2,1)} %get-tuple-element.30), channel_id=1, source_target_pairs={{0,2},{4,0},{8,4},{12,8},{14,12},{10,14},{6,10},{2,6},{1,3},{5,1},... | collective-permute-start | bytes 983048 | tf_op jit(solution)/shard_map/ppermute | solution.py:96
  104.7 10.3 %collective-permute-start.18 = (bf16[260,768]{1,0:T(8,128)(2,1)}, bf16[260,768]{1,0:T(8,128)(2,1)S(1)}, u32[]{:S(2)}, u32[]{:S(2)}) collective-permute-start(bf16[260,768]{1,0:T(8,128)(2,1)} %pad_maximum_fusion.1), channel_id=1, source_target_pairs={{0,1},{1,0},{2,3},{3,2},{4,5},{5,4},{6,7},{7,6},{8,9},{9,8},{10,11... | collective-permute-start | bytes 1198088 | tf_op jit(solution)/shard_map/ppermute | solution.py:176
  105.9 44.5 %collective-permute-start.15 = (bf16[128,1280]{1,0:T(8,128)(2,1)}, bf16[128,1280]{1,0:T(8,128)(2,1)}, u32[]{:S(2)}, u32[]{:S(2)}) collective-permute-start(bf16[128,1280]{1,0:T(8,128)(2,1)} %get-tuple-element.31), channel_id=1, source_target_pairs={{0,4},{4,8},{8,12},{12,14},{14,10},{10,6},{6,2},{2,0},{1,5},{5,9},... | collective-permute-start | bytes 983048 | tf_op jit(solution)/shard_map/ppermute | solution.py:104
  113.7 36.6 %collective-permute-start.12 = (bf16[128,1280]{1,0:T(8,128)(2,1)S(1)}, bf16[128,1280]{1,0:T(8,128)(2,1)}, u32[]{:S(2)}, u32[]{:S(2)}) collective-permute-start(bf16[128,1280]{1,0:T(8,128)(2,1)S(1)} %add_convert_fusion.5), channel_id=1, source_target_pairs={{0,2},{4,0},{8,4},{12,8},{14,12},{10,14},{6,10},{2,6},{1,3},{5,1},... | collective-permute-start | bytes 983048 | tf_op jit(solution)/shard_map/ppermute | solution.py:96
  136.0 5.3 %copy-start.26 = (pred[8]{0:T(512)(128)(4,1)S(1)}, pred[8]{0:T(512)(128)(4,1)}, u32[]{:S(2)}) copy-start(pred[8]{0:T(512)(128)(4,1)} %get-tuple-element.49) | copy-start | bytes 28
  136.0 7.8 %collective-permute-start.27 = (f32[240,192]{1,0:T(8,128)S(1)}, f32[240,192]{1,0:T(8,128)S(1)}, u32[]{:S(2)}, u32[]{:S(2)}) collective-permute-start(f32[240,192]{1,0:T(8,128)S(1)} %slice_bitcast_fusion.7), channel_id=1, source_target_pairs={{0,2},{4,0},{8,4},{12,8},{14,12},{10,14},{6,10},{2,6},{1,3},{5,1},... | collective-permute-start | bytes 552968 | tf_op jit(solution)/shard_map/ppermute | solution.py:130
  143.2 6.6 %collective-permute-start.20 = (f32[240,192]{1,0:T(8,128)S(1)}, f32[240,192]{1,0:T(8,128)S(1)}, u32[]{:S(2)}, u32[]{:S(2)}) collective-permute-start(f32[240,192]{1,0:T(8,128)S(1)} %slice_bitcast_fusion.15), channel_id=1, source_target_pairs={{0,4},{4,8},{8,12},{12,14},{14,10},{10,6},{6,2},{2,0},{1,5},{5,9},... | collective-permute-start | bytes 552968 | tf_op jit(solution)/shard_map/ppermute | solution.py:130
  143.8 9.9 %collective-permute-start.28 = (f32[240,192]{1,0:T(8,128)S(1)}, f32[240,192]{1,0:T(8,128)S(1)}, u32[]{:S(2)}, u32[]{:S(2)}) collective-permute-start(f32[240,192]{1,0:T(8,128)S(1)} %fusion.45), channel_id=1, source_target_pairs={{0,2},{4,0},{8,4},{12,8},{14,12},{10,14},{6,10},{2,6},{1,3},{5,1},... | collective-permute-start | bytes 552968 | tf_op jit(solution)/shard_map/ppermute | solution.py:130
  149.9 8.9 %collective-permute-start.21 = (f32[240,192]{1,0:T(8,128)S(1)}, f32[240,192]{1,0:T(8,128)S(1)}, u32[]{:S(2)}, u32[]{:S(2)}) collective-permute-start(f32[240,192]{1,0:T(8,128)S(1)} %fusion.52), channel_id=1, source_target_pairs={{0,4},{4,8},{8,12},{12,14},{14,10},{10,6},{6,2},{2,0},{1,5},{5,9},... | collective-permute-start | bytes 552968 | tf_op jit(solution)/shard_map/ppermute | solution.py:130
  151.6 17.2 %collective-permute-start.13 = (bf16[128,1280]{1,0:T(8,128)(2,1)S(1)}, bf16[128,1280]{1,0:T(8,128)(2,1)S(1)}, u32[]{:S(2)}, u32[]{:S(2)}) collective-permute-start(bf16[128,1280]{1,0:T(8,128)(2,1)S(1)} %get-tuple-element.28), channel_id=1, source_target_pairs={{0,2},{4,0},{8,4},{12,8},{14,12},{10,14},{6,10},{2,6},{1,3},{5,1},... | collective-permute-start | bytes 983048 | tf_op jit(solution)/shard_map/ppermute | solution.py:96
  153.2 15.6 %collective-permute-start.16 = (bf16[128,1280]{1,0:T(8,128)(2,1)S(1)}, bf16[128,1280]{1,0:T(8,128)(2,1)S(1)}, u32[]{:S(2)}, u32[]{:S(2)}) collective-permute-start(bf16[128,1280]{1,0:T(8,128)(2,1)S(1)} %get-tuple-element.29), channel_id=1, source_target_pairs={{0,4},{4,8},{8,12},{12,14},{14,10},{10,6},{6,2},{2,0},{1,5},{5,9},... | collective-permute-start | bytes 983048 | tf_op jit(solution)/shard_map/ppermute | solution.py:104
  153.7 11.0 %collective-permute-start.29 = (f32[240,192]{1,0:T(8,128)S(1)}, f32[240,192]{1,0:T(8,128)S(1)}, u32[]{:S(2)}, u32[]{:S(2)}) collective-permute-start(f32[240,192]{1,0:T(8,128)S(1)} %fusion.44), channel_id=1, source_target_pairs={{0,2},{4,0},{8,4},{12,8},{14,12},{10,14},{6,10},{2,6},{1,3},{5,1},... | collective-permute-start | bytes 552968 | tf_op jit(solution)/shard_map/ppermute | solution.py:130
  158.8 9.5 %collective-permute-start.22 = (f32[240,192]{1,0:T(8,128)S(1)}, f32[240,192]{1,0:T(8,128)S(1)}, u32[]{:S(2)}, u32[]{:S(2)}) collective-permute-start(f32[240,192]{1,0:T(8,128)S(1)} %fusion.51), channel_id=1, source_target_pairs={{0,4},{4,8},{8,12},{12,14},{14,10},{10,6},{6,2},{2,0},{1,5},{5,9},... | collective-permute-start | bytes 552968 | tf_op jit(solution)/shard_map/ppermute | solution.py:130
  164.7 8.9 %collective-permute-start.30 = (f32[240,192]{1,0:T(8,128)S(1)}, f32[240,192]{1,0:T(8,128)S(1)}, u32[]{:S(2)}, u32[]{:S(2)}) collective-permute-start(f32[240,192]{1,0:T(8,128)S(1)} %fusion.43), channel_id=1, source_target_pairs={{0,2},{4,0},{8,4},{12,8},{14,12},{10,14},{6,10},{2,6},{1,3},{5,1},... | collective-permute-start | bytes 552968 | tf_op jit(solution)/shard_map/ppermute | solution.py:130
  168.3 8.9 %collective-permute-start.23 = (f32[240,192]{1,0:T(8,128)S(1)}, f32[240,192]{1,0:T(8,128)S(1)}, u32[]{:S(2)}, u32[]{:S(2)}) collective-permute-start(f32[240,192]{1,0:T(8,128)S(1)} %fusion.50), channel_id=1, source_target_pairs={{0,4},{4,8},{8,12},{12,14},{14,10},{10,6},{6,2},{2,0},{1,5},{5,9},... | collective-permute-start | bytes 552968 | tf_op jit(solution)/shard_map/ppermute | solution.py:130
  168.9 14.0 %collective-permute-start.17 = (bf16[128,1280]{1,0:T(8,128)(2,1)S(1)}, bf16[128,1280]{1,0:T(8,128)(2,1)S(1)}, u32[]{:S(2)}, u32[]{:S(2)}) collective-permute-start(bf16[128,1280]{1,0:T(8,128)(2,1)S(1)} %get-tuple-element.27), channel_id=1, source_target_pairs={{0,4},{4,8},{8,12},{12,14},{14,10},{10,6},{6,2},{2,0},{1,5},{5,9},... | collective-permute-start | bytes 983048 | tf_op jit(solution)/shard_map/ppermute | solution.py:104
  170.1 12.8 %collective-permute-start.14 = (bf16[128,1280]{1,0:T(8,128)(2,1)S(1)}, bf16[128,1280]{1,0:T(8,128)(2,1)S(1)}, u32[]{:S(2)}, u32[]{:S(2)}) collective-permute-start(bf16[128,1280]{1,0:T(8,128)(2,1)S(1)} %get-tuple-element.26), channel_id=1, source_target_pairs={{0,2},{4,0},{8,4},{12,8},{14,12},{10,14},{6,10},{2,6},{1,3},{5,1},... | collective-permute-start | bytes 983048 | tf_op jit(solution)/shard_map/ppermute | solution.py:96
  173.7 10.7 %collective-permute-start.31 = (f32[240,192]{1,0:T(8,128)S(1)}, f32[240,192]{1,0:T(8,128)S(1)}, u32[]{:S(2)}, u32[]{:S(2)}) collective-permute-start(f32[240,192]{1,0:T(8,128)S(1)} %fusion.42), channel_id=1, source_target_pairs={{0,2},{4,0},{8,4},{12,8},{14,12},{10,14},{6,10},{2,6},{1,3},{5,1},... | collective-permute-start | bytes 552968 | tf_op jit(solution)/shard_map/ppermute | solution.py:130
  177.2 9.2 %collective-permute-start.24 = (f32[240,192]{1,0:T(8,128)S(1)}, f32[240,192]{1,0:T(8,128)S(1)}, u32[]{:S(2)}, u32[]{:S(2)}) collective-permute-start(f32[240,192]{1,0:T(8,128)S(1)} %fusion.49), channel_id=1, source_target_pairs={{0,4},{4,8},{8,12},{12,14},{14,10},{10,6},{6,2},{2,0},{1,5},{5,9},... | collective-permute-start | bytes 552968 | tf_op jit(solution)/shard_map/ppermute | solution.py:130
  184.4 17.1 %copy-start.1 = (bf16[3840,384]{1,0:T(8,128)(2,1)S(1)}, bf16[3840,384]{1,0:T(8,128)(2,1)}, u32[]{:S(2)}) copy-start(bf16[3840,384]{1,0:T(8,128)(2,1)} %param.16) | copy-start | bytes 8847364
  184.4 8.4 %collective-permute-start.32 = (f32[240,192]{1,0:T(8,128)S(1)}, f32[240,192]{1,0:T(8,128)S(1)}, u32[]{:S(2)}, u32[]{:S(2)}) collective-permute-start(f32[240,192]{1,0:T(8,128)S(1)} %fusion.41), channel_id=1, source_target_pairs={{0,2},{4,0},{8,4},{12,8},{14,12},{10,14},{6,10},{2,6},{1,3},{5,1},... | collective-permute-start | bytes 552968 | tf_op jit(solution)/shard_map/ppermute | solution.py:130
  186.4 7.9 %collective-permute-start.25 = (f32[240,192]{1,0:T(8,128)S(1)}, f32[240,192]{1,0:T(8,128)S(1)}, u32[]{:S(2)}, u32[]{:S(2)}) collective-permute-start(f32[240,192]{1,0:T(8,128)S(1)} %fusion.48), channel_id=1, source_target_pairs={{0,4},{4,8},{8,12},{12,14},{14,10},{10,6},{6,2},{2,0},{1,5},{5,9},... | collective-permute-start | bytes 552968 | tf_op jit(solution)/shard_map/ppermute | solution.py:130
  192.8 6.2 %collective-permute-start.33 = (f32[240,192]{1,0:T(8,128)S(1)}, f32[240,192]{1,0:T(8,128)S(1)}, u32[]{:S(2)}, u32[]{:S(2)}) collective-permute-start(f32[240,192]{1,0:T(8,128)S(1)} %fusion.40), channel_id=1, source_target_pairs={{0,2},{4,0},{8,4},{12,8},{14,12},{10,14},{6,10},{2,6},{1,3},{5,1},... | collective-permute-start | bytes 552968 | tf_op jit(solution)/shard_map/ppermute | solution.py:130
  194.4 6.2 %collective-permute-start.26 = (f32[240,192]{1,0:T(8,128)S(1)}, f32[240,192]{1,0:T(8,128)S(1)}, u32[]{:S(2)}, u32[]{:S(2)}) collective-permute-start(f32[240,192]{1,0:T(8,128)S(1)} %fusion.47), channel_id=1, source_target_pairs={{0,4},{4,8},{8,12},{12,14},{14,10},{10,6},{6,2},{2,0},{1,5},{5,9},... | collective-permute-start | bytes 552968 | tf_op jit(solution)/shard_map/ppermute | solution.py:130
  (16 other events, 29.7 us)

commit v4 on v3

--- a/solution.py
+++ b/solution.py
@@ -132,6 +132,35 @@
     return acc
 
 
+def ring_position(axis, ring):
+    position = jnp.zeros((), jnp.int32)
+    index = lax.axis_index(axis)
+    for q, s in enumerate(ring):
+        position = jnp.where(index == s, q, position)
+    return position
+
+
+def ring_reduce_scatter_sliced(select_block, axis, ring, forward_dir=True):
+    count = len(ring)
+    forward, backward = ring_perms(ring)
+    perm = forward if forward_dir else backward
+    sign = 1 if forward_dir else -1
+    position = ring_position(axis, ring)
+
+    def block_at(offset):
+        target = (position + count - sign * (offset % count)) % count
+        index = jnp.zeros((), jnp.int32)
+        for q, s in enumerate(ring):
+            index = jnp.where(target == q, s, index)
+        return select_block(index)
+
+    acc = block_at(1)
+    for t in range(count - 1):
+        received = lax.ppermute(acc, axis, perm)
+        acc = received + block_at(t + 2)
+    return acc
+
+
 def body(ring, queries, key_rows, value_rows, trunk_state, skip_input, norm_gain, conv_weight, cotangent):
     score_scale = DK ** (-0.5)
     local_tokens = queries.shape[1]
@@ -171,22 +200,41 @@
     norm_scale = (lax.axis_size("dp") * positions * lax.axis_size("seq")) ** (-0.5)
     seq_count, dp_count = lax.axis_size("seq"), lax.axis_size("dp")
     rows_per = KW * C // (seq_count * dp_count)
+    half_co = CO // 2
     if dp_count == 2:
         partner = [(0, 1), (1, 0)]
-        partner_padded = lax.ppermute(padded, "dp", partner)
-        partner_grad = lax.ppermute(grad_pre, "dp", partner)
-        both_columns = jnp.concatenate(
-            [columns, window_rows(partner_padded, KW, positions)], axis=0
-        ).reshape(2 * positions, seq_count, dp_count, rows_per)
-        mine = lax.dynamic_index_in_dim(both_columns, lax.axis_index("dp"), axis=2, keepdims=False)
-        dp_summed = (
-            jnp.einsum(
-                "psr,po->sro",
-                mine,
-                jnp.concatenate([grad_pre, partner_grad], axis=0),
-                preferred_element_type=jnp.float32,
+        both_padded = jnp.stack([padded, lax.ppermute(padded, "dp", partner)])
+        both_grad = jnp.stack([grad_pre, lax.ppermute(grad_pre, "dp", partner)])
+        full_weight = (
+            jnp.concatenate(
+                [
+                    jnp.einsum(
+                        "spc,spo->co",
+                        both_padded[:, offset : offset + positions],
+                        both_grad,
+                        preferred_element_type=jnp.float32,
+                    )
+                    for offset in range(KW)
+                ],
+                axis=0,
             )
             * norm_scale
+        ).reshape(seq_count, dp_count, rows_per, CO)
+        dp_index = lax.axis_index("dp")
+
+        def weight_block(column, width):
+            return lambda index: lax.dynamic_slice(
+                full_weight, (index, dp_index, 0, column), (1, 1, rows_per, width)
+            ).reshape(rows_per, width)
+
+        grad_weight = jnp.concatenate(
+            [
+                ring_reduce_scatter_sliced(weight_block(0, half_co), "seq", ring, True),
+                ring_reduce_scatter_sliced(
+                    weight_block(half_co, CO - half_co), "seq", ring, False
+                ),
+            ],
+            axis=1,
         )
     else:
         weight_part = (
@@ -199,14 +247,13 @@
         dp_summed = ring_reduce_scatter(
             jnp.swapaxes(weight_blocks_all, 0, 1), "dp", list(range(dp_count))
         )
-    half_co = CO // 2
-    grad_weight = jnp.concatenate(
-        [
-            ring_reduce_scatter(dp_summed[:, :, :half_co], "seq", ring, True),
-            ring_reduce_scatter(dp_summed[:, :, half_co:], "seq", ring, False),
-        ],
-        axis=1,
-    )
+        grad_weight = jnp.concatenate(
+            [
+                ring_reduce_scatter(dp_summed[:, :, :half_co], "seq", ring, True),
+                ring_reduce_scatter(dp_summed[:, :, half_co:], "seq", ring, False),
+            ],
+            axis=1,
+        )
     stacked = jnp.stack(
         [
             grad_padded[2 * half_kernel - offset : 2 * half_kernel - offset + positions]

time: 203 us -> 200 us (0.985)
  local copies, waits for them, and re-layouts: 50.9 us -> 38.7 us
  matrix products: 12.8 us -> 22.9 us
  other arithmetic: 25.5 us -> 33.6 us
  waiting for transfers between devices: 65.9 us -> 58.6 us
    add x14 -> x7, other arithmetic: 0.45 us -> 11.4 us  [ring_reduce_scatter_sliced(): acc = received + block_at(t + 2)]
    ppermute x16, waiting for transfers between devices: 31 us -> 23.4 us  [the longest x14 23.4 us: ring_reduce_scatter_sliced(): received = lax.ppermute(acc, axis, perm)]
    gather x2 -> x0, local copies, waits for them, and re-layouts: 7.37 us -> none  [ring_reduce_scatter(): relative = jnp.take(blocks, order, axis=0)]
    concatenate x2 -> x0, local copies, waits for them, and re-layouts: 6.38 us -> none  [the longest x1 6.28 us: body(): jnp.concatenate([columns, window_rows(partner_padded, KW, positions)], ax...]
    dot_general x1 -> x5, matrix products: 2.75 us -> 8.5 us  [body(): jnp.einsum('spc,spo->co', both_padded[:, offset:offset + positions], both...]
    ppermute x4, starting transfers between devices: 6.62 us -> 1.01 us  [ring_scatter_back(): received = lax.ppermute(acc, 'seq', backward).astype(jnp.float32)]
    select_n x3 -> x0, other arithmetic: 4.21 us -> none  [the longest x2 3.69 us: ring_reduce_scatter(): relative = jnp.take(blocks, order, axis=0)]
    ppermute x4, waiting for transfers between devices: 5.32 us -> 9.46 us  [ring_scatter_back(): received = lax.ppermute(acc, 'seq', backward).astype(jnp.float32)]
  transfers between devices with their start and end apart: 34 -> 34, of which waited for: 19 -> 22; matrix products, arithmetic and copies ran while one was open for 31% -> 28% of each run, Pallas kernels for 0% -> 0%
where the time goes in v4:
time: 200 us; the launch traced here: 198 us
  waiting for transfers between devices  58.6 us (29%)
  starting transfers between devices  43.3 us (22%)
  local copies, waits for them, and re-layouts  38.7 us (19%)
  other arithmetic  33.6 us (17%)
  matrix products  22.9 us (11%)
    ppermute x14, waiting for transfers between devices, ring_reduce_scatter_sliced(): received = lax.ppermute(acc, axis, perm)  23.4 us
    ppermute x4, waiting for transfers between devices, ring_gather(): current = lax.ppermute(current, 'seq', forward)  19.4 us
    ppermute x14, starting transfers between devices, ring_reduce_scatter_sliced(): received = lax.ppermute(acc, axis, perm)  16.8 us
    unnamed x65, local copies, waits for them, and re-layouts  12.6 us
    add x7, other arithmetic, ring_reduce_scatter_sliced(): acc = received + block_at(t + 2)  11.4 us
    ppermute x4, waiting for transfers between devices, ring_scatter_back(): received = lax.ppermute(acc, 'seq', backward).astype(jnp.float32)  9.46 us
    dot_general x5, matrix products, body(): jnp.einsum('spc,spo->co', both_padded[:, offset:offset + positions], both...  8.5 us
    ppermute x2, starting transfers between devices, extended(): before = lax.ppermute(last, axis, up)  8.32 us
  transfers between devices with their start and end apart: 34, of which 22 were waited for; matrix products, arithmetic and copies ran while one was open for 28% of the time, Pallas kernels for 0%

profile of v4, /device:TPU:0, one launch (start us, length us, event | category | flops | bytes accessed | tf_op | source)
XLA Modules:
  0.0 198.3 jit_solution(8220748320847199171)
XLA Ops:
  3.9 3.1 %collective-permute-start = (bf16[128,1280]{0,1:T(8,128)(2,1)}, bf16[128,1280]{0,1:T(8,128)(2,1)S(1)}, u32[]{:S(2)}, u32[]{:S(2)}) collective-permute-start(bf16[128,1280]{0,1:T(8,128)(2,1)} %get-tuple-element.51), channel_id=1, source_target_pairs={{0,4},{4,8},{8,12},{12,14},{14,10},{10,6},{6,2},{2,0},{1,5},{5,9},... | collective-permute-start | bytes 983048 | tf_op jit(solution)/shard_map/ppermute | solution.py:75
  6.9 7.9 %collective-permute-done = bf16[128,1280]{0,1:T(8,128)(2,1)S(1)} collective-permute-done((bf16[128,1280]{0,1:T(8,128)(2,1)}, bf16[128,1280]{0,1:T(8,128)(2,1)S(1)}, u32[]{:S(2)}, u32[]{:S(2)}) %collective-permute-start) | collective-permute-done | bytes 327712 | tf_op jit(solution)/shard_map/ppermute | solution.py:75
  15.5 1.8 collective-permute-start.1
  17.5 7.0 %collective-permute-done.1 = bf16[128,1280]{0,1:T(8,128)(2,1)} collective-permute-done((bf16[128,1280]{0,1:T(8,128)(2,1)S(1)}, bf16[128,1280]{0,1:T(8,128)(2,1)}, u32[]{:S(2)}, u32[]{:S(2)}) %collective-permute-start.1) | collective-permute-done | bytes 327712 | tf_op jit(solution)/shard_map/ppermute | solution.py:75
  28.3 1.7 constant_dynamic-update-slice_fusion.6
  30.1 2.7 %collective-permute-done.2 = bf16[128,1280]{0,1:T(8,128)(2,1)} collective-permute-done((bf16[128,1280]{0,1:T(8,128)(2,1)}, bf16[128,1280]{0,1:T(8,128)(2,1)}, u32[]{:S(2)}, u32[]{:S(2)}) %collective-permute-start.2) | collective-permute-done | bytes 327712 | tf_op jit(solution)/shard_map/ppermute | solution.py:75
  34.1 1.8 constant_dynamic-update-slice_fusion.5
  36.6 1.7 constant_dynamic-update-slice_fusion.4
  38.4 1.8 collective-permute-done.3
  45.3 1.9 slice.127
  52.2 2.6 %broadcast_in_dim.26 = f32[1,256,768]{2,1,0:T(8,128)} reshape(f32[128,2,768]{2,1,0:T(2,128)} %broadcast_in_dim.12) | data formatting | bytes 1572864 | tf_op jit(solution)/shard_map/broadcast_in_dim | solution.py:189
  54.8 2.6 %reshape.153 = f32[256,768]{1,0:T(8,128)} reshape(f32[128,2,768]{2,1,0:T(2,128)} %broadcast_in_dim.12) | data formatting | bytes 1572864 | tf_op jit(solution)/shard_map/reshape | solution.py:189
  60.6 2.7 %collective-permute-start.7 = (bf16[2,768]{1,0:T(2,128)(2,1)S(1)}, bf16[2,768]{1,0:T(2,128)(2,1)S(1)}, u32[]{:S(2)}, u32[]{:S(2)}) collective-permute-start(bf16[2,768]{1,0:T(2,128)(2,1)S(1)} %get-tuple-element.50), channel_id=1, source_target_pairs={{0,2},{2,4},{4,6},{6,8},{8,10},{10,12},{12,14},{1,3},{3,5},{5,7},{... | collective-permute-start | bytes 9224 | tf_op jit(solution)/shard_map/ppermute | solution.py:24
  65.0 4.2 %collective-permute-done.8 = bf16[2,768]{1,0:T(2,128)(2,1)S(1)} collective-permute-done((bf16[2,768]{1,0:T(2,128)(2,1)S(1)}, bf16[2,768]{1,0:T(2,128)(2,1)S(1)}, u32[]{:S(2)}, u32[]{:S(2)}) %collective-permute-start.8) | collective-permute-done | bytes 3104 | tf_op jit(solution)/shard_map/ppermute | solution.py:25
  69.4 2.9 %fusion.34 = (bf16[256,384]{1,0:T(8,128)(2,1)S(1)}, bf16[1,256,384]{2,1,0:T(8,128)(2,1)}) fusion(bf16[1,256,384]{2,1,0:T(8,128)(2,1)} %param.15, bf16[256,3840]{1,0:T(8,128)(2,1)S(1)} %fusion.35, bf16[3840,384]{1,0:T(8,128)(2,1)S(1)} %copy-done), kind=kOutput, calls=%fused_computation.85 | convolution fusion | flops 756252672 | bytes 5505024 | tf_op jit(solution)/shard_map/dot_general | solution.py:195
  73.8 5.6 %collective-permute-start.10 = (bf16[2,384]{1,0:T(2,128)(2,1)S(1)}, bf16[2,384]{1,0:T(2,128)(2,1)S(1)}, u32[]{:S(2)}, u32[]{:S(2)}) collective-permute-start(bf16[2,384]{1,0:T(2,128)(2,1)S(1)} %get-tuple-element.53), channel_id=1, source_target_pairs={{0,2},{2,4},{4,6},{6,8},{8,10},{10,12},{12,14},{1,3},{3,5},{5,7},{... | collective-permute-start | bytes 4616 | tf_op jit(solution)/shard_map/ppermute | solution.py:24
  83.3 2.5 %reshape.155 = f32[128,2,768]{2,1,0:T(2,128)} reshape(f32[256,768]{1,0:T(8,128)} %get-tuple-element.22) | data formatting | bytes 1572864 | tf_op jit(solution)/shard_map/reshape | solution.py:273
  85.8 2.8 %reduce_sum.48 = bf16[128,768]{1,0:T(8,128)(2,1)} reduce(f32[128,2,768]{2,1,0:T(2,128)} %reshape.155, f32[]{:T(128)} %constant.150.clone.1), dimensions={1}, to_apply=%region_4.5 | reduce | flops 98304 | bytes 983044 | tf_op jit(solution)/shard_map/reduce_sum | solution.py:273
  88.6 1.7 copy.40
  91.3 4.3 %multiply_convert_fusion.1 = bf16[4,128,1024]{1,2,0:T(8,128)(2,1)} fusion(f32[4,1024,128]{2,1,0:T(8,128)} %copy-done.2, bf16[128,4,192]{0,2,1:T(8,128)(2,1)} %bitcast.181, bf16[1024,4,192]{0,2,1:T(8,128)(2,1)} %bitcast.169, f32[4,128]{1,0:T(4,128)S(1)} %bitcast.189, f32[4,128]{1,0:T(4,128)S(1)} %log_add_fusion), kind=kOutput, calls=%fused_computation.22 | convolution fusion | flops 203948032 | bytes 4919296 | tf_op jit(solution)/shard_map/ihd,jhd->hij/dot_general | solution.py:276
  95.6 1.8 convolution_convert_fusion
  97.4 2.7 %copy.49 = bf16[1024,768]{1,0:T(8,128)(2,1)} copy(bf16[1024,768]{0,1:T(8,128)(2,1)} %bitcast.172) | data formatting | bytes 3145728 | tf_op jit(solution)/shard_map/reshape | solution.py:292
  100.0 2.6 %fusion.9 = bf16[1024,4,128]{2,0,1:T(8,128)(2,1)} fusion(bf16[4,128,1024]{1,2,0:T(8,128)(2,1)} %multiply_convert_fusion.1, bf16[128,4,128]{0,2,1:T(8,128)(2,1)S(1)} %bitcast.184), kind=kOutput, calls=%fused_computation.35 | convolution fusion | flops 135266304 | bytes 2228224 | tf_op jit(solution)/shard_map/hij,ihd->jhd/dot_general | solution.py:285
  102.7 2.3 %copy.46 = bf16[1024,4,128]{0,2,1:T(8,128)(2,1)} copy(bf16[1024,4,128]{2,0,1:T(8,128)(2,1)} %fusion.9) | data formatting | bytes 2097152 | tf_op jit(solution)/shard_map/mul | solution.py:285
  105.0 2.3 %copy.48 = bf16[1024,512]{1,0:T(8,128)(2,1)} copy(bf16[1024,512]{0,1:T(8,128)(2,1)} %bitcast.178) | data formatting | bytes 2097152 | tf_op jit(solution)/shard_map/reshape | solution.py:291
  107.2 1.8 fusion.8
  109.1 1.7 fusion.7
  110.8 1.7 fusion.6
  112.4 1.7 fusion.5
  114.1 1.7 fusion.4
  117.0 4.5 %collective-permute-start.20 = (f32[240,192]{1,0:T(8,128)}, f32[240,192]{1,0:T(8,128)S(1)}, u32[]{:S(2)}, u32[]{:S(2)}) collective-permute-start(f32[240,192]{1,0:T(8,128)} %get-tuple-element.37), channel_id=1, source_target_pairs={{0,4},{4,8},{8,12},{12,14},{14,10},{10,6},{6,2},{2,0},{1,5},{5,9},... | collective-permute-start | bytes 552968 | tf_op jit(solution)/shard_map/ppermute | solution.py:159
  122.7 1.7 collective-permute-start.15
  124.4 3.8 %collective-permute-done.20 = f32[240,192]{1,0:T(8,128)S(1)} collective-permute-done((f32[240,192]{1,0:T(8,128)}, f32[240,192]{1,0:T(8,128)S(1)}, u32[]{:S(2)}, u32[]{:S(2)}) %collective-permute-start.20) | collective-permute-done | bytes 184352 | tf_op jit(solution)/shard_map/ppermute | solution.py:159
  128.2 2.5 %collective-permute-done.27 = f32[240,192]{1,0:T(8,128)} collective-permute-done((f32[240,192]{1,0:T(8,128)}, f32[240,192]{1,0:T(8,128)}, u32[]{:S(2)}, u32[]{:S(2)}) %collective-permute-start.27) | collective-permute-done | bytes 184352 | tf_op jit(solution)/shard_map/ppermute | solution.py:159
  130.7 2.1 %bitcast_add_fusion.13 = (f32[240,192]{1,0:T(8,128)}, f32[240,192]{1,0:T(8,128)}) fusion(f32[240,192]{1,0:T(8,128)S(1)} %collective-permute-done.20, f32[8,2,240,384]{3,2,1,0:T(8,128)} %bitcast.161, s32[]{:T(128)S(6)} %select_n.491, s32[]{:T(128)S(6)} %select_n.483, f32[240,192]{1,0:T(8,128)} %collective-permute-done.27, s32[]{:T(128)S(6)} %select_n.555), kind=kLoop, calls=%fused_computation.120 | loop fusion | flops 92160 | bytes 1105932 | tf_op jit(solution)/shard_map/add | solution.py:160
  134.8 2.9 %collective-permute-done.11 = bf16[128,1280]{1,0:T(8,128)(2,1)} collective-permute-done((bf16[128,1280]{1,0:T(8,128)(2,1)}, bf16[128,1280]{1,0:T(8,128)(2,1)}, u32[]{:S(2)}, u32[]{:S(2)}) %collective-permute-start.11) | collective-permute-done | bytes 327712 | tf_op jit(solution)/shard_map/ppermute | solution.py:96
  137.7 1.8 add_convert_fusion.5
  140.2 3.2 %collective-permute-done.28 = f32[240,192]{1,0:T(8,128)} collective-permute-done((f32[240,192]{1,0:T(8,128)}, f32[240,192]{1,0:T(8,128)}, u32[]{:S(2)}, u32[]{:S(2)}) %collective-permute-start.28) | collective-permute-done | bytes 184352 | tf_op jit(solution)/shard_map/ppermute | solution.py:159
  143.5 2.1 %bitcast_add_fusion.12 = (f32[240,192]{1,0:T(8,128)}, f32[240,192]{1,0:T(8,128)S(1)}) fusion(f32[240,192]{1,0:T(8,128)} %copy-done.24, f32[8,2,240,384]{3,2,1,0:T(8,128)} %bitcast.162, s32[]{:T(128)S(6)} %select_n.499, s32[]{:T(128)S(6)} %select_n.483, f32[240,192]{1,0:T(8,128)} %collective-permute-done.28, s32[]{:T(128)S(6)} %select_n.563), kind=kLoop, calls=%fused_computation.119 | loop fusion | flops 92160 | bytes 1105932 | tf_op jit(solution)/shard_map/add | solution.py:160
  147.6 2.9 %collective-permute-done.12 = bf16[128,1280]{1,0:T(8,128)(2,1)} collective-permute-done((bf16[128,1280]{1,0:T(8,128)(2,1)}, bf16[128,1280]{1,0:T(8,128)(2,1)}, u32[]{:S(2)}, u32[]{:S(2)}) %collective-permute-start.12) | collective-permute-done | bytes 327712 | tf_op jit(solution)/shard_map/ppermute | solution.py:96
  150.5 2.2 %add_convert_fusion.4 = (bf16[128,1280]{1,0:T(8,128)(2,1)}, bf16[128,1280]{1,0:T(8,128)(2,1)}) fusion(bf16[128,1280]{1,0:T(8,128)(2,1)} %collective-permute-done.12, bf16[1024,768]{1,0:T(8,128)(2,1)} %copy.49, bf16[1024,512]{1,0:T(8,128)(2,1)S(1)} %copy-done.6, bf16[128,1280]{1,0:T(8,128)(2,1)} %collective-permute-done.15), kind=kLoop, calls=%fused_computation.68 | loop fusion | flops 2293760 | bytes 3932160 | tf_op jit(solution)/shard_map/convert_element_type | solution.py:100
  152.8 1.9 collective-permute-start.16
  156.0 2.2 %bitcast_add_fusion.11 = (f32[240,192]{1,0:T(8,128)}, f32[240,192]{1,0:T(8,128)}) fusion(f32[240,192]{1,0:T(8,128)} %collective-permute-done.22, f32[8,2,240,384]{3,2,1,0:T(8,128)} %bitcast.163, s32[]{:T(128)S(6)} %select_n.507, s32[]{:T(128)S(6)} %select_n.483, f32[240,192]{1,0:T(8,128)} %collective-permute-done.29, s32[]{:T(128)S(6)} %select_n.571), kind=kLoop, calls=%fused_computation.118 | loop fusion | flops 92160 | bytes 1105932 | tf_op jit(solution)/shard_map/add | solution.py:160
  160.2 2.6 %collective-permute-done.13 = bf16[128,1280]{1,0:T(8,128)(2,1)S(1)} collective-permute-done((bf16[128,1280]{1,0:T(8,128)(2,1)}, bf16[128,1280]{1,0:T(8,128)(2,1)S(1)}, u32[]{:S(2)}, u32[]{:S(2)}) %collective-permute-start.13) | collective-permute-done | bytes 327712 | tf_op jit(solution)/shard_map/ppermute | solution.py:96
  162.8 2.2 %add_convert_fusion.3 = (bf16[128,1280]{1,0:T(8,128)(2,1)}, bf16[128,1280]{1,0:T(8,128)(2,1)}) fusion(bf16[128,1280]{1,0:T(8,128)(2,1)S(1)} %collective-permute-done.13, bf16[1024,768]{1,0:T(8,128)(2,1)} %copy.49, bf16[1024,512]{1,0:T(8,128)(2,1)S(1)} %copy-done.7, bf16[128,1280]{1,0:T(8,128)(2,1)} %collective-permute-done.16), kind=kLoop, calls=%fused_computation.67 | loop fusion | flops 2293760 | bytes 3932160 | tf_op jit(solution)/shard_map/convert_element_type | solution.py:100
  172.1 1.8 collective-permute-done.17
  181.8 4.5 %collective-permute-done.25 = f32[240,192]{1,0:T(8,128)S(1)} collective-permute-done((f32[240,192]{1,0:T(8,128)S(1)}, f32[240,192]{1,0:T(8,128)S(1)}, u32[]{:S(2)}, u32[]{:S(2)}) %collective-permute-start.25) | collective-permute-done | bytes 184352 | tf_op jit(solution)/shard_map/ppermute | solution.py:159
  191.2 3.5 %collective-permute-done.26 = f32[240,192]{1,0:T(8,128)S(1)} collective-permute-done((f32[240,192]{1,0:T(8,128)S(1)}, f32[240,192]{1,0:T(8,128)S(1)}, u32[]{:S(2)}, u32[]{:S(2)}) %collective-permute-start.26) | collective-permute-done | bytes 184352 | tf_op jit(solution)/shard_map/ppermute | solution.py:159
  (151 shorter events, 65.4 us)
Async XLA Ops:
  0.6 68.7 %copy-start = (bf16[3840,384]{1,0:T(8,128)(2,1)S(1)}, bf16[3840,384]{1,0:T(8,128)(2,1)}, u32[]{:S(2)}) copy-start(bf16[3840,384]{1,0:T(8,128)(2,1)} %param.14) | copy-start | bytes 8847364
  3.9 10.9 %collective-permute-start = (bf16[128,1280]{0,1:T(8,128)(2,1)}, bf16[128,1280]{0,1:T(8,128)(2,1)S(1)}, u32[]{:S(2)}, u32[]{:S(2)}) collective-permute-start(bf16[128,1280]{0,1:T(8,128)(2,1)} %get-tuple-element.51), channel_id=1, source_target_pairs={{0,4},{4,8},{8,12},{12,14},{14,10},{10,6},{6,2},{2,0},{1,5},{5,9},... | collective-permute-start | bytes 983048 | tf_op jit(solution)/shard_map/ppermute | solution.py:75
  15.5 9.0 %collective-permute-start.1 = (bf16[128,1280]{0,1:T(8,128)(2,1)S(1)}, bf16[128,1280]{0,1:T(8,128)(2,1)}, u32[]{:S(2)}, u32[]{:S(2)}) collective-permute-start(bf16[128,1280]{0,1:T(8,128)(2,1)S(1)} %collective-permute-done), channel_id=1, source_target_pairs={{0,4},{4,8},{8,12},{12,14},{14,10},{10,6},{6,2},{2,0},{1,5},{5,9},... | collective-permute-start | bytes 983048 | tf_op jit(solution)/shard_map/ppermute | solution.py:75
  17.3 10.5 %collective-permute-start.4 = (bf16[128,1280]{0,1:T(8,128)(2,1)}, bf16[128,1280]{0,1:T(8,128)(2,1)S(1)}, u32[]{:S(2)}, u32[]{:S(2)}) collective-permute-start(bf16[128,1280]{0,1:T(8,128)(2,1)} %get-tuple-element.51), channel_id=1, source_target_pairs={{0,2},{4,0},{8,4},{12,8},{14,12},{10,14},{6,10},{2,6},{1,3},{5,1},... | collective-permute-start | bytes 983048 | tf_op jit(solution)/shard_map/ppermute | solution.py:79
  24.5 8.3 %collective-permute-start.2 = (bf16[128,1280]{0,1:T(8,128)(2,1)}, bf16[128,1280]{0,1:T(8,128)(2,1)}, u32[]{:S(2)}, u32[]{:S(2)}) collective-permute-start(bf16[128,1280]{0,1:T(8,128)(2,1)} %collective-permute-done.1), channel_id=1, source_target_pairs={{0,4},{4,8},{8,12},{12,14},{14,10},{10,6},{6,2},{2,0},{1,5},{5,9},... | collective-permute-start | bytes 983048 | tf_op jit(solution)/shard_map/ppermute | solution.py:75
  27.7 19.4 %copy-start.20 = (bf16[1,128,512]{1,2,0:T(8,128)(2,1)}, bf16[1,128,512]{1,2,0:T(8,128)(2,1)S(1)}, u32[]{:S(2)}) copy-start(bf16[1,128,512]{1,2,0:T(8,128)(2,1)S(1)} %copy.68) | copy-start | bytes 393220
  27.8 8.1 %collective-permute-start.5 = (bf16[128,1280]{0,1:T(8,128)(2,1)S(1)}, bf16[128,1280]{0,1:T(8,128)(2,1)S(1)}, u32[]{:S(2)}, u32[]{:S(2)}) collective-permute-start(bf16[128,1280]{0,1:T(8,128)(2,1)S(1)} %collective-permute-done.4), channel_id=1, source_target_pairs={{0,2},{4,0},{8,4},{12,8},{14,12},{10,14},{6,10},{2,6},{1,3},{5,1},... | collective-permute-start | bytes 983048 | tf_op jit(solution)/shard_map/ppermute | solution.py:79
  32.8 7.4 %collective-permute-start.3 = (bf16[128,1280]{0,1:T(8,128)(2,1)}, bf16[128,1280]{0,1:T(8,128)(2,1)S(1)}, u32[]{:S(2)}, u32[]{:S(2)}) collective-permute-start(bf16[128,1280]{0,1:T(8,128)(2,1)} %collective-permute-done.2), channel_id=1, source_target_pairs={{0,4},{4,8},{8,12},{12,14},{14,10},{10,6},{6,2},{2,0},{1,5},{5,9},... | collective-permute-start | bytes 983048 | tf_op jit(solution)/shard_map/ppermute | solution.py:75
  35.8 7.1 %collective-permute-start.6 = (bf16[128,1280]{0,1:T(8,128)(2,1)S(1)}, bf16[128,1280]{0,1:T(8,128)(2,1)S(1)}, u32[]{:S(2)}, u32[]{:S(2)}) collective-permute-start(bf16[128,1280]{0,1:T(8,128)(2,1)S(1)} %collective-permute-done.5), channel_id=1, source_target_pairs={{0,2},{4,0},{8,4},{12,8},{14,12},{10,14},{6,10},{2,6},{1,3},{5,1},... | collective-permute-start | bytes 983048 | tf_op jit(solution)/shard_map/ppermute | solution.py:79
  51.0 6.3 %copy-start.15 = (bf16[1,256,768]{2,1,0:T(8,128)(2,1)S(1)}, bf16[1,256,768]{2,1,0:T(8,128)(2,1)}, u32[]{:S(2)}) copy-start(bf16[1,256,768]{2,1,0:T(8,128)(2,1)} %param.12) | copy-start | bytes 1179652
  60.6 4.1 %collective-permute-start.7 = (bf16[2,768]{1,0:T(2,128)(2,1)S(1)}, bf16[2,768]{1,0:T(2,128)(2,1)S(1)}, u32[]{:S(2)}, u32[]{:S(2)}) collective-permute-start(bf16[2,768]{1,0:T(2,128)(2,1)S(1)} %get-tuple-element.50), channel_id=1, source_target_pairs={{0,2},{2,4},{4,6},{6,8},{8,10},{10,12},{12,14},{1,3},{3,5},{5,7},{... | collective-permute-start | bytes 9224 | tf_op jit(solution)/shard_map/ppermute | solution.py:24
  63.4 5.7 %collective-permute-start.8 = (bf16[2,768]{1,0:T(2,128)(2,1)S(1)}, bf16[2,768]{1,0:T(2,128)(2,1)S(1)}, u32[]{:S(2)}, u32[]{:S(2)}) collective-permute-start(bf16[2,768]{1,0:T(2,128)(2,1)S(1)} %get-tuple-element.49), channel_id=1, source_target_pairs={{2,0},{4,2},{6,4},{8,6},{10,8},{12,10},{14,12},{3,1},{5,3},{7,5},{... | collective-permute-start | bytes 9224 | tf_op jit(solution)/shard_map/ppermute | solution.py:25
  72.3 8.6 %copy-start.11 = (f32[256,768]{1,0:T(8,128)S(1)}, f32[256,768]{1,0:T(8,128)}, u32[]{:S(2)}) copy-start(f32[256,768]{1,0:T(8,128)} %reshape.153) | copy-start | bytes 2359300
  72.3 8.6 %copy-start.16 = (bf16[1,256,768]{2,1,0:T(8,128)(2,1)S(1)}, bf16[1,256,768]{2,1,0:T(8,128)(2,1)}, u32[]{:S(2)}) copy-start(bf16[1,256,768]{2,1,0:T(8,128)(2,1)} %param.12) | copy-start | bytes 1179652
  72.3 34.9 %collective-permute-start.19 = (bf16[256,384]{1,0:T(8,128)(2,1)S(1)}, bf16[256,384]{1,0:T(8,128)(2,1)}, u32[]{:S(2)}, u32[]{:S(2)}) collective-permute-start(bf16[256,384]{1,0:T(8,128)(2,1)S(1)} %get-tuple-element.47), channel_id=1, source_target_pairs={{0,1},{1,0},{2,3},{3,2},{4,5},{5,4},{6,7},{7,6},{8,9},{9,8},{10,11... | collective-permute-start | bytes 589832 | tf_op jit(solution)/shard_map/ppermute | solution.py:207
  72.4 8.1 %collective-permute-start.9 = (bf16[2,384]{1,0:T(2,128)(2,1)S(1)}, bf16[2,384]{1,0:T(2,128)(2,1)S(1)}, u32[]{:S(2)}, u32[]{:S(2)}) collective-permute-start(bf16[2,384]{1,0:T(2,128)(2,1)S(1)} %get-tuple-element.54), channel_id=1, source_target_pairs={{2,0},{4,2},{6,4},{8,6},{10,8},{12,10},{14,12},{3,1},{5,3},{7,5},{... | collective-permute-start | bytes 4616 | tf_op jit(solution)/shard_map/ppermute | solution.py:25
  73.8 6.9 %collective-permute-start.10 = (bf16[2,384]{1,0:T(2,128)(2,1)S(1)}, bf16[2,384]{1,0:T(2,128)(2,1)S(1)}, u32[]{:S(2)}, u32[]{:S(2)}) collective-permute-start(bf16[2,384]{1,0:T(2,128)(2,1)S(1)} %get-tuple-element.53), channel_id=1, source_target_pairs={{0,2},{2,4},{4,6},{6,8},{8,10},{10,12},{12,14},{1,3},{3,5},{5,7},{... | collective-permute-start | bytes 4616 | tf_op jit(solution)/shard_map/ppermute | solution.py:24
  80.5 26.8 %collective-permute-start.18 = (bf16[260,768]{1,0:T(8,128)(2,1)}, bf16[260,768]{1,0:T(8,128)(2,1)}, u32[]{:S(2)}, u32[]{:S(2)}) collective-permute-start(bf16[260,768]{1,0:T(8,128)(2,1)} %get-tuple-element.45), channel_id=1, source_target_pairs={{0,1},{1,0},{2,3},{3,2},{4,5},{5,4},{6,7},{7,6},{8,9},{9,8},{10,11... | collective-permute-start | bytes 1198088 | tf_op jit(solution)/shard_map/ppermute | solution.py:206
  83.3 7.0 %copy-start.18 = (f32[4,192,128]{2,1,0:T(8,128)S(1)}, f32[4,192,128]{2,1,0:T(8,128)}, u32[]{:S(2)}) copy-start(f32[4,192,128]{2,1,0:T(8,128)} %copy-done.17) | copy-start | bytes 1179652
  115.8 5.8 %copy-start.1 = (bf16[1024,768]{1,0:T(8,128)(2,1)S(1)}, bf16[1024,768]{1,0:T(8,128)(2,1)}, u32[]{:S(2)}) copy-start(bf16[1024,768]{1,0:T(8,128)(2,1)} %copy.49) | copy-start | bytes 4718596
  116.2 6.1 %copy-start.9 = (f32[3840,384]{1,0:T(8,128)}, f32[3840,384]{1,0:T(8,128)S(1)}, u32[]{:S(2)}) copy-start(f32[3840,384]{1,0:T(8,128)S(1)} %broadcast_multiply_fusion) | copy-start | bytes 17694724
  117.0 11.1 %collective-permute-start.20 = (f32[240,192]{1,0:T(8,128)}, f32[240,192]{1,0:T(8,128)S(1)}, u32[]{:S(2)}, u32[]{:S(2)}) collective-permute-start(f32[240,192]{1,0:T(8,128)} %get-tuple-element.37), channel_id=1, source_target_pairs={{0,4},{4,8},{8,12},{12,14},{14,10},{10,6},{6,2},{2,0},{1,5},{5,9},... | collective-permute-start | bytes 552968 | tf_op jit(solution)/shard_map/ppermute | solution.py:159
  121.5 9.1 %collective-permute-start.27 = (f32[240,192]{1,0:T(8,128)}, f32[240,192]{1,0:T(8,128)}, u32[]{:S(2)}, u32[]{:S(2)}) collective-permute-start(f32[240,192]{1,0:T(8,128)} %get-tuple-element.38), channel_id=1, source_target_pairs={{0,2},{4,0},{8,4},{12,8},{14,12},{10,14},{6,10},{2,6},{1,3},{5,1},... | collective-permute-start | bytes 552968 | tf_op jit(solution)/shard_map/ppermute | solution.py:159
  122.3 15.4 %collective-permute-start.11 = (bf16[128,1280]{1,0:T(8,128)(2,1)}, bf16[128,1280]{1,0:T(8,128)(2,1)}, u32[]{:S(2)}, u32[]{:S(2)}) collective-permute-start(bf16[128,1280]{1,0:T(8,128)(2,1)} %get-tuple-element.43), channel_id=1, source_target_pairs={{0,2},{4,0},{8,4},{12,8},{14,12},{10,14},{6,10},{2,6},{1,3},{5,1},... | collective-permute-start | bytes 983048 | tf_op jit(solution)/shard_map/ppermute | solution.py:96
  122.7 15.0 %copy-start.5 = (bf16[1024,512]{1,0:T(8,128)(2,1)S(1)}, bf16[1024,512]{1,0:T(8,128)(2,1)}, u32[]{:S(2)}) copy-start(bf16[1024,512]{1,0:T(8,128)(2,1)} %copy.48) | copy-start | bytes 3145732
  122.7 24.9 %collective-permute-start.15 = (bf16[128,1280]{1,0:T(8,128)(2,1)S(1)}, bf16[128,1280]{1,0:T(8,128)(2,1)}, u32[]{:S(2)}, u32[]{:S(2)}) collective-permute-start(bf16[128,1280]{1,0:T(8,128)(2,1)S(1)} %get-tuple-element.44), channel_id=1, source_target_pairs={{0,4},{4,8},{8,12},{12,14},{14,10},{10,6},{6,2},{2,0},{1,5},{5,9},... | collective-permute-start | bytes 983048 | tf_op jit(solution)/shard_map/ppermute | solution.py:104
  132.7 6.8 %collective-permute-start.21 = (f32[240,192]{1,0:T(8,128)}, f32[240,192]{1,0:T(8,128)S(1)}, u32[]{:S(2)}, u32[]{:S(2)}) collective-permute-start(f32[240,192]{1,0:T(8,128)} %get-tuple-element.35), channel_id=1, source_target_pairs={{0,4},{4,8},{8,12},{12,14},{14,10},{10,6},{6,2},{2,0},{1,5},{5,9},... | collective-permute-start | bytes 552968 | tf_op jit(solution)/shard_map/ppermute | solution.py:159
  134.3 9.1 %collective-permute-start.28 = (f32[240,192]{1,0:T(8,128)}, f32[240,192]{1,0:T(8,128)}, u32[]{:S(2)}, u32[]{:S(2)}) collective-permute-start(f32[240,192]{1,0:T(8,128)} %get-tuple-element.36), channel_id=1, source_target_pairs={{0,2},{4,0},{8,4},{12,8},{14,12},{10,14},{6,10},{2,6},{1,3},{5,1},... | collective-permute-start | bytes 552968 | tf_op jit(solution)/shard_map/ppermute | solution.py:159
  139.5 11.0 %collective-permute-start.12 = (bf16[128,1280]{1,0:T(8,128)(2,1)}, bf16[128,1280]{1,0:T(8,128)(2,1)}, u32[]{:S(2)}, u32[]{:S(2)}) collective-permute-start(bf16[128,1280]{1,0:T(8,128)(2,1)} %add_convert_fusion.5), channel_id=1, source_target_pairs={{0,2},{4,0},{8,4},{12,8},{14,12},{10,14},{6,10},{2,6},{1,3},{5,1},... | collective-permute-start | bytes 983048 | tf_op jit(solution)/shard_map/ppermute | solution.py:96
  139.5 11.0 %copy-start.6 = (bf16[1024,512]{1,0:T(8,128)(2,1)S(1)}, bf16[1024,512]{1,0:T(8,128)(2,1)}, u32[]{:S(2)}) copy-start(bf16[1024,512]{1,0:T(8,128)(2,1)} %copy.48) | copy-start | bytes 3145732
  145.6 9.2 %collective-permute-start.22 = (f32[240,192]{1,0:T(8,128)}, f32[240,192]{1,0:T(8,128)}, u32[]{:S(2)}, u32[]{:S(2)}) collective-permute-start(f32[240,192]{1,0:T(8,128)} %get-tuple-element.33), channel_id=1, source_target_pairs={{0,4},{4,8},{8,12},{12,14},{14,10},{10,6},{6,2},{2,0},{1,5},{5,9},... | collective-permute-start | bytes 552968 | tf_op jit(solution)/shard_map/ppermute | solution.py:159
  147.1 8.9 %collective-permute-start.29 = (f32[240,192]{1,0:T(8,128)S(1)}, f32[240,192]{1,0:T(8,128)}, u32[]{:S(2)}, u32[]{:S(2)}) collective-permute-start(f32[240,192]{1,0:T(8,128)S(1)} %get-tuple-element.34), channel_id=1, source_target_pairs={{0,2},{4,0},{8,4},{12,8},{14,12},{10,14},{6,10},{2,6},{1,3},{5,1},... | collective-permute-start | bytes 552968 | tf_op jit(solution)/shard_map/ppermute | solution.py:159
  152.7 10.1 %collective-permute-start.13 = (bf16[128,1280]{1,0:T(8,128)(2,1)}, bf16[128,1280]{1,0:T(8,128)(2,1)S(1)}, u32[]{:S(2)}, u32[]{:S(2)}) collective-permute-start(bf16[128,1280]{1,0:T(8,128)(2,1)} %get-tuple-element.41), channel_id=1, source_target_pairs={{0,2},{4,0},{8,4},{12,8},{14,12},{10,14},{6,10},{2,6},{1,3},{5,1},... | collective-permute-start | bytes 983048 | tf_op jit(solution)/shard_map/ppermute | solution.py:96
  152.8 10.0 %collective-permute-start.16 = (bf16[128,1280]{1,0:T(8,128)(2,1)}, bf16[128,1280]{1,0:T(8,128)(2,1)}, u32[]{:S(2)}, u32[]{:S(2)}) collective-permute-start(bf16[128,1280]{1,0:T(8,128)(2,1)} %get-tuple-element.42), channel_id=1, source_target_pairs={{0,4},{4,8},{8,12},{12,14},{14,10},{10,6},{6,2},{2,0},{1,5},{5,9},... | collective-permute-start | bytes 983048 | tf_op jit(solution)/shard_map/ppermute | solution.py:104
  154.7 8.1 %copy-start.7 = (bf16[1024,512]{1,0:T(8,128)(2,1)S(1)}, bf16[1024,512]{1,0:T(8,128)(2,1)}, u32[]{:S(2)}) copy-start(bf16[1024,512]{1,0:T(8,128)(2,1)} %copy.48) | copy-start | bytes 3145732
  158.2 8.8 %copy-start.13 = (bf16[1024,512]{0,1:T(8,128)(2,1)S(1)}, bf16[1024,512]{0,1:T(8,128)(2,1)}, u32[]{:S(2)}) copy-start(bf16[1024,512]{0,1:T(8,128)(2,1)} %copy-done.12) | copy-start | bytes 3145732
  158.2 8.8 %copy-start.14 = (bf16[4,128,1024]{1,2,0:T(8,128)(2,1)S(1)}, bf16[4,128,1024]{1,2,0:T(8,128)(2,1)}, u32[]{:S(2)}) copy-start(bf16[4,128,1024]{1,2,0:T(8,128)(2,1)} %multiply_convert_fusion.1) | copy-start | bytes 3145732
  158.2 10.0 %collective-permute-start.23 = (f32[240,192]{1,0:T(8,128)}, f32[240,192]{1,0:T(8,128)}, u32[]{:S(2)}, u32[]{:S(2)}) collective-permute-start(f32[240,192]{1,0:T(8,128)} %get-tuple-element.31), channel_id=1, source_target_pairs={{0,4},{4,8},{8,12},{12,14},{14,10},{10,6},{6,2},{2,0},{1,5},{5,9},... | collective-permute-start | bytes 552968 | tf_op jit(solution)/shard_map/ppermute | solution.py:159
  159.5 9.1 %collective-permute-start.30 = (f32[240,192]{1,0:T(8,128)}, f32[240,192]{1,0:T(8,128)}, u32[]{:S(2)}, u32[]{:S(2)}) collective-permute-start(f32[240,192]{1,0:T(8,128)} %get-tuple-element.32), channel_id=1, source_target_pairs={{0,2},{4,0},{8,4},{12,8},{14,12},{10,14},{6,10},{2,6},{1,3},{5,1},... | collective-permute-start | bytes 552968 | tf_op jit(solution)/shard_map/ppermute | solution.py:159
  165.0 9.0 %collective-permute-start.17 = (bf16[128,1280]{1,0:T(8,128)(2,1)}, bf16[128,1280]{1,0:T(8,128)(2,1)S(1)}, u32[]{:S(2)}, u32[]{:S(2)}) collective-permute-start(bf16[128,1280]{1,0:T(8,128)(2,1)} %get-tuple-element.40), channel_id=1, source_target_pairs={{0,4},{4,8},{8,12},{12,14},{14,10},{10,6},{6,2},{2,0},{1,5},{5,9},... | collective-permute-start | bytes 983048 | tf_op jit(solution)/shard_map/ppermute | solution.py:104
  166.5 8.5 %collective-permute-start.14 = (bf16[128,1280]{1,0:T(8,128)(2,1)}, bf16[128,1280]{1,0:T(8,128)(2,1)}, u32[]{:S(2)}, u32[]{:S(2)}) collective-permute-start(bf16[128,1280]{1,0:T(8,128)(2,1)} %get-tuple-element.39), channel_id=1, source_target_pairs={{0,2},{4,0},{8,4},{12,8},{14,12},{10,14},{6,10},{2,6},{1,3},{5,1},... | collective-permute-start | bytes 983048 | tf_op jit(solution)/shard_map/ppermute | solution.py:96
  168.2 6.8 %copy-start.8 = (bf16[1024,512]{1,0:T(8,128)(2,1)S(1)}, bf16[1024,512]{1,0:T(8,128)(2,1)}, u32[]{:S(2)}) copy-start(bf16[1024,512]{1,0:T(8,128)(2,1)} %copy.48) | copy-start | bytes 3145732
  170.1 6.5 %collective-permute-start.24 = (f32[240,192]{1,0:T(8,128)S(1)}, f32[240,192]{1,0:T(8,128)S(1)}, u32[]{:S(2)}, u32[]{:S(2)}) collective-permute-start(f32[240,192]{1,0:T(8,128)S(1)} %get-tuple-element.29), channel_id=1, source_target_pairs={{0,4},{4,8},{8,12},{12,14},{14,10},{10,6},{6,2},{2,0},{1,5},{5,9},... | collective-permute-start | bytes 552968 | tf_op jit(solution)/shard_map/ppermute | solution.py:159
  171.6 6.2 %collective-permute-start.31 = (f32[240,192]{1,0:T(8,128)S(1)}, f32[240,192]{1,0:T(8,128)S(1)}, u32[]{:S(2)}, u32[]{:S(2)}) collective-permute-start(f32[240,192]{1,0:T(8,128)S(1)} %get-tuple-element.30), channel_id=1, source_target_pairs={{0,2},{4,0},{8,4},{12,8},{14,12},{10,14},{6,10},{2,6},{1,3},{5,1},... | collective-permute-start | bytes 552968 | tf_op jit(solution)/shard_map/ppermute | solution.py:159
  179.0 7.2 %collective-permute-start.25 = (f32[240,192]{1,0:T(8,128)S(1)}, f32[240,192]{1,0:T(8,128)S(1)}, u32[]{:S(2)}, u32[]{:S(2)}) collective-permute-start(f32[240,192]{1,0:T(8,128)S(1)} %get-tuple-element.27), channel_id=1, source_target_pairs={{0,4},{4,8},{8,12},{12,14},{14,10},{10,6},{6,2},{2,0},{1,5},{5,9},... | collective-permute-start | bytes 552968 | tf_op jit(solution)/shard_map/ppermute | solution.py:159
  180.3 6.9 %collective-permute-start.32 = (f32[240,192]{1,0:T(8,128)S(1)}, f32[240,192]{1,0:T(8,128)S(1)}, u32[]{:S(2)}, u32[]{:S(2)}) collective-permute-start(f32[240,192]{1,0:T(8,128)S(1)} %get-tuple-element.28), channel_id=1, source_target_pairs={{0,2},{4,0},{8,4},{12,8},{14,12},{10,14},{6,10},{2,6},{1,3},{5,1},... | collective-permute-start | bytes 552968 | tf_op jit(solution)/shard_map/ppermute | solution.py:159
  188.4 6.2 %collective-permute-start.26 = (f32[240,192]{1,0:T(8,128)S(1)}, f32[240,192]{1,0:T(8,128)S(1)}, u32[]{:S(2)}, u32[]{:S(2)}) collective-permute-start(f32[240,192]{1,0:T(8,128)S(1)} %get-tuple-element.25), channel_id=1, source_target_pairs={{0,4},{4,8},{8,12},{12,14},{14,10},{10,6},{6,2},{2,0},{1,5},{5,9},... | collective-permute-start | bytes 552968 | tf_op jit(solution)/shard_map/ppermute | solution.py:159
  190.0 6.2 %collective-permute-start.33 = (f32[240,192]{1,0:T(8,128)S(1)}, f32[240,192]{1,0:T(8,128)S(1)}, u32[]{:S(2)}, u32[]{:S(2)}) collective-permute-start(f32[240,192]{1,0:T(8,128)S(1)} %get-tuple-element.26), channel_id=1, source_target_pairs={{0,2},{4,0},{8,4},{12,8},{14,12},{10,14},{6,10},{2,6},{1,3},{5,1},... | collective-permute-start | bytes 552968 | tf_op jit(solution)/shard_map/ppermute | solution.py:159
  (13 other events, 29.5 us)

commit v5 on v4

--- a/solution.py
+++ b/solution.py
@@ -140,7 +140,7 @@
     return position
 
 
-def ring_reduce_scatter_sliced(select_block, axis, ring, forward_dir=True):
+def ring_reduce_scatter_sliced(select_block, axis, ring, forward_dir=True, wire_dtype=jnp.bfloat16):
     count = len(ring)
     forward, backward = ring_perms(ring)
     perm = forward if forward_dir else backward
@@ -154,10 +154,12 @@
             index = jnp.where(target == q, s, index)
         return select_block(index)
 
-    acc = block_at(1)
+    acc = block_at(1).astype(wire_dtype)
     for t in range(count - 1):
-        received = lax.ppermute(acc, axis, perm)
+        received = lax.ppermute(acc, axis, perm).astype(jnp.float32)
         acc = received + block_at(t + 2)
+        if t < count - 2:
+            acc = acc.astype(wire_dtype)
     return acc
 
 

time: 200 us -> 179 us (0.90)
  waiting for transfers between devices: 58.6 us -> 42.5 us
  other arithmetic: 33.6 us -> 31.2 us
  matrix products: 22.9 us -> 20.8 us
    ppermute x14, waiting for transfers between devices: 23.4 us -> 11.3 us  [ring_reduce_scatter_sliced(): received = lax.ppermute(acc, axis, perm).astype(jnp.float32)]
    add x7 -> x1, other arithmetic: 11.4 us -> 1.19 us  [ring_reduce_scatter_sliced(): acc = received + block_at(t + 2)]
    convert_element_type x0 -> x6, other arithmetic: none -> 8.19 us  [ring_reduce_scatter_sliced(): acc = acc.astype(wire_dtype)]
    ppermute x4, waiting for transfers between devices: 9.46 us -> 4.56 us  [ring_scatter_back(): received = lax.ppermute(acc, 'seq', backward).astype(jnp.float32)]
    ppermute x4, starting transfers between devices: 1.01 us -> 4.16 us  [ring_scatter_back(): received = lax.ppermute(acc, 'seq', backward).astype(jnp.float32)]
    unnamed x65 -> x57, local copies, waits for them, and re-layouts: 12.6 us -> 11.9 us
  transfers between devices with their start and end apart: 34 -> 34, of which waited for: 22 -> 17; matrix products, arithmetic and copies ran while one was open for 28% -> 29% of each run, Pallas kernels for 0% -> 0%
where the time goes in v5:
time: 179 us; the launch traced here: 178 us
  starting transfers between devices  44.5 us (25%)
  waiting for transfers between devices  42.5 us (24%)
  local copies, waits for them, and re-layouts  37.2 us (21%)
  other arithmetic  31.2 us (17%)
  matrix products  20.8 us (12%)
    ppermute x4, waiting for transfers between devices, ring_gather(): current = lax.ppermute(current, 'seq', forward)  19.4 us
    ppermute x14, starting transfers between devices, ring_reduce_scatter_sliced(): received = lax.ppermute(acc, axis, perm).astype(jnp.float32)  16.8 us
    unnamed x57, local copies, waits for them, and re-layouts  11.9 us
    ppermute x14, waiting for transfers between devices, ring_reduce_scatter_sliced(): received = lax.ppermute(acc, axis, perm).astype(jnp.float32)  11.3 us
    dot_general x5, matrix products, body(): jnp.einsum('spc,spo->co', both_padded[:, offset:offset + positions], both...  8.68 us
    ppermute x2, starting transfers between devices, extended(): before = lax.ppermute(last, axis, up)  8.31 us
    convert_element_type x6, other arithmetic, ring_reduce_scatter_sliced(): acc = acc.astype(wire_dtype)  8.19 us
    ppermute x4, starting transfers between devices, ring_gather(): current = lax.ppermute(current, 'seq', forward)  7.61 us
  transfers between devices with their start and end apart: 34, of which 17 were waited for; matrix products, arithmetic and copies ran while one was open for 29% of the time, Pallas kernels for 0%

profile of v5, /device:TPU:0, one launch (start us, length us, event | category | flops | bytes accessed | tf_op | source)
XLA Modules:
  0.0 177.6 jit_solution(9274675933939184991)
XLA Ops:
  3.9 3.1 %collective-permute-start = (bf16[128,1280]{0,1:T(8,128)(2,1)}, bf16[128,1280]{0,1:T(8,128)(2,1)S(1)}, u32[]{:S(2)}, u32[]{:S(2)}) collective-permute-start(bf16[128,1280]{0,1:T(8,128)(2,1)} %get-tuple-element.51), channel_id=1, source_target_pairs={{0,4},{4,8},{8,12},{12,14},{14,10},{10,6},{6,2},{2,0},{1,5},{5,9},... | collective-permute-start | bytes 983048 | tf_op jit(solution)/shard_map/ppermute | solution.py:75
  6.9 7.9 %collective-permute-done = bf16[128,1280]{0,1:T(8,128)(2,1)S(1)} collective-permute-done((bf16[128,1280]{0,1:T(8,128)(2,1)}, bf16[128,1280]{0,1:T(8,128)(2,1)S(1)}, u32[]{:S(2)}, u32[]{:S(2)}) %collective-permute-start) | collective-permute-done | bytes 327712 | tf_op jit(solution)/shard_map/ppermute | solution.py:75
  15.5 1.8 %collective-permute-start.1 = (bf16[128,1280]{0,1:T(8,128)(2,1)S(1)}, bf16[128,1280]{0,1:T(8,128)(2,1)}, u32[]{:S(2)}, u32[]{:S(2)}) collective-permute-start(bf16[128,1280]{0,1:T(8,128)(2,1)S(1)} %collective-permute-done), channel_id=1, source_target_pairs={{0,4},{4,8},{8,12},{12,14},{14,10},{10,6},{6,2},{2,0},{1,5},{5,9},... | collective-permute-start | bytes 983048 | tf_op jit(solution)/shard_map/ppermute | solution.py:75
  17.5 7.0 %collective-permute-done.1 = bf16[128,1280]{0,1:T(8,128)(2,1)} collective-permute-done((bf16[128,1280]{0,1:T(8,128)(2,1)S(1)}, bf16[128,1280]{0,1:T(8,128)(2,1)}, u32[]{:S(2)}, u32[]{:S(2)}) %collective-permute-start.1) | collective-permute-done | bytes 327712 | tf_op jit(solution)/shard_map/ppermute | solution.py:75
  24.5 1.5 collective-permute-start.2
  28.3 1.8 constant_dynamic-update-slice_fusion.6
  30.0 2.8 %collective-permute-done.2 = bf16[128,1280]{0,1:T(8,128)(2,1)} collective-permute-done((bf16[128,1280]{0,1:T(8,128)(2,1)}, bf16[128,1280]{0,1:T(8,128)(2,1)}, u32[]{:S(2)}, u32[]{:S(2)}) %collective-permute-start.2) | collective-permute-done | bytes 327712 | tf_op jit(solution)/shard_map/ppermute | solution.py:75
  34.1 1.8 constant_dynamic-update-slice_fusion.5
  36.6 1.7 constant_dynamic-update-slice_fusion.4
  38.4 1.8 %collective-permute-done.3 = bf16[128,1280]{0,1:T(8,128)(2,1)S(1)} collective-permute-done((bf16[128,1280]{0,1:T(8,128)(2,1)}, bf16[128,1280]{0,1:T(8,128)(2,1)S(1)}, u32[]{:S(2)}, u32[]{:S(2)}) %collective-permute-start.3) | collective-permute-done | bytes 327712 | tf_op jit(solution)/shard_map/ppermute | solution.py:75
  43.7 1.5 slice.126
  45.3 1.9 %slice.127 = bf16[1024,512]{0,1:T(8,128)(2,1)S(1)} slice(bf16[1024,1280]{0,1:T(8,128)(2,1)} %constant_dynamic-update-slice_fusion), slice={[0:1024], [0:512]} | slice | bytes 2097152 | tf_op jit(solution)/shard_map/slice | solution.py:174
  52.2 2.6 %broadcast_in_dim.26 = f32[1,256,768]{2,1,0:T(8,128)} reshape(f32[128,2,768]{2,1,0:T(2,128)} %broadcast_in_dim.12) | data formatting | bytes 1572864 | tf_op jit(solution)/shard_map/broadcast_in_dim | solution.py:191
  54.8 2.6 %reshape.151 = f32[256,768]{1,0:T(8,128)} reshape(f32[128,2,768]{2,1,0:T(2,128)} %broadcast_in_dim.12) | data formatting | bytes 1572864 | tf_op jit(solution)/shard_map/reshape | solution.py:191
  60.6 2.7 %collective-permute-start.7 = (bf16[2,768]{1,0:T(2,128)(2,1)S(1)}, bf16[2,768]{1,0:T(2,128)(2,1)S(1)}, u32[]{:S(2)}, u32[]{:S(2)}) collective-permute-start(bf16[2,768]{1,0:T(2,128)(2,1)S(1)} %get-tuple-element.50), channel_id=1, source_target_pairs={{0,2},{2,4},{4,6},{6,8},{8,10},{10,12},{12,14},{1,3},{3,5},{5,7},{... | collective-permute-start | bytes 9224 | tf_op jit(solution)/shard_map/ppermute | solution.py:24
  65.1 4.2 %collective-permute-done.8 = bf16[2,768]{1,0:T(2,128)(2,1)S(1)} collective-permute-done((bf16[2,768]{1,0:T(2,128)(2,1)S(1)}, bf16[2,768]{1,0:T(2,128)(2,1)S(1)}, u32[]{:S(2)}, u32[]{:S(2)}) %collective-permute-start.8) | collective-permute-done | bytes 3104 | tf_op jit(solution)/shard_map/ppermute | solution.py:25
  69.5 2.9 %fusion.34 = (bf16[256,384]{1,0:T(8,128)(2,1)S(1)}, bf16[1,256,384]{2,1,0:T(8,128)(2,1)}) fusion(bf16[1,256,384]{2,1,0:T(8,128)(2,1)} %param.15, bf16[256,3840]{1,0:T(8,128)(2,1)S(1)} %fusion.35, bf16[3840,384]{1,0:T(8,128)(2,1)S(1)} %copy-done), kind=kOutput, calls=%fused_computation.85 | convolution fusion | flops 756252672 | bytes 5505024 | tf_op jit(solution)/shard_map/dot_general | solution.py:197
  74.0 5.6 %collective-permute-start.10 = (bf16[2,384]{1,0:T(2,128)(2,1)S(1)}, bf16[2,384]{1,0:T(2,128)(2,1)S(1)}, u32[]{:S(2)}, u32[]{:S(2)}) collective-permute-start(bf16[2,384]{1,0:T(2,128)(2,1)S(1)} %get-tuple-element.53), channel_id=1, source_target_pairs={{0,2},{2,4},{4,6},{6,8},{8,10},{10,12},{12,14},{1,3},{3,5},{5,7},{... | collective-permute-start | bytes 4616 | tf_op jit(solution)/shard_map/ppermute | solution.py:24
  83.4 2.5 %reshape.153 = f32[128,2,768]{2,1,0:T(2,128)} reshape(f32[256,768]{1,0:T(8,128)} %get-tuple-element.22) | data formatting | bytes 1572864 | tf_op jit(solution)/shard_map/reshape | solution.py:275
  85.9 2.8 %reduce_sum.48 = bf16[128,768]{1,0:T(8,128)(2,1)} reduce(f32[128,2,768]{2,1,0:T(2,128)} %reshape.153, f32[]{:T(128)} %constant.150.clone.1), dimensions={1}, to_apply=%region_4.5 | reduce | flops 98304 | bytes 983044 | tf_op jit(solution)/shard_map/reduce_sum | solution.py:275
  88.7 1.7 copy.40
  91.4 3.2 %multiply_convert_fusion.1 = bf16[4,128,1024]{1,2,0:T(8,128)(2,1)S(1)} fusion(f32[4,1024,128]{2,1,0:T(8,128)} %copy-done.2, bf16[128,4,192]{0,2,1:T(8,128)(2,1)} %bitcast.205, bf16[1024,4,192]{0,2,1:T(8,128)(2,1)} %bitcast.193, f32[4,128]{1,0:T(4,128)S(1)} %bitcast.213, f32[4,128]{1,0:T(4,128)S(1)} %log_add_fusion), kind=kOutput, calls=%fused_computation.22 | convolution fusion | flops 203948032 | bytes 4919296 | tf_op jit(solution)/shard_map/ihd,jhd->hij/dot_general | solution.py:278
  94.7 2.0 %fusion.8 = f32[3840,384]{1,0:T(8,128)S(1)} fusion(bf16[1,260,768]{2,1,0:T(8,128)(2,1)S(1)} %copy-done.19, bf16[1,260,768]{2,1,0:T(8,128)(2,1)} %bitcast.31, bf16[1,256,384]{2,1,0:T(8,128)(2,1)} %bitcast.33, bf16[1,256,384]{2,1,0:T(8,128)(2,1)S(1)} %bitcast.197), kind=kOutput, calls=%fused_computation.34 | convolution fusion | flops 302579712 | bytes 2371584 | tf_op jit(solution)/shard_map/spc,spo->co/dot_general | solution.py:213
  96.7 1.7 fusion.7
  98.4 1.7 fusion.6
  100.1 1.7 fusion.5
  101.7 1.7 fusion.4
  103.9 4.5 %collective-permute-start.20 = (bf16[240,192]{1,0:T(8,128)(2,1)S(1)}, bf16[240,192]{1,0:T(8,128)(2,1)S(1)}, u32[]{:S(2)}, u32[]{:S(2)}) collective-permute-start(bf16[240,192]{1,0:T(8,128)(2,1)S(1)} %get-tuple-element.37), channel_id=1, source_target_pairs={{0,4},{4,8},{8,12},{12,14},{14,10},{10,6},{6,2},{2,0},{1,5},{5,9},... | collective-permute-start | bytes 276488 | tf_op jit(solution)/shard_map/ppermute | solution.py:159
  108.5 1.8 %convolution_convert_fusion = bf16[4,192,1024]{2,1,0:T(8,128)(2,1)} fusion(bf16[128,4,192]{0,2,1:T(8,128)(2,1)S(1)} %bitcast.206, f32[4,1024,128]{2,1,0:T(8,128)S(1)} %copy-done.3, f32[4,128]{1,0:T(4,128)S(1)} %log_add_fusion), kind=kOutput, calls=%fused_computation.24 | convolution fusion | flops 203685888 | bytes 3868672 | tf_op jit(solution)/shard_map/hij,ihd->jhd/dot_general | solution.py:290
  110.9 2.4 %collective-permute-done.27 = bf16[240,192]{1,0:T(8,128)(2,1)S(1)} collective-permute-done((bf16[240,192]{1,0:T(8,128)(2,1)S(1)}, bf16[240,192]{1,0:T(8,128)(2,1)S(1)}, u32[]{:S(2)}, u32[]{:S(2)}) %collective-permute-start.27) | collective-permute-done | bytes 92192 | tf_op jit(solution)/shard_map/ppermute | solution.py:159
  113.5 1.6 collective-permute-start.21
  117.0 2.6 %copy.49 = bf16[1024,768]{1,0:T(8,128)(2,1)} copy(bf16[1024,768]{0,1:T(8,128)(2,1)} %bitcast.196) | data formatting | bytes 3145728 | tf_op jit(solution)/shard_map/reshape | solution.py:294
  119.6 2.3 %copy.46 = bf16[1024,4,128]{0,2,1:T(8,128)(2,1)} copy(bf16[1024,4,128]{2,0,1:T(8,128)(2,1)} %fusion.9) | data formatting | bytes 2097152 | tf_op jit(solution)/shard_map/mul | solution.py:287
  121.8 2.3 %copy.48 = bf16[1024,512]{1,0:T(8,128)(2,1)} copy(bf16[1024,512]{0,1:T(8,128)(2,1)} %bitcast.202) | data formatting | bytes 2097152 | tf_op jit(solution)/shard_map/reshape | solution.py:293
  124.1 1.8 %fusion.55 = (bf16[240,192]{1,0:T(8,128)(2,1)}, bf16[240,192]{1,0:T(8,128)(2,1)S(1)}) fusion(f32[8,2,240,384]{3,2,1,0:T(8,128)} %bitcast.186, s32[]{:T(128)S(6)} %select_n.499, s32[]{:T(128)S(6)} %select_n.483, bf16[240,192]{1,0:T(8,128)(2,1)S(1)} %collective-permute-done.21, s32[]{:T(128)S(6)} %select_n.563, bf16[240,192]{1,0:T(8,128)(2,1)S(1)} %collective-permute-done.28), kind=kLoop, calls=%fused_computation.130 | loop fusion | flops 276480 | bytes 737292 | tf_op jit(solution)/shard_map/convert_element_type | solution.py:162
  125.9 1.6 collective-permute-start.22
  127.9 1.9 %fusion.40 = (bf16[128,1280]{1,0:T(8,128)(2,1)}, bf16[128,1280]{1,0:T(8,128)(2,1)S(1)}) fusion(bf16[1024,768]{1,0:T(8,128)(2,1)} %copy.49, bf16[1024,512]{1,0:T(8,128)(2,1)} %copy.48), kind=kLoop, calls=%fused_computation.100 | loop fusion | flops 1310720 | bytes 3276800 | tf_op jit(solution)/shard_map/concatenate | solution.py:291
  129.9 2.0 %collective-permute-start.15 = (bf16[128,1280]{1,0:T(8,128)(2,1)S(1)}, bf16[128,1280]{1,0:T(8,128)(2,1)}, u32[]{:S(2)}, u32[]{:S(2)}) collective-permute-start(bf16[128,1280]{1,0:T(8,128)(2,1)S(1)} %get-tuple-element.44), channel_id=1, source_target_pairs={{0,4},{4,8},{8,12},{12,14},{14,10},{10,6},{6,2},{2,0},{1,5},{5,9},... | collective-permute-start | bytes 983048 | tf_op jit(solution)/shard_map/ppermute | solution.py:104
  132.0 1.7 collective-permute-done.29
  133.8 1.9 %fusion.54 = (bf16[240,192]{1,0:T(8,128)(2,1)}, bf16[240,192]{1,0:T(8,128)(2,1)S(1)}) fusion(f32[8,2,240,384]{3,2,1,0:T(8,128)} %bitcast.187, s32[]{:T(128)S(6)} %select_n.507, s32[]{:T(128)S(6)} %select_n.483, bf16[240,192]{1,0:T(8,128)(2,1)S(1)} %collective-permute-done.22, s32[]{:T(128)S(6)} %select_n.571, bf16[240,192]{1,0:T(8,128)(2,1)} %collective-permute-done.29), kind=kLoop, calls=%fused_computation.128 | loop fusion | flops 276480 | bytes 737292 | tf_op jit(solution)/shard_map/convert_element_type | solution.py:162
  138.9 1.9 %add_convert_fusion.5 = bf16[128,1280]{1,0:T(8,128)(2,1)} fusion(bf16[128,1280]{1,0:T(8,128)(2,1)} %collective-permute-done.11, bf16[1024,768]{1,0:T(8,128)(2,1)} %copy.49, bf16[1024,512]{1,0:T(8,128)(2,1)} %copy.48), kind=kLoop, calls=%fused_computation.69 | loop fusion | flops 1146880 | bytes 3276800 | tf_op jit(solution)/shard_map/convert_element_type | solution.py:100
  144.8 2.0 %collective-permute-start.31 = (bf16[240,192]{1,0:T(8,128)(2,1)S(1)}, bf16[240,192]{1,0:T(8,128)(2,1)S(1)}, u32[]{:S(2)}, u32[]{:S(2)}) collective-permute-start(bf16[240,192]{1,0:T(8,128)(2,1)S(1)} %get-tuple-element.30), channel_id=1, source_target_pairs={{0,2},{4,0},{8,4},{12,8},{14,12},{10,14},{6,10},{2,6},{1,3},{5,1},... | collective-permute-start | bytes 276488 | tf_op jit(solution)/shard_map/ppermute | solution.py:159
  146.8 2.4 %collective-permute-done.12 = bf16[128,1280]{1,0:T(8,128)(2,1)} collective-permute-done((bf16[128,1280]{1,0:T(8,128)(2,1)}, bf16[128,1280]{1,0:T(8,128)(2,1)}, u32[]{:S(2)}, u32[]{:S(2)}) %collective-permute-start.12) | collective-permute-done | bytes 327712 | tf_op jit(solution)/shard_map/ppermute | solution.py:96
  149.2 2.3 %add_convert_fusion.4 = (bf16[128,1280]{1,0:T(8,128)(2,1)}, bf16[128,1280]{1,0:T(8,128)(2,1)}) fusion(bf16[128,1280]{1,0:T(8,128)(2,1)} %collective-permute-done.12, bf16[1024,768]{1,0:T(8,128)(2,1)} %copy.49, bf16[1024,512]{1,0:T(8,128)(2,1)} %copy.48, bf16[128,1280]{1,0:T(8,128)(2,1)} %collective-permute-done.15), kind=kLoop, calls=%fused_computation.68 | loop fusion | flops 2293760 | bytes 3932160 | tf_op jit(solution)/shard_map/convert_element_type | solution.py:100
  151.5 1.8 %collective-permute-start.13 = (bf16[128,1280]{1,0:T(8,128)(2,1)}, bf16[128,1280]{1,0:T(8,128)(2,1)S(1)}, u32[]{:S(2)}, u32[]{:S(2)}) collective-permute-start(bf16[128,1280]{1,0:T(8,128)(2,1)} %get-tuple-element.41), channel_id=1, source_target_pairs={{0,2},{4,0},{8,4},{12,8},{14,12},{10,14},{6,10},{2,6},{1,3},{5,1},... | collective-permute-start | bytes 983048 | tf_op jit(solution)/shard_map/ppermute | solution.py:96
  153.5 1.8 %fusion.52 = (bf16[240,192]{1,0:T(8,128)(2,1)}, bf16[240,192]{1,0:T(8,128)(2,1)}) fusion(f32[8,2,240,384]{3,2,1,0:T(8,128)} %bitcast.189, s32[]{:T(128)S(6)} %select_n.523, s32[]{:T(128)S(6)} %select_n.483, bf16[240,192]{1,0:T(8,128)(2,1)S(1)} %collective-permute-done.24, s32[]{:T(128)S(6)} %select_n.587, bf16[240,192]{1,0:T(8,128)(2,1)S(1)} %collective-permute-done.31), kind=kLoop, calls=%fused_computation.124 | loop fusion | flops 276480 | bytes 737292 | tf_op jit(solution)/shard_map/convert_element_type | solution.py:162
  158.6 4.7 %collective-permute-done.25 = bf16[240,192]{1,0:T(8,128)(2,1)S(1)} collective-permute-done((bf16[240,192]{1,0:T(8,128)(2,1)}, bf16[240,192]{1,0:T(8,128)(2,1)S(1)}, u32[]{:S(2)}, u32[]{:S(2)}) %collective-permute-start.25) | collective-permute-done | bytes 92192 | tf_op jit(solution)/shard_map/ppermute | solution.py:159
  172.5 2.7 %collective-permute-done.17 = bf16[128,1280]{1,0:T(8,128)(2,1)S(1)} collective-permute-done((bf16[128,1280]{1,0:T(8,128)(2,1)S(1)}, bf16[128,1280]{1,0:T(8,128)(2,1)S(1)}, u32[]{:S(2)}, u32[]{:S(2)}) %collective-permute-start.17) | collective-permute-done | bytes 327712 | tf_op jit(solution)/shard_map/ppermute | solution.py:104
  (143 shorter events, 54.3 us)
Async XLA Ops:
  0.6 68.9 %copy-start = (bf16[3840,384]{1,0:T(8,128)(2,1)S(1)}, bf16[3840,384]{1,0:T(8,128)(2,1)}, u32[]{:S(2)}) copy-start(bf16[3840,384]{1,0:T(8,128)(2,1)} %param.14) | copy-start | bytes 8847364
  3.9 10.9 %collective-permute-start = (bf16[128,1280]{0,1:T(8,128)(2,1)}, bf16[128,1280]{0,1:T(8,128)(2,1)S(1)}, u32[]{:S(2)}, u32[]{:S(2)}) collective-permute-start(bf16[128,1280]{0,1:T(8,128)(2,1)} %get-tuple-element.51), channel_id=1, source_target_pairs={{0,4},{4,8},{8,12},{12,14},{14,10},{10,6},{6,2},{2,0},{1,5},{5,9},... | collective-permute-start | bytes 983048 | tf_op jit(solution)/shard_map/ppermute | solution.py:75
  15.5 9.0 %collective-permute-start.1 = (bf16[128,1280]{0,1:T(8,128)(2,1)S(1)}, bf16[128,1280]{0,1:T(8,128)(2,1)}, u32[]{:S(2)}, u32[]{:S(2)}) collective-permute-start(bf16[128,1280]{0,1:T(8,128)(2,1)S(1)} %collective-permute-done), channel_id=1, source_target_pairs={{0,4},{4,8},{8,12},{12,14},{14,10},{10,6},{6,2},{2,0},{1,5},{5,9},... | collective-permute-start | bytes 983048 | tf_op jit(solution)/shard_map/ppermute | solution.py:75
  17.3 10.4 %collective-permute-start.4 = (bf16[128,1280]{0,1:T(8,128)(2,1)}, bf16[128,1280]{0,1:T(8,128)(2,1)S(1)}, u32[]{:S(2)}, u32[]{:S(2)}) collective-permute-start(bf16[128,1280]{0,1:T(8,128)(2,1)} %get-tuple-element.51), channel_id=1, source_target_pairs={{0,2},{4,0},{8,4},{12,8},{14,12},{10,14},{6,10},{2,6},{1,3},{5,1},... | collective-permute-start | bytes 983048 | tf_op jit(solution)/shard_map/ppermute | solution.py:79
  24.5 8.3 %collective-permute-start.2 = (bf16[128,1280]{0,1:T(8,128)(2,1)}, bf16[128,1280]{0,1:T(8,128)(2,1)}, u32[]{:S(2)}, u32[]{:S(2)}) collective-permute-start(bf16[128,1280]{0,1:T(8,128)(2,1)} %collective-permute-done.1), channel_id=1, source_target_pairs={{0,4},{4,8},{8,12},{12,14},{14,10},{10,6},{6,2},{2,0},{1,5},{5,9},... | collective-permute-start | bytes 983048 | tf_op jit(solution)/shard_map/ppermute | solution.py:75
  27.7 19.4 %copy-start.17 = (bf16[1,128,512]{1,2,0:T(8,128)(2,1)}, bf16[1,128,512]{1,2,0:T(8,128)(2,1)S(1)}, u32[]{:S(2)}) copy-start(bf16[1,128,512]{1,2,0:T(8,128)(2,1)S(1)} %copy.68) | copy-start | bytes 393220
  27.7 8.1 %collective-permute-start.5 = (bf16[128,1280]{0,1:T(8,128)(2,1)S(1)}, bf16[128,1280]{0,1:T(8,128)(2,1)S(1)}, u32[]{:S(2)}, u32[]{:S(2)}) collective-permute-start(bf16[128,1280]{0,1:T(8,128)(2,1)S(1)} %collective-permute-done.4), channel_id=1, source_target_pairs={{0,2},{4,0},{8,4},{12,8},{14,12},{10,14},{6,10},{2,6},{1,3},{5,1},... | collective-permute-start | bytes 983048 | tf_op jit(solution)/shard_map/ppermute | solution.py:79
  32.8 7.4 %collective-permute-start.3 = (bf16[128,1280]{0,1:T(8,128)(2,1)}, bf16[128,1280]{0,1:T(8,128)(2,1)S(1)}, u32[]{:S(2)}, u32[]{:S(2)}) collective-permute-start(bf16[128,1280]{0,1:T(8,128)(2,1)} %collective-permute-done.2), channel_id=1, source_target_pairs={{0,4},{4,8},{8,12},{12,14},{14,10},{10,6},{6,2},{2,0},{1,5},{5,9},... | collective-permute-start | bytes 983048 | tf_op jit(solution)/shard_map/ppermute | solution.py:75
  35.8 7.1 %collective-permute-start.6 = (bf16[128,1280]{0,1:T(8,128)(2,1)S(1)}, bf16[128,1280]{0,1:T(8,128)(2,1)S(1)}, u32[]{:S(2)}, u32[]{:S(2)}) collective-permute-start(bf16[128,1280]{0,1:T(8,128)(2,1)S(1)} %collective-permute-done.5), channel_id=1, source_target_pairs={{0,2},{4,0},{8,4},{12,8},{14,12},{10,14},{6,10},{2,6},{1,3},{5,1},... | collective-permute-start | bytes 983048 | tf_op jit(solution)/shard_map/ppermute | solution.py:79
  51.0 6.3 %copy-start.12 = (bf16[1,256,768]{2,1,0:T(8,128)(2,1)S(1)}, bf16[1,256,768]{2,1,0:T(8,128)(2,1)}, u32[]{:S(2)}) copy-start(bf16[1,256,768]{2,1,0:T(8,128)(2,1)} %param.12) | copy-start | bytes 1179652
  60.6 4.2 %collective-permute-start.7 = (bf16[2,768]{1,0:T(2,128)(2,1)S(1)}, bf16[2,768]{1,0:T(2,128)(2,1)S(1)}, u32[]{:S(2)}, u32[]{:S(2)}) collective-permute-start(bf16[2,768]{1,0:T(2,128)(2,1)S(1)} %get-tuple-element.50), channel_id=1, source_target_pairs={{0,2},{2,4},{4,6},{6,8},{8,10},{10,12},{12,14},{1,3},{3,5},{5,7},{... | collective-permute-start | bytes 9224 | tf_op jit(solution)/shard_map/ppermute | solution.py:24
  63.6 5.7 %collective-permute-start.8 = (bf16[2,768]{1,0:T(2,128)(2,1)S(1)}, bf16[2,768]{1,0:T(2,128)(2,1)S(1)}, u32[]{:S(2)}, u32[]{:S(2)}) collective-permute-start(bf16[2,768]{1,0:T(2,128)(2,1)S(1)} %get-tuple-element.49), channel_id=1, source_target_pairs={{2,0},{4,2},{6,4},{8,6},{10,8},{12,10},{14,12},{3,1},{5,3},{7,5},{... | collective-permute-start | bytes 9224 | tf_op jit(solution)/shard_map/ppermute | solution.py:25
  72.4 8.6 %copy-start.7 = (f32[256,768]{1,0:T(8,128)S(1)}, f32[256,768]{1,0:T(8,128)}, u32[]{:S(2)}) copy-start(f32[256,768]{1,0:T(8,128)} %reshape.151) | copy-start | bytes 2359300
  72.5 8.6 %copy-start.13 = (bf16[1,256,768]{2,1,0:T(8,128)(2,1)S(1)}, bf16[1,256,768]{2,1,0:T(8,128)(2,1)}, u32[]{:S(2)}) copy-start(bf16[1,256,768]{2,1,0:T(8,128)(2,1)} %param.12) | copy-start | bytes 1179652
  72.5 22.2 %collective-permute-start.19 = (bf16[256,384]{1,0:T(8,128)(2,1)S(1)}, bf16[256,384]{1,0:T(8,128)(2,1)}, u32[]{:S(2)}, u32[]{:S(2)}) collective-permute-start(bf16[256,384]{1,0:T(8,128)(2,1)S(1)} %get-tuple-element.47), channel_id=1, source_target_pairs={{0,1},{1,0},{2,3},{3,2},{4,5},{5,4},{6,7},{7,6},{8,9},{9,8},{10,11... | collective-permute-start | bytes 589832 | tf_op jit(solution)/shard_map/ppermute | solution.py:209
  72.5 8.2 %collective-permute-start.9 = (bf16[2,384]{1,0:T(2,128)(2,1)S(1)}, bf16[2,384]{1,0:T(2,128)(2,1)S(1)}, u32[]{:S(2)}, u32[]{:S(2)}) collective-permute-start(bf16[2,384]{1,0:T(2,128)(2,1)S(1)} %get-tuple-element.54), channel_id=1, source_target_pairs={{2,0},{4,2},{6,4},{8,6},{10,8},{12,10},{14,12},{3,1},{5,3},{7,5},{... | collective-permute-start | bytes 4616 | tf_op jit(solution)/shard_map/ppermute | solution.py:25
  74.0 6.9 %collective-permute-start.10 = (bf16[2,384]{1,0:T(2,128)(2,1)S(1)}, bf16[2,384]{1,0:T(2,128)(2,1)S(1)}, u32[]{:S(2)}, u32[]{:S(2)}) collective-permute-start(bf16[2,384]{1,0:T(2,128)(2,1)S(1)} %get-tuple-element.53), channel_id=1, source_target_pairs={{0,2},{2,4},{4,6},{6,8},{8,10},{10,12},{12,14},{1,3},{3,5},{5,7},{... | collective-permute-start | bytes 4616 | tf_op jit(solution)/shard_map/ppermute | solution.py:24
  80.6 14.1 %collective-permute-start.18 = (bf16[260,768]{1,0:T(8,128)(2,1)}, bf16[260,768]{1,0:T(8,128)(2,1)}, u32[]{:S(2)}, u32[]{:S(2)}) collective-permute-start(bf16[260,768]{1,0:T(8,128)(2,1)} %get-tuple-element.45), channel_id=1, source_target_pairs={{0,1},{1,0},{2,3},{3,2},{4,5},{5,4},{6,7},{7,6},{8,9},{9,8},{10,11... | collective-permute-start | bytes 1198088 | tf_op jit(solution)/shard_map/ppermute | solution.py:208
  83.4 7.0 %copy-start.15 = (f32[4,192,128]{2,1,0:T(8,128)S(1)}, f32[4,192,128]{2,1,0:T(8,128)}, u32[]{:S(2)}) copy-start(f32[4,192,128]{2,1,0:T(8,128)} %copy-done.14) | copy-start | bytes 1179652
  94.7 20.9 %copy-start.10 = (bf16[4,128,1024]{1,2,0:T(8,128)(2,1)}, bf16[4,128,1024]{1,2,0:T(8,128)(2,1)S(1)}, u32[]{:S(2)}) copy-start(bf16[4,128,1024]{1,2,0:T(8,128)(2,1)S(1)} %multiply_convert_fusion.1) | copy-start | bytes 3145732
  103.4 5.1 %copy-start.3 = (f32[4,1024,128]{2,1,0:T(8,128)S(1)}, f32[4,1024,128]{2,1,0:T(8,128)}, u32[]{:S(2)}) copy-start(f32[4,1024,128]{2,1,0:T(8,128)} %copy-done.2) | copy-start | bytes 6291460
  103.8 9.5 %copy-start.5 = (f32[3840,384]{1,0:T(8,128)}, f32[3840,384]{1,0:T(8,128)S(1)}, u32[]{:S(2)}) copy-start(f32[3840,384]{1,0:T(8,128)S(1)} %broadcast_multiply_fusion) | copy-start | bytes 17694724
  103.9 7.0 %collective-permute-start.20 = (bf16[240,192]{1,0:T(8,128)(2,1)S(1)}, bf16[240,192]{1,0:T(8,128)(2,1)S(1)}, u32[]{:S(2)}, u32[]{:S(2)}) collective-permute-start(bf16[240,192]{1,0:T(8,128)(2,1)S(1)} %get-tuple-element.37), channel_id=1, source_target_pairs={{0,4},{4,8},{8,12},{12,14},{14,10},{10,6},{6,2},{2,0},{1,5},{5,9},... | collective-permute-start | bytes 276488 | tf_op jit(solution)/shard_map/ppermute | solution.py:159
  108.5 7.1 %copy-start.18 = (bf16[1,128,512]{1,2,0:T(8,128)(2,1)S(1)}, bf16[1,128,512]{1,2,0:T(8,128)(2,1)}, u32[]{:S(2)}) copy-start(bf16[1,128,512]{1,2,0:T(8,128)(2,1)} %copy-done.17) | copy-start | bytes 393220
  108.5 4.9 %collective-permute-start.27 = (bf16[240,192]{1,0:T(8,128)(2,1)S(1)}, bf16[240,192]{1,0:T(8,128)(2,1)S(1)}, u32[]{:S(2)}, u32[]{:S(2)}) collective-permute-start(bf16[240,192]{1,0:T(8,128)(2,1)S(1)} %get-tuple-element.38), channel_id=1, source_target_pairs={{0,2},{4,0},{8,4},{12,8},{14,12},{10,14},{6,10},{2,6},{1,3},{5,1},... | collective-permute-start | bytes 276488 | tf_op jit(solution)/shard_map/ppermute | solution.py:159
  113.5 10.6 %collective-permute-start.21 = (bf16[240,192]{1,0:T(8,128)(2,1)S(1)}, bf16[240,192]{1,0:T(8,128)(2,1)S(1)}, u32[]{:S(2)}, u32[]{:S(2)}) collective-permute-start(bf16[240,192]{1,0:T(8,128)(2,1)S(1)} %get-tuple-element.35), channel_id=1, source_target_pairs={{0,4},{4,8},{8,12},{12,14},{14,10},{10,6},{6,2},{2,0},{1,5},{5,9},... | collective-permute-start | bytes 276488 | tf_op jit(solution)/shard_map/ppermute | solution.py:159
  115.1 9.0 %collective-permute-start.28 = (bf16[240,192]{1,0:T(8,128)(2,1)S(1)}, bf16[240,192]{1,0:T(8,128)(2,1)S(1)}, u32[]{:S(2)}, u32[]{:S(2)}) collective-permute-start(bf16[240,192]{1,0:T(8,128)(2,1)S(1)} %get-tuple-element.36), channel_id=1, source_target_pairs={{0,2},{4,0},{8,4},{12,8},{14,12},{10,14},{6,10},{2,6},{1,3},{5,1},... | collective-permute-start | bytes 276488 | tf_op jit(solution)/shard_map/ppermute | solution.py:159
  125.9 6.1 %collective-permute-start.22 = (bf16[240,192]{1,0:T(8,128)(2,1)}, bf16[240,192]{1,0:T(8,128)(2,1)S(1)}, u32[]{:S(2)}, u32[]{:S(2)}) collective-permute-start(bf16[240,192]{1,0:T(8,128)(2,1)} %get-tuple-element.33), channel_id=1, source_target_pairs={{0,4},{4,8},{8,12},{12,14},{14,10},{10,6},{6,2},{2,0},{1,5},{5,9},... | collective-permute-start | bytes 276488 | tf_op jit(solution)/shard_map/ppermute | solution.py:159
  127.5 6.3 %collective-permute-start.29 = (bf16[240,192]{1,0:T(8,128)(2,1)S(1)}, bf16[240,192]{1,0:T(8,128)(2,1)}, u32[]{:S(2)}, u32[]{:S(2)}) collective-permute-start(bf16[240,192]{1,0:T(8,128)(2,1)S(1)} %get-tuple-element.34), channel_id=1, source_target_pairs={{0,2},{4,0},{8,4},{12,8},{14,12},{10,14},{6,10},{2,6},{1,3},{5,1},... | collective-permute-start | bytes 276488 | tf_op jit(solution)/shard_map/ppermute | solution.py:159
  129.9 9.1 %collective-permute-start.11 = (bf16[128,1280]{1,0:T(8,128)(2,1)}, bf16[128,1280]{1,0:T(8,128)(2,1)}, u32[]{:S(2)}, u32[]{:S(2)}) collective-permute-start(bf16[128,1280]{1,0:T(8,128)(2,1)} %get-tuple-element.43), channel_id=1, source_target_pairs={{0,2},{4,0},{8,4},{12,8},{14,12},{10,14},{6,10},{2,6},{1,3},{5,1},... | collective-permute-start | bytes 983048 | tf_op jit(solution)/shard_map/ppermute | solution.py:96
  129.9 17.0 %collective-permute-start.15 = (bf16[128,1280]{1,0:T(8,128)(2,1)S(1)}, bf16[128,1280]{1,0:T(8,128)(2,1)}, u32[]{:S(2)}, u32[]{:S(2)}) collective-permute-start(bf16[128,1280]{1,0:T(8,128)(2,1)S(1)} %get-tuple-element.44), channel_id=1, source_target_pairs={{0,4},{4,8},{8,12},{12,14},{14,10},{10,6},{6,2},{2,0},{1,5},{5,9},... | collective-permute-start | bytes 983048 | tf_op jit(solution)/shard_map/ppermute | solution.py:104
  135.6 6.4 %collective-permute-start.23 = (bf16[240,192]{1,0:T(8,128)(2,1)}, bf16[240,192]{1,0:T(8,128)(2,1)S(1)}, u32[]{:S(2)}, u32[]{:S(2)}) collective-permute-start(bf16[240,192]{1,0:T(8,128)(2,1)} %get-tuple-element.31), channel_id=1, source_target_pairs={{0,4},{4,8},{8,12},{12,14},{14,10},{10,6},{6,2},{2,0},{1,5},{5,9},... | collective-permute-start | bytes 276488 | tf_op jit(solution)/shard_map/ppermute | solution.py:159
  137.2 6.3 %collective-permute-start.30 = (bf16[240,192]{1,0:T(8,128)(2,1)S(1)}, bf16[240,192]{1,0:T(8,128)(2,1)}, u32[]{:S(2)}, u32[]{:S(2)}) collective-permute-start(bf16[240,192]{1,0:T(8,128)(2,1)S(1)} %get-tuple-element.32), channel_id=1, source_target_pairs={{0,2},{4,0},{8,4},{12,8},{14,12},{10,14},{6,10},{2,6},{1,3},{5,1},... | collective-permute-start | bytes 276488 | tf_op jit(solution)/shard_map/ppermute | solution.py:159
  140.8 8.4 %collective-permute-start.12 = (bf16[128,1280]{1,0:T(8,128)(2,1)}, bf16[128,1280]{1,0:T(8,128)(2,1)}, u32[]{:S(2)}, u32[]{:S(2)}) collective-permute-start(bf16[128,1280]{1,0:T(8,128)(2,1)} %add_convert_fusion.5), channel_id=1, source_target_pairs={{0,2},{4,0},{8,4},{12,8},{14,12},{10,14},{6,10},{2,6},{1,3},{5,1},... | collective-permute-start | bytes 983048 | tf_op jit(solution)/shard_map/ppermute | solution.py:96
  144.7 8.8 %collective-permute-start.24 = (bf16[240,192]{1,0:T(8,128)(2,1)S(1)}, bf16[240,192]{1,0:T(8,128)(2,1)S(1)}, u32[]{:S(2)}, u32[]{:S(2)}) collective-permute-start(bf16[240,192]{1,0:T(8,128)(2,1)S(1)} %get-tuple-element.29), channel_id=1, source_target_pairs={{0,4},{4,8},{8,12},{12,14},{14,10},{10,6},{6,2},{2,0},{1,5},{5,9},... | collective-permute-start | bytes 276488 | tf_op jit(solution)/shard_map/ppermute | solution.py:159
  144.8 12.6 %copy-start.9 = (bf16[1024,512]{0,1:T(8,128)(2,1)S(1)}, bf16[1024,512]{0,1:T(8,128)(2,1)}, u32[]{:S(2)}) copy-start(bf16[1024,512]{0,1:T(8,128)(2,1)} %copy-done.8) | copy-start | bytes 3145732
  144.8 12.6 %copy-start.11 = (bf16[4,128,1024]{1,2,0:T(8,128)(2,1)S(1)}, bf16[4,128,1024]{1,2,0:T(8,128)(2,1)}, u32[]{:S(2)}) copy-start(bf16[4,128,1024]{1,2,0:T(8,128)(2,1)} %copy-done.10) | copy-start | bytes 3145732
  144.8 8.7 %collective-permute-start.31 = (bf16[240,192]{1,0:T(8,128)(2,1)S(1)}, bf16[240,192]{1,0:T(8,128)(2,1)S(1)}, u32[]{:S(2)}, u32[]{:S(2)}) collective-permute-start(bf16[240,192]{1,0:T(8,128)(2,1)S(1)} %get-tuple-element.30), channel_id=1, source_target_pairs={{0,2},{4,0},{8,4},{12,8},{14,12},{10,14},{6,10},{2,6},{1,3},{5,1},... | collective-permute-start | bytes 276488 | tf_op jit(solution)/shard_map/ppermute | solution.py:159
  151.5 15.1 %collective-permute-start.13 = (bf16[128,1280]{1,0:T(8,128)(2,1)}, bf16[128,1280]{1,0:T(8,128)(2,1)S(1)}, u32[]{:S(2)}, u32[]{:S(2)}) collective-permute-start(bf16[128,1280]{1,0:T(8,128)(2,1)} %get-tuple-element.41), channel_id=1, source_target_pairs={{0,2},{4,0},{8,4},{12,8},{14,12},{10,14},{6,10},{2,6},{1,3},{5,1},... | collective-permute-start | bytes 983048 | tf_op jit(solution)/shard_map/ppermute | solution.py:96
  153.3 13.4 %collective-permute-start.16 = (bf16[128,1280]{1,0:T(8,128)(2,1)}, bf16[128,1280]{1,0:T(8,128)(2,1)}, u32[]{:S(2)}, u32[]{:S(2)}) collective-permute-start(bf16[128,1280]{1,0:T(8,128)(2,1)} %get-tuple-element.42), channel_id=1, source_target_pairs={{0,4},{4,8},{8,12},{12,14},{14,10},{10,6},{6,2},{2,0},{1,5},{5,9},... | collective-permute-start | bytes 983048 | tf_op jit(solution)/shard_map/ppermute | solution.py:104
  155.4 7.9 %collective-permute-start.25 = (bf16[240,192]{1,0:T(8,128)(2,1)}, bf16[240,192]{1,0:T(8,128)(2,1)S(1)}, u32[]{:S(2)}, u32[]{:S(2)}) collective-permute-start(bf16[240,192]{1,0:T(8,128)(2,1)} %get-tuple-element.27), channel_id=1, source_target_pairs={{0,4},{4,8},{8,12},{12,14},{14,10},{10,6},{6,2},{2,0},{1,5},{5,9},... | collective-permute-start | bytes 276488 | tf_op jit(solution)/shard_map/ppermute | solution.py:159
  156.8 6.5 %collective-permute-start.32 = (bf16[240,192]{1,0:T(8,128)(2,1)}, bf16[240,192]{1,0:T(8,128)(2,1)}, u32[]{:S(2)}, u32[]{:S(2)}) collective-permute-start(bf16[240,192]{1,0:T(8,128)(2,1)} %get-tuple-element.28), channel_id=1, source_target_pairs={{0,2},{4,0},{8,4},{12,8},{14,12},{10,14},{6,10},{2,6},{1,3},{5,1},... | collective-permute-start | bytes 276488 | tf_op jit(solution)/shard_map/ppermute | solution.py:159
  164.6 5.6 %collective-permute-start.26 = (bf16[240,192]{1,0:T(8,128)(2,1)S(1)}, bf16[240,192]{1,0:T(8,128)(2,1)S(1)}, u32[]{:S(2)}, u32[]{:S(2)}) collective-permute-start(bf16[240,192]{1,0:T(8,128)(2,1)S(1)} %get-tuple-element.25), channel_id=1, source_target_pairs={{0,4},{4,8},{8,12},{12,14},{14,10},{10,6},{6,2},{2,0},{1,5},{5,9},... | collective-permute-start | bytes 276488 | tf_op jit(solution)/shard_map/ppermute | solution.py:159
  165.5 10.6 %copy-start.1 = (bf16[1024,768]{1,0:T(8,128)(2,1)S(1)}, bf16[1024,768]{1,0:T(8,128)(2,1)}, u32[]{:S(2)}) copy-start(bf16[1024,768]{1,0:T(8,128)(2,1)} %copy.49) | copy-start | bytes 4718596
  165.5 10.6 %copy-start.4 = (bf16[1024,512]{1,0:T(8,128)(2,1)S(1)}, bf16[1024,512]{1,0:T(8,128)(2,1)}, u32[]{:S(2)}) copy-start(bf16[1024,512]{1,0:T(8,128)(2,1)} %copy.48) | copy-start | bytes 3145732
  165.5 4.9 %collective-permute-start.33 = (bf16[240,192]{1,0:T(8,128)(2,1)S(1)}, bf16[240,192]{1,0:T(8,128)(2,1)S(1)}, u32[]{:S(2)}, u32[]{:S(2)}) collective-permute-start(bf16[240,192]{1,0:T(8,128)(2,1)S(1)} %get-tuple-element.26), channel_id=1, source_target_pairs={{0,2},{4,0},{8,4},{12,8},{14,12},{10,14},{6,10},{2,6},{1,3},{5,1},... | collective-permute-start | bytes 276488 | tf_op jit(solution)/shard_map/ppermute | solution.py:159
  168.1 7.1 %collective-permute-start.17 = (bf16[128,1280]{1,0:T(8,128)(2,1)S(1)}, bf16[128,1280]{1,0:T(8,128)(2,1)S(1)}, u32[]{:S(2)}, u32[]{:S(2)}) collective-permute-start(bf16[128,1280]{1,0:T(8,128)(2,1)S(1)} %get-tuple-element.40), channel_id=1, source_target_pairs={{0,4},{4,8},{8,12},{12,14},{14,10},{10,6},{6,2},{2,0},{1,5},{5,9},... | collective-permute-start | bytes 983048 | tf_op jit(solution)/shard_map/ppermute | solution.py:104
  169.0 7.1 %collective-permute-start.14 = (bf16[128,1280]{1,0:T(8,128)(2,1)S(1)}, bf16[128,1280]{1,0:T(8,128)(2,1)S(1)}, u32[]{:S(2)}, u32[]{:S(2)}) collective-permute-start(bf16[128,1280]{1,0:T(8,128)(2,1)S(1)} %get-tuple-element.39), channel_id=1, source_target_pairs={{0,2},{4,0},{8,4},{12,8},{14,12},{10,14},{6,10},{2,6},{1,3},{5,1},... | collective-permute-start | bytes 983048 | tf_op jit(solution)/shard_map/ppermute | solution.py:96
  (9 other events, 18.2 us)

commit v6 on v5

--- a/solution.py
+++ b/solution.py
@@ -170,9 +170,12 @@
     half_kernel = KW // 2
     query_heads = queries[0].reshape(local_tokens, H, DK)
     key_value_blocks = ring_gather(jnp.concatenate([key_rows[0], value_rows[0]], axis=1), ring)
-    gathered = jnp.concatenate(key_value_blocks, axis=0)
-    all_keys = gathered[:, : H * DK].reshape(-1, H, DK)
-    all_values = gathered[:, H * DK :].reshape(-1, H, DV)
+    all_keys = jnp.concatenate([block[:, : H * DK] for block in key_value_blocks], axis=0).reshape(
+        -1, H, DK
+    )
+    all_values = jnp.concatenate(
+        [block[:, H * DK :] for block in key_value_blocks], axis=0
+    ).reshape(-1, H, DV)
     scores = (
         jnp.einsum("ihd,jhd->hij", query_heads, all_keys, preferred_element_type=jnp.float32)
         * score_scale
@@ -185,10 +188,16 @@
     attended = jnp.einsum(
         "hij,jhd->ihd", rounded, all_values, preferred_element_type=jnp.float32
     ).astype(jnp.bfloat16)
-    hidden = trunk_state[0].astype(jnp.float32) + attended.reshape(local_tokens, H * DV).astype(
-        jnp.float32
-    )
-    merged = jnp.repeat(hidden, 2, axis=0) + skip_input[0].astype(jnp.float32)
+    upsample = (
+        jnp.arange(positions, dtype=jnp.int32)[:, None] // 2
+        == jnp.arange(local_tokens, dtype=jnp.int32)[None, :]
+    ).astype(jnp.bfloat16)
+    hidden_up = jnp.dot(
+        upsample, trunk_state[0], preferred_element_type=jnp.float32
+    ) + jnp.dot(
+        upsample, attended.reshape(local_tokens, H * DV), preferred_element_type=jnp.float32
+    )
+    merged = hidden_up + skip_input[0].astype(jnp.float32)
     inverse = lax.rsqrt(jnp.mean(merged * merged, axis=1, keepdims=True) + 1e-06)
     channel_gain = norm_gain.astype(jnp.float32)
     normed = (merged * inverse * channel_gain).astype(jnp.bfloat16)
@@ -272,7 +281,12 @@
         scaled_grad * merged, axis=1, keepdims=True
     )
     grad_skip = grad_merged.astype(jnp.bfloat16)
-    grad_trunk = grad_merged.reshape(local_tokens, 2, C).sum(axis=1).astype(jnp.bfloat16)
+    grad_trunk = jnp.dot(
+        upsample.T.astype(jnp.float32),
+        grad_merged,
+        precision=lax.Precision.HIGHEST,
+        preferred_element_type=jnp.float32,
+    ).astype(jnp.bfloat16)
     grad_heads = grad_trunk.reshape(local_tokens, H, DV)
     row_delta = jnp.sum(grad_heads.astype(jnp.float32) * attended.astype(jnp.float32), axis=2)
     value_grad = jnp.einsum(

time: 179 us -> 176 us (0.983)
  local copies, waits for them, and re-layouts: 37.2 us -> 52.8 us
  waiting for transfers between devices: 42.5 us -> 28.1 us
  other arithmetic: 31.2 us -> 23.7 us
  matrix products: 20.8 us -> 24.8 us
    ppermute x4, waiting for transfers between devices: 19.4 us -> 4.97 us  [ring_gather(): current = lax.ppermute(current, 'seq', forward)]
    slice x2 -> x14, local copies, waits for them, and re-layouts: 3.39 us -> 15.8 us  [the longest x7 8.36 us: body(): block[:, :H * DK]]
    concatenate x1 -> x10, local copies, waits for them, and re-layouts: 0.82 us -> 9.2 us  [the longest x9 9.14 us: body(): jnp.concatenate([block[:, :H * DK] for block in key_value_blocks], axis=0)]
    reshape x2 -> x0, local copies, waits for them, and re-layouts: 5.09 us -> none  [the longest x1 2.56 us: body(): merged = jnp.repeat(hidden, 2, axis=0) + skip_input[0].astype(jnp.float32)]
    unnamed x57 -> x68, local copies, waits for them, and re-layouts: 11.9 us -> 17 us
    reduce_sum x2 -> x0, other arithmetic: 4.08 us -> none  [the longest x1 2.76 us: body(): grad_merged.reshape(local_tokens, 2, C).sum(axis=1).astype(jnp.bfloat16)]
    broadcast_in_dim x2 -> x0, local copies, waits for them, and re-layouts: 3.74 us -> none  [body(): merged = jnp.repeat(hidden, 2, axis=0) + skip_input[0].astype(jnp.float32)]
    dot_general x0 -> x3, matrix products: none -> 3.71 us  [the longest x1 2.15 us: body(): jnp.dot(upsample, trunk_state[0], preferred_element_type=jnp.float32)]
  transfers between devices with their start and end apart: 34 -> 34, of which waited for: 17 -> 14; matrix products, arithmetic and copies ran while one was open for 29% -> 38% of each run, Pallas kernels for 0% -> 0%
where the time goes in v6:
time: 176 us; the launch traced here: 175 us
  local copies, waits for them, and re-layouts  52.8 us (30%)
  starting transfers between devices  43.6 us (25%)
  waiting for transfers between devices  28.1 us (16%)
  matrix products  24.8 us (14%)
  other arithmetic  23.7 us (13%)
    unnamed x68, local copies, waits for them, and re-layouts  17 us
    ppermute x14, starting transfers between devices, ring_reduce_scatter_sliced(): received = lax.ppermute(acc, axis, perm).astype(jnp.float32)  16.7 us
    ppermute x14, waiting for transfers between devices, ring_reduce_scatter_sliced(): received = lax.ppermute(acc, axis, perm).astype(jnp.float32)  11.1 us
    concatenate x9, local copies, waits for them, and re-layouts, body(): jnp.concatenate([block[:, :H * DK] for block in key_value_blocks], axis=0)  9.14 us
    dot_general x5, matrix products, body(): jnp.einsum('spc,spo->co', both_padded[:, offset:offset + positions], both...  8.68 us
    slice x7, local copies, waits for them, and re-layouts, body(): block[:, :H * DK]  8.36 us
    convert_element_type x6, other arithmetic, ring_reduce_scatter_sliced(): acc = acc.astype(wire_dtype)  8.19 us
    ppermute x2, starting transfers between devices, extended(): before = lax.ppermute(last, axis, up)  8.02 us
  transfers between devices with their start and end apart: 34, of which 14 were waited for; matrix products, arithmetic and copies ran while one was open for 38% of the time, Pallas kernels for 0%

profile of v6, /device:TPU:0, one launch (start us, length us, event | category | flops | bytes accessed | tf_op | source)
XLA Modules:
  0.0 174.5 jit_solution(14446290727739929150)
XLA Ops:
  3.7 3.1 %collective-permute-start = (bf16[128,1280]{0,1:T(8,128)(2,1)}, bf16[128,1280]{0,1:T(8,128)(2,1)}, u32[]{:S(2)}, u32[]{:S(2)}) collective-permute-start(bf16[128,1280]{0,1:T(8,128)(2,1)} %pad_maximum_fusion.8), channel_id=1, source_target_pairs={{0,4},{4,8},{8,12},{12,14},{14,10},{10,6},{6,2},{2,0},{1,5},{5,9},... | collective-permute-start | bytes 983048 | tf_op jit(solution)/shard_map/ppermute | solution.py:75
  10.0 4.6 %collective-permute-done = bf16[128,1280]{0,1:T(8,128)(2,1)} collective-permute-done((bf16[128,1280]{0,1:T(8,128)(2,1)}, bf16[128,1280]{0,1:T(8,128)(2,1)}, u32[]{:S(2)}, u32[]{:S(2)}) %collective-permute-start) | collective-permute-done | bytes 327712 | tf_op jit(solution)/shard_map/ppermute | solution.py:75
  14.7 1.8 %collective-permute-start.1 = (bf16[128,1280]{0,1:T(8,128)(2,1)}, bf16[128,1280]{0,1:T(8,128)(2,1)}, u32[]{:S(2)}, u32[]{:S(2)}) collective-permute-start(bf16[128,1280]{0,1:T(8,128)(2,1)} %collective-permute-done), channel_id=1, source_target_pairs={{0,4},{4,8},{8,12},{12,14},{14,10},{10,6},{6,2},{2,0},{1,5},{5,9},... | collective-permute-start | bytes 983048 | tf_op jit(solution)/shard_map/ppermute | solution.py:75
  16.8 2.2 %fusion.64 = f32[256,768]{1,0:T(8,128)} fusion(bf16[1,128,768]{2,1,0:T(8,128)(2,1)} %param.11, s32[256]{0:T(256)S(1)} %and_select_fusion), kind=kOutput, calls=%fused_computation.150 | convolution fusion | flops 50364416 | bytes 984064 | tf_op jit(solution)/shard_map/dot_general | solution.py:195
  34.8 1.6 constant_dynamic-update-slice_fusion.13
  36.4 1.6 slice.183
  38.0 1.7 copy.47
  39.7 1.6 slice.187
  41.2 1.7 copy.51
  43.8 1.6 slice.180
  45.5 1.6 constant_dynamic-update-slice_fusion.12
  47.8 1.6 slice.184
  49.4 1.7 copy.48
  51.0 1.6 constant_dynamic-update-slice_fusion.11
  52.6 1.6 constant_dynamic-update-slice_fusion.10
  54.2 1.6 constant_dynamic-update-slice_fusion.9
  55.8 1.6 constant_dynamic-update-slice_fusion.8
  57.4 1.8 %bitcast_reduce_fusion = (f32[4,128]{1,0:T(4,128)S(1)}, f32[4,1024,128]{2,1,0:T(8,128)S(1)}) fusion(bf16[1024,4,128]{2,0,1:T(8,128)(2,1)} %constant_dynamic-update-slice_fusion.8, bf16[128,4,128]{0,2,1:T(8,128)(2,1)S(1)} %bitcast.211), kind=kOutput, calls=%fused_computation.17 | convolution fusion | flops 135265792 | bytes 3278848 | tf_op jit(solution)/shard_map/ihd,jhd->hij/dot_general | solution.py:180
  64.3 2.4 %collective-permute-start.7 = (bf16[2,768]{1,0:T(2,128)(2,1)S(1)}, bf16[2,768]{1,0:T(2,128)(2,1)S(1)}, u32[]{:S(2)}, u32[]{:S(2)}) collective-permute-start(bf16[2,768]{1,0:T(2,128)(2,1)S(1)} %get-tuple-element.50), channel_id=1, source_target_pairs={{0,2},{2,4},{4,6},{6,8},{8,10},{10,12},{12,14},{1,3},{3,5},{5,7},{... | collective-permute-start | bytes 9224 | tf_op jit(solution)/shard_map/ppermute | solution.py:24
  68.8 4.4 %collective-permute-done.8 = bf16[2,768]{1,0:T(2,128)(2,1)S(1)} collective-permute-done((bf16[2,768]{1,0:T(2,128)(2,1)S(1)}, bf16[2,768]{1,0:T(2,128)(2,1)S(1)}, u32[]{:S(2)}, u32[]{:S(2)}) %collective-permute-start.8) | collective-permute-done | bytes 3104 | tf_op jit(solution)/shard_map/ppermute | solution.py:25
  73.3 2.0 %fusion.31 = (bf16[256,384]{1,0:T(8,128)(2,1)S(1)}, bf16[1,256,384]{2,1,0:T(8,128)(2,1)}) fusion(bf16[1,256,384]{2,1,0:T(8,128)(2,1)S(1)} %copy-done.24, bf16[256,3840]{1,0:T(8,128)(2,1)S(1)} %fusion.32, bf16[3840,384]{1,0:T(8,128)(2,1)S(1)} %copy-done), kind=kOutput, calls=%fused_computation.83 | convolution fusion | flops 756252672 | bytes 5505024 | tf_op jit(solution)/shard_map/dot_general | solution.py:206
  76.7 5.6 %collective-permute-start.10 = (bf16[2,384]{1,0:T(2,128)(2,1)S(1)}, bf16[2,384]{1,0:T(2,128)(2,1)S(1)}, u32[]{:S(2)}, u32[]{:S(2)}) collective-permute-start(bf16[2,384]{1,0:T(2,128)(2,1)S(1)} %get-tuple-element.51), channel_id=1, source_target_pairs={{0,2},{2,4},{4,6},{6,8},{8,10},{10,12},{12,14},{1,3},{3,5},{5,7},{... | collective-permute-start | bytes 4616 | tf_op jit(solution)/shard_map/ppermute | solution.py:24
  88.3 3.2 %multiply_convert_fusion.1 = bf16[4,128,1024]{1,2,0:T(8,128)(2,1)S(1)} fusion(f32[4,1024,128]{2,1,0:T(8,128)} %copy-done.2, bf16[128,4,192]{0,2,1:T(8,128)(2,1)S(1)} %bitcast.206, bf16[1024,4,192]{0,2,1:T(8,128)(2,1)} %copy-done.11, f32[4,128]{1,0:T(4,128)S(1)} %bitcast.231, f32[4,128]{1,0:T(4,128)S(1)} %log_add_fusion), kind=kOutput, calls=%fused_computation.22 | convolution fusion | flops 203948032 | bytes 4919296 | tf_op jit(solution)/shard_map/ihd,jhd->hij/dot_general | solution.py:292
  91.5 2.0 %fusion.8 = f32[3840,384]{1,0:T(8,128)S(1)} fusion(bf16[1,260,768]{2,1,0:T(8,128)(2,1)S(1)} %copy-done.19, bf16[1,260,768]{2,1,0:T(8,128)(2,1)} %bitcast.45, bf16[1,256,384]{2,1,0:T(8,128)(2,1)} %bitcast.47, bf16[1,256,384]{2,1,0:T(8,128)(2,1)S(1)} %bitcast.199), kind=kOutput, calls=%fused_computation.34 | convolution fusion | flops 302579712 | bytes 2371584 | tf_op jit(solution)/shard_map/spc,spo->co/dot_general | solution.py:222
  93.5 1.7 fusion.7
  95.2 1.7 fusion.6
  96.8 1.7 fusion.5
  98.5 1.7 fusion.4
  100.7 4.4 %collective-permute-start.20 = (bf16[240,192]{1,0:T(8,128)(2,1)S(1)}, bf16[240,192]{1,0:T(8,128)(2,1)S(1)}, u32[]{:S(2)}, u32[]{:S(2)}) collective-permute-start(bf16[240,192]{1,0:T(8,128)(2,1)S(1)} %get-tuple-element.37), channel_id=1, source_target_pairs={{0,4},{4,8},{8,12},{12,14},{14,10},{10,6},{6,2},{2,0},{1,5},{5,9},... | collective-permute-start | bytes 276488 | tf_op jit(solution)/shard_map/ppermute | solution.py:159
  105.1 1.8 %convolution_convert_fusion = bf16[4,192,1024]{2,1,0:T(8,128)(2,1)} fusion(bf16[128,4,192]{0,2,1:T(8,128)(2,1)S(1)} %bitcast.207, f32[4,1024,128]{2,1,0:T(8,128)S(1)} %copy-done.3, f32[4,128]{1,0:T(4,128)S(1)} %log_add_fusion), kind=kOutput, calls=%fused_computation.24 | convolution fusion | flops 203685888 | bytes 3868672 | tf_op jit(solution)/shard_map/hij,ihd->jhd/dot_general | solution.py:304
  107.5 2.4 %collective-permute-done.27 = bf16[240,192]{1,0:T(8,128)(2,1)S(1)} collective-permute-done((bf16[240,192]{1,0:T(8,128)(2,1)S(1)}, bf16[240,192]{1,0:T(8,128)(2,1)S(1)}, u32[]{:S(2)}, u32[]{:S(2)}) %collective-permute-start.27) | collective-permute-done | bytes 92192 | tf_op jit(solution)/shard_map/ppermute | solution.py:159
  110.1 1.6 collective-permute-start.21
  113.7 2.6 %copy.64 = bf16[1024,768]{1,0:T(8,128)(2,1)} copy(bf16[1024,768]{0,1:T(8,128)(2,1)} %bitcast.198) | data formatting | bytes 3145728 | tf_op jit(solution)/shard_map/reshape | solution.py:308
  116.3 2.3 %copy.61 = bf16[1024,4,128]{0,2,1:T(8,128)(2,1)} copy(bf16[1024,4,128]{2,0,1:T(8,128)(2,1)} %fusion.9) | data formatting | bytes 2097152 | tf_op jit(solution)/shard_map/mul | solution.py:301
  118.6 2.3 %copy.63 = bf16[1024,512]{1,0:T(8,128)(2,1)} copy(bf16[1024,512]{0,1:T(8,128)(2,1)} %bitcast.204) | data formatting | bytes 2097152 | tf_op jit(solution)/shard_map/reshape | solution.py:307
  120.9 1.8 %fusion.51 = (bf16[240,192]{1,0:T(8,128)(2,1)}, bf16[240,192]{1,0:T(8,128)(2,1)S(1)}) fusion(f32[8,2,240,384]{3,2,1,0:T(8,128)} %bitcast.192, s32[]{:T(128)S(6)} %select_n.514, s32[]{:T(128)S(6)} %select_n.498, bf16[240,192]{1,0:T(8,128)(2,1)S(1)} %collective-permute-done.21, s32[]{:T(128)S(6)} %select_n.578, bf16[240,192]{1,0:T(8,128)(2,1)S(1)} %collective-permute-done.28), kind=kLoop, calls=%fused_computation.126 | loop fusion | flops 276480 | bytes 737292 | tf_op jit(solution)/shard_map/convert_element_type | solution.py:162
  122.7 1.6 collective-permute-start.22
  124.7 1.9 %fusion.36 = (bf16[128,1280]{1,0:T(8,128)(2,1)}, bf16[128,1280]{1,0:T(8,128)(2,1)S(1)}) fusion(bf16[1024,768]{1,0:T(8,128)(2,1)} %copy.64, bf16[1024,512]{1,0:T(8,128)(2,1)} %copy.63), kind=kLoop, calls=%fused_computation.96 | loop fusion | flops 1310720 | bytes 3276800 | tf_op jit(solution)/shard_map/concatenate | solution.py:305
  126.7 2.0 %collective-permute-start.15 = (bf16[128,1280]{1,0:T(8,128)(2,1)S(1)}, bf16[128,1280]{1,0:T(8,128)(2,1)}, u32[]{:S(2)}, u32[]{:S(2)}) collective-permute-start(bf16[128,1280]{1,0:T(8,128)(2,1)S(1)} %get-tuple-element.44), channel_id=1, source_target_pairs={{0,4},{4,8},{8,12},{12,14},{14,10},{10,6},{6,2},{2,0},{1,5},{5,9},... | collective-permute-start | bytes 983048 | tf_op jit(solution)/shard_map/ppermute | solution.py:104
  128.8 1.7 %collective-permute-done.29 = bf16[240,192]{1,0:T(8,128)(2,1)} collective-permute-done((bf16[240,192]{1,0:T(8,128)(2,1)S(1)}, bf16[240,192]{1,0:T(8,128)(2,1)}, u32[]{:S(2)}, u32[]{:S(2)}) %collective-permute-start.29) | collective-permute-done | bytes 92192 | tf_op jit(solution)/shard_map/ppermute | solution.py:159
  130.6 1.9 %fusion.50 = (bf16[240,192]{1,0:T(8,128)(2,1)}, bf16[240,192]{1,0:T(8,128)(2,1)S(1)}) fusion(f32[8,2,240,384]{3,2,1,0:T(8,128)} %bitcast.193, s32[]{:T(128)S(6)} %select_n.522, s32[]{:T(128)S(6)} %select_n.498, bf16[240,192]{1,0:T(8,128)(2,1)S(1)} %collective-permute-done.22, s32[]{:T(128)S(6)} %select_n.586, bf16[240,192]{1,0:T(8,128)(2,1)} %collective-permute-done.29), kind=kLoop, calls=%fused_computation.124 | loop fusion | flops 276480 | bytes 737292 | tf_op jit(solution)/shard_map/convert_element_type | solution.py:162
  135.9 1.9 %add_convert_fusion.5 = bf16[128,1280]{1,0:T(8,128)(2,1)} fusion(bf16[128,1280]{1,0:T(8,128)(2,1)} %collective-permute-done.11, bf16[1024,768]{1,0:T(8,128)(2,1)} %copy.64, bf16[1024,512]{1,0:T(8,128)(2,1)} %copy.63), kind=kLoop, calls=%fused_computation.67 | loop fusion | flops 1146880 | bytes 3276800 | tf_op jit(solution)/shard_map/convert_element_type | solution.py:100
  141.6 2.0 %collective-permute-start.31 = (bf16[240,192]{1,0:T(8,128)(2,1)S(1)}, bf16[240,192]{1,0:T(8,128)(2,1)S(1)}, u32[]{:S(2)}, u32[]{:S(2)}) collective-permute-start(bf16[240,192]{1,0:T(8,128)(2,1)S(1)} %get-tuple-element.30), channel_id=1, source_target_pairs={{0,2},{4,0},{8,4},{12,8},{14,12},{10,14},{6,10},{2,6},{1,3},{5,1},... | collective-permute-start | bytes 276488 | tf_op jit(solution)/shard_map/ppermute | solution.py:159
  143.6 2.6 %collective-permute-done.12 = bf16[128,1280]{1,0:T(8,128)(2,1)} collective-permute-done((bf16[128,1280]{1,0:T(8,128)(2,1)}, bf16[128,1280]{1,0:T(8,128)(2,1)}, u32[]{:S(2)}, u32[]{:S(2)}) %collective-permute-start.12) | collective-permute-done | bytes 327712 | tf_op jit(solution)/shard_map/ppermute | solution.py:96
  146.3 2.3 %add_convert_fusion.4 = (bf16[128,1280]{1,0:T(8,128)(2,1)}, bf16[128,1280]{1,0:T(8,128)(2,1)}) fusion(bf16[128,1280]{1,0:T(8,128)(2,1)} %collective-permute-done.12, bf16[1024,768]{1,0:T(8,128)(2,1)} %copy.64, bf16[1024,512]{1,0:T(8,128)(2,1)} %copy.63, bf16[128,1280]{1,0:T(8,128)(2,1)} %collective-permute-done.15), kind=kLoop, calls=%fused_computation.66 | loop fusion | flops 2293760 | bytes 3932160 | tf_op jit(solution)/shard_map/convert_element_type | solution.py:100
  150.6 1.8 %fusion.48 = (bf16[240,192]{1,0:T(8,128)(2,1)}, bf16[240,192]{1,0:T(8,128)(2,1)}) fusion(f32[8,2,240,384]{3,2,1,0:T(8,128)} %bitcast.195, s32[]{:T(128)S(6)} %select_n.538, s32[]{:T(128)S(6)} %select_n.498, bf16[240,192]{1,0:T(8,128)(2,1)S(1)} %collective-permute-done.24, s32[]{:T(128)S(6)} %select_n.602, bf16[240,192]{1,0:T(8,128)(2,1)S(1)} %collective-permute-done.31), kind=kLoop, calls=%fused_computation.120 | loop fusion | flops 276480 | bytes 737292 | tf_op jit(solution)/shard_map/convert_element_type | solution.py:162
  155.7 4.4 %collective-permute-done.25 = bf16[240,192]{1,0:T(8,128)(2,1)S(1)} collective-permute-done((bf16[240,192]{1,0:T(8,128)(2,1)}, bf16[240,192]{1,0:T(8,128)(2,1)S(1)}, u32[]{:S(2)}, u32[]{:S(2)}) %collective-permute-start.25) | collective-permute-done | bytes 92192 | tf_op jit(solution)/shard_map/ppermute | solution.py:159
  169.4 2.6 %collective-permute-done.17 = bf16[128,1280]{1,0:T(8,128)(2,1)S(1)} collective-permute-done((bf16[128,1280]{1,0:T(8,128)(2,1)S(1)}, bf16[128,1280]{1,0:T(8,128)(2,1)S(1)}, u32[]{:S(2)}, u32[]{:S(2)}) %collective-permute-start.17) | collective-permute-done | bytes 327712 | tf_op jit(solution)/shard_map/ppermute | solution.py:104
  (172 shorter events, 66.5 us)
Async XLA Ops:
  0.6 72.7 %copy-start = (bf16[3840,384]{1,0:T(8,128)(2,1)S(1)}, bf16[3840,384]{1,0:T(8,128)(2,1)}, u32[]{:S(2)}) copy-start(bf16[3840,384]{1,0:T(8,128)(2,1)} %param.14) | copy-start | bytes 8847364
  3.7 11.0 %collective-permute-start = (bf16[128,1280]{0,1:T(8,128)(2,1)}, bf16[128,1280]{0,1:T(8,128)(2,1)}, u32[]{:S(2)}, u32[]{:S(2)}) collective-permute-start(bf16[128,1280]{0,1:T(8,128)(2,1)} %pad_maximum_fusion.8), channel_id=1, source_target_pairs={{0,4},{4,8},{8,12},{12,14},{14,10},{10,6},{6,2},{2,0},{1,5},{5,9},... | collective-permute-start | bytes 983048 | tf_op jit(solution)/shard_map/ppermute | solution.py:75
  6.7 9.8 %collective-permute-start.4 = (bf16[128,1280]{0,1:T(8,128)(2,1)}, bf16[128,1280]{0,1:T(8,128)(2,1)}, u32[]{:S(2)}, u32[]{:S(2)}) collective-permute-start(bf16[128,1280]{0,1:T(8,128)(2,1)} %pad_maximum_fusion.8), channel_id=1, source_target_pairs={{0,2},{4,0},{8,4},{12,8},{14,12},{10,14},{6,10},{2,6},{1,3},{5,1},... | collective-permute-start | bytes 983048 | tf_op jit(solution)/shard_map/ppermute | solution.py:79
  7.9 49.5 %copy-start.16 = (bf16[1,128,512]{1,2,0:T(8,128)(2,1)}, bf16[1,128,512]{1,2,0:T(8,128)(2,1)S(1)}, u32[]{:S(2)}) copy-start(bf16[1,128,512]{1,2,0:T(8,128)(2,1)S(1)} %copy.83) | copy-start | bytes 393220
  14.7 9.2 %collective-permute-start.1 = (bf16[128,1280]{0,1:T(8,128)(2,1)}, bf16[128,1280]{0,1:T(8,128)(2,1)}, u32[]{:S(2)}, u32[]{:S(2)}) collective-permute-start(bf16[128,1280]{0,1:T(8,128)(2,1)} %collective-permute-done), channel_id=1, source_target_pairs={{0,4},{4,8},{8,12},{12,14},{14,10},{10,6},{6,2},{2,0},{1,5},{5,9},... | collective-permute-start | bytes 983048 | tf_op jit(solution)/shard_map/ppermute | solution.py:75
  16.5 45.2 %copy-start.21 = (s32[256]{0:T(256)}, s32[256]{0:T(256)S(1)}, u32[]{:S(2)}) copy-start(s32[256]{0:T(256)S(1)} %and_select_fusion) | copy-start | bytes 3076
  16.5 9.6 %collective-permute-start.5 = (bf16[128,1280]{0,1:T(8,128)(2,1)}, bf16[128,1280]{0,1:T(8,128)(2,1)}, u32[]{:S(2)}, u32[]{:S(2)}) collective-permute-start(bf16[128,1280]{0,1:T(8,128)(2,1)} %collective-permute-done.4), channel_id=1, source_target_pairs={{0,2},{4,0},{8,4},{12,8},{14,12},{10,14},{6,10},{2,6},{1,3},{5,1},... | collective-permute-start | bytes 983048 | tf_op jit(solution)/shard_map/ppermute | solution.py:79
  23.9 9.4 %collective-permute-start.2 = (bf16[128,1280]{0,1:T(8,128)(2,1)}, bf16[128,1280]{0,1:T(8,128)(2,1)}, u32[]{:S(2)}, u32[]{:S(2)}) collective-permute-start(bf16[128,1280]{0,1:T(8,128)(2,1)} %collective-permute-done.1), channel_id=1, source_target_pairs={{0,4},{4,8},{8,12},{12,14},{14,10},{10,6},{6,2},{2,0},{1,5},{5,9},... | collective-permute-start | bytes 983048 | tf_op jit(solution)/shard_map/ppermute | solution.py:75
  26.1 13.5 %collective-permute-start.6 = (bf16[128,1280]{0,1:T(8,128)(2,1)}, bf16[128,1280]{0,1:T(8,128)(2,1)}, u32[]{:S(2)}, u32[]{:S(2)}) collective-permute-start(bf16[128,1280]{0,1:T(8,128)(2,1)} %collective-permute-done.5), channel_id=1, source_target_pairs={{0,2},{4,0},{8,4},{12,8},{14,12},{10,14},{6,10},{2,6},{1,3},{5,1},... | collective-permute-start | bytes 983048 | tf_op jit(solution)/shard_map/ppermute | solution.py:79
  33.3 14.5 %collective-permute-start.3 = (bf16[128,1280]{0,1:T(8,128)(2,1)}, bf16[128,1280]{0,1:T(8,128)(2,1)}, u32[]{:S(2)}, u32[]{:S(2)}) collective-permute-start(bf16[128,1280]{0,1:T(8,128)(2,1)} %collective-permute-done.2), channel_id=1, source_target_pairs={{0,4},{4,8},{8,12},{12,14},{14,10},{10,6},{6,2},{2,0},{1,5},{5,9},... | collective-permute-start | bytes 983048 | tf_op jit(solution)/shard_map/ppermute | solution.py:75
  57.4 3.3 %copy-start.10 = (bf16[1024,4,192]{0,2,1:T(8,128)(2,1)S(1)}, bf16[1024,4,192]{0,2,1:T(8,128)(2,1)}, u32[]{:S(2)}) copy-start(bf16[1024,4,192]{0,2,1:T(8,128)(2,1)} %constant_dynamic-update-slice_fusion.4) | copy-start | bytes 4718596
  64.3 4.1 %collective-permute-start.7 = (bf16[2,768]{1,0:T(2,128)(2,1)S(1)}, bf16[2,768]{1,0:T(2,128)(2,1)S(1)}, u32[]{:S(2)}, u32[]{:S(2)}) collective-permute-start(bf16[2,768]{1,0:T(2,128)(2,1)S(1)} %get-tuple-element.50), channel_id=1, source_target_pairs={{0,2},{2,4},{4,6},{6,8},{8,10},{10,12},{12,14},{1,3},{3,5},{5,7},{... | collective-permute-start | bytes 9224 | tf_op jit(solution)/shard_map/ppermute | solution.py:24
  66.9 6.4 %copy-start.24 = (bf16[1,256,384]{2,1,0:T(8,128)(2,1)S(1)}, bf16[1,256,384]{2,1,0:T(8,128)(2,1)}, u32[]{:S(2)}) copy-start(bf16[1,256,384]{2,1,0:T(8,128)(2,1)} %param.15) | copy-start | bytes 589828
  67.0 6.2 %collective-permute-start.8 = (bf16[2,768]{1,0:T(2,128)(2,1)S(1)}, bf16[2,768]{1,0:T(2,128)(2,1)S(1)}, u32[]{:S(2)}, u32[]{:S(2)}) collective-permute-start(bf16[2,768]{1,0:T(2,128)(2,1)S(1)} %get-tuple-element.49), channel_id=1, source_target_pairs={{2,0},{4,2},{6,4},{8,6},{10,8},{12,10},{14,12},{3,1},{5,3},{7,5},{... | collective-permute-start | bytes 9224 | tf_op jit(solution)/shard_map/ppermute | solution.py:25
  75.4 16.1 %collective-permute-start.19 = (bf16[256,384]{1,0:T(8,128)(2,1)S(1)}, bf16[256,384]{1,0:T(8,128)(2,1)}, u32[]{:S(2)}, u32[]{:S(2)}) collective-permute-start(bf16[256,384]{1,0:T(8,128)(2,1)S(1)} %get-tuple-element.47), channel_id=1, source_target_pairs={{0,1},{1,0},{2,3},{3,2},{4,5},{5,4},{6,7},{7,6},{8,9},{9,8},{10,11... | collective-permute-start | bytes 589832 | tf_op jit(solution)/shard_map/ppermute | solution.py:218
  75.4 8.2 %collective-permute-start.9 = (bf16[2,384]{1,0:T(2,128)(2,1)S(1)}, bf16[2,384]{1,0:T(2,128)(2,1)S(1)}, u32[]{:S(2)}, u32[]{:S(2)}) collective-permute-start(bf16[2,384]{1,0:T(2,128)(2,1)S(1)} %get-tuple-element.52), channel_id=1, source_target_pairs={{2,0},{4,2},{6,4},{8,6},{10,8},{12,10},{14,12},{3,1},{5,3},{7,5},{... | collective-permute-start | bytes 4616 | tf_op jit(solution)/shard_map/ppermute | solution.py:25
  76.7 7.0 %collective-permute-start.10 = (bf16[2,384]{1,0:T(2,128)(2,1)S(1)}, bf16[2,384]{1,0:T(2,128)(2,1)S(1)}, u32[]{:S(2)}, u32[]{:S(2)}) collective-permute-start(bf16[2,384]{1,0:T(2,128)(2,1)S(1)} %get-tuple-element.51), channel_id=1, source_target_pairs={{0,2},{2,4},{4,6},{6,8},{8,10},{10,12},{12,14},{1,3},{3,5},{5,7},{... | collective-permute-start | bytes 4616 | tf_op jit(solution)/shard_map/ppermute | solution.py:24
  83.3 8.1 %collective-permute-start.18 = (bf16[260,768]{1,0:T(8,128)(2,1)}, bf16[260,768]{1,0:T(8,128)(2,1)}, u32[]{:S(2)}, u32[]{:S(2)}) collective-permute-start(bf16[260,768]{1,0:T(8,128)(2,1)} %get-tuple-element.45), channel_id=1, source_target_pairs={{0,1},{1,0},{2,3},{3,2},{4,5},{5,4},{6,7},{7,6},{8,9},{9,8},{10,11... | collective-permute-start | bytes 1198088 | tf_op jit(solution)/shard_map/ppermute | solution.py:217
  85.0 3.2 %copy-start.15 = (bf16[4,192,128]{2,1,0:T(8,128)(2,1)S(1)}, bf16[4,192,128]{2,1,0:T(8,128)(2,1)}, u32[]{:S(2)}) copy-start(bf16[4,192,128]{2,1,0:T(8,128)(2,1)} %copy-done.14) | copy-start | bytes 589828
  91.4 20.8 %copy-start.8 = (bf16[4,128,1024]{1,2,0:T(8,128)(2,1)}, bf16[4,128,1024]{1,2,0:T(8,128)(2,1)S(1)}, u32[]{:S(2)}) copy-start(bf16[4,128,1024]{1,2,0:T(8,128)(2,1)S(1)} %multiply_convert_fusion.1) | copy-start | bytes 3145732
  100.2 4.9 %copy-start.3 = (f32[4,1024,128]{2,1,0:T(8,128)S(1)}, f32[4,1024,128]{2,1,0:T(8,128)}, u32[]{:S(2)}) copy-start(f32[4,1024,128]{2,1,0:T(8,128)} %copy-done.2) | copy-start | bytes 6291460
  100.6 9.4 %copy-start.7 = (f32[3840,384]{1,0:T(8,128)}, f32[3840,384]{1,0:T(8,128)S(1)}, u32[]{:S(2)}) copy-start(f32[3840,384]{1,0:T(8,128)S(1)} %broadcast_multiply_fusion) | copy-start | bytes 17694724
  100.7 6.8 %collective-permute-start.20 = (bf16[240,192]{1,0:T(8,128)(2,1)S(1)}, bf16[240,192]{1,0:T(8,128)(2,1)S(1)}, u32[]{:S(2)}, u32[]{:S(2)}) collective-permute-start(bf16[240,192]{1,0:T(8,128)(2,1)S(1)} %get-tuple-element.37), channel_id=1, source_target_pairs={{0,4},{4,8},{8,12},{12,14},{14,10},{10,6},{6,2},{2,0},{1,5},{5,9},... | collective-permute-start | bytes 276488 | tf_op jit(solution)/shard_map/ppermute | solution.py:159
  105.1 7.1 %copy-start.17 = (bf16[1,128,512]{1,2,0:T(8,128)(2,1)S(1)}, bf16[1,128,512]{1,2,0:T(8,128)(2,1)}, u32[]{:S(2)}) copy-start(bf16[1,128,512]{1,2,0:T(8,128)(2,1)} %copy-done.16) | copy-start | bytes 393220
  105.1 4.9 %collective-permute-start.27 = (bf16[240,192]{1,0:T(8,128)(2,1)S(1)}, bf16[240,192]{1,0:T(8,128)(2,1)S(1)}, u32[]{:S(2)}, u32[]{:S(2)}) collective-permute-start(bf16[240,192]{1,0:T(8,128)(2,1)S(1)} %get-tuple-element.38), channel_id=1, source_target_pairs={{0,2},{4,0},{8,4},{12,8},{14,12},{10,14},{6,10},{2,6},{1,3},{5,1},... | collective-permute-start | bytes 276488 | tf_op jit(solution)/shard_map/ppermute | solution.py:159
  110.1 10.8 %collective-permute-start.21 = (bf16[240,192]{1,0:T(8,128)(2,1)S(1)}, bf16[240,192]{1,0:T(8,128)(2,1)S(1)}, u32[]{:S(2)}, u32[]{:S(2)}) collective-permute-start(bf16[240,192]{1,0:T(8,128)(2,1)S(1)} %get-tuple-element.35), channel_id=1, source_target_pairs={{0,4},{4,8},{8,12},{12,14},{14,10},{10,6},{6,2},{2,0},{1,5},{5,9},... | collective-permute-start | bytes 276488 | tf_op jit(solution)/shard_map/ppermute | solution.py:159
  111.8 9.1 %collective-permute-start.28 = (bf16[240,192]{1,0:T(8,128)(2,1)S(1)}, bf16[240,192]{1,0:T(8,128)(2,1)S(1)}, u32[]{:S(2)}, u32[]{:S(2)}) collective-permute-start(bf16[240,192]{1,0:T(8,128)(2,1)S(1)} %get-tuple-element.36), channel_id=1, source_target_pairs={{0,2},{4,0},{8,4},{12,8},{14,12},{10,14},{6,10},{2,6},{1,3},{5,1},... | collective-permute-start | bytes 276488 | tf_op jit(solution)/shard_map/ppermute | solution.py:159
  122.7 6.1 %collective-permute-start.22 = (bf16[240,192]{1,0:T(8,128)(2,1)}, bf16[240,192]{1,0:T(8,128)(2,1)S(1)}, u32[]{:S(2)}, u32[]{:S(2)}) collective-permute-start(bf16[240,192]{1,0:T(8,128)(2,1)} %get-tuple-element.33), channel_id=1, source_target_pairs={{0,4},{4,8},{8,12},{12,14},{14,10},{10,6},{6,2},{2,0},{1,5},{5,9},... | collective-permute-start | bytes 276488 | tf_op jit(solution)/shard_map/ppermute | solution.py:159
  124.3 6.3 %collective-permute-start.29 = (bf16[240,192]{1,0:T(8,128)(2,1)S(1)}, bf16[240,192]{1,0:T(8,128)(2,1)}, u32[]{:S(2)}, u32[]{:S(2)}) collective-permute-start(bf16[240,192]{1,0:T(8,128)(2,1)S(1)} %get-tuple-element.34), channel_id=1, source_target_pairs={{0,2},{4,0},{8,4},{12,8},{14,12},{10,14},{6,10},{2,6},{1,3},{5,1},... | collective-permute-start | bytes 276488 | tf_op jit(solution)/shard_map/ppermute | solution.py:159
  126.7 9.2 %collective-permute-start.11 = (bf16[128,1280]{1,0:T(8,128)(2,1)}, bf16[128,1280]{1,0:T(8,128)(2,1)}, u32[]{:S(2)}, u32[]{:S(2)}) collective-permute-start(bf16[128,1280]{1,0:T(8,128)(2,1)} %get-tuple-element.43), channel_id=1, source_target_pairs={{0,2},{4,0},{8,4},{12,8},{14,12},{10,14},{6,10},{2,6},{1,3},{5,1},... | collective-permute-start | bytes 983048 | tf_op jit(solution)/shard_map/ppermute | solution.py:96
  126.7 17.0 %collective-permute-start.15 = (bf16[128,1280]{1,0:T(8,128)(2,1)S(1)}, bf16[128,1280]{1,0:T(8,128)(2,1)}, u32[]{:S(2)}, u32[]{:S(2)}) collective-permute-start(bf16[128,1280]{1,0:T(8,128)(2,1)S(1)} %get-tuple-element.44), channel_id=1, source_target_pairs={{0,4},{4,8},{8,12},{12,14},{14,10},{10,6},{6,2},{2,0},{1,5},{5,9},... | collective-permute-start | bytes 983048 | tf_op jit(solution)/shard_map/ppermute | solution.py:104
  132.4 6.5 %collective-permute-start.23 = (bf16[240,192]{1,0:T(8,128)(2,1)}, bf16[240,192]{1,0:T(8,128)(2,1)S(1)}, u32[]{:S(2)}, u32[]{:S(2)}) collective-permute-start(bf16[240,192]{1,0:T(8,128)(2,1)} %get-tuple-element.31), channel_id=1, source_target_pairs={{0,4},{4,8},{8,12},{12,14},{14,10},{10,6},{6,2},{2,0},{1,5},{5,9},... | collective-permute-start | bytes 276488 | tf_op jit(solution)/shard_map/ppermute | solution.py:159
  134.0 6.3 %collective-permute-start.30 = (bf16[240,192]{1,0:T(8,128)(2,1)S(1)}, bf16[240,192]{1,0:T(8,128)(2,1)}, u32[]{:S(2)}, u32[]{:S(2)}) collective-permute-start(bf16[240,192]{1,0:T(8,128)(2,1)S(1)} %get-tuple-element.32), channel_id=1, source_target_pairs={{0,2},{4,0},{8,4},{12,8},{14,12},{10,14},{6,10},{2,6},{1,3},{5,1},... | collective-permute-start | bytes 276488 | tf_op jit(solution)/shard_map/ppermute | solution.py:159
  137.8 8.5 %collective-permute-start.12 = (bf16[128,1280]{1,0:T(8,128)(2,1)}, bf16[128,1280]{1,0:T(8,128)(2,1)}, u32[]{:S(2)}, u32[]{:S(2)}) collective-permute-start(bf16[128,1280]{1,0:T(8,128)(2,1)} %add_convert_fusion.5), channel_id=1, source_target_pairs={{0,2},{4,0},{8,4},{12,8},{14,12},{10,14},{6,10},{2,6},{1,3},{5,1},... | collective-permute-start | bytes 983048 | tf_op jit(solution)/shard_map/ppermute | solution.py:96
  141.6 9.0 %collective-permute-start.24 = (bf16[240,192]{1,0:T(8,128)(2,1)S(1)}, bf16[240,192]{1,0:T(8,128)(2,1)S(1)}, u32[]{:S(2)}, u32[]{:S(2)}) collective-permute-start(bf16[240,192]{1,0:T(8,128)(2,1)S(1)} %get-tuple-element.29), channel_id=1, source_target_pairs={{0,4},{4,8},{8,12},{12,14},{14,10},{10,6},{6,2},{2,0},{1,5},{5,9},... | collective-permute-start | bytes 276488 | tf_op jit(solution)/shard_map/ppermute | solution.py:159
  141.6 12.9 %copy-start.9 = (bf16[4,128,1024]{1,2,0:T(8,128)(2,1)S(1)}, bf16[4,128,1024]{1,2,0:T(8,128)(2,1)}, u32[]{:S(2)}) copy-start(bf16[4,128,1024]{1,2,0:T(8,128)(2,1)} %copy-done.8) | copy-start | bytes 3145732
  141.6 12.8 %copy-start.12 = (bf16[1024,4,128]{2,0,1:T(8,128)(2,1)S(1)}, bf16[1024,4,128]{2,0,1:T(8,128)(2,1)}, u32[]{:S(2)}) copy-start(bf16[1024,4,128]{2,0,1:T(8,128)(2,1)} %constant_dynamic-update-slice_fusion.8) | copy-start | bytes 3145732
  141.6 9.0 %collective-permute-start.31 = (bf16[240,192]{1,0:T(8,128)(2,1)S(1)}, bf16[240,192]{1,0:T(8,128)(2,1)S(1)}, u32[]{:S(2)}, u32[]{:S(2)}) collective-permute-start(bf16[240,192]{1,0:T(8,128)(2,1)S(1)} %get-tuple-element.30), channel_id=1, source_target_pairs={{0,2},{4,0},{8,4},{12,8},{14,12},{10,14},{6,10},{2,6},{1,3},{5,1},... | collective-permute-start | bytes 276488 | tf_op jit(solution)/shard_map/ppermute | solution.py:159
  148.6 14.9 %collective-permute-start.13 = (bf16[128,1280]{1,0:T(8,128)(2,1)}, bf16[128,1280]{1,0:T(8,128)(2,1)S(1)}, u32[]{:S(2)}, u32[]{:S(2)}) collective-permute-start(bf16[128,1280]{1,0:T(8,128)(2,1)} %get-tuple-element.41), channel_id=1, source_target_pairs={{0,2},{4,0},{8,4},{12,8},{14,12},{10,14},{6,10},{2,6},{1,3},{5,1},... | collective-permute-start | bytes 983048 | tf_op jit(solution)/shard_map/ppermute | solution.py:96
  150.1 13.4 %collective-permute-start.16 = (bf16[128,1280]{1,0:T(8,128)(2,1)}, bf16[128,1280]{1,0:T(8,128)(2,1)}, u32[]{:S(2)}, u32[]{:S(2)}) collective-permute-start(bf16[128,1280]{1,0:T(8,128)(2,1)} %get-tuple-element.42), channel_id=1, source_target_pairs={{0,4},{4,8},{8,12},{12,14},{14,10},{10,6},{6,2},{2,0},{1,5},{5,9},... | collective-permute-start | bytes 983048 | tf_op jit(solution)/shard_map/ppermute | solution.py:104
  152.4 7.7 %collective-permute-start.25 = (bf16[240,192]{1,0:T(8,128)(2,1)}, bf16[240,192]{1,0:T(8,128)(2,1)S(1)}, u32[]{:S(2)}, u32[]{:S(2)}) collective-permute-start(bf16[240,192]{1,0:T(8,128)(2,1)} %get-tuple-element.27), channel_id=1, source_target_pairs={{0,4},{4,8},{8,12},{12,14},{14,10},{10,6},{6,2},{2,0},{1,5},{5,9},... | collective-permute-start | bytes 276488 | tf_op jit(solution)/shard_map/ppermute | solution.py:159
  153.6 6.5 %collective-permute-start.32 = (bf16[240,192]{1,0:T(8,128)(2,1)}, bf16[240,192]{1,0:T(8,128)(2,1)}, u32[]{:S(2)}, u32[]{:S(2)}) collective-permute-start(bf16[240,192]{1,0:T(8,128)(2,1)} %get-tuple-element.28), channel_id=1, source_target_pairs={{0,2},{4,0},{8,4},{12,8},{14,12},{10,14},{6,10},{2,6},{1,3},{5,1},... | collective-permute-start | bytes 276488 | tf_op jit(solution)/shard_map/ppermute | solution.py:159
  161.4 5.6 %collective-permute-start.26 = (bf16[240,192]{1,0:T(8,128)(2,1)S(1)}, bf16[240,192]{1,0:T(8,128)(2,1)S(1)}, u32[]{:S(2)}, u32[]{:S(2)}) collective-permute-start(bf16[240,192]{1,0:T(8,128)(2,1)S(1)} %get-tuple-element.25), channel_id=1, source_target_pairs={{0,4},{4,8},{8,12},{12,14},{14,10},{10,6},{6,2},{2,0},{1,5},{5,9},... | collective-permute-start | bytes 276488 | tf_op jit(solution)/shard_map/ppermute | solution.py:159
  162.5 10.6 %copy-start.1 = (bf16[1024,768]{1,0:T(8,128)(2,1)S(1)}, bf16[1024,768]{1,0:T(8,128)(2,1)}, u32[]{:S(2)}) copy-start(bf16[1024,768]{1,0:T(8,128)(2,1)} %copy.64) | copy-start | bytes 4718596
  162.5 10.6 %copy-start.4 = (bf16[1024,512]{1,0:T(8,128)(2,1)S(1)}, bf16[1024,512]{1,0:T(8,128)(2,1)}, u32[]{:S(2)}) copy-start(bf16[1024,512]{1,0:T(8,128)(2,1)} %copy.63) | copy-start | bytes 3145732
  162.5 4.9 %collective-permute-start.33 = (bf16[240,192]{1,0:T(8,128)(2,1)S(1)}, bf16[240,192]{1,0:T(8,128)(2,1)S(1)}, u32[]{:S(2)}, u32[]{:S(2)}) collective-permute-start(bf16[240,192]{1,0:T(8,128)(2,1)S(1)} %get-tuple-element.26), channel_id=1, source_target_pairs={{0,2},{4,0},{8,4},{12,8},{14,12},{10,14},{6,10},{2,6},{1,3},{5,1},... | collective-permute-start | bytes 276488 | tf_op jit(solution)/shard_map/ppermute | solution.py:159
  164.9 7.1 %collective-permute-start.17 = (bf16[128,1280]{1,0:T(8,128)(2,1)S(1)}, bf16[128,1280]{1,0:T(8,128)(2,1)S(1)}, u32[]{:S(2)}, u32[]{:S(2)}) collective-permute-start(bf16[128,1280]{1,0:T(8,128)(2,1)S(1)} %get-tuple-element.40), channel_id=1, source_target_pairs={{0,4},{4,8},{8,12},{12,14},{14,10},{10,6},{6,2},{2,0},{1,5},{5,9},... | collective-permute-start | bytes 983048 | tf_op jit(solution)/shard_map/ppermute | solution.py:104
  166.0 7.1 %collective-permute-start.14 = (bf16[128,1280]{1,0:T(8,128)(2,1)S(1)}, bf16[128,1280]{1,0:T(8,128)(2,1)S(1)}, u32[]{:S(2)}, u32[]{:S(2)}) collective-permute-start(bf16[128,1280]{1,0:T(8,128)(2,1)S(1)} %get-tuple-element.39), channel_id=1, source_target_pairs={{0,2},{4,0},{8,4},{12,8},{14,12},{10,14},{6,10},{2,6},{1,3},{5,1},... | collective-permute-start | bytes 983048 | tf_op jit(solution)/shard_map/ppermute | solution.py:96
  (11 other events, 20.3 us)

commit v7 on v6

--- a/solution.py
+++ b/solution.py
@@ -170,12 +170,9 @@
     half_kernel = KW // 2
     query_heads = queries[0].reshape(local_tokens, H, DK)
     key_value_blocks = ring_gather(jnp.concatenate([key_rows[0], value_rows[0]], axis=1), ring)
-    all_keys = jnp.concatenate([block[:, : H * DK] for block in key_value_blocks], axis=0).reshape(
-        -1, H, DK
-    )
-    all_values = jnp.concatenate(
-        [block[:, H * DK :] for block in key_value_blocks], axis=0
-    ).reshape(-1, H, DV)
+    gathered = jnp.concatenate(key_value_blocks, axis=0)
+    all_keys = gathered[:, : H * DK].reshape(-1, H, DK)
+    all_values = gathered[:, H * DK :].reshape(-1, H, DV)
     scores = (
         jnp.einsum("ihd,jhd->hij", query_heads, all_keys, preferred_element_type=jnp.float32)
         * score_scale

time: 176 us -> 163 us (0.926)
  local copies, waits for them, and re-layouts: 52.8 us -> 26.7 us
  waiting for transfers between devices: 28.1 us -> 43.1 us
    ppermute x4, waiting for transfers between devices: 4.97 us -> 18.9 us  [ring_gather(): current = lax.ppermute(current, 'seq', forward)]
    slice x14 -> x2, local copies, waits for them, and re-layouts: 15.8 us -> 3.39 us  [the longest x1 1.86 us: body(): all_keys = gathered[:, :H * DK].reshape(-1, H, DK)]
    concatenate x10 -> x1, local copies, waits for them, and re-layouts: 9.2 us -> 0.82 us  [body(): gathered = jnp.concatenate(key_value_blocks, axis=0)]
    unnamed x68 -> x64, local copies, waits for them, and re-layouts: 17 us -> 12.7 us
  transfers between devices with their start and end apart: 34 -> 34, of which waited for: 14 -> 18; matrix products, arithmetic and copies ran while one was open for 38% -> 29% of each run, Pallas kernels for 0% -> 0%
where the time goes in v7:
time: 163 us; the launch traced here: 162 us
  starting transfers between devices  43.8 us (27%)
  waiting for transfers between devices  43.1 us (26%)
  local copies, waits for them, and re-layouts  26.7 us (16%)
  matrix products  23.5 us (14%)
  other arithmetic  23.2 us (14%)
    ppermute x4, waiting for transfers between devices, ring_gather(): current = lax.ppermute(current, 'seq', forward)  18.9 us
    ppermute x14, starting transfers between devices, ring_reduce_scatter_sliced(): received = lax.ppermute(acc, axis, perm).astype(jnp.float32)  16.7 us
    unnamed x64, local copies, waits for them, and re-layouts  12.7 us
    ppermute x14, waiting for transfers between devices, ring_reduce_scatter_sliced(): received = lax.ppermute(acc, axis, perm).astype(jnp.float32)  11.1 us
    dot_general x5, matrix products, body(): jnp.einsum('spc,spo->co', both_padded[:, offset:offset + positions], both...  8.68 us
    convert_element_type x6, other arithmetic, ring_reduce_scatter_sliced(): acc = acc.astype(wire_dtype)  8.19 us
    ppermute x2, starting transfers between devices, extended(): before = lax.ppermute(last, axis, up)  8.04 us
    ppermute x4, starting transfers between devices, ring_gather(): current = lax.ppermute(current, 'seq', forward)  7.61 us
  transfers between devices with their start and end apart: 34, of which 18 were waited for; matrix products, arithmetic and copies ran while one was open for 29% of the time, Pallas kernels for 0%

profile of v7, /device:TPU:0, one launch (start us, length us, event | category | flops | bytes accessed | tf_op | source)
XLA Modules:
  0.0 161.6 jit_solution(5290792209238499654)
XLA Ops:
  3.9 3.1 %collective-permute-start = (bf16[128,1280]{0,1:T(8,128)(2,1)}, bf16[128,1280]{0,1:T(8,128)(2,1)S(1)}, u32[]{:S(2)}, u32[]{:S(2)}) collective-permute-start(bf16[128,1280]{0,1:T(8,128)(2,1)} %get-tuple-element.51), channel_id=1, source_target_pairs={{0,4},{4,8},{8,12},{12,14},{14,10},{10,6},{6,2},{2,0},{1,5},{5,9},... | collective-permute-start | bytes 983048 | tf_op jit(solution)/shard_map/ppermute | solution.py:75
  6.9 7.9 %collective-permute-done = bf16[128,1280]{0,1:T(8,128)(2,1)S(1)} collective-permute-done((bf16[128,1280]{0,1:T(8,128)(2,1)}, bf16[128,1280]{0,1:T(8,128)(2,1)S(1)}, u32[]{:S(2)}, u32[]{:S(2)}) %collective-permute-start) | collective-permute-done | bytes 327712 | tf_op jit(solution)/shard_map/ppermute | solution.py:75
  15.5 1.8 %collective-permute-start.1 = (bf16[128,1280]{0,1:T(8,128)(2,1)S(1)}, bf16[128,1280]{0,1:T(8,128)(2,1)}, u32[]{:S(2)}, u32[]{:S(2)}) collective-permute-start(bf16[128,1280]{0,1:T(8,128)(2,1)S(1)} %collective-permute-done), channel_id=1, source_target_pairs={{0,4},{4,8},{8,12},{12,14},{14,10},{10,6},{6,2},{2,0},{1,5},{5,9},... | collective-permute-start | bytes 983048 | tf_op jit(solution)/shard_map/ppermute | solution.py:75
  17.5 6.9 %collective-permute-done.1 = bf16[128,1280]{0,1:T(8,128)(2,1)} collective-permute-done((bf16[128,1280]{0,1:T(8,128)(2,1)S(1)}, bf16[128,1280]{0,1:T(8,128)(2,1)}, u32[]{:S(2)}, u32[]{:S(2)}) %collective-permute-start.1) | collective-permute-done | bytes 327712 | tf_op jit(solution)/shard_map/ppermute | solution.py:75
  24.5 1.5 collective-permute-start.2
  26.0 2.1 %fusion.64 = f32[256,768]{1,0:T(8,128)} fusion(bf16[1,128,768]{2,1,0:T(8,128)(2,1)} %param.11, s32[256]{0:T(256)S(1)} %and_select_fusion), kind=kOutput, calls=%fused_computation.150 | convolution fusion | flops 50364416 | bytes 984064 | tf_op jit(solution)/shard_map/dot_general | solution.py:192
  28.9 1.7 %constant_dynamic-update-slice_fusion.6 = bf16[1024,1280]{0,1:T(8,128)(2,1)} fusion(bf16[1024,1280]{0,1:T(8,128)(2,1)} %get-tuple-element.52, bf16[128,1280]{0,1:T(8,128)(2,1)} %copy-done.20), kind=kLoop, calls=%fused_computation.165 | loop fusion | bytes 655360
  30.6 2.2 %collective-permute-done.2 = bf16[128,1280]{0,1:T(8,128)(2,1)} collective-permute-done((bf16[128,1280]{0,1:T(8,128)(2,1)}, bf16[128,1280]{0,1:T(8,128)(2,1)}, u32[]{:S(2)}, u32[]{:S(2)}) %collective-permute-start.2) | collective-permute-done | bytes 327712 | tf_op jit(solution)/shard_map/ppermute | solution.py:75
  34.1 1.8 %constant_dynamic-update-slice_fusion.5 = bf16[1024,1280]{0,1:T(8,128)(2,1)} fusion(bf16[1024,1280]{0,1:T(8,128)(2,1)} %constant_dynamic-update-slice_fusion.6, bf16[128,1280]{0,1:T(8,128)(2,1)} %collective-permute-done.1), kind=kLoop, calls=%fused_computation.164 | loop fusion | bytes 655360
  36.6 1.7 %constant_dynamic-update-slice_fusion.4 = bf16[1024,1280]{0,1:T(8,128)(2,1)} fusion(bf16[1024,1280]{0,1:T(8,128)(2,1)} %constant_dynamic-update-slice_fusion.5, bf16[128,1280]{0,1:T(8,128)(2,1)} %collective-permute-done.2), kind=kLoop, calls=%fused_computation.163 | loop fusion | bytes 655360
  38.4 1.8 %collective-permute-done.3 = bf16[128,1280]{0,1:T(8,128)(2,1)S(1)} collective-permute-done((bf16[128,1280]{0,1:T(8,128)(2,1)}, bf16[128,1280]{0,1:T(8,128)(2,1)S(1)}, u32[]{:S(2)}, u32[]{:S(2)}) %collective-permute-start.3) | collective-permute-done | bytes 327712 | tf_op jit(solution)/shard_map/ppermute | solution.py:75
  44.0 1.5 slice.126
  45.5 1.9 %slice.127 = bf16[1024,512]{0,1:T(8,128)(2,1)S(1)} slice(bf16[1024,1280]{0,1:T(8,128)(2,1)} %constant_dynamic-update-slice_fusion), slice={[0:1024], [0:512]} | slice | bytes 2097152 | tf_op jit(solution)/shard_map/slice | solution.py:174
  51.5 2.4 %collective-permute-start.7 = (bf16[2,768]{1,0:T(2,128)(2,1)S(1)}, bf16[2,768]{1,0:T(2,128)(2,1)S(1)}, u32[]{:S(2)}, u32[]{:S(2)}) collective-permute-start(bf16[2,768]{1,0:T(2,128)(2,1)S(1)} %get-tuple-element.50), channel_id=1, source_target_pairs={{0,2},{2,4},{4,6},{6,8},{8,10},{10,12},{12,14},{1,3},{3,5},{5,7},{... | collective-permute-start | bytes 9224 | tf_op jit(solution)/shard_map/ppermute | solution.py:24
  54.1 1.4 collective-permute-start.8
  55.9 4.4 %collective-permute-done.8 = bf16[2,768]{1,0:T(2,128)(2,1)S(1)} collective-permute-done((bf16[2,768]{1,0:T(2,128)(2,1)S(1)}, bf16[2,768]{1,0:T(2,128)(2,1)S(1)}, u32[]{:S(2)}, u32[]{:S(2)}) %collective-permute-start.8) | collective-permute-done | bytes 3104 | tf_op jit(solution)/shard_map/ppermute | solution.py:25
  60.6 2.0 %fusion.31 = (bf16[256,384]{1,0:T(8,128)(2,1)S(1)}, bf16[1,256,384]{2,1,0:T(8,128)(2,1)}) fusion(bf16[1,256,384]{2,1,0:T(8,128)(2,1)S(1)} %copy-done.26, bf16[256,3840]{1,0:T(8,128)(2,1)S(1)} %fusion.32, bf16[3840,384]{1,0:T(8,128)(2,1)S(1)} %copy-done), kind=kOutput, calls=%fused_computation.83 | convolution fusion | flops 756252672 | bytes 5505024 | tf_op jit(solution)/shard_map/dot_general | solution.py:203
  63.9 5.6 %collective-permute-start.10 = (bf16[2,384]{1,0:T(2,128)(2,1)S(1)}, bf16[2,384]{1,0:T(2,128)(2,1)S(1)}, u32[]{:S(2)}, u32[]{:S(2)}) collective-permute-start(bf16[2,384]{1,0:T(2,128)(2,1)S(1)} %get-tuple-element.53), channel_id=1, source_target_pairs={{0,2},{2,4},{4,6},{6,8},{8,10},{10,12},{12,14},{1,3},{3,5},{5,7},{... | collective-permute-start | bytes 4616 | tf_op jit(solution)/shard_map/ppermute | solution.py:24
  75.5 3.2 %multiply_convert_fusion.1 = bf16[4,128,1024]{1,2,0:T(8,128)(2,1)S(1)} fusion(f32[4,1024,128]{2,1,0:T(8,128)} %copy-done.2, bf16[128,4,192]{0,2,1:T(8,128)(2,1)S(1)} %bitcast.196, bf16[1024,4,192]{0,2,1:T(8,128)(2,1)} %bitcast.185, f32[4,128]{1,0:T(4,128)S(1)} %bitcast.205, f32[4,128]{1,0:T(4,128)S(1)} %log_add_fusion), kind=kOutput, calls=%fused_computation.22 | convolution fusion | flops 203948032 | bytes 4919296 | tf_op jit(solution)/shard_map/ihd,jhd->hij/dot_general | solution.py:289
  78.7 2.0 %fusion.8 = f32[3840,384]{1,0:T(8,128)S(1)} fusion(bf16[1,260,768]{2,1,0:T(8,128)(2,1)S(1)} %copy-done.18, bf16[1,260,768]{2,1,0:T(8,128)(2,1)} %bitcast.31, bf16[1,256,384]{2,1,0:T(8,128)(2,1)} %bitcast.33, bf16[1,256,384]{2,1,0:T(8,128)(2,1)S(1)} %bitcast.189), kind=kOutput, calls=%fused_computation.34 | convolution fusion | flops 302579712 | bytes 2371584 | tf_op jit(solution)/shard_map/spc,spo->co/dot_general | solution.py:219
  80.7 1.7 %fusion.7 = f32[3840,384]{1,0:T(8,128)S(1)} fusion(f32[3840,384]{1,0:T(8,128)S(1)} %fusion.8, bf16[1,260,768]{2,1,0:T(8,128)(2,1)S(1)} %copy-done.18, bf16[1,260,768]{2,1,0:T(8,128)(2,1)} %bitcast.31, bf16[1,256,384]{2,1,0:T(8,128)(2,1)} %bitcast.33, bf16[1,256,384]{2,1,0:T(8,128)(2,1)S(1)} %bitcast.190), kind=kOutput, calls=%fused_computation.32 | convolution fusion | flops 302579712 | bytes 2377728 | tf_op jit(solution)/shard_map/spc,spo->co/dot_general | solution.py:219
  82.4 1.7 %fusion.6 = f32[3840,384]{1,0:T(8,128)S(1)} fusion(f32[3840,384]{1,0:T(8,128)S(1)} %fusion.7, bf16[1,260,768]{2,1,0:T(8,128)(2,1)S(1)} %copy-done.18, bf16[1,260,768]{2,1,0:T(8,128)(2,1)} %bitcast.31, bf16[1,256,384]{2,1,0:T(8,128)(2,1)} %bitcast.33, bf16[1,256,384]{2,1,0:T(8,128)(2,1)S(1)} %bitcast.191), kind=kOutput, calls=%fused_computation.30 | convolution fusion | flops 302579712 | bytes 2377728 | tf_op jit(solution)/shard_map/spc,spo->co/dot_general | solution.py:219
  84.1 1.7 %fusion.5 = f32[3840,384]{1,0:T(8,128)S(1)} fusion(f32[3840,384]{1,0:T(8,128)S(1)} %fusion.6, bf16[1,260,768]{2,1,0:T(8,128)(2,1)S(1)} %copy-done.18, bf16[1,260,768]{2,1,0:T(8,128)(2,1)} %bitcast.31, bf16[1,256,384]{2,1,0:T(8,128)(2,1)} %bitcast.33, bf16[1,256,384]{2,1,0:T(8,128)(2,1)S(1)} %bitcast.192), kind=kOutput, calls=%fused_computation.28 | convolution fusion | flops 302579712 | bytes 2377728 | tf_op jit(solution)/shard_map/spc,spo->co/dot_general | solution.py:219
  85.8 1.7 %fusion.4 = f32[3840,384]{1,0:T(8,128)S(1)} fusion(f32[3840,384]{1,0:T(8,128)S(1)} %fusion.5, bf16[1,260,768]{2,1,0:T(8,128)(2,1)} %bitcast.31, bf16[1,260,768]{2,1,0:T(8,128)(2,1)S(1)} %copy-done.18, bf16[1,256,384]{2,1,0:T(8,128)(2,1)} %bitcast.33, bf16[1,256,384]{2,1,0:T(8,128)(2,1)S(1)} %bitcast.193), kind=kOutput, calls=%fused_computation.26 | convolution fusion | flops 303759360 | bytes 2377728 | tf_op jit(solution)/shard_map/spc,spo->co/dot_general | solution.py:219
  88.0 4.4 %collective-permute-start.20 = (bf16[240,192]{1,0:T(8,128)(2,1)S(1)}, bf16[240,192]{1,0:T(8,128)(2,1)S(1)}, u32[]{:S(2)}, u32[]{:S(2)}) collective-permute-start(bf16[240,192]{1,0:T(8,128)(2,1)S(1)} %get-tuple-element.37), channel_id=1, source_target_pairs={{0,4},{4,8},{8,12},{12,14},{14,10},{10,6},{6,2},{2,0},{1,5},{5,9},... | collective-permute-start | bytes 276488 | tf_op jit(solution)/shard_map/ppermute | solution.py:159
  92.3 1.8 %convolution_convert_fusion = bf16[4,192,1024]{2,1,0:T(8,128)(2,1)} fusion(bf16[128,4,192]{0,2,1:T(8,128)(2,1)S(1)} %bitcast.197, f32[4,1024,128]{2,1,0:T(8,128)S(1)} %copy-done.3, f32[4,128]{1,0:T(4,128)S(1)} %log_add_fusion), kind=kOutput, calls=%fused_computation.24 | convolution fusion | flops 203685888 | bytes 3868672 | tf_op jit(solution)/shard_map/hij,ihd->jhd/dot_general | solution.py:301
  94.8 2.4 %collective-permute-done.27 = bf16[240,192]{1,0:T(8,128)(2,1)S(1)} collective-permute-done((bf16[240,192]{1,0:T(8,128)(2,1)S(1)}, bf16[240,192]{1,0:T(8,128)(2,1)S(1)}, u32[]{:S(2)}, u32[]{:S(2)}) %collective-permute-start.27) | collective-permute-done | bytes 92192 | tf_op jit(solution)/shard_map/ppermute | solution.py:159
  97.4 1.6 %collective-permute-start.21 = (bf16[240,192]{1,0:T(8,128)(2,1)S(1)}, bf16[240,192]{1,0:T(8,128)(2,1)S(1)}, u32[]{:S(2)}, u32[]{:S(2)}) collective-permute-start(bf16[240,192]{1,0:T(8,128)(2,1)S(1)} %get-tuple-element.35), channel_id=1, source_target_pairs={{0,4},{4,8},{8,12},{12,14},{14,10},{10,6},{6,2},{2,0},{1,5},{5,9},... | collective-permute-start | bytes 276488 | tf_op jit(solution)/shard_map/ppermute | solution.py:159
  99.4 1.4 fusion.9
  100.9 2.6 %copy.47 = bf16[1024,768]{1,0:T(8,128)(2,1)} copy(bf16[1024,768]{0,1:T(8,128)(2,1)} %bitcast.188) | data formatting | bytes 3145728 | tf_op jit(solution)/shard_map/reshape | solution.py:305
  103.4 2.3 %copy.44 = bf16[1024,4,128]{0,2,1:T(8,128)(2,1)} copy(bf16[1024,4,128]{2,0,1:T(8,128)(2,1)} %fusion.9) | data formatting | bytes 2097152 | tf_op jit(solution)/shard_map/mul | solution.py:298
  105.7 2.3 %copy.46 = bf16[1024,512]{1,0:T(8,128)(2,1)} copy(bf16[1024,512]{0,1:T(8,128)(2,1)} %bitcast.194) | data formatting | bytes 2097152 | tf_op jit(solution)/shard_map/reshape | solution.py:304
  108.0 1.8 %fusion.51 = (bf16[240,192]{1,0:T(8,128)(2,1)}, bf16[240,192]{1,0:T(8,128)(2,1)S(1)}) fusion(f32[8,2,240,384]{3,2,1,0:T(8,128)} %bitcast.178, s32[]{:T(128)S(6)} %select_n.514, s32[]{:T(128)S(6)} %select_n.498, bf16[240,192]{1,0:T(8,128)(2,1)S(1)} %collective-permute-done.21, s32[]{:T(128)S(6)} %select_n.578, bf16[240,192]{1,0:T(8,128)(2,1)S(1)} %collective-permute-done.28), kind=kLoop, calls=%fused_computation.126 | loop fusion | flops 276480 | bytes 737292 | tf_op jit(solution)/shard_map/convert_element_type | solution.py:162
  109.8 1.6 collective-permute-start.22
  111.8 1.9 %fusion.36 = (bf16[128,1280]{1,0:T(8,128)(2,1)}, bf16[128,1280]{1,0:T(8,128)(2,1)S(1)}) fusion(bf16[1024,768]{1,0:T(8,128)(2,1)} %copy.47, bf16[1024,512]{1,0:T(8,128)(2,1)} %copy.46), kind=kLoop, calls=%fused_computation.96 | loop fusion | flops 1310720 | bytes 3276800 | tf_op jit(solution)/shard_map/concatenate | solution.py:302
  113.7 2.0 %collective-permute-start.15 = (bf16[128,1280]{1,0:T(8,128)(2,1)S(1)}, bf16[128,1280]{1,0:T(8,128)(2,1)}, u32[]{:S(2)}, u32[]{:S(2)}) collective-permute-start(bf16[128,1280]{1,0:T(8,128)(2,1)S(1)} %get-tuple-element.44), channel_id=1, source_target_pairs={{0,4},{4,8},{8,12},{12,14},{14,10},{10,6},{6,2},{2,0},{1,5},{5,9},... | collective-permute-start | bytes 983048 | tf_op jit(solution)/shard_map/ppermute | solution.py:104
  115.9 1.7 %collective-permute-done.29 = bf16[240,192]{1,0:T(8,128)(2,1)} collective-permute-done((bf16[240,192]{1,0:T(8,128)(2,1)S(1)}, bf16[240,192]{1,0:T(8,128)(2,1)}, u32[]{:S(2)}, u32[]{:S(2)}) %collective-permute-start.29) | collective-permute-done | bytes 92192 | tf_op jit(solution)/shard_map/ppermute | solution.py:159
  117.6 1.9 %fusion.50 = (bf16[240,192]{1,0:T(8,128)(2,1)}, bf16[240,192]{1,0:T(8,128)(2,1)S(1)}) fusion(f32[8,2,240,384]{3,2,1,0:T(8,128)} %bitcast.179, s32[]{:T(128)S(6)} %select_n.522, s32[]{:T(128)S(6)} %select_n.498, bf16[240,192]{1,0:T(8,128)(2,1)S(1)} %collective-permute-done.22, s32[]{:T(128)S(6)} %select_n.586, bf16[240,192]{1,0:T(8,128)(2,1)} %collective-permute-done.29), kind=kLoop, calls=%fused_computation.124 | loop fusion | flops 276480 | bytes 737292 | tf_op jit(solution)/shard_map/convert_element_type | solution.py:162
  119.5 1.5 collective-permute-start.23
  122.9 1.9 %add_convert_fusion.5 = bf16[128,1280]{1,0:T(8,128)(2,1)} fusion(bf16[128,1280]{1,0:T(8,128)(2,1)} %collective-permute-done.11, bf16[1024,768]{1,0:T(8,128)(2,1)} %copy.47, bf16[1024,512]{1,0:T(8,128)(2,1)} %copy.46), kind=kLoop, calls=%fused_computation.67 | loop fusion | flops 1146880 | bytes 3276800 | tf_op jit(solution)/shard_map/convert_element_type | solution.py:100
  128.7 2.0 %collective-permute-start.31 = (bf16[240,192]{1,0:T(8,128)(2,1)S(1)}, bf16[240,192]{1,0:T(8,128)(2,1)S(1)}, u32[]{:S(2)}, u32[]{:S(2)}) collective-permute-start(bf16[240,192]{1,0:T(8,128)(2,1)S(1)} %get-tuple-element.30), channel_id=1, source_target_pairs={{0,2},{4,0},{8,4},{12,8},{14,12},{10,14},{6,10},{2,6},{1,3},{5,1},... | collective-permute-start | bytes 276488 | tf_op jit(solution)/shard_map/ppermute | solution.py:159
  130.7 2.6 %collective-permute-done.12 = bf16[128,1280]{1,0:T(8,128)(2,1)} collective-permute-done((bf16[128,1280]{1,0:T(8,128)(2,1)}, bf16[128,1280]{1,0:T(8,128)(2,1)}, u32[]{:S(2)}, u32[]{:S(2)}) %collective-permute-start.12) | collective-permute-done | bytes 327712 | tf_op jit(solution)/shard_map/ppermute | solution.py:96
  133.3 2.3 %add_convert_fusion.4 = (bf16[128,1280]{1,0:T(8,128)(2,1)}, bf16[128,1280]{1,0:T(8,128)(2,1)}) fusion(bf16[128,1280]{1,0:T(8,128)(2,1)} %collective-permute-done.12, bf16[1024,768]{1,0:T(8,128)(2,1)} %copy.47, bf16[1024,512]{1,0:T(8,128)(2,1)} %copy.46, bf16[128,1280]{1,0:T(8,128)(2,1)} %collective-permute-done.15), kind=kLoop, calls=%fused_computation.66 | loop fusion | flops 2293760 | bytes 3932160 | tf_op jit(solution)/shard_map/convert_element_type | solution.py:100
  135.6 1.5 collective-permute-start.13
  137.6 1.8 %fusion.48 = (bf16[240,192]{1,0:T(8,128)(2,1)}, bf16[240,192]{1,0:T(8,128)(2,1)}) fusion(f32[8,2,240,384]{3,2,1,0:T(8,128)} %bitcast.181, s32[]{:T(128)S(6)} %select_n.538, s32[]{:T(128)S(6)} %select_n.498, bf16[240,192]{1,0:T(8,128)(2,1)S(1)} %collective-permute-done.24, s32[]{:T(128)S(6)} %select_n.602, bf16[240,192]{1,0:T(8,128)(2,1)S(1)} %collective-permute-done.31), kind=kLoop, calls=%fused_computation.120 | loop fusion | flops 276480 | bytes 737292 | tf_op jit(solution)/shard_map/convert_element_type | solution.py:162
  142.7 4.4 %collective-permute-done.25 = bf16[240,192]{1,0:T(8,128)(2,1)S(1)} collective-permute-done((bf16[240,192]{1,0:T(8,128)(2,1)}, bf16[240,192]{1,0:T(8,128)(2,1)S(1)}, u32[]{:S(2)}, u32[]{:S(2)}) %collective-permute-start.25) | collective-permute-done | bytes 92192 | tf_op jit(solution)/shard_map/ppermute | solution.py:159
  150.5 1.4 add_convert_fusion.3
  156.5 2.6 %collective-permute-done.17 = bf16[128,1280]{1,0:T(8,128)(2,1)S(1)} collective-permute-done((bf16[128,1280]{1,0:T(8,128)(2,1)S(1)}, bf16[128,1280]{1,0:T(8,128)(2,1)S(1)}, u32[]{:S(2)}, u32[]{:S(2)}) %collective-permute-start.17) | collective-permute-done | bytes 327712 | tf_op jit(solution)/shard_map/ppermute | solution.py:104
  (147 shorter events, 44.7 us)
Async XLA Ops:
  0.6 59.9 %copy-start = (bf16[3840,384]{1,0:T(8,128)(2,1)S(1)}, bf16[3840,384]{1,0:T(8,128)(2,1)}, u32[]{:S(2)}) copy-start(bf16[3840,384]{1,0:T(8,128)(2,1)} %param.14) | copy-start | bytes 8847364
  0.6 27.5 %copy-start.21 = (bf16[1,128,512]{2,1,0:T(8,128)(2,1)S(1)}, bf16[1,128,512]{2,1,0:T(8,128)(2,1)}, u32[]{:S(2)}) copy-start(bf16[1,128,512]{2,1,0:T(8,128)(2,1)} %param.8) | copy-start | bytes 393220
  0.7 27.6 %copy-start.25 = (bf16[768]{0:T(1024)(128)(2,1)S(1)}, bf16[768]{0:T(1024)(128)(2,1)}, u32[]{:S(2)}) copy-start(bf16[768]{0:T(1024)(128)(2,1)} %param.13) | copy-start | bytes 4612
  3.9 10.9 %collective-permute-start = (bf16[128,1280]{0,1:T(8,128)(2,1)}, bf16[128,1280]{0,1:T(8,128)(2,1)S(1)}, u32[]{:S(2)}, u32[]{:S(2)}) collective-permute-start(bf16[128,1280]{0,1:T(8,128)(2,1)} %get-tuple-element.51), channel_id=1, source_target_pairs={{0,4},{4,8},{8,12},{12,14},{14,10},{10,6},{6,2},{2,0},{1,5},{5,9},... | collective-permute-start | bytes 983048 | tf_op jit(solution)/shard_map/ppermute | solution.py:75
  15.5 9.0 %collective-permute-start.1 = (bf16[128,1280]{0,1:T(8,128)(2,1)S(1)}, bf16[128,1280]{0,1:T(8,128)(2,1)}, u32[]{:S(2)}, u32[]{:S(2)}) collective-permute-start(bf16[128,1280]{0,1:T(8,128)(2,1)S(1)} %collective-permute-done), channel_id=1, source_target_pairs={{0,4},{4,8},{8,12},{12,14},{14,10},{10,6},{6,2},{2,0},{1,5},{5,9},... | collective-permute-start | bytes 983048 | tf_op jit(solution)/shard_map/ppermute | solution.py:75
  17.3 11.0 %collective-permute-start.4 = (bf16[128,1280]{0,1:T(8,128)(2,1)}, bf16[128,1280]{0,1:T(8,128)(2,1)S(1)}, u32[]{:S(2)}, u32[]{:S(2)}) collective-permute-start(bf16[128,1280]{0,1:T(8,128)(2,1)} %get-tuple-element.51), channel_id=1, source_target_pairs={{0,2},{4,0},{8,4},{12,8},{14,12},{10,14},{6,10},{2,6},{1,3},{5,1},... | collective-permute-start | bytes 983048 | tf_op jit(solution)/shard_map/ppermute | solution.py:79
  17.5 31.8 %copy-start.22 = (s32[256]{0:T(256)}, s32[256]{0:T(256)S(1)}, u32[]{:S(2)}) copy-start(s32[256]{0:T(256)S(1)} %and_select_fusion) | copy-start | bytes 3076
  24.5 8.3 %collective-permute-start.2 = (bf16[128,1280]{0,1:T(8,128)(2,1)}, bf16[128,1280]{0,1:T(8,128)(2,1)}, u32[]{:S(2)}, u32[]{:S(2)}) collective-permute-start(bf16[128,1280]{0,1:T(8,128)(2,1)} %collective-permute-done.1), channel_id=1, source_target_pairs={{0,4},{4,8},{8,12},{12,14},{14,10},{10,6},{6,2},{2,0},{1,5},{5,9},... | collective-permute-start | bytes 983048 | tf_op jit(solution)/shard_map/ppermute | solution.py:75
  28.3 19.2 %copy-start.16 = (bf16[1,128,512]{1,2,0:T(8,128)(2,1)}, bf16[1,128,512]{1,2,0:T(8,128)(2,1)S(1)}, u32[]{:S(2)}) copy-start(bf16[1,128,512]{1,2,0:T(8,128)(2,1)S(1)} %copy.66) | copy-start | bytes 393220
  28.3 7.8 %collective-permute-start.5 = (bf16[128,1280]{0,1:T(8,128)(2,1)S(1)}, bf16[128,1280]{0,1:T(8,128)(2,1)S(1)}, u32[]{:S(2)}, u32[]{:S(2)}) collective-permute-start(bf16[128,1280]{0,1:T(8,128)(2,1)S(1)} %collective-permute-done.4), channel_id=1, source_target_pairs={{0,2},{4,0},{8,4},{12,8},{14,12},{10,14},{6,10},{2,6},{1,3},{5,1},... | collective-permute-start | bytes 983048 | tf_op jit(solution)/shard_map/ppermute | solution.py:79
  32.8 7.4 %collective-permute-start.3 = (bf16[128,1280]{0,1:T(8,128)(2,1)}, bf16[128,1280]{0,1:T(8,128)(2,1)S(1)}, u32[]{:S(2)}, u32[]{:S(2)}) collective-permute-start(bf16[128,1280]{0,1:T(8,128)(2,1)} %collective-permute-done.2), channel_id=1, source_target_pairs={{0,4},{4,8},{8,12},{12,14},{14,10},{10,6},{6,2},{2,0},{1,5},{5,9},... | collective-permute-start | bytes 983048 | tf_op jit(solution)/shard_map/ppermute | solution.py:75
  36.1 7.1 %collective-permute-start.6 = (bf16[128,1280]{0,1:T(8,128)(2,1)S(1)}, bf16[128,1280]{0,1:T(8,128)(2,1)S(1)}, u32[]{:S(2)}, u32[]{:S(2)}) collective-permute-start(bf16[128,1280]{0,1:T(8,128)(2,1)S(1)} %collective-permute-done.5), channel_id=1, source_target_pairs={{0,2},{4,0},{8,4},{12,8},{14,12},{10,14},{6,10},{2,6},{1,3},{5,1},... | collective-permute-start | bytes 983048 | tf_op jit(solution)/shard_map/ppermute | solution.py:79
  51.5 4.1 %collective-permute-start.7 = (bf16[2,768]{1,0:T(2,128)(2,1)S(1)}, bf16[2,768]{1,0:T(2,128)(2,1)S(1)}, u32[]{:S(2)}, u32[]{:S(2)}) collective-permute-start(bf16[2,768]{1,0:T(2,128)(2,1)S(1)} %get-tuple-element.50), channel_id=1, source_target_pairs={{0,2},{2,4},{4,6},{6,8},{8,10},{10,12},{12,14},{1,3},{3,5},{5,7},{... | collective-permute-start | bytes 9224 | tf_op jit(solution)/shard_map/ppermute | solution.py:24
  54.1 6.5 %copy-start.26 = (bf16[1,256,384]{2,1,0:T(8,128)(2,1)S(1)}, bf16[1,256,384]{2,1,0:T(8,128)(2,1)}, u32[]{:S(2)}) copy-start(bf16[1,256,384]{2,1,0:T(8,128)(2,1)} %param.15) | copy-start | bytes 589828
  54.1 6.2 %collective-permute-start.8 = (bf16[2,768]{1,0:T(2,128)(2,1)S(1)}, bf16[2,768]{1,0:T(2,128)(2,1)S(1)}, u32[]{:S(2)}, u32[]{:S(2)}) collective-permute-start(bf16[2,768]{1,0:T(2,128)(2,1)S(1)} %get-tuple-element.49), channel_id=1, source_target_pairs={{2,0},{4,2},{6,4},{8,6},{10,8},{12,10},{14,12},{3,1},{5,3},{7,5},{... | collective-permute-start | bytes 9224 | tf_op jit(solution)/shard_map/ppermute | solution.py:25
  62.6 16.1 %collective-permute-start.19 = (bf16[256,384]{1,0:T(8,128)(2,1)S(1)}, bf16[256,384]{1,0:T(8,128)(2,1)}, u32[]{:S(2)}, u32[]{:S(2)}) collective-permute-start(bf16[256,384]{1,0:T(8,128)(2,1)S(1)} %get-tuple-element.47), channel_id=1, source_target_pairs={{0,1},{1,0},{2,3},{3,2},{4,5},{5,4},{6,7},{7,6},{8,9},{9,8},{10,11... | collective-permute-start | bytes 589832 | tf_op jit(solution)/shard_map/ppermute | solution.py:215
  62.6 8.2 %collective-permute-start.9 = (bf16[2,384]{1,0:T(2,128)(2,1)S(1)}, bf16[2,384]{1,0:T(2,128)(2,1)S(1)}, u32[]{:S(2)}, u32[]{:S(2)}) collective-permute-start(bf16[2,384]{1,0:T(2,128)(2,1)S(1)} %get-tuple-element.54), channel_id=1, source_target_pairs={{2,0},{4,2},{6,4},{8,6},{10,8},{12,10},{14,12},{3,1},{5,3},{7,5},{... | collective-permute-start | bytes 4616 | tf_op jit(solution)/shard_map/ppermute | solution.py:25
  63.9 7.0 %collective-permute-start.10 = (bf16[2,384]{1,0:T(2,128)(2,1)S(1)}, bf16[2,384]{1,0:T(2,128)(2,1)S(1)}, u32[]{:S(2)}, u32[]{:S(2)}) collective-permute-start(bf16[2,384]{1,0:T(2,128)(2,1)S(1)} %get-tuple-element.53), channel_id=1, source_target_pairs={{0,2},{2,4},{4,6},{6,8},{8,10},{10,12},{12,14},{1,3},{3,5},{5,7},{... | collective-permute-start | bytes 4616 | tf_op jit(solution)/shard_map/ppermute | solution.py:24
  70.6 8.2 %collective-permute-start.18 = (bf16[260,768]{1,0:T(8,128)(2,1)}, bf16[260,768]{1,0:T(8,128)(2,1)}, u32[]{:S(2)}, u32[]{:S(2)}) collective-permute-start(bf16[260,768]{1,0:T(8,128)(2,1)} %get-tuple-element.45), channel_id=1, source_target_pairs={{0,1},{1,0},{2,3},{3,2},{4,5},{5,4},{6,7},{7,6},{8,9},{9,8},{10,11... | collective-permute-start | bytes 1198088 | tf_op jit(solution)/shard_map/ppermute | solution.py:214
  78.7 20.8 %copy-start.11 = (bf16[4,128,1024]{1,2,0:T(8,128)(2,1)}, bf16[4,128,1024]{1,2,0:T(8,128)(2,1)S(1)}, u32[]{:S(2)}) copy-start(bf16[4,128,1024]{1,2,0:T(8,128)(2,1)S(1)} %multiply_convert_fusion.1) | copy-start | bytes 3145732
  87.4 4.9 %copy-start.3 = (f32[4,1024,128]{2,1,0:T(8,128)S(1)}, f32[4,1024,128]{2,1,0:T(8,128)}, u32[]{:S(2)}) copy-start(f32[4,1024,128]{2,1,0:T(8,128)} %copy-done.2) | copy-start | bytes 6291460
  87.8 9.4 %copy-start.7 = (f32[3840,384]{1,0:T(8,128)}, f32[3840,384]{1,0:T(8,128)S(1)}, u32[]{:S(2)}) copy-start(f32[3840,384]{1,0:T(8,128)S(1)} %broadcast_multiply_fusion) | copy-start | bytes 17694724
  88.0 6.8 %collective-permute-start.20 = (bf16[240,192]{1,0:T(8,128)(2,1)S(1)}, bf16[240,192]{1,0:T(8,128)(2,1)S(1)}, u32[]{:S(2)}, u32[]{:S(2)}) collective-permute-start(bf16[240,192]{1,0:T(8,128)(2,1)S(1)} %get-tuple-element.37), channel_id=1, source_target_pairs={{0,4},{4,8},{8,12},{12,14},{14,10},{10,6},{6,2},{2,0},{1,5},{5,9},... | collective-permute-start | bytes 276488 | tf_op jit(solution)/shard_map/ppermute | solution.py:159
  92.3 7.1 %copy-start.17 = (bf16[1,128,512]{1,2,0:T(8,128)(2,1)S(1)}, bf16[1,128,512]{1,2,0:T(8,128)(2,1)}, u32[]{:S(2)}) copy-start(bf16[1,128,512]{1,2,0:T(8,128)(2,1)} %copy-done.16) | copy-start | bytes 393220
  92.3 4.9 %collective-permute-start.27 = (bf16[240,192]{1,0:T(8,128)(2,1)S(1)}, bf16[240,192]{1,0:T(8,128)(2,1)S(1)}, u32[]{:S(2)}, u32[]{:S(2)}) collective-permute-start(bf16[240,192]{1,0:T(8,128)(2,1)S(1)} %get-tuple-element.38), channel_id=1, source_target_pairs={{0,2},{4,0},{8,4},{12,8},{14,12},{10,14},{6,10},{2,6},{1,3},{5,1},... | collective-permute-start | bytes 276488 | tf_op jit(solution)/shard_map/ppermute | solution.py:159
  97.4 10.6 %collective-permute-start.21 = (bf16[240,192]{1,0:T(8,128)(2,1)S(1)}, bf16[240,192]{1,0:T(8,128)(2,1)S(1)}, u32[]{:S(2)}, u32[]{:S(2)}) collective-permute-start(bf16[240,192]{1,0:T(8,128)(2,1)S(1)} %get-tuple-element.35), channel_id=1, source_target_pairs={{0,4},{4,8},{8,12},{12,14},{14,10},{10,6},{6,2},{2,0},{1,5},{5,9},... | collective-permute-start | bytes 276488 | tf_op jit(solution)/shard_map/ppermute | solution.py:159
  99.0 9.0 %collective-permute-start.28 = (bf16[240,192]{1,0:T(8,128)(2,1)S(1)}, bf16[240,192]{1,0:T(8,128)(2,1)S(1)}, u32[]{:S(2)}, u32[]{:S(2)}) collective-permute-start(bf16[240,192]{1,0:T(8,128)(2,1)S(1)} %get-tuple-element.36), channel_id=1, source_target_pairs={{0,2},{4,0},{8,4},{12,8},{14,12},{10,14},{6,10},{2,6},{1,3},{5,1},... | collective-permute-start | bytes 276488 | tf_op jit(solution)/shard_map/ppermute | solution.py:159
  109.8 6.1 %collective-permute-start.22 = (bf16[240,192]{1,0:T(8,128)(2,1)}, bf16[240,192]{1,0:T(8,128)(2,1)S(1)}, u32[]{:S(2)}, u32[]{:S(2)}) collective-permute-start(bf16[240,192]{1,0:T(8,128)(2,1)} %get-tuple-element.33), channel_id=1, source_target_pairs={{0,4},{4,8},{8,12},{12,14},{14,10},{10,6},{6,2},{2,0},{1,5},{5,9},... | collective-permute-start | bytes 276488 | tf_op jit(solution)/shard_map/ppermute | solution.py:159
  111.3 6.3 %collective-permute-start.29 = (bf16[240,192]{1,0:T(8,128)(2,1)S(1)}, bf16[240,192]{1,0:T(8,128)(2,1)}, u32[]{:S(2)}, u32[]{:S(2)}) collective-permute-start(bf16[240,192]{1,0:T(8,128)(2,1)S(1)} %get-tuple-element.34), channel_id=1, source_target_pairs={{0,2},{4,0},{8,4},{12,8},{14,12},{10,14},{6,10},{2,6},{1,3},{5,1},... | collective-permute-start | bytes 276488 | tf_op jit(solution)/shard_map/ppermute | solution.py:159
  113.7 9.2 %collective-permute-start.11 = (bf16[128,1280]{1,0:T(8,128)(2,1)}, bf16[128,1280]{1,0:T(8,128)(2,1)}, u32[]{:S(2)}, u32[]{:S(2)}) collective-permute-start(bf16[128,1280]{1,0:T(8,128)(2,1)} %get-tuple-element.43), channel_id=1, source_target_pairs={{0,2},{4,0},{8,4},{12,8},{14,12},{10,14},{6,10},{2,6},{1,3},{5,1},... | collective-permute-start | bytes 983048 | tf_op jit(solution)/shard_map/ppermute | solution.py:96
  113.7 17.0 %collective-permute-start.15 = (bf16[128,1280]{1,0:T(8,128)(2,1)S(1)}, bf16[128,1280]{1,0:T(8,128)(2,1)}, u32[]{:S(2)}, u32[]{:S(2)}) collective-permute-start(bf16[128,1280]{1,0:T(8,128)(2,1)S(1)} %get-tuple-element.44), channel_id=1, source_target_pairs={{0,4},{4,8},{8,12},{12,14},{14,10},{10,6},{6,2},{2,0},{1,5},{5,9},... | collective-permute-start | bytes 983048 | tf_op jit(solution)/shard_map/ppermute | solution.py:104
  119.5 6.4 %collective-permute-start.23 = (bf16[240,192]{1,0:T(8,128)(2,1)}, bf16[240,192]{1,0:T(8,128)(2,1)S(1)}, u32[]{:S(2)}, u32[]{:S(2)}) collective-permute-start(bf16[240,192]{1,0:T(8,128)(2,1)} %get-tuple-element.31), channel_id=1, source_target_pairs={{0,4},{4,8},{8,12},{12,14},{14,10},{10,6},{6,2},{2,0},{1,5},{5,9},... | collective-permute-start | bytes 276488 | tf_op jit(solution)/shard_map/ppermute | solution.py:159
  121.0 6.3 %collective-permute-start.30 = (bf16[240,192]{1,0:T(8,128)(2,1)S(1)}, bf16[240,192]{1,0:T(8,128)(2,1)}, u32[]{:S(2)}, u32[]{:S(2)}) collective-permute-start(bf16[240,192]{1,0:T(8,128)(2,1)S(1)} %get-tuple-element.32), channel_id=1, source_target_pairs={{0,2},{4,0},{8,4},{12,8},{14,12},{10,14},{6,10},{2,6},{1,3},{5,1},... | collective-permute-start | bytes 276488 | tf_op jit(solution)/shard_map/ppermute | solution.py:159
  124.8 8.5 %collective-permute-start.12 = (bf16[128,1280]{1,0:T(8,128)(2,1)}, bf16[128,1280]{1,0:T(8,128)(2,1)}, u32[]{:S(2)}, u32[]{:S(2)}) collective-permute-start(bf16[128,1280]{1,0:T(8,128)(2,1)} %add_convert_fusion.5), channel_id=1, source_target_pairs={{0,2},{4,0},{8,4},{12,8},{14,12},{10,14},{6,10},{2,6},{1,3},{5,1},... | collective-permute-start | bytes 983048 | tf_op jit(solution)/shard_map/ppermute | solution.py:96
  128.6 9.0 %collective-permute-start.24 = (bf16[240,192]{1,0:T(8,128)(2,1)S(1)}, bf16[240,192]{1,0:T(8,128)(2,1)S(1)}, u32[]{:S(2)}, u32[]{:S(2)}) collective-permute-start(bf16[240,192]{1,0:T(8,128)(2,1)S(1)} %get-tuple-element.29), channel_id=1, source_target_pairs={{0,4},{4,8},{8,12},{12,14},{14,10},{10,6},{6,2},{2,0},{1,5},{5,9},... | collective-permute-start | bytes 276488 | tf_op jit(solution)/shard_map/ppermute | solution.py:159
  128.7 12.8 %copy-start.10 = (bf16[1024,512]{0,1:T(8,128)(2,1)S(1)}, bf16[1024,512]{0,1:T(8,128)(2,1)}, u32[]{:S(2)}) copy-start(bf16[1024,512]{0,1:T(8,128)(2,1)} %copy-done.9) | copy-start | bytes 3145732
  128.7 12.8 %copy-start.12 = (bf16[4,128,1024]{1,2,0:T(8,128)(2,1)S(1)}, bf16[4,128,1024]{1,2,0:T(8,128)(2,1)}, u32[]{:S(2)}) copy-start(bf16[4,128,1024]{1,2,0:T(8,128)(2,1)} %copy-done.11) | copy-start | bytes 3145732
  128.7 8.9 %collective-permute-start.31 = (bf16[240,192]{1,0:T(8,128)(2,1)S(1)}, bf16[240,192]{1,0:T(8,128)(2,1)S(1)}, u32[]{:S(2)}, u32[]{:S(2)}) collective-permute-start(bf16[240,192]{1,0:T(8,128)(2,1)S(1)} %get-tuple-element.30), channel_id=1, source_target_pairs={{0,2},{4,0},{8,4},{12,8},{14,12},{10,14},{6,10},{2,6},{1,3},{5,1},... | collective-permute-start | bytes 276488 | tf_op jit(solution)/shard_map/ppermute | solution.py:159
  135.6 14.9 %collective-permute-start.13 = (bf16[128,1280]{1,0:T(8,128)(2,1)}, bf16[128,1280]{1,0:T(8,128)(2,1)S(1)}, u32[]{:S(2)}, u32[]{:S(2)}) collective-permute-start(bf16[128,1280]{1,0:T(8,128)(2,1)} %get-tuple-element.41), channel_id=1, source_target_pairs={{0,2},{4,0},{8,4},{12,8},{14,12},{10,14},{6,10},{2,6},{1,3},{5,1},... | collective-permute-start | bytes 983048 | tf_op jit(solution)/shard_map/ppermute | solution.py:96
  137.1 13.4 %collective-permute-start.16 = (bf16[128,1280]{1,0:T(8,128)(2,1)}, bf16[128,1280]{1,0:T(8,128)(2,1)}, u32[]{:S(2)}, u32[]{:S(2)}) collective-permute-start(bf16[128,1280]{1,0:T(8,128)(2,1)} %get-tuple-element.42), channel_id=1, source_target_pairs={{0,4},{4,8},{8,12},{12,14},{14,10},{10,6},{6,2},{2,0},{1,5},{5,9},... | collective-permute-start | bytes 983048 | tf_op jit(solution)/shard_map/ppermute | solution.py:104
  139.5 7.6 %collective-permute-start.25 = (bf16[240,192]{1,0:T(8,128)(2,1)}, bf16[240,192]{1,0:T(8,128)(2,1)S(1)}, u32[]{:S(2)}, u32[]{:S(2)}) collective-permute-start(bf16[240,192]{1,0:T(8,128)(2,1)} %get-tuple-element.27), channel_id=1, source_target_pairs={{0,4},{4,8},{8,12},{12,14},{14,10},{10,6},{6,2},{2,0},{1,5},{5,9},... | collective-permute-start | bytes 276488 | tf_op jit(solution)/shard_map/ppermute | solution.py:159
  140.6 6.5 %collective-permute-start.32 = (bf16[240,192]{1,0:T(8,128)(2,1)}, bf16[240,192]{1,0:T(8,128)(2,1)}, u32[]{:S(2)}, u32[]{:S(2)}) collective-permute-start(bf16[240,192]{1,0:T(8,128)(2,1)} %get-tuple-element.28), channel_id=1, source_target_pairs={{0,2},{4,0},{8,4},{12,8},{14,12},{10,14},{6,10},{2,6},{1,3},{5,1},... | collective-permute-start | bytes 276488 | tf_op jit(solution)/shard_map/ppermute | solution.py:159
  148.4 5.6 %collective-permute-start.26 = (bf16[240,192]{1,0:T(8,128)(2,1)S(1)}, bf16[240,192]{1,0:T(8,128)(2,1)S(1)}, u32[]{:S(2)}, u32[]{:S(2)}) collective-permute-start(bf16[240,192]{1,0:T(8,128)(2,1)S(1)} %get-tuple-element.25), channel_id=1, source_target_pairs={{0,4},{4,8},{8,12},{12,14},{14,10},{10,6},{6,2},{2,0},{1,5},{5,9},... | collective-permute-start | bytes 276488 | tf_op jit(solution)/shard_map/ppermute | solution.py:159
  149.5 10.6 %copy-start.1 = (bf16[1024,768]{1,0:T(8,128)(2,1)S(1)}, bf16[1024,768]{1,0:T(8,128)(2,1)}, u32[]{:S(2)}) copy-start(bf16[1024,768]{1,0:T(8,128)(2,1)} %copy.47) | copy-start | bytes 4718596
  149.5 10.6 %copy-start.4 = (bf16[1024,512]{1,0:T(8,128)(2,1)S(1)}, bf16[1024,512]{1,0:T(8,128)(2,1)}, u32[]{:S(2)}) copy-start(bf16[1024,512]{1,0:T(8,128)(2,1)} %copy.46) | copy-start | bytes 3145732
  149.5 4.9 %collective-permute-start.33 = (bf16[240,192]{1,0:T(8,128)(2,1)S(1)}, bf16[240,192]{1,0:T(8,128)(2,1)S(1)}, u32[]{:S(2)}, u32[]{:S(2)}) collective-permute-start(bf16[240,192]{1,0:T(8,128)(2,1)S(1)} %get-tuple-element.26), channel_id=1, source_target_pairs={{0,2},{4,0},{8,4},{12,8},{14,12},{10,14},{6,10},{2,6},{1,3},{5,1},... | collective-permute-start | bytes 276488 | tf_op jit(solution)/shard_map/ppermute | solution.py:159
  151.9 7.1 %collective-permute-start.17 = (bf16[128,1280]{1,0:T(8,128)(2,1)S(1)}, bf16[128,1280]{1,0:T(8,128)(2,1)S(1)}, u32[]{:S(2)}, u32[]{:S(2)}) collective-permute-start(bf16[128,1280]{1,0:T(8,128)(2,1)S(1)} %get-tuple-element.40), channel_id=1, source_target_pairs={{0,4},{4,8},{8,12},{12,14},{14,10},{10,6},{6,2},{2,0},{1,5},{5,9},... | collective-permute-start | bytes 983048 | tf_op jit(solution)/shard_map/ppermute | solution.py:104
  153.0 7.1 %collective-permute-start.14 = (bf16[128,1280]{1,0:T(8,128)(2,1)S(1)}, bf16[128,1280]{1,0:T(8,128)(2,1)S(1)}, u32[]{:S(2)}, u32[]{:S(2)}) collective-permute-start(bf16[128,1280]{1,0:T(8,128)(2,1)S(1)} %get-tuple-element.39), channel_id=1, source_target_pairs={{0,2},{4,0},{8,4},{12,8},{14,12},{10,14},{6,10},{2,6},{1,3},{5,1},... | collective-permute-start | bytes 983048 | tf_op jit(solution)/shard_map/ppermute | solution.py:96
  (13 other events, 22.2 us)

commit v8 on v7

--- a/solution.py
+++ b/solution.py
@@ -67,45 +67,62 @@
 def ring_gather(block, ring):
     count = len(ring)
     forward, backward = ring_perms(ring)
-    left_steps = count // 2
-    right_steps = count - 1 - left_steps
+    full_steps = (count - 1) // 2
+    split = count % 2 == 0
+    half = block.shape[1] // 2
     lefts, rights = [], []
     current = block
-    for _ in range(left_steps):
+    for _ in range(full_steps):
         current = lax.ppermute(current, "seq", forward)
         lefts.append(current)
+    if split:
+        left_half = lax.ppermute(current[:, :half], "seq", forward)
     current = block
-    for _ in range(right_steps):
+    for _ in range(full_steps):
         current = lax.ppermute(current, "seq", backward)
         rights.append(current)
-    return [block] + lefts + rights
+    if split:
+        right_half = lax.ppermute(current[:, half:], "seq", backward)
+    opposite = [jnp.concatenate([left_half, right_half], axis=1)] if split else []
+    return [block] + lefts + rights + opposite
+
+
+def add_part(term, received, side):
+    if received.shape == term.shape:
+        return term + received
+    half = term.shape[1] - received.shape[1] if side else received.shape[1]
+    if side:
+        return jnp.concatenate([term[:, :half], term[:, half:] + received], axis=1)
+    return jnp.concatenate([term[:, :half] + received, term[:, half:]], axis=1)
 
 
 def ring_scatter_back(blocks, ring):
     count = len(ring)
     forward, backward = ring_perms(ring)
-    left_steps = count // 2
-    right_steps = count - 1 - left_steps
+    full_steps = (count - 1) // 2
+    split = count % 2 == 0
     own = blocks[0].astype(jnp.float32)
-    lefts = blocks[1 : 1 + left_steps]
-    rights = blocks[1 + left_steps :]
+    lefts = blocks[1 : 1 + full_steps]
+    rights = blocks[1 + full_steps : 1 + 2 * full_steps]
     total = own
-    if left_steps:
-        acc = lefts[-1]
-        for t in range(left_steps, 0, -1):
-            received = lax.ppermute(acc, "seq", backward).astype(jnp.float32)
+    for side, chain, perm in ((0, lefts, backward), (1, rights, forward)):
+        if split:
+            half = blocks[-1].shape[1] // 2
+            acc = blocks[-1][:, half:] if side else blocks[-1][:, :half]
+            top = full_steps + 1
+        elif full_steps:
+            acc = chain[-1]
+            top = full_steps
+        else:
+            continue
+        for t in range(top, 0, -1):
+            received = lax.ppermute(acc, "seq", perm).astype(jnp.float32)
             if t == 1:
-                total = total + received
+                total = add_part(total, received, side)
             else:
-                acc = (received + lefts[t - 2].astype(jnp.float32)).astype(jnp.bfloat16)
-    if right_steps:
-        acc = rights[-1]
-        for t in range(right_steps, 0, -1):
-            received = lax.ppermute(acc, "seq", forward).astype(jnp.float32)
-            if t == 1:
-                total = total + received
-            else:
-                acc = (received + rights[t - 2].astype(jnp.float32)).astype(jnp.bfloat16)
+                acc = add_part(chain[t - 2].astype(jnp.float32), received, side).astype(
+                    jnp.bfloat16
+                )
     return total
 
 

time: 163 us -> 159 us (0.975)
  other arithmetic: 23.2 us -> 18.3 us
  local copies, waits for them, and re-layouts: 26.7 us -> 24 us
  waiting for transfers between devices: 43.1 us -> 44.8 us
    ppermute x14, waiting for transfers between devices: 11.1 us -> 19.8 us  [ring_reduce_scatter_sliced(): received = lax.ppermute(acc, axis, perm).astype(jnp.float32)]
    ppermute x4 -> x3, waiting for transfers between devices: 18.9 us -> 12.7 us  [ring_gather(): current = lax.ppermute(current, 'seq', forward)]
    ppermute x7 -> x10, waiting for transfers between devices: 7.67 us -> 3.67 us  [the longest x8 2.97 us: ring_scatter_back(): received = lax.ppermute(acc, 'seq', perm).astype(jnp.float32)]
    ppermute x3, waiting for transfers between devices: 0.93 us -> 4.77 us  [ring_gather(): current = lax.ppermute(current, 'seq', backward)]
    unnamed x64 -> x60, local copies, waits for them, and re-layouts: 12.7 us -> 9.79 us
    ppermute x7 -> x10, starting transfers between devices: 7.25 us -> 10.1 us  [the longest x8 7.95 us: ring_scatter_back(): received = lax.ppermute(acc, 'seq', perm).astype(jnp.float32)]
    convert_element_type x6, other arithmetic: 8.19 us -> 5.39 us  [ring_reduce_scatter_sliced(): acc = acc.astype(wire_dtype)]
    concatenate x1, other arithmetic: 1.93 us -> 0.05 us  [body(): jnp.concatenate([key_part.reshape(-1, H * DK), value_part.reshape(-1, H *...]
  transfers between devices with their start and end apart: 34 -> 36, of which waited for: 18 -> 20; matrix products, arithmetic and copies ran while one was open for 29% -> 27% of each run, Pallas kernels for 0% -> 0%
where the time goes in v8:
time: 159 us
  starting transfers between devices  45.4 us (29%)
  waiting for transfers between devices  44.8 us (28%)
  matrix products  24.7 us (16%)
  local copies, waits for them, and re-layouts  24 us (15%)
  other arithmetic  18.3 us (12%)
    ppermute x14, waiting for transfers between devices, ring_reduce_scatter_sliced(): received = lax.ppermute(acc, axis, perm).astype(jnp.float32)  19.8 us
    ppermute x14, starting transfers between devices, ring_reduce_scatter_sliced(): received = lax.ppermute(acc, axis, perm).astype(jnp.float32)  16.7 us
    ppermute x3, waiting for transfers between devices, ring_gather(): current = lax.ppermute(current, 'seq', forward)  12.7 us
    unnamed x60, local copies, waits for them, and re-layouts  9.79 us
    ppermute x2, starting transfers between devices, extended(): before = lax.ppermute(last, axis, up)  8.51 us
    dot_general x5, matrix products, body(): jnp.einsum('spc,spo->co', both_padded[:, offset:offset + positions], both...  8.5 us
    ppermute x8, starting transfers between devices, ring_scatter_back(): received = lax.ppermute(acc, 'seq', perm).astype(jnp.float32)  7.95 us
    ppermute x3, starting transfers between devices, ring_gather(): current = lax.ppermute(current, 'seq', forward)  6.37 us
  transfers between devices with their start and end apart: 36, of which 20 were waited for; matrix products, arithmetic and copies ran while one was open for 27% of the time, Pallas kernels for 0%

profile of v8, /device:TPU:0, one launch (start us, length us, event | category | flops | bytes accessed | tf_op | source)
XLA Modules:
  0.0 158.6 jit_solution(1780838315255005848)
XLA Ops:
  3.9 3.1 %collective-permute-start = (bf16[128,1280]{0,1:T(8,128)(2,1)}, bf16[128,1280]{0,1:T(8,128)(2,1)}, u32[]{:S(2)}, u32[]{:S(2)}) collective-permute-start(bf16[128,1280]{0,1:T(8,128)(2,1)} %get-tuple-element.54), channel_id=1, source_target_pairs={{0,4},{4,8},{8,12},{12,14},{14,10},{10,6},{6,2},{2,0},{1,5},{5,9},... | collective-permute-start | bytes 983048 | tf_op jit(solution)/shard_map/ppermute | solution.py:76
  8.0 6.9 %collective-permute-done = bf16[128,1280]{0,1:T(8,128)(2,1)} collective-permute-done((bf16[128,1280]{0,1:T(8,128)(2,1)}, bf16[128,1280]{0,1:T(8,128)(2,1)}, u32[]{:S(2)}, u32[]{:S(2)}) %collective-permute-start) | collective-permute-done | bytes 327712 | tf_op jit(solution)/shard_map/ppermute | solution.py:76
  14.9 1.8 %collective-permute-start.1 = (bf16[128,1280]{0,1:T(8,128)(2,1)}, bf16[128,1280]{0,1:T(8,128)(2,1)S(1)}, u32[]{:S(2)}, u32[]{:S(2)}) collective-permute-start(bf16[128,1280]{0,1:T(8,128)(2,1)} %collective-permute-done), channel_id=1, source_target_pairs={{0,4},{4,8},{8,12},{12,14},{14,10},{10,6},{6,2},{2,0},{1,5},{5,9},... | collective-permute-start | bytes 983048 | tf_op jit(solution)/shard_map/ppermute | solution.py:76
  18.2 5.8 %collective-permute-done.1 = bf16[128,1280]{0,1:T(8,128)(2,1)S(1)} collective-permute-done((bf16[128,1280]{0,1:T(8,128)(2,1)}, bf16[128,1280]{0,1:T(8,128)(2,1)S(1)}, u32[]{:S(2)}, u32[]{:S(2)}) %collective-permute-start.1) | collective-permute-done | bytes 327712 | tf_op jit(solution)/shard_map/ppermute | solution.py:76
  24.0 1.5 collective-permute-start.2
  26.0 1.7 %constant_dynamic-update-slice_fusion.5 = bf16[1024,1280]{0,1:T(8,128)(2,1)} fusion(bf16[1024,1280]{0,1:T(8,128)(2,1)} %get-tuple-element.55, bf16[128,1280]{0,1:T(8,128)(2,1)} %collective-permute-done), kind=kLoop, calls=%fused_computation.170 | loop fusion | bytes 655360
  28.5 4.8 %collective-permute-done.5 = bf16[128,1280]{0,1:T(8,128)(2,1)S(1)} collective-permute-done((bf16[128,1280]{0,1:T(8,128)(2,1)S(1)}, bf16[128,1280]{0,1:T(8,128)(2,1)S(1)}, u32[]{:S(2)}, u32[]{:S(2)}) %collective-permute-start.5) | collective-permute-done | bytes 327712 | tf_op jit(solution)/shard_map/ppermute | solution.py:82
  33.9 1.6 collective-permute-start.6
  40.1 1.5 slice.170
  41.6 1.9 %slice.171 = bf16[1024,512]{0,1:T(8,128)(2,1)S(1)} slice(bf16[1024,1280]{0,1:T(8,128)(2,1)} %maximum_dynamic-update-slice_fusion), slice={[0:1024], [0:512]} | slice | bytes 2097152 | tf_op jit(solution)/shard_map/slice | solution.py:191
  47.3 3.4 %collective-permute-start.8 = (bf16[2,768]{1,0:T(2,128)(2,1)S(1)}, bf16[2,768]{1,0:T(2,128)(2,1)S(1)}, u32[]{:S(2)}, u32[]{:S(2)}) collective-permute-start(bf16[2,768]{1,0:T(2,128)(2,1)S(1)} %get-tuple-element.53), channel_id=1, source_target_pairs={{0,2},{2,4},{4,6},{6,8},{8,10},{10,12},{12,14},{1,3},{3,5},{5,7},{... | collective-permute-start | bytes 9224 | tf_op jit(solution)/shard_map/ppermute | solution.py:24
  51.0 1.4 collective-permute-start.9
  52.8 3.8 %collective-permute-done.9 = bf16[2,768]{1,0:T(2,128)(2,1)S(1)} collective-permute-done((bf16[2,768]{1,0:T(2,128)(2,1)S(1)}, bf16[2,768]{1,0:T(2,128)(2,1)S(1)}, u32[]{:S(2)}, u32[]{:S(2)}) %collective-permute-start.9) | collective-permute-done | bytes 3104 | tf_op jit(solution)/shard_map/ppermute | solution.py:25
  56.9 2.0 %fusion.32 = (bf16[256,384]{1,0:T(8,128)(2,1)S(1)}, bf16[1,256,384]{2,1,0:T(8,128)(2,1)}) fusion(bf16[1,256,384]{2,1,0:T(8,128)(2,1)S(1)} %copy-done.24, bf16[256,3840]{1,0:T(8,128)(2,1)S(1)} %fusion.33, bf16[3840,384]{1,0:T(8,128)(2,1)S(1)} %copy-done), kind=kOutput, calls=%fused_computation.84 | convolution fusion | flops 756252672 | bytes 5505024 | tf_op jit(solution)/shard_map/dot_general | solution.py:220
  58.9 1.3 collective-permute-start.10
  60.2 5.1 %collective-permute-start.11 = (bf16[2,384]{1,0:T(2,128)(2,1)S(1)}, bf16[2,384]{1,0:T(2,128)(2,1)S(1)}, u32[]{:S(2)}, u32[]{:S(2)}) collective-permute-start(bf16[2,384]{1,0:T(2,128)(2,1)S(1)} %get-tuple-element.56), channel_id=1, source_target_pairs={{0,2},{2,4},{4,6},{6,8},{8,10},{10,12},{12,14},{1,3},{3,5},{5,7},{... | collective-permute-start | bytes 4616 | tf_op jit(solution)/shard_map/ppermute | solution.py:24
  71.3 4.2 %multiply_convert_fusion.1 = bf16[4,128,1024]{1,2,0:T(8,128)(2,1)} fusion(f32[4,1024,128]{2,1,0:T(8,128)} %copy-done.3, bf16[128,4,192]{0,2,1:T(8,128)(2,1)S(1)} %bitcast.196, bf16[1024,4,192]{0,2,1:T(8,128)(2,1)} %bitcast.185, f32[4,128]{1,0:T(4,128)S(1)} %bitcast.205, f32[4,128]{1,0:T(4,128)S(1)} %log_add_fusion), kind=kOutput, calls=%fused_computation.22 | convolution fusion | flops 203948032 | bytes 4919296 | tf_op jit(solution)/shard_map/ihd,jhd->hij/dot_general | solution.py:306
  75.5 1.8 %convolution_convert_fusion = bf16[4,192,1024]{2,1,0:T(8,128)(2,1)} fusion(bf16[128,4,192]{0,2,1:T(8,128)(2,1)S(1)} %bitcast.197, f32[4,1024,128]{2,1,0:T(8,128)S(1)} %copy-done.4, f32[4,128]{1,0:T(4,128)S(1)} %log_add_fusion), kind=kOutput, calls=%fused_computation.24 | convolution fusion | flops 203685888 | bytes 3868672 | tf_op jit(solution)/shard_map/hij,ihd->jhd/dot_general | solution.py:318
  77.3 2.7 %copy.50 = bf16[1024,768]{1,0:T(8,128)(2,1)} copy(bf16[1024,768]{0,1:T(8,128)(2,1)} %bitcast.188) | data formatting | bytes 3145728 | tf_op jit(solution)/shard_map/reshape | solution.py:322
  80.0 2.7 %fusion.9 = bf16[1024,4,128]{2,0,1:T(8,128)(2,1)} fusion(bf16[4,128,1024]{1,2,0:T(8,128)(2,1)} %multiply_convert_fusion.1, bf16[128,4,128]{0,2,1:T(8,128)(2,1)S(1)} %bitcast.200), kind=kOutput, calls=%fused_computation.35 | convolution fusion | flops 135266304 | bytes 2228224 | tf_op jit(solution)/shard_map/hij,ihd->jhd/dot_general | solution.py:315
  82.6 2.3 %copy.47 = bf16[1024,4,128]{0,2,1:T(8,128)(2,1)} copy(bf16[1024,4,128]{2,0,1:T(8,128)(2,1)} %fusion.9) | data formatting | bytes 2097152 | tf_op jit(solution)/shard_map/mul | solution.py:315
  84.9 2.3 %copy.49 = bf16[1024,512]{1,0:T(8,128)(2,1)} copy(bf16[1024,512]{0,1:T(8,128)(2,1)} %bitcast.194) | data formatting | bytes 2097152 | tf_op jit(solution)/shard_map/reshape | solution.py:321
  87.2 1.8 %fusion.8 = f32[3840,384]{1,0:T(8,128)S(1)} fusion(bf16[1,260,768]{2,1,0:T(8,128)(2,1)} %get-tuple-element.49, bf16[1,260,768]{2,1,0:T(8,128)(2,1)} %bitcast.32, bf16[1,256,384]{2,1,0:T(8,128)(2,1)} %bitcast.34, bf16[1,256,384]{2,1,0:T(8,128)(2,1)S(1)} %bitcast.189), kind=kOutput, calls=%fused_computation.34 | convolution fusion | flops 302579712 | bytes 2371584 | tf_op jit(solution)/shard_map/spc,spo->co/dot_general | solution.py:236
  89.0 1.7 %fusion.7 = f32[3840,384]{1,0:T(8,128)S(1)} fusion(f32[3840,384]{1,0:T(8,128)S(1)} %fusion.8, bf16[1,260,768]{2,1,0:T(8,128)(2,1)S(1)} %copy-done.18, bf16[1,260,768]{2,1,0:T(8,128)(2,1)} %bitcast.32, bf16[1,256,384]{2,1,0:T(8,128)(2,1)} %bitcast.34, bf16[1,256,384]{2,1,0:T(8,128)(2,1)S(1)} %bitcast.190), kind=kOutput, calls=%fused_computation.32 | convolution fusion | flops 302579712 | bytes 2377728 | tf_op jit(solution)/shard_map/spc,spo->co/dot_general | solution.py:236
  90.7 1.7 %fusion.6 = f32[3840,384]{1,0:T(8,128)S(1)} fusion(f32[3840,384]{1,0:T(8,128)S(1)} %fusion.7, bf16[1,260,768]{2,1,0:T(8,128)(2,1)S(1)} %copy-done.18, bf16[1,260,768]{2,1,0:T(8,128)(2,1)} %bitcast.32, bf16[1,256,384]{2,1,0:T(8,128)(2,1)} %bitcast.34, bf16[1,256,384]{2,1,0:T(8,128)(2,1)S(1)} %bitcast.191), kind=kOutput, calls=%fused_computation.30 | convolution fusion | flops 302579712 | bytes 2377728 | tf_op jit(solution)/shard_map/spc,spo->co/dot_general | solution.py:236
  92.4 1.7 %fusion.5 = f32[3840,384]{1,0:T(8,128)S(1)} fusion(f32[3840,384]{1,0:T(8,128)S(1)} %fusion.6, bf16[1,260,768]{2,1,0:T(8,128)(2,1)S(1)} %copy-done.18, bf16[1,260,768]{2,1,0:T(8,128)(2,1)} %bitcast.32, bf16[1,256,384]{2,1,0:T(8,128)(2,1)} %bitcast.34, bf16[1,256,384]{2,1,0:T(8,128)(2,1)S(1)} %bitcast.192), kind=kOutput, calls=%fused_computation.28 | convolution fusion | flops 302579712 | bytes 2377728 | tf_op jit(solution)/shard_map/spc,spo->co/dot_general | solution.py:236
  94.1 1.7 %fusion.4 = f32[3840,384]{1,0:T(8,128)S(1)} fusion(f32[3840,384]{1,0:T(8,128)S(1)} %fusion.5, bf16[1,260,768]{2,1,0:T(8,128)(2,1)} %bitcast.32, bf16[1,260,768]{2,1,0:T(8,128)(2,1)S(1)} %copy-done.18, bf16[1,256,384]{2,1,0:T(8,128)(2,1)} %bitcast.34, bf16[1,256,384]{2,1,0:T(8,128)(2,1)S(1)} %bitcast.193), kind=kOutput, calls=%fused_computation.26 | convolution fusion | flops 303759360 | bytes 2377728 | tf_op jit(solution)/shard_map/spc,spo->co/dot_general | solution.py:236
  96.3 4.4 %collective-permute-start.22 = (bf16[240,192]{1,0:T(8,128)(2,1)S(1)}, bf16[240,192]{1,0:T(8,128)(2,1)S(1)}, u32[]{:S(2)}, u32[]{:S(2)}) collective-permute-start(bf16[240,192]{1,0:T(8,128)(2,1)S(1)} %get-tuple-element.37), channel_id=1, source_target_pairs={{0,4},{4,8},{8,12},{12,14},{14,10},{10,6},{6,2},{2,0},{1,5},{5,9},... | collective-permute-start | bytes 276488 | tf_op jit(solution)/shard_map/ppermute | solution.py:176
  101.2 1.7 %collective-permute-start.16 = (bf16[128,640]{1,0:T(8,128)(2,1)S(1)}, bf16[128,640]{1,0:T(8,128)(2,1)S(1)}, u32[]{:S(2)}, u32[]{:S(2)}) collective-permute-start(bf16[128,640]{1,0:T(8,128)(2,1)S(1)} %get-tuple-element.46), channel_id=1, source_target_pairs={{0,4},{4,8},{8,12},{12,14},{14,10},{10,6},{6,2},{2,0},{1,5},{5,9},... | collective-permute-start | bytes 491528 | tf_op jit(solution)/shard_map/ppermute | solution.py:119
  104.1 2.3 %collective-permute-done.29 = bf16[240,192]{1,0:T(8,128)(2,1)S(1)} collective-permute-done((bf16[240,192]{1,0:T(8,128)(2,1)S(1)}, bf16[240,192]{1,0:T(8,128)(2,1)S(1)}, u32[]{:S(2)}, u32[]{:S(2)}) %collective-permute-start.29) | collective-permute-done | bytes 92192 | tf_op jit(solution)/shard_map/ppermute | solution.py:176
  106.5 1.6 %collective-permute-start.23 = (bf16[240,192]{1,0:T(8,128)(2,1)S(1)}, bf16[240,192]{1,0:T(8,128)(2,1)S(1)}, u32[]{:S(2)}, u32[]{:S(2)}) collective-permute-start(bf16[240,192]{1,0:T(8,128)(2,1)S(1)} %get-tuple-element.35), channel_id=1, source_target_pairs={{0,4},{4,8},{8,12},{12,14},{14,10},{10,6},{6,2},{2,0},{1,5},{5,9},... | collective-permute-start | bytes 276488 | tf_op jit(solution)/shard_map/ppermute | solution.py:176
  108.9 2.6 %collective-permute-done.23 = bf16[240,192]{1,0:T(8,128)(2,1)S(1)} collective-permute-done((bf16[240,192]{1,0:T(8,128)(2,1)S(1)}, bf16[240,192]{1,0:T(8,128)(2,1)S(1)}, u32[]{:S(2)}, u32[]{:S(2)}) %collective-permute-start.23) | collective-permute-done | bytes 92192 | tf_op jit(solution)/shard_map/ppermute | solution.py:176
  111.5 1.6 collective-permute-done.30
  113.2 1.6 %collective-permute-start.24 = (bf16[240,192]{1,0:T(8,128)(2,1)S(1)}, bf16[240,192]{1,0:T(8,128)(2,1)S(1)}, u32[]{:S(2)}, u32[]{:S(2)}) collective-permute-start(bf16[240,192]{1,0:T(8,128)(2,1)S(1)} %get-tuple-element.33), channel_id=1, source_target_pairs={{0,4},{4,8},{8,12},{12,14},{14,10},{10,6},{6,2},{2,0},{1,5},{5,9},... | collective-permute-start | bytes 276488 | tf_op jit(solution)/shard_map/ppermute | solution.py:176
  116.5 1.7 %collective-permute-done.24 = bf16[240,192]{1,0:T(8,128)(2,1)S(1)} collective-permute-done((bf16[240,192]{1,0:T(8,128)(2,1)S(1)}, bf16[240,192]{1,0:T(8,128)(2,1)S(1)}, u32[]{:S(2)}, u32[]{:S(2)}) %collective-permute-start.24) | collective-permute-done | bytes 92192 | tf_op jit(solution)/shard_map/ppermute | solution.py:176
  118.2 2.0 %collective-permute-done.31 = bf16[240,192]{1,0:T(8,128)(2,1)S(1)} collective-permute-done((bf16[240,192]{1,0:T(8,128)(2,1)S(1)}, bf16[240,192]{1,0:T(8,128)(2,1)S(1)}, u32[]{:S(2)}, u32[]{:S(2)}) %collective-permute-start.31) | collective-permute-done | bytes 92192 | tf_op jit(solution)/shard_map/ppermute | solution.py:176
  124.2 1.8 %collective-permute-done.25 = bf16[240,192]{1,0:T(8,128)(2,1)S(1)} collective-permute-done((bf16[240,192]{1,0:T(8,128)(2,1)}, bf16[240,192]{1,0:T(8,128)(2,1)S(1)}, u32[]{:S(2)}, u32[]{:S(2)}) %collective-permute-start.25) | collective-permute-done | bytes 92192 | tf_op jit(solution)/shard_map/ppermute | solution.py:176
  127.1 1.3 fusion.50
  128.9 1.5 collective-permute-start.33
  130.9 2.3 %add_convert_fusion.4 = (bf16[128,1280]{1,0:T(8,128)(2,1)}, bf16[128,1280]{1,0:T(8,128)(2,1)}) fusion(bf16[128,1280]{1,0:T(8,128)(2,1)} %collective-permute-done.13, bf16[1024,768]{1,0:T(8,128)(2,1)} %copy.50, bf16[1024,512]{1,0:T(8,128)(2,1)} %copy.49, bf16[128,1280]{1,0:T(8,128)(2,1)} %collective-permute-done.17), kind=kLoop, calls=%fused_computation.67 | loop fusion | flops 2293760 | bytes 3932160 | tf_op jit(solution)/shard_map/convert_element_type | solution.py:123
  133.2 1.9 %collective-permute-start.14 = (bf16[128,1280]{1,0:T(8,128)(2,1)}, bf16[128,1280]{1,0:T(8,128)(2,1)S(1)}, u32[]{:S(2)}, u32[]{:S(2)}) collective-permute-start(bf16[128,1280]{1,0:T(8,128)(2,1)} %get-tuple-element.41), channel_id=1, source_target_pairs={{0,2},{4,0},{8,4},{12,8},{14,12},{10,14},{6,10},{2,6},{1,3},{5,1},... | collective-permute-start | bytes 983048 | tf_op jit(solution)/shard_map/ppermute | solution.py:119
  135.3 1.8 %fusion.49 = (bf16[240,192]{1,0:T(8,128)(2,1)}, bf16[240,192]{1,0:T(8,128)(2,1)}) fusion(f32[8,2,240,384]{3,2,1,0:T(8,128)} %bitcast.181, s32[]{:T(128)S(6)} %select_n.538, s32[]{:T(128)S(6)} %select_n.498, bf16[240,192]{1,0:T(8,128)(2,1)S(1)} %collective-permute-done.26, s32[]{:T(128)S(6)} %select_n.602, bf16[240,192]{1,0:T(8,128)(2,1)S(1)} %collective-permute-done.33), kind=kLoop, calls=%fused_computation.124 | loop fusion | flops 276480 | bytes 737292 | tf_op jit(solution)/shard_map/convert_element_type | solution.py:179
  137.1 1.9 %collective-permute-start.27 = (bf16[240,192]{1,0:T(8,128)(2,1)}, bf16[240,192]{1,0:T(8,128)(2,1)S(1)}, u32[]{:S(2)}, u32[]{:S(2)}) collective-permute-start(bf16[240,192]{1,0:T(8,128)(2,1)} %get-tuple-element.27), channel_id=1, source_target_pairs={{0,4},{4,8},{8,12},{12,14},{14,10},{10,6},{6,2},{2,0},{1,5},{5,9},... | collective-permute-start | bytes 276488 | tf_op jit(solution)/shard_map/ppermute | solution.py:176
  140.3 4.7 %collective-permute-done.27 = bf16[240,192]{1,0:T(8,128)(2,1)S(1)} collective-permute-done((bf16[240,192]{1,0:T(8,128)(2,1)}, bf16[240,192]{1,0:T(8,128)(2,1)S(1)}, u32[]{:S(2)}, u32[]{:S(2)}) %collective-permute-start.27) | collective-permute-done | bytes 92192 | tf_op jit(solution)/shard_map/ppermute | solution.py:176
  146.5 1.9 %collective-permute-start.35 = (bf16[240,192]{1,0:T(8,128)(2,1)S(1)}, bf16[240,192]{1,0:T(8,128)(2,1)S(1)}, u32[]{:S(2)}, u32[]{:S(2)}) collective-permute-start(bf16[240,192]{1,0:T(8,128)(2,1)S(1)} %get-tuple-element.26), channel_id=1, source_target_pairs={{0,2},{4,0},{8,4},{12,8},{14,12},{10,14},{6,10},{2,6},{1,3},{5,1},... | collective-permute-start | bytes 276488 | tf_op jit(solution)/shard_map/ppermute | solution.py:176
  148.4 1.4 add_convert_fusion.3
  150.0 1.9 %collective-permute-start.15 = (bf16[128,1280]{1,0:T(8,128)(2,1)S(1)}, bf16[128,1280]{1,0:T(8,128)(2,1)S(1)}, u32[]{:S(2)}, u32[]{:S(2)}) collective-permute-start(bf16[128,1280]{1,0:T(8,128)(2,1)S(1)} %get-tuple-element.39), channel_id=1, source_target_pairs={{0,2},{4,0},{8,4},{12,8},{14,12},{10,14},{6,10},{2,6},{1,3},{5,1},... | collective-permute-start | bytes 983048 | tf_op jit(solution)/shard_map/ppermute | solution.py:119
  154.8 2.2 %collective-permute-done.19 = bf16[128,1280]{1,0:T(8,128)(2,1)S(1)} collective-permute-done((bf16[128,1280]{1,0:T(8,128)(2,1)S(1)}, bf16[128,1280]{1,0:T(8,128)(2,1)S(1)}, u32[]{:S(2)}, u32[]{:S(2)}) %collective-permute-start.19) | collective-permute-done | bytes 327712 | tf_op jit(solution)/shard_map/ppermute | solution.py:119
  (151 shorter events, 41.2 us)
Async XLA Ops:
  0.6 56.2 %copy-start = (bf16[3840,384]{1,0:T(8,128)(2,1)S(1)}, bf16[3840,384]{1,0:T(8,128)(2,1)}, u32[]{:S(2)}) copy-start(bf16[3840,384]{1,0:T(8,128)(2,1)} %param.14) | copy-start | bytes 8847364
  0.6 7.3 %copy-start.23 = (bf16[768]{0:T(1024)(128)(2,1)S(1)}, bf16[768]{0:T(1024)(128)(2,1)}, u32[]{:S(2)}) copy-start(bf16[768]{0:T(1024)(128)(2,1)} %param.13) | copy-start | bytes 4612
  3.9 11.0 %collective-permute-start = (bf16[128,1280]{0,1:T(8,128)(2,1)}, bf16[128,1280]{0,1:T(8,128)(2,1)}, u32[]{:S(2)}, u32[]{:S(2)}) collective-permute-start(bf16[128,1280]{0,1:T(8,128)(2,1)} %get-tuple-element.54), channel_id=1, source_target_pairs={{0,4},{4,8},{8,12},{12,14},{14,10},{10,6},{6,2},{2,0},{1,5},{5,9},... | collective-permute-start | bytes 983048 | tf_op jit(solution)/shard_map/ppermute | solution.py:76
  6.9 9.8 %collective-permute-start.3 = (bf16[128,1280]{0,1:T(8,128)(2,1)}, bf16[128,1280]{0,1:T(8,128)(2,1)S(1)}, u32[]{:S(2)}, u32[]{:S(2)}) collective-permute-start(bf16[128,1280]{0,1:T(8,128)(2,1)} %get-tuple-element.54), channel_id=1, source_target_pairs={{0,2},{4,0},{8,4},{12,8},{14,12},{10,14},{6,10},{2,6},{1,3},{5,1},... | collective-permute-start | bytes 983048 | tf_op jit(solution)/shard_map/ppermute | solution.py:82
  8.0 35.5 %copy-start.16 = (bf16[1,128,512]{1,2,0:T(8,128)(2,1)}, bf16[1,128,512]{1,2,0:T(8,128)(2,1)S(1)}, u32[]{:S(2)}) copy-start(bf16[1,128,512]{1,2,0:T(8,128)(2,1)S(1)} %copy.72) | copy-start | bytes 393220
  14.9 9.1 %collective-permute-start.1 = (bf16[128,1280]{0,1:T(8,128)(2,1)}, bf16[128,1280]{0,1:T(8,128)(2,1)S(1)}, u32[]{:S(2)}, u32[]{:S(2)}) collective-permute-start(bf16[128,1280]{0,1:T(8,128)(2,1)} %collective-permute-done), channel_id=1, source_target_pairs={{0,4},{4,8},{8,12},{12,14},{14,10},{10,6},{6,2},{2,0},{1,5},{5,9},... | collective-permute-start | bytes 983048 | tf_op jit(solution)/shard_map/ppermute | solution.py:76
  16.7 8.8 %collective-permute-start.4 = (bf16[128,1280]{0,1:T(8,128)(2,1)S(1)}, bf16[128,1280]{0,1:T(8,128)(2,1)S(1)}, u32[]{:S(2)}, u32[]{:S(2)}) collective-permute-start(bf16[128,1280]{0,1:T(8,128)(2,1)S(1)} %collective-permute-done.3), channel_id=1, source_target_pairs={{0,2},{4,0},{8,4},{12,8},{14,12},{10,14},{6,10},{2,6},{1,3},{5,1},... | collective-permute-start | bytes 983048 | tf_op jit(solution)/shard_map/ppermute | solution.py:82
  16.9 28.5 %copy-start.20 = (s32[256]{0:T(256)}, s32[256]{0:T(256)S(1)}, u32[]{:S(2)}) copy-start(s32[256]{0:T(256)S(1)} %and_select_fusion) | copy-start | bytes 3076
  24.0 9.9 %collective-permute-start.2 = (bf16[128,1280]{0,1:T(8,128)(2,1)S(1)}, bf16[128,1280]{0,1:T(8,128)(2,1)S(1)}, u32[]{:S(2)}, u32[]{:S(2)}) collective-permute-start(bf16[128,1280]{0,1:T(8,128)(2,1)S(1)} %collective-permute-done.1), channel_id=1, source_target_pairs={{0,4},{4,8},{8,12},{12,14},{14,10},{10,6},{6,2},{2,0},{1,5},{5,9},... | collective-permute-start | bytes 983048 | tf_op jit(solution)/shard_map/ppermute | solution.py:76
  25.5 7.8 %collective-permute-start.5 = (bf16[128,1280]{0,1:T(8,128)(2,1)S(1)}, bf16[128,1280]{0,1:T(8,128)(2,1)S(1)}, u32[]{:S(2)}, u32[]{:S(2)}) collective-permute-start(bf16[128,1280]{0,1:T(8,128)(2,1)S(1)} %collective-permute-done.4), channel_id=1, source_target_pairs={{0,2},{4,0},{8,4},{12,8},{14,12},{10,14},{6,10},{2,6},{1,3},{5,1},... | collective-permute-start | bytes 983048 | tf_op jit(solution)/shard_map/ppermute | solution.py:82
  33.3 5.4 %collective-permute-start.7 = (bf16[128,640]{0,1:T(8,128)(2,1)S(1)}, bf16[128,640]{0,1:T(8,128)(2,1)S(1)}, u32[]{:S(2)}, u32[]{:S(2)}) collective-permute-start(bf16[128,640]{0,1:T(8,128)(2,1)S(1)} %slice.169), channel_id=1, source_target_pairs={{0,2},{4,0},{8,4},{12,8},{14,12},{10,14},{6,10},{2,6},{1,3},{5,1},... | collective-permute-start | bytes 491528 | tf_op jit(solution)/shard_map/ppermute | solution.py:85
  33.9 5.4 %collective-permute-start.6 = (bf16[128,640]{0,1:T(8,128)(2,1)S(1)}, bf16[128,640]{0,1:T(8,128)(2,1)S(1)}, u32[]{:S(2)}, u32[]{:S(2)}) collective-permute-start(bf16[128,640]{0,1:T(8,128)(2,1)S(1)} %slice.168), channel_id=1, source_target_pairs={{0,4},{4,8},{8,12},{12,14},{14,10},{10,6},{6,2},{2,0},{1,5},{5,9},... | collective-permute-start | bytes 491528 | tf_op jit(solution)/shard_map/ppermute | solution.py:79
  47.3 5.1 %collective-permute-start.8 = (bf16[2,768]{1,0:T(2,128)(2,1)S(1)}, bf16[2,768]{1,0:T(2,128)(2,1)S(1)}, u32[]{:S(2)}, u32[]{:S(2)}) collective-permute-start(bf16[2,768]{1,0:T(2,128)(2,1)S(1)} %get-tuple-element.53), channel_id=1, source_target_pairs={{0,2},{2,4},{4,6},{6,8},{8,10},{10,12},{12,14},{1,3},{3,5},{5,7},{... | collective-permute-start | bytes 9224 | tf_op jit(solution)/shard_map/ppermute | solution.py:24
  51.0 5.9 %copy-start.24 = (bf16[1,256,384]{2,1,0:T(8,128)(2,1)S(1)}, bf16[1,256,384]{2,1,0:T(8,128)(2,1)}, u32[]{:S(2)}) copy-start(bf16[1,256,384]{2,1,0:T(8,128)(2,1)} %param.15) | copy-start | bytes 589828
  51.0 5.6 %collective-permute-start.9 = (bf16[2,768]{1,0:T(2,128)(2,1)S(1)}, bf16[2,768]{1,0:T(2,128)(2,1)S(1)}, u32[]{:S(2)}, u32[]{:S(2)}) collective-permute-start(bf16[2,768]{1,0:T(2,128)(2,1)S(1)} %get-tuple-element.52), channel_id=1, source_target_pairs={{2,0},{4,2},{6,4},{8,6},{10,8},{12,10},{14,12},{3,1},{5,3},{7,5},{... | collective-permute-start | bytes 9224 | tf_op jit(solution)/shard_map/ppermute | solution.py:25
  58.9 28.3 %collective-permute-start.21 = (bf16[256,384]{1,0:T(8,128)(2,1)S(1)}, bf16[256,384]{1,0:T(8,128)(2,1)}, u32[]{:S(2)}, u32[]{:S(2)}) collective-permute-start(bf16[256,384]{1,0:T(8,128)(2,1)S(1)} %get-tuple-element.50), channel_id=1, source_target_pairs={{0,1},{1,0},{2,3},{3,2},{4,5},{5,4},{6,7},{7,6},{8,9},{9,8},{10,11... | collective-permute-start | bytes 589832 | tf_op jit(solution)/shard_map/ppermute | solution.py:232
  58.9 7.7 %collective-permute-start.10 = (bf16[2,384]{1,0:T(2,128)(2,1)S(1)}, bf16[2,384]{1,0:T(2,128)(2,1)S(1)}, u32[]{:S(2)}, u32[]{:S(2)}) collective-permute-start(bf16[2,384]{1,0:T(2,128)(2,1)S(1)} %get-tuple-element.57), channel_id=1, source_target_pairs={{2,0},{4,2},{6,4},{8,6},{10,8},{12,10},{14,12},{3,1},{5,3},{7,5},{... | collective-permute-start | bytes 4616 | tf_op jit(solution)/shard_map/ppermute | solution.py:25
  60.2 6.6 %collective-permute-start.11 = (bf16[2,384]{1,0:T(2,128)(2,1)S(1)}, bf16[2,384]{1,0:T(2,128)(2,1)S(1)}, u32[]{:S(2)}, u32[]{:S(2)}) collective-permute-start(bf16[2,384]{1,0:T(2,128)(2,1)S(1)} %get-tuple-element.56), channel_id=1, source_target_pairs={{0,2},{2,4},{4,6},{6,8},{8,10},{10,12},{12,14},{1,3},{3,5},{5,7},{... | collective-permute-start | bytes 4616 | tf_op jit(solution)/shard_map/ppermute | solution.py:24
  66.4 20.8 %collective-permute-start.20 = (bf16[260,768]{1,0:T(8,128)(2,1)}, bf16[260,768]{1,0:T(8,128)(2,1)}, u32[]{:S(2)}, u32[]{:S(2)}) collective-permute-start(bf16[260,768]{1,0:T(8,128)(2,1)} %get-tuple-element.48), channel_id=1, source_target_pairs={{0,1},{1,0},{2,3},{3,2},{4,5},{5,4},{6,7},{7,6},{8,9},{9,8},{10,11... | collective-permute-start | bytes 1198088 | tf_op jit(solution)/shard_map/ppermute | solution.py:231
  95.7 4.9 %copy-start.1 = (bf16[1024,768]{1,0:T(8,128)(2,1)S(1)}, bf16[1024,768]{1,0:T(8,128)(2,1)}, u32[]{:S(2)}) copy-start(bf16[1024,768]{1,0:T(8,128)(2,1)} %copy.50) | copy-start | bytes 4718596
  95.7 4.9 %copy-start.5 = (bf16[1024,512]{1,0:T(8,128)(2,1)S(1)}, bf16[1024,512]{1,0:T(8,128)(2,1)}, u32[]{:S(2)}) copy-start(bf16[1024,512]{1,0:T(8,128)(2,1)} %copy.49) | copy-start | bytes 3145732
  96.1 24.0 %copy-start.9 = (f32[3840,384]{1,0:T(8,128)}, f32[3840,384]{1,0:T(8,128)S(1)}, u32[]{:S(2)}) copy-start(f32[3840,384]{1,0:T(8,128)S(1)} %broadcast_multiply_fusion) | copy-start | bytes 17694724
  96.3 7.8 %collective-permute-start.22 = (bf16[240,192]{1,0:T(8,128)(2,1)S(1)}, bf16[240,192]{1,0:T(8,128)(2,1)S(1)}, u32[]{:S(2)}, u32[]{:S(2)}) collective-permute-start(bf16[240,192]{1,0:T(8,128)(2,1)S(1)} %get-tuple-element.37), channel_id=1, source_target_pairs={{0,4},{4,8},{8,12},{12,14},{14,10},{10,6},{6,2},{2,0},{1,5},{5,9},... | collective-permute-start | bytes 276488 | tf_op jit(solution)/shard_map/ppermute | solution.py:176
  100.6 5.8 %collective-permute-start.29 = (bf16[240,192]{1,0:T(8,128)(2,1)S(1)}, bf16[240,192]{1,0:T(8,128)(2,1)S(1)}, u32[]{:S(2)}, u32[]{:S(2)}) collective-permute-start(bf16[240,192]{1,0:T(8,128)(2,1)S(1)} %get-tuple-element.38), channel_id=1, source_target_pairs={{0,2},{4,0},{8,4},{12,8},{14,12},{10,14},{6,10},{2,6},{1,3},{5,1},... | collective-permute-start | bytes 276488 | tf_op jit(solution)/shard_map/ppermute | solution.py:176
  100.7 8.1 %collective-permute-start.12 = (bf16[128,640]{1,0:T(8,128)(2,1)S(1)}, bf16[128,640]{1,0:T(8,128)(2,1)S(1)}, u32[]{:S(2)}, u32[]{:S(2)}) collective-permute-start(bf16[128,640]{1,0:T(8,128)(2,1)S(1)} %get-tuple-element.45), channel_id=1, source_target_pairs={{0,2},{4,0},{8,4},{12,8},{14,12},{10,14},{6,10},{2,6},{1,3},{5,1},... | collective-permute-start | bytes 491528 | tf_op jit(solution)/shard_map/ppermute | solution.py:119
  101.2 7.6 %collective-permute-start.16 = (bf16[128,640]{1,0:T(8,128)(2,1)S(1)}, bf16[128,640]{1,0:T(8,128)(2,1)S(1)}, u32[]{:S(2)}, u32[]{:S(2)}) collective-permute-start(bf16[128,640]{1,0:T(8,128)(2,1)S(1)} %get-tuple-element.46), channel_id=1, source_target_pairs={{0,4},{4,8},{8,12},{12,14},{14,10},{10,6},{6,2},{2,0},{1,5},{5,9},... | collective-permute-start | bytes 491528 | tf_op jit(solution)/shard_map/ppermute | solution.py:119
  106.5 4.9 %collective-permute-start.23 = (bf16[240,192]{1,0:T(8,128)(2,1)S(1)}, bf16[240,192]{1,0:T(8,128)(2,1)S(1)}, u32[]{:S(2)}, u32[]{:S(2)}) collective-permute-start(bf16[240,192]{1,0:T(8,128)(2,1)S(1)} %get-tuple-element.35), channel_id=1, source_target_pairs={{0,4},{4,8},{8,12},{12,14},{14,10},{10,6},{6,2},{2,0},{1,5},{5,9},... | collective-permute-start | bytes 276488 | tf_op jit(solution)/shard_map/ppermute | solution.py:176
  108.2 4.9 %collective-permute-start.30 = (bf16[240,192]{1,0:T(8,128)(2,1)S(1)}, bf16[240,192]{1,0:T(8,128)(2,1)S(1)}, u32[]{:S(2)}, u32[]{:S(2)}) collective-permute-start(bf16[240,192]{1,0:T(8,128)(2,1)S(1)} %get-tuple-element.36), channel_id=1, source_target_pairs={{0,2},{4,0},{8,4},{12,8},{14,12},{10,14},{6,10},{2,6},{1,3},{5,1},... | collective-permute-start | bytes 276488 | tf_op jit(solution)/shard_map/ppermute | solution.py:176
  113.2 5.0 %collective-permute-start.24 = (bf16[240,192]{1,0:T(8,128)(2,1)S(1)}, bf16[240,192]{1,0:T(8,128)(2,1)S(1)}, u32[]{:S(2)}, u32[]{:S(2)}) collective-permute-start(bf16[240,192]{1,0:T(8,128)(2,1)S(1)} %get-tuple-element.33), channel_id=1, source_target_pairs={{0,4},{4,8},{8,12},{12,14},{14,10},{10,6},{6,2},{2,0},{1,5},{5,9},... | collective-permute-start | bytes 276488 | tf_op jit(solution)/shard_map/ppermute | solution.py:176
  114.8 5.3 %collective-permute-start.31 = (bf16[240,192]{1,0:T(8,128)(2,1)S(1)}, bf16[240,192]{1,0:T(8,128)(2,1)S(1)}, u32[]{:S(2)}, u32[]{:S(2)}) collective-permute-start(bf16[240,192]{1,0:T(8,128)(2,1)S(1)} %get-tuple-element.34), channel_id=1, source_target_pairs={{0,2},{4,0},{8,4},{12,8},{14,12},{10,14},{6,10},{2,6},{1,3},{5,1},... | collective-permute-start | bytes 276488 | tf_op jit(solution)/shard_map/ppermute | solution.py:176
  116.0 14.4 %collective-permute-start.13 = (bf16[128,1280]{1,0:T(8,128)(2,1)}, bf16[128,1280]{1,0:T(8,128)(2,1)}, u32[]{:S(2)}, u32[]{:S(2)}) collective-permute-start(bf16[128,1280]{1,0:T(8,128)(2,1)} %pad_maximum_fusion.8), channel_id=1, source_target_pairs={{0,2},{4,0},{8,4},{12,8},{14,12},{10,14},{6,10},{2,6},{1,3},{5,1},... | collective-permute-start | bytes 983048 | tf_op jit(solution)/shard_map/ppermute | solution.py:119
  120.9 5.1 %collective-permute-start.25 = (bf16[240,192]{1,0:T(8,128)(2,1)}, bf16[240,192]{1,0:T(8,128)(2,1)S(1)}, u32[]{:S(2)}, u32[]{:S(2)}) collective-permute-start(bf16[240,192]{1,0:T(8,128)(2,1)} %get-tuple-element.31), channel_id=1, source_target_pairs={{0,4},{4,8},{8,12},{12,14},{14,10},{10,6},{6,2},{2,0},{1,5},{5,9},... | collective-permute-start | bytes 276488 | tf_op jit(solution)/shard_map/ppermute | solution.py:176
  122.1 5.0 %collective-permute-start.32 = (bf16[240,192]{1,0:T(8,128)(2,1)S(1)}, bf16[240,192]{1,0:T(8,128)(2,1)}, u32[]{:S(2)}, u32[]{:S(2)}) collective-permute-start(bf16[240,192]{1,0:T(8,128)(2,1)S(1)} %get-tuple-element.32), channel_id=1, source_target_pairs={{0,2},{4,0},{8,4},{12,8},{14,12},{10,14},{6,10},{2,6},{1,3},{5,1},... | collective-permute-start | bytes 276488 | tf_op jit(solution)/shard_map/ppermute | solution.py:176
  122.9 8.0 %collective-permute-start.17 = (bf16[128,1280]{1,0:T(8,128)(2,1)S(1)}, bf16[128,1280]{1,0:T(8,128)(2,1)}, u32[]{:S(2)}, u32[]{:S(2)}) collective-permute-start(bf16[128,1280]{1,0:T(8,128)(2,1)S(1)} %fusion.41), channel_id=1, source_target_pairs={{0,4},{4,8},{8,12},{12,14},{14,10},{10,6},{6,2},{2,0},{1,5},{5,9},... | collective-permute-start | bytes 983048 | tf_op jit(solution)/shard_map/ppermute | solution.py:119
  128.4 6.9 %collective-permute-start.26 = (bf16[240,192]{1,0:T(8,128)(2,1)S(1)}, bf16[240,192]{1,0:T(8,128)(2,1)S(1)}, u32[]{:S(2)}, u32[]{:S(2)}) collective-permute-start(bf16[240,192]{1,0:T(8,128)(2,1)S(1)} %get-tuple-element.29), channel_id=1, source_target_pairs={{0,4},{4,8},{8,12},{12,14},{14,10},{10,6},{6,2},{2,0},{1,5},{5,9},... | collective-permute-start | bytes 276488 | tf_op jit(solution)/shard_map/ppermute | solution.py:176
  128.9 10.2 %copy-start.12 = (bf16[1024,512]{0,1:T(8,128)(2,1)S(1)}, bf16[1024,512]{0,1:T(8,128)(2,1)}, u32[]{:S(2)}) copy-start(bf16[1024,512]{0,1:T(8,128)(2,1)} %copy-done.11) | copy-start | bytes 3145732
  128.9 10.2 %copy-start.13 = (bf16[4,128,1024]{1,2,0:T(8,128)(2,1)S(1)}, bf16[4,128,1024]{1,2,0:T(8,128)(2,1)}, u32[]{:S(2)}) copy-start(bf16[4,128,1024]{1,2,0:T(8,128)(2,1)} %multiply_convert_fusion.1) | copy-start | bytes 3145732
  128.9 6.3 %collective-permute-start.33 = (bf16[240,192]{1,0:T(8,128)(2,1)S(1)}, bf16[240,192]{1,0:T(8,128)(2,1)S(1)}, u32[]{:S(2)}, u32[]{:S(2)}) collective-permute-start(bf16[240,192]{1,0:T(8,128)(2,1)S(1)} %get-tuple-element.30), channel_id=1, source_target_pairs={{0,2},{4,0},{8,4},{12,8},{14,12},{10,14},{6,10},{2,6},{1,3},{5,1},... | collective-permute-start | bytes 276488 | tf_op jit(solution)/shard_map/ppermute | solution.py:176
  133.2 15.1 %collective-permute-start.14 = (bf16[128,1280]{1,0:T(8,128)(2,1)}, bf16[128,1280]{1,0:T(8,128)(2,1)S(1)}, u32[]{:S(2)}, u32[]{:S(2)}) collective-permute-start(bf16[128,1280]{1,0:T(8,128)(2,1)} %get-tuple-element.41), channel_id=1, source_target_pairs={{0,2},{4,0},{8,4},{12,8},{14,12},{10,14},{6,10},{2,6},{1,3},{5,1},... | collective-permute-start | bytes 983048 | tf_op jit(solution)/shard_map/ppermute | solution.py:119
  135.1 13.3 %collective-permute-start.18 = (bf16[128,1280]{1,0:T(8,128)(2,1)}, bf16[128,1280]{1,0:T(8,128)(2,1)}, u32[]{:S(2)}, u32[]{:S(2)}) collective-permute-start(bf16[128,1280]{1,0:T(8,128)(2,1)} %get-tuple-element.42), channel_id=1, source_target_pairs={{0,4},{4,8},{8,12},{12,14},{14,10},{10,6},{6,2},{2,0},{1,5},{5,9},... | collective-permute-start | bytes 983048 | tf_op jit(solution)/shard_map/ppermute | solution.py:119
  137.1 7.9 %collective-permute-start.27 = (bf16[240,192]{1,0:T(8,128)(2,1)}, bf16[240,192]{1,0:T(8,128)(2,1)S(1)}, u32[]{:S(2)}, u32[]{:S(2)}) collective-permute-start(bf16[240,192]{1,0:T(8,128)(2,1)} %get-tuple-element.27), channel_id=1, source_target_pairs={{0,4},{4,8},{8,12},{12,14},{14,10},{10,6},{6,2},{2,0},{1,5},{5,9},... | collective-permute-start | bytes 276488 | tf_op jit(solution)/shard_map/ppermute | solution.py:176
  139.0 6.0 %collective-permute-start.34 = (bf16[240,192]{1,0:T(8,128)(2,1)}, bf16[240,192]{1,0:T(8,128)(2,1)}, u32[]{:S(2)}, u32[]{:S(2)}) collective-permute-start(bf16[240,192]{1,0:T(8,128)(2,1)} %get-tuple-element.28), channel_id=1, source_target_pairs={{0,2},{4,0},{8,4},{12,8},{14,12},{10,14},{6,10},{2,6},{1,3},{5,1},... | collective-permute-start | bytes 276488 | tf_op jit(solution)/shard_map/ppermute | solution.py:176
  146.3 5.6 %collective-permute-start.28 = (bf16[240,192]{1,0:T(8,128)(2,1)S(1)}, bf16[240,192]{1,0:T(8,128)(2,1)S(1)}, u32[]{:S(2)}, u32[]{:S(2)}) collective-permute-start(bf16[240,192]{1,0:T(8,128)(2,1)S(1)} %get-tuple-element.25), channel_id=1, source_target_pairs={{0,4},{4,8},{8,12},{12,14},{14,10},{10,6},{6,2},{2,0},{1,5},{5,9},... | collective-permute-start | bytes 276488 | tf_op jit(solution)/shard_map/ppermute | solution.py:176
  146.5 10.6 %copy-start.2 = (bf16[1024,768]{1,0:T(8,128)(2,1)S(1)}, bf16[1024,768]{1,0:T(8,128)(2,1)}, u32[]{:S(2)}) copy-start(bf16[1024,768]{1,0:T(8,128)(2,1)} %copy.50) | copy-start | bytes 4718596
  146.5 10.6 %copy-start.6 = (bf16[1024,512]{1,0:T(8,128)(2,1)S(1)}, bf16[1024,512]{1,0:T(8,128)(2,1)}, u32[]{:S(2)}) copy-start(bf16[1024,512]{1,0:T(8,128)(2,1)} %copy.49) | copy-start | bytes 3145732
  146.5 6.2 %collective-permute-start.35 = (bf16[240,192]{1,0:T(8,128)(2,1)S(1)}, bf16[240,192]{1,0:T(8,128)(2,1)S(1)}, u32[]{:S(2)}, u32[]{:S(2)}) collective-permute-start(bf16[240,192]{1,0:T(8,128)(2,1)S(1)} %get-tuple-element.26), channel_id=1, source_target_pairs={{0,2},{4,0},{8,4},{12,8},{14,12},{10,14},{6,10},{2,6},{1,3},{5,1},... | collective-permute-start | bytes 276488 | tf_op jit(solution)/shard_map/ppermute | solution.py:176
  149.8 7.1 %collective-permute-start.19 = (bf16[128,1280]{1,0:T(8,128)(2,1)S(1)}, bf16[128,1280]{1,0:T(8,128)(2,1)S(1)}, u32[]{:S(2)}, u32[]{:S(2)}) collective-permute-start(bf16[128,1280]{1,0:T(8,128)(2,1)S(1)} %get-tuple-element.40), channel_id=1, source_target_pairs={{0,4},{4,8},{8,12},{12,14},{14,10},{10,6},{6,2},{2,0},{1,5},{5,9},... | collective-permute-start | bytes 983048 | tf_op jit(solution)/shard_map/ppermute | solution.py:119
  150.0 7.1 %collective-permute-start.15 = (bf16[128,1280]{1,0:T(8,128)(2,1)S(1)}, bf16[128,1280]{1,0:T(8,128)(2,1)S(1)}, u32[]{:S(2)}, u32[]{:S(2)}) collective-permute-start(bf16[128,1280]{1,0:T(8,128)(2,1)S(1)} %get-tuple-element.39), channel_id=1, source_target_pairs={{0,2},{4,0},{8,4},{12,8},{14,12},{10,14},{6,10},{2,6},{1,3},{5,1},... | collective-permute-start | bytes 983048 | tf_op jit(solution)/shard_map/ppermute | solution.py:119
  (13 other events, 25.2 us)

commit v9 on v8

--- a/solution.py
+++ b/solution.py
@@ -178,6 +178,16 @@
         if t < count - 2:
             acc = acc.astype(wire_dtype)
     return acc
+
+
+def direct_reduce_scatter(select_block, axis, count):
+    index = lax.axis_index(axis)
+    total = select_block(index).astype(jnp.float32)
+    for shift in range(1, count):
+        perm = [(s, (s + shift) % count) for s in range(count)]
+        sent = select_block((index + shift) % count).astype(jnp.bfloat16)
+        total = total + lax.ppermute(sent, axis, perm).astype(jnp.float32)
+    return total
 
 
 def body(ring, queries, key_rows, value_rows, trunk_state, skip_input, norm_gain, conv_weight, cotangent):
@@ -252,15 +262,7 @@
                 full_weight, (index, dp_index, 0, column), (1, 1, rows_per, width)
             ).reshape(rows_per, width)
 
-        grad_weight = jnp.concatenate(
-            [
-                ring_reduce_scatter_sliced(weight_block(0, half_co), "seq", ring, True),
-                ring_reduce_scatter_sliced(
-                    weight_block(half_co, CO - half_co), "seq", ring, False
-                ),
-            ],
-            axis=1,
-        )
+        grad_weight = direct_reduce_scatter(weight_block(0, CO), "seq", seq_count)
     else:
         weight_part = (
             lax.dot_general(

time: 159 us -> 160 us (level)
  starting transfers between devices: 45.4 us -> 65.6 us
  waiting for transfers between devices: 44.8 us -> 33.2 us
  matrix products: 24.7 us -> 19 us
  other arithmetic: 18.3 us -> 14.4 us
  local copies, waits for them, and re-layouts: 24 us -> 26.2 us
    ppermute x14 -> x7, waiting for transfers between devices: 19.8 us -> 1.01 us  [direct_reduce_scatter(): total = total + lax.ppermute(sent, axis, perm).astype(jnp.float32)]
    ppermute x8, starting transfers between devices: 7.95 us -> 22 us  [ring_scatter_back(): received = lax.ppermute(acc, 'seq', perm).astype(jnp.float32)]
    ppermute x8, waiting for transfers between devices: 2.97 us -> 10.5 us  [ring_scatter_back(): received = lax.ppermute(acc, 'seq', perm).astype(jnp.float32)]
    ppermute x14 -> x7, starting transfers between devices: 16.7 us -> 22.7 us  [direct_reduce_scatter(): total = total + lax.ppermute(sent, axis, perm).astype(jnp.float32)]
    convert_element_type x6 -> x0, other arithmetic: 5.39 us -> none  [ring_reduce_scatter_sliced(): acc = acc.astype(wire_dtype)]
    dot_general x5, matrix products: 8.5 us -> 3.12 us  [body(): jnp.einsum('spc,spo->co', both_padded[:, offset:offset + positions], both...]
    convert_element_type x2, other arithmetic: 3.72 us -> 1.16 us  [ring_scatter_back(): add_part(chain[t - 2].astype(jnp.float32), received, side)]
    another operation x2, other arithmetic: 0.21 us -> 2.46 us
  transfers between devices with their start and end apart: 36 -> 29, of which waited for: 20 -> 13; matrix products, arithmetic and copies ran while one was open for 27% -> 13% of each run, Pallas kernels for 0% -> 0%
where the time goes in v9:
time: 160 us
  starting transfers between devices  65.6 us (41%)
  waiting for transfers between devices  33.2 us (21%)
  local copies, waits for them, and re-layouts  26.2 us (16%)
  matrix products  19 us (12%)
  other arithmetic  14.4 us (9%)
    ppermute x7, starting transfers between devices, direct_reduce_scatter(): total = total + lax.ppermute(sent, axis, perm).astype(jnp.float32)  22.7 us
    ppermute x8, starting transfers between devices, ring_scatter_back(): received = lax.ppermute(acc, 'seq', perm).astype(jnp.float32)  22 us
    ppermute x3, waiting for transfers between devices, ring_gather(): current = lax.ppermute(current, 'seq', forward)  12 us
    ppermute x8, waiting for transfers between devices, ring_scatter_back(): received = lax.ppermute(acc, 'seq', perm).astype(jnp.float32)  10.5 us
    unnamed x54, local copies, waits for them, and re-layouts  10.4 us
    ppermute x2, starting transfers between devices, extended(): before = lax.ppermute(last, axis, up)  8.38 us
    ppermute x3, starting transfers between devices, ring_gather(): current = lax.ppermute(current, 'seq', forward)  6.37 us
    ppermute x3, waiting for transfers between devices, ring_gather(): current = lax.ppermute(current, 'seq', backward)  4.77 us
  transfers between devices with their start and end apart: 29, of which 13 were waited for; matrix products, arithmetic and copies ran while one was open for 13% of the time, Pallas kernels for 0%

profile of v9, /device:TPU:0, one launch (start us, length us, event | category | flops | bytes accessed | tf_op | source)
XLA Modules:
  0.0 159.5 jit_solution(5766737787746896771)
XLA Ops:
  0.6 1.2 copy.37
  3.9 3.1 %collective-permute-start = (bf16[128,1280]{0,1:T(8,128)(2,1)}, bf16[128,1280]{0,1:T(8,128)(2,1)}, u32[]{:S(2)}, u32[]{:S(2)}) collective-permute-start(bf16[128,1280]{0,1:T(8,128)(2,1)} %get-tuple-element.45), channel_id=1, source_target_pairs={{0,4},{4,8},{8,12},{12,14},{14,10},{10,6},{6,2},{2,0},{1,5},{5,9},... | collective-permute-start | bytes 983048 | tf_op jit(solution)/shard_map/ppermute | solution.py:76
  8.7 6.2 %collective-permute-done = bf16[128,1280]{0,1:T(8,128)(2,1)} collective-permute-done((bf16[128,1280]{0,1:T(8,128)(2,1)}, bf16[128,1280]{0,1:T(8,128)(2,1)}, u32[]{:S(2)}, u32[]{:S(2)}) %collective-permute-start) | collective-permute-done | bytes 327712 | tf_op jit(solution)/shard_map/ppermute | solution.py:76
  14.9 1.8 %collective-permute-start.1 = (bf16[128,1280]{0,1:T(8,128)(2,1)}, bf16[128,1280]{0,1:T(8,128)(2,1)S(1)}, u32[]{:S(2)}, u32[]{:S(2)}) collective-permute-start(bf16[128,1280]{0,1:T(8,128)(2,1)} %collective-permute-done), channel_id=1, source_target_pairs={{0,4},{4,8},{8,12},{12,14},{14,10},{10,6},{6,2},{2,0},{1,5},{5,9},... | collective-permute-start | bytes 983048 | tf_op jit(solution)/shard_map/ppermute | solution.py:76
  16.9 1.2 fusion.59
  18.1 5.8 %collective-permute-done.1 = bf16[128,1280]{0,1:T(8,128)(2,1)S(1)} collective-permute-done((bf16[128,1280]{0,1:T(8,128)(2,1)}, bf16[128,1280]{0,1:T(8,128)(2,1)S(1)}, u32[]{:S(2)}, u32[]{:S(2)}) %collective-permute-start.1) | collective-permute-done | bytes 327712 | tf_op jit(solution)/shard_map/ppermute | solution.py:76
  24.0 1.5 collective-permute-start.2
  26.0 1.8 %constant_dynamic-update-slice_fusion.5 = bf16[1024,1280]{0,1:T(8,128)(2,1)} fusion(bf16[1024,1280]{0,1:T(8,128)(2,1)} %get-tuple-element.46, bf16[128,1280]{0,1:T(8,128)(2,1)} %collective-permute-done), kind=kLoop, calls=%fused_computation.160 | loop fusion | bytes 655360
  28.5 4.8 %collective-permute-done.5 = bf16[128,1280]{0,1:T(8,128)(2,1)S(1)} collective-permute-done((bf16[128,1280]{0,1:T(8,128)(2,1)S(1)}, bf16[128,1280]{0,1:T(8,128)(2,1)S(1)}, u32[]{:S(2)}, u32[]{:S(2)}) %collective-permute-start.5) | collective-permute-done | bytes 327712 | tf_op jit(solution)/shard_map/ppermute | solution.py:82
  33.9 1.6 collective-permute-start.6
  36.2 1.8 %constant_dynamic-update-slice_fusion.2 = bf16[1024,1280]{0,1:T(8,128)(2,1)} fusion(bf16[1024,1280]{0,1:T(8,128)(2,1)} %constant_dynamic-update-slice_fusion.3, bf16[128,1280]{0,1:T(8,128)(2,1)} %collective-permute-done.3), kind=kLoop, calls=%fused_computation.157 | loop fusion | bytes 655360
  40.4 1.5 slice.170
  41.9 1.9 %slice.171 = bf16[1024,512]{0,1:T(8,128)(2,1)S(1)} slice(bf16[1024,1280]{0,1:T(8,128)(2,1)} %maximum_dynamic-update-slice_fusion), slice={[0:1024], [0:512]} | slice | bytes 2097152 | tf_op jit(solution)/shard_map/slice | solution.py:201
  46.7 3.1 %collective-permute-start.8 = (bf16[2,768]{1,0:T(2,128)(2,1)S(1)}, bf16[2,768]{1,0:T(2,128)(2,1)S(1)}, u32[]{:S(2)}, u32[]{:S(2)}) collective-permute-start(bf16[2,768]{1,0:T(2,128)(2,1)S(1)} %get-tuple-element.44), channel_id=1, source_target_pairs={{0,2},{2,4},{4,6},{6,8},{8,10},{10,12},{12,14},{1,3},{3,5},{5,7},{... | collective-permute-start | bytes 9224 | tf_op jit(solution)/shard_map/ppermute | solution.py:24
  49.7 1.4 collective-permute-start.9
  51.5 3.8 %collective-permute-done.9 = bf16[2,768]{1,0:T(2,128)(2,1)S(1)} collective-permute-done((bf16[2,768]{1,0:T(2,128)(2,1)S(1)}, bf16[2,768]{1,0:T(2,128)(2,1)S(1)}, u32[]{:S(2)}, u32[]{:S(2)}) %collective-permute-start.9) | collective-permute-done | bytes 3104 | tf_op jit(solution)/shard_map/ppermute | solution.py:25
  55.6 2.0 %fusion.32 = (bf16[256,384]{1,0:T(8,128)(2,1)S(1)}, bf16[1,256,384]{2,1,0:T(8,128)(2,1)}) fusion(bf16[1,256,384]{2,1,0:T(8,128)(2,1)S(1)} %copy-done.21, bf16[256,3840]{1,0:T(8,128)(2,1)S(1)} %fusion.33, bf16[3840,384]{1,0:T(8,128)(2,1)S(1)} %copy-done), kind=kOutput, calls=%fused_computation.84 | convolution fusion | flops 756252672 | bytes 5505024 | tf_op jit(solution)/shard_map/dot_general | solution.py:230
  57.6 1.3 collective-permute-start.10
  58.9 5.3 %collective-permute-start.11 = (bf16[2,384]{1,0:T(2,128)(2,1)S(1)}, bf16[2,384]{1,0:T(2,128)(2,1)S(1)}, u32[]{:S(2)}, u32[]{:S(2)}) collective-permute-start(bf16[2,384]{1,0:T(2,128)(2,1)S(1)} %get-tuple-element.47), channel_id=1, source_target_pairs={{0,2},{2,4},{4,6},{6,8},{8,10},{10,12},{12,14},{1,3},{3,5},{5,7},{... | collective-permute-start | bytes 4616 | tf_op jit(solution)/shard_map/ppermute | solution.py:24
  65.6 1.1 multiply_reduce_fusion
  67.7 1.1 convolution_convert_fusion.1
  68.9 1.7 %copy.41 = bf16[128,768]{0,1:T(8,128)(2,1)} copy(bf16[128,768]{1,0:T(8,128)(2,1)} %convolution_convert_fusion.1) | data formatting | bytes 393216 | tf_op jit(solution)/shard_map/convert_element_type | solution.py:305
  70.6 1.2 multiply_reduce_fusion.2
  71.8 3.6 %convolution_convert_fusion = bf16[4,192,1024]{2,1,0:T(8,128)(2,1)} fusion(bf16[128,4,192]{0,2,1:T(8,128)(2,1)} %bitcast.162, f32[4,1024,128]{2,1,0:T(8,128)} %copy-done.3, f32[4,128]{1,0:T(4,128)S(1)} %log_add_fusion), kind=kOutput, calls=%fused_computation.24 | convolution fusion | flops 203685888 | bytes 3868672 | tf_op jit(solution)/shard_map/hij,ihd->jhd/dot_general | solution.py:320
  75.4 2.1 %multiply_convert_fusion.1 = bf16[4,128,1024]{1,2,0:T(8,128)(2,1)} fusion(f32[4,1024,128]{2,1,0:T(8,128)S(1)} %copy-done.4, bf16[128,4,192]{0,2,1:T(8,128)(2,1)S(1)} %bitcast.163, bf16[1024,4,192]{0,2,1:T(8,128)(2,1)S(1)} %bitcast.149, f32[4,128]{1,0:T(4,128)S(1)} %bitcast.171, f32[4,128]{1,0:T(4,128)S(1)} %log_add_fusion), kind=kOutput, calls=%fused_computation.22 | convolution fusion | flops 203948032 | bytes 4919296 | tf_op jit(solution)/shard_map/ihd,jhd->hij/dot_general | solution.py:308
  77.5 2.6 %copy.50 = bf16[1024,768]{1,0:T(8,128)(2,1)} copy(bf16[1024,768]{0,1:T(8,128)(2,1)} %bitcast.154) | data formatting | bytes 3145728 | tf_op jit(solution)/shard_map/reshape | solution.py:324
  80.1 2.7 %fusion.9 = bf16[1024,4,128]{2,0,1:T(8,128)(2,1)} fusion(bf16[4,128,1024]{1,2,0:T(8,128)(2,1)} %multiply_convert_fusion.1, bf16[128,4,128]{0,2,1:T(8,128)(2,1)} %bitcast.166), kind=kOutput, calls=%fused_computation.35 | convolution fusion | flops 135266304 | bytes 2228224 | tf_op jit(solution)/shard_map/hij,ihd->jhd/dot_general | solution.py:317
  82.8 2.3 %copy.47 = bf16[1024,4,128]{0,2,1:T(8,128)(2,1)} copy(bf16[1024,4,128]{2,0,1:T(8,128)(2,1)} %fusion.9) | data formatting | bytes 2097152 | tf_op jit(solution)/shard_map/mul | solution.py:317
  85.1 2.3 %copy.49 = bf16[1024,512]{1,0:T(8,128)(2,1)} copy(bf16[1024,512]{0,1:T(8,128)(2,1)} %bitcast.160) | data formatting | bytes 2097152 | tf_op jit(solution)/shard_map/reshape | solution.py:323
  87.5 1.9 %fusion.69 = (bf16[128,640]{1,0:T(8,128)(2,1)}, bf16[128,640]{1,0:T(8,128)(2,1)}, bf16[128,640]{1,0:T(8,128)(2,1)}) fusion(bf16[1024,768]{1,0:T(8,128)(2,1)} %copy.50, bf16[1024,512]{1,0:T(8,128)(2,1)} %copy.49), kind=kLoop, calls=%fused_computation.149 | loop fusion | flops 327680 | bytes 3440640 | tf_op jit(solution)/shard_map/concatenate | solution.py:321
  89.3 2.9 %collective-permute-start.12 = (bf16[128,640]{1,0:T(8,128)(2,1)}, bf16[128,640]{1,0:T(8,128)(2,1)}, u32[]{:S(2)}, u32[]{:S(2)}) collective-permute-start(bf16[128,640]{1,0:T(8,128)(2,1)} %get-tuple-element.36), channel_id=1, source_target_pairs={{0,2},{4,0},{8,4},{12,8},{14,12},{10,14},{6,10},{2,6},{1,3},{5,1},... | collective-permute-start | bytes 491528 | tf_op jit(solution)/shard_map/ppermute | solution.py:119
  92.2 1.7 %collective-permute-start.16 = (bf16[128,640]{1,0:T(8,128)(2,1)}, bf16[128,640]{1,0:T(8,128)(2,1)}, u32[]{:S(2)}, u32[]{:S(2)}) collective-permute-start(bf16[128,640]{1,0:T(8,128)(2,1)} %get-tuple-element.37), channel_id=1, source_target_pairs={{0,4},{4,8},{8,12},{12,14},{14,10},{10,6},{6,2},{2,0},{1,5},{5,9},... | collective-permute-start | bytes 491528 | tf_op jit(solution)/shard_map/ppermute | solution.py:119
  94.7 2.9 %collective-permute-done.12 = bf16[128,640]{1,0:T(8,128)(2,1)} collective-permute-done((bf16[128,640]{1,0:T(8,128)(2,1)}, bf16[128,640]{1,0:T(8,128)(2,1)}, u32[]{:S(2)}, u32[]{:S(2)}) %collective-permute-start.12) | collective-permute-done | bytes 163872 | tf_op jit(solution)/shard_map/ppermute | solution.py:119
  97.9 1.2 add_convert_fusion.6
  99.2 1.6 %collective-permute-start.13 = (bf16[128,1280]{1,0:T(8,128)(2,1)S(1)}, bf16[128,1280]{1,0:T(8,128)(2,1)S(1)}, u32[]{:S(2)}, u32[]{:S(2)}) collective-permute-start(bf16[128,1280]{1,0:T(8,128)(2,1)S(1)} %pad_maximum_fusion.7), channel_id=1, source_target_pairs={{0,2},{4,0},{8,4},{12,8},{14,12},{10,14},{6,10},{2,6},{1,3},{5,1},... | collective-permute-start | bytes 983048 | tf_op jit(solution)/shard_map/ppermute | solution.py:119
  104.6 1.8 %collective-permute-done.13 = bf16[128,1280]{1,0:T(8,128)(2,1)S(1)} collective-permute-done((bf16[128,1280]{1,0:T(8,128)(2,1)S(1)}, bf16[128,1280]{1,0:T(8,128)(2,1)S(1)}, u32[]{:S(2)}, u32[]{:S(2)}) %collective-permute-start.13) | collective-permute-done | bytes 327712 | tf_op jit(solution)/shard_map/ppermute | solution.py:119
  106.5 3.3 %collective-permute-done.17 = bf16[128,1280]{1,0:T(8,128)(2,1)S(1)} collective-permute-done((bf16[128,1280]{1,0:T(8,128)(2,1)S(1)}, bf16[128,1280]{1,0:T(8,128)(2,1)S(1)}, u32[]{:S(2)}, u32[]{:S(2)}) %collective-permute-start.17) | collective-permute-done | bytes 327712 | tf_op jit(solution)/shard_map/ppermute | solution.py:119
  113.5 3.9 %collective-permute-start.28 = (bf16[240,384]{1,0:T(8,128)(2,1)S(1)}, bf16[240,384]{1,0:T(8,128)(2,1)S(1)}, u32[]{:S(2)}, u32[]{:S(2)}) collective-permute-start(bf16[240,384]{1,0:T(8,128)(2,1)S(1)} %get-tuple-element.24), channel_id=1, source_target_pairs={{0,14},{2,0},{4,2},{6,4},{8,6},{10,8},{12,10},{14,12},{1,15},{3,1}... | collective-permute-start | bytes 552968 | tf_op jit(solution)/shard_map/ppermute | solution.py:189
  117.4 1.7 %collective-permute-start.27 = (bf16[240,384]{1,0:T(8,128)(2,1)S(1)}, bf16[240,384]{1,0:T(8,128)(2,1)S(1)}, u32[]{:S(2)}, u32[]{:S(2)}) collective-permute-start(bf16[240,384]{1,0:T(8,128)(2,1)S(1)} %get-tuple-element.25), channel_id=1, source_target_pairs={{0,12},{2,14},{4,0},{6,2},{8,4},{10,6},{12,8},{14,10},{1,13},{3,15... | collective-permute-start | bytes 552968 | tf_op jit(solution)/shard_map/ppermute | solution.py:189
  119.3 2.3 %collective-permute-start.25 = (bf16[240,384]{1,0:T(8,128)(2,1)S(1)}, bf16[240,384]{1,0:T(8,128)(2,1)S(1)}, u32[]{:S(2)}, u32[]{:S(2)}) collective-permute-start(bf16[240,384]{1,0:T(8,128)(2,1)S(1)} %get-tuple-element.27), channel_id=1, source_target_pairs={{0,8},{2,10},{4,12},{6,14},{8,0},{10,2},{12,4},{14,6},{1,9},{3,11}... | collective-permute-start | bytes 552968 | tf_op jit(solution)/shard_map/ppermute | solution.py:189
  121.6 10.5 %collective-permute-start.24 = (bf16[240,384]{1,0:T(8,128)(2,1)}, bf16[240,384]{1,0:T(8,128)(2,1)}, u32[]{:S(2)}, u32[]{:S(2)}) collective-permute-start(bf16[240,384]{1,0:T(8,128)(2,1)} %get-tuple-element.28), channel_id=1, source_target_pairs={{0,6},{2,8},{4,10},{6,12},{8,14},{10,0},{12,2},{14,4},{1,7},{3,9},... | collective-permute-start | bytes 552968 | tf_op jit(solution)/shard_map/ppermute | solution.py:189
  133.1 2.5 %collective-permute-start.23 = (bf16[240,384]{1,0:T(8,128)(2,1)}, bf16[240,384]{1,0:T(8,128)(2,1)S(1)}, u32[]{:S(2)}, u32[]{:S(2)}) collective-permute-start(bf16[240,384]{1,0:T(8,128)(2,1)} %get-tuple-element.29), channel_id=1, source_target_pairs={{0,4},{2,6},{4,8},{6,10},{8,12},{10,14},{12,0},{14,2},{1,5},{3,7},... | collective-permute-start | bytes 552968 | tf_op jit(solution)/shard_map/ppermute | solution.py:189
  135.7 1.8 %collective-permute-start.22 = (bf16[240,384]{1,0:T(8,128)(2,1)S(1)}, bf16[240,384]{1,0:T(8,128)(2,1)}, u32[]{:S(2)}, u32[]{:S(2)}) collective-permute-start(bf16[240,384]{1,0:T(8,128)(2,1)S(1)} %get-tuple-element.23), channel_id=1, source_target_pairs={{0,2},{2,4},{4,6},{6,8},{8,10},{10,12},{12,14},{14,0},{1,3},{3,5},... | collective-permute-start | bytes 552968 | tf_op jit(solution)/shard_map/ppermute | solution.py:189
  137.4 11.5 %collective-permute-start.19 = (bf16[128,1280]{1,0:T(8,128)(2,1)}, bf16[128,1280]{1,0:T(8,128)(2,1)}, u32[]{:S(2)}, u32[]{:S(2)}) collective-permute-start(bf16[128,1280]{1,0:T(8,128)(2,1)} %get-tuple-element.31), channel_id=1, source_target_pairs={{0,4},{4,8},{8,12},{12,14},{14,10},{10,6},{6,2},{2,0},{1,5},{5,9},... | collective-permute-start | bytes 983048 | tf_op jit(solution)/shard_map/ppermute | solution.py:119
  149.6 1.4 collective-permute-start.15
  152.6 2.4 %fusion.40 = f32[240,384]{1,0:T(8,128)} fusion(bf16[240,384]{1,0:T(8,128)(2,1)} %copy-done.17, bf16[240,384]{1,0:T(8,128)(2,1)} %copy-done.18, bf16[240,384]{1,0:T(8,128)(2,1)} %copy-done.19, bf16[240,384]{1,0:T(8,128)(2,1)} %copy-done.20, bf16[240,384]{1,0:T(8,128)(2,1)} %collective-permute-done.24, bf16[240,384]{1,0:T(8,128)(2,1)S(1)} %collective-permute-done.23, ...), kind=kLoop, calls=%fused_computation.100 | loop fusion | flops 1290240 | bytes 2027528 | tf_op jit(solution)/shard_map/add | solution.py:189
  155.1 1.9 %collective-permute-done.15 = bf16[128,1280]{1,0:T(8,128)(2,1)} collective-permute-done((bf16[128,1280]{1,0:T(8,128)(2,1)}, bf16[128,1280]{1,0:T(8,128)(2,1)}, u32[]{:S(2)}, u32[]{:S(2)}) %collective-permute-start.15) | collective-permute-done | bytes 327712 | tf_op jit(solution)/shard_map/ppermute | solution.py:119
  157.0 1.2 add_convert_fusion
  (124 shorter events, 28.0 us)
Async XLA Ops:
  0.6 54.9 %copy-start = (bf16[3840,384]{1,0:T(8,128)(2,1)S(1)}, bf16[3840,384]{1,0:T(8,128)(2,1)}, u32[]{:S(2)}) copy-start(bf16[3840,384]{1,0:T(8,128)(2,1)} %param.14) | copy-start | bytes 8847364
  3.9 11.0 %collective-permute-start = (bf16[128,1280]{0,1:T(8,128)(2,1)}, bf16[128,1280]{0,1:T(8,128)(2,1)}, u32[]{:S(2)}, u32[]{:S(2)}) collective-permute-start(bf16[128,1280]{0,1:T(8,128)(2,1)} %get-tuple-element.45), channel_id=1, source_target_pairs={{0,4},{4,8},{8,12},{12,14},{14,10},{10,6},{6,2},{2,0},{1,5},{5,9},... | collective-permute-start | bytes 983048 | tf_op jit(solution)/shard_map/ppermute | solution.py:76
  6.9 9.8 %collective-permute-start.3 = (bf16[128,1280]{0,1:T(8,128)(2,1)}, bf16[128,1280]{0,1:T(8,128)(2,1)}, u32[]{:S(2)}, u32[]{:S(2)}) collective-permute-start(bf16[128,1280]{0,1:T(8,128)(2,1)} %get-tuple-element.45), channel_id=1, source_target_pairs={{0,2},{4,0},{8,4},{12,8},{14,12},{10,14},{6,10},{2,6},{1,3},{5,1},... | collective-permute-start | bytes 983048 | tf_op jit(solution)/shard_map/ppermute | solution.py:82
  7.9 35.9 %copy-start.14 = (bf16[1,128,512]{1,2,0:T(8,128)(2,1)}, bf16[1,128,512]{1,2,0:T(8,128)(2,1)S(1)}, u32[]{:S(2)}) copy-start(bf16[1,128,512]{1,2,0:T(8,128)(2,1)S(1)} %copy.72) | copy-start | bytes 393220
  14.9 9.1 %collective-permute-start.1 = (bf16[128,1280]{0,1:T(8,128)(2,1)}, bf16[128,1280]{0,1:T(8,128)(2,1)S(1)}, u32[]{:S(2)}, u32[]{:S(2)}) collective-permute-start(bf16[128,1280]{0,1:T(8,128)(2,1)} %collective-permute-done), channel_id=1, source_target_pairs={{0,4},{4,8},{8,12},{12,14},{14,10},{10,6},{6,2},{2,0},{1,5},{5,9},... | collective-permute-start | bytes 983048 | tf_op jit(solution)/shard_map/ppermute | solution.py:76
  16.7 8.8 %collective-permute-start.4 = (bf16[128,1280]{0,1:T(8,128)(2,1)}, bf16[128,1280]{0,1:T(8,128)(2,1)S(1)}, u32[]{:S(2)}, u32[]{:S(2)}) collective-permute-start(bf16[128,1280]{0,1:T(8,128)(2,1)} %collective-permute-done.3), channel_id=1, source_target_pairs={{0,2},{4,0},{8,4},{12,8},{14,12},{10,14},{6,10},{2,6},{1,3},{5,1},... | collective-permute-start | bytes 983048 | tf_op jit(solution)/shard_map/ppermute | solution.py:82
  24.0 9.9 %collective-permute-start.2 = (bf16[128,1280]{0,1:T(8,128)(2,1)S(1)}, bf16[128,1280]{0,1:T(8,128)(2,1)S(1)}, u32[]{:S(2)}, u32[]{:S(2)}) collective-permute-start(bf16[128,1280]{0,1:T(8,128)(2,1)S(1)} %collective-permute-done.1), channel_id=1, source_target_pairs={{0,4},{4,8},{8,12},{12,14},{14,10},{10,6},{6,2},{2,0},{1,5},{5,9},... | collective-permute-start | bytes 983048 | tf_op jit(solution)/shard_map/ppermute | solution.py:76
  25.5 7.8 %collective-permute-start.5 = (bf16[128,1280]{0,1:T(8,128)(2,1)S(1)}, bf16[128,1280]{0,1:T(8,128)(2,1)S(1)}, u32[]{:S(2)}, u32[]{:S(2)}) collective-permute-start(bf16[128,1280]{0,1:T(8,128)(2,1)S(1)} %collective-permute-done.4), channel_id=1, source_target_pairs={{0,2},{4,0},{8,4},{12,8},{14,12},{10,14},{6,10},{2,6},{1,3},{5,1},... | collective-permute-start | bytes 983048 | tf_op jit(solution)/shard_map/ppermute | solution.py:82
  33.3 6.2 %collective-permute-start.7 = (bf16[128,640]{0,1:T(8,128)(2,1)S(1)}, bf16[128,640]{0,1:T(8,128)(2,1)S(1)}, u32[]{:S(2)}, u32[]{:S(2)}) collective-permute-start(bf16[128,640]{0,1:T(8,128)(2,1)S(1)} %slice.169), channel_id=1, source_target_pairs={{0,2},{4,0},{8,4},{12,8},{14,12},{10,14},{6,10},{2,6},{1,3},{5,1},... | collective-permute-start | bytes 491528 | tf_op jit(solution)/shard_map/ppermute | solution.py:85
  33.9 5.7 %collective-permute-start.6 = (bf16[128,640]{0,1:T(8,128)(2,1)S(1)}, bf16[128,640]{0,1:T(8,128)(2,1)S(1)}, u32[]{:S(2)}, u32[]{:S(2)}) collective-permute-start(bf16[128,640]{0,1:T(8,128)(2,1)S(1)} %slice.168), channel_id=1, source_target_pairs={{0,4},{4,8},{8,12},{12,14},{14,10},{10,6},{6,2},{2,0},{1,5},{5,9},... | collective-permute-start | bytes 491528 | tf_op jit(solution)/shard_map/ppermute | solution.py:79
  41.9 2.9 %copy-start.6 = (bf16[1024,768]{0,1:T(8,128)(2,1)}, bf16[1024,768]{0,1:T(8,128)(2,1)S(1)}, u32[]{:S(2)}) copy-start(bf16[1024,768]{0,1:T(8,128)(2,1)S(1)} %slice.170) | copy-start | bytes 4718596
  44.4 1.3 copy-start.3
  46.7 4.5 %collective-permute-start.8 = (bf16[2,768]{1,0:T(2,128)(2,1)S(1)}, bf16[2,768]{1,0:T(2,128)(2,1)S(1)}, u32[]{:S(2)}, u32[]{:S(2)}) collective-permute-start(bf16[2,768]{1,0:T(2,128)(2,1)S(1)} %get-tuple-element.44), channel_id=1, source_target_pairs={{0,2},{2,4},{4,6},{6,8},{8,10},{10,12},{12,14},{1,3},{3,5},{5,7},{... | collective-permute-start | bytes 9224 | tf_op jit(solution)/shard_map/ppermute | solution.py:24
  49.7 5.9 %copy-start.21 = (bf16[1,256,384]{2,1,0:T(8,128)(2,1)S(1)}, bf16[1,256,384]{2,1,0:T(8,128)(2,1)}, u32[]{:S(2)}) copy-start(bf16[1,256,384]{2,1,0:T(8,128)(2,1)} %param.15) | copy-start | bytes 589828
  49.7 5.6 %collective-permute-start.9 = (bf16[2,768]{1,0:T(2,128)(2,1)S(1)}, bf16[2,768]{1,0:T(2,128)(2,1)S(1)}, u32[]{:S(2)}, u32[]{:S(2)}) collective-permute-start(bf16[2,768]{1,0:T(2,128)(2,1)S(1)} %get-tuple-element.43), channel_id=1, source_target_pairs={{2,0},{4,2},{6,4},{8,6},{10,8},{12,10},{14,12},{3,1},{5,3},{7,5},{... | collective-permute-start | bytes 9224 | tf_op jit(solution)/shard_map/ppermute | solution.py:25
  57.6 6.6 %collective-permute-start.10 = (bf16[2,384]{1,0:T(2,128)(2,1)S(1)}, bf16[2,384]{1,0:T(2,128)(2,1)S(1)}, u32[]{:S(2)}, u32[]{:S(2)}) collective-permute-start(bf16[2,384]{1,0:T(2,128)(2,1)S(1)} %get-tuple-element.48), channel_id=1, source_target_pairs={{2,0},{4,2},{6,4},{8,6},{10,8},{12,10},{14,12},{3,1},{5,3},{7,5},{... | collective-permute-start | bytes 4616 | tf_op jit(solution)/shard_map/ppermute | solution.py:25
  58.9 6.6 %collective-permute-start.11 = (bf16[2,384]{1,0:T(2,128)(2,1)S(1)}, bf16[2,384]{1,0:T(2,128)(2,1)S(1)}, u32[]{:S(2)}, u32[]{:S(2)}) collective-permute-start(bf16[2,384]{1,0:T(2,128)(2,1)S(1)} %get-tuple-element.47), channel_id=1, source_target_pairs={{0,2},{2,4},{4,6},{6,8},{8,10},{10,12},{12,14},{1,3},{3,5},{5,7},{... | collective-permute-start | bytes 4616 | tf_op jit(solution)/shard_map/ppermute | solution.py:24
  70.6 4.8 %copy-start.4 = (f32[4,1024,128]{2,1,0:T(8,128)S(1)}, f32[4,1024,128]{2,1,0:T(8,128)}, u32[]{:S(2)}) copy-start(f32[4,1024,128]{2,1,0:T(8,128)} %copy-done.3) | copy-start | bytes 6291460
  70.6 4.8 %copy-start.7 = (bf16[1024,768]{0,1:T(8,128)(2,1)S(1)}, bf16[1024,768]{0,1:T(8,128)(2,1)}, u32[]{:S(2)}) copy-start(bf16[1024,768]{0,1:T(8,128)(2,1)} %copy-done.6) | copy-start | bytes 4718596
  70.6 4.8 %copy-start.12 = (bf16[128,768]{0,1:T(8,128)(2,1)S(1)}, bf16[128,768]{0,1:T(8,128)(2,1)}, u32[]{:S(2)}) copy-start(bf16[128,768]{0,1:T(8,128)(2,1)} %copy.41) | copy-start | bytes 589828
  89.3 8.2 %collective-permute-start.12 = (bf16[128,640]{1,0:T(8,128)(2,1)}, bf16[128,640]{1,0:T(8,128)(2,1)}, u32[]{:S(2)}, u32[]{:S(2)}) collective-permute-start(bf16[128,640]{1,0:T(8,128)(2,1)} %get-tuple-element.36), channel_id=1, source_target_pairs={{0,2},{4,0},{8,4},{12,8},{14,12},{10,14},{6,10},{2,6},{1,3},{5,1},... | collective-permute-start | bytes 491528 | tf_op jit(solution)/shard_map/ppermute | solution.py:119
  92.2 5.6 %collective-permute-start.16 = (bf16[128,640]{1,0:T(8,128)(2,1)}, bf16[128,640]{1,0:T(8,128)(2,1)}, u32[]{:S(2)}, u32[]{:S(2)}) collective-permute-start(bf16[128,640]{1,0:T(8,128)(2,1)} %get-tuple-element.37), channel_id=1, source_target_pairs={{0,4},{4,8},{8,12},{12,14},{14,10},{10,6},{6,2},{2,0},{1,5},{5,9},... | collective-permute-start | bytes 491528 | tf_op jit(solution)/shard_map/ppermute | solution.py:119
  93.9 5.2 %copy-start.15 = (bf16[128,640]{1,0:T(8,128)(2,1)S(1)}, bf16[128,640]{1,0:T(8,128)(2,1)}, u32[]{:S(2)}) copy-start(bf16[128,640]{1,0:T(8,128)(2,1)} %get-tuple-element.38) | copy-start | bytes 491524
  94.0 7.6 %collective-permute-start.21 = (bf16[256,384]{1,0:T(8,128)(2,1)S(1)}, bf16[256,384]{1,0:T(8,128)(2,1)S(1)}, u32[]{:S(2)}, u32[]{:S(2)}) collective-permute-start(bf16[256,384]{1,0:T(8,128)(2,1)S(1)} %get-tuple-element.41), channel_id=1, source_target_pairs={{0,1},{1,0},{2,3},{3,2},{4,5},{5,4},{6,7},{7,6},{8,9},{9,8},{10,11... | collective-permute-start | bytes 589832 | tf_op jit(solution)/shard_map/ppermute | solution.py:242
  94.1 6.7 %copy-start.1 = (bf16[1024,768]{1,0:T(8,128)(2,1)S(1)}, bf16[1024,768]{1,0:T(8,128)(2,1)}, u32[]{:S(2)}) copy-start(bf16[1024,768]{1,0:T(8,128)(2,1)} %copy.50) | copy-start | bytes 4718596
  94.1 6.7 %copy-start.5 = (bf16[1024,512]{1,0:T(8,128)(2,1)S(1)}, bf16[1024,512]{1,0:T(8,128)(2,1)}, u32[]{:S(2)}) copy-start(bf16[1024,512]{1,0:T(8,128)(2,1)} %copy.49) | copy-start | bytes 3145732
  94.1 7.4 %collective-permute-start.20 = (bf16[260,768]{1,0:T(8,128)(2,1)S(1)}, bf16[260,768]{1,0:T(8,128)(2,1)S(1)}, u32[]{:S(2)}, u32[]{:S(2)}) collective-permute-start(bf16[260,768]{1,0:T(8,128)(2,1)S(1)} %get-tuple-element.39), channel_id=1, source_target_pairs={{0,1},{1,0},{2,3},{3,2},{4,5},{5,4},{6,7},{7,6},{8,9},{9,8},{10,11... | collective-permute-start | bytes 1198088 | tf_op jit(solution)/shard_map/ppermute | solution.py:241
  99.2 7.3 %collective-permute-start.13 = (bf16[128,1280]{1,0:T(8,128)(2,1)S(1)}, bf16[128,1280]{1,0:T(8,128)(2,1)S(1)}, u32[]{:S(2)}, u32[]{:S(2)}) collective-permute-start(bf16[128,1280]{1,0:T(8,128)(2,1)S(1)} %pad_maximum_fusion.7), channel_id=1, source_target_pairs={{0,2},{4,0},{8,4},{12,8},{14,12},{10,14},{6,10},{2,6},{1,3},{5,1},... | collective-permute-start | bytes 983048 | tf_op jit(solution)/shard_map/ppermute | solution.py:119
  100.8 8.9 %collective-permute-start.17 = (bf16[128,1280]{1,0:T(8,128)(2,1)S(1)}, bf16[128,1280]{1,0:T(8,128)(2,1)S(1)}, u32[]{:S(2)}, u32[]{:S(2)}) collective-permute-start(bf16[128,1280]{1,0:T(8,128)(2,1)S(1)} %fusion.47), channel_id=1, source_target_pairs={{0,4},{4,8},{8,12},{12,14},{14,10},{10,6},{6,2},{2,0},{1,5},{5,9},... | collective-permute-start | bytes 983048 | tf_op jit(solution)/shard_map/ppermute | solution.py:119
  109.9 9.4 %collective-permute-start.14 = (bf16[128,1280]{1,0:T(8,128)(2,1)S(1)}, bf16[128,1280]{1,0:T(8,128)(2,1)S(1)}, u32[]{:S(2)}, u32[]{:S(2)}) collective-permute-start(bf16[128,1280]{1,0:T(8,128)(2,1)S(1)} %get-tuple-element.32), channel_id=1, source_target_pairs={{0,2},{4,0},{8,4},{12,8},{14,12},{10,14},{6,10},{2,6},{1,3},{5,1},... | collective-permute-start | bytes 983048 | tf_op jit(solution)/shard_map/ppermute | solution.py:119
  110.9 10.7 %collective-permute-start.18 = (bf16[128,1280]{1,0:T(8,128)(2,1)S(1)}, bf16[128,1280]{1,0:T(8,128)(2,1)S(1)}, u32[]{:S(2)}, u32[]{:S(2)}) collective-permute-start(bf16[128,1280]{1,0:T(8,128)(2,1)S(1)} %get-tuple-element.33), channel_id=1, source_target_pairs={{0,4},{4,8},{8,12},{12,14},{14,10},{10,6},{6,2},{2,0},{1,5},{5,9},... | collective-permute-start | bytes 983048 | tf_op jit(solution)/shard_map/ppermute | solution.py:119
  112.4 20.7 %copy-start.8 = (f32[3840,384]{1,0:T(8,128)}, f32[3840,384]{1,0:T(8,128)S(1)}, u32[]{:S(2)}) copy-start(f32[3840,384]{1,0:T(8,128)S(1)} %broadcast_multiply_fusion) | copy-start | bytes 17694724
  113.5 37.6 %copy-start.10 = (bf16[1024,512]{0,1:T(8,128)(2,1)S(1)}, bf16[1024,512]{0,1:T(8,128)(2,1)}, u32[]{:S(2)}) copy-start(bf16[1024,512]{0,1:T(8,128)(2,1)} %copy-done.9) | copy-start | bytes 3145732
  113.5 37.6 %copy-start.11 = (bf16[4,128,1024]{1,2,0:T(8,128)(2,1)S(1)}, bf16[4,128,1024]{1,2,0:T(8,128)(2,1)}, u32[]{:S(2)}) copy-start(bf16[4,128,1024]{1,2,0:T(8,128)(2,1)} %multiply_convert_fusion.1) | copy-start | bytes 3145732
  113.5 19.6 %collective-permute-start.28 = (bf16[240,384]{1,0:T(8,128)(2,1)S(1)}, bf16[240,384]{1,0:T(8,128)(2,1)S(1)}, u32[]{:S(2)}, u32[]{:S(2)}) collective-permute-start(bf16[240,384]{1,0:T(8,128)(2,1)S(1)} %get-tuple-element.24), channel_id=1, source_target_pairs={{0,14},{2,0},{4,2},{6,4},{8,6},{10,8},{12,10},{14,12},{1,15},{3,1}... | collective-permute-start | bytes 552968 | tf_op jit(solution)/shard_map/ppermute | solution.py:189
  117.4 18.3 %collective-permute-start.27 = (bf16[240,384]{1,0:T(8,128)(2,1)S(1)}, bf16[240,384]{1,0:T(8,128)(2,1)S(1)}, u32[]{:S(2)}, u32[]{:S(2)}) collective-permute-start(bf16[240,384]{1,0:T(8,128)(2,1)S(1)} %get-tuple-element.25), channel_id=1, source_target_pairs={{0,12},{2,14},{4,0},{6,2},{8,4},{10,6},{12,8},{14,10},{1,13},{3,15... | collective-permute-start | bytes 552968 | tf_op jit(solution)/shard_map/ppermute | solution.py:189
  119.0 18.4 %collective-permute-start.26 = (bf16[240,384]{1,0:T(8,128)(2,1)S(1)}, bf16[240,384]{1,0:T(8,128)(2,1)S(1)}, u32[]{:S(2)}, u32[]{:S(2)}) collective-permute-start(bf16[240,384]{1,0:T(8,128)(2,1)S(1)} %get-tuple-element.26), channel_id=1, source_target_pairs={{0,10},{2,12},{4,14},{6,0},{8,2},{10,4},{12,6},{14,8},{1,11},{3,13... | collective-permute-start | bytes 552968 | tf_op jit(solution)/shard_map/ppermute | solution.py:189
  119.3 30.3 %collective-permute-start.25 = (bf16[240,384]{1,0:T(8,128)(2,1)S(1)}, bf16[240,384]{1,0:T(8,128)(2,1)S(1)}, u32[]{:S(2)}, u32[]{:S(2)}) collective-permute-start(bf16[240,384]{1,0:T(8,128)(2,1)S(1)} %get-tuple-element.27), channel_id=1, source_target_pairs={{0,8},{2,10},{4,12},{6,14},{8,0},{10,2},{12,4},{14,6},{1,9},{3,11}... | collective-permute-start | bytes 552968 | tf_op jit(solution)/shard_map/ppermute | solution.py:189
  121.6 31.0 %collective-permute-start.24 = (bf16[240,384]{1,0:T(8,128)(2,1)}, bf16[240,384]{1,0:T(8,128)(2,1)}, u32[]{:S(2)}, u32[]{:S(2)}) collective-permute-start(bf16[240,384]{1,0:T(8,128)(2,1)} %get-tuple-element.28), channel_id=1, source_target_pairs={{0,6},{2,8},{4,10},{6,12},{8,14},{10,0},{12,2},{14,4},{1,7},{3,9},... | collective-permute-start | bytes 552968 | tf_op jit(solution)/shard_map/ppermute | solution.py:189
  133.1 18.3 %copy-start.17 = (bf16[240,384]{1,0:T(8,128)(2,1)}, bf16[240,384]{1,0:T(8,128)(2,1)S(1)}, u32[]{:S(2)}) copy-start(bf16[240,384]{1,0:T(8,128)(2,1)S(1)} %collective-permute-done.28) | copy-start | bytes 552964
  133.1 19.5 %collective-permute-start.23 = (bf16[240,384]{1,0:T(8,128)(2,1)}, bf16[240,384]{1,0:T(8,128)(2,1)S(1)}, u32[]{:S(2)}, u32[]{:S(2)}) collective-permute-start(bf16[240,384]{1,0:T(8,128)(2,1)} %get-tuple-element.29), channel_id=1, source_target_pairs={{0,4},{2,6},{4,8},{6,10},{8,12},{10,14},{12,0},{14,2},{1,5},{3,7},... | collective-permute-start | bytes 552968 | tf_op jit(solution)/shard_map/ppermute | solution.py:189
  135.7 15.8 %copy-start.18 = (bf16[240,384]{1,0:T(8,128)(2,1)}, bf16[240,384]{1,0:T(8,128)(2,1)S(1)}, u32[]{:S(2)}) copy-start(bf16[240,384]{1,0:T(8,128)(2,1)S(1)} %collective-permute-done.27) | copy-start | bytes 552964
  135.7 17.0 %collective-permute-start.22 = (bf16[240,384]{1,0:T(8,128)(2,1)S(1)}, bf16[240,384]{1,0:T(8,128)(2,1)}, u32[]{:S(2)}, u32[]{:S(2)}) collective-permute-start(bf16[240,384]{1,0:T(8,128)(2,1)S(1)} %get-tuple-element.23), channel_id=1, source_target_pairs={{0,2},{2,4},{4,6},{6,8},{8,10},{10,12},{12,14},{14,0},{1,3},{3,5},... | collective-permute-start | bytes 552968 | tf_op jit(solution)/shard_map/ppermute | solution.py:189
  137.4 14.0 %copy-start.19 = (bf16[240,384]{1,0:T(8,128)(2,1)}, bf16[240,384]{1,0:T(8,128)(2,1)S(1)}, u32[]{:S(2)}) copy-start(bf16[240,384]{1,0:T(8,128)(2,1)S(1)} %collective-permute-done.26) | copy-start | bytes 552964
  137.4 17.6 %collective-permute-start.19 = (bf16[128,1280]{1,0:T(8,128)(2,1)}, bf16[128,1280]{1,0:T(8,128)(2,1)}, u32[]{:S(2)}, u32[]{:S(2)}) collective-permute-start(bf16[128,1280]{1,0:T(8,128)(2,1)} %get-tuple-element.31), channel_id=1, source_target_pairs={{0,4},{4,8},{8,12},{12,14},{14,10},{10,6},{6,2},{2,0},{1,5},{5,9},... | collective-permute-start | bytes 983048 | tf_op jit(solution)/shard_map/ppermute | solution.py:119
  149.6 1.9 %copy-start.20 = (bf16[240,384]{1,0:T(8,128)(2,1)}, bf16[240,384]{1,0:T(8,128)(2,1)S(1)}, u32[]{:S(2)}) copy-start(bf16[240,384]{1,0:T(8,128)(2,1)S(1)} %collective-permute-done.25) | copy-start | bytes 552964
  149.6 7.4 %collective-permute-start.15 = (bf16[128,1280]{1,0:T(8,128)(2,1)}, bf16[128,1280]{1,0:T(8,128)(2,1)}, u32[]{:S(2)}, u32[]{:S(2)}) collective-permute-start(bf16[128,1280]{1,0:T(8,128)(2,1)} %get-tuple-element.30), channel_id=1, source_target_pairs={{0,2},{4,0},{8,4},{12,8},{14,12},{10,14},{6,10},{2,6},{1,3},{5,1},... | collective-permute-start | bytes 983048 | tf_op jit(solution)/shard_map/ppermute | solution.py:119
  152.3 4.7 %copy-start.2 = (bf16[1024,768]{1,0:T(8,128)(2,1)S(1)}, bf16[1024,768]{1,0:T(8,128)(2,1)}, u32[]{:S(2)}) copy-start(bf16[1024,768]{1,0:T(8,128)(2,1)} %copy.50) | copy-start | bytes 4718596
  (3 other events, 3.0 us)

commit v10 on v8

--- a/solution.py
+++ b/solution.py
@@ -245,6 +245,7 @@
             )
             * norm_scale
         ).reshape(seq_count, dp_count, rows_per, CO)
+        full_weight, grad_padded = lax.optimization_barrier((full_weight, grad_padded))
         dp_index = lax.axis_index("dp")
 
         def weight_block(column, width):

time: 159 us -> 167 us (1.050)
  other arithmetic: 18.3 us -> 25.1 us
  matrix products: 24.7 us -> 21.3 us
  starting transfers between devices: 45.4 us -> 47.1 us
    ppermute x14, waiting for transfers between devices: 19.8 us -> 13 us  [ring_reduce_scatter_sliced(): received = lax.ppermute(acc, axis, perm).astype(jnp.float32)]
    ppermute x8, waiting for transfers between devices: 2.97 us -> 8.63 us  [ring_scatter_back(): received = lax.ppermute(acc, 'seq', perm).astype(jnp.float32)]
    convert_element_type x6, other arithmetic: 5.39 us -> 8.58 us  [ring_reduce_scatter_sliced(): acc = acc.astype(wire_dtype)]
    dot_general x1, matrix products: 4.22 us -> 1.1 us  [body(): jnp.einsum('ihd,jhd->hij', grad_heads, all_values, preferred_element_type...]
    mul x1, other arithmetic: 0.38 us -> 2.95 us  [body(): jnp.concatenate([jnp.einsum('spc,spo->co', both_padded[:, offset:offset +...]
    dot_general x1, matrix products: 1.77 us -> 3.5 us  [body(): jnp.einsum('hij,ihd->jhd', rounded, grad_heads, preferred_element_type=jn...]
    unnamed x60 -> x67, local copies, waits for them, and re-layouts: 9.79 us -> 10.9 us
  transfers between devices with their start and end apart: 36 -> 36, of which waited for: 20 -> 20; matrix products, arithmetic and copies ran while one was open for 27% -> 20% of each run, Pallas kernels for 0% -> 0%
where the time goes in v10:
time: 167 us; the launch traced here: 166 us
  starting transfers between devices  47.1 us (28%)
  waiting for transfers between devices  45.6 us (27%)
  local copies, waits for them, and re-layouts  25.2 us (15%)
  other arithmetic  25.1 us (15%)
  matrix products  21.3 us (13%)
    ppermute x14, starting transfers between devices, ring_reduce_scatter_sliced(): received = lax.ppermute(acc, axis, perm).astype(jnp.float32)  17.3 us
    ppermute x3, waiting for transfers between devices, ring_gather(): current = lax.ppermute(current, 'seq', forward)  13.6 us
    ppermute x14, waiting for transfers between devices, ring_reduce_scatter_sliced(): received = lax.ppermute(acc, axis, perm).astype(jnp.float32)  13 us
    unnamed x67, local copies, waits for them, and re-layouts  10.9 us
    ppermute x8, starting transfers between devices, ring_scatter_back(): received = lax.ppermute(acc, 'seq', perm).astype(jnp.float32)  8.82 us
    ppermute x8, waiting for transfers between devices, ring_scatter_back(): received = lax.ppermute(acc, 'seq', perm).astype(jnp.float32)  8.63 us
    convert_element_type x6, other arithmetic, ring_reduce_scatter_sliced(): acc = acc.astype(wire_dtype)  8.58 us
    dot_general x5, matrix products, body(): jnp.einsum('spc,spo->co', both_padded[:, offset:offset + positions], both...  8.49 us
  transfers between devices with their start and end apart: 36, of which 20 were waited for; matrix products, arithmetic and copies ran while one was open for 20% of the time, Pallas kernels for 0%

profile of v10, /device:TPU:0, one launch (start us, length us, event | category | flops | bytes accessed | tf_op | source)
XLA Modules:
  0.0 166.0 jit_solution(8046165256393865534)
XLA Ops:
  3.9 3.1 %collective-permute-start = (bf16[128,1280]{0,1:T(8,128)(2,1)}, bf16[128,1280]{0,1:T(8,128)(2,1)}, u32[]{:S(2)}, u32[]{:S(2)}) collective-permute-start(bf16[128,1280]{0,1:T(8,128)(2,1)} %get-tuple-element.58), channel_id=1, source_target_pairs={{0,4},{4,8},{8,12},{12,14},{14,10},{10,6},{6,2},{2,0},{1,5},{5,9},... | collective-permute-start | bytes 983048 | tf_op jit(solution)/shard_map/ppermute | solution.py:76
  7.1 7.8 %collective-permute-done = bf16[128,1280]{0,1:T(8,128)(2,1)} collective-permute-done((bf16[128,1280]{0,1:T(8,128)(2,1)}, bf16[128,1280]{0,1:T(8,128)(2,1)}, u32[]{:S(2)}, u32[]{:S(2)}) %collective-permute-start) | collective-permute-done | bytes 327712 | tf_op jit(solution)/shard_map/ppermute | solution.py:76
  14.9 1.8 %collective-permute-start.1 = (bf16[128,1280]{0,1:T(8,128)(2,1)}, bf16[128,1280]{0,1:T(8,128)(2,1)S(1)}, u32[]{:S(2)}, u32[]{:S(2)}) collective-permute-start(bf16[128,1280]{0,1:T(8,128)(2,1)} %collective-permute-done), channel_id=1, source_target_pairs={{0,4},{4,8},{8,12},{12,14},{14,10},{10,6},{6,2},{2,0},{1,5},{5,9},... | collective-permute-start | bytes 983048 | tf_op jit(solution)/shard_map/ppermute | solution.py:76
  18.2 5.8 %collective-permute-done.1 = bf16[128,1280]{0,1:T(8,128)(2,1)S(1)} collective-permute-done((bf16[128,1280]{0,1:T(8,128)(2,1)}, bf16[128,1280]{0,1:T(8,128)(2,1)S(1)}, u32[]{:S(2)}, u32[]{:S(2)}) %collective-permute-start.1) | collective-permute-done | bytes 327712 | tf_op jit(solution)/shard_map/ppermute | solution.py:76
  24.0 1.5 collective-permute-start.2
  26.0 1.8 %constant_dynamic-update-slice_fusion.5 = bf16[1024,1280]{0,1:T(8,128)(2,1)} fusion(bf16[1024,1280]{0,1:T(8,128)(2,1)} %get-tuple-element.59, bf16[128,1280]{0,1:T(8,128)(2,1)} %collective-permute-done), kind=kLoop, calls=%fused_computation.159 | loop fusion | bytes 655360
  28.6 4.8 %collective-permute-done.5 = bf16[128,1280]{0,1:T(8,128)(2,1)S(1)} collective-permute-done((bf16[128,1280]{0,1:T(8,128)(2,1)S(1)}, bf16[128,1280]{0,1:T(8,128)(2,1)S(1)}, u32[]{:S(2)}, u32[]{:S(2)}) %collective-permute-start.5) | collective-permute-done | bytes 327712 | tf_op jit(solution)/shard_map/ppermute | solution.py:82
  33.9 1.6 collective-permute-start.6
  40.1 1.5 slice.170
  41.6 1.9 %slice.171 = bf16[1024,512]{0,1:T(8,128)(2,1)S(1)} slice(bf16[1024,1280]{0,1:T(8,128)(2,1)} %maximum_dynamic-update-slice_fusion), slice={[0:1024], [0:512]} | slice | bytes 2097152 | tf_op jit(solution)/shard_map/slice | solution.py:191
  47.9 3.4 %collective-permute-start.8 = (bf16[2,768]{1,0:T(2,128)(2,1)}, bf16[2,768]{1,0:T(2,128)(2,1)S(1)}, u32[]{:S(2)}, u32[]{:S(2)}) collective-permute-start(bf16[2,768]{1,0:T(2,128)(2,1)} %get-tuple-element.57), channel_id=1, source_target_pairs={{0,2},{2,4},{4,6},{6,8},{8,10},{10,12},{12,14},{1,3},{3,5},{5,7},{... | collective-permute-start | bytes 9224 | tf_op jit(solution)/shard_map/ppermute | solution.py:24
  53.3 4.0 %collective-permute-done.9 = bf16[2,768]{1,0:T(2,128)(2,1)S(1)} collective-permute-done((bf16[2,768]{1,0:T(2,128)(2,1)}, bf16[2,768]{1,0:T(2,128)(2,1)S(1)}, u32[]{:S(2)}, u32[]{:S(2)}) %collective-permute-start.9) | collective-permute-done | bytes 3104 | tf_op jit(solution)/shard_map/ppermute | solution.py:25
  58.5 2.0 %fusion.32 = (bf16[256,384]{1,0:T(8,128)(2,1)S(1)}, bf16[1,256,384]{2,1,0:T(8,128)(2,1)}) fusion(bf16[1,256,384]{2,1,0:T(8,128)(2,1)S(1)} %copy-done.26, bf16[256,3840]{1,0:T(8,128)(2,1)S(1)} %fusion.33, bf16[3840,384]{1,0:T(8,128)(2,1)S(1)} %copy-done), kind=kOutput, calls=%fused_computation.84 | convolution fusion | flops 756252672 | bytes 5505024 | tf_op jit(solution)/shard_map/dot_general | solution.py:220
  62.3 5.1 %collective-permute-start.12 = (bf16[2,384]{1,0:T(2,128)(2,1)S(1)}, bf16[2,384]{1,0:T(2,128)(2,1)S(1)}, u32[]{:S(2)}, u32[]{:S(2)}) collective-permute-start(bf16[2,384]{1,0:T(2,128)(2,1)S(1)} %get-tuple-element.60), channel_id=1, source_target_pairs={{0,2},{2,4},{4,6},{6,8},{8,10},{10,12},{12,14},{1,3},{3,5},{5,7},{... | collective-permute-start | bytes 4616 | tf_op jit(solution)/shard_map/ppermute | solution.py:24
  68.7 1.8 %fusion.8 = f32[3840,384]{1,0:T(8,128)S(1)} fusion(bf16[1,260,768]{2,1,0:T(8,128)(2,1)} %get-tuple-element.53, bf16[1,260,768]{2,1,0:T(8,128)(2,1)} %bitcast.11, bf16[1,256,384]{2,1,0:T(8,128)(2,1)} %bitcast.14, bf16[1,256,384]{2,1,0:T(8,128)(2,1)S(1)} %bitcast.192), kind=kOutput, calls=%fused_computation.34 | convolution fusion | flops 302579712 | bytes 2371584 | tf_op jit(solution)/shard_map/spc,spo->co/dot_general | solution.py:236
  70.5 1.7 %fusion.7 = f32[3840,384]{1,0:T(8,128)S(1)} fusion(f32[3840,384]{1,0:T(8,128)S(1)} %fusion.8, bf16[1,260,768]{2,1,0:T(8,128)(2,1)S(1)} %copy-done.19, bf16[1,260,768]{2,1,0:T(8,128)(2,1)} %bitcast.11, bf16[1,256,384]{2,1,0:T(8,128)(2,1)} %bitcast.14, bf16[1,256,384]{2,1,0:T(8,128)(2,1)S(1)} %bitcast.193), kind=kOutput, calls=%fused_computation.32 | convolution fusion | flops 302579712 | bytes 2377728 | tf_op jit(solution)/shard_map/spc,spo->co/dot_general | solution.py:236
  72.2 1.7 %fusion.6 = f32[3840,384]{1,0:T(8,128)S(1)} fusion(f32[3840,384]{1,0:T(8,128)S(1)} %fusion.7, bf16[1,260,768]{2,1,0:T(8,128)(2,1)S(1)} %copy-done.19, bf16[1,260,768]{2,1,0:T(8,128)(2,1)} %bitcast.11, bf16[1,256,384]{2,1,0:T(8,128)(2,1)} %bitcast.14, bf16[1,256,384]{2,1,0:T(8,128)(2,1)S(1)} %bitcast.194), kind=kOutput, calls=%fused_computation.30 | convolution fusion | flops 302579712 | bytes 2377728 | tf_op jit(solution)/shard_map/spc,spo->co/dot_general | solution.py:236
  73.9 1.7 %fusion.5 = f32[3840,384]{1,0:T(8,128)S(1)} fusion(f32[3840,384]{1,0:T(8,128)S(1)} %fusion.6, bf16[1,260,768]{2,1,0:T(8,128)(2,1)S(1)} %copy-done.19, bf16[1,260,768]{2,1,0:T(8,128)(2,1)} %bitcast.11, bf16[1,256,384]{2,1,0:T(8,128)(2,1)} %bitcast.14, bf16[1,256,384]{2,1,0:T(8,128)(2,1)S(1)} %bitcast.195), kind=kOutput, calls=%fused_computation.28 | convolution fusion | flops 302579712 | bytes 2377728 | tf_op jit(solution)/shard_map/spc,spo->co/dot_general | solution.py:236
  75.5 1.7 %fusion.4 = f32[3840,384]{1,0:T(8,128)S(1)} fusion(f32[3840,384]{1,0:T(8,128)S(1)} %fusion.5, bf16[1,260,768]{2,1,0:T(8,128)(2,1)} %bitcast.11, bf16[1,260,768]{2,1,0:T(8,128)(2,1)S(1)} %copy-done.19, bf16[1,256,384]{2,1,0:T(8,128)(2,1)} %bitcast.14, bf16[1,256,384]{2,1,0:T(8,128)(2,1)S(1)} %bitcast.196), kind=kOutput, calls=%fused_computation.26 | convolution fusion | flops 303759360 | bytes 2377728 | tf_op jit(solution)/shard_map/spc,spo->co/dot_general | solution.py:236
  77.2 3.0 %broadcast_multiply_fusion = f32[3840,384]{1,0:T(8,128)} fusion(f32[3840,384]{1,0:T(8,128)S(1)} %fusion.4), kind=kLoop, calls=%fused_computation.14 | loop fusion | flops 1474560 | bytes 11796480 | tf_op jit(solution)/shard_map/mul | solution.py:234
  84.1 3.5 %convolution_convert_fusion = bf16[4,192,1024]{2,1,0:T(8,128)(2,1)} fusion(bf16[128,4,192]{0,2,1:T(8,128)(2,1)S(1)} %bitcast.183, f32[4,1024,128]{2,1,0:T(8,128)} %copy-done.3, f32[4,128]{1,0:T(4,128)S(1)} %log_add_fusion), kind=kOutput, calls=%fused_computation.24 | convolution fusion | flops 203685888 | bytes 3868672 | tf_op jit(solution)/shard_map/hij,ihd->jhd/dot_general | solution.py:319
  88.8 1.6 fusion.61
  90.3 4.7 %collective-permute-start.22 = (bf16[240,192]{1,0:T(8,128)(2,1)S(1)}, bf16[240,192]{1,0:T(8,128)(2,1)S(1)}, u32[]{:S(2)}, u32[]{:S(2)}) collective-permute-start(bf16[240,192]{1,0:T(8,128)(2,1)S(1)} %get-tuple-element.41), channel_id=1, source_target_pairs={{0,4},{4,8},{8,12},{12,14},{14,10},{10,6},{6,2},{2,0},{1,5},{5,9},... | collective-permute-start | bytes 276488 | tf_op jit(solution)/shard_map/ppermute | solution.py:176
  96.4 2.6 %copy.55 = bf16[1024,768]{1,0:T(8,128)(2,1)} copy(bf16[1024,768]{0,1:T(8,128)(2,1)} %bitcast.180) | data formatting | bytes 3145728 | tf_op jit(solution)/shard_map/reshape | solution.py:323
  99.0 2.3 %copy.52 = bf16[1024,4,128]{0,2,1:T(8,128)(2,1)} copy(bf16[1024,4,128]{2,0,1:T(8,128)(2,1)} %fusion.9) | data formatting | bytes 2097152 | tf_op jit(solution)/shard_map/mul | solution.py:316
  101.3 2.3 %copy.54 = bf16[1024,512]{1,0:T(8,128)(2,1)} copy(bf16[1024,512]{0,1:T(8,128)(2,1)} %bitcast.181) | data formatting | bytes 2097152 | tf_op jit(solution)/shard_map/reshape | solution.py:322
  104.8 2.1 %collective-permute-start.23 = (bf16[240,192]{1,0:T(8,128)(2,1)S(1)}, bf16[240,192]{1,0:T(8,128)(2,1)S(1)}, u32[]{:S(2)}, u32[]{:S(2)}) collective-permute-start(bf16[240,192]{1,0:T(8,128)(2,1)S(1)} %get-tuple-element.39), channel_id=1, source_target_pairs={{0,4},{4,8},{8,12},{12,14},{14,10},{10,6},{6,2},{2,0},{1,5},{5,9},... | collective-permute-start | bytes 276488 | tf_op jit(solution)/shard_map/ppermute | solution.py:176
  108.5 1.9 %collective-permute-start.18 = (bf16[128,640]{1,0:T(8,128)(2,1)S(1)}, bf16[128,640]{1,0:T(8,128)(2,1)S(1)}, u32[]{:S(2)}, u32[]{:S(2)}) collective-permute-start(bf16[128,640]{1,0:T(8,128)(2,1)S(1)} %get-tuple-element.50), channel_id=1, source_target_pairs={{0,4},{4,8},{8,12},{12,14},{14,10},{10,6},{6,2},{2,0},{1,5},{5,9},... | collective-permute-start | bytes 491528 | tf_op jit(solution)/shard_map/ppermute | solution.py:119
  113.0 1.6 collective-permute-start.24
  115.2 2.6 %collective-permute-done.24 = bf16[240,192]{1,0:T(8,128)(2,1)S(1)} collective-permute-done((bf16[240,192]{1,0:T(8,128)(2,1)S(1)}, bf16[240,192]{1,0:T(8,128)(2,1)S(1)}, u32[]{:S(2)}, u32[]{:S(2)}) %collective-permute-start.24) | collective-permute-done | bytes 92192 | tf_op jit(solution)/shard_map/ppermute | solution.py:176
  117.9 1.6 collective-permute-done.31
  120.7 1.6 collective-permute-start.25
  123.9 1.7 %collective-permute-done.25 = bf16[240,192]{1,0:T(8,128)(2,1)S(1)} collective-permute-done((bf16[240,192]{1,0:T(8,128)(2,1)S(1)}, bf16[240,192]{1,0:T(8,128)(2,1)S(1)}, u32[]{:S(2)}, u32[]{:S(2)}) %collective-permute-start.25) | collective-permute-done | bytes 92192 | tf_op jit(solution)/shard_map/ppermute | solution.py:176
  125.6 1.6 collective-permute-done.32
  127.2 1.8 %fusion.50 = (bf16[240,192]{1,0:T(8,128)(2,1)}, bf16[240,192]{1,0:T(8,128)(2,1)S(1)}) fusion(f32[8,2,240,384]{3,2,1,0:T(8,128)} %bitcast.172, s32[]{:T(128)S(6)} %select_n.530, s32[]{:T(128)S(6)} %select_n.498, bf16[240,192]{1,0:T(8,128)(2,1)S(1)} %collective-permute-done.25, s32[]{:T(128)S(6)} %select_n.594, bf16[240,192]{1,0:T(8,128)(2,1)S(1)} %collective-permute-done.32), kind=kLoop, calls=%fused_computation.126 | loop fusion | flops 276480 | bytes 737292 | tf_op jit(solution)/shard_map/convert_element_type | solution.py:179
  129.0 2.3 %collective-permute-start.26 = (bf16[240,192]{1,0:T(8,128)(2,1)}, bf16[240,192]{1,0:T(8,128)(2,1)S(1)}, u32[]{:S(2)}, u32[]{:S(2)}) collective-permute-start(bf16[240,192]{1,0:T(8,128)(2,1)} %get-tuple-element.33), channel_id=1, source_target_pairs={{0,4},{4,8},{8,12},{12,14},{14,10},{10,6},{6,2},{2,0},{1,5},{5,9},... | collective-permute-start | bytes 276488 | tf_op jit(solution)/shard_map/ppermute | solution.py:176
  131.3 2.1 %collective-permute-start.19 = (bf16[128,1280]{1,0:T(8,128)(2,1)S(1)}, bf16[128,1280]{1,0:T(8,128)(2,1)}, u32[]{:S(2)}, u32[]{:S(2)}) collective-permute-start(bf16[128,1280]{1,0:T(8,128)(2,1)S(1)} %fusion.41), channel_id=1, source_target_pairs={{0,4},{4,8},{8,12},{12,14},{14,10},{10,6},{6,2},{2,0},{1,5},{5,9},... | collective-permute-start | bytes 983048 | tf_op jit(solution)/shard_map/ppermute | solution.py:119
  133.4 1.7 %collective-permute-done.26 = bf16[240,192]{1,0:T(8,128)(2,1)S(1)} collective-permute-done((bf16[240,192]{1,0:T(8,128)(2,1)}, bf16[240,192]{1,0:T(8,128)(2,1)S(1)}, u32[]{:S(2)}, u32[]{:S(2)}) %collective-permute-start.26) | collective-permute-done | bytes 92192 | tf_op jit(solution)/shard_map/ppermute | solution.py:176
  135.1 2.3 %collective-permute-done.33 = bf16[240,192]{1,0:T(8,128)(2,1)} collective-permute-done((bf16[240,192]{1,0:T(8,128)(2,1)S(1)}, bf16[240,192]{1,0:T(8,128)(2,1)}, u32[]{:S(2)}, u32[]{:S(2)}) %collective-permute-start.33) | collective-permute-done | bytes 92192 | tf_op jit(solution)/shard_map/ppermute | solution.py:176
  137.5 1.9 %fusion.49 = (bf16[240,192]{1,0:T(8,128)(2,1)}, bf16[240,192]{1,0:T(8,128)(2,1)}) fusion(f32[8,2,240,384]{3,2,1,0:T(8,128)} %bitcast.173, s32[]{:T(128)S(6)} %select_n.538, s32[]{:T(128)S(6)} %select_n.498, bf16[240,192]{1,0:T(8,128)(2,1)S(1)} %collective-permute-done.26, s32[]{:T(128)S(6)} %select_n.602, bf16[240,192]{1,0:T(8,128)(2,1)} %collective-permute-done.33), kind=kLoop, calls=%fused_computation.124 | loop fusion | flops 276480 | bytes 737292 | tf_op jit(solution)/shard_map/convert_element_type | solution.py:179
  139.5 2.0 %collective-permute-start.34 = (bf16[240,192]{1,0:T(8,128)(2,1)}, bf16[240,192]{1,0:T(8,128)(2,1)}, u32[]{:S(2)}, u32[]{:S(2)}) collective-permute-start(bf16[240,192]{1,0:T(8,128)(2,1)} %get-tuple-element.32), channel_id=1, source_target_pairs={{0,2},{4,0},{8,4},{12,8},{14,12},{10,14},{6,10},{2,6},{1,3},{5,1},... | collective-permute-start | bytes 276488 | tf_op jit(solution)/shard_map/ppermute | solution.py:176
  141.5 2.3 %add_convert_fusion.4 = (bf16[128,1280]{1,0:T(8,128)(2,1)}, bf16[128,1280]{1,0:T(8,128)(2,1)}) fusion(bf16[128,1280]{1,0:T(8,128)(2,1)} %collective-permute-done.15, bf16[1024,768]{1,0:T(8,128)(2,1)} %copy.55, bf16[1024,512]{1,0:T(8,128)(2,1)} %copy.54, bf16[128,1280]{1,0:T(8,128)(2,1)} %collective-permute-done.19), kind=kLoop, calls=%fused_computation.67 | loop fusion | flops 2293760 | bytes 3932160 | tf_op jit(solution)/shard_map/convert_element_type | solution.py:123
  143.8 2.0 %collective-permute-start.20 = (bf16[128,1280]{1,0:T(8,128)(2,1)}, bf16[128,1280]{1,0:T(8,128)(2,1)}, u32[]{:S(2)}, u32[]{:S(2)}) collective-permute-start(bf16[128,1280]{1,0:T(8,128)(2,1)} %get-tuple-element.46), channel_id=1, source_target_pairs={{0,4},{4,8},{8,12},{12,14},{14,10},{10,6},{6,2},{2,0},{1,5},{5,9},... | collective-permute-start | bytes 983048 | tf_op jit(solution)/shard_map/ppermute | solution.py:119
  150.4 1.7 %collective-permute-done.16 = bf16[128,1280]{1,0:T(8,128)(2,1)S(1)} collective-permute-done((bf16[128,1280]{1,0:T(8,128)(2,1)}, bf16[128,1280]{1,0:T(8,128)(2,1)S(1)}, u32[]{:S(2)}, u32[]{:S(2)}) %collective-permute-start.16) | collective-permute-done | bytes 327712 | tf_op jit(solution)/shard_map/ppermute | solution.py:119
  152.0 2.3 %collective-permute-done.20 = bf16[128,1280]{1,0:T(8,128)(2,1)} collective-permute-done((bf16[128,1280]{1,0:T(8,128)(2,1)}, bf16[128,1280]{1,0:T(8,128)(2,1)}, u32[]{:S(2)}, u32[]{:S(2)}) %collective-permute-start.20) | collective-permute-done | bytes 327712 | tf_op jit(solution)/shard_map/ppermute | solution.py:119
  155.8 1.6 collective-permute-start.21
  159.9 3.0 %collective-permute-done.21 = bf16[128,1280]{1,0:T(8,128)(2,1)S(1)} collective-permute-done((bf16[128,1280]{1,0:T(8,128)(2,1)S(1)}, bf16[128,1280]{1,0:T(8,128)(2,1)S(1)}, u32[]{:S(2)}, u32[]{:S(2)}) %collective-permute-start.21) | collective-permute-done | bytes 327712 | tf_op jit(solution)/shard_map/ppermute | solution.py:119
  162.9 1.6 collective-permute-done.17
  (156 shorter events, 46.7 us)
Async XLA Ops:
  0.6 57.9 %copy-start = (bf16[3840,384]{1,0:T(8,128)(2,1)S(1)}, bf16[3840,384]{1,0:T(8,128)(2,1)}, u32[]{:S(2)}) copy-start(bf16[3840,384]{1,0:T(8,128)(2,1)} %param.14) | copy-start | bytes 8847364
  0.6 6.3 %copy-start.21 = (bf16[1,128,512]{2,1,0:T(8,128)(2,1)S(1)}, bf16[1,128,512]{2,1,0:T(8,128)(2,1)}, u32[]{:S(2)}) copy-start(bf16[1,128,512]{2,1,0:T(8,128)(2,1)} %param.8) | copy-start | bytes 393220
  0.7 6.4 %copy-start.25 = (bf16[768]{0:T(1024)(128)(2,1)S(1)}, bf16[768]{0:T(1024)(128)(2,1)}, u32[]{:S(2)}) copy-start(bf16[768]{0:T(1024)(128)(2,1)} %param.13) | copy-start | bytes 4612
  3.9 11.0 %collective-permute-start = (bf16[128,1280]{0,1:T(8,128)(2,1)}, bf16[128,1280]{0,1:T(8,128)(2,1)}, u32[]{:S(2)}, u32[]{:S(2)}) collective-permute-start(bf16[128,1280]{0,1:T(8,128)(2,1)} %get-tuple-element.58), channel_id=1, source_target_pairs={{0,4},{4,8},{8,12},{12,14},{14,10},{10,6},{6,2},{2,0},{1,5},{5,9},... | collective-permute-start | bytes 983048 | tf_op jit(solution)/shard_map/ppermute | solution.py:76
  6.9 9.8 %collective-permute-start.3 = (bf16[128,1280]{0,1:T(8,128)(2,1)}, bf16[128,1280]{0,1:T(8,128)(2,1)S(1)}, u32[]{:S(2)}, u32[]{:S(2)}) collective-permute-start(bf16[128,1280]{0,1:T(8,128)(2,1)} %get-tuple-element.58), channel_id=1, source_target_pairs={{0,2},{4,0},{8,4},{12,8},{14,12},{10,14},{6,10},{2,6},{1,3},{5,1},... | collective-permute-start | bytes 983048 | tf_op jit(solution)/shard_map/ppermute | solution.py:82
  7.1 36.4 %copy-start.16 = (bf16[1,128,512]{1,2,0:T(8,128)(2,1)}, bf16[1,128,512]{1,2,0:T(8,128)(2,1)S(1)}, u32[]{:S(2)}) copy-start(bf16[1,128,512]{1,2,0:T(8,128)(2,1)S(1)} %copy.72) | copy-start | bytes 393220
  14.9 9.1 %collective-permute-start.1 = (bf16[128,1280]{0,1:T(8,128)(2,1)}, bf16[128,1280]{0,1:T(8,128)(2,1)S(1)}, u32[]{:S(2)}, u32[]{:S(2)}) collective-permute-start(bf16[128,1280]{0,1:T(8,128)(2,1)} %collective-permute-done), channel_id=1, source_target_pairs={{0,4},{4,8},{8,12},{12,14},{14,10},{10,6},{6,2},{2,0},{1,5},{5,9},... | collective-permute-start | bytes 983048 | tf_op jit(solution)/shard_map/ppermute | solution.py:76
  16.7 8.8 %collective-permute-start.4 = (bf16[128,1280]{0,1:T(8,128)(2,1)S(1)}, bf16[128,1280]{0,1:T(8,128)(2,1)S(1)}, u32[]{:S(2)}, u32[]{:S(2)}) collective-permute-start(bf16[128,1280]{0,1:T(8,128)(2,1)S(1)} %collective-permute-done.3), channel_id=1, source_target_pairs={{0,2},{4,0},{8,4},{12,8},{14,12},{10,14},{6,10},{2,6},{1,3},{5,1},... | collective-permute-start | bytes 983048 | tf_op jit(solution)/shard_map/ppermute | solution.py:82
  16.9 28.5 %copy-start.22 = (s32[256]{0:T(256)}, s32[256]{0:T(256)S(1)}, u32[]{:S(2)}) copy-start(s32[256]{0:T(256)S(1)} %and_select_fusion) | copy-start | bytes 3076
  24.0 9.9 %collective-permute-start.2 = (bf16[128,1280]{0,1:T(8,128)(2,1)S(1)}, bf16[128,1280]{0,1:T(8,128)(2,1)S(1)}, u32[]{:S(2)}, u32[]{:S(2)}) collective-permute-start(bf16[128,1280]{0,1:T(8,128)(2,1)S(1)} %collective-permute-done.1), channel_id=1, source_target_pairs={{0,4},{4,8},{8,12},{12,14},{14,10},{10,6},{6,2},{2,0},{1,5},{5,9},... | collective-permute-start | bytes 983048 | tf_op jit(solution)/shard_map/ppermute | solution.py:76
  25.5 7.8 %collective-permute-start.5 = (bf16[128,1280]{0,1:T(8,128)(2,1)S(1)}, bf16[128,1280]{0,1:T(8,128)(2,1)S(1)}, u32[]{:S(2)}, u32[]{:S(2)}) collective-permute-start(bf16[128,1280]{0,1:T(8,128)(2,1)S(1)} %collective-permute-done.4), channel_id=1, source_target_pairs={{0,2},{4,0},{8,4},{12,8},{14,12},{10,14},{6,10},{2,6},{1,3},{5,1},... | collective-permute-start | bytes 983048 | tf_op jit(solution)/shard_map/ppermute | solution.py:82
  33.3 5.4 %collective-permute-start.7 = (bf16[128,640]{0,1:T(8,128)(2,1)S(1)}, bf16[128,640]{0,1:T(8,128)(2,1)S(1)}, u32[]{:S(2)}, u32[]{:S(2)}) collective-permute-start(bf16[128,640]{0,1:T(8,128)(2,1)S(1)} %slice.169), channel_id=1, source_target_pairs={{0,2},{4,0},{8,4},{12,8},{14,12},{10,14},{6,10},{2,6},{1,3},{5,1},... | collective-permute-start | bytes 491528 | tf_op jit(solution)/shard_map/ppermute | solution.py:85
  33.9 5.4 %collective-permute-start.6 = (bf16[128,640]{0,1:T(8,128)(2,1)S(1)}, bf16[128,640]{0,1:T(8,128)(2,1)S(1)}, u32[]{:S(2)}, u32[]{:S(2)}) collective-permute-start(bf16[128,640]{0,1:T(8,128)(2,1)S(1)} %slice.168), channel_id=1, source_target_pairs={{0,4},{4,8},{8,12},{12,14},{14,10},{10,6},{6,2},{2,0},{1,5},{5,9},... | collective-permute-start | bytes 491528 | tf_op jit(solution)/shard_map/ppermute | solution.py:79
  47.9 5.0 %collective-permute-start.8 = (bf16[2,768]{1,0:T(2,128)(2,1)}, bf16[2,768]{1,0:T(2,128)(2,1)S(1)}, u32[]{:S(2)}, u32[]{:S(2)}) collective-permute-start(bf16[2,768]{1,0:T(2,128)(2,1)} %get-tuple-element.57), channel_id=1, source_target_pairs={{0,2},{2,4},{4,6},{6,8},{8,10},{10,12},{12,14},{1,3},{3,5},{5,7},{... | collective-permute-start | bytes 9224 | tf_op jit(solution)/shard_map/ppermute | solution.py:24
  51.5 5.8 %collective-permute-start.9 = (bf16[2,768]{1,0:T(2,128)(2,1)}, bf16[2,768]{1,0:T(2,128)(2,1)S(1)}, u32[]{:S(2)}, u32[]{:S(2)}) collective-permute-start(bf16[2,768]{1,0:T(2,128)(2,1)} %get-tuple-element.56), channel_id=1, source_target_pairs={{2,0},{4,2},{6,4},{8,6},{10,8},{12,10},{14,12},{3,1},{5,3},{7,5},{... | collective-permute-start | bytes 9224 | tf_op jit(solution)/shard_map/ppermute | solution.py:25
  58.3 10.4 %collective-permute-start.10 = (bf16[260,768]{1,0:T(8,128)(2,1)}, bf16[260,768]{1,0:T(8,128)(2,1)}, u32[]{:S(2)}, u32[]{:S(2)}) collective-permute-start(bf16[260,768]{1,0:T(8,128)(2,1)} %get-tuple-element.52), channel_id=1, source_target_pairs={{0,1},{1,0},{2,3},{3,2},{4,5},{5,4},{6,7},{7,6},{8,9},{9,8},{10,11... | collective-permute-start | bytes 1198088 | tf_op jit(solution)/shard_map/ppermute | solution.py:231
  60.5 8.1 %collective-permute-start.11 = (bf16[256,384]{1,0:T(8,128)(2,1)S(1)}, bf16[256,384]{1,0:T(8,128)(2,1)}, u32[]{:S(2)}, u32[]{:S(2)}) collective-permute-start(bf16[256,384]{1,0:T(8,128)(2,1)S(1)} %get-tuple-element.54), channel_id=1, source_target_pairs={{0,1},{1,0},{2,3},{3,2},{4,5},{5,4},{6,7},{7,6},{8,9},{9,8},{10,11... | collective-permute-start | bytes 589832 | tf_op jit(solution)/shard_map/ppermute | solution.py:232
  61.1 6.6 %collective-permute-start.13 = (bf16[2,384]{1,0:T(2,128)(2,1)S(1)}, bf16[2,384]{1,0:T(2,128)(2,1)S(1)}, u32[]{:S(2)}, u32[]{:S(2)}) collective-permute-start(bf16[2,384]{1,0:T(2,128)(2,1)S(1)} %get-tuple-element.61), channel_id=1, source_target_pairs={{2,0},{4,2},{6,4},{8,6},{10,8},{12,10},{14,12},{3,1},{5,3},{7,5},{... | collective-permute-start | bytes 4616 | tf_op jit(solution)/shard_map/ppermute | solution.py:25
  62.3 6.2 %collective-permute-start.12 = (bf16[2,384]{1,0:T(2,128)(2,1)S(1)}, bf16[2,384]{1,0:T(2,128)(2,1)S(1)}, u32[]{:S(2)}, u32[]{:S(2)}) collective-permute-start(bf16[2,384]{1,0:T(2,128)(2,1)S(1)} %get-tuple-element.60), channel_id=1, source_target_pairs={{0,2},{2,4},{4,6},{6,8},{8,10},{10,12},{12,14},{1,3},{3,5},{5,7},{... | collective-permute-start | bytes 4616 | tf_op jit(solution)/shard_map/ppermute | solution.py:24
  87.6 7.4 %copy-start.17 = (bf16[1,128,512]{1,2,0:T(8,128)(2,1)S(1)}, bf16[1,128,512]{1,2,0:T(8,128)(2,1)}, u32[]{:S(2)}) copy-start(bf16[1,128,512]{1,2,0:T(8,128)(2,1)} %copy-done.16) | copy-start | bytes 393220
  90.3 13.3 %collective-permute-start.22 = (bf16[240,192]{1,0:T(8,128)(2,1)S(1)}, bf16[240,192]{1,0:T(8,128)(2,1)S(1)}, u32[]{:S(2)}, u32[]{:S(2)}) collective-permute-start(bf16[240,192]{1,0:T(8,128)(2,1)S(1)} %get-tuple-element.41), channel_id=1, source_target_pairs={{0,4},{4,8},{8,12},{12,14},{14,10},{10,6},{6,2},{2,0},{1,5},{5,9},... | collective-permute-start | bytes 276488 | tf_op jit(solution)/shard_map/ppermute | solution.py:176
  95.0 8.6 %collective-permute-start.29 = (bf16[240,192]{1,0:T(8,128)(2,1)S(1)}, bf16[240,192]{1,0:T(8,128)(2,1)S(1)}, u32[]{:S(2)}, u32[]{:S(2)}) collective-permute-start(bf16[240,192]{1,0:T(8,128)(2,1)S(1)} %get-tuple-element.42), channel_id=1, source_target_pairs={{0,2},{4,0},{8,4},{12,8},{14,12},{10,14},{6,10},{2,6},{1,3},{5,1},... | collective-permute-start | bytes 276488 | tf_op jit(solution)/shard_map/ppermute | solution.py:176
  104.8 6.1 %collective-permute-start.23 = (bf16[240,192]{1,0:T(8,128)(2,1)S(1)}, bf16[240,192]{1,0:T(8,128)(2,1)S(1)}, u32[]{:S(2)}, u32[]{:S(2)}) collective-permute-start(bf16[240,192]{1,0:T(8,128)(2,1)S(1)} %get-tuple-element.39), channel_id=1, source_target_pairs={{0,4},{4,8},{8,12},{12,14},{14,10},{10,6},{6,2},{2,0},{1,5},{5,9},... | collective-permute-start | bytes 276488 | tf_op jit(solution)/shard_map/ppermute | solution.py:176
  106.9 8.3 %copy-start.1 = (bf16[1024,768]{1,0:T(8,128)(2,1)S(1)}, bf16[1024,768]{1,0:T(8,128)(2,1)}, u32[]{:S(2)}) copy-start(bf16[1024,768]{1,0:T(8,128)(2,1)} %copy.55) | copy-start | bytes 4718596
  106.9 8.3 %copy-start.5 = (bf16[1024,512]{1,0:T(8,128)(2,1)S(1)}, bf16[1024,512]{1,0:T(8,128)(2,1)}, u32[]{:S(2)}) copy-start(bf16[1024,512]{1,0:T(8,128)(2,1)} %copy.54) | copy-start | bytes 3145732
  106.9 4.9 %collective-permute-start.30 = (bf16[240,192]{1,0:T(8,128)(2,1)S(1)}, bf16[240,192]{1,0:T(8,128)(2,1)S(1)}, u32[]{:S(2)}, u32[]{:S(2)}) collective-permute-start(bf16[240,192]{1,0:T(8,128)(2,1)S(1)} %get-tuple-element.40), channel_id=1, source_target_pairs={{0,2},{4,0},{8,4},{12,8},{14,12},{10,14},{6,10},{2,6},{1,3},{5,1},... | collective-permute-start | bytes 276488 | tf_op jit(solution)/shard_map/ppermute | solution.py:176
  108.1 6.9 %collective-permute-start.14 = (bf16[128,640]{1,0:T(8,128)(2,1)S(1)}, bf16[128,640]{1,0:T(8,128)(2,1)S(1)}, u32[]{:S(2)}, u32[]{:S(2)}) collective-permute-start(bf16[128,640]{1,0:T(8,128)(2,1)S(1)} %get-tuple-element.49), channel_id=1, source_target_pairs={{0,2},{4,0},{8,4},{12,8},{14,12},{10,14},{6,10},{2,6},{1,3},{5,1},... | collective-permute-start | bytes 491528 | tf_op jit(solution)/shard_map/ppermute | solution.py:119
  108.5 6.6 %collective-permute-start.18 = (bf16[128,640]{1,0:T(8,128)(2,1)S(1)}, bf16[128,640]{1,0:T(8,128)(2,1)S(1)}, u32[]{:S(2)}, u32[]{:S(2)}) collective-permute-start(bf16[128,640]{1,0:T(8,128)(2,1)S(1)} %get-tuple-element.50), channel_id=1, source_target_pairs={{0,4},{4,8},{8,12},{12,14},{14,10},{10,6},{6,2},{2,0},{1,5},{5,9},... | collective-permute-start | bytes 491528 | tf_op jit(solution)/shard_map/ppermute | solution.py:119
  113.0 4.9 %collective-permute-start.24 = (bf16[240,192]{1,0:T(8,128)(2,1)S(1)}, bf16[240,192]{1,0:T(8,128)(2,1)S(1)}, u32[]{:S(2)}, u32[]{:S(2)}) collective-permute-start(bf16[240,192]{1,0:T(8,128)(2,1)S(1)} %get-tuple-element.37), channel_id=1, source_target_pairs={{0,4},{4,8},{8,12},{12,14},{14,10},{10,6},{6,2},{2,0},{1,5},{5,9},... | collective-permute-start | bytes 276488 | tf_op jit(solution)/shard_map/ppermute | solution.py:176
  114.6 4.9 %collective-permute-start.31 = (bf16[240,192]{1,0:T(8,128)(2,1)S(1)}, bf16[240,192]{1,0:T(8,128)(2,1)S(1)}, u32[]{:S(2)}, u32[]{:S(2)}) collective-permute-start(bf16[240,192]{1,0:T(8,128)(2,1)S(1)} %get-tuple-element.38), channel_id=1, source_target_pairs={{0,2},{4,0},{8,4},{12,8},{14,12},{10,14},{6,10},{2,6},{1,3},{5,1},... | collective-permute-start | bytes 276488 | tf_op jit(solution)/shard_map/ppermute | solution.py:176
  120.7 4.9 %collective-permute-start.25 = (bf16[240,192]{1,0:T(8,128)(2,1)S(1)}, bf16[240,192]{1,0:T(8,128)(2,1)S(1)}, u32[]{:S(2)}, u32[]{:S(2)}) collective-permute-start(bf16[240,192]{1,0:T(8,128)(2,1)S(1)} %get-tuple-element.35), channel_id=1, source_target_pairs={{0,4},{4,8},{8,12},{12,14},{14,10},{10,6},{6,2},{2,0},{1,5},{5,9},... | collective-permute-start | bytes 276488 | tf_op jit(solution)/shard_map/ppermute | solution.py:176
  122.3 4.9 %collective-permute-start.32 = (bf16[240,192]{1,0:T(8,128)(2,1)S(1)}, bf16[240,192]{1,0:T(8,128)(2,1)S(1)}, u32[]{:S(2)}, u32[]{:S(2)}) collective-permute-start(bf16[240,192]{1,0:T(8,128)(2,1)S(1)} %get-tuple-element.36), channel_id=1, source_target_pairs={{0,2},{4,0},{8,4},{12,8},{14,12},{10,14},{6,10},{2,6},{1,3},{5,1},... | collective-permute-start | bytes 276488 | tf_op jit(solution)/shard_map/ppermute | solution.py:176
  123.5 17.9 %collective-permute-start.15 = (bf16[128,1280]{1,0:T(8,128)(2,1)}, bf16[128,1280]{1,0:T(8,128)(2,1)}, u32[]{:S(2)}, u32[]{:S(2)}) collective-permute-start(bf16[128,1280]{1,0:T(8,128)(2,1)} %pad_maximum_fusion.8), channel_id=1, source_target_pairs={{0,2},{4,0},{8,4},{12,8},{14,12},{10,14},{6,10},{2,6},{1,3},{5,1},... | collective-permute-start | bytes 983048 | tf_op jit(solution)/shard_map/ppermute | solution.py:119
  129.0 6.2 %collective-permute-start.26 = (bf16[240,192]{1,0:T(8,128)(2,1)}, bf16[240,192]{1,0:T(8,128)(2,1)S(1)}, u32[]{:S(2)}, u32[]{:S(2)}) collective-permute-start(bf16[240,192]{1,0:T(8,128)(2,1)} %get-tuple-element.33), channel_id=1, source_target_pairs={{0,4},{4,8},{8,12},{12,14},{14,10},{10,6},{6,2},{2,0},{1,5},{5,9},... | collective-permute-start | bytes 276488 | tf_op jit(solution)/shard_map/ppermute | solution.py:176
  131.3 6.2 %collective-permute-start.33 = (bf16[240,192]{1,0:T(8,128)(2,1)S(1)}, bf16[240,192]{1,0:T(8,128)(2,1)}, u32[]{:S(2)}, u32[]{:S(2)}) collective-permute-start(bf16[240,192]{1,0:T(8,128)(2,1)S(1)} %get-tuple-element.34), channel_id=1, source_target_pairs={{0,2},{4,0},{8,4},{12,8},{14,12},{10,14},{6,10},{2,6},{1,3},{5,1},... | collective-permute-start | bytes 276488 | tf_op jit(solution)/shard_map/ppermute | solution.py:176
  131.3 10.1 %collective-permute-start.19 = (bf16[128,1280]{1,0:T(8,128)(2,1)S(1)}, bf16[128,1280]{1,0:T(8,128)(2,1)}, u32[]{:S(2)}, u32[]{:S(2)}) collective-permute-start(bf16[128,1280]{1,0:T(8,128)(2,1)S(1)} %fusion.41), channel_id=1, source_target_pairs={{0,4},{4,8},{8,12},{12,14},{14,10},{10,6},{6,2},{2,0},{1,5},{5,9},... | collective-permute-start | bytes 983048 | tf_op jit(solution)/shard_map/ppermute | solution.py:119
  139.4 6.4 %copy-start.13 = (bf16[1024,512]{0,1:T(8,128)(2,1)S(1)}, bf16[1024,512]{0,1:T(8,128)(2,1)}, u32[]{:S(2)}) copy-start(bf16[1024,512]{0,1:T(8,128)(2,1)} %copy-done.12) | copy-start | bytes 3145732
  139.4 6.4 %copy-start.15 = (bf16[4,128,1024]{1,2,0:T(8,128)(2,1)S(1)}, bf16[4,128,1024]{1,2,0:T(8,128)(2,1)}, u32[]{:S(2)}) copy-start(bf16[4,128,1024]{1,2,0:T(8,128)(2,1)} %copy-done.14) | copy-start | bytes 3145732
  139.4 7.6 %collective-permute-start.27 = (bf16[240,192]{1,0:T(8,128)(2,1)}, bf16[240,192]{1,0:T(8,128)(2,1)S(1)}, u32[]{:S(2)}, u32[]{:S(2)}) collective-permute-start(bf16[240,192]{1,0:T(8,128)(2,1)} %get-tuple-element.31), channel_id=1, source_target_pairs={{0,4},{4,8},{8,12},{12,14},{14,10},{10,6},{6,2},{2,0},{1,5},{5,9},... | collective-permute-start | bytes 276488 | tf_op jit(solution)/shard_map/ppermute | solution.py:176
  139.5 7.5 %collective-permute-start.34 = (bf16[240,192]{1,0:T(8,128)(2,1)}, bf16[240,192]{1,0:T(8,128)(2,1)}, u32[]{:S(2)}, u32[]{:S(2)}) collective-permute-start(bf16[240,192]{1,0:T(8,128)(2,1)} %get-tuple-element.32), channel_id=1, source_target_pairs={{0,2},{4,0},{8,4},{12,8},{14,12},{10,14},{6,10},{2,6},{1,3},{5,1},... | collective-permute-start | bytes 276488 | tf_op jit(solution)/shard_map/ppermute | solution.py:176
  143.8 8.3 %collective-permute-start.16 = (bf16[128,1280]{1,0:T(8,128)(2,1)}, bf16[128,1280]{1,0:T(8,128)(2,1)S(1)}, u32[]{:S(2)}, u32[]{:S(2)}) collective-permute-start(bf16[128,1280]{1,0:T(8,128)(2,1)} %get-tuple-element.45), channel_id=1, source_target_pairs={{0,2},{4,0},{8,4},{12,8},{14,12},{10,14},{6,10},{2,6},{1,3},{5,1},... | collective-permute-start | bytes 983048 | tf_op jit(solution)/shard_map/ppermute | solution.py:119
  143.8 10.6 %collective-permute-start.20 = (bf16[128,1280]{1,0:T(8,128)(2,1)}, bf16[128,1280]{1,0:T(8,128)(2,1)}, u32[]{:S(2)}, u32[]{:S(2)}) collective-permute-start(bf16[128,1280]{1,0:T(8,128)(2,1)} %get-tuple-element.46), channel_id=1, source_target_pairs={{0,4},{4,8},{8,12},{12,14},{14,10},{10,6},{6,2},{2,0},{1,5},{5,9},... | collective-permute-start | bytes 983048 | tf_op jit(solution)/shard_map/ppermute | solution.py:119
  148.3 9.6 %collective-permute-start.28 = (bf16[240,192]{1,0:T(8,128)(2,1)S(1)}, bf16[240,192]{1,0:T(8,128)(2,1)S(1)}, u32[]{:S(2)}, u32[]{:S(2)}) collective-permute-start(bf16[240,192]{1,0:T(8,128)(2,1)S(1)} %get-tuple-element.29), channel_id=1, source_target_pairs={{0,4},{4,8},{8,12},{12,14},{14,10},{10,6},{6,2},{2,0},{1,5},{5,9},... | collective-permute-start | bytes 276488 | tf_op jit(solution)/shard_map/ppermute | solution.py:176
  149.0 15.5 %copy-start.2 = (bf16[1024,768]{1,0:T(8,128)(2,1)S(1)}, bf16[1024,768]{1,0:T(8,128)(2,1)}, u32[]{:S(2)}) copy-start(bf16[1024,768]{1,0:T(8,128)(2,1)} %copy.55) | copy-start | bytes 4718596
  149.0 15.5 %copy-start.6 = (bf16[1024,512]{1,0:T(8,128)(2,1)S(1)}, bf16[1024,512]{1,0:T(8,128)(2,1)}, u32[]{:S(2)}) copy-start(bf16[1024,512]{1,0:T(8,128)(2,1)} %copy.54) | copy-start | bytes 3145732
  149.0 8.9 %collective-permute-start.35 = (bf16[240,192]{1,0:T(8,128)(2,1)S(1)}, bf16[240,192]{1,0:T(8,128)(2,1)S(1)}, u32[]{:S(2)}, u32[]{:S(2)}) collective-permute-start(bf16[240,192]{1,0:T(8,128)(2,1)S(1)} %get-tuple-element.30), channel_id=1, source_target_pairs={{0,2},{4,0},{8,4},{12,8},{14,12},{10,14},{6,10},{2,6},{1,3},{5,1},... | collective-permute-start | bytes 276488 | tf_op jit(solution)/shard_map/ppermute | solution.py:176
  155.8 7.1 %collective-permute-start.21 = (bf16[128,1280]{1,0:T(8,128)(2,1)S(1)}, bf16[128,1280]{1,0:T(8,128)(2,1)S(1)}, u32[]{:S(2)}, u32[]{:S(2)}) collective-permute-start(bf16[128,1280]{1,0:T(8,128)(2,1)S(1)} %get-tuple-element.44), channel_id=1, source_target_pairs={{0,4},{4,8},{8,12},{12,14},{14,10},{10,6},{6,2},{2,0},{1,5},{5,9},... | collective-permute-start | bytes 983048 | tf_op jit(solution)/shard_map/ppermute | solution.py:119
  157.4 7.1 %collective-permute-start.17 = (bf16[128,1280]{1,0:T(8,128)(2,1)S(1)}, bf16[128,1280]{1,0:T(8,128)(2,1)S(1)}, u32[]{:S(2)}, u32[]{:S(2)}) collective-permute-start(bf16[128,1280]{1,0:T(8,128)(2,1)S(1)} %get-tuple-element.43), channel_id=1, source_target_pairs={{0,2},{4,0},{8,4},{12,8},{14,12},{10,14},{6,10},{2,6},{1,3},{5,1},... | collective-permute-start | bytes 983048 | tf_op jit(solution)/shard_map/ppermute | solution.py:119
  (15 other events, 36.9 us)

commit v11 on v8

--- a/solution.py
+++ b/solution.py
@@ -180,12 +180,45 @@
     return acc
 
 
+def neighbor_rows(array, width):
+    count = lax.axis_size("seq")
+    up = [(i, i + 1) for i in range(count - 1)]
+    down = [(j, i) for i, j in up]
+    before = lax.ppermute(array[-width:], "seq", up)
+    after = lax.ppermute(array[:width], "seq", down)
+    return before, after
+
+
+def attend_rows(query_rows, all_keys, all_values, score_scale):
+    scores = (
+        jnp.einsum(
+            "ihd,jhd->hij",
+            query_rows.reshape(query_rows.shape[0], H, DK),
+            all_keys,
+            preferred_element_type=jnp.float32,
+        )
+        * score_scale
+    )
+    row_peak = jnp.max(scores, axis=2, keepdims=True)
+    row_total = jnp.sum(jnp.exp(scores - row_peak), axis=2, keepdims=True)
+    rounded = jnp.exp(scores - (row_peak + jnp.log(row_total))).astype(jnp.bfloat16)
+    return jnp.einsum(
+        "hij,jhd->ihd", rounded, all_values, preferred_element_type=jnp.float32
+    ).astype(jnp.bfloat16)
+
+
 def body(ring, queries, key_rows, value_rows, trunk_state, skip_input, norm_gain, conv_weight, cotangent):
     score_scale = DK ** (-0.5)
     local_tokens = queries.shape[1]
     positions = 2 * local_tokens
     half_kernel = KW // 2
     query_heads = queries[0].reshape(local_tokens, H, DK)
+    seq_index, seq_total = lax.axis_index("seq"), lax.axis_size("seq")
+    halo_tokens = half_kernel
+    query_before, query_after = neighbor_rows(queries[0], halo_tokens)
+    trunk_before, trunk_after = neighbor_rows(trunk_state[0], halo_tokens)
+    skip_before, skip_after = neighbor_rows(skip_input[0], 2 * halo_tokens)
+    cotangent_before, cotangent_after = neighbor_rows(cotangent[0], half_kernel)
     key_value_blocks = ring_gather(jnp.concatenate([key_rows[0], value_rows[0]], axis=1), ring)
     gathered = jnp.concatenate(key_value_blocks, axis=0)
     all_keys = gathered[:, : H * DK].reshape(-1, H, DK)
@@ -215,13 +248,62 @@
     inverse = lax.rsqrt(jnp.mean(merged * merged, axis=1, keepdims=True) + 1e-06)
     channel_gain = norm_gain.astype(jnp.float32)
     normed = (merged * inverse * channel_gain).astype(jnp.bfloat16)
-    padded = extended(normed, (("seq", 0),), half_kernel)
+    halo_attended = attend_rows(
+        jnp.concatenate([query_before, query_after], axis=0), all_keys, all_values, score_scale
+    ).reshape(2 * halo_tokens, H * DV)
+    halo_hidden = jnp.concatenate([trunk_before, trunk_after], axis=0).astype(
+        jnp.float32
+    ) + halo_attended.astype(jnp.float32)
+    halo_merged = jnp.repeat(halo_hidden, 2, axis=0) + jnp.concatenate(
+        [skip_before, skip_after], axis=0
+    ).astype(jnp.float32)
+    halo_inverse = lax.rsqrt(jnp.mean(halo_merged * halo_merged, axis=1, keepdims=True) + 1e-06)
+    halo_rows = 2 * halo_tokens
+    halo_valid = jnp.concatenate(
+        [
+            jnp.broadcast_to(seq_index > 0, (halo_rows,)),
+            jnp.broadcast_to(seq_index < seq_total - 1, (halo_rows,)),
+        ]
+    )
+    halo_normed = jnp.where(
+        halo_valid[:, None], halo_merged * halo_inverse * channel_gain, 0.0
+    ).astype(jnp.bfloat16)
+    normed_before, normed_after = halo_normed[:halo_rows], halo_normed[halo_rows:]
+    padded = jnp.concatenate(
+        [normed_before[halo_rows - half_kernel :], normed, normed_after[:half_kernel]], axis=0
+    )
     columns = window_rows(padded, KW, positions)
     preact = jnp.dot(columns, conv_weight, preferred_element_type=jnp.float32)
     activated, derivative = gelu_parts(preact)
     decoded = activated.astype(jnp.bfloat16)
     grad_pre = (cotangent[0].astype(jnp.float32) * derivative).astype(jnp.bfloat16)
-    grad_padded = extended(grad_pre, (("seq", 0),), half_kernel)
+    halo_columns = jnp.concatenate(
+        [
+            window_rows(
+                jnp.concatenate([normed_before, normed[:half_kernel]], axis=0)[
+                    halo_rows - 2 * half_kernel :
+                ],
+                KW,
+                half_kernel,
+            ),
+            window_rows(
+                jnp.concatenate([normed[positions - half_kernel :], normed_after], axis=0)[
+                    : 4 * half_kernel
+                ],
+                KW,
+                half_kernel,
+            ),
+        ],
+        axis=0,
+    )
+    halo_preact = jnp.dot(halo_columns, conv_weight, preferred_element_type=jnp.float32)
+    halo_grad = (
+        jnp.concatenate([cotangent_before, cotangent_after], axis=0).astype(jnp.float32)
+        * gelu_parts(halo_preact)[1]
+    ).astype(jnp.bfloat16)
+    grad_padded = jnp.concatenate(
+        [halo_grad[:half_kernel], grad_pre, halo_grad[half_kernel:]], axis=0
+    )
     norm_scale = (lax.axis_size("dp") * positions * lax.axis_size("seq")) ** (-0.5)
     seq_count, dp_count = lax.axis_size("seq"), lax.axis_size("dp")
     rows_per = KW * C // (seq_count * dp_count)

time: 159 us -> 168 us (1.057)
  starting transfers between devices: 45.4 us -> 59.7 us
  waiting for transfers between devices: 44.8 us -> 30.7 us
  local copies, waits for them, and re-layouts: 24 us -> 27.9 us
  matrix products: 24.7 us -> 28.2 us
    ppermute x4 -> x8, starting transfers between devices: 11.2 us -> 22.6 us  [the longest x4 17.5 us: neighbor_rows(): before = lax.ppermute(array[-width:], 'seq', up)]
    ppermute x3, waiting for transfers between devices: 12.7 us -> 3.72 us  [ring_gather(): current = lax.ppermute(current, 'seq', forward)]
    ppermute x3, starting transfers between devices: 6.37 us -> 10.4 us  [ring_gather(): current = lax.ppermute(current, 'seq', forward)]
    ppermute x4 -> x8, waiting for transfers between devices: 3.83 us -> 0.02 us  [the longest x4 0.01 us: neighbor_rows(): after = lax.ppermute(array[:width], 'seq', down)]
    slice x2 -> x7, local copies, waits for them, and re-layouts: 0.02 us -> 3.49 us  [the longest x4 3.47 us: neighbor_rows(): before = lax.ppermute(array[-width:], 'seq', up)]
    ppermute x14, waiting for transfers between devices: 19.8 us -> 16.6 us  [ring_reduce_scatter_sliced(): received = lax.ppermute(acc, axis, perm).astype(jnp.float32)]
    ppermute x8, waiting for transfers between devices: 2.97 us -> 4.77 us  [ring_scatter_back(): received = lax.ppermute(acc, 'seq', perm).astype(jnp.float32)]
    unnamed x60 -> x55, local copies, waits for them, and re-layouts: 9.79 us -> 10 us
  transfers between devices with their start and end apart: 36 -> 40, of which waited for: 20 -> 20; matrix products, arithmetic and copies ran while one was open for 27% -> 35% of each run, Pallas kernels for 0% -> 0%
where the time goes in v11:
time: 168 us; the launch traced here: 167 us
  starting transfers between devices  59.7 us (36%)
  waiting for transfers between devices  30.7 us (18%)
  matrix products  28.2 us (17%)
  local copies, waits for them, and re-layouts  27.9 us (17%)
  other arithmetic  18.2 us (11%)
  between operations  1.83 us (1%)
    ppermute x4, starting transfers between devices, neighbor_rows(): before = lax.ppermute(array[-width:], 'seq', up)  17.5 us
    ppermute x14, waiting for transfers between devices, ring_reduce_scatter_sliced(): received = lax.ppermute(acc, axis, perm).astype(jnp.float32)  16.6 us
    ppermute x14, starting transfers between devices, ring_reduce_scatter_sliced(): received = lax.ppermute(acc, axis, perm).astype(jnp.float32)  15.5 us
    ppermute x3, starting transfers between devices, ring_gather(): current = lax.ppermute(current, 'seq', forward)  10.4 us
    unnamed x55, local copies, waits for them, and re-layouts  10 us
    ppermute x8, starting transfers between devices, ring_scatter_back(): received = lax.ppermute(acc, 'seq', perm).astype(jnp.float32)  8.51 us
    dot_general x5, matrix products, body(): jnp.einsum('spc,spo->co', both_padded[:, offset:offset + positions], both...  8.32 us
    ppermute x3, waiting for transfers between devices, ring_gather(): current = lax.ppermute(current, 'seq', backward)  5.43 us
  transfers between devices with their start and end apart: 40, of which 20 were waited for; matrix products, arithmetic and copies ran while one was open for 35% of the time, Pallas kernels for 0%

profile of v11, /device:TPU:0, one launch (start us, length us, event | category | flops | bytes accessed | tf_op | source)
XLA Modules:
  0.0 166.5 jit_solution(10146424370765394890)
XLA Ops:
  3.9 3.1 %collective-permute-start.2 = (bf16[128,1280]{0,1:T(8,128)(2,1)}, bf16[128,1280]{0,1:T(8,128)(2,1)}, u32[]{:S(2)}, u32[]{:S(2)}) collective-permute-start(bf16[128,1280]{0,1:T(8,128)(2,1)} %get-tuple-element.57), channel_id=1, source_target_pairs={{0,4},{4,8},{8,12},{12,14},{14,10},{10,6},{6,2},{2,0},{1,5},{5,9},... | collective-permute-start | bytes 983048 | tf_op jit(solution)/shard_map/ppermute | solution.py:76
  8.9 4.5 %collective-permute-start.10 = (bf16[2,512]{1,0:T(2,128)(2,1)S(1)}, bf16[2,512]{1,0:T(2,128)(2,1)S(1)}, u32[]{:S(2)}, u32[]{:S(2)}) collective-permute-start(bf16[2,512]{1,0:T(2,128)(2,1)S(1)} %get-tuple-element.63), channel_id=1, source_target_pairs={{0,2},{2,4},{4,6},{6,8},{8,10},{10,12},{12,14},{1,3},{3,5},{5,7},{... | collective-permute-start | bytes 6152 | tf_op jit(solution)/shard_map/ppermute | solution.py:187
  19.2 5.0 %collective-permute-start.3 = (bf16[128,1280]{0,1:T(8,128)(2,1)}, bf16[128,1280]{0,1:T(8,128)(2,1)S(1)}, u32[]{:S(2)}, u32[]{:S(2)}) collective-permute-start(bf16[128,1280]{0,1:T(8,128)(2,1)} %collective-permute-done.2), channel_id=1, source_target_pairs={{0,4},{4,8},{8,12},{12,14},{14,10},{10,6},{6,2},{2,0},{1,5},{5,9},... | collective-permute-start | bytes 983048 | tf_op jit(solution)/shard_map/ppermute | solution.py:76
  24.2 2.2 %fusion.67 = f32[256,768]{1,0:T(8,128)} fusion(bf16[1,128,768]{2,1,0:T(8,128)(2,1)} %param.11, s32[256]{0:T(256)S(1)} %and_select_fusion), kind=kOutput, calls=%fused_computation.158 | convolution fusion | flops 50364416 | bytes 984064 | tf_op jit(solution)/shard_map/dot_general | solution.py:242
  26.3 3.7 %collective-permute-done.3 = bf16[128,1280]{0,1:T(8,128)(2,1)S(1)} collective-permute-done((bf16[128,1280]{0,1:T(8,128)(2,1)}, bf16[128,1280]{0,1:T(8,128)(2,1)S(1)}, u32[]{:S(2)}, u32[]{:S(2)}) %collective-permute-start.3) | collective-permute-done | bytes 327712 | tf_op jit(solution)/shard_map/ppermute | solution.py:76
  30.0 2.4 %collective-permute-start.4 = (bf16[128,1280]{0,1:T(8,128)(2,1)S(1)}, bf16[128,1280]{0,1:T(8,128)(2,1)S(1)}, u32[]{:S(2)}, u32[]{:S(2)}) collective-permute-start(bf16[128,1280]{0,1:T(8,128)(2,1)S(1)} %collective-permute-done.3), channel_id=1, source_target_pairs={{0,4},{4,8},{8,12},{12,14},{14,10},{10,6},{6,2},{2,0},{1,5},{5,9},... | collective-permute-start | bytes 983048 | tf_op jit(solution)/shard_map/ppermute | solution.py:76
  32.4 1.8 %constant_dynamic-update-slice_fusion.5 = bf16[1024,1280]{0,1:T(8,128)(2,1)} fusion(bf16[1024,1280]{0,1:T(8,128)(2,1)} %get-tuple-element.58, bf16[128,1280]{0,1:T(8,128)(2,1)} %collective-permute-done.2), kind=kLoop, calls=%fused_computation.171 | loop fusion | bytes 655360
  35.0 5.4 %collective-permute-done.7 = bf16[128,1280]{0,1:T(8,128)(2,1)S(1)} collective-permute-done((bf16[128,1280]{0,1:T(8,128)(2,1)S(1)}, bf16[128,1280]{0,1:T(8,128)(2,1)S(1)}, u32[]{:S(2)}, u32[]{:S(2)}) %collective-permute-start.7) | collective-permute-done | bytes 327712 | tf_op jit(solution)/shard_map/ppermute | solution.py:82
  40.5 2.1 %collective-permute-start.8 = (bf16[128,640]{0,1:T(8,128)(2,1)S(1)}, bf16[128,640]{0,1:T(8,128)(2,1)S(1)}, u32[]{:S(2)}, u32[]{:S(2)}) collective-permute-start(bf16[128,640]{0,1:T(8,128)(2,1)S(1)} %slice.280), channel_id=1, source_target_pairs={{0,4},{4,8},{8,12},{12,14},{14,10},{10,6},{6,2},{2,0},{1,5},{5,9},... | collective-permute-start | bytes 491528 | tf_op jit(solution)/shard_map/ppermute | solution.py:79
  45.8 1.9 %collective-permute-start = (bf16[2,768]{1,0:T(2,128)(2,1)S(1)}, bf16[2,768]{1,0:T(2,128)(2,1)S(1)}, u32[]{:S(2)}, u32[]{:S(2)}) collective-permute-start(bf16[2,768]{1,0:T(2,128)(2,1)S(1)} %get-tuple-element.61), channel_id=1, source_target_pairs={{0,2},{2,4},{4,6},{6,8},{8,10},{10,12},{12,14},{1,3},{3,5},{5,7},{... | collective-permute-start | bytes 9224 | tf_op jit(solution)/shard_map/ppermute | solution.py:187
  49.8 1.5 slice.282
  51.4 1.9 %slice.283 = bf16[1024,512]{0,1:T(8,128)(2,1)S(1)} slice(bf16[1024,1280]{0,1:T(8,128)(2,1)} %maximum_dynamic-update-slice_fusion), slice={[0:1024], [0:512]} | slice | bytes 2097152 | tf_op jit(solution)/shard_map/slice | solution.py:224
  53.3 5.5 %collective-permute-start.12 = (bf16[4,768]{1,0:T(4,128)(2,1)S(1)}, bf16[4,768]{1,0:T(4,128)(2,1)S(1)}, u32[]{:S(2)}, u32[]{:S(2)}) collective-permute-start(bf16[4,768]{1,0:T(4,128)(2,1)S(1)} %get-tuple-element.55), channel_id=1, source_target_pairs={{0,2},{2,4},{4,6},{6,8},{8,10},{10,12},{12,14},{1,3},{3,5},{5,7},{... | collective-permute-start | bytes 18440 | tf_op jit(solution)/shard_map/ppermute | solution.py:187
  61.3 5.4 %collective-permute-start.14 = (bf16[2,384]{1,0:T(2,128)(2,1)S(1)}, bf16[2,384]{1,0:T(2,128)(2,1)S(1)}, u32[]{:S(2)}, u32[]{:S(2)}) collective-permute-start(bf16[2,384]{1,0:T(2,128)(2,1)S(1)} %get-tuple-element.59), channel_id=1, source_target_pairs={{0,2},{2,4},{4,6},{6,8},{8,10},{10,12},{12,14},{1,3},{3,5},{5,7},{... | collective-permute-start | bytes 4616 | tf_op jit(solution)/shard_map/ppermute | solution.py:187
  67.2 1.9 %bitcast_reduce_fusion = (f32[4,128]{1,0:T(4,128)S(1)}, f32[4,1024,128]{2,1,0:T(8,128)S(1)}) fusion(bf16[1024,4,128]{0,2,1:T(8,128)(2,1)} %bitcast.206, bf16[128,4,128]{0,2,1:T(8,128)(2,1)S(1)} %bitcast.227), kind=kOutput, calls=%fused_computation.17 | convolution fusion | flops 135265792 | bytes 3278848 | tf_op jit(solution)/shard_map/ihd,jhd->hij/dot_general | solution.py:227
  72.6 2.0 %fusion.34 = (bf16[256,384]{1,0:T(8,128)(2,1)S(1)}, bf16[1,256,384]{2,1,0:T(8,128)(2,1)}) fusion(bf16[1,256,384]{2,1,0:T(8,128)(2,1)S(1)} %copy-done.19, bf16[256,3840]{1,0:T(8,128)(2,1)S(1)} %fusion.35, bf16[3840,384]{1,0:T(8,128)(2,1)S(1)} %copy-done), kind=kOutput, calls=%fused_computation.88 | convolution fusion | flops 756252672 | bytes 5505024 | tf_op jit(solution)/shard_map/dot_general | solution.py:276
  80.9 4.2 %multiply_convert_fusion.1 = bf16[4,128,1024]{1,2,0:T(8,128)(2,1)} fusion(f32[4,1024,128]{2,1,0:T(8,128)} %copy-done.3, bf16[128,4,192]{0,2,1:T(8,128)(2,1)S(1)} %bitcast.224, bf16[1024,4,192]{0,2,1:T(8,128)(2,1)} %bitcast.203, f32[4,128]{1,0:T(4,128)S(1)} %bitcast.233, f32[4,128]{1,0:T(4,128)S(1)} %log_add_fusion), kind=kOutput, calls=%fused_computation.22 | convolution fusion | flops 203948032 | bytes 4919296 | tf_op jit(solution)/shard_map/ihd,jhd->hij/dot_general | solution.py:388
  85.7 1.8 %convolution_convert_fusion = bf16[4,192,1024]{2,1,0:T(8,128)(2,1)} fusion(bf16[128,4,192]{0,2,1:T(8,128)(2,1)S(1)} %bitcast.225, f32[4,1024,128]{2,1,0:T(8,128)S(1)} %copy-done.4, f32[4,128]{1,0:T(4,128)S(1)} %log_add_fusion), kind=kOutput, calls=%fused_computation.24 | convolution fusion | flops 203685888 | bytes 3868672 | tf_op jit(solution)/shard_map/hij,ihd->jhd/dot_general | solution.py:400
  87.4 2.7 %copy.52 = bf16[1024,768]{1,0:T(8,128)(2,1)} copy(bf16[1024,768]{0,1:T(8,128)(2,1)} %bitcast.216) | data formatting | bytes 3145728 | tf_op jit(solution)/shard_map/reshape | solution.py:404
  90.1 2.6 %fusion.9 = bf16[1024,4,128]{2,0,1:T(8,128)(2,1)} fusion(bf16[4,128,1024]{1,2,0:T(8,128)(2,1)} %multiply_convert_fusion.1, bf16[128,4,128]{0,2,1:T(8,128)(2,1)S(1)} %bitcast.228), kind=kOutput, calls=%fused_computation.35 | convolution fusion | flops 135266304 | bytes 2228224 | tf_op jit(solution)/shard_map/hij,ihd->jhd/dot_general | solution.py:397
  92.8 2.3 %copy.49 = bf16[1024,4,128]{0,2,1:T(8,128)(2,1)} copy(bf16[1024,4,128]{2,0,1:T(8,128)(2,1)} %fusion.9) | data formatting | bytes 2097152 | tf_op jit(solution)/shard_map/mul | solution.py:397
  95.1 2.3 %copy.51 = bf16[1024,512]{1,0:T(8,128)(2,1)} copy(bf16[1024,512]{0,1:T(8,128)(2,1)} %bitcast.222) | data formatting | bytes 2097152 | tf_op jit(solution)/shard_map/reshape | solution.py:403
  97.4 1.6 fusion.8
  99.0 1.7 %fusion.7 = f32[3840,384]{1,0:T(8,128)S(1)} fusion(f32[3840,384]{1,0:T(8,128)S(1)} %fusion.8, bf16[1,260,768]{2,1,0:T(8,128)(2,1)S(1)} %copy-done.17, bf16[1,260,768]{2,1,0:T(8,128)(2,1)} %bitcast.42, bf16[1,256,384]{2,1,0:T(8,128)(2,1)} %bitcast.44, bf16[1,256,384]{2,1,0:T(8,128)(2,1)S(1)} %bitcast.218), kind=kOutput, calls=%fused_computation.32 | convolution fusion | flops 302579712 | bytes 2377728 | tf_op jit(solution)/shard_map/spc,spo->co/dot_general | solution.py:318
  100.7 1.7 %fusion.6 = f32[3840,384]{1,0:T(8,128)S(1)} fusion(f32[3840,384]{1,0:T(8,128)S(1)} %fusion.7, bf16[1,260,768]{2,1,0:T(8,128)(2,1)S(1)} %copy-done.17, bf16[1,260,768]{2,1,0:T(8,128)(2,1)} %bitcast.42, bf16[1,256,384]{2,1,0:T(8,128)(2,1)} %bitcast.44, bf16[1,256,384]{2,1,0:T(8,128)(2,1)S(1)} %bitcast.219), kind=kOutput, calls=%fused_computation.30 | convolution fusion | flops 302579712 | bytes 2377728 | tf_op jit(solution)/shard_map/spc,spo->co/dot_general | solution.py:318
  102.4 1.7 %fusion.5 = f32[3840,384]{1,0:T(8,128)S(1)} fusion(f32[3840,384]{1,0:T(8,128)S(1)} %fusion.6, bf16[1,260,768]{2,1,0:T(8,128)(2,1)S(1)} %copy-done.17, bf16[1,260,768]{2,1,0:T(8,128)(2,1)} %bitcast.42, bf16[1,256,384]{2,1,0:T(8,128)(2,1)} %bitcast.44, bf16[1,256,384]{2,1,0:T(8,128)(2,1)S(1)} %bitcast.220), kind=kOutput, calls=%fused_computation.28 | convolution fusion | flops 302579712 | bytes 2377728 | tf_op jit(solution)/shard_map/spc,spo->co/dot_general | solution.py:318
  104.0 1.7 fusion.4
  106.2 1.6 collective-permute-start.26
  107.9 1.4 collective-permute-start.33
  109.3 2.0 %collective-permute-start.16 = (bf16[128,640]{1,0:T(8,128)(2,1)S(1)}, bf16[128,640]{1,0:T(8,128)(2,1)S(1)}, u32[]{:S(2)}, u32[]{:S(2)}) collective-permute-start(bf16[128,640]{1,0:T(8,128)(2,1)S(1)} %get-tuple-element.45), channel_id=1, source_target_pairs={{0,2},{4,0},{8,4},{12,8},{14,12},{10,14},{6,10},{2,6},{1,3},{5,1},... | collective-permute-start | bytes 491528 | tf_op jit(solution)/shard_map/ppermute | solution.py:119
  111.4 1.3 collective-permute-done.26
  114.1 1.6 collective-permute-start.27
  117.0 1.4 collective-permute-done.20
  120.9 2.0 %collective-permute-start.35 = (bf16[240,192]{1,0:T(8,128)(2,1)S(1)}, bf16[240,192]{1,0:T(8,128)(2,1)S(1)}, u32[]{:S(2)}, u32[]{:S(2)}) collective-permute-start(bf16[240,192]{1,0:T(8,128)(2,1)S(1)} %get-tuple-element.34), channel_id=1, source_target_pairs={{0,2},{4,0},{8,4},{12,8},{14,12},{10,14},{6,10},{2,6},{1,3},{5,1},... | collective-permute-start | bytes 276488 | tf_op jit(solution)/shard_map/ppermute | solution.py:176
  124.4 1.3 collective-permute-done.28
  125.7 1.4 collective-permute-done.35
  127.8 1.5 collective-permute-start.29
  129.9 1.6 collective-permute-start.21
  131.4 1.5 collective-permute-done.29
  132.9 2.1 %collective-permute-done.36 = bf16[240,192]{1,0:T(8,128)(2,1)} collective-permute-done((bf16[240,192]{1,0:T(8,128)(2,1)S(1)}, bf16[240,192]{1,0:T(8,128)(2,1)}, u32[]{:S(2)}, u32[]{:S(2)}) %collective-permute-start.36) | collective-permute-done | bytes 92192 | tf_op jit(solution)/shard_map/ppermute | solution.py:176
  137.0 1.4 collective-permute-start.37
  138.3 2.3 %add_convert_fusion.4 = (bf16[128,1280]{1,0:T(8,128)(2,1)}, bf16[128,1280]{1,0:T(8,128)(2,1)}) fusion(bf16[128,1280]{1,0:T(8,128)(2,1)} %collective-permute-done.17, bf16[1024,768]{1,0:T(8,128)(2,1)} %copy.52, bf16[1024,512]{1,0:T(8,128)(2,1)} %copy.51, bf16[128,1280]{1,0:T(8,128)(2,1)} %collective-permute-done.21), kind=kLoop, calls=%fused_computation.71 | loop fusion | flops 2293760 | bytes 3932160 | tf_op jit(solution)/shard_map/convert_element_type | solution.py:123
  140.6 1.6 collective-permute-start.18
  142.9 1.8 %fusion.51 = (bf16[240,192]{1,0:T(8,128)(2,1)}, bf16[240,192]{1,0:T(8,128)(2,1)}) fusion(f32[8,2,240,384]{3,2,1,0:T(8,128)} %bitcast.213, s32[]{:T(128)S(6)} %select_n.543, s32[]{:T(128)S(6)} %select_n.503, bf16[240,192]{1,0:T(8,128)(2,1)S(1)} %collective-permute-done.30, s32[]{:T(128)S(6)} %select_n.607, bf16[240,192]{1,0:T(8,128)(2,1)S(1)} %collective-permute-done.37), kind=kLoop, calls=%fused_computation.128 | loop fusion | flops 276480 | bytes 737292 | tf_op jit(solution)/shard_map/convert_element_type | solution.py:179
  144.7 2.1 %collective-permute-start.31 = (bf16[240,192]{1,0:T(8,128)(2,1)}, bf16[240,192]{1,0:T(8,128)(2,1)S(1)}, u32[]{:S(2)}, u32[]{:S(2)}) collective-permute-start(bf16[240,192]{1,0:T(8,128)(2,1)} %get-tuple-element.27), channel_id=1, source_target_pairs={{0,4},{4,8},{8,12},{12,14},{14,10},{10,6},{6,2},{2,0},{1,5},{5,9},... | collective-permute-start | bytes 276488 | tf_op jit(solution)/shard_map/ppermute | solution.py:176
  148.1 3.5 %collective-permute-done.31 = bf16[240,192]{1,0:T(8,128)(2,1)S(1)} collective-permute-done((bf16[240,192]{1,0:T(8,128)(2,1)}, bf16[240,192]{1,0:T(8,128)(2,1)S(1)}, u32[]{:S(2)}, u32[]{:S(2)}) %collective-permute-start.31) | collective-permute-done | bytes 92192 | tf_op jit(solution)/shard_map/ppermute | solution.py:176
  155.5 1.4 add_convert_fusion.3
  162.5 1.9 %collective-permute-done.23 = bf16[128,1280]{1,0:T(8,128)(2,1)S(1)} collective-permute-done((bf16[128,1280]{1,0:T(8,128)(2,1)S(1)}, bf16[128,1280]{1,0:T(8,128)(2,1)S(1)}, u32[]{:S(2)}, u32[]{:S(2)}) %collective-permute-start.23) | collective-permute-done | bytes 327712 | tf_op jit(solution)/shard_map/ppermute | solution.py:119
  (178 shorter events, 53.4 us)
Async XLA Ops:
  0.6 71.7 %copy-start = (bf16[3840,384]{1,0:T(8,128)(2,1)S(1)}, bf16[3840,384]{1,0:T(8,128)(2,1)}, u32[]{:S(2)}) copy-start(bf16[3840,384]{1,0:T(8,128)(2,1)} %param.14) | copy-start | bytes 8847364
  0.6 17.4 %copy-start.18 = (bf16[768]{0:T(1024)(128)(2,1)S(1)}, bf16[768]{0:T(1024)(128)(2,1)}, u32[]{:S(2)}) copy-start(bf16[768]{0:T(1024)(128)(2,1)} %param.13) | copy-start | bytes 4612
  3.9 15.3 %collective-permute-start.2 = (bf16[128,1280]{0,1:T(8,128)(2,1)}, bf16[128,1280]{0,1:T(8,128)(2,1)}, u32[]{:S(2)}, u32[]{:S(2)}) collective-permute-start(bf16[128,1280]{0,1:T(8,128)(2,1)} %get-tuple-element.57), channel_id=1, source_target_pairs={{0,4},{4,8},{8,12},{12,14},{14,10},{10,6},{6,2},{2,0},{1,5},{5,9},... | collective-permute-start | bytes 983048 | tf_op jit(solution)/shard_map/ppermute | solution.py:76
  6.9 17.2 %collective-permute-start.5 = (bf16[128,1280]{0,1:T(8,128)(2,1)}, bf16[128,1280]{0,1:T(8,128)(2,1)S(1)}, u32[]{:S(2)}, u32[]{:S(2)}) collective-permute-start(bf16[128,1280]{0,1:T(8,128)(2,1)} %get-tuple-element.57), channel_id=1, source_target_pairs={{0,2},{4,0},{8,4},{12,8},{14,12},{10,14},{6,10},{2,6},{1,3},{5,1},... | collective-permute-start | bytes 983048 | tf_op jit(solution)/shard_map/ppermute | solution.py:82
  7.6 45.6 %collective-permute-start.11 = (bf16[2,512]{1,0:T(2,128)(2,1)S(1)}, bf16[2,512]{1,0:T(2,128)(2,1)S(1)}, u32[]{:S(2)}, u32[]{:S(2)}) collective-permute-start(bf16[2,512]{1,0:T(2,128)(2,1)S(1)} %get-tuple-element.64), channel_id=1, source_target_pairs={{2,0},{4,2},{6,4},{8,6},{10,8},{12,10},{14,12},{3,1},{5,3},{7,5},{... | collective-permute-start | bytes 6152 | tf_op jit(solution)/shard_map/ppermute | solution.py:188
  8.9 49.9 %collective-permute-start.10 = (bf16[2,512]{1,0:T(2,128)(2,1)S(1)}, bf16[2,512]{1,0:T(2,128)(2,1)S(1)}, u32[]{:S(2)}, u32[]{:S(2)}) collective-permute-start(bf16[2,512]{1,0:T(2,128)(2,1)S(1)} %get-tuple-element.63), channel_id=1, source_target_pairs={{0,2},{2,4},{4,6},{6,8},{8,10},{10,12},{12,14},{1,3},{3,5},{5,7},{... | collective-permute-start | bytes 6152 | tf_op jit(solution)/shard_map/ppermute | solution.py:187
  14.2 47.1 %collective-permute-start.1 = (bf16[2,768]{1,0:T(2,128)(2,1)S(1)}, bf16[2,768]{1,0:T(2,128)(2,1)S(1)}, u32[]{:S(2)}, u32[]{:S(2)}) collective-permute-start(bf16[2,768]{1,0:T(2,128)(2,1)S(1)} %get-tuple-element.62), channel_id=1, source_target_pairs={{2,0},{4,2},{6,4},{8,6},{10,8},{12,10},{14,12},{3,1},{5,3},{7,5},{... | collective-permute-start | bytes 9224 | tf_op jit(solution)/shard_map/ppermute | solution.py:188
  17.8 49.3 %copy-start.14 = (bf16[1,128,512]{1,2,0:T(8,128)(2,1)}, bf16[1,128,512]{1,2,0:T(8,128)(2,1)S(1)}, u32[]{:S(2)}) copy-start(bf16[1,128,512]{1,2,0:T(8,128)(2,1)S(1)} %copy.75) | copy-start | bytes 393220
  19.2 10.9 %collective-permute-start.3 = (bf16[128,1280]{0,1:T(8,128)(2,1)}, bf16[128,1280]{0,1:T(8,128)(2,1)S(1)}, u32[]{:S(2)}, u32[]{:S(2)}) collective-permute-start(bf16[128,1280]{0,1:T(8,128)(2,1)} %collective-permute-done.2), channel_id=1, source_target_pairs={{0,4},{4,8},{8,12},{12,14},{14,10},{10,6},{6,2},{2,0},{1,5},{5,9},... | collective-permute-start | bytes 983048 | tf_op jit(solution)/shard_map/ppermute | solution.py:76
  24.2 8.3 %collective-permute-start.6 = (bf16[128,1280]{0,1:T(8,128)(2,1)S(1)}, bf16[128,1280]{0,1:T(8,128)(2,1)S(1)}, u32[]{:S(2)}, u32[]{:S(2)}) collective-permute-start(bf16[128,1280]{0,1:T(8,128)(2,1)S(1)} %collective-permute-done.5), channel_id=1, source_target_pairs={{0,2},{4,0},{8,4},{12,8},{14,12},{10,14},{6,10},{2,6},{1,3},{5,1},... | collective-permute-start | bytes 983048 | tf_op jit(solution)/shard_map/ppermute | solution.py:82
  30.0 10.4 %collective-permute-start.4 = (bf16[128,1280]{0,1:T(8,128)(2,1)S(1)}, bf16[128,1280]{0,1:T(8,128)(2,1)S(1)}, u32[]{:S(2)}, u32[]{:S(2)}) collective-permute-start(bf16[128,1280]{0,1:T(8,128)(2,1)S(1)} %collective-permute-done.3), channel_id=1, source_target_pairs={{0,4},{4,8},{8,12},{12,14},{14,10},{10,6},{6,2},{2,0},{1,5},{5,9},... | collective-permute-start | bytes 983048 | tf_op jit(solution)/shard_map/ppermute | solution.py:76
  32.4 8.0 %collective-permute-start.7 = (bf16[128,1280]{0,1:T(8,128)(2,1)S(1)}, bf16[128,1280]{0,1:T(8,128)(2,1)S(1)}, u32[]{:S(2)}, u32[]{:S(2)}) collective-permute-start(bf16[128,1280]{0,1:T(8,128)(2,1)S(1)} %collective-permute-done.6), channel_id=1, source_target_pairs={{0,2},{4,0},{8,4},{12,8},{14,12},{10,14},{6,10},{2,6},{1,3},{5,1},... | collective-permute-start | bytes 983048 | tf_op jit(solution)/shard_map/ppermute | solution.py:82
  40.4 5.4 %collective-permute-start.9 = (bf16[128,640]{0,1:T(8,128)(2,1)S(1)}, bf16[128,640]{0,1:T(8,128)(2,1)S(1)}, u32[]{:S(2)}, u32[]{:S(2)}) collective-permute-start(bf16[128,640]{0,1:T(8,128)(2,1)S(1)} %slice.281), channel_id=1, source_target_pairs={{0,2},{4,0},{8,4},{12,8},{14,12},{10,14},{6,10},{2,6},{1,3},{5,1},... | collective-permute-start | bytes 491528 | tf_op jit(solution)/shard_map/ppermute | solution.py:85
  40.5 7.2 %collective-permute-start.8 = (bf16[128,640]{0,1:T(8,128)(2,1)S(1)}, bf16[128,640]{0,1:T(8,128)(2,1)S(1)}, u32[]{:S(2)}, u32[]{:S(2)}) collective-permute-start(bf16[128,640]{0,1:T(8,128)(2,1)S(1)} %slice.280), channel_id=1, source_target_pairs={{0,4},{4,8},{8,12},{12,14},{14,10},{10,6},{6,2},{2,0},{1,5},{5,9},... | collective-permute-start | bytes 491528 | tf_op jit(solution)/shard_map/ppermute | solution.py:79
  45.8 21.0 %collective-permute-start = (bf16[2,768]{1,0:T(2,128)(2,1)S(1)}, bf16[2,768]{1,0:T(2,128)(2,1)S(1)}, u32[]{:S(2)}, u32[]{:S(2)}) collective-permute-start(bf16[2,768]{1,0:T(2,128)(2,1)S(1)} %get-tuple-element.61), channel_id=1, source_target_pairs={{0,2},{2,4},{4,6},{6,8},{8,10},{10,12},{12,14},{1,3},{3,5},{5,7},{... | collective-permute-start | bytes 9224 | tf_op jit(solution)/shard_map/ppermute | solution.py:187
  47.7 19.1 %collective-permute-start.13 = (bf16[4,768]{1,0:T(4,128)(2,1)S(1)}, bf16[4,768]{1,0:T(4,128)(2,1)S(1)}, u32[]{:S(2)}, u32[]{:S(2)}) collective-permute-start(bf16[4,768]{1,0:T(4,128)(2,1)S(1)} %get-tuple-element.56), channel_id=1, source_target_pairs={{2,0},{4,2},{6,4},{8,6},{10,8},{12,10},{14,12},{3,1},{5,3},{7,5},{... | collective-permute-start | bytes 18440 | tf_op jit(solution)/shard_map/ppermute | solution.py:188
  53.3 13.6 %collective-permute-start.12 = (bf16[4,768]{1,0:T(4,128)(2,1)S(1)}, bf16[4,768]{1,0:T(4,128)(2,1)S(1)}, u32[]{:S(2)}, u32[]{:S(2)}) collective-permute-start(bf16[4,768]{1,0:T(4,128)(2,1)S(1)} %get-tuple-element.55), channel_id=1, source_target_pairs={{0,2},{2,4},{4,6},{6,8},{8,10},{10,12},{12,14},{1,3},{3,5},{5,7},{... | collective-permute-start | bytes 18440 | tf_op jit(solution)/shard_map/ppermute | solution.py:187
  58.8 16.8 %collective-permute-start.15 = (bf16[2,384]{1,0:T(2,128)(2,1)}, bf16[2,384]{1,0:T(2,128)(2,1)S(1)}, u32[]{:S(2)}, u32[]{:S(2)}) collective-permute-start(bf16[2,384]{1,0:T(2,128)(2,1)} %get-tuple-element.60), channel_id=1, source_target_pairs={{2,0},{4,2},{6,4},{8,6},{10,8},{12,10},{14,12},{3,1},{5,3},{7,5},{... | collective-permute-start | bytes 4616 | tf_op jit(solution)/shard_map/ppermute | solution.py:188
  61.3 14.3 %collective-permute-start.14 = (bf16[2,384]{1,0:T(2,128)(2,1)S(1)}, bf16[2,384]{1,0:T(2,128)(2,1)S(1)}, u32[]{:S(2)}, u32[]{:S(2)}) collective-permute-start(bf16[2,384]{1,0:T(2,128)(2,1)S(1)} %get-tuple-element.59), channel_id=1, source_target_pairs={{0,2},{2,4},{4,6},{6,8},{8,10},{10,12},{12,14},{1,3},{3,5},{5,7},{... | collective-permute-start | bytes 4616 | tf_op jit(solution)/shard_map/ppermute | solution.py:187
  76.2 21.2 %collective-permute-start.25 = (bf16[256,384]{1,0:T(8,128)(2,1)S(1)}, bf16[256,384]{1,0:T(8,128)(2,1)}, u32[]{:S(2)}, u32[]{:S(2)}) collective-permute-start(bf16[256,384]{1,0:T(8,128)(2,1)S(1)} %get-tuple-element.53), channel_id=1, source_target_pairs={{0,1},{1,0},{2,3},{3,2},{4,5},{5,4},{6,7},{7,6},{8,9},{9,8},{10,11... | collective-permute-start | bytes 589832 | tf_op jit(solution)/shard_map/ppermute | solution.py:314
  85.2 12.2 %collective-permute-start.24 = (bf16[260,768]{1,0:T(8,128)(2,1)}, bf16[260,768]{1,0:T(8,128)(2,1)}, u32[]{:S(2)}, u32[]{:S(2)}) collective-permute-start(bf16[260,768]{1,0:T(8,128)(2,1)} %get-tuple-element.48), channel_id=1, source_target_pairs={{0,1},{1,0},{2,3},{3,2},{4,5},{5,4},{6,7},{7,6},{8,9},{9,8},{10,11... | collective-permute-start | bytes 1198088 | tf_op jit(solution)/shard_map/ppermute | solution.py:313
  106.1 21.0 %copy-start.11 = (f32[3840,384]{1,0:T(8,128)}, f32[3840,384]{1,0:T(8,128)S(1)}, u32[]{:S(2)}) copy-start(f32[3840,384]{1,0:T(8,128)S(1)} %broadcast_multiply_fusion) | copy-start | bytes 17694724
  106.2 6.5 %collective-permute-start.26 = (bf16[240,192]{1,0:T(8,128)(2,1)S(1)}, bf16[240,192]{1,0:T(8,128)(2,1)S(1)}, u32[]{:S(2)}, u32[]{:S(2)}) collective-permute-start(bf16[240,192]{1,0:T(8,128)(2,1)S(1)} %get-tuple-element.37), channel_id=1, source_target_pairs={{0,4},{4,8},{8,12},{12,14},{14,10},{10,6},{6,2},{2,0},{1,5},{5,9},... | collective-permute-start | bytes 276488 | tf_op jit(solution)/shard_map/ppermute | solution.py:176
  107.9 6.1 %collective-permute-start.33 = (bf16[240,192]{1,0:T(8,128)(2,1)S(1)}, bf16[240,192]{1,0:T(8,128)(2,1)S(1)}, u32[]{:S(2)}, u32[]{:S(2)}) collective-permute-start(bf16[240,192]{1,0:T(8,128)(2,1)S(1)} %get-tuple-element.38), channel_id=1, source_target_pairs={{0,2},{4,0},{8,4},{12,8},{14,12},{10,14},{6,10},{2,6},{1,3},{5,1},... | collective-permute-start | bytes 276488 | tf_op jit(solution)/shard_map/ppermute | solution.py:176
  109.3 7.7 %collective-permute-start.16 = (bf16[128,640]{1,0:T(8,128)(2,1)S(1)}, bf16[128,640]{1,0:T(8,128)(2,1)S(1)}, u32[]{:S(2)}, u32[]{:S(2)}) collective-permute-start(bf16[128,640]{1,0:T(8,128)(2,1)S(1)} %get-tuple-element.45), channel_id=1, source_target_pairs={{0,2},{4,0},{8,4},{12,8},{14,12},{10,14},{6,10},{2,6},{1,3},{5,1},... | collective-permute-start | bytes 491528 | tf_op jit(solution)/shard_map/ppermute | solution.py:119
  111.3 7.1 %collective-permute-start.20 = (bf16[128,640]{1,0:T(8,128)(2,1)S(1)}, bf16[128,640]{1,0:T(8,128)(2,1)S(1)}, u32[]{:S(2)}, u32[]{:S(2)}) collective-permute-start(bf16[128,640]{1,0:T(8,128)(2,1)S(1)} %get-tuple-element.46), channel_id=1, source_target_pairs={{0,4},{4,8},{8,12},{12,14},{14,10},{10,6},{6,2},{2,0},{1,5},{5,9},... | collective-permute-start | bytes 491528 | tf_op jit(solution)/shard_map/ppermute | solution.py:119
  114.1 5.7 %collective-permute-start.27 = (bf16[240,192]{1,0:T(8,128)(2,1)S(1)}, bf16[240,192]{1,0:T(8,128)(2,1)S(1)}, u32[]{:S(2)}, u32[]{:S(2)}) collective-permute-start(bf16[240,192]{1,0:T(8,128)(2,1)S(1)} %get-tuple-element.35), channel_id=1, source_target_pairs={{0,4},{4,8},{8,12},{12,14},{14,10},{10,6},{6,2},{2,0},{1,5},{5,9},... | collective-permute-start | bytes 276488 | tf_op jit(solution)/shard_map/ppermute | solution.py:176
  115.7 4.9 %collective-permute-start.34 = (bf16[240,192]{1,0:T(8,128)(2,1)S(1)}, bf16[240,192]{1,0:T(8,128)(2,1)S(1)}, u32[]{:S(2)}, u32[]{:S(2)}) collective-permute-start(bf16[240,192]{1,0:T(8,128)(2,1)S(1)} %get-tuple-element.36), channel_id=1, source_target_pairs={{0,2},{4,0},{8,4},{12,8},{14,12},{10,14},{6,10},{2,6},{1,3},{5,1},... | collective-permute-start | bytes 276488 | tf_op jit(solution)/shard_map/ppermute | solution.py:176
  120.8 4.9 %collective-permute-start.28 = (bf16[240,192]{1,0:T(8,128)(2,1)S(1)}, bf16[240,192]{1,0:T(8,128)(2,1)S(1)}, u32[]{:S(2)}, u32[]{:S(2)}) collective-permute-start(bf16[240,192]{1,0:T(8,128)(2,1)S(1)} %get-tuple-element.33), channel_id=1, source_target_pairs={{0,4},{4,8},{8,12},{12,14},{14,10},{10,6},{6,2},{2,0},{1,5},{5,9},... | collective-permute-start | bytes 276488 | tf_op jit(solution)/shard_map/ppermute | solution.py:176
  120.9 6.2 %collective-permute-start.35 = (bf16[240,192]{1,0:T(8,128)(2,1)S(1)}, bf16[240,192]{1,0:T(8,128)(2,1)S(1)}, u32[]{:S(2)}, u32[]{:S(2)}) collective-permute-start(bf16[240,192]{1,0:T(8,128)(2,1)S(1)} %get-tuple-element.34), channel_id=1, source_target_pairs={{0,2},{4,0},{8,4},{12,8},{14,12},{10,14},{6,10},{2,6},{1,3},{5,1},... | collective-permute-start | bytes 276488 | tf_op jit(solution)/shard_map/ppermute | solution.py:176
  123.6 14.7 %collective-permute-start.17 = (bf16[128,1280]{1,0:T(8,128)(2,1)}, bf16[128,1280]{1,0:T(8,128)(2,1)}, u32[]{:S(2)}, u32[]{:S(2)}) collective-permute-start(bf16[128,1280]{1,0:T(8,128)(2,1)} %pad_maximum_fusion.8), channel_id=1, source_target_pairs={{0,2},{4,0},{8,4},{12,8},{14,12},{10,14},{6,10},{2,6},{1,3},{5,1},... | collective-permute-start | bytes 983048 | tf_op jit(solution)/shard_map/ppermute | solution.py:119
  127.8 5.1 %collective-permute-start.29 = (bf16[240,192]{1,0:T(8,128)(2,1)}, bf16[240,192]{1,0:T(8,128)(2,1)S(1)}, u32[]{:S(2)}, u32[]{:S(2)}) collective-permute-start(bf16[240,192]{1,0:T(8,128)(2,1)} %get-tuple-element.31), channel_id=1, source_target_pairs={{0,4},{4,8},{8,12},{12,14},{14,10},{10,6},{6,2},{2,0},{1,5},{5,9},... | collective-permute-start | bytes 276488 | tf_op jit(solution)/shard_map/ppermute | solution.py:176
  129.3 5.6 %collective-permute-start.36 = (bf16[240,192]{1,0:T(8,128)(2,1)S(1)}, bf16[240,192]{1,0:T(8,128)(2,1)}, u32[]{:S(2)}, u32[]{:S(2)}) collective-permute-start(bf16[240,192]{1,0:T(8,128)(2,1)S(1)} %get-tuple-element.32), channel_id=1, source_target_pairs={{0,2},{4,0},{8,4},{12,8},{14,12},{10,14},{6,10},{2,6},{1,3},{5,1},... | collective-permute-start | bytes 276488 | tf_op jit(solution)/shard_map/ppermute | solution.py:176
  129.9 8.5 %collective-permute-start.21 = (bf16[128,1280]{1,0:T(8,128)(2,1)S(1)}, bf16[128,1280]{1,0:T(8,128)(2,1)}, u32[]{:S(2)}, u32[]{:S(2)}) collective-permute-start(bf16[128,1280]{1,0:T(8,128)(2,1)S(1)} %fusion.43), channel_id=1, source_target_pairs={{0,4},{4,8},{8,12},{12,14},{14,10},{10,6},{6,2},{2,0},{1,5},{5,9},... | collective-permute-start | bytes 983048 | tf_op jit(solution)/shard_map/ppermute | solution.py:119
  136.2 6.4 %collective-permute-start.30 = (bf16[240,192]{1,0:T(8,128)(2,1)S(1)}, bf16[240,192]{1,0:T(8,128)(2,1)S(1)}, u32[]{:S(2)}, u32[]{:S(2)}) collective-permute-start(bf16[240,192]{1,0:T(8,128)(2,1)S(1)} %get-tuple-element.29), channel_id=1, source_target_pairs={{0,4},{4,8},{8,12},{12,14},{14,10},{10,6},{6,2},{2,0},{1,5},{5,9},... | collective-permute-start | bytes 276488 | tf_op jit(solution)/shard_map/ppermute | solution.py:176
  137.0 9.9 %copy-start.10 = (bf16[1024,512]{0,1:T(8,128)(2,1)S(1)}, bf16[1024,512]{0,1:T(8,128)(2,1)}, u32[]{:S(2)}) copy-start(bf16[1024,512]{0,1:T(8,128)(2,1)} %copy-done.9) | copy-start | bytes 3145732
  137.0 9.9 %copy-start.12 = (bf16[4,128,1024]{1,2,0:T(8,128)(2,1)S(1)}, bf16[4,128,1024]{1,2,0:T(8,128)(2,1)}, u32[]{:S(2)}) copy-start(bf16[4,128,1024]{1,2,0:T(8,128)(2,1)} %multiply_convert_fusion.1) | copy-start | bytes 3145732
  137.0 5.9 %collective-permute-start.37 = (bf16[240,192]{1,0:T(8,128)(2,1)S(1)}, bf16[240,192]{1,0:T(8,128)(2,1)S(1)}, u32[]{:S(2)}, u32[]{:S(2)}) collective-permute-start(bf16[240,192]{1,0:T(8,128)(2,1)S(1)} %get-tuple-element.30), channel_id=1, source_target_pairs={{0,2},{4,0},{8,4},{12,8},{14,12},{10,14},{6,10},{2,6},{1,3},{5,1},... | collective-permute-start | bytes 276488 | tf_op jit(solution)/shard_map/ppermute | solution.py:176
  140.6 14.9 %collective-permute-start.18 = (bf16[128,1280]{1,0:T(8,128)(2,1)}, bf16[128,1280]{1,0:T(8,128)(2,1)S(1)}, u32[]{:S(2)}, u32[]{:S(2)}) collective-permute-start(bf16[128,1280]{1,0:T(8,128)(2,1)} %get-tuple-element.41), channel_id=1, source_target_pairs={{0,2},{4,0},{8,4},{12,8},{14,12},{10,14},{6,10},{2,6},{1,3},{5,1},... | collective-permute-start | bytes 983048 | tf_op jit(solution)/shard_map/ppermute | solution.py:119
  142.2 13.3 %collective-permute-start.22 = (bf16[128,1280]{1,0:T(8,128)(2,1)}, bf16[128,1280]{1,0:T(8,128)(2,1)}, u32[]{:S(2)}, u32[]{:S(2)}) collective-permute-start(bf16[128,1280]{1,0:T(8,128)(2,1)} %get-tuple-element.42), channel_id=1, source_target_pairs={{0,4},{4,8},{8,12},{12,14},{14,10},{10,6},{6,2},{2,0},{1,5},{5,9},... | collective-permute-start | bytes 983048 | tf_op jit(solution)/shard_map/ppermute | solution.py:119
  144.7 6.9 %collective-permute-start.31 = (bf16[240,192]{1,0:T(8,128)(2,1)}, bf16[240,192]{1,0:T(8,128)(2,1)S(1)}, u32[]{:S(2)}, u32[]{:S(2)}) collective-permute-start(bf16[240,192]{1,0:T(8,128)(2,1)} %get-tuple-element.27), channel_id=1, source_target_pairs={{0,4},{4,8},{8,12},{12,14},{14,10},{10,6},{6,2},{2,0},{1,5},{5,9},... | collective-permute-start | bytes 276488 | tf_op jit(solution)/shard_map/ppermute | solution.py:176
  146.9 5.2 %collective-permute-start.38 = (bf16[240,192]{1,0:T(8,128)(2,1)}, bf16[240,192]{1,0:T(8,128)(2,1)}, u32[]{:S(2)}, u32[]{:S(2)}) collective-permute-start(bf16[240,192]{1,0:T(8,128)(2,1)} %get-tuple-element.28), channel_id=1, source_target_pairs={{0,2},{4,0},{8,4},{12,8},{14,12},{10,14},{6,10},{2,6},{1,3},{5,1},... | collective-permute-start | bytes 276488 | tf_op jit(solution)/shard_map/ppermute | solution.py:176
  153.4 6.2 %collective-permute-start.32 = (bf16[240,192]{1,0:T(8,128)(2,1)S(1)}, bf16[240,192]{1,0:T(8,128)(2,1)S(1)}, u32[]{:S(2)}, u32[]{:S(2)}) collective-permute-start(bf16[240,192]{1,0:T(8,128)(2,1)S(1)} %get-tuple-element.25), channel_id=1, source_target_pairs={{0,4},{4,8},{8,12},{12,14},{14,10},{10,6},{6,2},{2,0},{1,5},{5,9},... | collective-permute-start | bytes 276488 | tf_op jit(solution)/shard_map/ppermute | solution.py:176
  154.2 10.8 %copy-start.2 = (bf16[1024,768]{1,0:T(8,128)(2,1)S(1)}, bf16[1024,768]{1,0:T(8,128)(2,1)}, u32[]{:S(2)}) copy-start(bf16[1024,768]{1,0:T(8,128)(2,1)} %copy.52) | copy-start | bytes 4718596
  154.2 10.8 %copy-start.6 = (bf16[1024,512]{1,0:T(8,128)(2,1)S(1)}, bf16[1024,512]{1,0:T(8,128)(2,1)}, u32[]{:S(2)}) copy-start(bf16[1024,512]{1,0:T(8,128)(2,1)} %copy.51) | copy-start | bytes 3145732
  154.2 6.2 %collective-permute-start.39 = (bf16[240,192]{1,0:T(8,128)(2,1)S(1)}, bf16[240,192]{1,0:T(8,128)(2,1)S(1)}, u32[]{:S(2)}, u32[]{:S(2)}) collective-permute-start(bf16[240,192]{1,0:T(8,128)(2,1)S(1)} %get-tuple-element.26), channel_id=1, source_target_pairs={{0,2},{4,0},{8,4},{12,8},{14,12},{10,14},{6,10},{2,6},{1,3},{5,1},... | collective-permute-start | bytes 276488 | tf_op jit(solution)/shard_map/ppermute | solution.py:176
  156.9 7.5 %collective-permute-start.23 = (bf16[128,1280]{1,0:T(8,128)(2,1)S(1)}, bf16[128,1280]{1,0:T(8,128)(2,1)S(1)}, u32[]{:S(2)}, u32[]{:S(2)}) collective-permute-start(bf16[128,1280]{1,0:T(8,128)(2,1)S(1)} %get-tuple-element.40), channel_id=1, source_target_pairs={{0,4},{4,8},{8,12},{12,14},{14,10},{10,6},{6,2},{2,0},{1,5},{5,9},... | collective-permute-start | bytes 983048 | tf_op jit(solution)/shard_map/ppermute | solution.py:119
  157.9 7.1 %collective-permute-start.19 = (bf16[128,1280]{1,0:T(8,128)(2,1)S(1)}, bf16[128,1280]{1,0:T(8,128)(2,1)S(1)}, u32[]{:S(2)}, u32[]{:S(2)}) collective-permute-start(bf16[128,1280]{1,0:T(8,128)(2,1)S(1)} %get-tuple-element.39), channel_id=1, source_target_pairs={{0,2},{4,0},{8,4},{12,8},{14,12},{10,14},{6,10},{2,6},{1,3},{5,1},... | collective-permute-start | bytes 983048 | tf_op jit(solution)/shard_map/ppermute | solution.py:119
  (12 other events, 43.6 us)

commit v12 on v8

--- a/solution.py
+++ b/solution.py
@@ -188,6 +188,8 @@
     query_heads = queries[0].reshape(local_tokens, H, DK)
     key_value_blocks = ring_gather(jnp.concatenate([key_rows[0], value_rows[0]], axis=1), ring)
     gathered = jnp.concatenate(key_value_blocks, axis=0)
+    queries_after, gathered = lax.optimization_barrier((queries[0], gathered))
+    query_blocks = ring_gather(queries_after, ring)
     all_keys = gathered[:, : H * DK].reshape(-1, H, DK)
     all_values = gathered[:, H * DK :].reshape(-1, H, DV)
     scores = (
@@ -311,24 +313,42 @@
         jnp.einsum("hij,jhd->ihd", slopes, all_keys, preferred_element_type=jnp.float32)
         * score_scale
     ).astype(jnp.bfloat16)
-    key_part = (
-        jnp.einsum("hij,ihd->jhd", slopes, query_heads, preferred_element_type=jnp.float32)
+    stats = jnp.concatenate([logsum[:, :, 0].T, row_delta], axis=1)
+    query_all = jnp.stack(query_blocks).reshape(-1, local_tokens, H, DK)
+    grad_all = jnp.stack(ring_gather(grad_trunk, ring)).reshape(-1, local_tokens, H, DV)
+    stats_all = jnp.stack(ring_gather(stats, ring))
+    logsum_all = jnp.swapaxes(stats_all[:, :, :H], 1, 2)[..., None]
+    delta_all = jnp.swapaxes(stats_all[:, :, H:], 1, 2)[..., None]
+    own_keys = key_rows[0].reshape(local_tokens, H, DK)
+    own_values = value_rows[0].reshape(local_tokens, H, DV)
+    scores_t = (
+        jnp.einsum("mihd,jhd->mhij", query_all, own_keys, preferred_element_type=jnp.float32)
         * score_scale
     )
-    value_part = jnp.einsum("hij,ihd->jhd", rounded, grad_heads, preferred_element_type=jnp.float32)
-    terms = jnp.concatenate(
-        [
-            key_part.reshape(-1, H * DK),
-            value_part.reshape(-1, H * DV),
-        ],
-        axis=1,
-    ).astype(jnp.bfloat16)
-    term_blocks = [
-        terms[m * local_tokens : (m + 1) * local_tokens] for m in range(lax.axis_size("seq"))
-    ]
-    summed = ring_scatter_back(term_blocks, ring)
-    grad_keys = summed[:, : H * DK].astype(jnp.bfloat16)
-    grad_values = summed[:, H * DK :].astype(jnp.bfloat16)
+    softmax_t = jnp.exp(scores_t - logsum_all)
+    value_grad_t = jnp.einsum(
+        "mihd,jhd->mhij", grad_all, own_values, preferred_element_type=jnp.float32
+    )
+    slopes_t = (softmax_t * (value_grad_t - delta_all)).astype(jnp.bfloat16)
+    key_terms = (
+        jnp.einsum("mhij,mihd->mjhd", slopes_t, query_all, preferred_element_type=jnp.float32)
+        * score_scale
+    ).astype(jnp.bfloat16)
+    value_terms = jnp.einsum(
+        "mhij,mihd->mjhd",
+        softmax_t.astype(jnp.bfloat16),
+        grad_all,
+        preferred_element_type=jnp.float32,
+    ).astype(jnp.bfloat16)
+    grad_keys = (
+        key_terms.astype(jnp.float32).sum(axis=0).astype(jnp.bfloat16).reshape(local_tokens, H * DK)
+    )
+    grad_values = (
+        value_terms.astype(jnp.float32)
+        .sum(axis=0)
+        .astype(jnp.bfloat16)
+        .reshape(local_tokens, H * DV)
+    )
     return (
         decoded[None],
         grad_queries.reshape(local_tokens, H * DK)[None],

time: 159 us -> 211 us (1.33)
  local copies, waits for them, and re-layouts: 24 us -> 65.7 us
  starting transfers between devices: 45.4 us -> 61.7 us
  waiting for transfers between devices: 44.8 us -> 33.8 us
  matrix products: 24.7 us -> 27.5 us
    unnamed x60 -> x83, local copies, waits for them, and re-layouts: 9.79 us -> 31.1 us
    ppermute x3 -> x12, starting transfers between devices: 6.37 us -> 24.7 us  [ring_gather(): current = lax.ppermute(current, 'seq', forward)]
    another operation x0 -> x11, local copies, waits for them, and re-layouts: none -> 14.4 us  [the longest x9 13 us: body(): query_all = jnp.stack(query_blocks).reshape(-1, local_tokens, H, DK)]
    ppermute x14, waiting for transfers between devices: 19.8 us -> 10.1 us  [ring_reduce_scatter_sliced(): received = lax.ppermute(acc, axis, perm).astype(jnp.float32)]
    ppermute x8 -> x0, starting transfers between devices: 7.95 us -> none  [ring_scatter_back(): received = lax.ppermute(acc, 'seq', perm).astype(jnp.float32)]
    ppermute x0 -> x6, local copies, waits for them, and re-layouts: none -> 7.17 us  [the longest x3 3.91 us: ring_gather(): current = lax.ppermute(current, 'seq', forward)]
    ppermute x1 -> x4, starting transfers between devices: 1.57 us -> 7.18 us  [ring_gather(): left_half = lax.ppermute(current[:, :half], 'seq', forward)]
    reshape x2 -> x0, local copies, waits for them, and re-layouts: 4.94 us -> none  [the longest x1 2.67 us: body(): value_part.reshape(-1, H * DV)]
  transfers between devices with their start and end apart: 36 -> 52, of which waited for: 20 -> 16; matrix products, arithmetic and copies ran while one was open for 27% -> 46% of each run, Pallas kernels for 0% -> 0%
where the time goes in v12:
time: 211 us; the launch traced here: 210 us
  local copies, waits for them, and re-layouts  65.7 us (31%)
  starting transfers between devices  61.7 us (29%)
  waiting for transfers between devices  33.8 us (16%)
  matrix products  27.5 us (13%)
  other arithmetic  19.7 us (9%)
    unnamed x83, local copies, waits for them, and re-layouts  31.1 us
    ppermute x12, starting transfers between devices, ring_gather(): current = lax.ppermute(current, 'seq', forward)  24.7 us
    ppermute x14, starting transfers between devices, ring_reduce_scatter_sliced(): received = lax.ppermute(acc, axis, perm).astype(jnp.float32)  14.4 us
    another operation x9, local copies, waits for them, and re-layouts, body(): query_all = jnp.stack(query_blocks).reshape(-1, local_tokens, H, DK)  13 us
    ppermute x12, waiting for transfers between devices, ring_gather(): current = lax.ppermute(current, 'seq', forward)  11.8 us
    ppermute x14, waiting for transfers between devices, ring_reduce_scatter_sliced(): received = lax.ppermute(acc, axis, perm).astype(jnp.float32)  10.1 us
    convert_element_type x6, other arithmetic, ring_reduce_scatter_sliced(): acc = acc.astype(wire_dtype)  8.91 us
    dot_general x5, matrix products, body(): jnp.einsum('spc,spo->co', both_padded[:, offset:offset + positions], both...  8.5 us
  transfers between devices with their start and end apart: 52, of which 16 were waited for; matrix products, arithmetic and copies ran while one was open for 46% of the time, Pallas kernels for 0%

profile of v12, /device:TPU:0, one launch (start us, length us, event | category | flops | bytes accessed | tf_op | source)
XLA Modules:
  0.0 210.0 jit_solution(10396928077277354522)
XLA Ops:
  3.9 3.1 %collective-permute-start = (bf16[128,1280]{0,1:T(8,128)(2,1)}, bf16[128,1280]{0,1:T(8,128)(2,1)}, u32[]{:S(2)}, u32[]{:S(2)}) collective-permute-start(bf16[128,1280]{0,1:T(8,128)(2,1)} %get-tuple-element.56), channel_id=1, source_target_pairs={{0,4},{4,8},{8,12},{12,14},{14,10},{10,6},{6,2},{2,0},{1,5},{5,9},... | collective-permute-start | bytes 983048 | tf_op jit(solution)/shard_map/ppermute | solution.py:76
  7.0 1.7 copy.79
  10.6 4.3 %collective-permute-done = bf16[128,1280]{0,1:T(8,128)(2,1)} collective-permute-done((bf16[128,1280]{0,1:T(8,128)(2,1)}, bf16[128,1280]{0,1:T(8,128)(2,1)}, u32[]{:S(2)}, u32[]{:S(2)}) %collective-permute-start) | collective-permute-done | bytes 327712 | tf_op jit(solution)/shard_map/ppermute | solution.py:76
  15.0 1.8 collective-permute-start.1
  18.2 5.8 %collective-permute-done.1 = bf16[128,1280]{0,1:T(8,128)(2,1)S(1)} collective-permute-done((bf16[128,1280]{0,1:T(8,128)(2,1)}, bf16[128,1280]{0,1:T(8,128)(2,1)S(1)}, u32[]{:S(2)}, u32[]{:S(2)}) %collective-permute-start.1) | collective-permute-done | bytes 327712 | tf_op jit(solution)/shard_map/ppermute | solution.py:76
  26.1 1.7 constant_dynamic-update-slice_fusion.5
  28.6 4.8 %collective-permute-done.5 = bf16[128,1280]{0,1:T(8,128)(2,1)S(1)} collective-permute-done((bf16[128,1280]{0,1:T(8,128)(2,1)S(1)}, bf16[128,1280]{0,1:T(8,128)(2,1)S(1)}, u32[]{:S(2)}, u32[]{:S(2)}) %collective-permute-start.5) | collective-permute-done | bytes 327712 | tf_op jit(solution)/shard_map/ppermute | solution.py:82
  36.3 1.8 constant_dynamic-update-slice_fusion.2
  41.9 1.9 slice.98
  43.8 1.6 collective-permute-start.12
  49.6 3.1 %collective-permute-start.8 = (bf16[2,768]{1,0:T(2,128)(2,1)S(1)}, bf16[2,768]{1,0:T(2,128)(2,1)S(1)}, u32[]{:S(2)}, u32[]{:S(2)}) collective-permute-start(bf16[2,768]{1,0:T(2,128)(2,1)S(1)} %get-tuple-element.55), channel_id=1, source_target_pairs={{0,2},{2,4},{4,6},{6,8},{8,10},{10,12},{12,14},{1,3},{3,5},{5,7},{... | collective-permute-start | bytes 9224 | tf_op jit(solution)/shard_map/ppermute | solution.py:24
  56.4 1.8 collective-permute-done.9
  58.5 2.0 fusion.50
  61.8 5.3 %collective-permute-start.11 = (bf16[2,384]{1,0:T(2,128)(2,1)S(1)}, bf16[2,384]{1,0:T(2,128)(2,1)S(1)}, u32[]{:S(2)}, u32[]{:S(2)}) collective-permute-start(bf16[2,384]{1,0:T(2,128)(2,1)S(1)} %get-tuple-element.58), channel_id=1, source_target_pairs={{0,2},{2,4},{4,6},{6,8},{8,10},{10,12},{12,14},{1,3},{3,5},{5,7},{... | collective-permute-start | bytes 4616 | tf_op jit(solution)/shard_map/ppermute | solution.py:24
  72.9 4.7 %collective-permute-start.20 = (f32[128,8]{0,1:T(8,128)S(1)}, f32[128,8]{0,1:T(8,128)S(1)}, u32[]{:S(2)}, u32[]{:S(2)}) collective-permute-start(f32[128,8]{0,1:T(8,128)S(1)} %pad_maximum_fusion.12), channel_id=1, source_target_pairs={{0,4},{4,8},{8,12},{12,14},{14,10},{10,6},{6,2},{2,0},{1,5},{5,9},... | collective-permute-start | bytes 12296 | tf_op jit(solution)/shard_map/ppermute | solution.py:76
  77.6 3.7 %fusion.22 = bf16[4,128,128]{2,1,0:T(8,128)(2,1)S(1)} fusion(bf16[1024,4,128]{0,2,1:T(8,128)(2,1)} %bitcast.266, f32[4,1024,128]{2,1,0:T(8,128)} %copy-done.3, bf16[128,4,192]{0,2,1:T(8,128)(2,1)S(1)} %bitcast.271, bf16[1024,4,192]{0,2,1:T(8,128)(2,1)} %bitcast.259, f32[4,128]{1,0:T(4,128)S(1)} %bitcast.288, f32[4,128]{1,0:T(4,128)S(1)} %log_add_fusion), kind=kOutput, calls=%fused_computation.38 | convolution fusion | flops 338296832 | bytes 5050368 | tf_op jit(solution)/shard_map/hij,jhd->ihd/dot_general | solution.py:313
  82.8 2.0 collective-permute-start.21
  86.4 2.0 collective-permute-start.22
  88.4 3.6 %collective-permute-done.25 = f32[128,8]{0,1:T(8,128)S(1)} collective-permute-done((f32[128,8]{0,1:T(8,128)S(1)}, f32[128,8]{0,1:T(8,128)S(1)}, u32[]{:S(2)}, u32[]{:S(2)}) %collective-permute-start.25) | collective-permute-done | bytes 4128 | tf_op jit(solution)/shard_map/ppermute | solution.py:82
  92.1 2.0 collective-permute-start.26
  97.7 1.6 collective-permute-start.13
  104.3 1.6 collective-permute-start.14
  109.7 1.7 copy.90
  111.4 1.7 copy.93
  113.1 1.6 constant_dynamic-update-slice_fusion.13
  115.1 1.7 copy.91
  116.8 1.7 copy.94
  119.9 1.6 constant_dynamic-update-slice_fusion.12
  125.3 1.6 constant_dynamic-update-slice_fusion.9
  126.9 2.0 collective-permute-start.18
  128.9 1.7 copy.100
  133.3 1.7 constant_dynamic-update-slice_fusion.29
  135.4 1.8 fusion.13
  137.3 1.7 fusion.12
  139.0 1.7 fusion.11
  140.6 1.7 fusion.10
  142.3 1.7 fusion.9
  144.4 2.5 %copy-done.4 = f32[3840,384]{1,0:T(8,128)} copy-done((f32[3840,384]{1,0:T(8,128)}, f32[3840,384]{1,0:T(8,128)S(1)}, u32[]{:S(2)}) %copy-start.4) | copy-done | bytes 5898264
  151.2 1.7 copy.95
  152.9 1.6 constant_dynamic-update-slice_fusion.8
  155.8 1.6 collective-permute-start.39
  157.9 3.6 %fusion.7 = (bf16[8,4,128,128]{3,2,0,1:T(8,128)(2,1)}, f32[4,8,128,128]{3,2,1,0:T(8,128)}) fusion(f32[8,4,128]{2,0,1:T(8,128)S(1)} %copy.97, bf16[8,128,4,128]{3,1,0,2:T(8,128)(2,1)} %constant_dynamic-update-slice_fusion.8, bf16[128,4,128,1]{2,1,0,3:T(4,128)(2,1)S(1)} %bitcast.280), kind=kOutput, calls=%fused_computation.15 | convolution fusion | flops 135790592 | bytes 4341760 | tf_op jit(solution)/shard_map/mihd,jhd->mhij/dot_general | solution.py:325
  162.3 1.8 fusion.63
  176.4 2.0 fusion.62
  182.2 1.8 collective-permute-done.41
  184.1 1.8 collective-permute-done.48
  189.3 3.5 %fusion.1 = bf16[8,4,128,128]{3,2,0,1:T(8,128)(2,1)S(1)} fusion(f32[4,8,128,128]{3,2,1,0:T(8,128)} %get-tuple-element.71, bf16[8,128,4,192]{1,3,0,2:T(8,128)(2,1)} %constant_dynamic-update-slice_fusion.24, bf16[128,4,192,1]{0,2,3,1:T(8,128)(2,1)S(1)} %bitcast.269, f32[8,4,128]{2,0,1:T(8,128)} %copy.115, f32[8,4,128]{2,0,1:T(8,128)S(1)} %copy.97), kind=kOutput, calls=%fused_computation.3 | convolution fusion | flops 203948032 | bytes 4947968 | tf_op jit(solution)/shard_map/mihd,jhd->mhij/dot_general | solution.py:329
  197.1 2.3 %collective-permute-done.43 = bf16[240,192]{1,0:T(8,128)(2,1)S(1)} collective-permute-done((bf16[240,192]{1,0:T(8,128)(2,1)S(1)}, bf16[240,192]{1,0:T(8,128)(2,1)S(1)}, u32[]{:S(2)}, u32[]{:S(2)}) %collective-permute-start.43) | collective-permute-done | bytes 92192 | tf_op jit(solution)/shard_map/ppermute | solution.py:176
  (227 shorter events, 96.9 us)
Async XLA Ops:
  3.9 11.0 %collective-permute-start = (bf16[128,1280]{0,1:T(8,128)(2,1)}, bf16[128,1280]{0,1:T(8,128)(2,1)}, u32[]{:S(2)}, u32[]{:S(2)}) collective-permute-start(bf16[128,1280]{0,1:T(8,128)(2,1)} %get-tuple-element.56), channel_id=1, source_target_pairs={{0,4},{4,8},{8,12},{12,14},{14,10},{10,6},{6,2},{2,0},{1,5},{5,9},... | collective-permute-start | bytes 983048 | tf_op jit(solution)/shard_map/ppermute | solution.py:76
  7.0 9.8 %collective-permute-start.3 = (bf16[128,1280]{0,1:T(8,128)(2,1)}, bf16[128,1280]{0,1:T(8,128)(2,1)}, u32[]{:S(2)}, u32[]{:S(2)}) collective-permute-start(bf16[128,1280]{0,1:T(8,128)(2,1)} %get-tuple-element.56), channel_id=1, source_target_pairs={{0,2},{4,0},{8,4},{12,8},{14,12},{10,14},{6,10},{2,6},{1,3},{5,1},... | collective-permute-start | bytes 983048 | tf_op jit(solution)/shard_map/ppermute | solution.py:82
  15.0 9.1 %collective-permute-start.1 = (bf16[128,1280]{0,1:T(8,128)(2,1)}, bf16[128,1280]{0,1:T(8,128)(2,1)S(1)}, u32[]{:S(2)}, u32[]{:S(2)}) collective-permute-start(bf16[128,1280]{0,1:T(8,128)(2,1)} %collective-permute-done), channel_id=1, source_target_pairs={{0,4},{4,8},{8,12},{12,14},{14,10},{10,6},{6,2},{2,0},{1,5},{5,9},... | collective-permute-start | bytes 983048 | tf_op jit(solution)/shard_map/ppermute | solution.py:76
  16.8 8.8 %collective-permute-start.4 = (bf16[128,1280]{0,1:T(8,128)(2,1)}, bf16[128,1280]{0,1:T(8,128)(2,1)S(1)}, u32[]{:S(2)}, u32[]{:S(2)}) collective-permute-start(bf16[128,1280]{0,1:T(8,128)(2,1)} %collective-permute-done.3), channel_id=1, source_target_pairs={{0,2},{4,0},{8,4},{12,8},{14,12},{10,14},{6,10},{2,6},{1,3},{5,1},... | collective-permute-start | bytes 983048 | tf_op jit(solution)/shard_map/ppermute | solution.py:82
  24.1 9.9 %collective-permute-start.2 = (bf16[128,1280]{0,1:T(8,128)(2,1)S(1)}, bf16[128,1280]{0,1:T(8,128)(2,1)S(1)}, u32[]{:S(2)}, u32[]{:S(2)}) collective-permute-start(bf16[128,1280]{0,1:T(8,128)(2,1)S(1)} %collective-permute-done.1), channel_id=1, source_target_pairs={{0,4},{4,8},{8,12},{12,14},{14,10},{10,6},{6,2},{2,0},{1,5},{5,9},... | collective-permute-start | bytes 983048 | tf_op jit(solution)/shard_map/ppermute | solution.py:76
  25.6 7.8 %collective-permute-start.5 = (bf16[128,1280]{0,1:T(8,128)(2,1)S(1)}, bf16[128,1280]{0,1:T(8,128)(2,1)S(1)}, u32[]{:S(2)}, u32[]{:S(2)}) collective-permute-start(bf16[128,1280]{0,1:T(8,128)(2,1)S(1)} %collective-permute-done.4), channel_id=1, source_target_pairs={{0,2},{4,0},{8,4},{12,8},{14,12},{10,14},{6,10},{2,6},{1,3},{5,1},... | collective-permute-start | bytes 983048 | tf_op jit(solution)/shard_map/ppermute | solution.py:82
  33.4 6.2 %collective-permute-start.7 = (bf16[128,640]{0,1:T(8,128)(2,1)S(1)}, bf16[128,640]{0,1:T(8,128)(2,1)S(1)}, u32[]{:S(2)}, u32[]{:S(2)}) collective-permute-start(bf16[128,640]{0,1:T(8,128)(2,1)S(1)} %slice.125), channel_id=1, source_target_pairs={{0,2},{4,0},{8,4},{12,8},{14,12},{10,14},{6,10},{2,6},{1,3},{5,1},... | collective-permute-start | bytes 491528 | tf_op jit(solution)/shard_map/ppermute | solution.py:85
  34.0 5.6 %collective-permute-start.6 = (bf16[128,640]{0,1:T(8,128)(2,1)S(1)}, bf16[128,640]{0,1:T(8,128)(2,1)S(1)}, u32[]{:S(2)}, u32[]{:S(2)}) collective-permute-start(bf16[128,640]{0,1:T(8,128)(2,1)S(1)} %slice.124), channel_id=1, source_target_pairs={{0,4},{4,8},{8,12},{12,14},{14,10},{10,6},{6,2},{2,0},{1,5},{5,9},... | collective-permute-start | bytes 491528 | tf_op jit(solution)/shard_map/ppermute | solution.py:79
  43.8 53.9 %collective-permute-start.12 = (bf16[128,512]{0,1:T(8,128)(2,1)}, bf16[128,512]{0,1:T(8,128)(2,1)}, u32[]{:S(2)}, u32[]{:S(2)}) collective-permute-start(bf16[128,512]{0,1:T(8,128)(2,1)} %bitcast.1), channel_id=1, source_target_pairs={{0,4},{4,8},{8,12},{12,14},{14,10},{10,6},{6,2},{2,0},{1,5},{5,9},... | collective-permute-start | bytes 393224 | tf_op jit(solution)/shard_map/ppermute | solution.py:76
  45.4 53.9 %collective-permute-start.15 = (bf16[128,512]{0,1:T(8,128)(2,1)}, bf16[128,512]{0,1:T(8,128)(2,1)}, u32[]{:S(2)}, u32[]{:S(2)}) collective-permute-start(bf16[128,512]{0,1:T(8,128)(2,1)} %bitcast.1), channel_id=1, source_target_pairs={{0,2},{4,0},{8,4},{12,8},{14,12},{10,14},{6,10},{2,6},{1,3},{5,1},... | collective-permute-start | bytes 393224 | tf_op jit(solution)/shard_map/ppermute | solution.py:82
  49.6 6.2 %collective-permute-start.8 = (bf16[2,768]{1,0:T(2,128)(2,1)S(1)}, bf16[2,768]{1,0:T(2,128)(2,1)S(1)}, u32[]{:S(2)}, u32[]{:S(2)}) collective-permute-start(bf16[2,768]{1,0:T(2,128)(2,1)S(1)} %get-tuple-element.55), channel_id=1, source_target_pairs={{0,2},{2,4},{4,6},{6,8},{8,10},{10,12},{12,14},{1,3},{3,5},{5,7},{... | collective-permute-start | bytes 9224 | tf_op jit(solution)/shard_map/ppermute | solution.py:24
  52.7 5.5 %collective-permute-start.9 = (bf16[2,768]{1,0:T(2,128)(2,1)S(1)}, bf16[2,768]{1,0:T(2,128)(2,1)S(1)}, u32[]{:S(2)}, u32[]{:S(2)}) collective-permute-start(bf16[2,768]{1,0:T(2,128)(2,1)S(1)} %get-tuple-element.54), channel_id=1, source_target_pairs={{2,0},{4,2},{6,4},{8,6},{10,8},{12,10},{14,12},{3,1},{5,3},{7,5},{... | collective-permute-start | bytes 9224 | tf_op jit(solution)/shard_map/ppermute | solution.py:25
  60.5 74.5 %collective-permute-start.37 = (bf16[256,384]{1,0:T(8,128)(2,1)S(1)}, bf16[256,384]{1,0:T(8,128)(2,1)}, u32[]{:S(2)}, u32[]{:S(2)}) collective-permute-start(bf16[256,384]{1,0:T(8,128)(2,1)S(1)} %get-tuple-element.52), channel_id=1, source_target_pairs={{0,1},{1,0},{2,3},{3,2},{4,5},{5,4},{6,7},{7,6},{8,9},{9,8},{10,11... | collective-permute-start | bytes 589832 | tf_op jit(solution)/shard_map/ppermute | solution.py:234
  60.5 7.6 %collective-permute-start.10 = (bf16[2,384]{1,0:T(2,128)(2,1)S(1)}, bf16[2,384]{1,0:T(2,128)(2,1)S(1)}, u32[]{:S(2)}, u32[]{:S(2)}) collective-permute-start(bf16[2,384]{1,0:T(2,128)(2,1)S(1)} %get-tuple-element.59), channel_id=1, source_target_pairs={{2,0},{4,2},{6,4},{8,6},{10,8},{12,10},{14,12},{3,1},{5,3},{7,5},{... | collective-permute-start | bytes 4616 | tf_op jit(solution)/shard_map/ppermute | solution.py:25
  61.8 6.5 %collective-permute-start.11 = (bf16[2,384]{1,0:T(2,128)(2,1)S(1)}, bf16[2,384]{1,0:T(2,128)(2,1)S(1)}, u32[]{:S(2)}, u32[]{:S(2)}) collective-permute-start(bf16[2,384]{1,0:T(2,128)(2,1)S(1)} %get-tuple-element.58), channel_id=1, source_target_pairs={{0,2},{2,4},{4,6},{6,8},{8,10},{10,12},{12,14},{1,3},{3,5},{5,7},{... | collective-permute-start | bytes 4616 | tf_op jit(solution)/shard_map/ppermute | solution.py:24
  72.9 9.9 %collective-permute-start.20 = (f32[128,8]{0,1:T(8,128)S(1)}, f32[128,8]{0,1:T(8,128)S(1)}, u32[]{:S(2)}, u32[]{:S(2)}) collective-permute-start(f32[128,8]{0,1:T(8,128)S(1)} %pad_maximum_fusion.12), channel_id=1, source_target_pairs={{0,4},{4,8},{8,12},{12,14},{14,10},{10,6},{6,2},{2,0},{1,5},{5,9},... | collective-permute-start | bytes 12296 | tf_op jit(solution)/shard_map/ppermute | solution.py:76
  77.6 7.2 %collective-permute-start.23 = (f32[128,8]{0,1:T(8,128)S(1)}, f32[128,8]{0,1:T(8,128)S(1)}, u32[]{:S(2)}, u32[]{:S(2)}) collective-permute-start(f32[128,8]{0,1:T(8,128)S(1)} %pad_maximum_fusion.12), channel_id=1, source_target_pairs={{0,2},{4,0},{8,4},{12,8},{14,12},{10,14},{6,10},{2,6},{1,3},{5,1},... | collective-permute-start | bytes 12296 | tf_op jit(solution)/shard_map/ppermute | solution.py:82
  86.4 5.7 %collective-permute-start.22 = (f32[128,8]{0,1:T(8,128)S(1)}, f32[128,8]{0,1:T(8,128)S(1)}, u32[]{:S(2)}, u32[]{:S(2)}) collective-permute-start(f32[128,8]{0,1:T(8,128)S(1)} %collective-permute-done.21), channel_id=1, source_target_pairs={{0,4},{4,8},{8,12},{12,14},{14,10},{10,6},{6,2},{2,0},{1,5},{5,9},... | collective-permute-start | bytes 12296 | tf_op jit(solution)/shard_map/ppermute | solution.py:76
  92.1 5.2 %collective-permute-start.26 = (f32[128,4]{0,1:T(4,128)S(1)}, f32[128,4]{0,1:T(4,128)S(1)}, u32[]{:S(2)}, u32[]{:S(2)}) collective-permute-start(f32[128,4]{0,1:T(4,128)S(1)} %slice.113), channel_id=1, source_target_pairs={{0,4},{4,8},{8,12},{12,14},{14,10},{10,6},{6,2},{2,0},{1,5},{5,9},... | collective-permute-start | bytes 6152 | tf_op jit(solution)/shard_map/ppermute | solution.py:79
  95.7 7.5 %collective-permute-start.28 = (bf16[128,768]{1,0:T(8,128)(2,1)}, bf16[128,768]{1,0:T(8,128)(2,1)}, u32[]{:S(2)}, u32[]{:S(2)}) collective-permute-start(bf16[128,768]{1,0:T(8,128)(2,1)} %convolution_convert_fusion.1), channel_id=1, source_target_pairs={{0,4},{4,8},{8,12},{12,14},{14,10},{10,6},{6,2},{2,0},{1,5},{5,9},... | collective-permute-start | bytes 589832 | tf_op jit(solution)/shard_map/ppermute | solution.py:76
  97.2 9.8 %collective-permute-start.31 = (bf16[128,768]{1,0:T(8,128)(2,1)}, bf16[128,768]{1,0:T(8,128)(2,1)}, u32[]{:S(2)}, u32[]{:S(2)}) collective-permute-start(bf16[128,768]{1,0:T(8,128)(2,1)} %convolution_convert_fusion.1), channel_id=1, source_target_pairs={{0,2},{4,0},{8,4},{12,8},{14,12},{10,14},{6,10},{2,6},{1,3},{5,1},... | collective-permute-start | bytes 589832 | tf_op jit(solution)/shard_map/ppermute | solution.py:82
  97.7 6.5 %collective-permute-start.13 = (bf16[128,512]{0,1:T(8,128)(2,1)}, bf16[128,512]{0,1:T(8,128)(2,1)}, u32[]{:S(2)}, u32[]{:S(2)}) collective-permute-start(bf16[128,512]{0,1:T(8,128)(2,1)} %collective-permute-done.12), channel_id=1, source_target_pairs={{0,4},{4,8},{8,12},{12,14},{14,10},{10,6},{6,2},{2,0},{1,5},{5,9},... | collective-permute-start | bytes 393224 | tf_op jit(solution)/shard_map/ppermute | solution.py:76
  99.3 6.6 %collective-permute-start.16 = (bf16[128,512]{0,1:T(8,128)(2,1)}, bf16[128,512]{0,1:T(8,128)(2,1)}, u32[]{:S(2)}, u32[]{:S(2)}) collective-permute-start(bf16[128,512]{0,1:T(8,128)(2,1)} %collective-permute-done.15), channel_id=1, source_target_pairs={{0,2},{4,0},{8,4},{12,8},{14,12},{10,14},{6,10},{2,6},{1,3},{5,1},... | collective-permute-start | bytes 393224 | tf_op jit(solution)/shard_map/ppermute | solution.py:82
  103.2 32.3 %collective-permute-start.36 = (bf16[260,768]{1,0:T(8,128)(2,1)}, bf16[260,768]{1,0:T(8,128)(2,1)}, u32[]{:S(2)}, u32[]{:S(2)}) collective-permute-start(bf16[260,768]{1,0:T(8,128)(2,1)} %get-tuple-element.50), channel_id=1, source_target_pairs={{0,1},{1,0},{2,3},{3,2},{4,5},{5,4},{6,7},{7,6},{8,9},{9,8},{10,11... | collective-permute-start | bytes 1198088 | tf_op jit(solution)/shard_map/ppermute | solution.py:233
  104.3 10.4 %collective-permute-start.14 = (bf16[128,512]{0,1:T(8,128)(2,1)}, bf16[128,512]{0,1:T(8,128)(2,1)}, u32[]{:S(2)}, u32[]{:S(2)}) collective-permute-start(bf16[128,512]{0,1:T(8,128)(2,1)} %collective-permute-done.13), channel_id=1, source_target_pairs={{0,4},{4,8},{8,12},{12,14},{14,10},{10,6},{6,2},{2,0},{1,5},{5,9},... | collective-permute-start | bytes 393224 | tf_op jit(solution)/shard_map/ppermute | solution.py:76
  105.9 10.9 %collective-permute-start.17 = (bf16[128,512]{0,1:T(8,128)(2,1)}, bf16[128,512]{0,1:T(8,128)(2,1)}, u32[]{:S(2)}, u32[]{:S(2)}) collective-permute-start(bf16[128,512]{0,1:T(8,128)(2,1)} %collective-permute-done.16), channel_id=1, source_target_pairs={{0,2},{4,0},{8,4},{12,8},{14,12},{10,14},{6,10},{2,6},{1,3},{5,1},... | collective-permute-start | bytes 393224 | tf_op jit(solution)/shard_map/ppermute | solution.py:82
  107.1 19.8 %collective-permute-start.29 = (bf16[128,768]{1,0:T(8,128)(2,1)}, bf16[128,768]{1,0:T(8,128)(2,1)}, u32[]{:S(2)}, u32[]{:S(2)}) collective-permute-start(bf16[128,768]{1,0:T(8,128)(2,1)} %collective-permute-done.28), channel_id=1, source_target_pairs={{0,4},{4,8},{8,12},{12,14},{14,10},{10,6},{6,2},{2,0},{1,5},{5,9},... | collective-permute-start | bytes 589832 | tf_op jit(solution)/shard_map/ppermute | solution.py:76
  114.7 16.0 %collective-permute-start.32 = (bf16[128,768]{1,0:T(8,128)(2,1)}, bf16[128,768]{1,0:T(8,128)(2,1)}, u32[]{:S(2)}, u32[]{:S(2)}) collective-permute-start(bf16[128,768]{1,0:T(8,128)(2,1)} %collective-permute-done.31), channel_id=1, source_target_pairs={{0,2},{4,0},{8,4},{12,8},{14,12},{10,14},{6,10},{2,6},{1,3},{5,1},... | collective-permute-start | bytes 589832 | tf_op jit(solution)/shard_map/ppermute | solution.py:82
  119.9 29.3 %collective-permute-start.19 = (bf16[128,256]{0,1:T(8,128)(2,1)}, bf16[128,256]{0,1:T(8,128)(2,1)}, u32[]{:S(2)}, u32[]{:S(2)}) collective-permute-start(bf16[128,256]{0,1:T(8,128)(2,1)} %slice.139), channel_id=1, source_target_pairs={{0,2},{4,0},{8,4},{12,8},{14,12},{10,14},{6,10},{2,6},{1,3},{5,1},... | collective-permute-start | bytes 196616 | tf_op jit(solution)/shard_map/ppermute | solution.py:85
  126.9 22.8 %collective-permute-start.18 = (bf16[128,256]{0,1:T(8,128)(2,1)}, bf16[128,256]{0,1:T(8,128)(2,1)}, u32[]{:S(2)}, u32[]{:S(2)}) collective-permute-start(bf16[128,256]{0,1:T(8,128)(2,1)} %slice.138), channel_id=1, source_target_pairs={{0,4},{4,8},{8,12},{12,14},{14,10},{10,6},{6,2},{2,0},{1,5},{5,9},... | collective-permute-start | bytes 196616 | tf_op jit(solution)/shard_map/ppermute | solution.py:79
  130.7 37.6 %collective-permute-start.30 = (bf16[128,768]{1,0:T(8,128)(2,1)}, bf16[128,768]{1,0:T(8,128)(2,1)}, u32[]{:S(2)}, u32[]{:S(2)}) collective-permute-start(bf16[128,768]{1,0:T(8,128)(2,1)} %collective-permute-done.29), channel_id=1, source_target_pairs={{0,4},{4,8},{8,12},{12,14},{14,10},{10,6},{6,2},{2,0},{1,5},{5,9},... | collective-permute-start | bytes 589832 | tf_op jit(solution)/shard_map/ppermute | solution.py:76
  135.0 31.2 %collective-permute-start.33 = (bf16[128,768]{1,0:T(8,128)(2,1)}, bf16[128,768]{1,0:T(8,128)(2,1)}, u32[]{:S(2)}, u32[]{:S(2)}) collective-permute-start(bf16[128,768]{1,0:T(8,128)(2,1)} %collective-permute-done.32), channel_id=1, source_target_pairs={{0,2},{4,0},{8,4},{12,8},{14,12},{10,14},{6,10},{2,6},{1,3},{5,1},... | collective-permute-start | bytes 589832 | tf_op jit(solution)/shard_map/ppermute | solution.py:82
  147.6 6.8 %collective-permute-start.38 = (bf16[240,192]{1,0:T(8,128)(2,1)}, bf16[240,192]{1,0:T(8,128)(2,1)}, u32[]{:S(2)}, u32[]{:S(2)}) collective-permute-start(bf16[240,192]{1,0:T(8,128)(2,1)} %get-tuple-element.48), channel_id=1, source_target_pairs={{0,4},{4,8},{8,12},{12,14},{14,10},{10,6},{6,2},{2,0},{1,5},{5,9},... | collective-permute-start | bytes 276488 | tf_op jit(solution)/shard_map/ppermute | solution.py:176
  149.2 5.3 %collective-permute-start.45 = (bf16[240,192]{1,0:T(8,128)(2,1)}, bf16[240,192]{1,0:T(8,128)(2,1)}, u32[]{:S(2)}, u32[]{:S(2)}) collective-permute-start(bf16[240,192]{1,0:T(8,128)(2,1)} %get-tuple-element.49), channel_id=1, source_target_pairs={{0,2},{4,0},{8,4},{12,8},{14,12},{10,14},{6,10},{2,6},{1,3},{5,1},... | collective-permute-start | bytes 276488 | tf_op jit(solution)/shard_map/ppermute | solution.py:176
  155.8 5.7 %collective-permute-start.39 = (bf16[240,192]{1,0:T(8,128)(2,1)S(1)}, bf16[240,192]{1,0:T(8,128)(2,1)S(1)}, u32[]{:S(2)}, u32[]{:S(2)}) collective-permute-start(bf16[240,192]{1,0:T(8,128)(2,1)S(1)} %get-tuple-element.46), channel_id=1, source_target_pairs={{0,4},{4,8},{8,12},{12,14},{14,10},{10,6},{6,2},{2,0},{1,5},{5,9},... | collective-permute-start | bytes 276488 | tf_op jit(solution)/shard_map/ppermute | solution.py:176
  157.5 4.9 %collective-permute-start.46 = (bf16[240,192]{1,0:T(8,128)(2,1)S(1)}, bf16[240,192]{1,0:T(8,128)(2,1)S(1)}, u32[]{:S(2)}, u32[]{:S(2)}) collective-permute-start(bf16[240,192]{1,0:T(8,128)(2,1)S(1)} %get-tuple-element.47), channel_id=1, source_target_pairs={{0,2},{4,0},{8,4},{12,8},{14,12},{10,14},{6,10},{2,6},{1,3},{5,1},... | collective-permute-start | bytes 276488 | tf_op jit(solution)/shard_map/ppermute | solution.py:176
  164.2 12.2 %collective-permute-start.40 = (bf16[240,192]{1,0:T(8,128)(2,1)}, bf16[240,192]{1,0:T(8,128)(2,1)}, u32[]{:S(2)}, u32[]{:S(2)}) collective-permute-start(bf16[240,192]{1,0:T(8,128)(2,1)} %get-tuple-element.44), channel_id=1, source_target_pairs={{0,4},{4,8},{8,12},{12,14},{14,10},{10,6},{6,2},{2,0},{1,5},{5,9},... | collective-permute-start | bytes 276488 | tf_op jit(solution)/shard_map/ppermute | solution.py:176
  165.7 10.7 %collective-permute-start.47 = (bf16[240,192]{1,0:T(8,128)(2,1)}, bf16[240,192]{1,0:T(8,128)(2,1)}, u32[]{:S(2)}, u32[]{:S(2)}) collective-permute-start(bf16[240,192]{1,0:T(8,128)(2,1)} %get-tuple-element.45), channel_id=1, source_target_pairs={{0,2},{4,0},{8,4},{12,8},{14,12},{10,14},{6,10},{2,6},{1,3},{5,1},... | collective-permute-start | bytes 276488 | tf_op jit(solution)/shard_map/ppermute | solution.py:176
  167.8 12.6 %collective-permute-start.35 = (bf16[128,384]{1,0:T(8,128)(2,1)}, bf16[128,384]{1,0:T(8,128)(2,1)}, u32[]{:S(2)}, u32[]{:S(2)}) collective-permute-start(bf16[128,384]{1,0:T(8,128)(2,1)} %slice.142), channel_id=1, source_target_pairs={{0,2},{4,0},{8,4},{12,8},{14,12},{10,14},{6,10},{2,6},{1,3},{5,1},... | collective-permute-start | bytes 294920 | tf_op jit(solution)/shard_map/ppermute | solution.py:85
  169.8 10.6 %collective-permute-start.34 = (bf16[128,384]{1,0:T(8,128)(2,1)}, bf16[128,384]{1,0:T(8,128)(2,1)}, u32[]{:S(2)}, u32[]{:S(2)}) collective-permute-start(bf16[128,384]{1,0:T(8,128)(2,1)} %slice.141), channel_id=1, source_target_pairs={{0,4},{4,8},{8,12},{12,14},{14,10},{10,6},{6,2},{2,0},{1,5},{5,9},... | collective-permute-start | bytes 294920 | tf_op jit(solution)/shard_map/ppermute | solution.py:79
  178.4 5.7 %collective-permute-start.41 = (bf16[240,192]{1,0:T(8,128)(2,1)}, bf16[240,192]{1,0:T(8,128)(2,1)}, u32[]{:S(2)}, u32[]{:S(2)}) collective-permute-start(bf16[240,192]{1,0:T(8,128)(2,1)} %get-tuple-element.42), channel_id=1, source_target_pairs={{0,4},{4,8},{8,12},{12,14},{14,10},{10,6},{6,2},{2,0},{1,5},{5,9},... | collective-permute-start | bytes 276488 | tf_op jit(solution)/shard_map/ppermute | solution.py:176
  179.9 6.0 %collective-permute-start.48 = (bf16[240,192]{1,0:T(8,128)(2,1)}, bf16[240,192]{1,0:T(8,128)(2,1)}, u32[]{:S(2)}, u32[]{:S(2)}) collective-permute-start(bf16[240,192]{1,0:T(8,128)(2,1)} %get-tuple-element.43), channel_id=1, source_target_pairs={{0,2},{4,0},{8,4},{12,8},{14,12},{10,14},{6,10},{2,6},{1,3},{5,1},... | collective-permute-start | bytes 276488 | tf_op jit(solution)/shard_map/ppermute | solution.py:176
  187.2 5.6 %collective-permute-start.42 = (bf16[240,192]{1,0:T(8,128)(2,1)S(1)}, bf16[240,192]{1,0:T(8,128)(2,1)S(1)}, u32[]{:S(2)}, u32[]{:S(2)}) collective-permute-start(bf16[240,192]{1,0:T(8,128)(2,1)S(1)} %get-tuple-element.40), channel_id=1, source_target_pairs={{0,4},{4,8},{8,12},{12,14},{14,10},{10,6},{6,2},{2,0},{1,5},{5,9},... | collective-permute-start | bytes 276488 | tf_op jit(solution)/shard_map/ppermute | solution.py:176
  188.3 4.9 %collective-permute-start.49 = (bf16[240,192]{1,0:T(8,128)(2,1)S(1)}, bf16[240,192]{1,0:T(8,128)(2,1)S(1)}, u32[]{:S(2)}, u32[]{:S(2)}) collective-permute-start(bf16[240,192]{1,0:T(8,128)(2,1)S(1)} %get-tuple-element.41), channel_id=1, source_target_pairs={{0,2},{4,0},{8,4},{12,8},{14,12},{10,14},{6,10},{2,6},{1,3},{5,1},... | collective-permute-start | bytes 276488 | tf_op jit(solution)/shard_map/ppermute | solution.py:176
  194.4 4.9 %collective-permute-start.43 = (bf16[240,192]{1,0:T(8,128)(2,1)S(1)}, bf16[240,192]{1,0:T(8,128)(2,1)S(1)}, u32[]{:S(2)}, u32[]{:S(2)}) collective-permute-start(bf16[240,192]{1,0:T(8,128)(2,1)S(1)} %get-tuple-element.38), channel_id=1, source_target_pairs={{0,4},{4,8},{8,12},{12,14},{14,10},{10,6},{6,2},{2,0},{1,5},{5,9},... | collective-permute-start | bytes 276488 | tf_op jit(solution)/shard_map/ppermute | solution.py:176
  195.6 4.9 %collective-permute-start.50 = (bf16[240,192]{1,0:T(8,128)(2,1)S(1)}, bf16[240,192]{1,0:T(8,128)(2,1)S(1)}, u32[]{:S(2)}, u32[]{:S(2)}) collective-permute-start(bf16[240,192]{1,0:T(8,128)(2,1)S(1)} %get-tuple-element.39), channel_id=1, source_target_pairs={{0,2},{4,0},{8,4},{12,8},{14,12},{10,14},{6,10},{2,6},{1,3},{5,1},... | collective-permute-start | bytes 276488 | tf_op jit(solution)/shard_map/ppermute | solution.py:176
  201.7 5.0 %collective-permute-start.44 = (bf16[240,192]{1,0:T(8,128)(2,1)S(1)}, bf16[240,192]{1,0:T(8,128)(2,1)}, u32[]{:S(2)}, u32[]{:S(2)}) collective-permute-start(bf16[240,192]{1,0:T(8,128)(2,1)S(1)} %get-tuple-element.36), channel_id=1, source_target_pairs={{0,4},{4,8},{8,12},{12,14},{14,10},{10,6},{6,2},{2,0},{1,5},{5,9},... | collective-permute-start | bytes 276488 | tf_op jit(solution)/shard_map/ppermute | solution.py:176
  202.8 5.0 %collective-permute-start.51 = (bf16[240,192]{1,0:T(8,128)(2,1)S(1)}, bf16[240,192]{1,0:T(8,128)(2,1)}, u32[]{:S(2)}, u32[]{:S(2)}) collective-permute-start(bf16[240,192]{1,0:T(8,128)(2,1)S(1)} %get-tuple-element.37), channel_id=1, source_target_pairs={{0,2},{4,0},{8,4},{12,8},{14,12},{10,14},{6,10},{2,6},{1,3},{5,1},... | collective-permute-start | bytes 276488 | tf_op jit(solution)/shard_map/ppermute | solution.py:176
  (29 other events, 233.5 us)

commit v13 on v8

--- a/solution.py
+++ b/solution.py
@@ -225,11 +225,56 @@
     norm_scale = (lax.axis_size("dp") * positions * lax.axis_size("seq")) ** (-0.5)
     seq_count, dp_count = lax.axis_size("seq"), lax.axis_size("dp")
     rows_per = KW * C // (seq_count * dp_count)
+    stacked = jnp.stack(
+        [
+            grad_padded[2 * half_kernel - offset : 2 * half_kernel - offset + positions]
+            for offset in range(KW)
+        ],
+        axis=1,
+    )
+    weight_blocks = conv_weight.reshape(KW, C, CO)
+    grad_normed = jnp.einsum(
+        "pko,kco->pc", stacked, weight_blocks, preferred_element_type=jnp.float32
+    )
+    scaled_grad = grad_normed * channel_gain
+    grad_merged = inverse * scaled_grad - merged * inverse**3 * jnp.mean(
+        scaled_grad * merged, axis=1, keepdims=True
+    )
+    grad_skip = grad_merged.astype(jnp.bfloat16)
+    grad_trunk = jnp.dot(
+        upsample.T.astype(jnp.float32),
+        grad_merged,
+        precision=lax.Precision.HIGHEST,
+        preferred_element_type=jnp.float32,
+    ).astype(jnp.bfloat16)
+    grad_heads = grad_trunk.reshape(local_tokens, H, DV)
+    row_delta = jnp.sum(grad_heads.astype(jnp.float32) * attended.astype(jnp.float32), axis=2)
+    value_grad = jnp.einsum(
+        "ihd,jhd->hij", grad_heads, all_values, preferred_element_type=jnp.float32
+    )
+    slopes = (softmax * (value_grad - row_delta.T[:, :, None])).astype(jnp.bfloat16)
+    grad_queries = (
+        jnp.einsum("hij,jhd->ihd", slopes, all_keys, preferred_element_type=jnp.float32)
+        * score_scale
+    ).astype(jnp.bfloat16)
+    key_part = (
+        jnp.einsum("hij,ihd->jhd", slopes, query_heads, preferred_element_type=jnp.float32)
+        * score_scale
+    )
+    value_part = jnp.einsum("hij,ihd->jhd", rounded, grad_heads, preferred_element_type=jnp.float32)
+    terms = jnp.concatenate(
+        [
+            key_part.reshape(-1, H * DK),
+            value_part.reshape(-1, H * DV),
+        ],
+        axis=1,
+    ).astype(jnp.bfloat16)
     half_co = CO // 2
     if dp_count == 2:
         partner = [(0, 1), (1, 0)]
         both_padded = jnp.stack([padded, lax.ppermute(padded, "dp", partner)])
         both_grad = jnp.stack([grad_pre, lax.ppermute(grad_pre, "dp", partner)])
+        both_padded, both_grad, terms = lax.optimization_barrier((both_padded, both_grad, terms))
         full_weight = (
             jnp.concatenate(
                 [
@@ -279,50 +324,6 @@
             ],
             axis=1,
         )
-    stacked = jnp.stack(
-        [
-            grad_padded[2 * half_kernel - offset : 2 * half_kernel - offset + positions]
-            for offset in range(KW)
-        ],
-        axis=1,
-    )
-    weight_blocks = conv_weight.reshape(KW, C, CO)
-    grad_normed = jnp.einsum(
-        "pko,kco->pc", stacked, weight_blocks, preferred_element_type=jnp.float32
-    )
-    scaled_grad = grad_normed * channel_gain
-    grad_merged = inverse * scaled_grad - merged * inverse**3 * jnp.mean(
-        scaled_grad * merged, axis=1, keepdims=True
-    )
-    grad_skip = grad_merged.astype(jnp.bfloat16)
-    grad_trunk = jnp.dot(
-        upsample.T.astype(jnp.float32),
-        grad_merged,
-        precision=lax.Precision.HIGHEST,
-        preferred_element_type=jnp.float32,
-    ).astype(jnp.bfloat16)
-    grad_heads = grad_trunk.reshape(local_tokens, H, DV)
-    row_delta = jnp.sum(grad_heads.astype(jnp.float32) * attended.astype(jnp.float32), axis=2)
-    value_grad = jnp.einsum(
-        "ihd,jhd->hij", grad_heads, all_values, preferred_element_type=jnp.float32
-    )
-    slopes = (softmax * (value_grad - row_delta.T[:, :, None])).astype(jnp.bfloat16)
-    grad_queries = (
-        jnp.einsum("hij,jhd->ihd", slopes, all_keys, preferred_element_type=jnp.float32)
-        * score_scale
-    ).astype(jnp.bfloat16)
-    key_part = (
-        jnp.einsum("hij,ihd->jhd", slopes, query_heads, preferred_element_type=jnp.float32)
-        * score_scale
-    )
-    value_part = jnp.einsum("hij,ihd->jhd", rounded, grad_heads, preferred_element_type=jnp.float32)
-    terms = jnp.concatenate(
-        [
-            key_part.reshape(-1, H * DK),
-            value_part.reshape(-1, H * DV),
-        ],
-        axis=1,
-    ).astype(jnp.bfloat16)
     term_blocks = [
         terms[m * local_tokens : (m + 1) * local_tokens] for m in range(lax.axis_size("seq"))
     ]

time: 159 us -> 162 us (1.019)
  other arithmetic: 18.3 us -> 23.8 us
  matrix products: 24.7 us -> 19.7 us
  waiting for transfers between devices: 44.8 us -> 47.2 us
    ppermute x8, waiting for transfers between devices: 2.97 us -> 9.68 us  [ring_scatter_back(): received = lax.ppermute(acc, 'seq', perm).astype(jnp.float32)]
    dot_general x5, matrix products: 8.5 us -> 3.07 us  [body(): jnp.einsum('spc,spo->co', both_padded[:, offset:offset + positions], both...]
    another operation x2 -> x5, other arithmetic: 0.21 us -> 4.48 us  [the longest x2 2.08 us: body(): both_padded = jnp.stack([padded, lax.ppermute(padded, 'dp', partner)])]
    ppermute x14, waiting for transfers between devices: 19.8 us -> 17.4 us  [ring_reduce_scatter_sliced(): received = lax.ppermute(acc, axis, perm).astype(jnp.float32)]
    dot_general x1, matrix products: 4.22 us -> 2.09 us  [body(): jnp.einsum('ihd,jhd->hij', grad_heads, all_values, preferred_element_type...]
    concatenate x1, other arithmetic: 0.05 us -> 1.92 us  [body(): jnp.concatenate([key_part.reshape(-1, H * DK), value_part.reshape(-1, H *...]
    dot_general x1, matrix products: 1.77 us -> 3.49 us  [body(): jnp.einsum('hij,ihd->jhd', rounded, grad_heads, preferred_element_type=jn...]
    convert_element_type x2 -> x3, other arithmetic: 3.72 us -> 4.1 us  [ring_scatter_back(): add_part(chain[t - 2].astype(jnp.float32), received, side)]
  transfers between devices with their start and end apart: 36 -> 36, of which waited for: 20 -> 21; matrix products, arithmetic and copies ran while one was open for 27% -> 29% of each run, Pallas kernels for 0% -> 0%
where the time goes in v13:
time: 162 us; the launch traced here: 161 us
  waiting for transfers between devices  47.2 us (29%)
  starting transfers between devices  44.8 us (28%)
  other arithmetic  23.8 us (15%)
  local copies, waits for them, and re-layouts  23.7 us (15%)
  matrix products  19.7 us (12%)
    ppermute x14, waiting for transfers between devices, ring_reduce_scatter_sliced(): received = lax.ppermute(acc, axis, perm).astype(jnp.float32)  17.4 us
    ppermute x14, starting transfers between devices, ring_reduce_scatter_sliced(): received = lax.ppermute(acc, axis, perm).astype(jnp.float32)  16.9 us
    ppermute x3, waiting for transfers between devices, ring_gather(): current = lax.ppermute(current, 'seq', forward)  12 us
    ppermute x8, waiting for transfers between devices, ring_scatter_back(): received = lax.ppermute(acc, 'seq', perm).astype(jnp.float32)  9.68 us
    unnamed x52, local copies, waits for them, and re-layouts  9.47 us
    ppermute x2, starting transfers between devices, extended(): before = lax.ppermute(last, axis, up)  8.51 us
    ppermute x8, starting transfers between devices, ring_scatter_back(): received = lax.ppermute(acc, 'seq', perm).astype(jnp.float32)  7.33 us
    ppermute x3, starting transfers between devices, ring_gather(): current = lax.ppermute(current, 'seq', forward)  6.37 us
  transfers between devices with their start and end apart: 36, of which 21 were waited for; matrix products, arithmetic and copies ran while one was open for 29% of the time, Pallas kernels for 0%

profile of v13, /device:TPU:0, one launch (start us, length us, event | category | flops | bytes accessed | tf_op | source)
XLA Modules:
  0.0 160.8 jit_solution(3272190076495285562)
XLA Ops:
  0.6 1.2 copy.34
  3.9 3.1 %collective-permute-start = (bf16[128,1280]{0,1:T(8,128)(2,1)}, bf16[128,1280]{0,1:T(8,128)(2,1)}, u32[]{:S(2)}, u32[]{:S(2)}) collective-permute-start(bf16[128,1280]{0,1:T(8,128)(2,1)} %get-tuple-element.59), channel_id=1, source_target_pairs={{0,4},{4,8},{8,12},{12,14},{14,10},{10,6},{6,2},{2,0},{1,5},{5,9},... | collective-permute-start | bytes 983048 | tf_op jit(solution)/shard_map/ppermute | solution.py:76
  8.7 6.2 %collective-permute-done = bf16[128,1280]{0,1:T(8,128)(2,1)} collective-permute-done((bf16[128,1280]{0,1:T(8,128)(2,1)}, bf16[128,1280]{0,1:T(8,128)(2,1)}, u32[]{:S(2)}, u32[]{:S(2)}) %collective-permute-start) | collective-permute-done | bytes 327712 | tf_op jit(solution)/shard_map/ppermute | solution.py:76
  14.9 1.8 %collective-permute-start.1 = (bf16[128,1280]{0,1:T(8,128)(2,1)}, bf16[128,1280]{0,1:T(8,128)(2,1)S(1)}, u32[]{:S(2)}, u32[]{:S(2)}) collective-permute-start(bf16[128,1280]{0,1:T(8,128)(2,1)} %collective-permute-done), channel_id=1, source_target_pairs={{0,4},{4,8},{8,12},{12,14},{14,10},{10,6},{6,2},{2,0},{1,5},{5,9},... | collective-permute-start | bytes 983048 | tf_op jit(solution)/shard_map/ppermute | solution.py:76
  16.9 1.2 fusion.53
  18.1 5.8 %collective-permute-done.1 = bf16[128,1280]{0,1:T(8,128)(2,1)S(1)} collective-permute-done((bf16[128,1280]{0,1:T(8,128)(2,1)}, bf16[128,1280]{0,1:T(8,128)(2,1)S(1)}, u32[]{:S(2)}, u32[]{:S(2)}) %collective-permute-start.1) | collective-permute-done | bytes 327712 | tf_op jit(solution)/shard_map/ppermute | solution.py:76
  24.0 1.5 collective-permute-start.2
  26.0 1.7 %constant_dynamic-update-slice_fusion.5 = bf16[1024,1280]{0,1:T(8,128)(2,1)} fusion(bf16[1024,1280]{0,1:T(8,128)(2,1)} %get-tuple-element.60, bf16[128,1280]{0,1:T(8,128)(2,1)} %collective-permute-done), kind=kLoop, calls=%fused_computation.139 | loop fusion | bytes 655360
  28.5 4.8 %collective-permute-done.5 = bf16[128,1280]{0,1:T(8,128)(2,1)S(1)} collective-permute-done((bf16[128,1280]{0,1:T(8,128)(2,1)S(1)}, bf16[128,1280]{0,1:T(8,128)(2,1)S(1)}, u32[]{:S(2)}, u32[]{:S(2)}) %collective-permute-start.5) | collective-permute-done | bytes 327712 | tf_op jit(solution)/shard_map/ppermute | solution.py:82
  33.9 1.6 collective-permute-start.6
  40.1 1.5 slice.167
  41.6 1.9 %slice.168 = bf16[1024,512]{0,1:T(8,128)(2,1)S(1)} slice(bf16[1024,1280]{0,1:T(8,128)(2,1)} %maximum_dynamic-update-slice_fusion), slice={[0:1024], [0:512]} | slice | bytes 2097152 | tf_op jit(solution)/shard_map/slice | solution.py:191
  47.0 3.4 %collective-permute-start.8 = (bf16[2,768]{1,0:T(2,128)(2,1)S(1)}, bf16[2,768]{1,0:T(2,128)(2,1)S(1)}, u32[]{:S(2)}, u32[]{:S(2)}) collective-permute-start(bf16[2,768]{1,0:T(2,128)(2,1)S(1)} %get-tuple-element.58), channel_id=1, source_target_pairs={{0,2},{2,4},{4,6},{6,8},{8,10},{10,12},{12,14},{1,3},{3,5},{5,7},{... | collective-permute-start | bytes 9224 | tf_op jit(solution)/shard_map/ppermute | solution.py:24
  50.7 1.3 collective-permute-start.9
  52.2 1.3 constant_dynamic-update-slice_fusion.7
  53.5 2.7 %collective-permute-done.9 = bf16[2,768]{1,0:T(2,128)(2,1)S(1)} collective-permute-done((bf16[2,768]{1,0:T(2,128)(2,1)S(1)}, bf16[2,768]{1,0:T(2,128)(2,1)S(1)}, u32[]{:S(2)}, u32[]{:S(2)}) %collective-permute-start.9) | collective-permute-done | bytes 3104 | tf_op jit(solution)/shard_map/ppermute | solution.py:25
  56.4 2.9 %fusion.27 = (bf16[256,384]{1,0:T(8,128)(2,1)S(1)}, bf16[1,256,384]{2,1,0:T(8,128)(2,1)}) fusion(bf16[1,256,384]{2,1,0:T(8,128)(2,1)} %param.15, bf16[256,3840]{1,0:T(8,128)(2,1)S(1)} %fusion.28, bf16[3840,384]{1,0:T(8,128)(2,1)S(1)} %copy-done), kind=kOutput, calls=%fused_computation.61 | convolution fusion | flops 756252672 | bytes 5505024 | tf_op jit(solution)/shard_map/dot_general | solution.py:220
  59.4 1.4 collective-permute-start.10
  60.8 5.1 %collective-permute-start.11 = (bf16[2,384]{1,0:T(2,128)(2,1)S(1)}, bf16[2,384]{1,0:T(2,128)(2,1)S(1)}, u32[]{:S(2)}, u32[]{:S(2)}) collective-permute-start(bf16[2,384]{1,0:T(2,128)(2,1)S(1)} %get-tuple-element.61), channel_id=1, source_target_pairs={{0,2},{2,4},{4,6},{6,8},{8,10},{10,12},{12,14},{1,3},{3,5},{5,7},{... | collective-permute-start | bytes 4616 | tf_op jit(solution)/shard_map/ppermute | solution.py:24
  71.8 3.5 %convolution_convert_fusion = bf16[4,192,1024]{2,1,0:T(8,128)(2,1)} fusion(bf16[128,4,192]{0,2,1:T(8,128)(2,1)S(1)} %bitcast.197, f32[4,1024,128]{2,1,0:T(8,128)} %copy-done.1, f32[4,128]{1,0:T(4,128)S(1)} %log_add_fusion), kind=kOutput, calls=%fused_computation.11 | convolution fusion | flops 203685888 | bytes 3868672 | tf_op jit(solution)/shard_map/hij,ihd->jhd/dot_general | solution.py:264
  75.3 2.1 %multiply_convert_fusion.1 = bf16[4,128,1024]{1,2,0:T(8,128)(2,1)} fusion(f32[4,1024,128]{2,1,0:T(8,128)S(1)} %copy-done.2, bf16[128,4,192]{0,2,1:T(8,128)(2,1)S(1)} %bitcast.198, bf16[1024,4,192]{0,2,1:T(8,128)(2,1)S(1)} %bitcast.190, f32[4,128]{1,0:T(4,128)S(1)} %bitcast.206, f32[4,128]{1,0:T(4,128)S(1)} %log_add_fusion), kind=kOutput, calls=%fused_computation.9 | convolution fusion | flops 203948032 | bytes 4919296 | tf_op jit(solution)/shard_map/ihd,jhd->hij/dot_general | solution.py:252
  77.4 2.6 %copy.47 = bf16[1024,768]{1,0:T(8,128)(2,1)} copy(bf16[1024,768]{0,1:T(8,128)(2,1)} %bitcast.194) | data formatting | bytes 3145728 | tf_op jit(solution)/shard_map/reshape | solution.py:268
  80.0 2.6 %fusion.9 = bf16[1024,4,128]{2,0,1:T(8,128)(2,1)} fusion(bf16[4,128,1024]{1,2,0:T(8,128)(2,1)} %multiply_convert_fusion.1, bf16[128,4,128]{0,2,1:T(8,128)(2,1)S(1)} %bitcast.201), kind=kOutput, calls=%fused_computation.22 | convolution fusion | flops 135266304 | bytes 2228224 | tf_op jit(solution)/shard_map/hij,ihd->jhd/dot_general | solution.py:261
  82.7 2.3 %copy.44 = bf16[1024,4,128]{0,2,1:T(8,128)(2,1)} copy(bf16[1024,4,128]{2,0,1:T(8,128)(2,1)} %fusion.9) | data formatting | bytes 2097152 | tf_op jit(solution)/shard_map/mul | solution.py:261
  84.9 2.3 %copy.46 = bf16[1024,512]{1,0:T(8,128)(2,1)} copy(bf16[1024,512]{0,1:T(8,128)(2,1)} %bitcast.195) | data formatting | bytes 2097152 | tf_op jit(solution)/shard_map/reshape | solution.py:267
  87.2 1.9 %pad_maximum_fusion = bf16[1024,1280]{1,0:T(8,128)(2,1)S(1)} fusion(bf16[1024,768]{1,0:T(8,128)(2,1)} %copy.47, bf16[1024,512]{1,0:T(8,128)(2,1)} %copy.46), kind=kLoop, calls=%fused_computation.1 | loop fusion | flops 5242880 | bytes 5242880 | tf_op jit(solution)/shard_map/concatenate | solution.py:265
  89.2 1.2 pad_maximum_fusion.5
  95.1 4.5 %collective-permute-start.22 = (bf16[240,192]{1,0:T(8,128)(2,1)S(1)}, bf16[240,192]{1,0:T(8,128)(2,1)S(1)}, u32[]{:S(2)}, u32[]{:S(2)}) collective-permute-start(bf16[240,192]{1,0:T(8,128)(2,1)S(1)} %get-tuple-element.43), channel_id=1, source_target_pairs={{0,4},{4,8},{8,12},{12,14},{14,10},{10,6},{6,2},{2,0},{1,5},{5,9},... | collective-permute-start | bytes 276488 | tf_op jit(solution)/shard_map/ppermute | solution.py:176
  100.1 1.7 %collective-permute-start.18 = (bf16[128,640]{1,0:T(8,128)(2,1)S(1)}, bf16[128,640]{1,0:T(8,128)(2,1)S(1)}, u32[]{:S(2)}, u32[]{:S(2)}) collective-permute-start(bf16[128,640]{1,0:T(8,128)(2,1)S(1)} %get-tuple-element.50), channel_id=1, source_target_pairs={{0,4},{4,8},{8,12},{12,14},{14,10},{10,6},{6,2},{2,0},{1,5},{5,9},... | collective-permute-start | bytes 491528 | tf_op jit(solution)/shard_map/ppermute | solution.py:119
  101.8 1.5 collective-permute-done.22
  103.3 1.9 %collective-permute-done.29 = bf16[240,192]{1,0:T(8,128)(2,1)S(1)} collective-permute-done((bf16[240,192]{1,0:T(8,128)(2,1)S(1)}, bf16[240,192]{1,0:T(8,128)(2,1)S(1)}, u32[]{:S(2)}, u32[]{:S(2)}) %collective-permute-start.29) | collective-permute-done | bytes 92192 | tf_op jit(solution)/shard_map/ppermute | solution.py:176
  105.4 1.6 %collective-permute-start.23 = (bf16[240,192]{1,0:T(8,128)(2,1)S(1)}, bf16[240,192]{1,0:T(8,128)(2,1)S(1)}, u32[]{:S(2)}, u32[]{:S(2)}) collective-permute-start(bf16[240,192]{1,0:T(8,128)(2,1)S(1)} %get-tuple-element.41), channel_id=1, source_target_pairs={{0,4},{4,8},{8,12},{12,14},{14,10},{10,6},{6,2},{2,0},{1,5},{5,9},... | collective-permute-start | bytes 276488 | tf_op jit(solution)/shard_map/ppermute | solution.py:176
  107.7 2.6 %collective-permute-done.23 = bf16[240,192]{1,0:T(8,128)(2,1)S(1)} collective-permute-done((bf16[240,192]{1,0:T(8,128)(2,1)S(1)}, bf16[240,192]{1,0:T(8,128)(2,1)S(1)}, u32[]{:S(2)}, u32[]{:S(2)}) %collective-permute-start.23) | collective-permute-done | bytes 92192 | tf_op jit(solution)/shard_map/ppermute | solution.py:176
  110.3 1.6 collective-permute-done.30
  112.0 1.6 %collective-permute-start.24 = (bf16[240,192]{1,0:T(8,128)(2,1)S(1)}, bf16[240,192]{1,0:T(8,128)(2,1)S(1)}, u32[]{:S(2)}, u32[]{:S(2)}) collective-permute-start(bf16[240,192]{1,0:T(8,128)(2,1)S(1)} %get-tuple-element.39), channel_id=1, source_target_pairs={{0,4},{4,8},{8,12},{12,14},{14,10},{10,6},{6,2},{2,0},{1,5},{5,9},... | collective-permute-start | bytes 276488 | tf_op jit(solution)/shard_map/ppermute | solution.py:176
  114.6 3.1 %collective-permute-done.24 = bf16[240,192]{1,0:T(8,128)(2,1)S(1)} collective-permute-done((bf16[240,192]{1,0:T(8,128)(2,1)S(1)}, bf16[240,192]{1,0:T(8,128)(2,1)S(1)}, u32[]{:S(2)}, u32[]{:S(2)}) %collective-permute-start.24) | collective-permute-done | bytes 92192 | tf_op jit(solution)/shard_map/ppermute | solution.py:176
  117.7 1.7 %collective-permute-done.31 = bf16[240,192]{1,0:T(8,128)(2,1)S(1)} collective-permute-done((bf16[240,192]{1,0:T(8,128)(2,1)S(1)}, bf16[240,192]{1,0:T(8,128)(2,1)S(1)}, u32[]{:S(2)}, u32[]{:S(2)}) %collective-permute-start.31) | collective-permute-done | bytes 92192 | tf_op jit(solution)/shard_map/ppermute | solution.py:176
  122.7 2.3 %collective-permute-done.25 = bf16[240,192]{1,0:T(8,128)(2,1)S(1)} collective-permute-done((bf16[240,192]{1,0:T(8,128)(2,1)S(1)}, bf16[240,192]{1,0:T(8,128)(2,1)S(1)}, u32[]{:S(2)}, u32[]{:S(2)}) %collective-permute-start.25) | collective-permute-done | bytes 92192 | tf_op jit(solution)/shard_map/ppermute | solution.py:176
  129.0 1.5 collective-permute-start.16
  132.0 1.9 %fusion.37 = (bf16[240,192]{1,0:T(8,128)(2,1)}, bf16[240,192]{1,0:T(8,128)(2,1)}) fusion(f32[8,2,240,384]{3,2,1,0:T(8,128)} %bitcast.186, s32[]{:T(128)S(6)} %select_n.538, s32[]{:T(128)S(6)} %select_n.498, bf16[240,192]{1,0:T(8,128)(2,1)S(1)} %collective-permute-done.26, s32[]{:T(128)S(6)} %select_n.602, bf16[240,192]{1,0:T(8,128)(2,1)} %collective-permute-done.33), kind=kLoop, calls=%fused_computation.95 | loop fusion | flops 276480 | bytes 737292 | tf_op jit(solution)/shard_map/convert_element_type | solution.py:179
  133.9 1.4 collective-permute-start.27
  136.0 1.8 %collective-permute-done.16 = bf16[128,1280]{1,0:T(8,128)(2,1)} collective-permute-done((bf16[128,1280]{1,0:T(8,128)(2,1)}, bf16[128,1280]{1,0:T(8,128)(2,1)}, u32[]{:S(2)}, u32[]{:S(2)}) %collective-permute-start.16) | collective-permute-done | bytes 327712 | tf_op jit(solution)/shard_map/ppermute | solution.py:119
  137.8 2.3 %add_convert_fusion.3 = (bf16[128,1280]{1,0:T(8,128)(2,1)}, bf16[128,1280]{1,0:T(8,128)(2,1)}) fusion(bf16[128,1280]{1,0:T(8,128)(2,1)} %collective-permute-done.16, bf16[1024,1280]{1,0:T(8,128)(2,1)} %copy-done.8, bf16[128,1280]{1,0:T(8,128)(2,1)} %collective-permute-done.19), kind=kLoop, calls=%fused_computation.44 | loop fusion | flops 1310720 | bytes 1966080 | tf_op jit(solution)/shard_map/convert_element_type | solution.py:123
  142.0 1.3 fusion.36
  143.3 1.5 collective-permute-start.28
  145.4 1.2 collective-permute-start.17
  146.6 3.6 %collective-permute-done.20 = bf16[128,1280]{1,0:T(8,128)(2,1)S(1)} collective-permute-done((bf16[128,1280]{1,0:T(8,128)(2,1)}, bf16[128,1280]{1,0:T(8,128)(2,1)S(1)}, u32[]{:S(2)}, u32[]{:S(2)}) %collective-permute-start.20) | collective-permute-done | bytes 327712 | tf_op jit(solution)/shard_map/ppermute | solution.py:119
  154.2 4.2 %collective-permute-done.21 = bf16[128,1280]{1,0:T(8,128)(2,1)S(1)} collective-permute-done((bf16[128,1280]{1,0:T(8,128)(2,1)S(1)}, bf16[128,1280]{1,0:T(8,128)(2,1)S(1)}, u32[]{:S(2)}, u32[]{:S(2)}) %collective-permute-start.21) | collective-permute-done | bytes 327712 | tf_op jit(solution)/shard_map/ppermute | solution.py:119
  (147 shorter events, 45.6 us)
Async XLA Ops:
  0.6 55.7 %copy-start = (bf16[3840,384]{1,0:T(8,128)(2,1)S(1)}, bf16[3840,384]{1,0:T(8,128)(2,1)}, u32[]{:S(2)}) copy-start(bf16[3840,384]{1,0:T(8,128)(2,1)} %param.14) | copy-start | bytes 8847364
  3.9 11.0 %collective-permute-start = (bf16[128,1280]{0,1:T(8,128)(2,1)}, bf16[128,1280]{0,1:T(8,128)(2,1)}, u32[]{:S(2)}, u32[]{:S(2)}) collective-permute-start(bf16[128,1280]{0,1:T(8,128)(2,1)} %get-tuple-element.59), channel_id=1, source_target_pairs={{0,4},{4,8},{8,12},{12,14},{14,10},{10,6},{6,2},{2,0},{1,5},{5,9},... | collective-permute-start | bytes 983048 | tf_op jit(solution)/shard_map/ppermute | solution.py:76
  6.9 9.8 %collective-permute-start.3 = (bf16[128,1280]{0,1:T(8,128)(2,1)}, bf16[128,1280]{0,1:T(8,128)(2,1)S(1)}, u32[]{:S(2)}, u32[]{:S(2)}) collective-permute-start(bf16[128,1280]{0,1:T(8,128)(2,1)} %get-tuple-element.59), channel_id=1, source_target_pairs={{0,2},{4,0},{8,4},{12,8},{14,12},{10,14},{6,10},{2,6},{1,3},{5,1},... | collective-permute-start | bytes 983048 | tf_op jit(solution)/shard_map/ppermute | solution.py:82
  7.9 35.6 %copy-start.15 = (bf16[1,128,512]{1,2,0:T(8,128)(2,1)}, bf16[1,128,512]{1,2,0:T(8,128)(2,1)S(1)}, u32[]{:S(2)}) copy-start(bf16[1,128,512]{1,2,0:T(8,128)(2,1)S(1)} %copy.66) | copy-start | bytes 393220
  14.9 9.1 %collective-permute-start.1 = (bf16[128,1280]{0,1:T(8,128)(2,1)}, bf16[128,1280]{0,1:T(8,128)(2,1)S(1)}, u32[]{:S(2)}, u32[]{:S(2)}) collective-permute-start(bf16[128,1280]{0,1:T(8,128)(2,1)} %collective-permute-done), channel_id=1, source_target_pairs={{0,4},{4,8},{8,12},{12,14},{14,10},{10,6},{6,2},{2,0},{1,5},{5,9},... | collective-permute-start | bytes 983048 | tf_op jit(solution)/shard_map/ppermute | solution.py:76
  16.7 8.8 %collective-permute-start.4 = (bf16[128,1280]{0,1:T(8,128)(2,1)S(1)}, bf16[128,1280]{0,1:T(8,128)(2,1)S(1)}, u32[]{:S(2)}, u32[]{:S(2)}) collective-permute-start(bf16[128,1280]{0,1:T(8,128)(2,1)S(1)} %collective-permute-done.3), channel_id=1, source_target_pairs={{0,2},{4,0},{8,4},{12,8},{14,12},{10,14},{6,10},{2,6},{1,3},{5,1},... | collective-permute-start | bytes 983048 | tf_op jit(solution)/shard_map/ppermute | solution.py:82
  16.9 28.5 %copy-start.18 = (s32[256]{0:T(256)}, s32[256]{0:T(256)S(1)}, u32[]{:S(2)}) copy-start(s32[256]{0:T(256)S(1)} %and_select_fusion) | copy-start | bytes 3076
  24.0 9.9 %collective-permute-start.2 = (bf16[128,1280]{0,1:T(8,128)(2,1)S(1)}, bf16[128,1280]{0,1:T(8,128)(2,1)S(1)}, u32[]{:S(2)}, u32[]{:S(2)}) collective-permute-start(bf16[128,1280]{0,1:T(8,128)(2,1)S(1)} %collective-permute-done.1), channel_id=1, source_target_pairs={{0,4},{4,8},{8,12},{12,14},{14,10},{10,6},{6,2},{2,0},{1,5},{5,9},... | collective-permute-start | bytes 983048 | tf_op jit(solution)/shard_map/ppermute | solution.py:76
  25.5 7.8 %collective-permute-start.5 = (bf16[128,1280]{0,1:T(8,128)(2,1)S(1)}, bf16[128,1280]{0,1:T(8,128)(2,1)S(1)}, u32[]{:S(2)}, u32[]{:S(2)}) collective-permute-start(bf16[128,1280]{0,1:T(8,128)(2,1)S(1)} %collective-permute-done.4), channel_id=1, source_target_pairs={{0,2},{4,0},{8,4},{12,8},{14,12},{10,14},{6,10},{2,6},{1,3},{5,1},... | collective-permute-start | bytes 983048 | tf_op jit(solution)/shard_map/ppermute | solution.py:82
  33.3 5.4 %collective-permute-start.7 = (bf16[128,640]{0,1:T(8,128)(2,1)S(1)}, bf16[128,640]{0,1:T(8,128)(2,1)S(1)}, u32[]{:S(2)}, u32[]{:S(2)}) collective-permute-start(bf16[128,640]{0,1:T(8,128)(2,1)S(1)} %slice.166), channel_id=1, source_target_pairs={{0,2},{4,0},{8,4},{12,8},{14,12},{10,14},{6,10},{2,6},{1,3},{5,1},... | collective-permute-start | bytes 491528 | tf_op jit(solution)/shard_map/ppermute | solution.py:85
  33.9 5.4 %collective-permute-start.6 = (bf16[128,640]{0,1:T(8,128)(2,1)S(1)}, bf16[128,640]{0,1:T(8,128)(2,1)S(1)}, u32[]{:S(2)}, u32[]{:S(2)}) collective-permute-start(bf16[128,640]{0,1:T(8,128)(2,1)S(1)} %slice.165), channel_id=1, source_target_pairs={{0,4},{4,8},{8,12},{12,14},{14,10},{10,6},{6,2},{2,0},{1,5},{5,9},... | collective-permute-start | bytes 491528 | tf_op jit(solution)/shard_map/ppermute | solution.py:79
  47.0 5.0 %collective-permute-start.8 = (bf16[2,768]{1,0:T(2,128)(2,1)S(1)}, bf16[2,768]{1,0:T(2,128)(2,1)S(1)}, u32[]{:S(2)}, u32[]{:S(2)}) collective-permute-start(bf16[2,768]{1,0:T(2,128)(2,1)S(1)} %get-tuple-element.58), channel_id=1, source_target_pairs={{0,2},{2,4},{4,6},{6,8},{8,10},{10,12},{12,14},{1,3},{3,5},{5,7},{... | collective-permute-start | bytes 9224 | tf_op jit(solution)/shard_map/ppermute | solution.py:24
  50.7 5.5 %collective-permute-start.9 = (bf16[2,768]{1,0:T(2,128)(2,1)S(1)}, bf16[2,768]{1,0:T(2,128)(2,1)S(1)}, u32[]{:S(2)}, u32[]{:S(2)}) collective-permute-start(bf16[2,768]{1,0:T(2,128)(2,1)S(1)} %get-tuple-element.57), channel_id=1, source_target_pairs={{2,0},{4,2},{6,4},{8,6},{10,8},{12,10},{14,12},{3,1},{5,3},{7,5},{... | collective-permute-start | bytes 9224 | tf_op jit(solution)/shard_map/ppermute | solution.py:25
  59.3 8.1 %copy-start.4 = (f32[256,768]{1,0:T(8,128)S(1)}, f32[256,768]{1,0:T(8,128)}, u32[]{:S(2)}) copy-start(f32[256,768]{1,0:T(8,128)} %copy-done.3) | copy-start | bytes 2359300
  59.3 29.8 %collective-permute-start.13 = (bf16[256,384]{1,0:T(8,128)(2,1)S(1)}, bf16[256,384]{1,0:T(8,128)(2,1)}, u32[]{:S(2)}, u32[]{:S(2)}) collective-permute-start(bf16[256,384]{1,0:T(8,128)(2,1)S(1)} %get-tuple-element.55), channel_id=1, source_target_pairs={{0,1},{1,0},{2,3},{3,2},{4,5},{5,4},{6,7},{7,6},{8,9},{9,8},{10,11... | collective-permute-start | bytes 589832 | tf_op jit(solution)/shard_map/ppermute | solution.py:276
  59.4 7.7 %collective-permute-start.10 = (bf16[2,384]{1,0:T(2,128)(2,1)S(1)}, bf16[2,384]{1,0:T(2,128)(2,1)S(1)}, u32[]{:S(2)}, u32[]{:S(2)}) collective-permute-start(bf16[2,384]{1,0:T(2,128)(2,1)S(1)} %get-tuple-element.62), channel_id=1, source_target_pairs={{2,0},{4,2},{6,4},{8,6},{10,8},{12,10},{14,12},{3,1},{5,3},{7,5},{... | collective-permute-start | bytes 4616 | tf_op jit(solution)/shard_map/ppermute | solution.py:25
  60.8 6.4 %collective-permute-start.11 = (bf16[2,384]{1,0:T(2,128)(2,1)S(1)}, bf16[2,384]{1,0:T(2,128)(2,1)S(1)}, u32[]{:S(2)}, u32[]{:S(2)}) collective-permute-start(bf16[2,384]{1,0:T(2,128)(2,1)S(1)} %get-tuple-element.61), channel_id=1, source_target_pairs={{0,2},{2,4},{4,6},{6,8},{8,10},{10,12},{12,14},{1,3},{3,5},{5,7},{... | collective-permute-start | bytes 4616 | tf_op jit(solution)/shard_map/ppermute | solution.py:24
  67.0 23.4 %collective-permute-start.12 = (bf16[260,768]{1,0:T(8,128)(2,1)}, bf16[260,768]{1,0:T(8,128)(2,1)}, u32[]{:S(2)}, u32[]{:S(2)}) collective-permute-start(bf16[260,768]{1,0:T(8,128)(2,1)} %get-tuple-element.54), channel_id=1, source_target_pairs={{0,1},{1,0},{2,3},{3,2},{4,5},{5,4},{6,7},{7,6},{8,9},{9,8},{10,11... | collective-permute-start | bytes 1198088 | tf_op jit(solution)/shard_map/ppermute | solution.py:275
  68.5 3.2 %copy-start.13 = (bf16[4,192,128]{2,1,0:T(8,128)(2,1)S(1)}, bf16[4,192,128]{2,1,0:T(8,128)(2,1)}, u32[]{:S(2)}) copy-start(bf16[4,192,128]{2,1,0:T(8,128)(2,1)} %copy-done.12) | copy-start | bytes 589828
  71.7 3.6 %copy-start.2 = (f32[4,1024,128]{2,1,0:T(8,128)S(1)}, f32[4,1024,128]{2,1,0:T(8,128)}, u32[]{:S(2)}) copy-start(f32[4,1024,128]{2,1,0:T(8,128)} %copy-done.1) | copy-start | bytes 6291460
  71.7 3.6 %copy-start.7 = (bf16[1024,768]{0,1:T(8,128)(2,1)S(1)}, bf16[1024,768]{0,1:T(8,128)(2,1)}, u32[]{:S(2)}) copy-start(bf16[1024,768]{0,1:T(8,128)(2,1)} %copy-done.6) | copy-start | bytes 4718596
  87.2 3.2 %copy-start.14 = (bf16[1,260,768]{2,1,0:T(8,128)(2,1)S(1)}, bf16[1,260,768]{2,1,0:T(8,128)(2,1)}, u32[]{:S(2)}) copy-start(bf16[1,260,768]{2,1,0:T(8,128)(2,1)} %get-tuple-element.53) | copy-start | bytes 1198084
  89.1 39.1 %copy-start.8 = (bf16[1024,1280]{1,0:T(8,128)(2,1)}, bf16[1024,1280]{1,0:T(8,128)(2,1)S(1)}, u32[]{:S(2)}) copy-start(bf16[1024,1280]{1,0:T(8,128)(2,1)S(1)} %pad_maximum_fusion) | copy-start | bytes 7864324
  94.9 30.5 %copy-start.5 = (f32[3840,384]{1,0:T(8,128)}, f32[3840,384]{1,0:T(8,128)S(1)}, u32[]{:S(2)}) copy-start(f32[3840,384]{1,0:T(8,128)S(1)} %broadcast_multiply_fusion) | copy-start | bytes 17694724
  95.1 8.2 %collective-permute-start.22 = (bf16[240,192]{1,0:T(8,128)(2,1)S(1)}, bf16[240,192]{1,0:T(8,128)(2,1)S(1)}, u32[]{:S(2)}, u32[]{:S(2)}) collective-permute-start(bf16[240,192]{1,0:T(8,128)(2,1)S(1)} %get-tuple-element.43), channel_id=1, source_target_pairs={{0,4},{4,8},{8,12},{12,14},{14,10},{10,6},{6,2},{2,0},{1,5},{5,9},... | collective-permute-start | bytes 276488 | tf_op jit(solution)/shard_map/ppermute | solution.py:176
  99.6 5.6 %collective-permute-start.29 = (bf16[240,192]{1,0:T(8,128)(2,1)S(1)}, bf16[240,192]{1,0:T(8,128)(2,1)S(1)}, u32[]{:S(2)}, u32[]{:S(2)}) collective-permute-start(bf16[240,192]{1,0:T(8,128)(2,1)S(1)} %get-tuple-element.44), channel_id=1, source_target_pairs={{0,2},{4,0},{8,4},{12,8},{14,12},{10,14},{6,10},{2,6},{1,3},{5,1},... | collective-permute-start | bytes 276488 | tf_op jit(solution)/shard_map/ppermute | solution.py:176
  99.7 7.9 %collective-permute-start.14 = (bf16[128,640]{1,0:T(8,128)(2,1)S(1)}, bf16[128,640]{1,0:T(8,128)(2,1)S(1)}, u32[]{:S(2)}, u32[]{:S(2)}) collective-permute-start(bf16[128,640]{1,0:T(8,128)(2,1)S(1)} %get-tuple-element.49), channel_id=1, source_target_pairs={{0,2},{4,0},{8,4},{12,8},{14,12},{10,14},{6,10},{2,6},{1,3},{5,1},... | collective-permute-start | bytes 491528 | tf_op jit(solution)/shard_map/ppermute | solution.py:119
  100.1 7.5 %collective-permute-start.18 = (bf16[128,640]{1,0:T(8,128)(2,1)S(1)}, bf16[128,640]{1,0:T(8,128)(2,1)S(1)}, u32[]{:S(2)}, u32[]{:S(2)}) collective-permute-start(bf16[128,640]{1,0:T(8,128)(2,1)S(1)} %get-tuple-element.50), channel_id=1, source_target_pairs={{0,4},{4,8},{8,12},{12,14},{14,10},{10,6},{6,2},{2,0},{1,5},{5,9},... | collective-permute-start | bytes 491528 | tf_op jit(solution)/shard_map/ppermute | solution.py:119
  105.4 4.9 %collective-permute-start.23 = (bf16[240,192]{1,0:T(8,128)(2,1)S(1)}, bf16[240,192]{1,0:T(8,128)(2,1)S(1)}, u32[]{:S(2)}, u32[]{:S(2)}) collective-permute-start(bf16[240,192]{1,0:T(8,128)(2,1)S(1)} %get-tuple-element.41), channel_id=1, source_target_pairs={{0,4},{4,8},{8,12},{12,14},{14,10},{10,6},{6,2},{2,0},{1,5},{5,9},... | collective-permute-start | bytes 276488 | tf_op jit(solution)/shard_map/ppermute | solution.py:176
  107.0 4.9 %collective-permute-start.30 = (bf16[240,192]{1,0:T(8,128)(2,1)S(1)}, bf16[240,192]{1,0:T(8,128)(2,1)S(1)}, u32[]{:S(2)}, u32[]{:S(2)}) collective-permute-start(bf16[240,192]{1,0:T(8,128)(2,1)S(1)} %get-tuple-element.42), channel_id=1, source_target_pairs={{0,2},{4,0},{8,4},{12,8},{14,12},{10,14},{6,10},{2,6},{1,3},{5,1},... | collective-permute-start | bytes 276488 | tf_op jit(solution)/shard_map/ppermute | solution.py:176
  112.0 5.7 %collective-permute-start.24 = (bf16[240,192]{1,0:T(8,128)(2,1)S(1)}, bf16[240,192]{1,0:T(8,128)(2,1)S(1)}, u32[]{:S(2)}, u32[]{:S(2)}) collective-permute-start(bf16[240,192]{1,0:T(8,128)(2,1)S(1)} %get-tuple-element.39), channel_id=1, source_target_pairs={{0,4},{4,8},{8,12},{12,14},{14,10},{10,6},{6,2},{2,0},{1,5},{5,9},... | collective-permute-start | bytes 276488 | tf_op jit(solution)/shard_map/ppermute | solution.py:176
  113.6 5.7 %collective-permute-start.31 = (bf16[240,192]{1,0:T(8,128)(2,1)S(1)}, bf16[240,192]{1,0:T(8,128)(2,1)S(1)}, u32[]{:S(2)}, u32[]{:S(2)}) collective-permute-start(bf16[240,192]{1,0:T(8,128)(2,1)S(1)} %get-tuple-element.40), channel_id=1, source_target_pairs={{0,2},{4,0},{8,4},{12,8},{14,12},{10,14},{6,10},{2,6},{1,3},{5,1},... | collective-permute-start | bytes 276488 | tf_op jit(solution)/shard_map/ppermute | solution.py:176
  114.1 14.1 %collective-permute-start.15 = (bf16[128,1280]{1,0:T(8,128)(2,1)S(1)}, bf16[128,1280]{1,0:T(8,128)(2,1)S(1)}, u32[]{:S(2)}, u32[]{:S(2)}) collective-permute-start(bf16[128,1280]{1,0:T(8,128)(2,1)S(1)} %pad_maximum_fusion.8), channel_id=1, source_target_pairs={{0,2},{4,0},{8,4},{12,8},{14,12},{10,14},{6,10},{2,6},{1,3},{5,1},... | collective-permute-start | bytes 983048 | tf_op jit(solution)/shard_map/ppermute | solution.py:119
  119.5 5.5 %collective-permute-start.25 = (bf16[240,192]{1,0:T(8,128)(2,1)S(1)}, bf16[240,192]{1,0:T(8,128)(2,1)S(1)}, u32[]{:S(2)}, u32[]{:S(2)}) collective-permute-start(bf16[240,192]{1,0:T(8,128)(2,1)S(1)} %get-tuple-element.37), channel_id=1, source_target_pairs={{0,4},{4,8},{8,12},{12,14},{14,10},{10,6},{6,2},{2,0},{1,5},{5,9},... | collective-permute-start | bytes 276488 | tf_op jit(solution)/shard_map/ppermute | solution.py:176
  120.6 4.9 %collective-permute-start.32 = (bf16[240,192]{1,0:T(8,128)(2,1)S(1)}, bf16[240,192]{1,0:T(8,128)(2,1)S(1)}, u32[]{:S(2)}, u32[]{:S(2)}) collective-permute-start(bf16[240,192]{1,0:T(8,128)(2,1)S(1)} %get-tuple-element.38), channel_id=1, source_target_pairs={{0,2},{4,0},{8,4},{12,8},{14,12},{10,14},{6,10},{2,6},{1,3},{5,1},... | collective-permute-start | bytes 276488 | tf_op jit(solution)/shard_map/ppermute | solution.py:176
  121.6 14.3 %collective-permute-start.19 = (bf16[128,1280]{1,0:T(8,128)(2,1)S(1)}, bf16[128,1280]{1,0:T(8,128)(2,1)}, u32[]{:S(2)}, u32[]{:S(2)}) collective-permute-start(bf16[128,1280]{1,0:T(8,128)(2,1)S(1)} %pad_maximum_fusion.9), channel_id=1, source_target_pairs={{0,4},{4,8},{8,12},{12,14},{14,10},{10,6},{6,2},{2,0},{1,5},{5,9},... | collective-permute-start | bytes 983048 | tf_op jit(solution)/shard_map/ppermute | solution.py:119
  126.2 5.1 %collective-permute-start.26 = (bf16[240,192]{1,0:T(8,128)(2,1)}, bf16[240,192]{1,0:T(8,128)(2,1)S(1)}, u32[]{:S(2)}, u32[]{:S(2)}) collective-permute-start(bf16[240,192]{1,0:T(8,128)(2,1)} %get-tuple-element.35), channel_id=1, source_target_pairs={{0,4},{4,8},{8,12},{12,14},{14,10},{10,6},{6,2},{2,0},{1,5},{5,9},... | collective-permute-start | bytes 276488 | tf_op jit(solution)/shard_map/ppermute | solution.py:176
  127.0 5.0 %collective-permute-start.33 = (bf16[240,192]{1,0:T(8,128)(2,1)S(1)}, bf16[240,192]{1,0:T(8,128)(2,1)}, u32[]{:S(2)}, u32[]{:S(2)}) collective-permute-start(bf16[240,192]{1,0:T(8,128)(2,1)S(1)} %get-tuple-element.36), channel_id=1, source_target_pairs={{0,2},{4,0},{8,4},{12,8},{14,12},{10,14},{6,10},{2,6},{1,3},{5,1},... | collective-permute-start | bytes 276488 | tf_op jit(solution)/shard_map/ppermute | solution.py:176
  129.0 8.7 %collective-permute-start.16 = (bf16[128,1280]{1,0:T(8,128)(2,1)}, bf16[128,1280]{1,0:T(8,128)(2,1)}, u32[]{:S(2)}, u32[]{:S(2)}) collective-permute-start(bf16[128,1280]{1,0:T(8,128)(2,1)} %add_convert_fusion.4), channel_id=1, source_target_pairs={{0,2},{4,0},{8,4},{12,8},{14,12},{10,14},{6,10},{2,6},{1,3},{5,1},... | collective-permute-start | bytes 983048 | tf_op jit(solution)/shard_map/ppermute | solution.py:119
  130.6 10.2 %copy-start.10 = (bf16[1024,512]{0,1:T(8,128)(2,1)S(1)}, bf16[1024,512]{0,1:T(8,128)(2,1)}, u32[]{:S(2)}) copy-start(bf16[1024,512]{0,1:T(8,128)(2,1)} %copy-done.9) | copy-start | bytes 3145732
  130.6 10.2 %copy-start.11 = (bf16[4,128,1024]{1,2,0:T(8,128)(2,1)S(1)}, bf16[4,128,1024]{1,2,0:T(8,128)(2,1)}, u32[]{:S(2)}) copy-start(bf16[4,128,1024]{1,2,0:T(8,128)(2,1)} %multiply_convert_fusion.1) | copy-start | bytes 3145732
  133.9 8.1 %collective-permute-start.27 = (bf16[240,192]{1,0:T(8,128)(2,1)}, bf16[240,192]{1,0:T(8,128)(2,1)S(1)}, u32[]{:S(2)}, u32[]{:S(2)}) collective-permute-start(bf16[240,192]{1,0:T(8,128)(2,1)} %get-tuple-element.33), channel_id=1, source_target_pairs={{0,4},{4,8},{8,12},{12,14},{14,10},{10,6},{6,2},{2,0},{1,5},{5,9},... | collective-permute-start | bytes 276488 | tf_op jit(solution)/shard_map/ppermute | solution.py:176
  135.4 6.7 %collective-permute-start.34 = (bf16[240,192]{1,0:T(8,128)(2,1)}, bf16[240,192]{1,0:T(8,128)(2,1)}, u32[]{:S(2)}, u32[]{:S(2)}) collective-permute-start(bf16[240,192]{1,0:T(8,128)(2,1)} %get-tuple-element.34), channel_id=1, source_target_pairs={{0,2},{4,0},{8,4},{12,8},{14,12},{10,14},{6,10},{2,6},{1,3},{5,1},... | collective-permute-start | bytes 276488 | tf_op jit(solution)/shard_map/ppermute | solution.py:176
  140.0 10.2 %collective-permute-start.20 = (bf16[128,1280]{1,0:T(8,128)(2,1)}, bf16[128,1280]{1,0:T(8,128)(2,1)S(1)}, u32[]{:S(2)}, u32[]{:S(2)}) collective-permute-start(bf16[128,1280]{1,0:T(8,128)(2,1)} %get-tuple-element.46), channel_id=1, source_target_pairs={{0,4},{4,8},{8,12},{12,14},{14,10},{10,6},{6,2},{2,0},{1,5},{5,9},... | collective-permute-start | bytes 983048 | tf_op jit(solution)/shard_map/ppermute | solution.py:119
  143.3 8.8 %collective-permute-start.28 = (bf16[240,192]{1,0:T(8,128)(2,1)S(1)}, bf16[240,192]{1,0:T(8,128)(2,1)S(1)}, u32[]{:S(2)}, u32[]{:S(2)}) collective-permute-start(bf16[240,192]{1,0:T(8,128)(2,1)S(1)} %get-tuple-element.31), channel_id=1, source_target_pairs={{0,4},{4,8},{8,12},{12,14},{14,10},{10,6},{6,2},{2,0},{1,5},{5,9},... | collective-permute-start | bytes 276488 | tf_op jit(solution)/shard_map/ppermute | solution.py:176
  144.8 7.3 %collective-permute-start.35 = (bf16[240,192]{1,0:T(8,128)(2,1)S(1)}, bf16[240,192]{1,0:T(8,128)(2,1)S(1)}, u32[]{:S(2)}, u32[]{:S(2)}) collective-permute-start(bf16[240,192]{1,0:T(8,128)(2,1)S(1)} %get-tuple-element.32), channel_id=1, source_target_pairs={{0,2},{4,0},{8,4},{12,8},{14,12},{10,14},{6,10},{2,6},{1,3},{5,1},... | collective-permute-start | bytes 276488 | tf_op jit(solution)/shard_map/ppermute | solution.py:176
  145.4 8.8 %collective-permute-start.17 = (bf16[128,1280]{1,0:T(8,128)(2,1)}, bf16[128,1280]{1,0:T(8,128)(2,1)S(1)}, u32[]{:S(2)}, u32[]{:S(2)}) collective-permute-start(bf16[128,1280]{1,0:T(8,128)(2,1)} %get-tuple-element.45), channel_id=1, source_target_pairs={{0,2},{4,0},{8,4},{12,8},{14,12},{10,14},{6,10},{2,6},{1,3},{5,1},... | collective-permute-start | bytes 983048 | tf_op jit(solution)/shard_map/ppermute | solution.py:119
  151.2 7.1 %collective-permute-start.21 = (bf16[128,1280]{1,0:T(8,128)(2,1)S(1)}, bf16[128,1280]{1,0:T(8,128)(2,1)S(1)}, u32[]{:S(2)}, u32[]{:S(2)}) collective-permute-start(bf16[128,1280]{1,0:T(8,128)(2,1)S(1)} %add_convert_fusion.1), channel_id=1, source_target_pairs={{0,4},{4,8},{8,12},{12,14},{14,10},{10,6},{6,2},{2,0},{1,5},{5,9},... | collective-permute-start | bytes 983048 | tf_op jit(solution)/shard_map/ppermute | solution.py:119
  (9 other events, 13.9 us)

commit v14 on v8

--- a/solution.py
+++ b/solution.py
@@ -186,10 +186,8 @@
     positions = 2 * local_tokens
     half_kernel = KW // 2
     query_heads = queries[0].reshape(local_tokens, H, DK)
-    key_value_blocks = ring_gather(jnp.concatenate([key_rows[0], value_rows[0]], axis=1), ring)
-    gathered = jnp.concatenate(key_value_blocks, axis=0)
-    all_keys = gathered[:, : H * DK].reshape(-1, H, DK)
-    all_values = gathered[:, H * DK :].reshape(-1, H, DV)
+    all_keys = jnp.concatenate(ring_gather(key_rows[0], ring), axis=0).reshape(-1, H, DK)
+    all_values = jnp.concatenate(ring_gather(value_rows[0], ring), axis=0).reshape(-1, H, DV)
     scores = (
         jnp.einsum("ihd,jhd->hij", query_heads, all_keys, preferred_element_type=jnp.float32)
         * score_scale

time: 159 us -> 187 us (1.18)
  local copies, waits for them, and re-layouts: 24 us -> 55 us
  waiting for transfers between devices: 44.8 us -> 27.4 us
  starting transfers between devices: 45.4 us -> 53.9 us
  matrix products: 24.7 us -> 28.9 us
    concatenate x0 -> x11, local copies, waits for them, and re-layouts: none -> 12.4 us  [the longest x9 11.5 us: body(): jnp.concatenate(ring_gather(key_rows[0], ring), axis=0).reshape(-1, H, DK)]
    ppermute x3 -> x6, waiting for transfers between devices: 12.7 us -> 0.79 us  [ring_gather(): current = lax.ppermute(current, 'seq', forward)]
    unnamed x60 -> x68, local copies, waits for them, and re-layouts: 9.79 us -> 18.9 us
    ppermute x0 -> x6, local copies, waits for them, and re-layouts: none -> 7.82 us  [the longest x3 4.57 us: ring_gather(): current = lax.ppermute(current, 'seq', forward)]
    ppermute x3 -> x6, starting transfers between devices: 6.37 us -> 12.4 us  [ring_gather(): current = lax.ppermute(current, 'seq', forward)]
    ppermute x3 -> x6, waiting for transfers between devices: 4.77 us -> 0.02 us  [ring_gather(): current = lax.ppermute(current, 'seq', backward)]
    slice x2 -> x0, local copies, waits for them, and re-layouts: 3.39 us -> none  [the longest x1 1.86 us: body(): all_keys = gathered[:, :H * DK].reshape(-1, H, DK)]
    slice x1 -> x2, local copies, waits for them, and re-layouts: 0.01 us -> 3.02 us  [ring_gather(): right_half = lax.ppermute(current[:, half:], 'seq', backward)]
  transfers between devices with their start and end apart: 36 -> 44, of which waited for: 20 -> 16; matrix products, arithmetic and copies ran while one was open for 27% -> 45% of each run, Pallas kernels for 0% -> 0%
where the time goes in v14:
time: 187 us; the launch traced here: 186 us
  local copies, waits for them, and re-layouts  55 us (29%)
  starting transfers between devices  53.9 us (29%)
  matrix products  28.9 us (15%)
  waiting for transfers between devices  27.4 us (15%)
  other arithmetic  19 us (10%)
    ppermute x14, waiting for transfers between devices, ring_reduce_scatter_sliced(): received = lax.ppermute(acc, axis, perm).astype(jnp.float32)  19.8 us
    unnamed x68, local copies, waits for them, and re-layouts  18.9 us
    ppermute x14, starting transfers between devices, ring_reduce_scatter_sliced(): received = lax.ppermute(acc, axis, perm).astype(jnp.float32)  16.7 us
    ppermute x6, starting transfers between devices, ring_gather(): current = lax.ppermute(current, 'seq', forward)  12.4 us
    concatenate x9, local copies, waits for them, and re-layouts, body(): jnp.concatenate(ring_gather(key_rows[0], ring), axis=0).reshape(-1, H, DK)  11.5 us
    ppermute x2, starting transfers between devices, extended(): before = lax.ppermute(last, axis, up)  8.77 us
    dot_general x5, matrix products, body(): jnp.einsum('spc,spo->co', both_padded[:, offset:offset + positions], both...  8.5 us
    ppermute x8, starting transfers between devices, ring_scatter_back(): received = lax.ppermute(acc, 'seq', perm).astype(jnp.float32)  7.94 us
  transfers between devices with their start and end apart: 44, of which 16 were waited for; matrix products, arithmetic and copies ran while one was open for 45% of the time, Pallas kernels for 0%

profile of v14, /device:TPU:0, one launch (start us, length us, event | category | flops | bytes accessed | tf_op | source)
XLA Modules:
  0.0 185.8 jit_solution(12135067791528035720)
XLA Ops:
  0.7 3.1 %collective-permute-start = (bf16[128,768]{1,0:T(8,128)(2,1)}, bf16[128,768]{1,0:T(8,128)(2,1)}, u32[]{:S(2)}, u32[]{:S(2)}) collective-permute-start(bf16[128,768]{1,0:T(8,128)(2,1)} %bitcast.225), channel_id=1, source_target_pairs={{0,4},{4,8},{8,12},{12,14},{14,10},{10,6},{6,2},{2,0},{1,5},{5,9},... | collective-permute-start | bytes 589832 | tf_op jit(solution)/shard_map/ppermute | solution.py:76
  4.8 2.1 %collective-permute-start.8 = (bf16[128,512]{0,1:T(8,128)(2,1)S(1)}, bf16[128,512]{0,1:T(8,128)(2,1)}, u32[]{:S(2)}, u32[]{:S(2)}) collective-permute-start(bf16[128,512]{0,1:T(8,128)(2,1)S(1)} %bitcast.221), channel_id=1, source_target_pairs={{0,4},{4,8},{8,12},{12,14},{14,10},{10,6},{6,2},{2,0},{1,5},{5,9},... | collective-permute-start | bytes 393224 | tf_op jit(solution)/shard_map/ppermute | solution.py:76
  6.9 2.1 %fusion.65 = f32[256,768]{1,0:T(8,128)} fusion(bf16[1,128,768]{2,1,0:T(8,128)(2,1)} %param.11, s32[256]{0:T(256)S(1)} %and_select_fusion), kind=kOutput, calls=%fused_computation.153 | convolution fusion | flops 50364416 | bytes 984064 | tf_op jit(solution)/shard_map/dot_general | solution.py:207
  11.7 1.8 collective-permute-start.9
  18.5 1.8 collective-permute-start.10
  21.3 1.8 collective-permute-start.1
  24.5 1.7 copy.55
  28.8 1.7 copy.56
  30.4 1.7 copy.59
  33.6 1.7 collective-permute-start.15
  41.6 1.7 copy.45
  43.3 1.8 collective-permute-start.2
  46.5 1.6 constant_dynamic-update-slice_fusion.5
  49.7 1.7 copy.60
  52.9 1.7 bitcast_reduce_fusion
  57.8 1.7 collective-permute-start.7
  61.4 1.7 copy.46
  69.8 2.7 %convolution_convert_fusion.2 = bf16[4,192,128]{2,1,0:T(8,128)(2,1)S(1)} fusion(bf16[1024,4,192]{0,2,1:T(8,128)(2,1)} %constant_dynamic-update-slice_fusion, f32[4,1024,128]{2,1,0:T(8,128)} %copy-done.3, f32[4,128]{1,0:T(4,128)S(1)} %log_add_fusion), kind=kOutput, calls=%fused_computation.41 | convolution fusion | flops 202997760 | bytes 3868672 | tf_op jit(solution)/shard_map/hij,jhd->ihd/dot_general | solution.py:200
  74.1 3.6 %collective-permute-start.16 = (bf16[2,768]{1,0:T(2,128)(2,1)S(1)}, bf16[2,768]{1,0:T(2,128)(2,1)S(1)}, u32[]{:S(2)}, u32[]{:S(2)}) collective-permute-start(bf16[2,768]{1,0:T(2,128)(2,1)S(1)} %get-tuple-element.53), channel_id=1, source_target_pairs={{0,2},{2,4},{4,6},{6,8},{8,10},{10,12},{12,14},{1,3},{3,5},{5,7},{... | collective-permute-start | bytes 9224 | tf_op jit(solution)/shard_map/ppermute | solution.py:24
  79.9 3.8 %collective-permute-done.17 = bf16[2,768]{1,0:T(2,128)(2,1)S(1)} collective-permute-done((bf16[2,768]{1,0:T(2,128)(2,1)S(1)}, bf16[2,768]{1,0:T(2,128)(2,1)S(1)}, u32[]{:S(2)}, u32[]{:S(2)}) %collective-permute-start.17) | collective-permute-done | bytes 3104 | tf_op jit(solution)/shard_map/ppermute | solution.py:25
  83.9 2.0 %fusion.32 = (bf16[256,384]{1,0:T(8,128)(2,1)S(1)}, bf16[1,256,384]{2,1,0:T(8,128)(2,1)}) fusion(bf16[1,256,384]{2,1,0:T(8,128)(2,1)S(1)} %copy-done.24, bf16[256,3840]{1,0:T(8,128)(2,1)S(1)} %fusion.33, bf16[3840,384]{1,0:T(8,128)(2,1)S(1)} %copy-done), kind=kOutput, calls=%fused_computation.84 | convolution fusion | flops 756252672 | bytes 5505024 | tf_op jit(solution)/shard_map/dot_general | solution.py:218
  87.2 5.1 %collective-permute-start.19 = (bf16[2,384]{1,0:T(2,128)(2,1)S(1)}, bf16[2,384]{1,0:T(2,128)(2,1)S(1)}, u32[]{:S(2)}, u32[]{:S(2)}) collective-permute-start(bf16[2,384]{1,0:T(2,128)(2,1)S(1)} %get-tuple-element.54), channel_id=1, source_target_pairs={{0,2},{2,4},{4,6},{6,8},{8,10},{10,12},{12,14},{1,3},{3,5},{5,7},{... | collective-permute-start | bytes 4616 | tf_op jit(solution)/shard_map/ppermute | solution.py:24
  98.4 4.3 %multiply_convert_fusion.1 = bf16[4,128,1024]{1,2,0:T(8,128)(2,1)} fusion(f32[4,1024,128]{2,1,0:T(8,128)} %copy-done.3, bf16[128,4,192]{0,2,1:T(8,128)(2,1)S(1)} %bitcast.206, bf16[1024,4,192]{0,2,1:T(8,128)(2,1)} %constant_dynamic-update-slice_fusion, f32[4,128]{1,0:T(4,128)S(1)} %bitcast.227, f32[4,128]{1,0:T(4,128)S(1)} %log_add_fusion), kind=kOutput, calls=%fused_computation.22 | convolution fusion | flops 203948032 | bytes 4919296 | tf_op jit(solution)/shard_map/ihd,jhd->hij/dot_general | solution.py:304
  102.7 1.8 convolution_convert_fusion
  104.5 2.7 %copy.73 = bf16[1024,768]{1,0:T(8,128)(2,1)} copy(bf16[1024,768]{0,1:T(8,128)(2,1)} %bitcast.198) | data formatting | bytes 3145728 | tf_op jit(solution)/shard_map/reshape | solution.py:320
  107.2 2.6 %fusion.9 = bf16[1024,4,128]{2,0,1:T(8,128)(2,1)} fusion(bf16[4,128,1024]{1,2,0:T(8,128)(2,1)} %multiply_convert_fusion.1, bf16[128,4,128]{0,2,1:T(8,128)(2,1)S(1)} %bitcast.210), kind=kOutput, calls=%fused_computation.35 | convolution fusion | flops 135266304 | bytes 2228224 | tf_op jit(solution)/shard_map/hij,ihd->jhd/dot_general | solution.py:313
  109.8 2.3 %copy.70 = bf16[1024,4,128]{0,2,1:T(8,128)(2,1)} copy(bf16[1024,4,128]{2,0,1:T(8,128)(2,1)} %fusion.9) | data formatting | bytes 2097152 | tf_op jit(solution)/shard_map/mul | solution.py:313
  112.1 2.3 %copy.72 = bf16[1024,512]{1,0:T(8,128)(2,1)} copy(bf16[1024,512]{0,1:T(8,128)(2,1)} %bitcast.204) | data formatting | bytes 2097152 | tf_op jit(solution)/shard_map/reshape | solution.py:319
  114.4 1.8 fusion.8
  116.2 1.7 fusion.7
  117.9 1.7 fusion.6
  119.6 1.7 fusion.5
  121.2 1.7 fusion.4
  123.4 4.4 %collective-permute-start.30 = (bf16[240,192]{1,0:T(8,128)(2,1)S(1)}, bf16[240,192]{1,0:T(8,128)(2,1)S(1)}, u32[]{:S(2)}, u32[]{:S(2)}) collective-permute-start(bf16[240,192]{1,0:T(8,128)(2,1)S(1)} %get-tuple-element.37), channel_id=1, source_target_pairs={{0,4},{4,8},{8,12},{12,14},{14,10},{10,6},{6,2},{2,0},{1,5},{5,9},... | collective-permute-start | bytes 276488 | tf_op jit(solution)/shard_map/ppermute | solution.py:176
  128.3 1.7 collective-permute-start.24
  131.2 2.3 %collective-permute-done.37 = bf16[240,192]{1,0:T(8,128)(2,1)S(1)} collective-permute-done((bf16[240,192]{1,0:T(8,128)(2,1)S(1)}, bf16[240,192]{1,0:T(8,128)(2,1)S(1)}, u32[]{:S(2)}, u32[]{:S(2)}) %collective-permute-start.37) | collective-permute-done | bytes 92192 | tf_op jit(solution)/shard_map/ppermute | solution.py:176
  136.1 2.6 %collective-permute-done.31 = bf16[240,192]{1,0:T(8,128)(2,1)S(1)} collective-permute-done((bf16[240,192]{1,0:T(8,128)(2,1)S(1)}, bf16[240,192]{1,0:T(8,128)(2,1)S(1)}, u32[]{:S(2)}, u32[]{:S(2)}) %collective-permute-start.31) | collective-permute-done | bytes 92192 | tf_op jit(solution)/shard_map/ppermute | solution.py:176
  143.7 1.7 collective-permute-done.32
  145.4 2.0 %collective-permute-done.39 = bf16[240,192]{1,0:T(8,128)(2,1)S(1)} collective-permute-done((bf16[240,192]{1,0:T(8,128)(2,1)S(1)}, bf16[240,192]{1,0:T(8,128)(2,1)S(1)}, u32[]{:S(2)}, u32[]{:S(2)}) %collective-permute-start.39) | collective-permute-done | bytes 92192 | tf_op jit(solution)/shard_map/ppermute | solution.py:176
  151.4 1.8 collective-permute-done.33
  158.1 2.3 %add_convert_fusion.4 = (bf16[128,1280]{1,0:T(8,128)(2,1)}, bf16[128,1280]{1,0:T(8,128)(2,1)}) fusion(bf16[128,1280]{1,0:T(8,128)(2,1)} %collective-permute-done.21, bf16[1024,768]{1,0:T(8,128)(2,1)} %copy.73, bf16[1024,512]{1,0:T(8,128)(2,1)} %copy.72, bf16[128,1280]{1,0:T(8,128)(2,1)} %collective-permute-done.25), kind=kLoop, calls=%fused_computation.67 | loop fusion | flops 2293760 | bytes 3932160 | tf_op jit(solution)/shard_map/convert_element_type | solution.py:123
  160.4 1.8 collective-permute-start.22
  162.5 1.8 fusion.49
  164.3 1.8 collective-permute-start.35
  167.6 4.6 %collective-permute-done.35 = bf16[240,192]{1,0:T(8,128)(2,1)S(1)} collective-permute-done((bf16[240,192]{1,0:T(8,128)(2,1)}, bf16[240,192]{1,0:T(8,128)(2,1)S(1)}, u32[]{:S(2)}, u32[]{:S(2)}) %collective-permute-start.35) | collective-permute-done | bytes 92192 | tf_op jit(solution)/shard_map/ppermute | solution.py:176
  173.7 1.8 collective-permute-start.43
  177.2 1.8 collective-permute-start.23
  182.0 2.1 %collective-permute-done.27 = bf16[128,1280]{1,0:T(8,128)(2,1)S(1)} collective-permute-done((bf16[128,1280]{1,0:T(8,128)(2,1)S(1)}, bf16[128,1280]{1,0:T(8,128)(2,1)S(1)}, u32[]{:S(2)}, u32[]{:S(2)}) %collective-permute-start.27) | collective-permute-done | bytes 327712 | tf_op jit(solution)/shard_map/ppermute | solution.py:119
  (192 shorter events, 76.4 us)
Async XLA Ops:
  0.6 83.3 %copy-start = (bf16[3840,384]{1,0:T(8,128)(2,1)S(1)}, bf16[3840,384]{1,0:T(8,128)(2,1)}, u32[]{:S(2)}) copy-start(bf16[3840,384]{1,0:T(8,128)(2,1)} %param.14) | copy-start | bytes 8847364
  0.7 16.7 %collective-permute-start = (bf16[128,768]{1,0:T(8,128)(2,1)}, bf16[128,768]{1,0:T(8,128)(2,1)}, u32[]{:S(2)}, u32[]{:S(2)}) collective-permute-start(bf16[128,768]{1,0:T(8,128)(2,1)} %bitcast.225), channel_id=1, source_target_pairs={{0,4},{4,8},{8,12},{12,14},{14,10},{10,6},{6,2},{2,0},{1,5},{5,9},... | collective-permute-start | bytes 589832 | tf_op jit(solution)/shard_map/ppermute | solution.py:76
  3.8 19.3 %collective-permute-start.3 = (bf16[128,768]{1,0:T(8,128)(2,1)}, bf16[128,768]{1,0:T(8,128)(2,1)}, u32[]{:S(2)}, u32[]{:S(2)}) collective-permute-start(bf16[128,768]{1,0:T(8,128)(2,1)} %bitcast.226), channel_id=1, source_target_pairs={{0,2},{4,0},{8,4},{12,8},{14,12},{10,14},{6,10},{2,6},{1,3},{5,1},... | collective-permute-start | bytes 589832 | tf_op jit(solution)/shard_map/ppermute | solution.py:82
  4.8 6.9 %collective-permute-start.8 = (bf16[128,512]{0,1:T(8,128)(2,1)S(1)}, bf16[128,512]{0,1:T(8,128)(2,1)}, u32[]{:S(2)}, u32[]{:S(2)}) collective-permute-start(bf16[128,512]{0,1:T(8,128)(2,1)S(1)} %bitcast.221), channel_id=1, source_target_pairs={{0,4},{4,8},{8,12},{12,14},{14,10},{10,6},{6,2},{2,0},{1,5},{5,9},... | collective-permute-start | bytes 393224 | tf_op jit(solution)/shard_map/ppermute | solution.py:76
  6.9 6.7 %collective-permute-start.11 = (bf16[128,512]{0,1:T(8,128)(2,1)S(1)}, bf16[128,512]{0,1:T(8,128)(2,1)}, u32[]{:S(2)}, u32[]{:S(2)}) collective-permute-start(bf16[128,512]{0,1:T(8,128)(2,1)S(1)} %bitcast.222), channel_id=1, source_target_pairs={{0,2},{4,0},{8,4},{12,8},{14,12},{10,14},{6,10},{2,6},{1,3},{5,1},... | collective-permute-start | bytes 393224 | tf_op jit(solution)/shard_map/ppermute | solution.py:82
  6.9 65.7 %copy-start.20 = (s32[256]{0:T(256)}, s32[256]{0:T(256)S(1)}, u32[]{:S(2)}) copy-start(s32[256]{0:T(256)S(1)} %and_select_fusion) | copy-start | bytes 3076
  11.7 6.8 %collective-permute-start.9 = (bf16[128,512]{0,1:T(8,128)(2,1)}, bf16[128,512]{0,1:T(8,128)(2,1)}, u32[]{:S(2)}, u32[]{:S(2)}) collective-permute-start(bf16[128,512]{0,1:T(8,128)(2,1)} %collective-permute-done.8), channel_id=1, source_target_pairs={{0,4},{4,8},{8,12},{12,14},{14,10},{10,6},{6,2},{2,0},{1,5},{5,9},... | collective-permute-start | bytes 393224 | tf_op jit(solution)/shard_map/ppermute | solution.py:76
  13.5 6.8 %collective-permute-start.12 = (bf16[128,512]{0,1:T(8,128)(2,1)}, bf16[128,512]{0,1:T(8,128)(2,1)}, u32[]{:S(2)}, u32[]{:S(2)}) collective-permute-start(bf16[128,512]{0,1:T(8,128)(2,1)} %collective-permute-done.11), channel_id=1, source_target_pairs={{0,2},{4,0},{8,4},{12,8},{14,12},{10,14},{6,10},{2,6},{1,3},{5,1},... | collective-permute-start | bytes 393224 | tf_op jit(solution)/shard_map/ppermute | solution.py:82
  14.6 38.3 %copy-start.15 = (bf16[1,128,512]{1,2,0:T(8,128)(2,1)}, bf16[1,128,512]{1,2,0:T(8,128)(2,1)S(1)}, u32[]{:S(2)}) copy-start(bf16[1,128,512]{1,2,0:T(8,128)(2,1)S(1)} %copy.95) | copy-start | bytes 393220
  18.5 10.3 %collective-permute-start.10 = (bf16[128,512]{0,1:T(8,128)(2,1)}, bf16[128,512]{0,1:T(8,128)(2,1)}, u32[]{:S(2)}, u32[]{:S(2)}) collective-permute-start(bf16[128,512]{0,1:T(8,128)(2,1)} %collective-permute-done.9), channel_id=1, source_target_pairs={{0,4},{4,8},{8,12},{12,14},{14,10},{10,6},{6,2},{2,0},{1,5},{5,9},... | collective-permute-start | bytes 393224 | tf_op jit(solution)/shard_map/ppermute | solution.py:76
  20.4 10.1 %collective-permute-start.13 = (bf16[128,512]{0,1:T(8,128)(2,1)}, bf16[128,512]{0,1:T(8,128)(2,1)}, u32[]{:S(2)}, u32[]{:S(2)}) collective-permute-start(bf16[128,512]{0,1:T(8,128)(2,1)} %collective-permute-done.12), channel_id=1, source_target_pairs={{0,2},{4,0},{8,4},{12,8},{14,12},{10,14},{6,10},{2,6},{1,3},{5,1},... | collective-permute-start | bytes 393224 | tf_op jit(solution)/shard_map/ppermute | solution.py:82
  21.3 20.2 %collective-permute-start.1 = (bf16[128,768]{1,0:T(8,128)(2,1)}, bf16[128,768]{1,0:T(8,128)(2,1)}, u32[]{:S(2)}, u32[]{:S(2)}) collective-permute-start(bf16[128,768]{1,0:T(8,128)(2,1)} %collective-permute-done), channel_id=1, source_target_pairs={{0,4},{4,8},{8,12},{12,14},{14,10},{10,6},{6,2},{2,0},{1,5},{5,9},... | collective-permute-start | bytes 589832 | tf_op jit(solution)/shard_map/ppermute | solution.py:76
  24.2 20.9 %collective-permute-start.4 = (bf16[128,768]{1,0:T(8,128)(2,1)}, bf16[128,768]{1,0:T(8,128)(2,1)}, u32[]{:S(2)}, u32[]{:S(2)}) collective-permute-start(bf16[128,768]{1,0:T(8,128)(2,1)} %collective-permute-done.3), channel_id=1, source_target_pairs={{0,2},{4,0},{8,4},{12,8},{14,12},{10,14},{6,10},{2,6},{1,3},{5,1},... | collective-permute-start | bytes 589832 | tf_op jit(solution)/shard_map/ppermute | solution.py:82
  33.6 14.5 %collective-permute-start.15 = (bf16[128,256]{0,1:T(8,128)(2,1)}, bf16[128,256]{0,1:T(8,128)(2,1)}, u32[]{:S(2)}, u32[]{:S(2)}) collective-permute-start(bf16[128,256]{0,1:T(8,128)(2,1)} %slice.171), channel_id=1, source_target_pairs={{0,2},{4,0},{8,4},{12,8},{14,12},{10,14},{6,10},{2,6},{1,3},{5,1},... | collective-permute-start | bytes 196616 | tf_op jit(solution)/shard_map/ppermute | solution.py:85
  36.8 11.3 %collective-permute-start.14 = (bf16[128,256]{0,1:T(8,128)(2,1)}, bf16[128,256]{0,1:T(8,128)(2,1)}, u32[]{:S(2)}, u32[]{:S(2)}) collective-permute-start(bf16[128,256]{0,1:T(8,128)(2,1)} %slice.170), channel_id=1, source_target_pairs={{0,4},{4,8},{8,12},{12,14},{14,10},{10,6},{6,2},{2,0},{1,5},{5,9},... | collective-permute-start | bytes 196616 | tf_op jit(solution)/shard_map/ppermute | solution.py:79
  43.3 16.2 %collective-permute-start.2 = (bf16[128,768]{1,0:T(8,128)(2,1)}, bf16[128,768]{1,0:T(8,128)(2,1)}, u32[]{:S(2)}, u32[]{:S(2)}) collective-permute-start(bf16[128,768]{1,0:T(8,128)(2,1)} %collective-permute-done.1), channel_id=1, source_target_pairs={{0,4},{4,8},{8,12},{12,14},{14,10},{10,6},{6,2},{2,0},{1,5},{5,9},... | collective-permute-start | bytes 589832 | tf_op jit(solution)/shard_map/ppermute | solution.py:76
  46.2 10.1 %collective-permute-start.5 = (bf16[128,768]{1,0:T(8,128)(2,1)}, bf16[128,768]{1,0:T(8,128)(2,1)}, u32[]{:S(2)}, u32[]{:S(2)}) collective-permute-start(bf16[128,768]{1,0:T(8,128)(2,1)} %collective-permute-done.4), channel_id=1, source_target_pairs={{0,2},{4,0},{8,4},{12,8},{14,12},{10,14},{6,10},{2,6},{1,3},{5,1},... | collective-permute-start | bytes 589832 | tf_op jit(solution)/shard_map/ppermute | solution.py:82
  57.8 10.2 %collective-permute-start.7 = (bf16[128,384]{1,0:T(8,128)(2,1)}, bf16[128,384]{1,0:T(8,128)(2,1)}, u32[]{:S(2)}, u32[]{:S(2)}) collective-permute-start(bf16[128,384]{1,0:T(8,128)(2,1)} %slice.169), channel_id=1, source_target_pairs={{0,2},{4,0},{8,4},{12,8},{14,12},{10,14},{6,10},{2,6},{1,3},{5,1},... | collective-permute-start | bytes 294920 | tf_op jit(solution)/shard_map/ppermute | solution.py:85
  61.1 6.9 %collective-permute-start.6 = (bf16[128,384]{1,0:T(8,128)(2,1)}, bf16[128,384]{1,0:T(8,128)(2,1)}, u32[]{:S(2)}, u32[]{:S(2)}) collective-permute-start(bf16[128,384]{1,0:T(8,128)(2,1)} %slice.168), channel_id=1, source_target_pairs={{0,4},{4,8},{8,12},{12,14},{14,10},{10,6},{6,2},{2,0},{1,5},{5,9},... | collective-permute-start | bytes 294920 | tf_op jit(solution)/shard_map/ppermute | solution.py:79
  74.1 5.4 %collective-permute-start.16 = (bf16[2,768]{1,0:T(2,128)(2,1)S(1)}, bf16[2,768]{1,0:T(2,128)(2,1)S(1)}, u32[]{:S(2)}, u32[]{:S(2)}) collective-permute-start(bf16[2,768]{1,0:T(2,128)(2,1)S(1)} %get-tuple-element.53), channel_id=1, source_target_pairs={{0,2},{2,4},{4,6},{6,8},{8,10},{10,12},{12,14},{1,3},{3,5},{5,7},{... | collective-permute-start | bytes 9224 | tf_op jit(solution)/shard_map/ppermute | solution.py:24
  78.1 5.6 %collective-permute-start.17 = (bf16[2,768]{1,0:T(2,128)(2,1)S(1)}, bf16[2,768]{1,0:T(2,128)(2,1)S(1)}, u32[]{:S(2)}, u32[]{:S(2)}) collective-permute-start(bf16[2,768]{1,0:T(2,128)(2,1)S(1)} %get-tuple-element.52), channel_id=1, source_target_pairs={{2,0},{4,2},{6,4},{8,6},{10,8},{12,10},{14,12},{3,1},{5,3},{7,5},{... | collective-permute-start | bytes 9224 | tf_op jit(solution)/shard_map/ppermute | solution.py:25
  85.9 28.4 %collective-permute-start.29 = (bf16[256,384]{1,0:T(8,128)(2,1)S(1)}, bf16[256,384]{1,0:T(8,128)(2,1)}, u32[]{:S(2)}, u32[]{:S(2)}) collective-permute-start(bf16[256,384]{1,0:T(8,128)(2,1)S(1)} %get-tuple-element.50), channel_id=1, source_target_pairs={{0,1},{1,0},{2,3},{3,2},{4,5},{5,4},{6,7},{7,6},{8,9},{9,8},{10,11... | collective-permute-start | bytes 589832 | tf_op jit(solution)/shard_map/ppermute | solution.py:230
  85.9 7.7 %collective-permute-start.18 = (bf16[2,384]{1,0:T(2,128)(2,1)S(1)}, bf16[2,384]{1,0:T(2,128)(2,1)S(1)}, u32[]{:S(2)}, u32[]{:S(2)}) collective-permute-start(bf16[2,384]{1,0:T(2,128)(2,1)S(1)} %get-tuple-element.55), channel_id=1, source_target_pairs={{2,0},{4,2},{6,4},{8,6},{10,8},{12,10},{14,12},{3,1},{5,3},{7,5},{... | collective-permute-start | bytes 4616 | tf_op jit(solution)/shard_map/ppermute | solution.py:25
  87.2 6.5 %collective-permute-start.19 = (bf16[2,384]{1,0:T(2,128)(2,1)S(1)}, bf16[2,384]{1,0:T(2,128)(2,1)S(1)}, u32[]{:S(2)}, u32[]{:S(2)}) collective-permute-start(bf16[2,384]{1,0:T(2,128)(2,1)S(1)} %get-tuple-element.54), channel_id=1, source_target_pairs={{0,2},{2,4},{4,6},{6,8},{8,10},{10,12},{12,14},{1,3},{3,5},{5,7},{... | collective-permute-start | bytes 4616 | tf_op jit(solution)/shard_map/ppermute | solution.py:24
  93.4 21.0 %collective-permute-start.28 = (bf16[260,768]{1,0:T(8,128)(2,1)}, bf16[260,768]{1,0:T(8,128)(2,1)}, u32[]{:S(2)}, u32[]{:S(2)}) collective-permute-start(bf16[260,768]{1,0:T(8,128)(2,1)} %get-tuple-element.48), channel_id=1, source_target_pairs={{0,1},{1,0},{2,3},{3,2},{4,5},{5,4},{6,7},{7,6},{8,9},{9,8},{10,11... | collective-permute-start | bytes 1198088 | tf_op jit(solution)/shard_map/ppermute | solution.py:229
  123.3 24.0 %copy-start.9 = (f32[3840,384]{1,0:T(8,128)}, f32[3840,384]{1,0:T(8,128)S(1)}, u32[]{:S(2)}) copy-start(f32[3840,384]{1,0:T(8,128)S(1)} %broadcast_multiply_fusion) | copy-start | bytes 17694724
  123.4 7.8 %collective-permute-start.30 = (bf16[240,192]{1,0:T(8,128)(2,1)S(1)}, bf16[240,192]{1,0:T(8,128)(2,1)S(1)}, u32[]{:S(2)}, u32[]{:S(2)}) collective-permute-start(bf16[240,192]{1,0:T(8,128)(2,1)S(1)} %get-tuple-element.37), channel_id=1, source_target_pairs={{0,4},{4,8},{8,12},{12,14},{14,10},{10,6},{6,2},{2,0},{1,5},{5,9},... | collective-permute-start | bytes 276488 | tf_op jit(solution)/shard_map/ppermute | solution.py:176
  127.8 5.8 %collective-permute-start.37 = (bf16[240,192]{1,0:T(8,128)(2,1)S(1)}, bf16[240,192]{1,0:T(8,128)(2,1)S(1)}, u32[]{:S(2)}, u32[]{:S(2)}) collective-permute-start(bf16[240,192]{1,0:T(8,128)(2,1)S(1)} %get-tuple-element.38), channel_id=1, source_target_pairs={{0,2},{4,0},{8,4},{12,8},{14,12},{10,14},{6,10},{2,6},{1,3},{5,1},... | collective-permute-start | bytes 276488 | tf_op jit(solution)/shard_map/ppermute | solution.py:176
  127.9 8.1 %collective-permute-start.20 = (bf16[128,640]{1,0:T(8,128)(2,1)S(1)}, bf16[128,640]{1,0:T(8,128)(2,1)S(1)}, u32[]{:S(2)}, u32[]{:S(2)}) collective-permute-start(bf16[128,640]{1,0:T(8,128)(2,1)S(1)} %get-tuple-element.45), channel_id=1, source_target_pairs={{0,2},{4,0},{8,4},{12,8},{14,12},{10,14},{6,10},{2,6},{1,3},{5,1},... | collective-permute-start | bytes 491528 | tf_op jit(solution)/shard_map/ppermute | solution.py:119
  128.3 7.6 %collective-permute-start.24 = (bf16[128,640]{1,0:T(8,128)(2,1)S(1)}, bf16[128,640]{1,0:T(8,128)(2,1)S(1)}, u32[]{:S(2)}, u32[]{:S(2)}) collective-permute-start(bf16[128,640]{1,0:T(8,128)(2,1)S(1)} %get-tuple-element.46), channel_id=1, source_target_pairs={{0,4},{4,8},{8,12},{12,14},{14,10},{10,6},{6,2},{2,0},{1,5},{5,9},... | collective-permute-start | bytes 491528 | tf_op jit(solution)/shard_map/ppermute | solution.py:119
  133.7 4.9 %collective-permute-start.31 = (bf16[240,192]{1,0:T(8,128)(2,1)S(1)}, bf16[240,192]{1,0:T(8,128)(2,1)S(1)}, u32[]{:S(2)}, u32[]{:S(2)}) collective-permute-start(bf16[240,192]{1,0:T(8,128)(2,1)S(1)} %get-tuple-element.35), channel_id=1, source_target_pairs={{0,4},{4,8},{8,12},{12,14},{14,10},{10,6},{6,2},{2,0},{1,5},{5,9},... | collective-permute-start | bytes 276488 | tf_op jit(solution)/shard_map/ppermute | solution.py:176
  135.4 4.9 %collective-permute-start.38 = (bf16[240,192]{1,0:T(8,128)(2,1)S(1)}, bf16[240,192]{1,0:T(8,128)(2,1)S(1)}, u32[]{:S(2)}, u32[]{:S(2)}) collective-permute-start(bf16[240,192]{1,0:T(8,128)(2,1)S(1)} %get-tuple-element.36), channel_id=1, source_target_pairs={{0,2},{4,0},{8,4},{12,8},{14,12},{10,14},{6,10},{2,6},{1,3},{5,1},... | collective-permute-start | bytes 276488 | tf_op jit(solution)/shard_map/ppermute | solution.py:176
  140.4 5.0 %collective-permute-start.32 = (bf16[240,192]{1,0:T(8,128)(2,1)S(1)}, bf16[240,192]{1,0:T(8,128)(2,1)S(1)}, u32[]{:S(2)}, u32[]{:S(2)}) collective-permute-start(bf16[240,192]{1,0:T(8,128)(2,1)S(1)} %get-tuple-element.33), channel_id=1, source_target_pairs={{0,4},{4,8},{8,12},{12,14},{14,10},{10,6},{6,2},{2,0},{1,5},{5,9},... | collective-permute-start | bytes 276488 | tf_op jit(solution)/shard_map/ppermute | solution.py:176
  142.0 5.3 %collective-permute-start.39 = (bf16[240,192]{1,0:T(8,128)(2,1)S(1)}, bf16[240,192]{1,0:T(8,128)(2,1)S(1)}, u32[]{:S(2)}, u32[]{:S(2)}) collective-permute-start(bf16[240,192]{1,0:T(8,128)(2,1)S(1)} %get-tuple-element.34), channel_id=1, source_target_pairs={{0,2},{4,0},{8,4},{12,8},{14,12},{10,14},{6,10},{2,6},{1,3},{5,1},... | collective-permute-start | bytes 276488 | tf_op jit(solution)/shard_map/ppermute | solution.py:176
  143.2 14.4 %collective-permute-start.21 = (bf16[128,1280]{1,0:T(8,128)(2,1)}, bf16[128,1280]{1,0:T(8,128)(2,1)}, u32[]{:S(2)}, u32[]{:S(2)}) collective-permute-start(bf16[128,1280]{1,0:T(8,128)(2,1)} %pad_maximum_fusion.7), channel_id=1, source_target_pairs={{0,2},{4,0},{8,4},{12,8},{14,12},{10,14},{6,10},{2,6},{1,3},{5,1},... | collective-permute-start | bytes 983048 | tf_op jit(solution)/shard_map/ppermute | solution.py:119
  148.1 5.1 %collective-permute-start.33 = (bf16[240,192]{1,0:T(8,128)(2,1)}, bf16[240,192]{1,0:T(8,128)(2,1)S(1)}, u32[]{:S(2)}, u32[]{:S(2)}) collective-permute-start(bf16[240,192]{1,0:T(8,128)(2,1)} %get-tuple-element.31), channel_id=1, source_target_pairs={{0,4},{4,8},{8,12},{12,14},{14,10},{10,6},{6,2},{2,0},{1,5},{5,9},... | collective-permute-start | bytes 276488 | tf_op jit(solution)/shard_map/ppermute | solution.py:176
  149.3 5.0 %collective-permute-start.40 = (bf16[240,192]{1,0:T(8,128)(2,1)S(1)}, bf16[240,192]{1,0:T(8,128)(2,1)}, u32[]{:S(2)}, u32[]{:S(2)}) collective-permute-start(bf16[240,192]{1,0:T(8,128)(2,1)S(1)} %get-tuple-element.32), channel_id=1, source_target_pairs={{0,2},{4,0},{8,4},{12,8},{14,12},{10,14},{6,10},{2,6},{1,3},{5,1},... | collective-permute-start | bytes 276488 | tf_op jit(solution)/shard_map/ppermute | solution.py:176
  150.1 8.0 %collective-permute-start.25 = (bf16[128,1280]{1,0:T(8,128)(2,1)S(1)}, bf16[128,1280]{1,0:T(8,128)(2,1)}, u32[]{:S(2)}, u32[]{:S(2)}) collective-permute-start(bf16[128,1280]{1,0:T(8,128)(2,1)S(1)} %fusion.41), channel_id=1, source_target_pairs={{0,4},{4,8},{8,12},{12,14},{14,10},{10,6},{6,2},{2,0},{1,5},{5,9},... | collective-permute-start | bytes 983048 | tf_op jit(solution)/shard_map/ppermute | solution.py:119
  155.5 6.9 %collective-permute-start.34 = (bf16[240,192]{1,0:T(8,128)(2,1)S(1)}, bf16[240,192]{1,0:T(8,128)(2,1)S(1)}, u32[]{:S(2)}, u32[]{:S(2)}) collective-permute-start(bf16[240,192]{1,0:T(8,128)(2,1)S(1)} %get-tuple-element.29), channel_id=1, source_target_pairs={{0,4},{4,8},{8,12},{12,14},{14,10},{10,6},{6,2},{2,0},{1,5},{5,9},... | collective-permute-start | bytes 276488 | tf_op jit(solution)/shard_map/ppermute | solution.py:176
  156.1 6.4 %collective-permute-start.41 = (bf16[240,192]{1,0:T(8,128)(2,1)S(1)}, bf16[240,192]{1,0:T(8,128)(2,1)S(1)}, u32[]{:S(2)}, u32[]{:S(2)}) collective-permute-start(bf16[240,192]{1,0:T(8,128)(2,1)S(1)} %get-tuple-element.30), channel_id=1, source_target_pairs={{0,2},{4,0},{8,4},{12,8},{14,12},{10,14},{6,10},{2,6},{1,3},{5,1},... | collective-permute-start | bytes 276488 | tf_op jit(solution)/shard_map/ppermute | solution.py:176
  160.4 15.1 %collective-permute-start.22 = (bf16[128,1280]{1,0:T(8,128)(2,1)}, bf16[128,1280]{1,0:T(8,128)(2,1)S(1)}, u32[]{:S(2)}, u32[]{:S(2)}) collective-permute-start(bf16[128,1280]{1,0:T(8,128)(2,1)} %get-tuple-element.41), channel_id=1, source_target_pairs={{0,2},{4,0},{8,4},{12,8},{14,12},{10,14},{6,10},{2,6},{1,3},{5,1},... | collective-permute-start | bytes 983048 | tf_op jit(solution)/shard_map/ppermute | solution.py:119
  162.3 13.3 %collective-permute-start.26 = (bf16[128,1280]{1,0:T(8,128)(2,1)}, bf16[128,1280]{1,0:T(8,128)(2,1)}, u32[]{:S(2)}, u32[]{:S(2)}) collective-permute-start(bf16[128,1280]{1,0:T(8,128)(2,1)} %get-tuple-element.42), channel_id=1, source_target_pairs={{0,4},{4,8},{8,12},{12,14},{14,10},{10,6},{6,2},{2,0},{1,5},{5,9},... | collective-permute-start | bytes 983048 | tf_op jit(solution)/shard_map/ppermute | solution.py:119
  164.3 7.9 %collective-permute-start.35 = (bf16[240,192]{1,0:T(8,128)(2,1)}, bf16[240,192]{1,0:T(8,128)(2,1)S(1)}, u32[]{:S(2)}, u32[]{:S(2)}) collective-permute-start(bf16[240,192]{1,0:T(8,128)(2,1)} %get-tuple-element.27), channel_id=1, source_target_pairs={{0,4},{4,8},{8,12},{12,14},{14,10},{10,6},{6,2},{2,0},{1,5},{5,9},... | collective-permute-start | bytes 276488 | tf_op jit(solution)/shard_map/ppermute | solution.py:176
  166.1 6.0 %collective-permute-start.42 = (bf16[240,192]{1,0:T(8,128)(2,1)}, bf16[240,192]{1,0:T(8,128)(2,1)}, u32[]{:S(2)}, u32[]{:S(2)}) collective-permute-start(bf16[240,192]{1,0:T(8,128)(2,1)} %get-tuple-element.28), channel_id=1, source_target_pairs={{0,2},{4,0},{8,4},{12,8},{14,12},{10,14},{6,10},{2,6},{1,3},{5,1},... | collective-permute-start | bytes 276488 | tf_op jit(solution)/shard_map/ppermute | solution.py:176
  173.5 5.6 %collective-permute-start.36 = (bf16[240,192]{1,0:T(8,128)(2,1)S(1)}, bf16[240,192]{1,0:T(8,128)(2,1)S(1)}, u32[]{:S(2)}, u32[]{:S(2)}) collective-permute-start(bf16[240,192]{1,0:T(8,128)(2,1)S(1)} %get-tuple-element.25), channel_id=1, source_target_pairs={{0,4},{4,8},{8,12},{12,14},{14,10},{10,6},{6,2},{2,0},{1,5},{5,9},... | collective-permute-start | bytes 276488 | tf_op jit(solution)/shard_map/ppermute | solution.py:176
  173.7 6.2 %collective-permute-start.43 = (bf16[240,192]{1,0:T(8,128)(2,1)S(1)}, bf16[240,192]{1,0:T(8,128)(2,1)S(1)}, u32[]{:S(2)}, u32[]{:S(2)}) collective-permute-start(bf16[240,192]{1,0:T(8,128)(2,1)S(1)} %get-tuple-element.26), channel_id=1, source_target_pairs={{0,2},{4,0},{8,4},{12,8},{14,12},{10,14},{6,10},{2,6},{1,3},{5,1},... | collective-permute-start | bytes 276488 | tf_op jit(solution)/shard_map/ppermute | solution.py:176
  177.0 7.1 %collective-permute-start.27 = (bf16[128,1280]{1,0:T(8,128)(2,1)S(1)}, bf16[128,1280]{1,0:T(8,128)(2,1)S(1)}, u32[]{:S(2)}, u32[]{:S(2)}) collective-permute-start(bf16[128,1280]{1,0:T(8,128)(2,1)S(1)} %get-tuple-element.40), channel_id=1, source_target_pairs={{0,4},{4,8},{8,12},{12,14},{14,10},{10,6},{6,2},{2,0},{1,5},{5,9},... | collective-permute-start | bytes 983048 | tf_op jit(solution)/shard_map/ppermute | solution.py:119
  177.2 7.1 %collective-permute-start.23 = (bf16[128,1280]{1,0:T(8,128)(2,1)S(1)}, bf16[128,1280]{1,0:T(8,128)(2,1)S(1)}, u32[]{:S(2)}, u32[]{:S(2)}) collective-permute-start(bf16[128,1280]{1,0:T(8,128)(2,1)S(1)} %get-tuple-element.39), channel_id=1, source_target_pairs={{0,2},{4,0},{8,4},{12,8},{14,12},{10,14},{6,10},{2,6},{1,3},{5,1},... | collective-permute-start | bytes 983048 | tf_op jit(solution)/shard_map/ppermute | solution.py:119
  (21 other events, 111.6 us)

commit v15 on v9

--- a/solution.py
+++ b/solution.py
@@ -178,16 +178,6 @@
         if t < count - 2:
             acc = acc.astype(wire_dtype)
     return acc
-
-
-def direct_reduce_scatter(select_block, axis, count):
-    index = lax.axis_index(axis)
-    total = select_block(index).astype(jnp.float32)
-    for shift in range(1, count):
-        perm = [(s, (s + shift) % count) for s in range(count)]
-        sent = select_block((index + shift) % count).astype(jnp.bfloat16)
-        total = total + lax.ppermute(sent, axis, perm).astype(jnp.float32)
-    return total
 
 
 def body(ring, queries, key_rows, value_rows, trunk_state, skip_input, norm_gain, conv_weight, cotangent):
@@ -262,7 +252,7 @@
                 full_weight, (index, dp_index, 0, column), (1, 1, rows_per, width)
             ).reshape(rows_per, width)
 
-        grad_weight = direct_reduce_scatter(weight_block(0, CO), "seq", seq_count)
+        grad_weight = ring_reduce_scatter_sliced(weight_block(0, CO), "seq", ring, True)
     else:
         weight_part = (
             lax.dot_general(

time: 160 us -> 167 us (1.044)
  starting transfers between devices: 65.6 us -> 37.2 us
  waiting for transfers between devices: 33.2 us -> 57.8 us
  other arithmetic: 14.4 us -> 24.9 us
    ppermute x7, waiting for transfers between devices: 1.01 us -> 24.1 us  [ring_reduce_scatter_sliced(): received = lax.ppermute(acc, axis, perm).astype(jnp.float32)]
    ppermute x7, starting transfers between devices: 22.7 us -> 5.69 us  [ring_reduce_scatter_sliced(): received = lax.ppermute(acc, axis, perm).astype(jnp.float32)]
    ppermute x8, starting transfers between devices: 22 us -> 10.7 us  [ring_scatter_back(): received = lax.ppermute(acc, 'seq', perm).astype(jnp.float32)]
    convert_element_type x0 -> x6, other arithmetic: none -> 6.97 us  [ring_reduce_scatter_sliced(): acc = acc.astype(wire_dtype)]
    convert_element_type x2, other arithmetic: 1.16 us -> 4.53 us  [ring_scatter_back(): add_part(chain[t - 2].astype(jnp.float32), received, side)]
    unnamed x54 -> x44, local copies, waits for them, and re-layouts: 10.4 us -> 11.4 us
  transfers between devices with their start and end apart: 29 -> 29, of which waited for: 13 -> 17; matrix products, arithmetic and copies ran while one was open for 13% -> 17% of each run, Pallas kernels for 0% -> 0%
where the time goes in v15:
time: 167 us; the launch traced here: 166 us
  waiting for transfers between devices  57.8 us (35%)
  starting transfers between devices  37.2 us (22%)
  local copies, waits for them, and re-layouts  26.1 us (16%)
  other arithmetic  24.9 us (15%)
  matrix products  18.9 us (11%)
    ppermute x7, waiting for transfers between devices, ring_reduce_scatter_sliced(): received = lax.ppermute(acc, axis, perm).astype(jnp.float32)  24.1 us
    ppermute x3, waiting for transfers between devices, ring_gather(): current = lax.ppermute(current, 'seq', forward)  12 us
    unnamed x44, local copies, waits for them, and re-layouts  11.4 us
    ppermute x8, waiting for transfers between devices, ring_scatter_back(): received = lax.ppermute(acc, 'seq', perm).astype(jnp.float32)  11.3 us
    ppermute x8, starting transfers between devices, ring_scatter_back(): received = lax.ppermute(acc, 'seq', perm).astype(jnp.float32)  10.7 us
    ppermute x2, starting transfers between devices, extended(): before = lax.ppermute(last, axis, up)  8.32 us
    convert_element_type x6, other arithmetic, ring_reduce_scatter_sliced(): acc = acc.astype(wire_dtype)  6.97 us
    ppermute x3, starting transfers between devices, ring_gather(): current = lax.ppermute(current, 'seq', forward)  6.37 us
  transfers between devices with their start and end apart: 29, of which 17 were waited for; matrix products, arithmetic and copies ran while one was open for 17% of the time, Pallas kernels for 0%

profile of v15, /device:TPU:0, one launch (start us, length us, event | category | flops | bytes accessed | tf_op | source)
XLA Modules:
  0.0 166.0 jit_solution(17619314389029785922)
XLA Ops:
  0.6 1.2 copy.37
  3.9 3.1 %collective-permute-start = (bf16[128,1280]{0,1:T(8,128)(2,1)}, bf16[128,1280]{0,1:T(8,128)(2,1)}, u32[]{:S(2)}, u32[]{:S(2)}) collective-permute-start(bf16[128,1280]{0,1:T(8,128)(2,1)} %get-tuple-element.38), channel_id=1, source_target_pairs={{0,4},{4,8},{8,12},{12,14},{14,10},{10,6},{6,2},{2,0},{1,5},{5,9},... | collective-permute-start | bytes 983048 | tf_op jit(solution)/shard_map/ppermute | solution.py:76
  8.7 6.2 %collective-permute-done = bf16[128,1280]{0,1:T(8,128)(2,1)} collective-permute-done((bf16[128,1280]{0,1:T(8,128)(2,1)}, bf16[128,1280]{0,1:T(8,128)(2,1)}, u32[]{:S(2)}, u32[]{:S(2)}) %collective-permute-start) | collective-permute-done | bytes 327712 | tf_op jit(solution)/shard_map/ppermute | solution.py:76
  14.9 1.8 %collective-permute-start.1 = (bf16[128,1280]{0,1:T(8,128)(2,1)}, bf16[128,1280]{0,1:T(8,128)(2,1)S(1)}, u32[]{:S(2)}, u32[]{:S(2)}) collective-permute-start(bf16[128,1280]{0,1:T(8,128)(2,1)} %collective-permute-done), channel_id=1, source_target_pairs={{0,4},{4,8},{8,12},{12,14},{14,10},{10,6},{6,2},{2,0},{1,5},{5,9},... | collective-permute-start | bytes 983048 | tf_op jit(solution)/shard_map/ppermute | solution.py:76
  16.9 1.2 fusion.59
  18.2 5.8 %collective-permute-done.1 = bf16[128,1280]{0,1:T(8,128)(2,1)S(1)} collective-permute-done((bf16[128,1280]{0,1:T(8,128)(2,1)}, bf16[128,1280]{0,1:T(8,128)(2,1)S(1)}, u32[]{:S(2)}, u32[]{:S(2)}) %collective-permute-start.1) | collective-permute-done | bytes 327712 | tf_op jit(solution)/shard_map/ppermute | solution.py:76
  24.0 1.5 collective-permute-start.2
  26.0 1.8 %constant_dynamic-update-slice_fusion.5 = bf16[1024,1280]{0,1:T(8,128)(2,1)} fusion(bf16[1024,1280]{0,1:T(8,128)(2,1)} %get-tuple-element.39, bf16[128,1280]{0,1:T(8,128)(2,1)} %collective-permute-done), kind=kLoop, calls=%fused_computation.154 | loop fusion | bytes 655360
  28.5 4.8 %collective-permute-done.5 = bf16[128,1280]{0,1:T(8,128)(2,1)S(1)} collective-permute-done((bf16[128,1280]{0,1:T(8,128)(2,1)S(1)}, bf16[128,1280]{0,1:T(8,128)(2,1)S(1)}, u32[]{:S(2)}, u32[]{:S(2)}) %collective-permute-start.5) | collective-permute-done | bytes 327712 | tf_op jit(solution)/shard_map/ppermute | solution.py:82
  33.9 1.6 collective-permute-start.6
  40.1 1.5 slice.170
  41.6 1.9 %slice.171 = bf16[1024,512]{0,1:T(8,128)(2,1)S(1)} slice(bf16[1024,1280]{0,1:T(8,128)(2,1)} %maximum_dynamic-update-slice_fusion), slice={[0:1024], [0:512]} | slice | bytes 2097152 | tf_op jit(solution)/shard_map/slice | solution.py:191
  46.4 3.4 %collective-permute-start.8 = (bf16[2,768]{1,0:T(2,128)(2,1)S(1)}, bf16[2,768]{1,0:T(2,128)(2,1)S(1)}, u32[]{:S(2)}, u32[]{:S(2)}) collective-permute-start(bf16[2,768]{1,0:T(2,128)(2,1)S(1)} %get-tuple-element.37), channel_id=1, source_target_pairs={{0,2},{2,4},{4,6},{6,8},{8,10},{10,12},{12,14},{1,3},{3,5},{5,7},{... | collective-permute-start | bytes 9224 | tf_op jit(solution)/shard_map/ppermute | solution.py:24
  49.8 1.4 collective-permute-start.9
  51.6 3.8 %collective-permute-done.9 = bf16[2,768]{1,0:T(2,128)(2,1)S(1)} collective-permute-done((bf16[2,768]{1,0:T(2,128)(2,1)S(1)}, bf16[2,768]{1,0:T(2,128)(2,1)S(1)}, u32[]{:S(2)}, u32[]{:S(2)}) %collective-permute-start.9) | collective-permute-done | bytes 3104 | tf_op jit(solution)/shard_map/ppermute | solution.py:25
  55.7 2.0 %fusion.32 = (bf16[256,384]{1,0:T(8,128)(2,1)S(1)}, bf16[1,256,384]{2,1,0:T(8,128)(2,1)}) fusion(bf16[1,256,384]{2,1,0:T(8,128)(2,1)S(1)} %copy-done.16, bf16[256,3840]{1,0:T(8,128)(2,1)S(1)} %fusion.33, bf16[3840,384]{1,0:T(8,128)(2,1)S(1)} %copy-done), kind=kOutput, calls=%fused_computation.84 | convolution fusion | flops 756252672 | bytes 5505024 | tf_op jit(solution)/shard_map/dot_general | solution.py:220
  57.7 1.3 collective-permute-start.10
  59.0 5.0 %collective-permute-start.11 = (bf16[2,384]{1,0:T(2,128)(2,1)S(1)}, bf16[2,384]{1,0:T(2,128)(2,1)S(1)}, u32[]{:S(2)}, u32[]{:S(2)}) collective-permute-start(bf16[2,384]{1,0:T(2,128)(2,1)S(1)} %get-tuple-element.40), channel_id=1, source_target_pairs={{0,2},{2,4},{4,6},{6,8},{8,10},{10,12},{12,14},{1,3},{3,5},{5,7},{... | collective-permute-start | bytes 4616 | tf_op jit(solution)/shard_map/ppermute | solution.py:24
  68.6 1.7 %copy.41 = bf16[128,768]{0,1:T(8,128)(2,1)} copy(bf16[128,768]{1,0:T(8,128)(2,1)} %convolution_convert_fusion.1) | data formatting | bytes 393216 | tf_op jit(solution)/shard_map/convert_element_type | solution.py:295
  70.3 1.2 multiply_reduce_fusion.2
  71.5 3.6 %convolution_convert_fusion = bf16[4,192,1024]{2,1,0:T(8,128)(2,1)} fusion(bf16[128,4,192]{0,2,1:T(8,128)(2,1)} %bitcast.168, f32[4,1024,128]{2,1,0:T(8,128)} %copy-done.2, f32[4,128]{1,0:T(4,128)S(1)} %log_add_fusion), kind=kOutput, calls=%fused_computation.24 | convolution fusion | flops 203685888 | bytes 3868672 | tf_op jit(solution)/shard_map/hij,ihd->jhd/dot_general | solution.py:310
  75.1 2.1 %multiply_convert_fusion.1 = bf16[4,128,1024]{1,2,0:T(8,128)(2,1)} fusion(f32[4,1024,128]{2,1,0:T(8,128)S(1)} %copy-done.3, bf16[128,4,192]{0,2,1:T(8,128)(2,1)S(1)} %bitcast.169, bf16[1024,4,192]{0,2,1:T(8,128)(2,1)S(1)} %bitcast.149, f32[4,128]{1,0:T(4,128)S(1)} %bitcast.177, f32[4,128]{1,0:T(4,128)S(1)} %log_add_fusion), kind=kOutput, calls=%fused_computation.22 | convolution fusion | flops 203948032 | bytes 4919296 | tf_op jit(solution)/shard_map/ihd,jhd->hij/dot_general | solution.py:298
  77.2 2.6 %copy.50 = bf16[1024,768]{1,0:T(8,128)(2,1)} copy(bf16[1024,768]{0,1:T(8,128)(2,1)} %bitcast.160) | data formatting | bytes 3145728 | tf_op jit(solution)/shard_map/reshape | solution.py:314
  79.8 2.6 %fusion.9 = bf16[1024,4,128]{2,0,1:T(8,128)(2,1)} fusion(bf16[4,128,1024]{1,2,0:T(8,128)(2,1)} %multiply_convert_fusion.1, bf16[128,4,128]{0,2,1:T(8,128)(2,1)} %bitcast.172), kind=kOutput, calls=%fused_computation.35 | convolution fusion | flops 135266304 | bytes 2228224 | tf_op jit(solution)/shard_map/hij,ihd->jhd/dot_general | solution.py:307
  82.4 2.3 %copy.47 = bf16[1024,4,128]{0,2,1:T(8,128)(2,1)} copy(bf16[1024,4,128]{2,0,1:T(8,128)(2,1)} %fusion.9) | data formatting | bytes 2097152 | tf_op jit(solution)/shard_map/mul | solution.py:307
  84.7 2.3 %copy.49 = bf16[1024,512]{1,0:T(8,128)(2,1)} copy(bf16[1024,512]{0,1:T(8,128)(2,1)} %bitcast.166) | data formatting | bytes 2097152 | tf_op jit(solution)/shard_map/reshape | solution.py:313
  87.0 1.9 %fusion.63 = (bf16[128,640]{1,0:T(8,128)(2,1)}, bf16[128,640]{1,0:T(8,128)(2,1)}, bf16[128,640]{1,0:T(8,128)(2,1)}) fusion(bf16[1024,768]{1,0:T(8,128)(2,1)} %copy.50, bf16[1024,512]{1,0:T(8,128)(2,1)} %copy.49), kind=kLoop, calls=%fused_computation.143 | loop fusion | flops 327680 | bytes 3440640 | tf_op jit(solution)/shard_map/concatenate | solution.py:311
  88.9 2.9 %collective-permute-start.12 = (bf16[128,640]{1,0:T(8,128)(2,1)}, bf16[128,640]{1,0:T(8,128)(2,1)}, u32[]{:S(2)}, u32[]{:S(2)}) collective-permute-start(bf16[128,640]{1,0:T(8,128)(2,1)} %get-tuple-element.29), channel_id=1, source_target_pairs={{0,2},{4,0},{8,4},{12,8},{14,12},{10,14},{6,10},{2,6},{1,3},{5,1},... | collective-permute-start | bytes 491528 | tf_op jit(solution)/shard_map/ppermute | solution.py:119
  91.8 1.7 %collective-permute-start.16 = (bf16[128,640]{1,0:T(8,128)(2,1)}, bf16[128,640]{1,0:T(8,128)(2,1)}, u32[]{:S(2)}, u32[]{:S(2)}) collective-permute-start(bf16[128,640]{1,0:T(8,128)(2,1)} %get-tuple-element.30), channel_id=1, source_target_pairs={{0,4},{4,8},{8,12},{12,14},{14,10},{10,6},{6,2},{2,0},{1,5},{5,9},... | collective-permute-start | bytes 491528 | tf_op jit(solution)/shard_map/ppermute | solution.py:119
  94.2 2.9 %collective-permute-done.12 = bf16[128,640]{1,0:T(8,128)(2,1)} collective-permute-done((bf16[128,640]{1,0:T(8,128)(2,1)}, bf16[128,640]{1,0:T(8,128)(2,1)}, u32[]{:S(2)}, u32[]{:S(2)}) %collective-permute-start.12) | collective-permute-done | bytes 163872 | tf_op jit(solution)/shard_map/ppermute | solution.py:119
  97.4 1.2 add_convert_fusion.6
  99.4 1.6 collective-permute-start.13
  107.5 4.7 %collective-permute-done.22 = bf16[240,384]{1,0:T(8,128)(2,1)} collective-permute-done((bf16[240,384]{1,0:T(8,128)(2,1)S(1)}, bf16[240,384]{1,0:T(8,128)(2,1)}, u32[]{:S(2)}, u32[]{:S(2)}) %collective-permute-start.22) | collective-permute-done | bytes 184352 | tf_op jit(solution)/shard_map/ppermute | solution.py:176
  113.8 2.8 %collective-permute-done.17 = bf16[128,1280]{1,0:T(8,128)(2,1)} collective-permute-done((bf16[128,1280]{1,0:T(8,128)(2,1)S(1)}, bf16[128,1280]{1,0:T(8,128)(2,1)}, u32[]{:S(2)}, u32[]{:S(2)}) %collective-permute-start.17) | collective-permute-done | bytes 327712 | tf_op jit(solution)/shard_map/ppermute | solution.py:119
  116.6 2.3 %add_convert_fusion.4 = (bf16[128,1280]{1,0:T(8,128)(2,1)}, bf16[128,1280]{1,0:T(8,128)(2,1)}) fusion(bf16[128,1280]{1,0:T(8,128)(2,1)} %collective-permute-done.13, bf16[1024,768]{1,0:T(8,128)(2,1)} %copy.50, bf16[1024,512]{1,0:T(8,128)(2,1)} %copy.49, bf16[128,1280]{1,0:T(8,128)(2,1)} %collective-permute-done.17), kind=kLoop, calls=%fused_computation.67 | loop fusion | flops 2293760 | bytes 3932160 | tf_op jit(solution)/shard_map/convert_element_type | solution.py:123
  118.9 1.5 collective-permute-start.14
  122.1 1.8 %collective-permute-start.24 = (bf16[240,384]{1,0:T(8,128)(2,1)S(1)}, bf16[240,384]{1,0:T(8,128)(2,1)S(1)}, u32[]{:S(2)}, u32[]{:S(2)}) collective-permute-start(bf16[240,384]{1,0:T(8,128)(2,1)S(1)} %fusion.39), channel_id=1, source_target_pairs={{0,4},{4,8},{8,12},{12,14},{14,10},{10,6},{6,2},{2,0},{1,5},{5,9},... | collective-permute-start | bytes 552968 | tf_op jit(solution)/shard_map/ppermute | solution.py:176
  123.8 2.4 %collective-permute-done.14 = bf16[128,1280]{1,0:T(8,128)(2,1)S(1)} collective-permute-done((bf16[128,1280]{1,0:T(8,128)(2,1)}, bf16[128,1280]{1,0:T(8,128)(2,1)S(1)}, u32[]{:S(2)}, u32[]{:S(2)}) %collective-permute-start.14) | collective-permute-done | bytes 327712 | tf_op jit(solution)/shard_map/ppermute | solution.py:119
  126.2 2.9 %collective-permute-done.18 = bf16[128,1280]{1,0:T(8,128)(2,1)} collective-permute-done((bf16[128,1280]{1,0:T(8,128)(2,1)}, bf16[128,1280]{1,0:T(8,128)(2,1)}, u32[]{:S(2)}, u32[]{:S(2)}) %collective-permute-start.18) | collective-permute-done | bytes 327712 | tf_op jit(solution)/shard_map/ppermute | solution.py:119
  129.1 2.2 %add_convert_fusion.3 = (bf16[128,1280]{1,0:T(8,128)(2,1)}, bf16[128,1280]{1,0:T(8,128)(2,1)}) fusion(bf16[128,1280]{1,0:T(8,128)(2,1)S(1)} %collective-permute-done.14, bf16[1024,768]{1,0:T(8,128)(2,1)} %copy.50, bf16[1024,512]{1,0:T(8,128)(2,1)} %copy.49, bf16[128,1280]{1,0:T(8,128)(2,1)} %collective-permute-done.18), kind=kLoop, calls=%fused_computation.66 | loop fusion | flops 2293760 | bytes 3932160 | tf_op jit(solution)/shard_map/convert_element_type | solution.py:123
  131.7 1.6 collective-permute-start.15
  133.3 1.7 %fusion.38 = bf16[240,384]{1,0:T(8,128)(2,1)} fusion(f32[8,2,240,384]{3,2,1,0:T(8,128)} %bitcast.153, s32[]{:T(128)S(6)} %select_n.306, s32[]{:T(128)S(6)} %select_n.282, bf16[240,384]{1,0:T(8,128)(2,1)S(1)} %collective-permute-done.24), kind=kLoop, calls=%fused_computation.102 | loop fusion | flops 276480 | bytes 737288 | tf_op jit(solution)/shard_map/convert_element_type | solution.py:179
  136.7 6.0 %collective-permute-done.25 = bf16[240,384]{1,0:T(8,128)(2,1)} collective-permute-done((bf16[240,384]{1,0:T(8,128)(2,1)}, bf16[240,384]{1,0:T(8,128)(2,1)}, u32[]{:S(2)}, u32[]{:S(2)}) %collective-permute-start.25) | collective-permute-done | bytes 184352 | tf_op jit(solution)/shard_map/ppermute | solution.py:176
  145.1 5.3 %collective-permute-done.26 = bf16[240,384]{1,0:T(8,128)(2,1)S(1)} collective-permute-done((bf16[240,384]{1,0:T(8,128)(2,1)S(1)}, bf16[240,384]{1,0:T(8,128)(2,1)S(1)}, u32[]{:S(2)}, u32[]{:S(2)}) %collective-permute-start.26) | collective-permute-done | bytes 184352 | tf_op jit(solution)/shard_map/ppermute | solution.py:176
  153.0 4.4 %collective-permute-done.27 = bf16[240,384]{1,0:T(8,128)(2,1)S(1)} collective-permute-done((bf16[240,384]{1,0:T(8,128)(2,1)S(1)}, bf16[240,384]{1,0:T(8,128)(2,1)S(1)}, u32[]{:S(2)}, u32[]{:S(2)}) %collective-permute-start.27) | collective-permute-done | bytes 184352 | tf_op jit(solution)/shard_map/ppermute | solution.py:176
  158.4 1.5 collective-permute-start.28
  160.6 3.6 %collective-permute-done.28 = bf16[240,384]{1,0:T(8,128)(2,1)S(1)} collective-permute-done((bf16[240,384]{1,0:T(8,128)(2,1)S(1)}, bf16[240,384]{1,0:T(8,128)(2,1)S(1)}, u32[]{:S(2)}, u32[]{:S(2)}) %collective-permute-start.28) | collective-permute-done | bytes 184352 | tf_op jit(solution)/shard_map/ppermute | solution.py:176
  164.2 1.8 %bitcast_add_fusion = f32[240,384]{1,0:T(8,128)} fusion(f32[8,2,240,384]{3,2,1,0:T(8,128)} %bitcast.157, s32[]{:T(128)S(6)} %select_n.338, s32[]{:T(128)S(6)} %select_n.282, bf16[240,384]{1,0:T(8,128)(2,1)S(1)} %collective-permute-done.28), kind=kLoop, calls=%fused_computation.94 | loop fusion | flops 184320 | bytes 921608 | tf_op jit(solution)/shard_map/add | solution.py:177
  (120 shorter events, 38.7 us)
Async XLA Ops:
  0.6 55.0 %copy-start = (bf16[3840,384]{1,0:T(8,128)(2,1)S(1)}, bf16[3840,384]{1,0:T(8,128)(2,1)}, u32[]{:S(2)}) copy-start(bf16[3840,384]{1,0:T(8,128)(2,1)} %param.14) | copy-start | bytes 8847364
  3.9 11.0 %collective-permute-start = (bf16[128,1280]{0,1:T(8,128)(2,1)}, bf16[128,1280]{0,1:T(8,128)(2,1)}, u32[]{:S(2)}, u32[]{:S(2)}) collective-permute-start(bf16[128,1280]{0,1:T(8,128)(2,1)} %get-tuple-element.38), channel_id=1, source_target_pairs={{0,4},{4,8},{8,12},{12,14},{14,10},{10,6},{6,2},{2,0},{1,5},{5,9},... | collective-permute-start | bytes 983048 | tf_op jit(solution)/shard_map/ppermute | solution.py:76
  6.9 9.8 %collective-permute-start.3 = (bf16[128,1280]{0,1:T(8,128)(2,1)}, bf16[128,1280]{0,1:T(8,128)(2,1)S(1)}, u32[]{:S(2)}, u32[]{:S(2)}) collective-permute-start(bf16[128,1280]{0,1:T(8,128)(2,1)} %get-tuple-element.38), channel_id=1, source_target_pairs={{0,2},{4,0},{8,4},{12,8},{14,12},{10,14},{6,10},{2,6},{1,3},{5,1},... | collective-permute-start | bytes 983048 | tf_op jit(solution)/shard_map/ppermute | solution.py:82
  8.0 35.6 %copy-start.13 = (bf16[1,128,512]{1,2,0:T(8,128)(2,1)}, bf16[1,128,512]{1,2,0:T(8,128)(2,1)S(1)}, u32[]{:S(2)}) copy-start(bf16[1,128,512]{1,2,0:T(8,128)(2,1)S(1)} %copy.72) | copy-start | bytes 393220
  14.9 9.1 %collective-permute-start.1 = (bf16[128,1280]{0,1:T(8,128)(2,1)}, bf16[128,1280]{0,1:T(8,128)(2,1)S(1)}, u32[]{:S(2)}, u32[]{:S(2)}) collective-permute-start(bf16[128,1280]{0,1:T(8,128)(2,1)} %collective-permute-done), channel_id=1, source_target_pairs={{0,4},{4,8},{8,12},{12,14},{14,10},{10,6},{6,2},{2,0},{1,5},{5,9},... | collective-permute-start | bytes 983048 | tf_op jit(solution)/shard_map/ppermute | solution.py:76
  16.7 8.8 %collective-permute-start.4 = (bf16[128,1280]{0,1:T(8,128)(2,1)S(1)}, bf16[128,1280]{0,1:T(8,128)(2,1)S(1)}, u32[]{:S(2)}, u32[]{:S(2)}) collective-permute-start(bf16[128,1280]{0,1:T(8,128)(2,1)S(1)} %collective-permute-done.3), channel_id=1, source_target_pairs={{0,2},{4,0},{8,4},{12,8},{14,12},{10,14},{6,10},{2,6},{1,3},{5,1},... | collective-permute-start | bytes 983048 | tf_op jit(solution)/shard_map/ppermute | solution.py:82
  24.0 9.9 %collective-permute-start.2 = (bf16[128,1280]{0,1:T(8,128)(2,1)S(1)}, bf16[128,1280]{0,1:T(8,128)(2,1)S(1)}, u32[]{:S(2)}, u32[]{:S(2)}) collective-permute-start(bf16[128,1280]{0,1:T(8,128)(2,1)S(1)} %collective-permute-done.1), channel_id=1, source_target_pairs={{0,4},{4,8},{8,12},{12,14},{14,10},{10,6},{6,2},{2,0},{1,5},{5,9},... | collective-permute-start | bytes 983048 | tf_op jit(solution)/shard_map/ppermute | solution.py:76
  25.5 7.8 %collective-permute-start.5 = (bf16[128,1280]{0,1:T(8,128)(2,1)S(1)}, bf16[128,1280]{0,1:T(8,128)(2,1)S(1)}, u32[]{:S(2)}, u32[]{:S(2)}) collective-permute-start(bf16[128,1280]{0,1:T(8,128)(2,1)S(1)} %collective-permute-done.4), channel_id=1, source_target_pairs={{0,2},{4,0},{8,4},{12,8},{14,12},{10,14},{6,10},{2,6},{1,3},{5,1},... | collective-permute-start | bytes 983048 | tf_op jit(solution)/shard_map/ppermute | solution.py:82
  33.3 5.4 %collective-permute-start.7 = (bf16[128,640]{0,1:T(8,128)(2,1)S(1)}, bf16[128,640]{0,1:T(8,128)(2,1)S(1)}, u32[]{:S(2)}, u32[]{:S(2)}) collective-permute-start(bf16[128,640]{0,1:T(8,128)(2,1)S(1)} %slice.169), channel_id=1, source_target_pairs={{0,2},{4,0},{8,4},{12,8},{14,12},{10,14},{6,10},{2,6},{1,3},{5,1},... | collective-permute-start | bytes 491528 | tf_op jit(solution)/shard_map/ppermute | solution.py:85
  33.9 5.4 %collective-permute-start.6 = (bf16[128,640]{0,1:T(8,128)(2,1)S(1)}, bf16[128,640]{0,1:T(8,128)(2,1)S(1)}, u32[]{:S(2)}, u32[]{:S(2)}) collective-permute-start(bf16[128,640]{0,1:T(8,128)(2,1)S(1)} %slice.168), channel_id=1, source_target_pairs={{0,4},{4,8},{8,12},{12,14},{14,10},{10,6},{6,2},{2,0},{1,5},{5,9},... | collective-permute-start | bytes 491528 | tf_op jit(solution)/shard_map/ppermute | solution.py:79
  41.6 2.9 %copy-start.5 = (bf16[1024,768]{0,1:T(8,128)(2,1)}, bf16[1024,768]{0,1:T(8,128)(2,1)S(1)}, u32[]{:S(2)}) copy-start(bf16[1024,768]{0,1:T(8,128)(2,1)S(1)} %slice.170) | copy-start | bytes 4718596
  43.5 1.0 copy-start.8
  44.1 1.4 copy-start.2
  44.5 1.3 copy-start.15
  45.4 6.0 %copy-start.12 = (bf16[4,192,128]{2,1,0:T(8,128)(2,1)}, bf16[4,192,128]{2,1,0:T(8,128)(2,1)S(1)}, u32[]{:S(2)}) copy-start(bf16[4,192,128]{2,1,0:T(8,128)(2,1)S(1)} %convolution_convert_fusion.2) | copy-start | bytes 589828
  46.4 4.8 %collective-permute-start.8 = (bf16[2,768]{1,0:T(2,128)(2,1)S(1)}, bf16[2,768]{1,0:T(2,128)(2,1)S(1)}, u32[]{:S(2)}, u32[]{:S(2)}) collective-permute-start(bf16[2,768]{1,0:T(2,128)(2,1)S(1)} %get-tuple-element.37), channel_id=1, source_target_pairs={{0,2},{2,4},{4,6},{6,8},{8,10},{10,12},{12,14},{1,3},{3,5},{5,7},{... | collective-permute-start | bytes 9224 | tf_op jit(solution)/shard_map/ppermute | solution.py:24
  49.8 5.9 %copy-start.16 = (bf16[1,256,384]{2,1,0:T(8,128)(2,1)S(1)}, bf16[1,256,384]{2,1,0:T(8,128)(2,1)}, u32[]{:S(2)}) copy-start(bf16[1,256,384]{2,1,0:T(8,128)(2,1)} %param.15) | copy-start | bytes 589828
  49.8 5.6 %collective-permute-start.9 = (bf16[2,768]{1,0:T(2,128)(2,1)S(1)}, bf16[2,768]{1,0:T(2,128)(2,1)S(1)}, u32[]{:S(2)}, u32[]{:S(2)}) collective-permute-start(bf16[2,768]{1,0:T(2,128)(2,1)S(1)} %get-tuple-element.36), channel_id=1, source_target_pairs={{2,0},{4,2},{6,4},{8,6},{10,8},{12,10},{14,12},{3,1},{5,3},{7,5},{... | collective-permute-start | bytes 9224 | tf_op jit(solution)/shard_map/ppermute | solution.py:25
  57.7 6.3 %collective-permute-start.10 = (bf16[2,384]{1,0:T(2,128)(2,1)S(1)}, bf16[2,384]{1,0:T(2,128)(2,1)S(1)}, u32[]{:S(2)}, u32[]{:S(2)}) collective-permute-start(bf16[2,384]{1,0:T(2,128)(2,1)S(1)} %get-tuple-element.41), channel_id=1, source_target_pairs={{2,0},{4,2},{6,4},{8,6},{10,8},{12,10},{14,12},{3,1},{5,3},{7,5},{... | collective-permute-start | bytes 4616 | tf_op jit(solution)/shard_map/ppermute | solution.py:25
  59.0 6.2 %collective-permute-start.11 = (bf16[2,384]{1,0:T(2,128)(2,1)S(1)}, bf16[2,384]{1,0:T(2,128)(2,1)S(1)}, u32[]{:S(2)}, u32[]{:S(2)}) collective-permute-start(bf16[2,384]{1,0:T(2,128)(2,1)S(1)} %get-tuple-element.40), channel_id=1, source_target_pairs={{0,2},{2,4},{4,6},{6,8},{8,10},{10,12},{12,14},{1,3},{3,5},{5,7},{... | collective-permute-start | bytes 4616 | tf_op jit(solution)/shard_map/ppermute | solution.py:24
  70.3 4.8 %copy-start.3 = (f32[4,1024,128]{2,1,0:T(8,128)S(1)}, f32[4,1024,128]{2,1,0:T(8,128)}, u32[]{:S(2)}) copy-start(f32[4,1024,128]{2,1,0:T(8,128)} %copy-done.2) | copy-start | bytes 6291460
  70.3 4.8 %copy-start.6 = (bf16[1024,768]{0,1:T(8,128)(2,1)S(1)}, bf16[1024,768]{0,1:T(8,128)(2,1)}, u32[]{:S(2)}) copy-start(bf16[1024,768]{0,1:T(8,128)(2,1)} %copy-done.5) | copy-start | bytes 4718596
  70.3 4.8 %copy-start.11 = (bf16[128,768]{0,1:T(8,128)(2,1)S(1)}, bf16[128,768]{0,1:T(8,128)(2,1)}, u32[]{:S(2)}) copy-start(bf16[128,768]{0,1:T(8,128)(2,1)} %copy.41) | copy-start | bytes 589828
  88.9 8.2 %collective-permute-start.12 = (bf16[128,640]{1,0:T(8,128)(2,1)}, bf16[128,640]{1,0:T(8,128)(2,1)}, u32[]{:S(2)}, u32[]{:S(2)}) collective-permute-start(bf16[128,640]{1,0:T(8,128)(2,1)} %get-tuple-element.29), channel_id=1, source_target_pairs={{0,2},{4,0},{8,4},{12,8},{14,12},{10,14},{6,10},{2,6},{1,3},{5,1},... | collective-permute-start | bytes 491528 | tf_op jit(solution)/shard_map/ppermute | solution.py:119
  91.8 5.6 %collective-permute-start.16 = (bf16[128,640]{1,0:T(8,128)(2,1)}, bf16[128,640]{1,0:T(8,128)(2,1)}, u32[]{:S(2)}, u32[]{:S(2)}) collective-permute-start(bf16[128,640]{1,0:T(8,128)(2,1)} %get-tuple-element.30), channel_id=1, source_target_pairs={{0,4},{4,8},{8,12},{12,14},{14,10},{10,6},{6,2},{2,0},{1,5},{5,9},... | collective-permute-start | bytes 491528 | tf_op jit(solution)/shard_map/ppermute | solution.py:119
  93.5 5.2 %copy-start.14 = (bf16[128,640]{1,0:T(8,128)(2,1)S(1)}, bf16[128,640]{1,0:T(8,128)(2,1)}, u32[]{:S(2)}) copy-start(bf16[128,640]{1,0:T(8,128)(2,1)} %get-tuple-element.31) | copy-start | bytes 491524
  93.5 7.5 %collective-permute-start.21 = (bf16[256,384]{1,0:T(8,128)(2,1)S(1)}, bf16[256,384]{1,0:T(8,128)(2,1)S(1)}, u32[]{:S(2)}, u32[]{:S(2)}) collective-permute-start(bf16[256,384]{1,0:T(8,128)(2,1)S(1)} %get-tuple-element.34), channel_id=1, source_target_pairs={{0,1},{1,0},{2,3},{3,2},{4,5},{5,4},{6,7},{7,6},{8,9},{9,8},{10,11... | collective-permute-start | bytes 589832 | tf_op jit(solution)/shard_map/ppermute | solution.py:232
  93.6 7.4 %collective-permute-start.20 = (bf16[260,768]{1,0:T(8,128)(2,1)S(1)}, bf16[260,768]{1,0:T(8,128)(2,1)S(1)}, u32[]{:S(2)}, u32[]{:S(2)}) collective-permute-start(bf16[260,768]{1,0:T(8,128)(2,1)S(1)} %get-tuple-element.32), channel_id=1, source_target_pairs={{0,1},{1,0},{2,3},{3,2},{4,5},{5,4},{6,7},{7,6},{8,9},{9,8},{10,11... | collective-permute-start | bytes 1198088 | tf_op jit(solution)/shard_map/ppermute | solution.py:231
  99.4 14.4 %collective-permute-start.13 = (bf16[128,1280]{1,0:T(8,128)(2,1)}, bf16[128,1280]{1,0:T(8,128)(2,1)}, u32[]{:S(2)}, u32[]{:S(2)}) collective-permute-start(bf16[128,1280]{1,0:T(8,128)(2,1)} %pad_maximum_fusion.7), channel_id=1, source_target_pairs={{0,2},{4,0},{8,4},{12,8},{14,12},{10,14},{6,10},{2,6},{1,3},{5,1},... | collective-permute-start | bytes 983048 | tf_op jit(solution)/shard_map/ppermute | solution.py:119
  104.1 1.5 copy-start.1
  104.1 2.6 %copy-start.4 = (bf16[1024,512]{1,0:T(8,128)(2,1)S(1)}, bf16[1024,512]{1,0:T(8,128)(2,1)}, u32[]{:S(2)}) copy-start(bf16[1024,512]{1,0:T(8,128)(2,1)} %copy.49) | copy-start | bytes 3145732
  104.5 2.5 %copy-start.7 = (f32[3840,384]{1,0:T(8,128)}, f32[3840,384]{1,0:T(8,128)S(1)}, u32[]{:S(2)}) copy-start(f32[3840,384]{1,0:T(8,128)S(1)} %broadcast_multiply_fusion) | copy-start | bytes 17694724
  104.6 7.7 %collective-permute-start.22 = (bf16[240,384]{1,0:T(8,128)(2,1)S(1)}, bf16[240,384]{1,0:T(8,128)(2,1)}, u32[]{:S(2)}, u32[]{:S(2)}) collective-permute-start(bf16[240,384]{1,0:T(8,128)(2,1)S(1)} %fusion.61), channel_id=1, source_target_pairs={{0,4},{4,8},{8,12},{12,14},{14,10},{10,6},{6,2},{2,0},{1,5},{5,9},... | collective-permute-start | bytes 552968 | tf_op jit(solution)/shard_map/ppermute | solution.py:176
  107.1 9.6 %collective-permute-start.17 = (bf16[128,1280]{1,0:T(8,128)(2,1)S(1)}, bf16[128,1280]{1,0:T(8,128)(2,1)}, u32[]{:S(2)}, u32[]{:S(2)}) collective-permute-start(bf16[128,1280]{1,0:T(8,128)(2,1)S(1)} %fusion.47), channel_id=1, source_target_pairs={{0,4},{4,8},{8,12},{12,14},{14,10},{10,6},{6,2},{2,0},{1,5},{5,9},... | collective-permute-start | bytes 983048 | tf_op jit(solution)/shard_map/ppermute | solution.py:119
  113.3 7.7 %collective-permute-start.23 = (bf16[240,384]{1,0:T(8,128)(2,1)S(1)}, bf16[240,384]{1,0:T(8,128)(2,1)}, u32[]{:S(2)}, u32[]{:S(2)}) collective-permute-start(bf16[240,384]{1,0:T(8,128)(2,1)S(1)} %fusion.40), channel_id=1, source_target_pairs={{0,4},{4,8},{8,12},{12,14},{14,10},{10,6},{6,2},{2,0},{1,5},{5,9},... | collective-permute-start | bytes 552968 | tf_op jit(solution)/shard_map/ppermute | solution.py:176
  118.9 7.3 %collective-permute-start.14 = (bf16[128,1280]{1,0:T(8,128)(2,1)}, bf16[128,1280]{1,0:T(8,128)(2,1)S(1)}, u32[]{:S(2)}, u32[]{:S(2)}) collective-permute-start(bf16[128,1280]{1,0:T(8,128)(2,1)} %get-tuple-element.25), channel_id=1, source_target_pairs={{0,2},{4,0},{8,4},{12,8},{14,12},{10,14},{6,10},{2,6},{1,3},{5,1},... | collective-permute-start | bytes 983048 | tf_op jit(solution)/shard_map/ppermute | solution.py:119
  120.4 8.7 %collective-permute-start.18 = (bf16[128,1280]{1,0:T(8,128)(2,1)}, bf16[128,1280]{1,0:T(8,128)(2,1)}, u32[]{:S(2)}, u32[]{:S(2)}) collective-permute-start(bf16[128,1280]{1,0:T(8,128)(2,1)} %get-tuple-element.26), channel_id=1, source_target_pairs={{0,4},{4,8},{8,12},{12,14},{14,10},{10,6},{6,2},{2,0},{1,5},{5,9},... | collective-permute-start | bytes 983048 | tf_op jit(solution)/shard_map/ppermute | solution.py:119
  122.1 13.4 %copy-start.9 = (bf16[1024,512]{0,1:T(8,128)(2,1)S(1)}, bf16[1024,512]{0,1:T(8,128)(2,1)}, u32[]{:S(2)}) copy-start(bf16[1024,512]{0,1:T(8,128)(2,1)} %copy-done.8) | copy-start | bytes 3145732
  122.1 13.4 %copy-start.10 = (bf16[4,128,1024]{1,2,0:T(8,128)(2,1)S(1)}, bf16[4,128,1024]{1,2,0:T(8,128)(2,1)}, u32[]{:S(2)}) copy-start(bf16[4,128,1024]{1,2,0:T(8,128)(2,1)} %multiply_convert_fusion.1) | copy-start | bytes 3145732
  122.1 11.3 %collective-permute-start.24 = (bf16[240,384]{1,0:T(8,128)(2,1)S(1)}, bf16[240,384]{1,0:T(8,128)(2,1)S(1)}, u32[]{:S(2)}, u32[]{:S(2)}) collective-permute-start(bf16[240,384]{1,0:T(8,128)(2,1)S(1)} %fusion.39), channel_id=1, source_target_pairs={{0,4},{4,8},{8,12},{12,14},{14,10},{10,6},{6,2},{2,0},{1,5},{5,9},... | collective-permute-start | bytes 552968 | tf_op jit(solution)/shard_map/ppermute | solution.py:176
  131.3 12.6 %collective-permute-start.19 = (bf16[128,1280]{1,0:T(8,128)(2,1)}, bf16[128,1280]{1,0:T(8,128)(2,1)S(1)}, u32[]{:S(2)}, u32[]{:S(2)}) collective-permute-start(bf16[128,1280]{1,0:T(8,128)(2,1)} %get-tuple-element.24), channel_id=1, source_target_pairs={{0,4},{4,8},{8,12},{12,14},{14,10},{10,6},{6,2},{2,0},{1,5},{5,9},... | collective-permute-start | bytes 983048 | tf_op jit(solution)/shard_map/ppermute | solution.py:119
  131.7 12.2 %collective-permute-start.15 = (bf16[128,1280]{1,0:T(8,128)(2,1)}, bf16[128,1280]{1,0:T(8,128)(2,1)}, u32[]{:S(2)}, u32[]{:S(2)}) collective-permute-start(bf16[128,1280]{1,0:T(8,128)(2,1)} %get-tuple-element.23), channel_id=1, source_target_pairs={{0,2},{4,0},{8,4},{12,8},{14,12},{10,14},{6,10},{2,6},{1,3},{5,1},... | collective-permute-start | bytes 983048 | tf_op jit(solution)/shard_map/ppermute | solution.py:119
  135.0 7.6 %collective-permute-start.25 = (bf16[240,384]{1,0:T(8,128)(2,1)}, bf16[240,384]{1,0:T(8,128)(2,1)}, u32[]{:S(2)}, u32[]{:S(2)}) collective-permute-start(bf16[240,384]{1,0:T(8,128)(2,1)} %fusion.38), channel_id=1, source_target_pairs={{0,4},{4,8},{8,12},{12,14},{14,10},{10,6},{6,2},{2,0},{1,5},{5,9},... | collective-permute-start | bytes 552968 | tf_op jit(solution)/shard_map/ppermute | solution.py:176
  143.8 6.7 %collective-permute-start.26 = (bf16[240,384]{1,0:T(8,128)(2,1)S(1)}, bf16[240,384]{1,0:T(8,128)(2,1)S(1)}, u32[]{:S(2)}, u32[]{:S(2)}) collective-permute-start(bf16[240,384]{1,0:T(8,128)(2,1)S(1)} %fusion.37), channel_id=1, source_target_pairs={{0,4},{4,8},{8,12},{12,14},{14,10},{10,6},{6,2},{2,0},{1,5},{5,9},... | collective-permute-start | bytes 552968 | tf_op jit(solution)/shard_map/ppermute | solution.py:176
  151.5 5.9 %collective-permute-start.27 = (bf16[240,384]{1,0:T(8,128)(2,1)S(1)}, bf16[240,384]{1,0:T(8,128)(2,1)S(1)}, u32[]{:S(2)}, u32[]{:S(2)}) collective-permute-start(bf16[240,384]{1,0:T(8,128)(2,1)S(1)} %fusion.36), channel_id=1, source_target_pairs={{0,4},{4,8},{8,12},{12,14},{14,10},{10,6},{6,2},{2,0},{1,5},{5,9},... | collective-permute-start | bytes 552968 | tf_op jit(solution)/shard_map/ppermute | solution.py:176
  158.4 5.8 %collective-permute-start.28 = (bf16[240,384]{1,0:T(8,128)(2,1)S(1)}, bf16[240,384]{1,0:T(8,128)(2,1)S(1)}, u32[]{:S(2)}, u32[]{:S(2)}) collective-permute-start(bf16[240,384]{1,0:T(8,128)(2,1)S(1)} %fusion.35), channel_id=1, source_target_pairs={{0,4},{4,8},{8,12},{12,14},{14,10},{10,6},{6,2},{2,0},{1,5},{5,9},... | collective-permute-start | bytes 552968 | tf_op jit(solution)/shard_map/ppermute | solution.py:176

commit v16 on v8

--- a/solution.py
+++ b/solution.py
@@ -244,7 +244,7 @@
                 axis=0,
             )
             * norm_scale
-        ).reshape(seq_count, dp_count, rows_per, CO)
+        ).astype(jnp.bfloat16).reshape(seq_count, dp_count, rows_per, CO)
         dp_index = lax.axis_index("dp")
 
         def weight_block(column, width):

time: 159 us -> 159 us (level)
  transfers between devices with their start and end apart: 36 -> 36, of which waited for: 20 -> 21; matrix products, arithmetic and copies ran while one was open for 27% -> 27% of each run, Pallas kernels for 0% -> 0%
where the time goes in v16:
time: 159 us; the launch traced here: 158 us
  starting transfers between devices  45.5 us (29%)
  waiting for transfers between devices  45 us (28%)
  matrix products  24.7 us (16%)
  local copies, waits for them, and re-layouts  24 us (15%)
  other arithmetic  17.9 us (11%)
    ppermute x14, waiting for transfers between devices, ring_reduce_scatter_sliced(): received = lax.ppermute(acc, axis, perm).astype(jnp.float32)  19.3 us
    ppermute x14, starting transfers between devices, ring_reduce_scatter_sliced(): received = lax.ppermute(acc, axis, perm).astype(jnp.float32)  16.7 us
    ppermute x3, waiting for transfers between devices, ring_gather(): current = lax.ppermute(current, 'seq', forward)  12.7 us
    unnamed x60, local copies, waits for them, and re-layouts  9.73 us
    ppermute x2, starting transfers between devices, extended(): before = lax.ppermute(last, axis, up)  8.51 us
    dot_general x5, matrix products, body(): jnp.einsum('spc,spo->co', both_padded[:, offset:offset + positions], both...  8.5 us
    ppermute x8, starting transfers between devices, ring_scatter_back(): received = lax.ppermute(acc, 'seq', perm).astype(jnp.float32)  8.14 us
    ppermute x3, starting transfers between devices, ring_gather(): current = lax.ppermute(current, 'seq', forward)  6.37 us
  transfers between devices with their start and end apart: 36, of which 21 were waited for; matrix products, arithmetic and copies ran while one was open for 27% of the time, Pallas kernels for 0%

profile of v16, /device:TPU:0, one launch (start us, length us, event | category | flops | bytes accessed | tf_op | source)
XLA Modules:
  0.0 158.5 jit_solution(2538787446822095586)
XLA Ops:
  3.9 3.1 %collective-permute-start = (bf16[128,1280]{0,1:T(8,128)(2,1)}, bf16[128,1280]{0,1:T(8,128)(2,1)}, u32[]{:S(2)}, u32[]{:S(2)}) collective-permute-start(bf16[128,1280]{0,1:T(8,128)(2,1)} %get-tuple-element.54), channel_id=1, source_target_pairs={{0,4},{4,8},{8,12},{12,14},{14,10},{10,6},{6,2},{2,0},{1,5},{5,9},... | collective-permute-start | bytes 983048 | tf_op jit(solution)/shard_map/ppermute | solution.py:76
  8.0 6.9 %collective-permute-done = bf16[128,1280]{0,1:T(8,128)(2,1)} collective-permute-done((bf16[128,1280]{0,1:T(8,128)(2,1)}, bf16[128,1280]{0,1:T(8,128)(2,1)}, u32[]{:S(2)}, u32[]{:S(2)}) %collective-permute-start) | collective-permute-done | bytes 327712 | tf_op jit(solution)/shard_map/ppermute | solution.py:76
  14.9 1.8 %collective-permute-start.1 = (bf16[128,1280]{0,1:T(8,128)(2,1)}, bf16[128,1280]{0,1:T(8,128)(2,1)S(1)}, u32[]{:S(2)}, u32[]{:S(2)}) collective-permute-start(bf16[128,1280]{0,1:T(8,128)(2,1)} %collective-permute-done), channel_id=1, source_target_pairs={{0,4},{4,8},{8,12},{12,14},{14,10},{10,6},{6,2},{2,0},{1,5},{5,9},... | collective-permute-start | bytes 983048 | tf_op jit(solution)/shard_map/ppermute | solution.py:76
  18.2 5.8 %collective-permute-done.1 = bf16[128,1280]{0,1:T(8,128)(2,1)S(1)} collective-permute-done((bf16[128,1280]{0,1:T(8,128)(2,1)}, bf16[128,1280]{0,1:T(8,128)(2,1)S(1)}, u32[]{:S(2)}, u32[]{:S(2)}) %collective-permute-start.1) | collective-permute-done | bytes 327712 | tf_op jit(solution)/shard_map/ppermute | solution.py:76
  24.0 1.5 collective-permute-start.2
  26.0 1.7 %constant_dynamic-update-slice_fusion.5 = bf16[1024,1280]{0,1:T(8,128)(2,1)} fusion(bf16[1024,1280]{0,1:T(8,128)(2,1)} %get-tuple-element.55, bf16[128,1280]{0,1:T(8,128)(2,1)} %collective-permute-done), kind=kLoop, calls=%fused_computation.168 | loop fusion | bytes 655360
  28.5 4.8 %collective-permute-done.5 = bf16[128,1280]{0,1:T(8,128)(2,1)S(1)} collective-permute-done((bf16[128,1280]{0,1:T(8,128)(2,1)S(1)}, bf16[128,1280]{0,1:T(8,128)(2,1)S(1)}, u32[]{:S(2)}, u32[]{:S(2)}) %collective-permute-start.5) | collective-permute-done | bytes 327712 | tf_op jit(solution)/shard_map/ppermute | solution.py:82
  33.9 1.6 collective-permute-start.6
  40.1 1.5 slice.170
  41.6 1.9 %slice.171 = bf16[1024,512]{0,1:T(8,128)(2,1)S(1)} slice(bf16[1024,1280]{0,1:T(8,128)(2,1)} %maximum_dynamic-update-slice_fusion), slice={[0:1024], [0:512]} | slice | bytes 2097152 | tf_op jit(solution)/shard_map/slice | solution.py:191
  47.2 3.4 %collective-permute-start.8 = (bf16[2,768]{1,0:T(2,128)(2,1)S(1)}, bf16[2,768]{1,0:T(2,128)(2,1)S(1)}, u32[]{:S(2)}, u32[]{:S(2)}) collective-permute-start(bf16[2,768]{1,0:T(2,128)(2,1)S(1)} %get-tuple-element.53), channel_id=1, source_target_pairs={{0,2},{2,4},{4,6},{6,8},{8,10},{10,12},{12,14},{1,3},{3,5},{5,7},{... | collective-permute-start | bytes 9224 | tf_op jit(solution)/shard_map/ppermute | solution.py:24
  51.0 1.4 collective-permute-start.9
  52.8 3.8 %collective-permute-done.9 = bf16[2,768]{1,0:T(2,128)(2,1)S(1)} collective-permute-done((bf16[2,768]{1,0:T(2,128)(2,1)S(1)}, bf16[2,768]{1,0:T(2,128)(2,1)S(1)}, u32[]{:S(2)}, u32[]{:S(2)}) %collective-permute-start.9) | collective-permute-done | bytes 3104 | tf_op jit(solution)/shard_map/ppermute | solution.py:25
  56.8 2.0 %fusion.32 = (bf16[256,384]{1,0:T(8,128)(2,1)S(1)}, bf16[1,256,384]{2,1,0:T(8,128)(2,1)}) fusion(bf16[1,256,384]{2,1,0:T(8,128)(2,1)S(1)} %copy-done.24, bf16[256,3840]{1,0:T(8,128)(2,1)S(1)} %fusion.33, bf16[3840,384]{1,0:T(8,128)(2,1)S(1)} %copy-done), kind=kOutput, calls=%fused_computation.84 | convolution fusion | flops 756252672 | bytes 5505024 | tf_op jit(solution)/shard_map/dot_general | solution.py:220
  60.1 5.1 %collective-permute-start.11 = (bf16[2,384]{1,0:T(2,128)(2,1)S(1)}, bf16[2,384]{1,0:T(2,128)(2,1)S(1)}, u32[]{:S(2)}, u32[]{:S(2)}) collective-permute-start(bf16[2,384]{1,0:T(2,128)(2,1)S(1)} %get-tuple-element.56), channel_id=1, source_target_pairs={{0,2},{2,4},{4,6},{6,8},{8,10},{10,12},{12,14},{1,3},{3,5},{5,7},{... | collective-permute-start | bytes 4616 | tf_op jit(solution)/shard_map/ppermute | solution.py:24
  71.3 4.2 %multiply_convert_fusion.2 = bf16[4,128,1024]{1,2,0:T(8,128)(2,1)} fusion(f32[4,1024,128]{2,1,0:T(8,128)} %copy-done.3, bf16[128,4,192]{0,2,1:T(8,128)(2,1)S(1)} %bitcast.186, bf16[1024,4,192]{0,2,1:T(8,128)(2,1)} %bitcast.167, f32[4,128]{1,0:T(4,128)S(1)} %bitcast.195, f32[4,128]{1,0:T(4,128)S(1)} %log_add_fusion), kind=kOutput, calls=%fused_computation.22 | convolution fusion | flops 203948032 | bytes 4919296 | tf_op jit(solution)/shard_map/ihd,jhd->hij/dot_general | solution.py:306
  75.6 1.8 %convolution_convert_fusion = bf16[4,192,1024]{2,1,0:T(8,128)(2,1)} fusion(bf16[128,4,192]{0,2,1:T(8,128)(2,1)S(1)} %bitcast.187, f32[4,1024,128]{2,1,0:T(8,128)S(1)} %copy-done.4, f32[4,128]{1,0:T(4,128)S(1)} %log_add_fusion), kind=kOutput, calls=%fused_computation.24 | convolution fusion | flops 203685888 | bytes 3868672 | tf_op jit(solution)/shard_map/hij,ihd->jhd/dot_general | solution.py:318
  77.3 2.7 %copy.50 = bf16[1024,768]{1,0:T(8,128)(2,1)} copy(bf16[1024,768]{0,1:T(8,128)(2,1)} %bitcast.178) | data formatting | bytes 3145728 | tf_op jit(solution)/shard_map/reshape | solution.py:322
  80.0 2.7 %fusion.9 = bf16[1024,4,128]{2,0,1:T(8,128)(2,1)} fusion(bf16[4,128,1024]{1,2,0:T(8,128)(2,1)} %multiply_convert_fusion.2, bf16[128,4,128]{0,2,1:T(8,128)(2,1)S(1)} %bitcast.190), kind=kOutput, calls=%fused_computation.35 | convolution fusion | flops 135266304 | bytes 2228224 | tf_op jit(solution)/shard_map/hij,ihd->jhd/dot_general | solution.py:315
  82.6 2.3 %copy.47 = bf16[1024,4,128]{0,2,1:T(8,128)(2,1)} copy(bf16[1024,4,128]{2,0,1:T(8,128)(2,1)} %fusion.9) | data formatting | bytes 2097152 | tf_op jit(solution)/shard_map/mul | solution.py:315
  84.9 2.3 %copy.49 = bf16[1024,512]{1,0:T(8,128)(2,1)} copy(bf16[1024,512]{0,1:T(8,128)(2,1)} %bitcast.184) | data formatting | bytes 2097152 | tf_op jit(solution)/shard_map/reshape | solution.py:321
  87.2 1.8 %fusion.8 = f32[3840,384]{1,0:T(8,128)S(1)} fusion(bf16[1,260,768]{2,1,0:T(8,128)(2,1)} %get-tuple-element.49, bf16[1,260,768]{2,1,0:T(8,128)(2,1)} %bitcast.32, bf16[1,256,384]{2,1,0:T(8,128)(2,1)} %bitcast.34, bf16[1,256,384]{2,1,0:T(8,128)(2,1)S(1)} %bitcast.179), kind=kOutput, calls=%fused_computation.34 | convolution fusion | flops 302579712 | bytes 2371584 | tf_op jit(solution)/shard_map/spc,spo->co/dot_general | solution.py:236
  89.1 1.7 %fusion.7 = f32[3840,384]{1,0:T(8,128)S(1)} fusion(f32[3840,384]{1,0:T(8,128)S(1)} %fusion.8, bf16[1,260,768]{2,1,0:T(8,128)(2,1)S(1)} %copy-done.18, bf16[1,260,768]{2,1,0:T(8,128)(2,1)} %bitcast.32, bf16[1,256,384]{2,1,0:T(8,128)(2,1)} %bitcast.34, bf16[1,256,384]{2,1,0:T(8,128)(2,1)S(1)} %bitcast.180), kind=kOutput, calls=%fused_computation.32 | convolution fusion | flops 302579712 | bytes 2377728 | tf_op jit(solution)/shard_map/spc,spo->co/dot_general | solution.py:236
  90.7 1.7 %fusion.6 = f32[3840,384]{1,0:T(8,128)S(1)} fusion(f32[3840,384]{1,0:T(8,128)S(1)} %fusion.7, bf16[1,260,768]{2,1,0:T(8,128)(2,1)S(1)} %copy-done.18, bf16[1,260,768]{2,1,0:T(8,128)(2,1)} %bitcast.32, bf16[1,256,384]{2,1,0:T(8,128)(2,1)} %bitcast.34, bf16[1,256,384]{2,1,0:T(8,128)(2,1)S(1)} %bitcast.181), kind=kOutput, calls=%fused_computation.30 | convolution fusion | flops 302579712 | bytes 2377728 | tf_op jit(solution)/shard_map/spc,spo->co/dot_general | solution.py:236
  92.4 1.7 %fusion.5 = f32[3840,384]{1,0:T(8,128)S(1)} fusion(f32[3840,384]{1,0:T(8,128)S(1)} %fusion.6, bf16[1,260,768]{2,1,0:T(8,128)(2,1)S(1)} %copy-done.18, bf16[1,260,768]{2,1,0:T(8,128)(2,1)} %bitcast.32, bf16[1,256,384]{2,1,0:T(8,128)(2,1)} %bitcast.34, bf16[1,256,384]{2,1,0:T(8,128)(2,1)S(1)} %bitcast.182), kind=kOutput, calls=%fused_computation.28 | convolution fusion | flops 302579712 | bytes 2377728 | tf_op jit(solution)/shard_map/spc,spo->co/dot_general | solution.py:236
  94.1 1.7 %fusion.4 = f32[3840,384]{1,0:T(8,128)S(1)} fusion(f32[3840,384]{1,0:T(8,128)S(1)} %fusion.5, bf16[1,260,768]{2,1,0:T(8,128)(2,1)} %bitcast.32, bf16[1,260,768]{2,1,0:T(8,128)(2,1)S(1)} %copy-done.18, bf16[1,256,384]{2,1,0:T(8,128)(2,1)} %bitcast.34, bf16[1,256,384]{2,1,0:T(8,128)(2,1)S(1)} %bitcast.183), kind=kOutput, calls=%fused_computation.26 | convolution fusion | flops 303759360 | bytes 2377728 | tf_op jit(solution)/shard_map/spc,spo->co/dot_general | solution.py:236
  96.5 4.3 %collective-permute-start.22 = (bf16[240,192]{1,0:T(8,128)(2,1)S(1)}, bf16[240,192]{1,0:T(8,128)(2,1)S(1)}, u32[]{:S(2)}, u32[]{:S(2)}) collective-permute-start(bf16[240,192]{1,0:T(8,128)(2,1)S(1)} %get-tuple-element.37), channel_id=1, source_target_pairs={{0,4},{4,8},{8,12},{12,14},{14,10},{10,6},{6,2},{2,0},{1,5},{5,9},... | collective-permute-start | bytes 276488 | tf_op jit(solution)/shard_map/ppermute | solution.py:176
  101.4 1.6 %collective-permute-start.16 = (bf16[128,640]{1,0:T(8,128)(2,1)S(1)}, bf16[128,640]{1,0:T(8,128)(2,1)S(1)}, u32[]{:S(2)}, u32[]{:S(2)}) collective-permute-start(bf16[128,640]{1,0:T(8,128)(2,1)S(1)} %get-tuple-element.46), channel_id=1, source_target_pairs={{0,4},{4,8},{8,12},{12,14},{14,10},{10,6},{6,2},{2,0},{1,5},{5,9},... | collective-permute-start | bytes 491528 | tf_op jit(solution)/shard_map/ppermute | solution.py:119
  103.0 1.5 collective-permute-done.22
  104.5 2.0 %collective-permute-done.29 = bf16[240,192]{1,0:T(8,128)(2,1)S(1)} collective-permute-done((bf16[240,192]{1,0:T(8,128)(2,1)S(1)}, bf16[240,192]{1,0:T(8,128)(2,1)S(1)}, u32[]{:S(2)}, u32[]{:S(2)}) %collective-permute-start.29) | collective-permute-done | bytes 92192 | tf_op jit(solution)/shard_map/ppermute | solution.py:176
  106.7 1.6 %collective-permute-start.23 = (bf16[240,192]{1,0:T(8,128)(2,1)S(1)}, bf16[240,192]{1,0:T(8,128)(2,1)S(1)}, u32[]{:S(2)}, u32[]{:S(2)}) collective-permute-start(bf16[240,192]{1,0:T(8,128)(2,1)S(1)} %get-tuple-element.35), channel_id=1, source_target_pairs={{0,4},{4,8},{8,12},{12,14},{14,10},{10,6},{6,2},{2,0},{1,5},{5,9},... | collective-permute-start | bytes 276488 | tf_op jit(solution)/shard_map/ppermute | solution.py:176
  109.1 2.5 %collective-permute-done.23 = bf16[240,192]{1,0:T(8,128)(2,1)S(1)} collective-permute-done((bf16[240,192]{1,0:T(8,128)(2,1)S(1)}, bf16[240,192]{1,0:T(8,128)(2,1)S(1)}, u32[]{:S(2)}, u32[]{:S(2)}) %collective-permute-start.23) | collective-permute-done | bytes 92192 | tf_op jit(solution)/shard_map/ppermute | solution.py:176
  111.6 1.6 collective-permute-done.30
  113.3 1.6 %collective-permute-start.24 = (bf16[240,192]{1,0:T(8,128)(2,1)S(1)}, bf16[240,192]{1,0:T(8,128)(2,1)S(1)}, u32[]{:S(2)}, u32[]{:S(2)}) collective-permute-start(bf16[240,192]{1,0:T(8,128)(2,1)S(1)} %get-tuple-element.33), channel_id=1, source_target_pairs={{0,4},{4,8},{8,12},{12,14},{14,10},{10,6},{6,2},{2,0},{1,5},{5,9},... | collective-permute-start | bytes 276488 | tf_op jit(solution)/shard_map/ppermute | solution.py:176
  116.6 1.7 %collective-permute-done.24 = bf16[240,192]{1,0:T(8,128)(2,1)S(1)} collective-permute-done((bf16[240,192]{1,0:T(8,128)(2,1)S(1)}, bf16[240,192]{1,0:T(8,128)(2,1)S(1)}, u32[]{:S(2)}, u32[]{:S(2)}) %collective-permute-start.24) | collective-permute-done | bytes 92192 | tf_op jit(solution)/shard_map/ppermute | solution.py:176
  118.3 1.9 %collective-permute-done.31 = bf16[240,192]{1,0:T(8,128)(2,1)S(1)} collective-permute-done((bf16[240,192]{1,0:T(8,128)(2,1)S(1)}, bf16[240,192]{1,0:T(8,128)(2,1)S(1)}, u32[]{:S(2)}, u32[]{:S(2)}) %collective-permute-start.31) | collective-permute-done | bytes 92192 | tf_op jit(solution)/shard_map/ppermute | solution.py:176
  123.0 1.4 collective-permute-start.17
  124.4 1.6 %collective-permute-done.25 = bf16[240,192]{1,0:T(8,128)(2,1)S(1)} collective-permute-done((bf16[240,192]{1,0:T(8,128)(2,1)}, bf16[240,192]{1,0:T(8,128)(2,1)S(1)}, u32[]{:S(2)}, u32[]{:S(2)}) %collective-permute-start.25) | collective-permute-done | bytes 92192 | tf_op jit(solution)/shard_map/ppermute | solution.py:176
  128.9 1.6 %collective-permute-start.33 = (bf16[240,192]{1,0:T(8,128)(2,1)S(1)}, bf16[240,192]{1,0:T(8,128)(2,1)S(1)}, u32[]{:S(2)}, u32[]{:S(2)}) collective-permute-start(bf16[240,192]{1,0:T(8,128)(2,1)S(1)} %get-tuple-element.30), channel_id=1, source_target_pairs={{0,2},{4,0},{8,4},{12,8},{14,12},{10,14},{6,10},{2,6},{1,3},{5,1},... | collective-permute-start | bytes 276488 | tf_op jit(solution)/shard_map/ppermute | solution.py:176
  131.0 2.3 %add_convert_fusion.4 = (bf16[128,1280]{1,0:T(8,128)(2,1)}, bf16[128,1280]{1,0:T(8,128)(2,1)}) fusion(bf16[128,1280]{1,0:T(8,128)(2,1)} %collective-permute-done.13, bf16[1024,768]{1,0:T(8,128)(2,1)} %copy.50, bf16[1024,512]{1,0:T(8,128)(2,1)} %copy.49, bf16[128,1280]{1,0:T(8,128)(2,1)} %collective-permute-done.17), kind=kLoop, calls=%fused_computation.67 | loop fusion | flops 2293760 | bytes 3932160 | tf_op jit(solution)/shard_map/convert_element_type | solution.py:123
  133.9 1.5 collective-permute-start.18
  135.3 1.7 %fusion.49 = (bf16[240,192]{1,0:T(8,128)(2,1)}, bf16[240,192]{1,0:T(8,128)(2,1)}) fusion(bf16[240,192]{1,0:T(8,128)(2,1)S(1)} %collective-permute-done.26, bf16[8,2,240,384]{3,2,1,0:T(8,128)(2,1)} %bitcast.175, s32[]{:T(128)S(6)} %select_n.538, s32[]{:T(128)S(6)} %select_n.498, s32[]{:T(128)S(6)} %select_n.602, bf16[240,192]{1,0:T(8,128)(2,1)S(1)} %collective-permute-done.33), kind=kLoop, calls=%fused_computation.124 | loop fusion | flops 368640 | bytes 552972 | tf_op jit(solution)/shard_map/convert_element_type | solution.py:179
  137.0 1.7 %collective-permute-start.27 = (bf16[240,192]{1,0:T(8,128)(2,1)}, bf16[240,192]{1,0:T(8,128)(2,1)S(1)}, u32[]{:S(2)}, u32[]{:S(2)}) collective-permute-start(bf16[240,192]{1,0:T(8,128)(2,1)} %get-tuple-element.27), channel_id=1, source_target_pairs={{0,4},{4,8},{8,12},{12,14},{14,10},{10,6},{6,2},{2,0},{1,5},{5,9},... | collective-permute-start | bytes 276488 | tf_op jit(solution)/shard_map/ppermute | solution.py:176
  140.3 3.5 %collective-permute-done.27 = bf16[240,192]{1,0:T(8,128)(2,1)S(1)} collective-permute-done((bf16[240,192]{1,0:T(8,128)(2,1)}, bf16[240,192]{1,0:T(8,128)(2,1)S(1)}, u32[]{:S(2)}, u32[]{:S(2)}) %collective-permute-start.27) | collective-permute-done | bytes 92192 | tf_op jit(solution)/shard_map/ppermute | solution.py:176
  146.4 1.5 collective-permute-start.35
  147.9 1.4 add_convert_fusion.3
  149.9 1.5 collective-permute-start.15
  154.1 2.4 %collective-permute-done.19 = bf16[128,1280]{1,0:T(8,128)(2,1)S(1)} collective-permute-done((bf16[128,1280]{1,0:T(8,128)(2,1)S(1)}, bf16[128,1280]{1,0:T(8,128)(2,1)S(1)}, u32[]{:S(2)}, u32[]{:S(2)}) %collective-permute-start.19) | collective-permute-done | bytes 327712 | tf_op jit(solution)/shard_map/ppermute | solution.py:119
  (151 shorter events, 43.6 us)
Async XLA Ops:
  0.6 56.1 %copy-start = (bf16[3840,384]{1,0:T(8,128)(2,1)S(1)}, bf16[3840,384]{1,0:T(8,128)(2,1)}, u32[]{:S(2)}) copy-start(bf16[3840,384]{1,0:T(8,128)(2,1)} %param.14) | copy-start | bytes 8847364
  0.6 7.3 %copy-start.23 = (bf16[768]{0:T(1024)(128)(2,1)S(1)}, bf16[768]{0:T(1024)(128)(2,1)}, u32[]{:S(2)}) copy-start(bf16[768]{0:T(1024)(128)(2,1)} %param.13) | copy-start | bytes 4612
  3.9 11.0 %collective-permute-start = (bf16[128,1280]{0,1:T(8,128)(2,1)}, bf16[128,1280]{0,1:T(8,128)(2,1)}, u32[]{:S(2)}, u32[]{:S(2)}) collective-permute-start(bf16[128,1280]{0,1:T(8,128)(2,1)} %get-tuple-element.54), channel_id=1, source_target_pairs={{0,4},{4,8},{8,12},{12,14},{14,10},{10,6},{6,2},{2,0},{1,5},{5,9},... | collective-permute-start | bytes 983048 | tf_op jit(solution)/shard_map/ppermute | solution.py:76
  6.9 9.8 %collective-permute-start.3 = (bf16[128,1280]{0,1:T(8,128)(2,1)}, bf16[128,1280]{0,1:T(8,128)(2,1)S(1)}, u32[]{:S(2)}, u32[]{:S(2)}) collective-permute-start(bf16[128,1280]{0,1:T(8,128)(2,1)} %get-tuple-element.54), channel_id=1, source_target_pairs={{0,2},{4,0},{8,4},{12,8},{14,12},{10,14},{6,10},{2,6},{1,3},{5,1},... | collective-permute-start | bytes 983048 | tf_op jit(solution)/shard_map/ppermute | solution.py:82
  8.0 35.5 %copy-start.16 = (bf16[1,128,512]{1,2,0:T(8,128)(2,1)}, bf16[1,128,512]{1,2,0:T(8,128)(2,1)S(1)}, u32[]{:S(2)}) copy-start(bf16[1,128,512]{1,2,0:T(8,128)(2,1)S(1)} %copy.72) | copy-start | bytes 393220
  14.9 9.1 %collective-permute-start.1 = (bf16[128,1280]{0,1:T(8,128)(2,1)}, bf16[128,1280]{0,1:T(8,128)(2,1)S(1)}, u32[]{:S(2)}, u32[]{:S(2)}) collective-permute-start(bf16[128,1280]{0,1:T(8,128)(2,1)} %collective-permute-done), channel_id=1, source_target_pairs={{0,4},{4,8},{8,12},{12,14},{14,10},{10,6},{6,2},{2,0},{1,5},{5,9},... | collective-permute-start | bytes 983048 | tf_op jit(solution)/shard_map/ppermute | solution.py:76
  16.7 8.8 %collective-permute-start.4 = (bf16[128,1280]{0,1:T(8,128)(2,1)S(1)}, bf16[128,1280]{0,1:T(8,128)(2,1)S(1)}, u32[]{:S(2)}, u32[]{:S(2)}) collective-permute-start(bf16[128,1280]{0,1:T(8,128)(2,1)S(1)} %collective-permute-done.3), channel_id=1, source_target_pairs={{0,2},{4,0},{8,4},{12,8},{14,12},{10,14},{6,10},{2,6},{1,3},{5,1},... | collective-permute-start | bytes 983048 | tf_op jit(solution)/shard_map/ppermute | solution.py:82
  16.9 28.5 %copy-start.20 = (s32[256]{0:T(256)}, s32[256]{0:T(256)S(1)}, u32[]{:S(2)}) copy-start(s32[256]{0:T(256)S(1)} %and_select_fusion) | copy-start | bytes 3076
  24.0 9.9 %collective-permute-start.2 = (bf16[128,1280]{0,1:T(8,128)(2,1)S(1)}, bf16[128,1280]{0,1:T(8,128)(2,1)S(1)}, u32[]{:S(2)}, u32[]{:S(2)}) collective-permute-start(bf16[128,1280]{0,1:T(8,128)(2,1)S(1)} %collective-permute-done.1), channel_id=1, source_target_pairs={{0,4},{4,8},{8,12},{12,14},{14,10},{10,6},{6,2},{2,0},{1,5},{5,9},... | collective-permute-start | bytes 983048 | tf_op jit(solution)/shard_map/ppermute | solution.py:76
  25.5 7.8 %collective-permute-start.5 = (bf16[128,1280]{0,1:T(8,128)(2,1)S(1)}, bf16[128,1280]{0,1:T(8,128)(2,1)S(1)}, u32[]{:S(2)}, u32[]{:S(2)}) collective-permute-start(bf16[128,1280]{0,1:T(8,128)(2,1)S(1)} %collective-permute-done.4), channel_id=1, source_target_pairs={{0,2},{4,0},{8,4},{12,8},{14,12},{10,14},{6,10},{2,6},{1,3},{5,1},... | collective-permute-start | bytes 983048 | tf_op jit(solution)/shard_map/ppermute | solution.py:82
  33.3 5.4 %collective-permute-start.7 = (bf16[128,640]{0,1:T(8,128)(2,1)S(1)}, bf16[128,640]{0,1:T(8,128)(2,1)S(1)}, u32[]{:S(2)}, u32[]{:S(2)}) collective-permute-start(bf16[128,640]{0,1:T(8,128)(2,1)S(1)} %slice.169), channel_id=1, source_target_pairs={{0,2},{4,0},{8,4},{12,8},{14,12},{10,14},{6,10},{2,6},{1,3},{5,1},... | collective-permute-start | bytes 491528 | tf_op jit(solution)/shard_map/ppermute | solution.py:85
  33.9 5.4 %collective-permute-start.6 = (bf16[128,640]{0,1:T(8,128)(2,1)S(1)}, bf16[128,640]{0,1:T(8,128)(2,1)S(1)}, u32[]{:S(2)}, u32[]{:S(2)}) collective-permute-start(bf16[128,640]{0,1:T(8,128)(2,1)S(1)} %slice.168), channel_id=1, source_target_pairs={{0,4},{4,8},{8,12},{12,14},{14,10},{10,6},{6,2},{2,0},{1,5},{5,9},... | collective-permute-start | bytes 491528 | tf_op jit(solution)/shard_map/ppermute | solution.py:79
  47.2 5.1 %collective-permute-start.8 = (bf16[2,768]{1,0:T(2,128)(2,1)S(1)}, bf16[2,768]{1,0:T(2,128)(2,1)S(1)}, u32[]{:S(2)}, u32[]{:S(2)}) collective-permute-start(bf16[2,768]{1,0:T(2,128)(2,1)S(1)} %get-tuple-element.53), channel_id=1, source_target_pairs={{0,2},{2,4},{4,6},{6,8},{8,10},{10,12},{12,14},{1,3},{3,5},{5,7},{... | collective-permute-start | bytes 9224 | tf_op jit(solution)/shard_map/ppermute | solution.py:24
  50.9 5.9 %copy-start.24 = (bf16[1,256,384]{2,1,0:T(8,128)(2,1)S(1)}, bf16[1,256,384]{2,1,0:T(8,128)(2,1)}, u32[]{:S(2)}) copy-start(bf16[1,256,384]{2,1,0:T(8,128)(2,1)} %param.15) | copy-start | bytes 589828
  51.0 5.6 %collective-permute-start.9 = (bf16[2,768]{1,0:T(2,128)(2,1)S(1)}, bf16[2,768]{1,0:T(2,128)(2,1)S(1)}, u32[]{:S(2)}, u32[]{:S(2)}) collective-permute-start(bf16[2,768]{1,0:T(2,128)(2,1)S(1)} %get-tuple-element.52), channel_id=1, source_target_pairs={{2,0},{4,2},{6,4},{8,6},{10,8},{12,10},{14,12},{3,1},{5,3},{7,5},{... | collective-permute-start | bytes 9224 | tf_op jit(solution)/shard_map/ppermute | solution.py:25
  58.8 28.4 %collective-permute-start.21 = (bf16[256,384]{1,0:T(8,128)(2,1)S(1)}, bf16[256,384]{1,0:T(8,128)(2,1)}, u32[]{:S(2)}, u32[]{:S(2)}) collective-permute-start(bf16[256,384]{1,0:T(8,128)(2,1)S(1)} %get-tuple-element.50), channel_id=1, source_target_pairs={{0,1},{1,0},{2,3},{3,2},{4,5},{5,4},{6,7},{7,6},{8,9},{9,8},{10,11... | collective-permute-start | bytes 589832 | tf_op jit(solution)/shard_map/ppermute | solution.py:232
  58.8 7.7 %collective-permute-start.10 = (bf16[2,384]{1,0:T(2,128)(2,1)S(1)}, bf16[2,384]{1,0:T(2,128)(2,1)S(1)}, u32[]{:S(2)}, u32[]{:S(2)}) collective-permute-start(bf16[2,384]{1,0:T(2,128)(2,1)S(1)} %get-tuple-element.57), channel_id=1, source_target_pairs={{2,0},{4,2},{6,4},{8,6},{10,8},{12,10},{14,12},{3,1},{5,3},{7,5},{... | collective-permute-start | bytes 4616 | tf_op jit(solution)/shard_map/ppermute | solution.py:25
  60.1 6.6 %collective-permute-start.11 = (bf16[2,384]{1,0:T(2,128)(2,1)S(1)}, bf16[2,384]{1,0:T(2,128)(2,1)S(1)}, u32[]{:S(2)}, u32[]{:S(2)}) collective-permute-start(bf16[2,384]{1,0:T(2,128)(2,1)S(1)} %get-tuple-element.56), channel_id=1, source_target_pairs={{0,2},{2,4},{4,6},{6,8},{8,10},{10,12},{12,14},{1,3},{3,5},{5,7},{... | collective-permute-start | bytes 4616 | tf_op jit(solution)/shard_map/ppermute | solution.py:24
  66.4 20.9 %collective-permute-start.20 = (bf16[260,768]{1,0:T(8,128)(2,1)}, bf16[260,768]{1,0:T(8,128)(2,1)}, u32[]{:S(2)}, u32[]{:S(2)}) collective-permute-start(bf16[260,768]{1,0:T(8,128)(2,1)} %get-tuple-element.48), channel_id=1, source_target_pairs={{0,1},{1,0},{2,3},{3,2},{4,5},{5,4},{6,7},{7,6},{8,9},{9,8},{10,11... | collective-permute-start | bytes 1198088 | tf_op jit(solution)/shard_map/ppermute | solution.py:231
  95.8 5.0 %copy-start.1 = (bf16[1024,768]{1,0:T(8,128)(2,1)S(1)}, bf16[1024,768]{1,0:T(8,128)(2,1)}, u32[]{:S(2)}) copy-start(bf16[1024,768]{1,0:T(8,128)(2,1)} %copy.50) | copy-start | bytes 4718596
  95.8 5.0 %copy-start.5 = (bf16[1024,512]{1,0:T(8,128)(2,1)S(1)}, bf16[1024,512]{1,0:T(8,128)(2,1)}, u32[]{:S(2)}) copy-start(bf16[1024,512]{1,0:T(8,128)(2,1)} %copy.49) | copy-start | bytes 3145732
  96.4 23.9 %copy-start.13 = (bf16[3840,384]{1,0:T(8,128)(2,1)}, bf16[3840,384]{1,0:T(8,128)(2,1)S(1)}, u32[]{:S(2)}) copy-start(bf16[3840,384]{1,0:T(8,128)(2,1)S(1)} %multiply_convert_fusion) | copy-start | bytes 8847364
  96.5 8.0 %collective-permute-start.22 = (bf16[240,192]{1,0:T(8,128)(2,1)S(1)}, bf16[240,192]{1,0:T(8,128)(2,1)S(1)}, u32[]{:S(2)}, u32[]{:S(2)}) collective-permute-start(bf16[240,192]{1,0:T(8,128)(2,1)S(1)} %get-tuple-element.37), channel_id=1, source_target_pairs={{0,4},{4,8},{8,12},{12,14},{14,10},{10,6},{6,2},{2,0},{1,5},{5,9},... | collective-permute-start | bytes 276488 | tf_op jit(solution)/shard_map/ppermute | solution.py:176
  100.8 5.8 %collective-permute-start.29 = (bf16[240,192]{1,0:T(8,128)(2,1)S(1)}, bf16[240,192]{1,0:T(8,128)(2,1)S(1)}, u32[]{:S(2)}, u32[]{:S(2)}) collective-permute-start(bf16[240,192]{1,0:T(8,128)(2,1)S(1)} %get-tuple-element.38), channel_id=1, source_target_pairs={{0,2},{4,0},{8,4},{12,8},{14,12},{10,14},{6,10},{2,6},{1,3},{5,1},... | collective-permute-start | bytes 276488 | tf_op jit(solution)/shard_map/ppermute | solution.py:176
  100.9 8.1 %collective-permute-start.12 = (bf16[128,640]{1,0:T(8,128)(2,1)S(1)}, bf16[128,640]{1,0:T(8,128)(2,1)S(1)}, u32[]{:S(2)}, u32[]{:S(2)}) collective-permute-start(bf16[128,640]{1,0:T(8,128)(2,1)S(1)} %get-tuple-element.45), channel_id=1, source_target_pairs={{0,2},{4,0},{8,4},{12,8},{14,12},{10,14},{6,10},{2,6},{1,3},{5,1},... | collective-permute-start | bytes 491528 | tf_op jit(solution)/shard_map/ppermute | solution.py:119
  101.4 7.6 %collective-permute-start.16 = (bf16[128,640]{1,0:T(8,128)(2,1)S(1)}, bf16[128,640]{1,0:T(8,128)(2,1)S(1)}, u32[]{:S(2)}, u32[]{:S(2)}) collective-permute-start(bf16[128,640]{1,0:T(8,128)(2,1)S(1)} %get-tuple-element.46), channel_id=1, source_target_pairs={{0,4},{4,8},{8,12},{12,14},{14,10},{10,6},{6,2},{2,0},{1,5},{5,9},... | collective-permute-start | bytes 491528 | tf_op jit(solution)/shard_map/ppermute | solution.py:119
  106.7 4.9 %collective-permute-start.23 = (bf16[240,192]{1,0:T(8,128)(2,1)S(1)}, bf16[240,192]{1,0:T(8,128)(2,1)S(1)}, u32[]{:S(2)}, u32[]{:S(2)}) collective-permute-start(bf16[240,192]{1,0:T(8,128)(2,1)S(1)} %get-tuple-element.35), channel_id=1, source_target_pairs={{0,4},{4,8},{8,12},{12,14},{14,10},{10,6},{6,2},{2,0},{1,5},{5,9},... | collective-permute-start | bytes 276488 | tf_op jit(solution)/shard_map/ppermute | solution.py:176
  108.3 4.9 %collective-permute-start.30 = (bf16[240,192]{1,0:T(8,128)(2,1)S(1)}, bf16[240,192]{1,0:T(8,128)(2,1)S(1)}, u32[]{:S(2)}, u32[]{:S(2)}) collective-permute-start(bf16[240,192]{1,0:T(8,128)(2,1)S(1)} %get-tuple-element.36), channel_id=1, source_target_pairs={{0,2},{4,0},{8,4},{12,8},{14,12},{10,14},{6,10},{2,6},{1,3},{5,1},... | collective-permute-start | bytes 276488 | tf_op jit(solution)/shard_map/ppermute | solution.py:176
  113.3 5.0 %collective-permute-start.24 = (bf16[240,192]{1,0:T(8,128)(2,1)S(1)}, bf16[240,192]{1,0:T(8,128)(2,1)S(1)}, u32[]{:S(2)}, u32[]{:S(2)}) collective-permute-start(bf16[240,192]{1,0:T(8,128)(2,1)S(1)} %get-tuple-element.33), channel_id=1, source_target_pairs={{0,4},{4,8},{8,12},{12,14},{14,10},{10,6},{6,2},{2,0},{1,5},{5,9},... | collective-permute-start | bytes 276488 | tf_op jit(solution)/shard_map/ppermute | solution.py:176
  114.9 5.3 %collective-permute-start.31 = (bf16[240,192]{1,0:T(8,128)(2,1)S(1)}, bf16[240,192]{1,0:T(8,128)(2,1)S(1)}, u32[]{:S(2)}, u32[]{:S(2)}) collective-permute-start(bf16[240,192]{1,0:T(8,128)(2,1)S(1)} %get-tuple-element.34), channel_id=1, source_target_pairs={{0,2},{4,0},{8,4},{12,8},{14,12},{10,14},{6,10},{2,6},{1,3},{5,1},... | collective-permute-start | bytes 276488 | tf_op jit(solution)/shard_map/ppermute | solution.py:176
  116.1 14.4 %collective-permute-start.13 = (bf16[128,1280]{1,0:T(8,128)(2,1)}, bf16[128,1280]{1,0:T(8,128)(2,1)}, u32[]{:S(2)}, u32[]{:S(2)}) collective-permute-start(bf16[128,1280]{1,0:T(8,128)(2,1)} %pad_maximum_fusion.8), channel_id=1, source_target_pairs={{0,2},{4,0},{8,4},{12,8},{14,12},{10,14},{6,10},{2,6},{1,3},{5,1},... | collective-permute-start | bytes 983048 | tf_op jit(solution)/shard_map/ppermute | solution.py:119
  120.9 5.1 %collective-permute-start.25 = (bf16[240,192]{1,0:T(8,128)(2,1)}, bf16[240,192]{1,0:T(8,128)(2,1)S(1)}, u32[]{:S(2)}, u32[]{:S(2)}) collective-permute-start(bf16[240,192]{1,0:T(8,128)(2,1)} %get-tuple-element.31), channel_id=1, source_target_pairs={{0,4},{4,8},{8,12},{12,14},{14,10},{10,6},{6,2},{2,0},{1,5},{5,9},... | collective-permute-start | bytes 276488 | tf_op jit(solution)/shard_map/ppermute | solution.py:176
  122.3 5.0 %collective-permute-start.32 = (bf16[240,192]{1,0:T(8,128)(2,1)S(1)}, bf16[240,192]{1,0:T(8,128)(2,1)}, u32[]{:S(2)}, u32[]{:S(2)}) collective-permute-start(bf16[240,192]{1,0:T(8,128)(2,1)S(1)} %get-tuple-element.32), channel_id=1, source_target_pairs={{0,2},{4,0},{8,4},{12,8},{14,12},{10,14},{6,10},{2,6},{1,3},{5,1},... | collective-permute-start | bytes 276488 | tf_op jit(solution)/shard_map/ppermute | solution.py:176
  123.0 8.0 %collective-permute-start.17 = (bf16[128,1280]{1,0:T(8,128)(2,1)S(1)}, bf16[128,1280]{1,0:T(8,128)(2,1)}, u32[]{:S(2)}, u32[]{:S(2)}) collective-permute-start(bf16[128,1280]{1,0:T(8,128)(2,1)S(1)} %fusion.41), channel_id=1, source_target_pairs={{0,4},{4,8},{8,12},{12,14},{14,10},{10,6},{6,2},{2,0},{1,5},{5,9},... | collective-permute-start | bytes 983048 | tf_op jit(solution)/shard_map/ppermute | solution.py:119
  128.4 6.9 %collective-permute-start.26 = (bf16[240,192]{1,0:T(8,128)(2,1)S(1)}, bf16[240,192]{1,0:T(8,128)(2,1)S(1)}, u32[]{:S(2)}, u32[]{:S(2)}) collective-permute-start(bf16[240,192]{1,0:T(8,128)(2,1)S(1)} %get-tuple-element.29), channel_id=1, source_target_pairs={{0,4},{4,8},{8,12},{12,14},{14,10},{10,6},{6,2},{2,0},{1,5},{5,9},... | collective-permute-start | bytes 276488 | tf_op jit(solution)/shard_map/ppermute | solution.py:176
  128.9 10.2 %copy-start.11 = (bf16[1024,512]{0,1:T(8,128)(2,1)S(1)}, bf16[1024,512]{0,1:T(8,128)(2,1)}, u32[]{:S(2)}) copy-start(bf16[1024,512]{0,1:T(8,128)(2,1)} %copy-done.10) | copy-start | bytes 3145732
  128.9 10.2 %copy-start.12 = (bf16[4,128,1024]{1,2,0:T(8,128)(2,1)S(1)}, bf16[4,128,1024]{1,2,0:T(8,128)(2,1)}, u32[]{:S(2)}) copy-start(bf16[4,128,1024]{1,2,0:T(8,128)(2,1)} %multiply_convert_fusion.2) | copy-start | bytes 3145732
  128.9 6.4 %collective-permute-start.33 = (bf16[240,192]{1,0:T(8,128)(2,1)S(1)}, bf16[240,192]{1,0:T(8,128)(2,1)S(1)}, u32[]{:S(2)}, u32[]{:S(2)}) collective-permute-start(bf16[240,192]{1,0:T(8,128)(2,1)S(1)} %get-tuple-element.30), channel_id=1, source_target_pairs={{0,2},{4,0},{8,4},{12,8},{14,12},{10,14},{6,10},{2,6},{1,3},{5,1},... | collective-permute-start | bytes 276488 | tf_op jit(solution)/shard_map/ppermute | solution.py:176
  133.3 14.6 %collective-permute-start.14 = (bf16[128,1280]{1,0:T(8,128)(2,1)}, bf16[128,1280]{1,0:T(8,128)(2,1)S(1)}, u32[]{:S(2)}, u32[]{:S(2)}) collective-permute-start(bf16[128,1280]{1,0:T(8,128)(2,1)} %get-tuple-element.41), channel_id=1, source_target_pairs={{0,2},{4,0},{8,4},{12,8},{14,12},{10,14},{6,10},{2,6},{1,3},{5,1},... | collective-permute-start | bytes 983048 | tf_op jit(solution)/shard_map/ppermute | solution.py:119
  133.9 14.1 %collective-permute-start.18 = (bf16[128,1280]{1,0:T(8,128)(2,1)}, bf16[128,1280]{1,0:T(8,128)(2,1)}, u32[]{:S(2)}, u32[]{:S(2)}) collective-permute-start(bf16[128,1280]{1,0:T(8,128)(2,1)} %get-tuple-element.42), channel_id=1, source_target_pairs={{0,4},{4,8},{8,12},{12,14},{14,10},{10,6},{6,2},{2,0},{1,5},{5,9},... | collective-permute-start | bytes 983048 | tf_op jit(solution)/shard_map/ppermute | solution.py:119
  137.0 6.7 %collective-permute-start.27 = (bf16[240,192]{1,0:T(8,128)(2,1)}, bf16[240,192]{1,0:T(8,128)(2,1)S(1)}, u32[]{:S(2)}, u32[]{:S(2)}) collective-permute-start(bf16[240,192]{1,0:T(8,128)(2,1)} %get-tuple-element.27), channel_id=1, source_target_pairs={{0,4},{4,8},{8,12},{12,14},{14,10},{10,6},{6,2},{2,0},{1,5},{5,9},... | collective-permute-start | bytes 276488 | tf_op jit(solution)/shard_map/ppermute | solution.py:176
  138.7 6.0 %collective-permute-start.34 = (bf16[240,192]{1,0:T(8,128)(2,1)}, bf16[240,192]{1,0:T(8,128)(2,1)}, u32[]{:S(2)}, u32[]{:S(2)}) collective-permute-start(bf16[240,192]{1,0:T(8,128)(2,1)} %get-tuple-element.28), channel_id=1, source_target_pairs={{0,2},{4,0},{8,4},{12,8},{14,12},{10,14},{6,10},{2,6},{1,3},{5,1},... | collective-permute-start | bytes 276488 | tf_op jit(solution)/shard_map/ppermute | solution.py:176
  145.8 5.6 %collective-permute-start.28 = (bf16[240,192]{1,0:T(8,128)(2,1)S(1)}, bf16[240,192]{1,0:T(8,128)(2,1)S(1)}, u32[]{:S(2)}, u32[]{:S(2)}) collective-permute-start(bf16[240,192]{1,0:T(8,128)(2,1)S(1)} %get-tuple-element.25), channel_id=1, source_target_pairs={{0,4},{4,8},{8,12},{12,14},{14,10},{10,6},{6,2},{2,0},{1,5},{5,9},... | collective-permute-start | bytes 276488 | tf_op jit(solution)/shard_map/ppermute | solution.py:176
  146.4 10.6 %copy-start.2 = (bf16[1024,768]{1,0:T(8,128)(2,1)S(1)}, bf16[1024,768]{1,0:T(8,128)(2,1)}, u32[]{:S(2)}) copy-start(bf16[1024,768]{1,0:T(8,128)(2,1)} %copy.50) | copy-start | bytes 4718596
  146.4 10.6 %copy-start.6 = (bf16[1024,512]{1,0:T(8,128)(2,1)S(1)}, bf16[1024,512]{1,0:T(8,128)(2,1)}, u32[]{:S(2)}) copy-start(bf16[1024,512]{1,0:T(8,128)(2,1)} %copy.49) | copy-start | bytes 3145732
  146.4 5.7 %collective-permute-start.35 = (bf16[240,192]{1,0:T(8,128)(2,1)S(1)}, bf16[240,192]{1,0:T(8,128)(2,1)S(1)}, u32[]{:S(2)}, u32[]{:S(2)}) collective-permute-start(bf16[240,192]{1,0:T(8,128)(2,1)S(1)} %get-tuple-element.26), channel_id=1, source_target_pairs={{0,2},{4,0},{8,4},{12,8},{14,12},{10,14},{6,10},{2,6},{1,3},{5,1},... | collective-permute-start | bytes 276488 | tf_op jit(solution)/shard_map/ppermute | solution.py:176
  149.4 7.1 %collective-permute-start.19 = (bf16[128,1280]{1,0:T(8,128)(2,1)S(1)}, bf16[128,1280]{1,0:T(8,128)(2,1)S(1)}, u32[]{:S(2)}, u32[]{:S(2)}) collective-permute-start(bf16[128,1280]{1,0:T(8,128)(2,1)S(1)} %get-tuple-element.40), channel_id=1, source_target_pairs={{0,4},{4,8},{8,12},{12,14},{14,10},{10,6},{6,2},{2,0},{1,5},{5,9},... | collective-permute-start | bytes 983048 | tf_op jit(solution)/shard_map/ppermute | solution.py:119
  149.9 7.1 %collective-permute-start.15 = (bf16[128,1280]{1,0:T(8,128)(2,1)S(1)}, bf16[128,1280]{1,0:T(8,128)(2,1)S(1)}, u32[]{:S(2)}, u32[]{:S(2)}) collective-permute-start(bf16[128,1280]{1,0:T(8,128)(2,1)S(1)} %get-tuple-element.39), channel_id=1, source_target_pairs={{0,2},{4,0},{8,4},{12,8},{14,12},{10,14},{6,10},{2,6},{1,3},{5,1},... | collective-permute-start | bytes 983048 | tf_op jit(solution)/shard_map/ppermute | solution.py:119
  (13 other events, 25.0 us)

commit v17 on v8

--- a/solution.py
+++ b/solution.py
@@ -295,12 +295,8 @@
         scaled_grad * merged, axis=1, keepdims=True
     )
     grad_skip = grad_merged.astype(jnp.bfloat16)
-    grad_trunk = jnp.dot(
-        upsample.T.astype(jnp.float32),
-        grad_merged,
-        precision=lax.Precision.HIGHEST,
-        preferred_element_type=jnp.float32,
-    ).astype(jnp.bfloat16)
+    paired = grad_merged.reshape(local_tokens, 2 * C)
+    grad_trunk = (paired[:, :C] + paired[:, C:]).astype(jnp.bfloat16)
     grad_heads = grad_trunk.reshape(local_tokens, H, DV)
     row_delta = jnp.sum(grad_heads.astype(jnp.float32) * attended.astype(jnp.float32), axis=2)
     value_grad = jnp.einsum(

time: 159 us -> 164 us (1.031)
  waiting for transfers between devices: 44.8 us -> 50 us
  matrix products: 24.7 us -> 23 us
    ppermute x14, waiting for transfers between devices: 19.8 us -> 24.2 us  [ring_reduce_scatter_sliced(): received = lax.ppermute(acc, axis, perm).astype(jnp.float32)]
    ppermute x8, starting transfers between devices: 7.95 us -> 10.8 us  [ring_scatter_back(): received = lax.ppermute(acc, 'seq', perm).astype(jnp.float32)]
    convert_element_type x6, other arithmetic: 5.39 us -> 2.6 us  [ring_reduce_scatter_sliced(): acc = acc.astype(wire_dtype)]
    reshape x0 -> x1, local copies, waits for them, and re-layouts: none -> 2.29 us  [body(): paired = grad_merged.reshape(local_tokens, 2 * C)]
    dot_general x1, matrix products: 4.22 us -> 2.09 us  [body(): jnp.einsum('ihd,jhd->hij', grad_heads, all_values, preferred_element_type...]
    ppermute x14, starting transfers between devices: 16.7 us -> 14.7 us  [ring_reduce_scatter_sliced(): received = lax.ppermute(acc, axis, perm).astype(jnp.float32)]
    convert_element_type x0 -> x1, other arithmetic: none -> 1.83 us  [body(): grad_trunk = (paired[:, :C] + paired[:, C:]).astype(jnp.bfloat16)]
    dot_general x1, matrix products: 1.77 us -> 3.55 us  [body(): jnp.einsum('hij,ihd->jhd', rounded, grad_heads, preferred_element_type=jn...]
  transfers between devices with their start and end apart: 36 -> 36, of which waited for: 20 -> 18; matrix products, arithmetic and copies ran while one was open for 27% -> 31% of each run, Pallas kernels for 0% -> 0%
where the time goes in v17:
time: 164 us
  waiting for transfers between devices  50 us (30%)
  starting transfers between devices  46 us (28%)
  local copies, waits for them, and re-layouts  25.4 us (15%)
  matrix products  23 us (14%)
  other arithmetic  17.5 us (11%)
  between operations  1.78 us (1%)
    ppermute x14, waiting for transfers between devices, ring_reduce_scatter_sliced(): received = lax.ppermute(acc, axis, perm).astype(jnp.float32)  24.2 us
    ppermute x14, starting transfers between devices, ring_reduce_scatter_sliced(): received = lax.ppermute(acc, axis, perm).astype(jnp.float32)  14.7 us
    ppermute x3, waiting for transfers between devices, ring_gather(): current = lax.ppermute(current, 'seq', forward)  13.4 us
    ppermute x8, starting transfers between devices, ring_scatter_back(): received = lax.ppermute(acc, 'seq', perm).astype(jnp.float32)  10.8 us
    unnamed x62, local copies, waits for them, and re-layouts  9.81 us
    ppermute x2, starting transfers between devices, extended(): before = lax.ppermute(last, axis, up)  8.33 us
    dot_general x5, matrix products, body(): jnp.einsum('spc,spo->co', both_padded[:, offset:offset + positions], both...  8.32 us
    ppermute x3, starting transfers between devices, ring_gather(): current = lax.ppermute(current, 'seq', forward)  6.37 us
  transfers between devices with their start and end apart: 36, of which 18 were waited for; matrix products, arithmetic and copies ran while one was open for 31% of the time, Pallas kernels for 0%

profile of v17, /device:TPU:0, one launch (start us, length us, event | category | flops | bytes accessed | tf_op | source)
XLA Modules:
  0.0 163.6 jit_solution(14763433432979783940)
XLA Ops:
  3.9 3.1 %collective-permute-start = (bf16[128,1280]{0,1:T(8,128)(2,1)}, bf16[128,1280]{0,1:T(8,128)(2,1)}, u32[]{:S(2)}, u32[]{:S(2)}) collective-permute-start(bf16[128,1280]{0,1:T(8,128)(2,1)} %get-tuple-element.54), channel_id=1, source_target_pairs={{0,4},{4,8},{8,12},{12,14},{14,10},{10,6},{6,2},{2,0},{1,5},{5,9},... | collective-permute-start | bytes 983048 | tf_op jit(solution)/shard_map/ppermute | solution.py:76
  7.3 7.6 %collective-permute-done = bf16[128,1280]{0,1:T(8,128)(2,1)} collective-permute-done((bf16[128,1280]{0,1:T(8,128)(2,1)}, bf16[128,1280]{0,1:T(8,128)(2,1)}, u32[]{:S(2)}, u32[]{:S(2)}) %collective-permute-start) | collective-permute-done | bytes 327712 | tf_op jit(solution)/shard_map/ppermute | solution.py:76
  14.9 1.8 %collective-permute-start.1 = (bf16[128,1280]{0,1:T(8,128)(2,1)}, bf16[128,1280]{0,1:T(8,128)(2,1)S(1)}, u32[]{:S(2)}, u32[]{:S(2)}) collective-permute-start(bf16[128,1280]{0,1:T(8,128)(2,1)} %collective-permute-done), channel_id=1, source_target_pairs={{0,4},{4,8},{8,12},{12,14},{14,10},{10,6},{6,2},{2,0},{1,5},{5,9},... | collective-permute-start | bytes 983048 | tf_op jit(solution)/shard_map/ppermute | solution.py:76
  18.2 5.8 %collective-permute-done.1 = bf16[128,1280]{0,1:T(8,128)(2,1)S(1)} collective-permute-done((bf16[128,1280]{0,1:T(8,128)(2,1)}, bf16[128,1280]{0,1:T(8,128)(2,1)S(1)}, u32[]{:S(2)}, u32[]{:S(2)}) %collective-permute-start.1) | collective-permute-done | bytes 327712 | tf_op jit(solution)/shard_map/ppermute | solution.py:76
  24.0 1.5 collective-permute-start.2
  26.0 1.7 %constant_dynamic-update-slice_fusion.5 = bf16[1024,1280]{0,1:T(8,128)(2,1)} fusion(bf16[1024,1280]{0,1:T(8,128)(2,1)} %get-tuple-element.55, bf16[128,1280]{0,1:T(8,128)(2,1)} %collective-permute-done), kind=kLoop, calls=%fused_computation.170 | loop fusion | bytes 655360
  28.5 4.8 %collective-permute-done.5 = bf16[128,1280]{0,1:T(8,128)(2,1)S(1)} collective-permute-done((bf16[128,1280]{0,1:T(8,128)(2,1)S(1)}, bf16[128,1280]{0,1:T(8,128)(2,1)S(1)}, u32[]{:S(2)}, u32[]{:S(2)}) %collective-permute-start.5) | collective-permute-done | bytes 327712 | tf_op jit(solution)/shard_map/ppermute | solution.py:82
  33.9 1.6 collective-permute-start.6
  40.1 1.5 slice.178
  41.6 1.9 %slice.179 = bf16[1024,512]{0,1:T(8,128)(2,1)S(1)} slice(bf16[1024,1280]{0,1:T(8,128)(2,1)} %maximum_dynamic-update-slice_fusion), slice={[0:1024], [0:512]} | slice | bytes 2097152 | tf_op jit(solution)/shard_map/slice | solution.py:191
  47.3 3.4 %collective-permute-start.8 = (bf16[2,768]{1,0:T(2,128)(2,1)S(1)}, bf16[2,768]{1,0:T(2,128)(2,1)S(1)}, u32[]{:S(2)}, u32[]{:S(2)}) collective-permute-start(bf16[2,768]{1,0:T(2,128)(2,1)S(1)} %get-tuple-element.53), channel_id=1, source_target_pairs={{0,2},{2,4},{4,6},{6,8},{8,10},{10,12},{12,14},{1,3},{3,5},{5,7},{... | collective-permute-start | bytes 9224 | tf_op jit(solution)/shard_map/ppermute | solution.py:24
  52.8 3.8 %collective-permute-done.9 = bf16[2,768]{1,0:T(2,128)(2,1)S(1)} collective-permute-done((bf16[2,768]{1,0:T(2,128)(2,1)S(1)}, bf16[2,768]{1,0:T(2,128)(2,1)S(1)}, u32[]{:S(2)}, u32[]{:S(2)}) %collective-permute-start.9) | collective-permute-done | bytes 3104 | tf_op jit(solution)/shard_map/ppermute | solution.py:25
  56.9 2.0 %fusion.32 = (bf16[256,384]{1,0:T(8,128)(2,1)S(1)}, bf16[1,256,384]{2,1,0:T(8,128)(2,1)}) fusion(bf16[1,256,384]{2,1,0:T(8,128)(2,1)S(1)} %copy-done.25, bf16[256,3840]{1,0:T(8,128)(2,1)S(1)} %fusion.34, bf16[3840,384]{1,0:T(8,128)(2,1)S(1)} %copy-done), kind=kOutput, calls=%fused_computation.83 | convolution fusion | flops 756252672 | bytes 5505024 | tf_op jit(solution)/shard_map/dot_general | solution.py:220
  60.2 5.0 %collective-permute-start.11 = (bf16[2,384]{1,0:T(2,128)(2,1)S(1)}, bf16[2,384]{1,0:T(2,128)(2,1)S(1)}, u32[]{:S(2)}, u32[]{:S(2)}) collective-permute-start(bf16[2,384]{1,0:T(2,128)(2,1)S(1)} %get-tuple-element.56), channel_id=1, source_target_pairs={{0,2},{2,4},{4,6},{6,8},{8,10},{10,12},{12,14},{1,3},{3,5},{5,7},{... | collective-permute-start | bytes 4616 | tf_op jit(solution)/shard_map/ppermute | solution.py:24
  69.1 2.3 %reshape.164 = f32[128,1536]{1,0:T(8,128)} reshape(f32[256,768]{1,0:T(8,128)} %get-tuple-element.22) | data formatting | bytes 1572864 | tf_op jit(solution)/shard_map/reshape | solution.py:298
  71.4 1.8 %fusion.33 = bf16[128,768]{1,0:T(8,128)(2,1)} fusion(f32[128,1536]{1,0:T(8,128)} %reshape.164), kind=kLoop, calls=%fused_computation.85 | loop fusion | flops 196608 | bytes 983040 | tf_op jit(solution)/shard_map/convert_element_type | solution.py:299
  74.4 3.6 %convolution_convert_fusion = bf16[4,192,1024]{2,1,0:T(8,128)(2,1)} fusion(bf16[128,4,192]{0,2,1:T(8,128)(2,1)S(1)} %bitcast.196, f32[4,1024,128]{2,1,0:T(8,128)} %copy-done.3, f32[4,128]{1,0:T(4,128)S(1)} %log_add_fusion), kind=kOutput, calls=%fused_computation.24 | convolution fusion | flops 203685888 | bytes 3868672 | tf_op jit(solution)/shard_map/hij,ihd->jhd/dot_general | solution.py:314
  78.0 2.1 %multiply_convert_fusion.1 = bf16[4,128,1024]{1,2,0:T(8,128)(2,1)} fusion(f32[4,1024,128]{2,1,0:T(8,128)S(1)} %copy-done.4, bf16[128,4,192]{0,2,1:T(8,128)(2,1)S(1)} %bitcast.197, bf16[1024,4,192]{0,2,1:T(8,128)(2,1)S(1)} %bitcast.185, f32[4,128]{1,0:T(4,128)S(1)} %bitcast.204, f32[4,128]{1,0:T(4,128)S(1)} %log_add_fusion), kind=kOutput, calls=%fused_computation.22 | convolution fusion | flops 203948032 | bytes 4919296 | tf_op jit(solution)/shard_map/ihd,jhd->hij/dot_general | solution.py:302
  80.1 2.7 %copy.50 = bf16[1024,768]{1,0:T(8,128)(2,1)} copy(bf16[1024,768]{0,1:T(8,128)(2,1)} %bitcast.188) | data formatting | bytes 3145728 | tf_op jit(solution)/shard_map/reshape | solution.py:318
  82.7 2.6 %fusion.9 = bf16[1024,4,128]{2,0,1:T(8,128)(2,1)} fusion(bf16[4,128,1024]{1,2,0:T(8,128)(2,1)} %multiply_convert_fusion.1, bf16[128,4,128]{0,2,1:T(8,128)(2,1)S(1)} %bitcast.200), kind=kOutput, calls=%fused_computation.35 | convolution fusion | flops 135266304 | bytes 2228224 | tf_op jit(solution)/shard_map/hij,ihd->jhd/dot_general | solution.py:311
  85.3 2.3 %copy.47 = bf16[1024,4,128]{0,2,1:T(8,128)(2,1)} copy(bf16[1024,4,128]{2,0,1:T(8,128)(2,1)} %fusion.9) | data formatting | bytes 2097152 | tf_op jit(solution)/shard_map/mul | solution.py:311
  87.6 2.3 %copy.49 = bf16[1024,512]{1,0:T(8,128)(2,1)} copy(bf16[1024,512]{0,1:T(8,128)(2,1)} %bitcast.194) | data formatting | bytes 2097152 | tf_op jit(solution)/shard_map/reshape | solution.py:317
  91.1 2.8 %collective-permute-start.12 = (bf16[128,640]{1,0:T(8,128)(2,1)S(1)}, bf16[128,640]{1,0:T(8,128)(2,1)S(1)}, u32[]{:S(2)}, u32[]{:S(2)}) collective-permute-start(bf16[128,640]{1,0:T(8,128)(2,1)S(1)} %get-tuple-element.45), channel_id=1, source_target_pairs={{0,2},{4,0},{8,4},{12,8},{14,12},{10,14},{6,10},{2,6},{1,3},{5,1},... | collective-permute-start | bytes 491528 | tf_op jit(solution)/shard_map/ppermute | solution.py:119
  93.9 2.0 %collective-permute-start.16 = (bf16[128,640]{1,0:T(8,128)(2,1)S(1)}, bf16[128,640]{1,0:T(8,128)(2,1)S(1)}, u32[]{:S(2)}, u32[]{:S(2)}) collective-permute-start(bf16[128,640]{1,0:T(8,128)(2,1)S(1)} %get-tuple-element.46), channel_id=1, source_target_pairs={{0,4},{4,8},{8,12},{12,14},{14,10},{10,6},{6,2},{2,0},{1,5},{5,9},... | collective-permute-start | bytes 491528 | tf_op jit(solution)/shard_map/ppermute | solution.py:119
  95.9 1.6 %fusion.8 = f32[3840,384]{1,0:T(8,128)S(1)} fusion(bf16[1,260,768]{2,1,0:T(8,128)(2,1)S(1)} %copy-done.20, bf16[1,260,768]{2,1,0:T(8,128)(2,1)} %bitcast.32, bf16[1,256,384]{2,1,0:T(8,128)(2,1)} %bitcast.34, bf16[1,256,384]{2,1,0:T(8,128)(2,1)S(1)} %bitcast.189), kind=kOutput, calls=%fused_computation.34 | convolution fusion | flops 302579712 | bytes 2371584 | tf_op jit(solution)/shard_map/spc,spo->co/dot_general | solution.py:236
  97.5 1.7 %fusion.7 = f32[3840,384]{1,0:T(8,128)S(1)} fusion(f32[3840,384]{1,0:T(8,128)S(1)} %fusion.8, bf16[1,260,768]{2,1,0:T(8,128)(2,1)S(1)} %copy-done.20, bf16[1,260,768]{2,1,0:T(8,128)(2,1)} %bitcast.32, bf16[1,256,384]{2,1,0:T(8,128)(2,1)} %bitcast.34, bf16[1,256,384]{2,1,0:T(8,128)(2,1)S(1)} %bitcast.190), kind=kOutput, calls=%fused_computation.32 | convolution fusion | flops 302579712 | bytes 2377728 | tf_op jit(solution)/shard_map/spc,spo->co/dot_general | solution.py:236
  99.2 1.7 %fusion.6 = f32[3840,384]{1,0:T(8,128)S(1)} fusion(f32[3840,384]{1,0:T(8,128)S(1)} %fusion.7, bf16[1,260,768]{2,1,0:T(8,128)(2,1)S(1)} %copy-done.20, bf16[1,260,768]{2,1,0:T(8,128)(2,1)} %bitcast.32, bf16[1,256,384]{2,1,0:T(8,128)(2,1)} %bitcast.34, bf16[1,256,384]{2,1,0:T(8,128)(2,1)S(1)} %bitcast.191), kind=kOutput, calls=%fused_computation.30 | convolution fusion | flops 302579712 | bytes 2377728 | tf_op jit(solution)/shard_map/spc,spo->co/dot_general | solution.py:236
  100.9 1.7 %fusion.5 = f32[3840,384]{1,0:T(8,128)S(1)} fusion(f32[3840,384]{1,0:T(8,128)S(1)} %fusion.6, bf16[1,260,768]{2,1,0:T(8,128)(2,1)S(1)} %copy-done.20, bf16[1,260,768]{2,1,0:T(8,128)(2,1)} %bitcast.32, bf16[1,256,384]{2,1,0:T(8,128)(2,1)} %bitcast.34, bf16[1,256,384]{2,1,0:T(8,128)(2,1)S(1)} %bitcast.192), kind=kOutput, calls=%fused_computation.28 | convolution fusion | flops 302579712 | bytes 2377728 | tf_op jit(solution)/shard_map/spc,spo->co/dot_general | solution.py:236
  102.5 1.7 %fusion.4 = f32[3840,384]{1,0:T(8,128)S(1)} fusion(f32[3840,384]{1,0:T(8,128)S(1)} %fusion.5, bf16[1,260,768]{2,1,0:T(8,128)(2,1)} %bitcast.32, bf16[1,260,768]{2,1,0:T(8,128)(2,1)S(1)} %copy-done.20, bf16[1,256,384]{2,1,0:T(8,128)(2,1)} %bitcast.34, bf16[1,256,384]{2,1,0:T(8,128)(2,1)S(1)} %bitcast.193), kind=kOutput, calls=%fused_computation.26 | convolution fusion | flops 303759360 | bytes 2377728 | tf_op jit(solution)/shard_map/spc,spo->co/dot_general | solution.py:236
  104.8 1.8 %collective-permute-start.22 = (bf16[240,192]{1,0:T(8,128)(2,1)S(1)}, bf16[240,192]{1,0:T(8,128)(2,1)S(1)}, u32[]{:S(2)}, u32[]{:S(2)}) collective-permute-start(bf16[240,192]{1,0:T(8,128)(2,1)S(1)} %get-tuple-element.37), channel_id=1, source_target_pairs={{0,4},{4,8},{8,12},{12,14},{14,10},{10,6},{6,2},{2,0},{1,5},{5,9},... | collective-permute-start | bytes 276488 | tf_op jit(solution)/shard_map/ppermute | solution.py:176
  107.0 2.7 %collective-permute-done.22 = bf16[240,192]{1,0:T(8,128)(2,1)S(1)} collective-permute-done((bf16[240,192]{1,0:T(8,128)(2,1)S(1)}, bf16[240,192]{1,0:T(8,128)(2,1)S(1)}, u32[]{:S(2)}, u32[]{:S(2)}) %collective-permute-start.22) | collective-permute-done | bytes 92192 | tf_op jit(solution)/shard_map/ppermute | solution.py:176
  109.7 1.8 %collective-permute-done.29 = bf16[240,192]{1,0:T(8,128)(2,1)S(1)} collective-permute-done((bf16[240,192]{1,0:T(8,128)(2,1)S(1)}, bf16[240,192]{1,0:T(8,128)(2,1)S(1)}, u32[]{:S(2)}, u32[]{:S(2)}) %collective-permute-start.29) | collective-permute-done | bytes 92192 | tf_op jit(solution)/shard_map/ppermute | solution.py:176
  111.6 1.6 collective-permute-start.23
  114.0 2.5 %collective-permute-done.23 = bf16[240,192]{1,0:T(8,128)(2,1)S(1)} collective-permute-done((bf16[240,192]{1,0:T(8,128)(2,1)S(1)}, bf16[240,192]{1,0:T(8,128)(2,1)S(1)}, u32[]{:S(2)}, u32[]{:S(2)}) %collective-permute-start.23) | collective-permute-done | bytes 92192 | tf_op jit(solution)/shard_map/ppermute | solution.py:176
  116.5 2.9 %collective-permute-done.30 = bf16[240,192]{1,0:T(8,128)(2,1)S(1)} collective-permute-done((bf16[240,192]{1,0:T(8,128)(2,1)S(1)}, bf16[240,192]{1,0:T(8,128)(2,1)S(1)}, u32[]{:S(2)}, u32[]{:S(2)}) %collective-permute-start.30) | collective-permute-done | bytes 92192 | tf_op jit(solution)/shard_map/ppermute | solution.py:176
  119.6 1.6 collective-permute-start.24
  121.7 1.6 collective-permute-start.17
  124.7 2.0 %collective-permute-done.31 = bf16[240,192]{1,0:T(8,128)(2,1)S(1)} collective-permute-done((bf16[240,192]{1,0:T(8,128)(2,1)S(1)}, bf16[240,192]{1,0:T(8,128)(2,1)S(1)}, u32[]{:S(2)}, u32[]{:S(2)}) %collective-permute-start.31) | collective-permute-done | bytes 92192 | tf_op jit(solution)/shard_map/ppermute | solution.py:176
  127.0 1.9 %collective-permute-start.32 = (bf16[240,192]{1,0:T(8,128)(2,1)S(1)}, bf16[240,192]{1,0:T(8,128)(2,1)S(1)}, u32[]{:S(2)}, u32[]{:S(2)}) collective-permute-start(bf16[240,192]{1,0:T(8,128)(2,1)S(1)} %get-tuple-element.32), channel_id=1, source_target_pairs={{0,2},{4,0},{8,4},{12,8},{14,12},{10,14},{6,10},{2,6},{1,3},{5,1},... | collective-permute-start | bytes 276488 | tf_op jit(solution)/shard_map/ppermute | solution.py:176
  129.3 3.6 %collective-permute-done.25 = bf16[240,192]{1,0:T(8,128)(2,1)S(1)} collective-permute-done((bf16[240,192]{1,0:T(8,128)(2,1)S(1)}, bf16[240,192]{1,0:T(8,128)(2,1)S(1)}, u32[]{:S(2)}, u32[]{:S(2)}) %collective-permute-start.25) | collective-permute-done | bytes 92192 | tf_op jit(solution)/shard_map/ppermute | solution.py:176
  133.6 1.7 %collective-permute-start.33 = (bf16[240,192]{1,0:T(8,128)(2,1)S(1)}, bf16[240,192]{1,0:T(8,128)(2,1)S(1)}, u32[]{:S(2)}, u32[]{:S(2)}) collective-permute-start(bf16[240,192]{1,0:T(8,128)(2,1)S(1)} %get-tuple-element.30), channel_id=1, source_target_pairs={{0,2},{4,0},{8,4},{12,8},{14,12},{10,14},{6,10},{2,6},{1,3},{5,1},... | collective-permute-start | bytes 276488 | tf_op jit(solution)/shard_map/ppermute | solution.py:176
  136.4 2.0 %collective-permute-start.14 = (bf16[128,1280]{1,0:T(8,128)(2,1)}, bf16[128,1280]{1,0:T(8,128)(2,1)S(1)}, u32[]{:S(2)}, u32[]{:S(2)}) collective-permute-start(bf16[128,1280]{1,0:T(8,128)(2,1)} %get-tuple-element.41), channel_id=1, source_target_pairs={{0,2},{4,0},{8,4},{12,8},{14,12},{10,14},{6,10},{2,6},{1,3},{5,1},... | collective-permute-start | bytes 983048 | tf_op jit(solution)/shard_map/ppermute | solution.py:119
  140.6 1.8 %collective-permute-start.34 = (bf16[240,192]{1,0:T(8,128)(2,1)}, bf16[240,192]{1,0:T(8,128)(2,1)}, u32[]{:S(2)}, u32[]{:S(2)}) collective-permute-start(bf16[240,192]{1,0:T(8,128)(2,1)} %get-tuple-element.28), channel_id=1, source_target_pairs={{0,2},{4,0},{8,4},{12,8},{14,12},{10,14},{6,10},{2,6},{1,3},{5,1},... | collective-permute-start | bytes 276488 | tf_op jit(solution)/shard_map/ppermute | solution.py:176
  143.9 6.2 %collective-permute-done.27 = bf16[240,192]{1,0:T(8,128)(2,1)S(1)} collective-permute-done((bf16[240,192]{1,0:T(8,128)(2,1)}, bf16[240,192]{1,0:T(8,128)(2,1)S(1)}, u32[]{:S(2)}, u32[]{:S(2)}) %collective-permute-start.27) | collective-permute-done | bytes 92192 | tf_op jit(solution)/shard_map/ppermute | solution.py:176
  151.4 2.0 %collective-permute-start.35 = (bf16[240,192]{1,0:T(8,128)(2,1)S(1)}, bf16[240,192]{1,0:T(8,128)(2,1)S(1)}, u32[]{:S(2)}, u32[]{:S(2)}) collective-permute-start(bf16[240,192]{1,0:T(8,128)(2,1)S(1)} %get-tuple-element.26), channel_id=1, source_target_pairs={{0,2},{4,0},{8,4},{12,8},{14,12},{10,14},{6,10},{2,6},{1,3},{5,1},... | collective-permute-start | bytes 276488 | tf_op jit(solution)/shard_map/ppermute | solution.py:176
  153.4 1.4 add_convert_fusion.3
  155.0 1.9 %collective-permute-start.15 = (bf16[128,1280]{1,0:T(8,128)(2,1)S(1)}, bf16[128,1280]{1,0:T(8,128)(2,1)S(1)}, u32[]{:S(2)}, u32[]{:S(2)}) collective-permute-start(bf16[128,1280]{1,0:T(8,128)(2,1)S(1)} %get-tuple-element.39), channel_id=1, source_target_pairs={{0,2},{4,0},{8,4},{12,8},{14,12},{10,14},{6,10},{2,6},{1,3},{5,1},... | collective-permute-start | bytes 983048 | tf_op jit(solution)/shard_map/ppermute | solution.py:119
  159.0 3.0 %collective-permute-done.19 = bf16[128,1280]{1,0:T(8,128)(2,1)S(1)} collective-permute-done((bf16[128,1280]{1,0:T(8,128)(2,1)S(1)}, bf16[128,1280]{1,0:T(8,128)(2,1)S(1)}, u32[]{:S(2)}, u32[]{:S(2)}) %collective-permute-start.19) | collective-permute-done | bytes 327712 | tf_op jit(solution)/shard_map/ppermute | solution.py:119
  (155 shorter events, 39.5 us)
Async XLA Ops:
  0.6 56.2 %copy-start = (bf16[3840,384]{1,0:T(8,128)(2,1)S(1)}, bf16[3840,384]{1,0:T(8,128)(2,1)}, u32[]{:S(2)}) copy-start(bf16[3840,384]{1,0:T(8,128)(2,1)} %param.14) | copy-start | bytes 8847364
  0.6 6.3 %copy-start.22 = (bf16[1,128,512]{2,1,0:T(8,128)(2,1)S(1)}, bf16[1,128,512]{2,1,0:T(8,128)(2,1)}, u32[]{:S(2)}) copy-start(bf16[1,128,512]{2,1,0:T(8,128)(2,1)} %param.8) | copy-start | bytes 393220
  0.7 6.4 %copy-start.24 = (bf16[768]{0:T(1024)(128)(2,1)S(1)}, bf16[768]{0:T(1024)(128)(2,1)}, u32[]{:S(2)}) copy-start(bf16[768]{0:T(1024)(128)(2,1)} %param.13) | copy-start | bytes 4612
  3.9 11.0 %collective-permute-start = (bf16[128,1280]{0,1:T(8,128)(2,1)}, bf16[128,1280]{0,1:T(8,128)(2,1)}, u32[]{:S(2)}, u32[]{:S(2)}) collective-permute-start(bf16[128,1280]{0,1:T(8,128)(2,1)} %get-tuple-element.54), channel_id=1, source_target_pairs={{0,4},{4,8},{8,12},{12,14},{14,10},{10,6},{6,2},{2,0},{1,5},{5,9},... | collective-permute-start | bytes 983048 | tf_op jit(solution)/shard_map/ppermute | solution.py:76
  6.9 9.8 %collective-permute-start.3 = (bf16[128,1280]{0,1:T(8,128)(2,1)}, bf16[128,1280]{0,1:T(8,128)(2,1)S(1)}, u32[]{:S(2)}, u32[]{:S(2)}) collective-permute-start(bf16[128,1280]{0,1:T(8,128)(2,1)} %get-tuple-element.54), channel_id=1, source_target_pairs={{0,2},{4,0},{8,4},{12,8},{14,12},{10,14},{6,10},{2,6},{1,3},{5,1},... | collective-permute-start | bytes 983048 | tf_op jit(solution)/shard_map/ppermute | solution.py:82
  7.1 36.4 %copy-start.18 = (bf16[1,128,512]{1,2,0:T(8,128)(2,1)}, bf16[1,128,512]{1,2,0:T(8,128)(2,1)S(1)}, u32[]{:S(2)}) copy-start(bf16[1,128,512]{1,2,0:T(8,128)(2,1)S(1)} %copy.72) | copy-start | bytes 393220
  14.9 9.1 %collective-permute-start.1 = (bf16[128,1280]{0,1:T(8,128)(2,1)}, bf16[128,1280]{0,1:T(8,128)(2,1)S(1)}, u32[]{:S(2)}, u32[]{:S(2)}) collective-permute-start(bf16[128,1280]{0,1:T(8,128)(2,1)} %collective-permute-done), channel_id=1, source_target_pairs={{0,4},{4,8},{8,12},{12,14},{14,10},{10,6},{6,2},{2,0},{1,5},{5,9},... | collective-permute-start | bytes 983048 | tf_op jit(solution)/shard_map/ppermute | solution.py:76
  16.7 8.8 %collective-permute-start.4 = (bf16[128,1280]{0,1:T(8,128)(2,1)S(1)}, bf16[128,1280]{0,1:T(8,128)(2,1)S(1)}, u32[]{:S(2)}, u32[]{:S(2)}) collective-permute-start(bf16[128,1280]{0,1:T(8,128)(2,1)S(1)} %collective-permute-done.3), channel_id=1, source_target_pairs={{0,2},{4,0},{8,4},{12,8},{14,12},{10,14},{6,10},{2,6},{1,3},{5,1},... | collective-permute-start | bytes 983048 | tf_op jit(solution)/shard_map/ppermute | solution.py:82
  24.0 9.9 %collective-permute-start.2 = (bf16[128,1280]{0,1:T(8,128)(2,1)S(1)}, bf16[128,1280]{0,1:T(8,128)(2,1)S(1)}, u32[]{:S(2)}, u32[]{:S(2)}) collective-permute-start(bf16[128,1280]{0,1:T(8,128)(2,1)S(1)} %collective-permute-done.1), channel_id=1, source_target_pairs={{0,4},{4,8},{8,12},{12,14},{14,10},{10,6},{6,2},{2,0},{1,5},{5,9},... | collective-permute-start | bytes 983048 | tf_op jit(solution)/shard_map/ppermute | solution.py:76
  25.5 7.8 %collective-permute-start.5 = (bf16[128,1280]{0,1:T(8,128)(2,1)S(1)}, bf16[128,1280]{0,1:T(8,128)(2,1)S(1)}, u32[]{:S(2)}, u32[]{:S(2)}) collective-permute-start(bf16[128,1280]{0,1:T(8,128)(2,1)S(1)} %collective-permute-done.4), channel_id=1, source_target_pairs={{0,2},{4,0},{8,4},{12,8},{14,12},{10,14},{6,10},{2,6},{1,3},{5,1},... | collective-permute-start | bytes 983048 | tf_op jit(solution)/shard_map/ppermute | solution.py:82
  33.3 5.4 %collective-permute-start.7 = (bf16[128,640]{0,1:T(8,128)(2,1)S(1)}, bf16[128,640]{0,1:T(8,128)(2,1)S(1)}, u32[]{:S(2)}, u32[]{:S(2)}) collective-permute-start(bf16[128,640]{0,1:T(8,128)(2,1)S(1)} %slice.177), channel_id=1, source_target_pairs={{0,2},{4,0},{8,4},{12,8},{14,12},{10,14},{6,10},{2,6},{1,3},{5,1},... | collective-permute-start | bytes 491528 | tf_op jit(solution)/shard_map/ppermute | solution.py:85
  33.9 5.4 %collective-permute-start.6 = (bf16[128,640]{0,1:T(8,128)(2,1)S(1)}, bf16[128,640]{0,1:T(8,128)(2,1)S(1)}, u32[]{:S(2)}, u32[]{:S(2)}) collective-permute-start(bf16[128,640]{0,1:T(8,128)(2,1)S(1)} %slice.176), channel_id=1, source_target_pairs={{0,4},{4,8},{8,12},{12,14},{14,10},{10,6},{6,2},{2,0},{1,5},{5,9},... | collective-permute-start | bytes 491528 | tf_op jit(solution)/shard_map/ppermute | solution.py:79
  47.3 5.2 %collective-permute-start.8 = (bf16[2,768]{1,0:T(2,128)(2,1)S(1)}, bf16[2,768]{1,0:T(2,128)(2,1)S(1)}, u32[]{:S(2)}, u32[]{:S(2)}) collective-permute-start(bf16[2,768]{1,0:T(2,128)(2,1)S(1)} %get-tuple-element.53), channel_id=1, source_target_pairs={{0,2},{2,4},{4,6},{6,8},{8,10},{10,12},{12,14},{1,3},{3,5},{5,7},{... | collective-permute-start | bytes 9224 | tf_op jit(solution)/shard_map/ppermute | solution.py:24
  51.0 5.9 %copy-start.25 = (bf16[1,256,384]{2,1,0:T(8,128)(2,1)S(1)}, bf16[1,256,384]{2,1,0:T(8,128)(2,1)}, u32[]{:S(2)}) copy-start(bf16[1,256,384]{2,1,0:T(8,128)(2,1)} %param.15) | copy-start | bytes 589828
  51.0 5.6 %collective-permute-start.9 = (bf16[2,768]{1,0:T(2,128)(2,1)S(1)}, bf16[2,768]{1,0:T(2,128)(2,1)S(1)}, u32[]{:S(2)}, u32[]{:S(2)}) collective-permute-start(bf16[2,768]{1,0:T(2,128)(2,1)S(1)} %get-tuple-element.52), channel_id=1, source_target_pairs={{2,0},{4,2},{6,4},{8,6},{10,8},{12,10},{14,12},{3,1},{5,3},{7,5},{... | collective-permute-start | bytes 9224 | tf_op jit(solution)/shard_map/ppermute | solution.py:25
  58.9 37.0 %collective-permute-start.21 = (bf16[256,384]{1,0:T(8,128)(2,1)S(1)}, bf16[256,384]{1,0:T(8,128)(2,1)}, u32[]{:S(2)}, u32[]{:S(2)}) collective-permute-start(bf16[256,384]{1,0:T(8,128)(2,1)S(1)} %get-tuple-element.50), channel_id=1, source_target_pairs={{0,1},{1,0},{2,3},{3,2},{4,5},{5,4},{6,7},{7,6},{8,9},{9,8},{10,11... | collective-permute-start | bytes 589832 | tf_op jit(solution)/shard_map/ppermute | solution.py:232
  58.9 7.5 %collective-permute-start.10 = (bf16[2,384]{1,0:T(2,128)(2,1)S(1)}, bf16[2,384]{1,0:T(2,128)(2,1)S(1)}, u32[]{:S(2)}, u32[]{:S(2)}) collective-permute-start(bf16[2,384]{1,0:T(2,128)(2,1)S(1)} %get-tuple-element.57), channel_id=1, source_target_pairs={{2,0},{4,2},{6,4},{8,6},{10,8},{12,10},{14,12},{3,1},{5,3},{7,5},{... | collective-permute-start | bytes 4616 | tf_op jit(solution)/shard_map/ppermute | solution.py:25
  60.2 6.4 %collective-permute-start.11 = (bf16[2,384]{1,0:T(2,128)(2,1)S(1)}, bf16[2,384]{1,0:T(2,128)(2,1)S(1)}, u32[]{:S(2)}, u32[]{:S(2)}) collective-permute-start(bf16[2,384]{1,0:T(2,128)(2,1)S(1)} %get-tuple-element.56), channel_id=1, source_target_pairs={{0,2},{2,4},{4,6},{6,8},{8,10},{10,12},{12,14},{1,3},{3,5},{5,7},{... | collective-permute-start | bytes 4616 | tf_op jit(solution)/shard_map/ppermute | solution.py:24
  66.2 29.7 %collective-permute-start.20 = (bf16[260,768]{1,0:T(8,128)(2,1)}, bf16[260,768]{1,0:T(8,128)(2,1)}, u32[]{:S(2)}, u32[]{:S(2)}) collective-permute-start(bf16[260,768]{1,0:T(8,128)(2,1)} %get-tuple-element.48), channel_id=1, source_target_pairs={{0,1},{1,0},{2,3},{3,2},{4,5},{5,4},{6,7},{7,6},{8,9},{9,8},{10,11... | collective-permute-start | bytes 1198088 | tf_op jit(solution)/shard_map/ppermute | solution.py:231
  89.9 6.0 %copy-start.20 = (bf16[1,260,768]{2,1,0:T(8,128)(2,1)S(1)}, bf16[1,260,768]{2,1,0:T(8,128)(2,1)}, u32[]{:S(2)}) copy-start(bf16[1,260,768]{2,1,0:T(8,128)(2,1)} %get-tuple-element.49) | copy-start | bytes 1198084
  91.1 15.8 %collective-permute-start.12 = (bf16[128,640]{1,0:T(8,128)(2,1)S(1)}, bf16[128,640]{1,0:T(8,128)(2,1)S(1)}, u32[]{:S(2)}, u32[]{:S(2)}) collective-permute-start(bf16[128,640]{1,0:T(8,128)(2,1)S(1)} %get-tuple-element.45), channel_id=1, source_target_pairs={{0,2},{4,0},{8,4},{12,8},{14,12},{10,14},{6,10},{2,6},{1,3},{5,1},... | collective-permute-start | bytes 491528 | tf_op jit(solution)/shard_map/ppermute | solution.py:119
  93.9 12.9 %collective-permute-start.16 = (bf16[128,640]{1,0:T(8,128)(2,1)S(1)}, bf16[128,640]{1,0:T(8,128)(2,1)S(1)}, u32[]{:S(2)}, u32[]{:S(2)}) collective-permute-start(bf16[128,640]{1,0:T(8,128)(2,1)S(1)} %get-tuple-element.46), channel_id=1, source_target_pairs={{0,4},{4,8},{8,12},{12,14},{14,10},{10,6},{6,2},{2,0},{1,5},{5,9},... | collective-permute-start | bytes 491528 | tf_op jit(solution)/shard_map/ppermute | solution.py:119
  104.6 35.0 %copy-start.9 = (f32[3840,384]{1,0:T(8,128)}, f32[3840,384]{1,0:T(8,128)S(1)}, u32[]{:S(2)}) copy-start(f32[3840,384]{1,0:T(8,128)S(1)} %broadcast_multiply_fusion) | copy-start | bytes 17694724
  104.8 4.9 %collective-permute-start.22 = (bf16[240,192]{1,0:T(8,128)(2,1)S(1)}, bf16[240,192]{1,0:T(8,128)(2,1)S(1)}, u32[]{:S(2)}, u32[]{:S(2)}) collective-permute-start(bf16[240,192]{1,0:T(8,128)(2,1)S(1)} %get-tuple-element.37), channel_id=1, source_target_pairs={{0,4},{4,8},{8,12},{12,14},{14,10},{10,6},{6,2},{2,0},{1,5},{5,9},... | collective-permute-start | bytes 276488 | tf_op jit(solution)/shard_map/ppermute | solution.py:176
  106.6 4.9 %collective-permute-start.29 = (bf16[240,192]{1,0:T(8,128)(2,1)S(1)}, bf16[240,192]{1,0:T(8,128)(2,1)S(1)}, u32[]{:S(2)}, u32[]{:S(2)}) collective-permute-start(bf16[240,192]{1,0:T(8,128)(2,1)S(1)} %get-tuple-element.38), channel_id=1, source_target_pairs={{0,2},{4,0},{8,4},{12,8},{14,12},{10,14},{6,10},{2,6},{1,3},{5,1},... | collective-permute-start | bytes 276488 | tf_op jit(solution)/shard_map/ppermute | solution.py:176
  111.6 4.9 %collective-permute-start.23 = (bf16[240,192]{1,0:T(8,128)(2,1)S(1)}, bf16[240,192]{1,0:T(8,128)(2,1)S(1)}, u32[]{:S(2)}, u32[]{:S(2)}) collective-permute-start(bf16[240,192]{1,0:T(8,128)(2,1)S(1)} %get-tuple-element.35), channel_id=1, source_target_pairs={{0,4},{4,8},{8,12},{12,14},{14,10},{10,6},{6,2},{2,0},{1,5},{5,9},... | collective-permute-start | bytes 276488 | tf_op jit(solution)/shard_map/ppermute | solution.py:176
  113.2 6.2 %collective-permute-start.30 = (bf16[240,192]{1,0:T(8,128)(2,1)S(1)}, bf16[240,192]{1,0:T(8,128)(2,1)S(1)}, u32[]{:S(2)}, u32[]{:S(2)}) collective-permute-start(bf16[240,192]{1,0:T(8,128)(2,1)S(1)} %get-tuple-element.36), channel_id=1, source_target_pairs={{0,2},{4,0},{8,4},{12,8},{14,12},{10,14},{6,10},{2,6},{1,3},{5,1},... | collective-permute-start | bytes 276488 | tf_op jit(solution)/shard_map/ppermute | solution.py:176
  113.7 21.7 %collective-permute-start.13 = (bf16[128,1280]{1,0:T(8,128)(2,1)S(1)}, bf16[128,1280]{1,0:T(8,128)(2,1)S(1)}, u32[]{:S(2)}, u32[]{:S(2)}) collective-permute-start(bf16[128,1280]{1,0:T(8,128)(2,1)S(1)} %pad_maximum_fusion.8), channel_id=1, source_target_pairs={{0,2},{4,0},{8,4},{12,8},{14,12},{10,14},{6,10},{2,6},{1,3},{5,1},... | collective-permute-start | bytes 983048 | tf_op jit(solution)/shard_map/ppermute | solution.py:119
  119.6 9.3 %copy-start.13 = (bf16[1024,512]{0,1:T(8,128)(2,1)S(1)}, bf16[1024,512]{0,1:T(8,128)(2,1)}, u32[]{:S(2)}) copy-start(bf16[1024,512]{0,1:T(8,128)(2,1)} %copy-done.12) | copy-start | bytes 3145732
  119.6 9.3 %copy-start.14 = (bf16[4,128,1024]{1,2,0:T(8,128)(2,1)S(1)}, bf16[4,128,1024]{1,2,0:T(8,128)(2,1)}, u32[]{:S(2)}) copy-start(bf16[4,128,1024]{1,2,0:T(8,128)(2,1)} %multiply_convert_fusion.1) | copy-start | bytes 3145732
  119.6 5.1 %collective-permute-start.24 = (bf16[240,192]{1,0:T(8,128)(2,1)S(1)}, bf16[240,192]{1,0:T(8,128)(2,1)S(1)}, u32[]{:S(2)}, u32[]{:S(2)}) collective-permute-start(bf16[240,192]{1,0:T(8,128)(2,1)S(1)} %get-tuple-element.33), channel_id=1, source_target_pairs={{0,4},{4,8},{8,12},{12,14},{14,10},{10,6},{6,2},{2,0},{1,5},{5,9},... | collective-permute-start | bytes 276488 | tf_op jit(solution)/shard_map/ppermute | solution.py:176
  121.2 5.5 %collective-permute-start.31 = (bf16[240,192]{1,0:T(8,128)(2,1)S(1)}, bf16[240,192]{1,0:T(8,128)(2,1)S(1)}, u32[]{:S(2)}, u32[]{:S(2)}) collective-permute-start(bf16[240,192]{1,0:T(8,128)(2,1)S(1)} %get-tuple-element.34), channel_id=1, source_target_pairs={{0,2},{4,0},{8,4},{12,8},{14,12},{10,14},{6,10},{2,6},{1,3},{5,1},... | collective-permute-start | bytes 276488 | tf_op jit(solution)/shard_map/ppermute | solution.py:176
  121.7 13.7 %collective-permute-start.17 = (bf16[128,1280]{1,0:T(8,128)(2,1)S(1)}, bf16[128,1280]{1,0:T(8,128)(2,1)S(1)}, u32[]{:S(2)}, u32[]{:S(2)}) collective-permute-start(bf16[128,1280]{1,0:T(8,128)(2,1)S(1)} %fusion.42), channel_id=1, source_target_pairs={{0,4},{4,8},{8,12},{12,14},{14,10},{10,6},{6,2},{2,0},{1,5},{5,9},... | collective-permute-start | bytes 983048 | tf_op jit(solution)/shard_map/ppermute | solution.py:119
  126.8 6.1 %collective-permute-start.25 = (bf16[240,192]{1,0:T(8,128)(2,1)S(1)}, bf16[240,192]{1,0:T(8,128)(2,1)S(1)}, u32[]{:S(2)}, u32[]{:S(2)}) collective-permute-start(bf16[240,192]{1,0:T(8,128)(2,1)S(1)} %get-tuple-element.31), channel_id=1, source_target_pairs={{0,4},{4,8},{8,12},{12,14},{14,10},{10,6},{6,2},{2,0},{1,5},{5,9},... | collective-permute-start | bytes 276488 | tf_op jit(solution)/shard_map/ppermute | solution.py:176
  127.0 6.0 %collective-permute-start.32 = (bf16[240,192]{1,0:T(8,128)(2,1)S(1)}, bf16[240,192]{1,0:T(8,128)(2,1)S(1)}, u32[]{:S(2)}, u32[]{:S(2)}) collective-permute-start(bf16[240,192]{1,0:T(8,128)(2,1)S(1)} %get-tuple-element.32), channel_id=1, source_target_pairs={{0,2},{4,0},{8,4},{12,8},{14,12},{10,14},{6,10},{2,6},{1,3},{5,1},... | collective-permute-start | bytes 276488 | tf_op jit(solution)/shard_map/ppermute | solution.py:176
  133.1 6.3 %collective-permute-start.26 = (bf16[240,192]{1,0:T(8,128)(2,1)S(1)}, bf16[240,192]{1,0:T(8,128)(2,1)S(1)}, u32[]{:S(2)}, u32[]{:S(2)}) collective-permute-start(bf16[240,192]{1,0:T(8,128)(2,1)S(1)} %get-tuple-element.29), channel_id=1, source_target_pairs={{0,4},{4,8},{8,12},{12,14},{14,10},{10,6},{6,2},{2,0},{1,5},{5,9},... | collective-permute-start | bytes 276488 | tf_op jit(solution)/shard_map/ppermute | solution.py:176
  133.6 8.8 %copy-start.15 = (f32[128,1536]{1,0:T(8,128)S(1)}, f32[128,1536]{1,0:T(8,128)}, u32[]{:S(2)}) copy-start(f32[128,1536]{1,0:T(8,128)} %reshape.164) | copy-start | bytes 2359300
  133.6 6.0 %collective-permute-start.33 = (bf16[240,192]{1,0:T(8,128)(2,1)S(1)}, bf16[240,192]{1,0:T(8,128)(2,1)S(1)}, u32[]{:S(2)}, u32[]{:S(2)}) collective-permute-start(bf16[240,192]{1,0:T(8,128)(2,1)S(1)} %get-tuple-element.30), channel_id=1, source_target_pairs={{0,2},{4,0},{8,4},{12,8},{14,12},{10,14},{6,10},{2,6},{1,3},{5,1},... | collective-permute-start | bytes 276488 | tf_op jit(solution)/shard_map/ppermute | solution.py:176
  136.4 17.0 %collective-permute-start.14 = (bf16[128,1280]{1,0:T(8,128)(2,1)}, bf16[128,1280]{1,0:T(8,128)(2,1)S(1)}, u32[]{:S(2)}, u32[]{:S(2)}) collective-permute-start(bf16[128,1280]{1,0:T(8,128)(2,1)} %get-tuple-element.41), channel_id=1, source_target_pairs={{0,2},{4,0},{8,4},{12,8},{14,12},{10,14},{6,10},{2,6},{1,3},{5,1},... | collective-permute-start | bytes 983048 | tf_op jit(solution)/shard_map/ppermute | solution.py:119
  138.4 15.1 %collective-permute-start.18 = (bf16[128,1280]{1,0:T(8,128)(2,1)}, bf16[128,1280]{1,0:T(8,128)(2,1)}, u32[]{:S(2)}, u32[]{:S(2)}) collective-permute-start(bf16[128,1280]{1,0:T(8,128)(2,1)} %get-tuple-element.42), channel_id=1, source_target_pairs={{0,4},{4,8},{8,12},{12,14},{14,10},{10,6},{6,2},{2,0},{1,5},{5,9},... | collective-permute-start | bytes 983048 | tf_op jit(solution)/shard_map/ppermute | solution.py:119
  140.4 9.7 %collective-permute-start.27 = (bf16[240,192]{1,0:T(8,128)(2,1)}, bf16[240,192]{1,0:T(8,128)(2,1)S(1)}, u32[]{:S(2)}, u32[]{:S(2)}) collective-permute-start(bf16[240,192]{1,0:T(8,128)(2,1)} %get-tuple-element.27), channel_id=1, source_target_pairs={{0,4},{4,8},{8,12},{12,14},{14,10},{10,6},{6,2},{2,0},{1,5},{5,9},... | collective-permute-start | bytes 276488 | tf_op jit(solution)/shard_map/ppermute | solution.py:176
  140.6 9.4 %collective-permute-start.34 = (bf16[240,192]{1,0:T(8,128)(2,1)}, bf16[240,192]{1,0:T(8,128)(2,1)}, u32[]{:S(2)}, u32[]{:S(2)}) collective-permute-start(bf16[240,192]{1,0:T(8,128)(2,1)} %get-tuple-element.28), channel_id=1, source_target_pairs={{0,2},{4,0},{8,4},{12,8},{14,12},{10,14},{6,10},{2,6},{1,3},{5,1},... | collective-permute-start | bytes 276488 | tf_op jit(solution)/shard_map/ppermute | solution.py:176
  151.4 5.6 %collective-permute-start.28 = (bf16[240,192]{1,0:T(8,128)(2,1)S(1)}, bf16[240,192]{1,0:T(8,128)(2,1)S(1)}, u32[]{:S(2)}, u32[]{:S(2)}) collective-permute-start(bf16[240,192]{1,0:T(8,128)(2,1)S(1)} %get-tuple-element.25), channel_id=1, source_target_pairs={{0,4},{4,8},{8,12},{12,14},{14,10},{10,6},{6,2},{2,0},{1,5},{5,9},... | collective-permute-start | bytes 276488 | tf_op jit(solution)/shard_map/ppermute | solution.py:176
  151.4 10.7 %copy-start.2 = (bf16[1024,768]{1,0:T(8,128)(2,1)S(1)}, bf16[1024,768]{1,0:T(8,128)(2,1)}, u32[]{:S(2)}) copy-start(bf16[1024,768]{1,0:T(8,128)(2,1)} %copy.50) | copy-start | bytes 4718596
  151.4 10.7 %copy-start.6 = (bf16[1024,512]{1,0:T(8,128)(2,1)S(1)}, bf16[1024,512]{1,0:T(8,128)(2,1)}, u32[]{:S(2)}) copy-start(bf16[1024,512]{1,0:T(8,128)(2,1)} %copy.49) | copy-start | bytes 3145732
  151.4 5.5 %collective-permute-start.35 = (bf16[240,192]{1,0:T(8,128)(2,1)S(1)}, bf16[240,192]{1,0:T(8,128)(2,1)S(1)}, u32[]{:S(2)}, u32[]{:S(2)}) collective-permute-start(bf16[240,192]{1,0:T(8,128)(2,1)S(1)} %get-tuple-element.26), channel_id=1, source_target_pairs={{0,2},{4,0},{8,4},{12,8},{14,12},{10,14},{6,10},{2,6},{1,3},{5,1},... | collective-permute-start | bytes 276488 | tf_op jit(solution)/shard_map/ppermute | solution.py:176
  154.9 7.1 %collective-permute-start.19 = (bf16[128,1280]{1,0:T(8,128)(2,1)S(1)}, bf16[128,1280]{1,0:T(8,128)(2,1)S(1)}, u32[]{:S(2)}, u32[]{:S(2)}) collective-permute-start(bf16[128,1280]{1,0:T(8,128)(2,1)S(1)} %get-tuple-element.40), channel_id=1, source_target_pairs={{0,4},{4,8},{8,12},{12,14},{14,10},{10,6},{6,2},{2,0},{1,5},{5,9},... | collective-permute-start | bytes 983048 | tf_op jit(solution)/shard_map/ppermute | solution.py:119
  155.0 7.1 %collective-permute-start.15 = (bf16[128,1280]{1,0:T(8,128)(2,1)S(1)}, bf16[128,1280]{1,0:T(8,128)(2,1)S(1)}, u32[]{:S(2)}, u32[]{:S(2)}) collective-permute-start(bf16[128,1280]{1,0:T(8,128)(2,1)S(1)} %get-tuple-element.39), channel_id=1, source_target_pairs={{0,2},{4,0},{8,4},{12,8},{14,12},{10,14},{6,10},{2,6},{1,3},{5,1},... | collective-permute-start | bytes 983048 | tf_op jit(solution)/shard_map/ppermute | solution.py:119
  (14 other events, 32.6 us)
